TPU v7x, 32 devices: a whole 2x2x4 slice. The times are simulated.
32 devices in a mesh: seq: 16 (over z, y, core), head: 2 (over x).
Axes of the slice: x: 2, y: 2, z: 4, core: 2. Of those that a mesh axis runs over, the one named last changes fastest.
Arguments:
- queries: bfloat16 [4096, 4096], P(('seq', 'head')), may hold values from -6 to 6
- keys: bfloat16 [4096, 4096], P(('seq', 'head')), may hold values from -6 to 6
- values: bfloat16 [4096, 4096], P(('seq', 'head')), may hold values from -75 to 75
- out_weight: bfloat16 [4096, 4096], P('seq', 'head'), may hold values from -0.09375 to 0.09375
- norm_gain: float32 [4096], P('head'), may hold values from 0.5 to 1.5
Outputs:
- projected: bfloat16 [4096, 4096], P('seq', 'head')
All inputs are finite; a program needn't handle non-finite values.
Results may differ from a plain program's by a relative error of at most 0.0058.
Values may be sent and summed in bfloat16 or wider, within the bound.
No kernel may reach another device: no remote copies, remote signals or barrier semaphores. Data moves between devices by JAX's collectives and lax.ppermute only.
A program may use at most 128 MiB of HBM per device.

v0:
```python
import jax
import jax.numpy as jnp
from jax import lax
from jax.sharding import PartitionSpec as P

HEAD_DIM = 128


def carried_in(part, axis, combine, identity):
    place = lax.axis_index(axis)
    gathered = lax.all_gather(part, axis)
    state = jnp.zeros_like(part) + jnp.asarray(identity, part.dtype)

    def one(hop, state):
        return combine(state, lax.dynamic_index_in_dim(gathered, hop, 0, False))

    return lax.fori_loop(0, place, one, state)


def add_states(earlier, later):
    return earlier + later


def local(queries, keys, values, out_weight, norm_gain):
    heads_dev = norm_gain.shape[0] // HEAD_DIM
    query_block, key_block, value_block = (
        lax.all_to_all(queries, "head", split_axis=1, concat_axis=0, tiled=True),
        lax.all_to_all(keys, "head", split_axis=1, concat_axis=0, tiled=True),
        lax.all_to_all(values, "head", split_axis=1, concat_axis=0, tiled=True),
    )
    row_count = query_block.shape[0]
    query_heads = query_block.reshape(row_count, heads_dev, HEAD_DIM)
    key_heads = key_block.reshape(row_count, heads_dev, HEAD_DIM)
    value_heads = value_block.reshape(row_count, heads_dev, HEAD_DIM)
    kv_state = jnp.einsum(
        "thd,the->hde", key_heads, value_heads, preferred_element_type=jnp.float32
    )
    prefix = carried_in(kv_state, "seq", add_states, jnp.zeros_like(kv_state))
    carried = jnp.einsum(
        "thd,hde->the", query_heads, prefix.astype(jnp.bfloat16), preferred_element_type=jnp.float32
    )
    block_rows = min(512, row_count)
    parts_list = []
    for first_row in range(0, row_count, block_rows):
        last_row = min(first_row + block_rows, row_count)
        scores = jnp.einsum(
            "thd,shd->hts",
            query_heads[first_row:last_row],
            key_heads[:last_row],
            preferred_element_type=jnp.float32,
        )
        row_index = first_row + lax.broadcasted_iota(jnp.int32, (last_row - first_row, last_row), 0)
        col_index = lax.broadcasted_iota(jnp.int32, (last_row - first_row, last_row), 1)
        scores = jnp.where((col_index <= row_index)[None], scores, jnp.zeros_like(scores)).astype(
            jnp.bfloat16
        )
        parts_list.append(
            jnp.einsum(
                "hts,she->the", scores, value_heads[:last_row], preferred_element_type=jnp.float32
            )
        )
    within_block = jnp.concatenate(parts_list, axis=0)
    attended = carried + within_block
    mean_square = jnp.mean(attended * attended, axis=2, keepdims=True)
    gain_heads = norm_gain.reshape(heads_dev, HEAD_DIM)
    normed = (attended * lax.rsqrt(mean_square + 1e-06) * gain_heads[None]).astype(jnp.bfloat16)
    normed = normed.reshape(row_count, heads_dev * HEAD_DIM)
    returned = lax.all_to_all(normed, "head", split_axis=0, concat_axis=1, tiled=True)
    gathered = lax.all_gather(returned, "head", axis=0, tiled=True)
    outcome = jnp.dot(
        gathered,
        lax.all_gather(out_weight, "seq", axis=0, tiled=True),
        preferred_element_type=jnp.float32,
    )
    return outcome.astype(jnp.bfloat16)


def solution(mesh):
    return jax.shard_map(
        local,
        mesh=mesh,
        in_specs=(
            P(("seq", "head"), None),
            P(("seq", "head"), None),
            P(("seq", "head"), None),
            P("seq", "head"),
            P("head"),
        ),
        out_specs=P("seq", "head"),
        check_vma=False,
    )
```

profile of v0, /device:TPU:13, one launch (start us, length us, event | category | flops | bytes accessed | tf_op | source)
XLA Modules:
  0.0 359.5 jit_solution(12308427636008386715)
XLA Ops:
  6.5 2.4 copy.44
  8.9 3.6 all-to-all-start.1
  13.8 11.7 %all-to-all-done.1 = bf16[128,2,2048]{2,0,1:T(8,128)(2,1)S(1)} async-done(((bf16[128,2,2048]{2,0,1:T(8,128)(2,1)}), bf16[128,2,2048]{2,0,1:T(8,128)(2,1)S(1)}, u32[]{:S(2)}, u32[]{:S(2)}) %all-to-all-start.1) | async-done | bytes 1048608 | tf_op jit(solution)/shard_map/all_to_all | solution.py:29
  25.5 3.6 all-to-all-start
  30.2 11.0 %all-to-all-done = bf16[128,2,2048]{0,2,1:T(8,128)(2,1)S(1)} async-done(((bf16[128,2,2048]{0,2,1:T(8,128)(2,1)}), bf16[128,2,2048]{0,2,1:T(8,128)(2,1)S(1)}, u32[]{:S(2)}, u32[]{:S(2)}) %all-to-all-start) | async-done | bytes 1048608 | tf_op jit(solution)/shard_map/all_to_all | solution.py:28
  41.2 8.6 %copy.18 = bf16[2,128,2048]{1,0,2:T(2,128)(2,1)S(1)} copy(bf16[2,128,2048]{1,2,0:T(8,128)(2,1)S(1)} %bitcast.44) | data formatting | bytes 2097152 | tf_op jit(solution)/shard_map/all_to_all | solution.py:28
  50.5 1.4 fusion.6
  53.8 3.6 all-to-all-start.2
  57.5 11.2 %all-to-all-done.2 = bf16[128,2,2048]{2,0,1:T(8,128)(2,1)S(1)} async-done(((bf16[128,2,2048]{2,0,1:T(8,128)(2,1)}), bf16[128,2,2048]{2,0,1:T(8,128)(2,1)S(1)}, u32[]{:S(2)}, u32[]{:S(2)}) %all-to-all-start.2) | async-done | bytes 1048608 | tf_op jit(solution)/shard_map/all_to_all | solution.py:27
  69.8 3.8 %fusion = f32[16,256,128]{1,2,0:T(8,128)} fusion(bf16[256,16,128]{0,2,1:T(8,128)(2,1)S(1)} %copy.26, bf16[256,16,128]{0,2,1:T(8,128)(2,1)S(1)} %reshape.42, pred[256,256]{1,0:T(8,128)(4,1)S(1)} %iota_compare_fusion, bf16[256,16,128]{2,1,0:T(8,128)(2,1)} %bitcast.47), kind=kOutput, calls=%fused_computation.6 | convolution fusion | flops 538968064 | bytes 5308416 | tf_op jit(solution)/shard_map/hts,she->the/dot_general | solution.py:58
  73.7 104.9 %all-gather.9.cloned.1.call-done = f32[256,128,128]{2,1,0:T(8,128)} async-done(((f32[16,128,128]{2,1,0:T(8,128)}), f32[256,128,128]{2,1,0:T(8,128)}) %all-gather.9.cloned.1.call-update) | async-done | bytes 16777232 | tf_op jit(solution)/shard_map/all_gather | solution.py:11
  178.7 10.7 %while.10 = (s32[]{:T(128)}, f32[16,128,128]{2,1,0:T(8,128)S(1)}, s32[]{:T(128)}, f32[16,16,128,128]{3,2,1,0:T(8,128)}, s32[]{:T(128)}, /*index=5*/s32[]{:T(128)}, s32[]{:T(128)}) while((s32[]{:T(128)}, f32[16,128,128]{2,1,0:T(8,128)S(1)}, s32[]{:T(128)}, f32[16,16,128,128]{3,2,1,0:T(8,128)}, s32[]{:T(128)}, /*index=5*/s32[]{:T(128)}, ...), condition=%wide.region_1.2_spmd, body=%wide.region_0.1_spmd.sunk | while | flops 262149 | bytes 3145843 | solution.py:17
  178.7 1.6 bitcast_add_fusion.3
  180.3 1.5 bitcast_add_fusion.3
  181.8 1.5 bitcast_add_fusion.3
  183.3 1.5 bitcast_add_fusion.3
  184.9 1.5 bitcast_add_fusion.3
  186.4 1.5 bitcast_add_fusion.3
  187.9 1.5 bitcast_add_fusion.3
  189.5 2.5 multiply_reduce_fusion
  192.8 16.4 %all_to_all.67 = bf16[2,128,2048]{1,2,0:T(8,128)(2,1)} all-to-all(bf16[2,128,2048]{1,2,0:T(8,128)(2,1)S(1)} %copy.27), channel_id=1, replica_groups=mesh['seq'=16,'head'=2] {'head'}, dimensions={0} | all-to-all | bytes 2097152 | tf_op jit(solution)/shard_map/all_to_all | solution.py:68
  209.2 96.7 %all-gather.7.cloned.1.call-done = bf16[4096,2048]{1,0:T(8,128)(2,1)} async-done(((bf16[256,2048]{1,0:T(8,128)(2,1)}), bf16[4096,2048]{1,0:T(8,128)(2,1)}) %all-gather.7.cloned.1.call-update) | async-done | bytes 16777232 | tf_op jit(solution)/shard_map/all_gather | solution.py:72
  305.8 35.3 %all-gather.5.cloned.1.call-done = bf16[256,4096]{0,1:T(8,128)(2,1)} async-done(((bf16[128,4096]{0,1:T(8,128)(2,1)}), bf16[256,4096]{0,1:T(8,128)(2,1)}) %all-gather.5.cloned.1.call-update) | async-done | bytes 2097168 | tf_op jit(solution)/shard_map/all_gather | solution.py:69
  341.1 11.9 %convolution_convert_fusion = bf16[256,2048]{1,0:T(8,128)(2,1)} fusion(bf16[256,4096]{0,1:T(8,128)(2,1)} %all-gather.5.cloned.1.call-done, bf16[4096,2048]{1,0:T(8,128)(2,1)} %all-gather.7.cloned.1.call-done), kind=kOutput, calls=%fused_computation.2 | convolution fusion | flops 4295491584 | bytes 19922944 | tf_op jit(solution)/shard_map/dot_general | solution.py:70
  (26 shorter events, 7.1 us)
Async XLA Ops:
  6.5 6.0 %copy-start.1 = (bf16[128,4096]{1,0:T(8,128)(2,1)S(1)}, bf16[128,4096]{1,0:T(8,128)(2,1)}, u32[]{:S(2)}) copy-start(bf16[128,4096]{1,0:T(8,128)(2,1)} %param.8) | copy-start | bytes 3145732
  8.9 16.6 %all-to-all-start.1 = ((bf16[128,2,2048]{2,0,1:T(8,128)(2,1)}), bf16[128,2,2048]{2,0,1:T(8,128)(2,1)S(1)}, u32[]{:S(2)}, u32[]{:S(2)}) async-start(bf16[128,2,2048]{2,0,1:T(8,128)(2,1)} %bitcast.38), calls=%async_computation.1 | async-start | bytes 2097152 | tf_op jit(solution)/shard_map/all_to_all | solution.py:29
  25.5 15.6 %all-to-all-start = ((bf16[128,2,2048]{0,2,1:T(8,128)(2,1)}), bf16[128,2,2048]{0,2,1:T(8,128)(2,1)S(1)}, u32[]{:S(2)}, u32[]{:S(2)}) async-start(bf16[128,2,2048]{0,2,1:T(8,128)(2,1)} %bitcast.1), calls=%async_computation | async-start | bytes 2097152 | tf_op jit(solution)/shard_map/all_to_all | solution.py:28
  29.1 149.5 %all-gather.9.cloned.1.call-start = ((), (), s32[]{:S(2)}) async-start(), calls=%async_computation.6 | async-start | bytes 17825792 | tf_op jit(solution)/shard_map/all_gather | solution.py:11
  50.5 2.2 copy-start.2
  52.0 253.9 %all-gather.7.cloned.1.call-start = ((), (), s32[]{:S(2)}) async-start(), calls=%async_computation.5 | async-start | bytes 17825792 | tf_op jit(solution)/shard_map/all_gather | solution.py:72
  53.8 14.8 %all-to-all-start.2 = ((bf16[128,2,2048]{2,0,1:T(8,128)(2,1)}), bf16[128,2,2048]{2,0,1:T(8,128)(2,1)S(1)}, u32[]{:S(2)}, u32[]{:S(2)}) async-start(bf16[128,2,2048]{2,0,1:T(8,128)(2,1)} %bitcast.43), calls=%async_computation.2 | async-start | bytes 2097152 | tf_op jit(solution)/shard_map/all_to_all | solution.py:27
  57.4 283.7 %all-gather.5.cloned.1.call-start = ((), (), s32[]{:S(2)}) async-start(), calls=%async_computation.4 | async-start | bytes 3145728 | tf_op jit(solution)/shard_map/all_gather | solution.py:69
  178.7 10.8 %copy-start = (bf16[32,8,16,128]{3,2,1,0:T(8,128)(2,1)S(1)}, bf16[32,8,16,128]{3,2,1,0:T(8,128)(2,1)}, u32[]{:S(2)}) copy-start(bf16[32,8,16,128]{3,2,1,0:T(8,128)(2,1)} %copy.33) | copy-start | bytes 3145732
  189.5 2.5 copy-start.3
Sparse Core Ops, SparseCore 0:
  52.1 126.4 all-gather.8
  180.7 125.0 all-gather.6
  307.4 33.6 all-gather.4
where the time goes:
time: 362 us; the launch traced here: 360 us
  waiting for transfers between devices  271 us (75%)
  matrix products  19.6 us (5%)
  local copies, waits for them, and re-layouts  16.9 us (5%)
  blocking collectives  16.4 us (5%)
  between operations  13.3 us (4%)
  starting transfers between devices  10.9 us (3%)
  other arithmetic  10.9 us (3%)
    all_gather x1, waiting for transfers between devices, carried_in(): gathered = lax.all_gather(part, axis)  105 us
    all_gather x1, waiting for transfers between devices, local(): lax.all_gather(out_weight, 'seq', axis=0, tiled=True)  96.7 us
    all_gather x1, waiting for transfers between devices, local(): gathered = lax.all_gather(returned, 'head', axis=0, tiled=True)  35.3 us
    all_to_all x1, blocking collectives, local(): lax.all_to_all(normed, 'head', split_axis=0, concat_axis=1, tiled=True)  16.4 us
    dot_general x1, matrix products, local(): jnp.dot(gathered, lax.all_gather(out_weight, 'seq', axis=0, tiled=True),...  11.9 us
    all_to_all x1, waiting for transfers between devices, local(): lax.all_to_all(values, 'head', split_axis=1, concat_axis=0, tiled=True)  11.7 us
    all_to_all x1, waiting for transfers between devices, local(): lax.all_to_all(queries, 'head', split_axis=1, concat_axis=0, tiled=True)  11.2 us
    all_to_all x1, waiting for transfers between devices, local(): lax.all_to_all(keys, 'head', split_axis=1, concat_axis=0, tiled=True)  11 us
  transfers between devices with their start and end apart: 6, of which 6 were waited for; matrix products, arithmetic and copies ran while one was open for 6% of the time, Pallas kernels for 0%

commit v1 on v0

v1 whole, which is shorter than its diff:
```python
import functools

import jax
import jax.numpy as jnp
from jax import lax
from jax.sharding import PartitionSpec as P

HEAD_DIM = 128


def exclusive_prefix(state, axis, size):
    total = state
    shift = 1
    while shift < size:
        pairs = [(i, i + shift) for i in range(size - shift)]
        total = total + lax.ppermute(total, axis, pairs)
        shift *= 2
    return total - state


def pair_order(own, other, place, axis):
    first = jnp.where(place == 0, own, other)
    second = jnp.where(place == 0, other, own)
    return jnp.concatenate([first, second], axis=axis)


def local(queries, keys, values, out_weight, norm_gain, n_seq, n_head):
    heads_dev = norm_gain.shape[0] // HEAD_DIM
    width = heads_dev * HEAD_DIM
    rows = queries.shape[0]
    weight_full = lax.all_gather(out_weight, "seq", axis=0, tiled=True)
    if n_head == 2:
        place = lax.axis_index("head")
        stacked = jnp.stack([queries, keys, values]).reshape(3, rows, 2, width)
        own = lax.dynamic_index_in_dim(stacked, place, 2, False)
        sent = lax.dynamic_index_in_dim(stacked, 1 - place, 2, False)
        other = lax.ppermute(sent, "head", [(0, 1), (1, 0)])
        block = pair_order(own, other, place, 1)
        query_block, key_block, value_block = block[0], block[1], block[2]
    else:
        query_block, key_block, value_block = (
            lax.all_to_all(queries, "head", split_axis=1, concat_axis=0, tiled=True),
            lax.all_to_all(keys, "head", split_axis=1, concat_axis=0, tiled=True),
            lax.all_to_all(values, "head", split_axis=1, concat_axis=0, tiled=True),
        )
    row_count = query_block.shape[0]
    query_heads = query_block.reshape(row_count, heads_dev, HEAD_DIM)
    key_heads = key_block.reshape(row_count, heads_dev, HEAD_DIM)
    value_heads = value_block.reshape(row_count, heads_dev, HEAD_DIM)
    kv_state = jnp.einsum(
        "thd,the->hde", key_heads, value_heads, preferred_element_type=jnp.float32
    )
    prefix = exclusive_prefix(kv_state, "seq", n_seq)
    carried = jnp.einsum(
        "thd,hde->the", query_heads, prefix.astype(jnp.bfloat16), preferred_element_type=jnp.float32
    )
    block_rows = min(512, row_count)
    parts_list = []
    for first_row in range(0, row_count, block_rows):
        last_row = min(first_row + block_rows, row_count)
        scores = jnp.einsum(
            "thd,shd->hts",
            query_heads[first_row:last_row],
            key_heads[:last_row],
            preferred_element_type=jnp.float32,
        )
        row_index = first_row + lax.broadcasted_iota(jnp.int32, (last_row - first_row, last_row), 0)
        col_index = lax.broadcasted_iota(jnp.int32, (last_row - first_row, last_row), 1)
        scores = jnp.where((col_index <= row_index)[None], scores, jnp.zeros_like(scores)).astype(
            jnp.bfloat16
        )
        parts_list.append(
            jnp.einsum(
                "hts,she->the", scores, value_heads[:last_row], preferred_element_type=jnp.float32
            )
        )
    within_block = jnp.concatenate(parts_list, axis=0)
    attended = carried + within_block
    mean_square = jnp.mean(attended * attended, axis=2, keepdims=True)
    gain_heads = norm_gain.reshape(heads_dev, HEAD_DIM)
    normed = (attended * lax.rsqrt(mean_square + 1e-06) * gain_heads[None]).astype(jnp.bfloat16)
    normed = normed.reshape(row_count, width)
    if n_head == 2:
        other = lax.ppermute(normed, "head", [(0, 1), (1, 0)])
        gathered = pair_order(normed, other, place, 1)
    else:
        gathered = lax.all_gather(normed, "head", axis=1, tiled=True)
    outcome = jnp.dot(gathered, weight_full, preferred_element_type=jnp.float32)
    return outcome.astype(jnp.bfloat16)


def solution(mesh):
    body = functools.partial(local, n_seq=mesh.shape["seq"], n_head=mesh.shape["head"])
    return jax.shard_map(
        body,
        mesh=mesh,
        in_specs=(
            P(("seq", "head"), None),
            P(("seq", "head"), None),
            P(("seq", "head"), None),
            P("seq", "head"),
            P("head"),
        ),
        out_specs=P("seq", "head"),
        check_vma=False,
    )
```

time: 362 us -> 286 us (0.79)
  the two profiles are of different devices: /device:TPU:13 before, /device:TPU:26 now
where the time goes in v1:
time: 286 us; the launch traced here: 285 us
  waiting for transfers between devices  231 us (81%)
  matrix products  19.8 us (7%)
  between operations  13.5 us (5%)
  starting transfers between devices  7.51 us (3%)
  other arithmetic  7.05 us (2%)
  local copies, waits for them, and re-layouts  6.24 us (2%)
    ppermute x4, waiting for transfers between devices, exclusive_prefix(): total = total + lax.ppermute(total, axis, pairs)  170 us
    ppermute x1, waiting for transfers between devices, local(): other = lax.ppermute(sent, 'head', [(0, 1), (1, 0)])  35.9 us
    ppermute x1, waiting for transfers between devices, local(): other = lax.ppermute(normed, 'head', [(0, 1), (1, 0)])  24.6 us
    dot_general x1, matrix products, local(): outcome = jnp.dot(gathered, weight_full, preferred_element_type=jnp.float32)  12.3 us
    ppermute x4, starting transfers between devices, exclusive_prefix(): total = total + lax.ppermute(total, axis, pairs)  6.41 us
  transfers between devices with their start and end apart: 7, of which 6 were waited for; matrix products, arithmetic and copies ran while one was open for 7% of the time, Pallas kernels for 0%

profile of v1, /device:TPU:26, one launch (start us, length us, event | category | flops | bytes accessed | tf_op | source)
XLA Modules:
  0.0 285.2 jit_solution(9465771504735247999)
XLA Ops:
  6.5 0.7 all-gather.2.cloned.1.call-update
  7.3 2.4 copy.19
  9.6 1.3 copy.20
  10.9 1.3 copy.21
  12.2 2.2 pad_maximum_fusion
  14.4 1.3 dynamic-slice_bitcast_fusion
  15.7 0.5 collective-permute-start
  16.2 35.9 %collective-permute-done = bf16[3,128,2048]{1,2,0:T(8,128)(2,1)} collective-permute-done((bf16[3,128,2048]{1,2,0:T(8,128)(2,1)}, bf16[3,128,2048]{1,2,0:T(8,128)(2,1)}, u32[]{:S(2)}, u32[]{:S(2)}) %collective-permute-start) | collective-permute-done | bytes 1572896 | tf_op jit(solution)/shard_map/ppermute | solution.py:37
  52.2 1.6 bitcast_select_fusion
  53.8 1.3 fusion.8
  55.5 1.9 collective-permute-start.1
  57.4 52.1 %collective-permute-done.1 = f32[16,128,128]{2,1,0:T(8,128)S(1)} collective-permute-done((f32[16,128,128]{2,1,0:T(8,128)S(1)}, f32[16,128,128]{2,1,0:T(8,128)S(1)}, u32[]{:S(2)}, u32[]{:S(2)}) %collective-permute-start.1) | collective-permute-done | bytes 1048608 | tf_op jit(solution)/shard_map/ppermute | solution.py:16
  109.7 1.9 collective-permute-start.2
  111.6 50.8 %collective-permute-done.2 = f32[16,128,128]{2,1,0:T(8,128)S(1)} collective-permute-done((f32[16,128,128]{2,1,0:T(8,128)S(1)}, f32[16,128,128]{2,1,0:T(8,128)S(1)}, u32[]{:S(2)}, u32[]{:S(2)}) %collective-permute-start.2) | collective-permute-done | bytes 1048608 | tf_op jit(solution)/shard_map/ppermute | solution.py:16
  162.6 1.3 collective-permute-start.3
  163.9 24.6 %collective-permute-done.3 = f32[16,128,128]{2,1,0:T(8,128)S(1)} collective-permute-done((f32[16,128,128]{2,1,0:T(8,128)S(1)}, f32[16,128,128]{2,1,0:T(8,128)S(1)}, u32[]{:S(2)}, u32[]{:S(2)}) %collective-permute-start.3) | collective-permute-done | bytes 1048608 | tf_op jit(solution)/shard_map/ppermute | solution.py:16
  188.5 1.1 add.41
  189.5 1.3 collective-permute-start.4
  190.9 3.9 %fusion.6 = f32[16,128,256]{2,1,0:T(8,128)} fusion(bf16[256,16,128]{0,2,1:T(8,128)(2,1)S(1)} %bitcast.34, bf16[256,16,128]{0,2,1:T(8,128)(2,1)} %bitcast.35, bf16[256,16,128]{0,2,1:T(8,128)(2,1)S(1)} %bitcast.32, pred[256,256]{1,0:T(8,128)(4,1)S(1)} %iota_compare_fusion), kind=kOutput, calls=%fused_computation.15 | convolution fusion | flops 538968064 | bytes 5308416 | tf_op jit(solution)/shard_map/hts,she->the/dot_general | solution.py:73
  194.8 42.4 %collective-permute-done.4 = f32[16,128,128]{2,1,0:T(8,128)} collective-permute-done((f32[16,128,128]{2,1,0:T(8,128)}, f32[16,128,128]{2,1,0:T(8,128)}, u32[]{:S(2)}, u32[]{:S(2)}) %collective-permute-start.4) | collective-permute-done | bytes 1048608 | tf_op jit(solution)/shard_map/ppermute | solution.py:16
  237.2 3.1 %fusion.3 = (f32[256,16]{0,1:T(8,128)S(1)}, f32[16,128,256]{2,1,0:T(8,128)S(1)}) fusion(f32[16,128,256]{2,1,0:T(8,128)} %fusion.6, bf16[256,16,128]{0,2,1:T(8,128)(2,1)} %bitcast.36, f32[16,128,128]{2,1,0:T(8,128)S(1)} %fusion.11, f32[16,128,128]{2,1,0:T(8,128)} %add.41, f32[16,128,128]{2,1,0:T(8,128)} %collective-permute-done.4), kind=kOutput, calls=%fused_computation.12 | convolution fusion | flops 136572928 | bytes 8404992 | tf_op jit(solution)/shard_map/thd,hde->the/dot_general | solution.py:54
  240.7 0.6 collective-permute-start.5
  241.2 24.6 %collective-permute-done.5 = bf16[256,2048]{0,1:T(8,128)(2,1)S(1)} collective-permute-done((bf16[256,2048]{0,1:T(8,128)(2,1)S(1)}, bf16[256,2048]{0,1:T(8,128)(2,1)S(1)}, u32[]{:S(2)}, u32[]{:S(2)}) %collective-permute-start.5) | collective-permute-done | bytes 1048608 | tf_op jit(solution)/shard_map/ppermute | solution.py:84
  266.1 12.3 %convolution_convert_fusion = bf16[256,2048]{1,0:T(8,128)(2,1)} fusion(bf16[4096,2048]{1,0:T(8,128)(2,1)} %all-gather.2.cloned.1.call-done, bf16[256,2048]{0,1:T(8,128)(2,1)S(1)} %get-tuple-element.11, bf16[256,2048]{0,1:T(8,128)(2,1)S(1)} %get-tuple-element.10), kind=kOutput, calls=%fused_computation.6 | convolution fusion | flops 4299685888 | bytes 19922944 | tf_op jit(solution)/shard_map/dot_general | solution.py:88
  (15 shorter events, 1.3 us)
Async XLA Ops:
  6.5 3.1 %copy-start = (bf16[128,4096]{1,0:T(8,128)(2,1)S(1)}, bf16[128,4096]{1,0:T(8,128)(2,1)}, u32[]{:S(2)}) copy-start(bf16[128,4096]{1,0:T(8,128)(2,1)} %param.6) | copy-start | bytes 3145732
  6.5 259.5 %all-gather.2.cloned.1.call-start = ((), (), s32[]{:S(2)}) async-start(), calls=%async_computation | async-start | bytes 17825792 | tf_op jit(solution)/shard_map/all_gather | solution.py:31
  7.3 3.7 %copy-start.1 = (bf16[128,4096]{1,0:T(8,128)(2,1)S(1)}, bf16[128,4096]{1,0:T(8,128)(2,1)}, u32[]{:S(2)}) copy-start(bf16[128,4096]{1,0:T(8,128)(2,1)} %param.7) | copy-start | bytes 3145732
  15.7 36.5 %collective-permute-start = (bf16[3,128,2048]{1,2,0:T(8,128)(2,1)}, bf16[3,128,2048]{1,2,0:T(8,128)(2,1)}, u32[]{:S(2)}, u32[]{:S(2)}) collective-permute-start(bf16[3,128,2048]{1,2,0:T(8,128)(2,1)} %dynamic-slice_bitcast_fusion), channel_id=1, source_target_pairs={{0,1},{1,0},{2,3},{3,2},{4,5},{5,4},{6,7},{7,6},{8,9},{9,8},{10,11... | collective-permute-start | bytes 4718600 | tf_op jit(solution)/shard_map/ppermute | solution.py:37
  55.5 54.0 %collective-permute-start.1 = (f32[16,128,128]{2,1,0:T(8,128)S(1)}, f32[16,128,128]{2,1,0:T(8,128)S(1)}, u32[]{:S(2)}, u32[]{:S(2)}) collective-permute-start(f32[16,128,128]{2,1,0:T(8,128)S(1)} %fusion.11), channel_id=1, source_target_pairs={{0,2},{2,4},{4,6},{6,8},{8,10},{10,12},{12,14},{14,16},{16,18},{18... | collective-permute-start | bytes 3145736 | tf_op jit(solution)/shard_map/ppermute | solution.py:16
  109.7 52.7 %collective-permute-start.2 = (f32[16,128,128]{2,1,0:T(8,128)S(1)}, f32[16,128,128]{2,1,0:T(8,128)S(1)}, u32[]{:S(2)}, u32[]{:S(2)}) collective-permute-start(f32[16,128,128]{2,1,0:T(8,128)S(1)} %add.39), channel_id=1, source_target_pairs={{0,4},{2,6},{4,8},{6,10},{8,12},{10,14},{12,16},{14,18},{16,20},{1... | collective-permute-start | bytes 3145736 | tf_op jit(solution)/shard_map/ppermute | solution.py:16
  162.6 25.9 %collective-permute-start.3 = (f32[16,128,128]{2,1,0:T(8,128)S(1)}, f32[16,128,128]{2,1,0:T(8,128)S(1)}, u32[]{:S(2)}, u32[]{:S(2)}) collective-permute-start(f32[16,128,128]{2,1,0:T(8,128)S(1)} %add.40), channel_id=1, source_target_pairs={{0,8},{2,10},{4,12},{6,14},{8,16},{10,18},{12,20},{14,22},{16,24},... | collective-permute-start | bytes 3145736 | tf_op jit(solution)/shard_map/ppermute | solution.py:16
  189.5 47.6 %collective-permute-start.4 = (f32[16,128,128]{2,1,0:T(8,128)}, f32[16,128,128]{2,1,0:T(8,128)}, u32[]{:S(2)}, u32[]{:S(2)}) collective-permute-start(f32[16,128,128]{2,1,0:T(8,128)} %add.41), channel_id=1, source_target_pairs={{0,16},{2,18},{4,20},{6,22},{8,24},{10,26},{12,28},{14,30},{1,17},... | collective-permute-start | bytes 3145736 | tf_op jit(solution)/shard_map/ppermute | solution.py:16
  194.8 45.5 %copy-start.2 = (f32[2048]{0:T(1024)S(1)}, f32[2048]{0:T(1024)}, u32[]{:S(2)}) copy-start(f32[2048]{0:T(1024)} %param.9) | copy-start | bytes 24580
  240.7 25.1 %collective-permute-start.5 = (bf16[256,2048]{0,1:T(8,128)(2,1)S(1)}, bf16[256,2048]{0,1:T(8,128)(2,1)S(1)}, u32[]{:S(2)}, u32[]{:S(2)}) collective-permute-start(bf16[256,2048]{0,1:T(8,128)(2,1)S(1)} %bitcast.37), channel_id=1, source_target_pairs={{0,1},{1,0},{2,3},{3,2},{4,5},{5,4},{6,7},{7,6},{8,9},{9,8},{10,11... | collective-permute-start | bytes 3145736 | tf_op jit(solution)/shard_map/ppermute | solution.py:84
Sparse Core Ops, SparseCore 0:
  9.5 153.2 all-gather.1

commit v2 on v1

v2 whole, which is shorter than its diff:
```python
import functools

import jax
import jax.numpy as jnp
from jax import lax
from jax.sharding import Mesh
from jax.sharding import PartitionSpec as P

HEAD_DIM = 128
SWAP = [(0, 1), (1, 0)]


def exclusive_prefix(state, axis, size):
    total = state
    shift = 1
    while shift < size:
        pairs = [(i, i + shift) for i in range(size - shift)]
        total = total + lax.ppermute(total, axis, pairs)
        shift *= 2
    return total - state


def pair_order(own, other, place, axis):
    first = jnp.where(place == 0, own, other)
    second = jnp.where(place == 0, other, own)
    return jnp.concatenate([first, second], axis=axis)


def head_blocks(arrays, n_head, place):
    if n_head == 2:
        rows = arrays[0].shape[0]
        width = arrays[0].shape[1] // 2
        stacked = jnp.stack(arrays).reshape(len(arrays), rows, 2, width)
        own = lax.dynamic_index_in_dim(stacked, place, 2, False)
        sent = lax.dynamic_index_in_dim(stacked, 1 - place, 2, False)
        other = lax.ppermute(sent, "head", SWAP)
        block = pair_order(own, other, place, 1)
        return [block[i] for i in range(len(arrays))]
    return [
        lax.all_to_all(a, "head", split_axis=1, concat_axis=0, tiled=True) for a in arrays
    ]


def local(queries, keys, values, out_weight, norm_gain, n_chip, n_head):
    heads_dev = norm_gain.shape[0] // HEAD_DIM
    width = heads_dev * HEAD_DIM
    core = lax.axis_index("core")
    place = lax.axis_index("head") if n_head == 2 else 0
    weight_own = lax.all_gather(out_weight, "chip", axis=0, tiled=True)
    weight_other = lax.ppermute(weight_own, "core", SWAP)

    key_block, value_block = head_blocks([keys, values], n_head, place)
    (query_block,) = head_blocks([queries], n_head, place)
    row_count = query_block.shape[0]
    query_heads = query_block.reshape(row_count, heads_dev, HEAD_DIM)
    key_heads = key_block.reshape(row_count, heads_dev, HEAD_DIM)
    value_heads = value_block.reshape(row_count, heads_dev, HEAD_DIM)
    kv_state = jnp.einsum(
        "thd,the->hde", key_heads, value_heads, preferred_element_type=jnp.float32
    )
    partner_state = lax.ppermute(kv_state, "core", SWAP)
    chip_state = kv_state + partner_state
    half = heads_dev // 2
    chip_half = lax.dynamic_slice_in_dim(chip_state, core * half, half, 0)
    chip_prefix_half = exclusive_prefix(chip_half, "chip", n_chip)
    other_half = lax.ppermute(chip_prefix_half, "core", SWAP)
    chip_prefix = pair_order(chip_prefix_half, other_half, core, 0)
    prefix = chip_prefix + jnp.where(core == 1, partner_state, jnp.zeros_like(partner_state))

    carried = jnp.einsum(
        "thd,hde->the", query_heads, prefix.astype(jnp.bfloat16), preferred_element_type=jnp.float32
    )
    block_rows = min(512, row_count)
    parts_list = []
    for first_row in range(0, row_count, block_rows):
        last_row = min(first_row + block_rows, row_count)
        scores = jnp.einsum(
            "thd,shd->hts",
            query_heads[first_row:last_row],
            key_heads[:last_row],
            preferred_element_type=jnp.float32,
        )
        row_index = first_row + lax.broadcasted_iota(jnp.int32, (last_row - first_row, last_row), 0)
        col_index = lax.broadcasted_iota(jnp.int32, (last_row - first_row, last_row), 1)
        scores = jnp.where((col_index <= row_index)[None], scores, jnp.zeros_like(scores)).astype(
            jnp.bfloat16
        )
        parts_list.append(
            jnp.einsum(
                "hts,she->the", scores, value_heads[:last_row], preferred_element_type=jnp.float32
            )
        )
    within_block = jnp.concatenate(parts_list, axis=0)
    attended = carried + within_block
    mean_square = jnp.mean(attended * attended, axis=2, keepdims=True)
    gain_heads = norm_gain.reshape(heads_dev, HEAD_DIM)
    normed = (attended * lax.rsqrt(mean_square + 1e-06) * gain_heads[None]).astype(jnp.bfloat16)
    normed = normed.reshape(row_count, width)
    if n_head == 2:
        other = lax.ppermute(normed, "head", SWAP)
        gathered = pair_order(normed, other, place, 1)
    else:
        gathered = lax.all_gather(normed, "head", axis=1, tiled=True)
    weight_rows = out_weight.shape[0]
    split = gathered.reshape(row_count, n_chip, 2, weight_rows)
    normed_own = lax.dynamic_index_in_dim(split, core, 2, False).reshape(row_count, -1)
    normed_other = lax.dynamic_index_in_dim(split, 1 - core, 2, False).reshape(row_count, -1)
    outcome = jnp.dot(normed_own, weight_own, preferred_element_type=jnp.float32)
    outcome = outcome + jnp.dot(normed_other, weight_other, preferred_element_type=jnp.float32)
    return outcome.astype(jnp.bfloat16)


def solution(mesh):
    n_seq = mesh.shape["seq"]
    n_head = mesh.shape["head"]
    fine = Mesh(mesh.devices.reshape(n_seq // 2, 2, n_head), ("chip", "core", "head"))
    rows = ("chip", "core", "head")
    body = functools.partial(local, n_chip=n_seq // 2, n_head=n_head)
    return jax.shard_map(
        body,
        mesh=fine,
        in_specs=(
            P(rows, None),
            P(rows, None),
            P(rows, None),
            P(("chip", "core"), "head"),
            P("head"),
        ),
        out_specs=P(("chip", "core"), "head"),
        check_vma=False,
    )
```

time: 286 us -> 268 us (0.937)
  the two profiles are of different devices: /device:TPU:26 before, /device:TPU:13 now
where the time goes in v2:
time: 268 us; the launch traced here: 265 us
  waiting for transfers between devices  188 us (70%)
  starting transfers between devices  18.7 us (7%)
  matrix products  17.4 us (6%)
  other arithmetic  14.6 us (5%)
  between operations  13.6 us (5%)
  local copies, waits for them, and re-layouts  11.9 us (4%)
    all_gather x1, waiting for transfers between devices, local(): weight_own = lax.all_gather(out_weight, 'chip', axis=0, tiled=True)  96.3 us
    ppermute x3, waiting for transfers between devices, exclusive_prefix(): total = total + lax.ppermute(total, axis, pairs)  34 us
    ppermute x1, waiting for transfers between devices, local(): other = lax.ppermute(normed, 'head', SWAP)  22.9 us
    ppermute x2, waiting for transfers between devices, head_blocks(): other = lax.ppermute(sent, 'head', SWAP)  22.9 us
    ppermute x3, starting transfers between devices, exclusive_prefix(): total = total + lax.ppermute(total, axis, pairs)  12.3 us
    ppermute x1, waiting for transfers between devices, local(): partner_state = lax.ppermute(kv_state, 'core', SWAP)  11.6 us
    dot_general x1, matrix products, local(): jnp.dot(normed_other, weight_other, preferred_element_type=jnp.float32)  6.7 us
    dot_general x1, matrix products, local(): jnp.dot(normed_own, weight_own, preferred_element_type=jnp.float32)  5.74 us
  transfers between devices with their start and end apart: 10, of which 7 were waited for; matrix products, arithmetic and copies ran while one was open for 14% of the time, Pallas kernels for 0%

profile of v2, /device:TPU:13, one launch (start us, length us, event | category | flops | bytes accessed | tf_op | source)
XLA Modules:
  0.0 264.6 jit_solution(16753475121576344755)
XLA Ops:
  7.3 1.6 copy.32
  11.0 22.9 %collective-permute-done = bf16[2,128,2048]{1,2,0:T(8,128)(2,1)} collective-permute-done((bf16[2,128,2048]{1,2,0:T(8,128)(2,1)S(1)}, bf16[2,128,2048]{1,2,0:T(8,128)(2,1)}, u32[]{:S(2)}, u32[]{:S(2)}) %collective-permute-start) | collective-permute-done | bytes 1048608 | tf_op jit(solution)/shard_map/ppermute | solution.py:36
  33.9 2.4 broadcast_select_fusion.1
  36.2 96.3 %all-gather.2.cloned.1.call-done = bf16[2048,2048]{1,0:T(8,128)(2,1)} async-done(((bf16[256,2048]{1,0:T(8,128)(2,1)}), bf16[2048,2048]{1,0:T(8,128)(2,1)}) %all-gather.2.cloned.1.call-update) | async-done | bytes 8388624 | tf_op jit(solution)/shard_map/all_gather | solution.py:49
  133.4 1.4 fusion.5
  136.2 11.6 %collective-permute-done.1 = f32[16,128,128]{2,1,0:T(8,128)} collective-permute-done((f32[16,128,128]{2,1,0:T(8,128)S(1)}, f32[16,128,128]{2,1,0:T(8,128)}, u32[]{:S(2)}, u32[]{:S(2)}) %collective-permute-start.1) | collective-permute-done | bytes 1048608 | tf_op jit(solution)/shard_map/ppermute | solution.py:61
  149.1 5.1 %collective-permute-start.2 = (f32[8,128,128]{2,1,0:T(8,128)S(1)}, f32[8,128,128]{2,1,0:T(8,128)}, u32[]{:S(2)}, u32[]{:S(2)}) collective-permute-start(f32[8,128,128]{2,1,0:T(8,128)S(1)} %dynamic-slice_add_fusion), channel_id=1, source_target_pairs={{0,4},{4,8},{8,12},{12,16},{16,20},{20,24},{24,28},{1,5},{5,9},{9,... | collective-permute-start | bytes 1572872 | tf_op jit(solution)/shard_map/ppermute | solution.py:18
  154.1 2.3 copy.19
  156.4 8.6 %collective-permute-done.2 = f32[8,128,128]{2,1,0:T(8,128)} collective-permute-done((f32[8,128,128]{2,1,0:T(8,128)S(1)}, f32[8,128,128]{2,1,0:T(8,128)}, u32[]{:S(2)}, u32[]{:S(2)}) %collective-permute-start.2) | collective-permute-done | bytes 524320 | tf_op jit(solution)/shard_map/ppermute | solution.py:18
  166.1 3.3 %collective-permute-start.3 = (f32[8,128,128]{2,1,0:T(8,128)S(1)}, f32[8,128,128]{2,1,0:T(8,128)}, u32[]{:S(2)}, u32[]{:S(2)}) collective-permute-start(f32[8,128,128]{2,1,0:T(8,128)S(1)} %add.61), channel_id=1, source_target_pairs={{0,8},{4,12},{8,16},{12,20},{16,24},{20,28},{1,9},{5,13},{9,17},{1... | collective-permute-start | bytes 1572872 | tf_op jit(solution)/shard_map/ppermute | solution.py:18
  170.5 2.1 copy.21
  173.8 6.6 %collective-permute-done.3 = f32[8,128,128]{2,1,0:T(8,128)} collective-permute-done((f32[8,128,128]{2,1,0:T(8,128)S(1)}, f32[8,128,128]{2,1,0:T(8,128)}, u32[]{:S(2)}, u32[]{:S(2)}) %collective-permute-start.3) | collective-permute-done | bytes 524320 | tf_op jit(solution)/shard_map/ppermute | solution.py:18
  180.4 1.9 add.62
  182.3 3.9 %collective-permute-start.4 = (f32[8,128,128]{2,1,0:T(8,128)}, f32[8,128,128]{2,1,0:T(8,128)}, u32[]{:S(2)}, u32[]{:S(2)}) collective-permute-start(f32[8,128,128]{2,1,0:T(8,128)} %add.62), channel_id=1, source_target_pairs={{0,16},{4,20},{8,24},{12,28},{1,17},{5,21},{9,25},{13,29},{2,18},{... | collective-permute-start | bytes 1572872 | tf_op jit(solution)/shard_map/ppermute | solution.py:18
  188.6 18.8 %collective-permute-done.4 = f32[8,128,128]{2,1,0:T(8,128)} collective-permute-done((f32[8,128,128]{2,1,0:T(8,128)}, f32[8,128,128]{2,1,0:T(8,128)}, u32[]{:S(2)}, u32[]{:S(2)}) %collective-permute-start.4) | collective-permute-done | bytes 524320 | tf_op jit(solution)/shard_map/ppermute | solution.py:18
  207.4 2.1 add_subtract_fusion
  209.5 1.7 collective-permute-start.5
  212.2 1.5 copy.22
  213.7 2.7 %fusion.4 = f32[16,128,256]{2,1,0:T(8,128)} fusion(bf16[256,16,128]{0,2,1:T(8,128)(2,1)S(1)} %bitcast.47, bf16[256,16,128]{0,2,1:T(8,128)(2,1)S(1)} %bitcast.52, bf16[256,16,128]{0,2,1:T(8,128)(2,1)S(1)} %bitcast.45, pred[256,256]{1,0:T(8,128)(4,1)S(1)} %iota_compare_fusion), kind=kOutput, calls=%fused_computation.15 | convolution fusion | flops 538968064 | bytes 5308416 | tf_op jit(solution)/shard_map/hts,she->the/dot_general | solution.py:89
  216.4 1.4 broadcast_select_fusion.5
  218.3 1.8 fusion.1
  221.8 22.9 %collective-permute-done.7 = bf16[256,2048]{0,1:T(8,128)(2,1)S(1)} collective-permute-done((bf16[256,2048]{0,1:T(8,128)(2,1)S(1)}, bf16[256,2048]{0,1:T(8,128)(2,1)S(1)}, u32[]{:S(2)}, u32[]{:S(2)}) %collective-permute-start.7) | collective-permute-done | bytes 1048608 | tf_op jit(solution)/shard_map/ppermute | solution.py:100
  245.3 5.7 %fusion.18 = f32[256,2048]{1,0:T(8,128)S(1)} fusion(bf16[256,2048]{0,1:T(8,128)(2,1)S(1)} %bitcast.56, bf16[2048,2048]{1,0:T(8,128)(2,1)} %all-gather.2.cloned.1.call-done), kind=kOutput, calls=%fused_computation.48 | convolution fusion | flops 2147483648 | bytes 11534336 | tf_op jit(solution)/shard_map/dot_general | solution.py:108
  251.0 6.7 %fusion = bf16[256,2048]{1,0:T(8,128)(2,1)} fusion(f32[256,2048]{1,0:T(8,128)S(1)} %fusion.18, bf16[256,2048]{0,1:T(8,128)(2,1)S(1)} %bitcast.55, bf16[2048,2048]{1,0:T(8,128)(2,1)} %collective-permute-done.8), kind=kOutput, calls=%fused_computation.2 | convolution fusion | flops 2148532224 | bytes 12582912 | tf_op jit(solution)/shard_map/dot_general | solution.py:109
  (35 shorter events, 15.8 us)
Async XLA Ops:
  6.5 2.4 copy-start.3
  6.5 126.0 %all-gather.2.cloned.1.call-start = ((), (), s32[]{:S(2)}) async-start(), calls=%async_computation | async-start | bytes 9437184 | tf_op jit(solution)/shard_map/all_gather | solution.py:49
  9.7 24.2 %collective-permute-start = (bf16[2,128,2048]{1,2,0:T(8,128)(2,1)S(1)}, bf16[2,128,2048]{1,2,0:T(8,128)(2,1)}, u32[]{:S(2)}, u32[]{:S(2)}) collective-permute-start(bf16[2,128,2048]{1,2,0:T(8,128)(2,1)S(1)} %fusion.7), channel_id=1, source_target_pairs={{0,1},{1,0},{2,3},{3,2},{4,5},{5,4},{6,7},{7,6},{8,9},{9,8},{10,11... | collective-permute-start | bytes 3145736 | tf_op jit(solution)/shard_map/ppermute | solution.py:36
  132.5 118.5 %collective-permute-start.8 = (bf16[2048,2048]{1,0:T(8,128)(2,1)}, bf16[2048,2048]{1,0:T(8,128)(2,1)}, u32[]{:S(2)}, u32[]{:S(2)}) collective-permute-start(bf16[2048,2048]{1,0:T(8,128)(2,1)} %all-gather.2.cloned.1.call-done), channel_id=1, source_target_pairs={{0,2},{2,0},{1,3},{3,1},{4,6},{6,4},{5,7},{7,5},{8,10},{10,8},{9,1... | collective-permute-start | bytes 25165832 | tf_op jit(solution)/shard_map/ppermute | solution.py:50
  135.3 1.0 copy-start.2
  135.3 12.5 %collective-permute-start.1 = (f32[16,128,128]{2,1,0:T(8,128)S(1)}, f32[16,128,128]{2,1,0:T(8,128)}, u32[]{:S(2)}, u32[]{:S(2)}) collective-permute-start(f32[16,128,128]{2,1,0:T(8,128)S(1)} %fusion.17), channel_id=1, source_target_pairs={{0,2},{2,0},{1,3},{3,1},{4,6},{6,4},{5,7},{7,5},{8,10},{10,8},{9,1... | collective-permute-start | bytes 3145736 | tf_op jit(solution)/shard_map/ppermute | solution.py:61
  149.1 16.0 %collective-permute-start.2 = (f32[8,128,128]{2,1,0:T(8,128)S(1)}, f32[8,128,128]{2,1,0:T(8,128)}, u32[]{:S(2)}, u32[]{:S(2)}) collective-permute-start(f32[8,128,128]{2,1,0:T(8,128)S(1)} %dynamic-slice_add_fusion), channel_id=1, source_target_pairs={{0,4},{4,8},{8,12},{12,16},{16,20},{20,24},{24,28},{1,5},{5,9},{9,... | collective-permute-start | bytes 1572872 | tf_op jit(solution)/shard_map/ppermute | solution.py:18
  156.4 13.1 %copy-start.1 = (bf16[128,4096]{0,1:T(8,128)(2,1)S(1)}, bf16[128,4096]{0,1:T(8,128)(2,1)}, u32[]{:S(2)}) copy-start(bf16[128,4096]{0,1:T(8,128)(2,1)} %copy.19) | copy-start | bytes 3145732
  166.1 14.2 %collective-permute-start.3 = (f32[8,128,128]{2,1,0:T(8,128)S(1)}, f32[8,128,128]{2,1,0:T(8,128)}, u32[]{:S(2)}, u32[]{:S(2)}) collective-permute-start(f32[8,128,128]{2,1,0:T(8,128)S(1)} %add.61), channel_id=1, source_target_pairs={{0,8},{4,12},{8,16},{12,20},{16,24},{20,28},{1,9},{5,13},{9,17},{1... | collective-permute-start | bytes 1572872 | tf_op jit(solution)/shard_map/ppermute | solution.py:18
  172.6 14.9 %collective-permute-start.6 = (bf16[1,128,2048]{2,1,0:T(8,128)(2,1)}, bf16[1,128,2048]{2,1,0:T(8,128)(2,1)}, u32[]{:S(2)}, u32[]{:S(2)}) collective-permute-start(bf16[1,128,2048]{2,1,0:T(8,128)(2,1)} %bitcast.59), channel_id=1, source_target_pairs={{0,1},{1,0},{2,3},{3,2},{4,5},{5,4},{6,7},{7,6},{8,9},{9,8},{10,11... | collective-permute-start | bytes 1572872 | tf_op jit(solution)/shard_map/ppermute | solution.py:36
  182.3 25.1 %collective-permute-start.4 = (f32[8,128,128]{2,1,0:T(8,128)}, f32[8,128,128]{2,1,0:T(8,128)}, u32[]{:S(2)}, u32[]{:S(2)}) collective-permute-start(f32[8,128,128]{2,1,0:T(8,128)} %add.62), channel_id=1, source_target_pairs={{0,16},{4,20},{8,24},{12,28},{1,17},{5,21},{9,25},{13,29},{2,18},{... | collective-permute-start | bytes 1572872 | tf_op jit(solution)/shard_map/ppermute | solution.py:18
  209.5 6.9 %collective-permute-start.5 = (f32[8,128,128]{2,1,0:T(8,128)}, f32[8,128,128]{2,1,0:T(8,128)}, u32[]{:S(2)}, u32[]{:S(2)}) collective-permute-start(f32[8,128,128]{2,1,0:T(8,128)} %add_subtract_fusion), channel_id=1, source_target_pairs={{0,2},{2,0},{1,3},{3,1},{4,6},{6,4},{5,7},{7,5},{8,10},{10,8},{9,1... | collective-permute-start | bytes 1572872 | tf_op jit(solution)/shard_map/ppermute | solution.py:66
  216.4 1.9 copy-start
  218.3 1.8 copy-start.4
  220.5 24.3 %collective-permute-start.7 = (bf16[256,2048]{0,1:T(8,128)(2,1)S(1)}, bf16[256,2048]{0,1:T(8,128)(2,1)S(1)}, u32[]{:S(2)}, u32[]{:S(2)}) collective-permute-start(bf16[256,2048]{0,1:T(8,128)(2,1)S(1)} %bitcast.57), channel_id=1, source_target_pairs={{0,1},{1,0},{2,3},{3,2},{4,5},{5,4},{6,7},{7,6},{8,9},{9,8},{10,11... | collective-permute-start | bytes 3145736 | tf_op jit(solution)/shard_map/ppermute | solution.py:100
Sparse Core Ops, SparseCore 0:
  9.5 122.9 all-gather.1

commit v3 on v2

--- a/solution.py
+++ b/solution.py
@@ -47,7 +47,6 @@
     core = lax.axis_index("core")
     place = lax.axis_index("head") if n_head == 2 else 0
     weight_own = lax.all_gather(out_weight, "chip", axis=0, tiled=True)
-    weight_other = lax.ppermute(weight_own, "core", SWAP)
 
     key_block, value_block = head_blocks([keys, values], n_head, place)
     (query_block,) = head_blocks([queries], n_head, place)
@@ -101,6 +100,8 @@
         gathered = pair_order(normed, other, place, 1)
     else:
         gathered = lax.all_gather(normed, "head", axis=1, tiled=True)
+    weight_own, gathered = lax.optimization_barrier((weight_own, gathered))
+    weight_other = lax.ppermute(weight_own, "core", SWAP)
     weight_rows = out_weight.shape[0]
     split = gathered.reshape(row_count, n_chip, 2, weight_rows)
     normed_own = lax.dynamic_index_in_dim(split, core, 2, False).reshape(row_count, -1)

time: 268 us -> 230 us (0.86)
  waiting for transfers between devices: 188 us -> 155 us
    all_gather x1, waiting for transfers between devices: 96.3 us -> 0.02 us  [local(): weight_own = lax.all_gather(out_weight, 'chip', axis=0, tiled=True)]
    ppermute x3, waiting for transfers between devices: 34 us -> 98.3 us  [exclusive_prefix(): total = total + lax.ppermute(total, axis, pairs)]
    ppermute x1, waiting for transfers between devices: 11.6 us -> 2.42 us  [local(): partner_state = lax.ppermute(kv_state, 'core', SWAP)]
    ppermute x1, waiting for transfers between devices: 0.01 us -> 7.54 us  [local(): weight_other = lax.ppermute(weight_own, 'core', SWAP)]
    ppermute x3, starting transfers between devices: 12.3 us -> 8.43 us  [exclusive_prefix(): total = total + lax.ppermute(total, axis, pairs)]
  transfers between devices with their start and end apart: 10 -> 10, of which waited for: 7 -> 7; matrix products, arithmetic and copies ran while one was open for 14% -> 15% of each run, Pallas kernels for 0% -> 0%
where the time goes in v3:
time: 230 us; the launch traced here: 226 us
  waiting for transfers between devices  155 us (67%)
  matrix products  17.5 us (8%)
  starting transfers between devices  16.1 us (7%)
  between operations  13.6 us (6%)
  other arithmetic  12.4 us (5%)
  local copies, waits for them, and re-layouts  11.1 us (5%)
    ppermute x3, waiting for transfers between devices, exclusive_prefix(): total = total + lax.ppermute(total, axis, pairs)  98.3 us
    ppermute x1, waiting for transfers between devices, local(): other = lax.ppermute(normed, 'head', SWAP)  23 us
    ppermute x2, waiting for transfers between devices, head_blocks(): other = lax.ppermute(sent, 'head', SWAP)  22.9 us
    ppermute x3, starting transfers between devices, exclusive_prefix(): total = total + lax.ppermute(total, axis, pairs)  8.43 us
    ppermute x1, waiting for transfers between devices, local(): weight_other = lax.ppermute(weight_own, 'core', SWAP)  7.54 us
    dot_general x1, matrix products, local(): jnp.dot(normed_other, weight_other, preferred_element_type=jnp.float32)  6.7 us
    dot_general x1, matrix products, local(): jnp.dot(normed_own, weight_own, preferred_element_type=jnp.float32)  5.74 us
  transfers between devices with their start and end apart: 10, of which 7 were waited for; matrix products, arithmetic and copies ran while one was open for 15% of the time, Pallas kernels for 0%

profile of v3, /device:TPU:13, one launch (start us, length us, event | category | flops | bytes accessed | tf_op | source)
XLA Modules:
  0.0 225.6 jit_solution(5697802563167051884)
XLA Ops:
  7.3 1.6 copy.32
  11.0 22.9 %collective-permute-done = bf16[2,128,2048]{1,2,0:T(8,128)(2,1)} collective-permute-done((bf16[2,128,2048]{1,2,0:T(8,128)(2,1)S(1)}, bf16[2,128,2048]{1,2,0:T(8,128)(2,1)}, u32[]{:S(2)}, u32[]{:S(2)}) %collective-permute-start) | collective-permute-done | bytes 1048608 | tf_op jit(solution)/shard_map/ppermute | solution.py:36
  33.9 1.4 broadcast_select_fusion.1
  36.0 1.6 collective-permute-start.1
  37.5 2.4 %collective-permute-done.1 = f32[16,128,128]{2,1,0:T(8,128)} collective-permute-done((f32[16,128,128]{2,1,0:T(8,128)S(1)}, f32[16,128,128]{2,1,0:T(8,128)}, u32[]{:S(2)}, u32[]{:S(2)}) %collective-permute-start.1) | collective-permute-done | bytes 1048608 | tf_op jit(solution)/shard_map/ppermute | solution.py:60
  41.2 3.2 %collective-permute-start.2 = (f32[8,128,128]{2,1,0:T(8,128)S(1)}, f32[8,128,128]{2,1,0:T(8,128)}, u32[]{:S(2)}, u32[]{:S(2)}) collective-permute-start(f32[8,128,128]{2,1,0:T(8,128)S(1)} %dynamic-slice_add_fusion), channel_id=1, source_target_pairs={{0,4},{4,8},{8,12},{12,16},{16,20},{20,24},{24,28},{1,5},{5,9},{9,... | collective-permute-start | bytes 1572872 | tf_op jit(solution)/shard_map/ppermute | solution.py:18
  44.4 2.3 %copy.19 = bf16[128,4096]{0,1:T(8,128)(2,1)} copy(bf16[128,4096]{1,0:T(8,128)(2,1)} %param.5) | data formatting | bytes 2097152 | tf_op args[0]
  46.7 18.7 %collective-permute-done.2 = f32[8,128,128]{2,1,0:T(8,128)} collective-permute-done((f32[8,128,128]{2,1,0:T(8,128)S(1)}, f32[8,128,128]{2,1,0:T(8,128)}, u32[]{:S(2)}, u32[]{:S(2)}) %collective-permute-start.2) | collective-permute-done | bytes 524320 | tf_op jit(solution)/shard_map/ppermute | solution.py:18
  66.5 3.2 %collective-permute-start.3 = (f32[8,128,128]{2,1,0:T(8,128)S(1)}, f32[8,128,128]{2,1,0:T(8,128)}, u32[]{:S(2)}, u32[]{:S(2)}) collective-permute-start(f32[8,128,128]{2,1,0:T(8,128)S(1)} %add.61), channel_id=1, source_target_pairs={{0,8},{4,12},{8,16},{12,20},{16,24},{20,28},{1,9},{5,13},{9,17},{1... | collective-permute-start | bytes 1572872 | tf_op jit(solution)/shard_map/ppermute | solution.py:18
  70.7 2.2 copy.21
  74.1 29.3 %collective-permute-done.3 = f32[8,128,128]{2,1,0:T(8,128)} collective-permute-done((f32[8,128,128]{2,1,0:T(8,128)S(1)}, f32[8,128,128]{2,1,0:T(8,128)}, u32[]{:S(2)}, u32[]{:S(2)}) %collective-permute-start.3) | collective-permute-done | bytes 524320 | tf_op jit(solution)/shard_map/ppermute | solution.py:18
  103.3 1.9 add.62
  105.2 2.1 collective-permute-start.4
  109.7 50.3 %collective-permute-done.4 = f32[8,128,128]{2,1,0:T(8,128)} collective-permute-done((f32[8,128,128]{2,1,0:T(8,128)}, f32[8,128,128]{2,1,0:T(8,128)}, u32[]{:S(2)}, u32[]{:S(2)}) %collective-permute-start.4) | collective-permute-done | bytes 524320 | tf_op jit(solution)/shard_map/ppermute | solution.py:18
  160.1 2.1 add_subtract_fusion
  162.2 2.3 %collective-permute-start.5 = (f32[8,128,128]{2,1,0:T(8,128)}, f32[8,128,128]{2,1,0:T(8,128)}, u32[]{:S(2)}, u32[]{:S(2)}) collective-permute-start(f32[8,128,128]{2,1,0:T(8,128)} %add_subtract_fusion), channel_id=1, source_target_pairs={{0,2},{2,0},{1,3},{3,1},{4,6},{6,4},{5,7},{7,5},{8,10},{10,8},{9,1... | collective-permute-start | bytes 1572872 | tf_op jit(solution)/shard_map/ppermute | solution.py:65
  165.5 1.5 copy.22
  167.0 2.8 %fusion.4 = f32[16,128,256]{2,1,0:T(8,128)} fusion(bf16[256,16,128]{0,2,1:T(8,128)(2,1)S(1)} %bitcast.47, bf16[256,16,128]{0,2,1:T(8,128)(2,1)S(1)} %bitcast.52, bf16[256,16,128]{0,2,1:T(8,128)(2,1)S(1)} %bitcast.45, pred[256,256]{1,0:T(8,128)(4,1)S(1)} %iota_compare_fusion), kind=kOutput, calls=%fused_computation.15 | convolution fusion | flops 538968064 | bytes 5308416 | tf_op jit(solution)/shard_map/hts,she->the/dot_general | solution.py:88
  169.8 1.4 broadcast_select_fusion.5
  171.7 1.8 fusion.1
  175.1 23.0 %collective-permute-done.7 = bf16[256,2048]{0,1:T(8,128)(2,1)S(1)} collective-permute-done((bf16[256,2048]{0,1:T(8,128)(2,1)S(1)}, bf16[256,2048]{0,1:T(8,128)(2,1)S(1)}, u32[]{:S(2)}, u32[]{:S(2)}) %collective-permute-start.7) | collective-permute-done | bytes 1048608 | tf_op jit(solution)/shard_map/ppermute | solution.py:99
  198.8 5.7 %fusion.18 = f32[256,2048]{1,0:T(8,128)S(1)} fusion(bf16[256,2048]{0,1:T(8,128)(2,1)S(1)} %bitcast.56, bf16[2048,2048]{1,0:T(8,128)(2,1)} %all-gather.2.cloned.1.call-done), kind=kOutput, calls=%fused_computation.48 | convolution fusion | flops 2147483648 | bytes 11534336 | tf_op jit(solution)/shard_map/dot_general | solution.py:109
  204.5 7.5 %collective-permute-done.8 = bf16[2048,2048]{1,0:T(8,128)(2,1)} collective-permute-done((bf16[2048,2048]{1,0:T(8,128)(2,1)}, bf16[2048,2048]{1,0:T(8,128)(2,1)}, u32[]{:S(2)}, u32[]{:S(2)}) %collective-permute-start.8) | collective-permute-done | bytes 8388640 | tf_op jit(solution)/shard_map/ppermute | solution.py:104
  212.1 6.7 %fusion = bf16[256,2048]{1,0:T(8,128)(2,1)} fusion(f32[256,2048]{1,0:T(8,128)S(1)} %fusion.18, bf16[256,2048]{0,1:T(8,128)(2,1)S(1)} %bitcast.55, bf16[2048,2048]{1,0:T(8,128)(2,1)} %collective-permute-done.8), kind=kOutput, calls=%fused_computation.2 | convolution fusion | flops 2148532224 | bytes 12582912 | tf_op jit(solution)/shard_map/dot_general | solution.py:110
  (35 shorter events, 14.2 us)
Async XLA Ops:
  6.5 2.4 %copy-start.3 = (bf16[128,4096]{1,0:T(8,128)(2,1)S(1)}, bf16[128,4096]{1,0:T(8,128)(2,1)}, u32[]{:S(2)}) copy-start(bf16[128,4096]{1,0:T(8,128)(2,1)} %param.7) | copy-start | bytes 3145732
  6.5 192.0 %all-gather.2.cloned.1.call-start = ((), (), s32[]{:S(2)}) async-start(), calls=%async_computation | async-start | bytes 9437184 | tf_op jit(solution)/shard_map/all_gather | solution.py:49
  9.7 24.2 %collective-permute-start = (bf16[2,128,2048]{1,2,0:T(8,128)(2,1)S(1)}, bf16[2,128,2048]{1,2,0:T(8,128)(2,1)}, u32[]{:S(2)}, u32[]{:S(2)}) collective-permute-start(bf16[2,128,2048]{1,2,0:T(8,128)(2,1)S(1)} %fusion.7), channel_id=1, source_target_pairs={{0,1},{1,0},{2,3},{3,2},{4,5},{5,4},{6,7},{7,6},{8,9},{9,8},{10,11... | collective-permute-start | bytes 3145736 | tf_op jit(solution)/shard_map/ppermute | solution.py:36
  35.9 1.6 copy-start.2
  36.0 4.0 %collective-permute-start.1 = (f32[16,128,128]{2,1,0:T(8,128)S(1)}, f32[16,128,128]{2,1,0:T(8,128)}, u32[]{:S(2)}, u32[]{:S(2)}) collective-permute-start(f32[16,128,128]{2,1,0:T(8,128)S(1)} %fusion.17), channel_id=1, source_target_pairs={{0,2},{2,0},{1,3},{3,1},{4,6},{6,4},{5,7},{7,5},{8,10},{10,8},{9,1... | collective-permute-start | bytes 3145736 | tf_op jit(solution)/shard_map/ppermute | solution.py:60
  41.2 24.2 %collective-permute-start.2 = (f32[8,128,128]{2,1,0:T(8,128)S(1)}, f32[8,128,128]{2,1,0:T(8,128)}, u32[]{:S(2)}, u32[]{:S(2)}) collective-permute-start(f32[8,128,128]{2,1,0:T(8,128)S(1)} %dynamic-slice_add_fusion), channel_id=1, source_target_pairs={{0,4},{4,8},{8,12},{12,16},{16,20},{20,24},{24,28},{1,5},{5,9},{9,... | collective-permute-start | bytes 1572872 | tf_op jit(solution)/shard_map/ppermute | solution.py:18
  46.7 23.0 %copy-start.1 = (bf16[128,4096]{0,1:T(8,128)(2,1)S(1)}, bf16[128,4096]{0,1:T(8,128)(2,1)}, u32[]{:S(2)}) copy-start(bf16[128,4096]{0,1:T(8,128)(2,1)} %copy.19) | copy-start | bytes 3145732
  66.5 36.8 %collective-permute-start.3 = (f32[8,128,128]{2,1,0:T(8,128)S(1)}, f32[8,128,128]{2,1,0:T(8,128)}, u32[]{:S(2)}, u32[]{:S(2)}) collective-permute-start(f32[8,128,128]{2,1,0:T(8,128)S(1)} %add.61), channel_id=1, source_target_pairs={{0,8},{4,12},{8,16},{12,20},{16,24},{20,28},{1,9},{5,13},{9,17},{1... | collective-permute-start | bytes 1572872 | tf_op jit(solution)/shard_map/ppermute | solution.py:18
  72.9 35.7 %collective-permute-start.6 = (bf16[1,128,2048]{2,1,0:T(8,128)(2,1)}, bf16[1,128,2048]{2,1,0:T(8,128)(2,1)}, u32[]{:S(2)}, u32[]{:S(2)}) collective-permute-start(bf16[1,128,2048]{2,1,0:T(8,128)(2,1)} %bitcast.59), channel_id=1, source_target_pairs={{0,1},{1,0},{2,3},{3,2},{4,5},{5,4},{6,7},{7,6},{8,9},{9,8},{10,11... | collective-permute-start | bytes 1572872 | tf_op jit(solution)/shard_map/ppermute | solution.py:36
  105.2 54.8 %collective-permute-start.4 = (f32[8,128,128]{2,1,0:T(8,128)}, f32[8,128,128]{2,1,0:T(8,128)}, u32[]{:S(2)}, u32[]{:S(2)}) collective-permute-start(f32[8,128,128]{2,1,0:T(8,128)} %add.62), channel_id=1, source_target_pairs={{0,16},{4,20},{8,24},{12,28},{1,17},{5,21},{9,25},{13,29},{2,18},{... | collective-permute-start | bytes 1572872 | tf_op jit(solution)/shard_map/ppermute | solution.py:18
  162.2 7.6 %collective-permute-start.5 = (f32[8,128,128]{2,1,0:T(8,128)}, f32[8,128,128]{2,1,0:T(8,128)}, u32[]{:S(2)}, u32[]{:S(2)}) collective-permute-start(f32[8,128,128]{2,1,0:T(8,128)} %add_subtract_fusion), channel_id=1, source_target_pairs={{0,2},{2,0},{1,3},{3,1},{4,6},{6,4},{5,7},{7,5},{8,10},{10,8},{9,1... | collective-permute-start | bytes 1572872 | tf_op jit(solution)/shard_map/ppermute | solution.py:65
  169.8 1.9 copy-start
  171.7 1.8 copy-start.4
  173.9 24.2 %collective-permute-start.7 = (bf16[256,2048]{0,1:T(8,128)(2,1)S(1)}, bf16[256,2048]{0,1:T(8,128)(2,1)S(1)}, u32[]{:S(2)}, u32[]{:S(2)}) collective-permute-start(bf16[256,2048]{0,1:T(8,128)(2,1)S(1)} %bitcast.57), channel_id=1, source_target_pairs={{0,1},{1,0},{2,3},{3,2},{4,5},{5,4},{6,7},{7,6},{8,9},{9,8},{10,11... | collective-permute-start | bytes 3145736 | tf_op jit(solution)/shard_map/ppermute | solution.py:99
  198.5 13.6 %collective-permute-start.8 = (bf16[2048,2048]{1,0:T(8,128)(2,1)}, bf16[2048,2048]{1,0:T(8,128)(2,1)}, u32[]{:S(2)}, u32[]{:S(2)}) collective-permute-start(bf16[2048,2048]{1,0:T(8,128)(2,1)} %all-gather.2.cloned.1.call-done), channel_id=1, source_target_pairs={{0,2},{2,0},{1,3},{3,1},{4,6},{6,4},{5,7},{7,5},{8,10},{10,8},{9,1... | collective-permute-start | bytes 25165832 | tf_op jit(solution)/shard_map/ppermute | solution.py:104
Sparse Core Ops, SparseCore 0:
  9.5 161.4 all-gather.1

commit v4 on v2

--- a/solution.py
+++ b/solution.py
@@ -41,13 +41,60 @@
     ]
 
 
-def local(queries, keys, values, out_weight, norm_gain, n_chip, n_head):
+def chip_cycle(devices):
+    n = devices.shape[0]
+    coords = [getattr(devices[j, 0, 0], "coords", None) for j in range(n)]
+    if n > 16 or any(c is None for c in coords):
+        return None
+
+    def adjacent(a, b):
+        return sum(abs(int(u) - int(v)) for u, v in zip(coords[a], coords[b])) == 1
+
+    path = [0]
+
+    def search():
+        if len(path) == n:
+            return adjacent(path[-1], path[0])
+        for k in range(n):
+            if k not in path and adjacent(path[-1], k):
+                path.append(k)
+                if search():
+                    return True
+                path.pop()
+        return False
+
+    return list(path) if search() else None
+
+
+def ring_gather(block, order):
+    n = len(order)
+    forward = [(order[i], order[(i + 1) % n]) for i in range(n)]
+    backward = [(order[(i + 1) % n], order[i]) for i in range(n)]
+    half_rows = block.shape[0] // 2
+    got, offsets = [block], [0]
+    ahead, behind = block, block
+    for step in range(1, n // 2):
+        ahead = lax.ppermute(ahead, "chip", forward)
+        behind = lax.ppermute(behind, "chip", backward)
+        got += [ahead, behind]
+        offsets += [step, -step]
+    last_ahead = lax.ppermute(ahead[:half_rows], "chip", forward)
+    last_behind = lax.ppermute(behind[half_rows:], "chip", backward)
+    got.append(jnp.concatenate([last_ahead, last_behind], 0))
+    offsets.append(n // 2)
+    return got, offsets
+
+
+def local(queries, keys, values, out_weight, norm_gain, n_chip, n_head, order):
     heads_dev = norm_gain.shape[0] // HEAD_DIM
     width = heads_dev * HEAD_DIM
     core = lax.axis_index("core")
     place = lax.axis_index("head") if n_head == 2 else 0
-    weight_own = lax.all_gather(out_weight, "chip", axis=0, tiled=True)
-    weight_other = lax.ppermute(weight_own, "core", SWAP)
+    if order is None:
+        weight_own, offsets = [lax.all_gather(out_weight, "chip", axis=0, tiled=True)], [0]
+    else:
+        weight_own, offsets = ring_gather(out_weight, order)
+        weight_other = [lax.ppermute(w, "core", SWAP) for w in weight_own]
 
     key_block, value_block = head_blocks([keys, values], n_head, place)
     (query_block,) = head_blocks([queries], n_head, place)
@@ -103,10 +150,24 @@
         gathered = lax.all_gather(normed, "head", axis=1, tiled=True)
     weight_rows = out_weight.shape[0]
     split = gathered.reshape(row_count, n_chip, 2, weight_rows)
-    normed_own = lax.dynamic_index_in_dim(split, core, 2, False).reshape(row_count, -1)
-    normed_other = lax.dynamic_index_in_dim(split, 1 - core, 2, False).reshape(row_count, -1)
-    outcome = jnp.dot(normed_own, weight_own, preferred_element_type=jnp.float32)
-    outcome = outcome + jnp.dot(normed_other, weight_other, preferred_element_type=jnp.float32)
+    if order is None:
+        weight_own, split = lax.optimization_barrier((weight_own[0], split))
+        weight_other = lax.ppermute(weight_own, "core", SWAP)
+        normed_own = lax.dynamic_index_in_dim(split, core, 2, False).reshape(row_count, -1)
+        normed_other = lax.dynamic_index_in_dim(split, 1 - core, 2, False).reshape(row_count, -1)
+        outcome = jnp.dot(normed_own, weight_own, preferred_element_type=jnp.float32)
+        outcome = outcome + jnp.dot(normed_other, weight_other, preferred_element_type=jnp.float32)
+        return outcome.astype(jnp.bfloat16)
+    ring_place = jnp.asarray([order.index(j) for j in range(n_chip)], jnp.int32)[lax.axis_index("chip")]
+    sources = jnp.asarray(order, jnp.int32)[(ring_place - jnp.asarray(offsets, jnp.int32)) % n_chip]
+    by_offset = jnp.take(split, sources, axis=1)
+    normed_own = lax.dynamic_index_in_dim(by_offset, core, 2, False)
+    normed_other = lax.dynamic_index_in_dim(by_offset, 1 - core, 2, False)
+    outcome = None
+    for i in range(len(offsets)):
+        part = jnp.dot(normed_own[:, i], weight_own[i], preferred_element_type=jnp.float32)
+        part = part + jnp.dot(normed_other[:, i], weight_other[i], preferred_element_type=jnp.float32)
+        outcome = part if outcome is None else outcome + part
     return outcome.astype(jnp.bfloat16)
 
 
@@ -115,7 +176,8 @@
     n_head = mesh.shape["head"]
     fine = Mesh(mesh.devices.reshape(n_seq // 2, 2, n_head), ("chip", "core", "head"))
     rows = ("chip", "core", "head")
-    body = functools.partial(local, n_chip=n_seq // 2, n_head=n_head)
+    order = chip_cycle(fine.devices)
+    body = functools.partial(local, n_chip=n_seq // 2, n_head=n_head, order=order)
     return jax.shard_map(
         body,
         mesh=fine,

time: 268 us -> 208 us (0.78)
  waiting for transfers between devices: 188 us -> 113 us
  starting transfers between devices: 18.7 us -> 34.6 us
  between operations: 13.6 us -> 0.47 us
  matrix products: 17.4 us -> 27.1 us
  local copies, waits for them, and re-layouts: 11.9 us -> 17.2 us
    all_gather x1 -> x0, waiting for transfers between devices: 96.3 us -> none  [local(): weight_own = lax.all_gather(out_weight, 'chip', axis=0, tiled=True)]
    ppermute x1 -> x16, waiting for transfers between devices: 0.01 us -> 39.2 us  [the longest x3 31.4 us: ring_gather(): ahead = lax.ppermute(ahead, 'chip', forward)]
    ppermute x1, waiting for transfers between devices: 22.9 us -> 0.01 us  [local(): other = lax.ppermute(normed, 'head', SWAP)]
    ppermute x1 -> x16, starting transfers between devices: 0.9 us -> 17.2 us  [the longest x8 9.51 us: local(): weight_other = [lax.ppermute(w, 'core', SWAP) for w in weight_own]]
    ppermute x3, waiting for transfers between devices: 34 us -> 48.4 us  [exclusive_prefix(): total = total + lax.ppermute(total, axis, pairs)]
    dot_general x2 -> x16, matrix products: 12.4 us -> 22.1 us  [the longest x8 11.1 us: local(): jnp.dot(normed_other[:, i], weight_other[i], preferred_element_type=jnp.f...]
    ppermute x1, waiting for transfers between devices: 11.6 us -> 2.42 us  [local(): partner_state = lax.ppermute(kv_state, 'core', SWAP)]
    gather x0 -> x2, local copies, waits for them, and re-layouts: none -> 2.69 us  [the longest x1 2.05 us: local(): by_offset = jnp.take(split, sources, axis=1)]
  transfers between devices with their start and end apart: 10 -> 24, of which waited for: 7 -> 9; matrix products, arithmetic and copies ran while one was open for 14% -> 25% of each run, Pallas kernels for 0% -> 0%
where the time goes in v4:
time: 208 us; the launch traced here: 207 us
  waiting for transfers between devices  113 us (54%)
  starting transfers between devices  34.6 us (17%)
  matrix products  27.1 us (13%)
  local copies, waits for them, and re-layouts  17.2 us (8%)
  other arithmetic  14.8 us (7%)
    ppermute x3, waiting for transfers between devices, exclusive_prefix(): total = total + lax.ppermute(total, axis, pairs)  48.4 us
    ppermute x3, waiting for transfers between devices, ring_gather(): ahead = lax.ppermute(ahead, 'chip', forward)  31.4 us
    ppermute x2, waiting for transfers between devices, head_blocks(): other = lax.ppermute(sent, 'head', SWAP)  22.9 us
    ppermute x3, starting transfers between devices, exclusive_prefix(): total = total + lax.ppermute(total, axis, pairs)  11.4 us
    dot_general x8, matrix products, local(): jnp.dot(normed_other[:, i], weight_other[i], preferred_element_type=jnp.f...  11.1 us
    dot_general x8, matrix products, local(): jnp.dot(normed_own[:, i], weight_own[i], preferred_element_type=jnp.float32)  11 us
    ppermute x8, starting transfers between devices, local(): weight_other = [lax.ppermute(w, 'core', SWAP) for w in weight_own]  9.51 us
    ppermute x1, waiting for transfers between devices, ring_gather(): last_ahead = lax.ppermute(ahead[:half_rows], 'chip', forward)  6.83 us
  transfers between devices with their start and end apart: 24, of which 9 were waited for; matrix products, arithmetic and copies ran while one was open for 25% of the time, Pallas kernels for 0%

profile of v4, /device:TPU:13, one launch (start us, length us, event | category | flops | bytes accessed | tf_op | source)
XLA Modules:
  0.0 207.2 jit_solution(15580276531097984589)
XLA Ops:
  3.8 22.9 %collective-permute-done = bf16[2,128,2048]{1,2,0:T(8,128)(2,1)} collective-permute-done((bf16[2,128,2048]{1,2,0:T(8,128)(2,1)S(1)}, bf16[2,128,2048]{1,2,0:T(8,128)(2,1)}, u32[]{:S(2)}, u32[]{:S(2)}) %collective-permute-start) | collective-permute-done | bytes 1048608 | tf_op jit(solution)/shard_map/ppermute | solution.py:36
  30.4 2.4 %collective-permute-done.1 = f32[16,128,128]{2,1,0:T(8,128)} collective-permute-done((f32[16,128,128]{2,1,0:T(8,128)S(1)}, f32[16,128,128]{2,1,0:T(8,128)}, u32[]{:S(2)}, u32[]{:S(2)}) %collective-permute-start.1) | collective-permute-done | bytes 1048608 | tf_op jit(solution)/shard_map/ppermute | solution.py:108
  34.0 3.2 %collective-permute-start.2 = (f32[8,128,128]{2,1,0:T(8,128)S(1)}, f32[8,128,128]{2,1,0:T(8,128)}, u32[]{:S(2)}, u32[]{:S(2)}) collective-permute-start(f32[8,128,128]{2,1,0:T(8,128)S(1)} %dynamic-slice_add_fusion), channel_id=1, source_target_pairs={{0,4},{4,8},{8,12},{12,16},{16,20},{20,24},{24,28},{1,5},{5,9},{9,... | collective-permute-start | bytes 1572872 | tf_op jit(solution)/shard_map/ppermute | solution.py:18
  38.7 2.3 %copy.22 = bf16[128,4096]{0,1:T(8,128)(2,1)} copy(bf16[128,4096]{1,0:T(8,128)(2,1)} %param.8) | data formatting | bytes 2097152 | tf_op args[0]
  41.0 8.2 %collective-permute-done.2 = f32[8,128,128]{2,1,0:T(8,128)} collective-permute-done((f32[8,128,128]{2,1,0:T(8,128)S(1)}, f32[8,128,128]{2,1,0:T(8,128)}, u32[]{:S(2)}, u32[]{:S(2)}) %collective-permute-start.2) | collective-permute-done | bytes 524320 | tf_op jit(solution)/shard_map/ppermute | solution.py:18
  50.3 3.2 %collective-permute-start.3 = (f32[8,128,128]{2,1,0:T(8,128)S(1)}, f32[8,128,128]{2,1,0:T(8,128)}, u32[]{:S(2)}, u32[]{:S(2)}) collective-permute-start(f32[8,128,128]{2,1,0:T(8,128)S(1)} %add.134), channel_id=1, source_target_pairs={{0,8},{4,12},{8,16},{12,20},{16,24},{20,28},{1,9},{5,13},{9,17},{1... | collective-permute-start | bytes 1572872 | tf_op jit(solution)/shard_map/ppermute | solution.py:18
  54.6 2.0 copy.24
  60.9 21.9 %collective-permute-done.3 = f32[8,128,128]{2,1,0:T(8,128)} collective-permute-done((f32[8,128,128]{2,1,0:T(8,128)S(1)}, f32[8,128,128]{2,1,0:T(8,128)}, u32[]{:S(2)}, u32[]{:S(2)}) %collective-permute-start.3) | collective-permute-done | bytes 524320 | tf_op jit(solution)/shard_map/ppermute | solution.py:18
  82.8 1.9 add.135
  84.7 5.1 %collective-permute-start.4 = (f32[8,128,128]{2,1,0:T(8,128)}, f32[8,128,128]{2,1,0:T(8,128)}, u32[]{:S(2)}, u32[]{:S(2)}) collective-permute-start(f32[8,128,128]{2,1,0:T(8,128)} %add.135), channel_id=1, source_target_pairs={{0,16},{4,20},{8,24},{12,28},{1,17},{5,21},{9,25},{13,29},{2,18},{... | collective-permute-start | bytes 1572872 | tf_op jit(solution)/shard_map/ppermute | solution.py:18
  93.7 18.3 %collective-permute-done.4 = f32[8,128,128]{2,1,0:T(8,128)} collective-permute-done((f32[8,128,128]{2,1,0:T(8,128)}, f32[8,128,128]{2,1,0:T(8,128)}, u32[]{:S(2)}, u32[]{:S(2)}) %collective-permute-start.4) | collective-permute-done | bytes 524320 | tf_op jit(solution)/shard_map/ppermute | solution.py:18
  112.0 2.1 add_subtract_fusion
  117.3 2.7 %fusion.11 = f32[16,128,256]{2,1,0:T(8,128)} fusion(bf16[256,16,128]{0,2,1:T(8,128)(2,1)S(1)} %bitcast.118, bf16[256,16,128]{0,2,1:T(8,128)(2,1)S(1)} %bitcast.123, bf16[256,16,128]{0,2,1:T(8,128)(2,1)S(1)} %bitcast.116, pred[256,256]{1,0:T(8,128)(4,1)S(1)} %iota_compare_fusion), kind=kOutput, calls=%fused_computation.32 | convolution fusion | flops 538968064 | bytes 5308416 | tf_op jit(solution)/shard_map/hts,she->the/dot_general | solution.py:136
  120.0 14.5 %collective-permute-done.13 = bf16[256,2048]{1,0:T(8,128)(2,1)} collective-permute-done((bf16[256,2048]{1,0:T(8,128)(2,1)}, bf16[256,2048]{1,0:T(8,128)(2,1)}, u32[]{:S(2)}, u32[]{:S(2)}) %collective-permute-start.13) | collective-permute-done | bytes 1048608 | tf_op jit(solution)/shard_map/ppermute | solution.py:77
  134.5 2.2 %collective-permute-start.17 = (bf16[256,2048]{1,0:T(8,128)(2,1)}, bf16[256,2048]{1,0:T(8,128)(2,1)}, u32[]{:S(2)}, u32[]{:S(2)}) collective-permute-start(bf16[256,2048]{1,0:T(8,128)(2,1)} %collective-permute-done.13), channel_id=1, source_target_pairs={{0,4},{4,12},{12,20},{20,28},{28,24},{24,16},{16,8},{8,0},{1,5},{5... | collective-permute-start | bytes 3145736 | tf_op jit(solution)/shard_map/ppermute | solution.py:77
  138.1 1.8 fusion.8
  142.2 16.9 %collective-permute-done.17 = bf16[256,2048]{1,0:T(8,128)(2,1)} collective-permute-done((bf16[256,2048]{1,0:T(8,128)(2,1)}, bf16[256,2048]{1,0:T(8,128)(2,1)}, u32[]{:S(2)}, u32[]{:S(2)}) %collective-permute-start.17) | collective-permute-done | bytes 1048608 | tf_op jit(solution)/shard_map/ppermute | solution.py:77
  160.1 2.3 %collective-permute-start.21 = (bf16[128,2048]{1,0:T(8,128)(2,1)S(1)}, bf16[128,2048]{1,0:T(8,128)(2,1)S(1)}, u32[]{:S(2)}, u32[]{:S(2)}) collective-permute-start(bf16[128,2048]{1,0:T(8,128)(2,1)S(1)} %slice.101), channel_id=1, source_target_pairs={{0,4},{4,12},{12,20},{20,28},{28,24},{24,16},{16,8},{8,0},{1,5},{5... | collective-permute-start | bytes 1572872 | tf_op jit(solution)/shard_map/ppermute | solution.py:81
  165.4 6.8 %collective-permute-done.21 = bf16[128,2048]{1,0:T(8,128)(2,1)S(1)} collective-permute-done((bf16[128,2048]{1,0:T(8,128)(2,1)S(1)}, bf16[128,2048]{1,0:T(8,128)(2,1)S(1)}, u32[]{:S(2)}, u32[]{:S(2)}) %collective-permute-start.21) | collective-permute-done | bytes 524320 | tf_op jit(solution)/shard_map/ppermute | solution.py:81
  172.3 2.3 %collective-permute-start.12 = (bf16[256,2048]{1,0:T(8,128)(2,1)}, bf16[256,2048]{1,0:T(8,128)(2,1)}, u32[]{:S(2)}, u32[]{:S(2)}) collective-permute-start(bf16[256,2048]{1,0:T(8,128)(2,1)} %collective-permute-done.11), channel_id=1, source_target_pairs={{0,2},{2,0},{1,3},{3,1},{4,6},{6,4},{5,7},{7,5},{8,10},{10,8},{9,1... | collective-permute-start | bytes 3145736 | tf_op jit(solution)/shard_map/ppermute | solution.py:97
  175.5 2.5 %collective-permute-start.14 = (bf16[256,2048]{1,0:T(8,128)(2,1)}, bf16[256,2048]{1,0:T(8,128)(2,1)}, u32[]{:S(2)}, u32[]{:S(2)}) collective-permute-start(bf16[256,2048]{1,0:T(8,128)(2,1)} %collective-permute-done.13), channel_id=1, source_target_pairs={{0,2},{2,0},{1,3},{3,1},{4,6},{6,4},{5,7},{7,5},{8,10},{10,8},{9,1... | collective-permute-start | bytes 3145736 | tf_op jit(solution)/shard_map/ppermute | solution.py:97
  178.6 2.0 gather_fusion.1
  180.6 1.9 broadcast_select_fusion
  196.1 1.8 fusion.4
  (97 shorter events, 55.6 us)
Async XLA Ops:
  2.5 24.2 %collective-permute-start = (bf16[2,128,2048]{1,2,0:T(8,128)(2,1)S(1)}, bf16[2,128,2048]{1,2,0:T(8,128)(2,1)}, u32[]{:S(2)}, u32[]{:S(2)}) collective-permute-start(bf16[2,128,2048]{1,2,0:T(8,128)(2,1)S(1)} %fusion.14), channel_id=1, source_target_pairs={{0,1},{1,0},{2,3},{3,2},{4,5},{5,4},{6,7},{7,6},{8,9},{9,8},{10,11... | collective-permute-start | bytes 3145736 | tf_op jit(solution)/shard_map/ppermute | solution.py:36
  28.8 4.0 %collective-permute-start.1 = (f32[16,128,128]{2,1,0:T(8,128)S(1)}, f32[16,128,128]{2,1,0:T(8,128)}, u32[]{:S(2)}, u32[]{:S(2)}) collective-permute-start(f32[16,128,128]{2,1,0:T(8,128)S(1)} %fusion.34), channel_id=1, source_target_pairs={{0,2},{2,0},{1,3},{3,1},{4,6},{6,4},{5,7},{7,5},{8,10},{10,8},{9,1... | collective-permute-start | bytes 3145736 | tf_op jit(solution)/shard_map/ppermute | solution.py:108
  34.0 15.1 %collective-permute-start.2 = (f32[8,128,128]{2,1,0:T(8,128)S(1)}, f32[8,128,128]{2,1,0:T(8,128)}, u32[]{:S(2)}, u32[]{:S(2)}) collective-permute-start(f32[8,128,128]{2,1,0:T(8,128)S(1)} %dynamic-slice_add_fusion), channel_id=1, source_target_pairs={{0,4},{4,8},{8,12},{12,16},{16,20},{20,24},{24,28},{1,5},{5,9},{9,... | collective-permute-start | bytes 1572872 | tf_op jit(solution)/shard_map/ppermute | solution.py:18
  37.2 53.9 %collective-permute-start.9 = (bf16[256,2048]{1,0:T(8,128)(2,1)}, bf16[256,2048]{1,0:T(8,128)(2,1)}, u32[]{:S(2)}, u32[]{:S(2)}) collective-permute-start(bf16[256,2048]{1,0:T(8,128)(2,1)} %param.11), channel_id=1, source_target_pairs={{0,4},{4,12},{12,20},{20,28},{28,24},{24,16},{16,8},{8,0},{1,5},{5... | collective-permute-start | bytes 3145736 | tf_op jit(solution)/shard_map/ppermute | solution.py:77
  38.6 52.6 %collective-permute-start.11 = (bf16[256,2048]{1,0:T(8,128)(2,1)}, bf16[256,2048]{1,0:T(8,128)(2,1)}, u32[]{:S(2)}, u32[]{:S(2)}) collective-permute-start(bf16[256,2048]{1,0:T(8,128)(2,1)} %param.11), channel_id=1, source_target_pairs={{4,0},{12,4},{20,12},{28,20},{24,28},{16,24},{8,16},{0,8},{5,1},{1... | collective-permute-start | bytes 3145736 | tf_op jit(solution)/shard_map/ppermute | solution.py:78
  50.3 32.6 %collective-permute-start.3 = (f32[8,128,128]{2,1,0:T(8,128)S(1)}, f32[8,128,128]{2,1,0:T(8,128)}, u32[]{:S(2)}, u32[]{:S(2)}) collective-permute-start(f32[8,128,128]{2,1,0:T(8,128)S(1)} %add.134), channel_id=1, source_target_pairs={{0,8},{4,12},{8,16},{12,20},{16,24},{20,28},{1,9},{5,13},{9,17},{1... | collective-permute-start | bytes 1572872 | tf_op jit(solution)/shard_map/ppermute | solution.py:18
  56.6 36.0 %collective-permute-start.6 = (bf16[1,128,2048]{2,1,0:T(8,128)(2,1)}, bf16[1,128,2048]{2,1,0:T(8,128)(2,1)}, u32[]{:S(2)}, u32[]{:S(2)}) collective-permute-start(bf16[1,128,2048]{2,1,0:T(8,128)(2,1)} %bitcast.128), channel_id=1, source_target_pairs={{0,1},{1,0},{2,3},{3,2},{4,5},{5,4},{6,7},{7,6},{8,9},{9,8},{10,11... | collective-permute-start | bytes 1572872 | tf_op jit(solution)/shard_map/ppermute | solution.py:36
  57.8 126.3 %collective-permute-start.8 = (bf16[256,2048]{1,0:T(8,128)(2,1)}, bf16[256,2048]{1,0:T(8,128)(2,1)}, u32[]{:S(2)}, u32[]{:S(2)}) collective-permute-start(bf16[256,2048]{1,0:T(8,128)(2,1)} %param.11), channel_id=1, source_target_pairs={{0,2},{2,0},{1,3},{3,1},{4,6},{6,4},{5,7},{7,5},{8,10},{10,8},{9,1... | collective-permute-start | bytes 3145736 | tf_op jit(solution)/shard_map/ppermute | solution.py:97
  84.7 27.3 %collective-permute-start.4 = (f32[8,128,128]{2,1,0:T(8,128)}, f32[8,128,128]{2,1,0:T(8,128)}, u32[]{:S(2)}, u32[]{:S(2)}) collective-permute-start(f32[8,128,128]{2,1,0:T(8,128)} %add.135), channel_id=1, source_target_pairs={{0,16},{4,20},{8,24},{12,28},{1,17},{5,21},{9,25},{13,29},{2,18},{... | collective-permute-start | bytes 1572872 | tf_op jit(solution)/shard_map/ppermute | solution.py:18
  91.1 43.4 %collective-permute-start.13 = (bf16[256,2048]{1,0:T(8,128)(2,1)}, bf16[256,2048]{1,0:T(8,128)(2,1)}, u32[]{:S(2)}, u32[]{:S(2)}) collective-permute-start(bf16[256,2048]{1,0:T(8,128)(2,1)} %collective-permute-done.9), channel_id=1, source_target_pairs={{0,4},{4,12},{12,20},{20,28},{28,24},{24,16},{16,8},{8,0},{1,5},{5... | collective-permute-start | bytes 3145736 | tf_op jit(solution)/shard_map/ppermute | solution.py:77
  91.2 45.6 %collective-permute-start.15 = (bf16[256,2048]{1,0:T(8,128)(2,1)}, bf16[256,2048]{1,0:T(8,128)(2,1)}, u32[]{:S(2)}, u32[]{:S(2)}) collective-permute-start(bf16[256,2048]{1,0:T(8,128)(2,1)} %collective-permute-done.11), channel_id=1, source_target_pairs={{4,0},{12,4},{20,12},{28,20},{24,28},{16,24},{8,16},{0,8},{5,1},{1... | collective-permute-start | bytes 3145736 | tf_op jit(solution)/shard_map/ppermute | solution.py:78
  114.1 22.6 %collective-permute-start.5 = (f32[8,128,128]{2,1,0:T(8,128)}, f32[8,128,128]{2,1,0:T(8,128)}, u32[]{:S(2)}, u32[]{:S(2)}) collective-permute-start(f32[8,128,128]{2,1,0:T(8,128)} %add_subtract_fusion), channel_id=1, source_target_pairs={{0,2},{2,0},{1,3},{3,1},{4,6},{6,4},{5,7},{7,5},{8,10},{10,8},{9,1... | collective-permute-start | bytes 1572872 | tf_op jit(solution)/shard_map/ppermute | solution.py:113
  134.5 24.6 %collective-permute-start.17 = (bf16[256,2048]{1,0:T(8,128)(2,1)}, bf16[256,2048]{1,0:T(8,128)(2,1)}, u32[]{:S(2)}, u32[]{:S(2)}) collective-permute-start(bf16[256,2048]{1,0:T(8,128)(2,1)} %collective-permute-done.13), channel_id=1, source_target_pairs={{0,4},{4,12},{12,20},{20,28},{28,24},{24,16},{16,8},{8,0},{1,5},{5... | collective-permute-start | bytes 3145736 | tf_op jit(solution)/shard_map/ppermute | solution.py:77
  136.7 25.7 %collective-permute-start.19 = (bf16[256,2048]{1,0:T(8,128)(2,1)}, bf16[256,2048]{1,0:T(8,128)(2,1)}, u32[]{:S(2)}, u32[]{:S(2)}) collective-permute-start(bf16[256,2048]{1,0:T(8,128)(2,1)} %collective-permute-done.15), channel_id=1, source_target_pairs={{4,0},{12,4},{20,12},{28,20},{24,28},{16,24},{8,16},{0,8},{5,1},{1... | collective-permute-start | bytes 3145736 | tf_op jit(solution)/shard_map/ppermute | solution.py:78
  140.3 37.8 %collective-permute-start.7 = (bf16[256,2048]{0,1:T(8,128)(2,1)S(1)}, bf16[256,2048]{0,1:T(8,128)(2,1)S(1)}, u32[]{:S(2)}, u32[]{:S(2)}) collective-permute-start(bf16[256,2048]{0,1:T(8,128)(2,1)S(1)} %bitcast.126), channel_id=1, source_target_pairs={{0,1},{1,0},{2,3},{3,2},{4,5},{5,4},{6,7},{7,6},{8,9},{9,8},{10,11... | collective-permute-start | bytes 3145736 | tf_op jit(solution)/shard_map/ppermute | solution.py:147
  160.1 12.1 %collective-permute-start.21 = (bf16[128,2048]{1,0:T(8,128)(2,1)S(1)}, bf16[128,2048]{1,0:T(8,128)(2,1)S(1)}, u32[]{:S(2)}, u32[]{:S(2)}) collective-permute-start(bf16[128,2048]{1,0:T(8,128)(2,1)S(1)} %slice.101), channel_id=1, source_target_pairs={{0,4},{4,12},{12,20},{20,28},{28,24},{24,16},{16,8},{8,0},{1,5},{5... | collective-permute-start | bytes 1572872 | tf_op jit(solution)/shard_map/ppermute | solution.py:81
  163.5 12.0 %collective-permute-start.22 = (bf16[128,2048]{1,0:T(8,128)(2,1)S(1)}, bf16[128,2048]{1,0:T(8,128)(2,1)S(1)}, u32[]{:S(2)}, u32[]{:S(2)}) collective-permute-start(bf16[128,2048]{1,0:T(8,128)(2,1)S(1)} %slice.102), channel_id=1, source_target_pairs={{4,0},{12,4},{20,12},{28,20},{24,28},{16,24},{8,16},{0,8},{5,1},{1... | collective-permute-start | bytes 1572872 | tf_op jit(solution)/shard_map/ppermute | solution.py:82
  163.8 28.3 %collective-permute-start.10 = (bf16[256,2048]{1,0:T(8,128)(2,1)}, bf16[256,2048]{1,0:T(8,128)(2,1)}, u32[]{:S(2)}, u32[]{:S(2)}) collective-permute-start(bf16[256,2048]{1,0:T(8,128)(2,1)} %collective-permute-done.9), channel_id=1, source_target_pairs={{0,2},{2,0},{1,3},{3,1},{4,6},{6,4},{5,7},{7,5},{8,10},{10,8},{9,1... | collective-permute-start | bytes 3145736 | tf_op jit(solution)/shard_map/ppermute | solution.py:97
  172.3 22.0 %collective-permute-start.12 = (bf16[256,2048]{1,0:T(8,128)(2,1)}, bf16[256,2048]{1,0:T(8,128)(2,1)}, u32[]{:S(2)}, u32[]{:S(2)}) collective-permute-start(bf16[256,2048]{1,0:T(8,128)(2,1)} %collective-permute-done.11), channel_id=1, source_target_pairs={{0,2},{2,0},{1,3},{3,1},{4,6},{6,4},{5,7},{7,5},{8,10},{10,8},{9,1... | collective-permute-start | bytes 3145736 | tf_op jit(solution)/shard_map/ppermute | solution.py:97
  175.5 20.5 %collective-permute-start.14 = (bf16[256,2048]{1,0:T(8,128)(2,1)}, bf16[256,2048]{1,0:T(8,128)(2,1)}, u32[]{:S(2)}, u32[]{:S(2)}) collective-permute-start(bf16[256,2048]{1,0:T(8,128)(2,1)} %collective-permute-done.13), channel_id=1, source_target_pairs={{0,2},{2,0},{1,3},{3,1},{4,6},{6,4},{5,7},{7,5},{8,10},{10,8},{9,1... | collective-permute-start | bytes 3145736 | tf_op jit(solution)/shard_map/ppermute | solution.py:97
  178.1 25.3 %collective-permute-start.16 = (bf16[256,2048]{1,0:T(8,128)(2,1)}, bf16[256,2048]{1,0:T(8,128)(2,1)}, u32[]{:S(2)}, u32[]{:S(2)}) collective-permute-start(bf16[256,2048]{1,0:T(8,128)(2,1)} %collective-permute-done.15), channel_id=1, source_target_pairs={{0,2},{2,0},{1,3},{3,1},{4,6},{6,4},{5,7},{7,5},{8,10},{10,8},{9,1... | collective-permute-start | bytes 3145736 | tf_op jit(solution)/shard_map/ppermute | solution.py:97
  184.2 7.3 %collective-permute-start.23 = (bf16[256,2048]{1,0:T(8,128)(2,1)S(1)}, bf16[256,2048]{1,0:T(8,128)(2,1)S(1)}, u32[]{:S(2)}, u32[]{:S(2)}) collective-permute-start(bf16[256,2048]{1,0:T(8,128)(2,1)S(1)} %constant_dynamic-update-slice_fusion), channel_id=1, source_target_pairs={{0,2},{2,0},{1,3},{3,1},{4,6},{6,4},{5,7},{7,5},{8,10},{10,8},{9,1... | collective-permute-start | bytes 3145736 | tf_op jit(solution)/shard_map/ppermute | solution.py:97
  191.5 13.6 %collective-permute-start.18 = (bf16[256,2048]{1,0:T(8,128)(2,1)}, bf16[256,2048]{1,0:T(8,128)(2,1)S(1)}, u32[]{:S(2)}, u32[]{:S(2)}) collective-permute-start(bf16[256,2048]{1,0:T(8,128)(2,1)} %collective-permute-done.17), channel_id=1, source_target_pairs={{0,2},{2,0},{1,3},{3,1},{4,6},{6,4},{5,7},{7,5},{8,10},{10,8},{9,1... | collective-permute-start | bytes 3145736 | tf_op jit(solution)/shard_map/ppermute | solution.py:97
  192.0 13.6 %collective-permute-start.20 = (bf16[256,2048]{1,0:T(8,128)(2,1)}, bf16[256,2048]{1,0:T(8,128)(2,1)S(1)}, u32[]{:S(2)}, u32[]{:S(2)}) collective-permute-start(bf16[256,2048]{1,0:T(8,128)(2,1)} %collective-permute-done.19), channel_id=1, source_target_pairs={{0,2},{2,0},{1,3},{3,1},{4,6},{6,4},{5,7},{7,5},{8,10},{10,8},{9,1... | collective-permute-start | bytes 3145736 | tf_op jit(solution)/shard_map/ppermute | solution.py:97
  (9 other events, 76.5 us)

commit v5 on v4

--- a/solution.py
+++ b/solution.py
@@ -66,23 +66,21 @@
     return list(path) if search() else None
 
 
-def ring_gather(block, order):
+def ring_links(order):
     n = len(order)
     forward = [(order[i], order[(i + 1) % n]) for i in range(n)]
     backward = [(order[(i + 1) % n], order[i]) for i in range(n)]
-    half_rows = block.shape[0] // 2
-    got, offsets = [block], [0]
-    ahead, behind = block, block
-    for step in range(1, n // 2):
-        ahead = lax.ppermute(ahead, "chip", forward)
-        behind = lax.ppermute(behind, "chip", backward)
-        got += [ahead, behind]
-        offsets += [step, -step]
-    last_ahead = lax.ppermute(ahead[:half_rows], "chip", forward)
-    last_behind = lax.ppermute(behind[half_rows:], "chip", backward)
-    got.append(jnp.concatenate([last_ahead, last_behind], 0))
-    offsets.append(n // 2)
-    return got, offsets
+    return forward, backward
+
+
+def ring_step(ahead, behind, order, last=False):
+    forward, backward = ring_links(order)
+    if last:
+        half_rows = ahead.shape[0] // 2
+        return lax.ppermute(ahead[:half_rows], "chip", forward), lax.ppermute(
+            behind[half_rows:], "chip", backward
+        )
+    return lax.ppermute(ahead, "chip", forward), lax.ppermute(behind, "chip", backward)
 
 
 def local(queries, keys, values, out_weight, norm_gain, n_chip, n_head, order):
@@ -90,13 +88,14 @@
     width = heads_dev * HEAD_DIM
     core = lax.axis_index("core")
     place = lax.axis_index("head") if n_head == 2 else 0
+    key_block, value_block = head_blocks([keys, values], n_head, place)
     if order is None:
         weight_own, offsets = [lax.all_gather(out_weight, "chip", axis=0, tiled=True)], [0]
     else:
-        weight_own, offsets = ring_gather(out_weight, order)
-        weight_other = [lax.ppermute(w, "core", SWAP) for w in weight_own]
-
-    key_block, value_block = head_blocks([keys, values], n_head, place)
+        ahead, behind = ring_step(out_weight, out_weight, order, last=len(order) == 2)
+        ahead, behind, key_block, value_block = lax.optimization_barrier(
+            (ahead, behind, key_block, value_block)
+        )
     (query_block,) = head_blocks([queries], n_head, place)
     row_count = query_block.shape[0]
     query_heads = query_block.reshape(row_count, heads_dev, HEAD_DIM)
@@ -113,6 +112,27 @@
     other_half = lax.ppermute(chip_prefix_half, "core", SWAP)
     chip_prefix = pair_order(chip_prefix_half, other_half, core, 0)
     prefix = chip_prefix + jnp.where(core == 1, partner_state, jnp.zeros_like(partner_state))
+    if order is not None:
+        n_steps = len(order) // 2
+        got, offsets = [out_weight], [0]
+        if n_steps > 1:
+            got += [ahead, behind]
+            offsets += [1, -1]
+        ahead, behind, prefix = lax.optimization_barrier((ahead, behind, prefix))
+        pending = []
+        for step in range(2, n_steps + 1):
+            ahead, behind = ring_step(ahead, behind, order, last=step == n_steps)
+            if step == n_steps:
+                got.append(jnp.concatenate([ahead, behind], 0))
+                offsets.append(step)
+            else:
+                got += [ahead, behind]
+                offsets += [step, -step]
+            pending.append(len(got))
+        if n_steps == 1:
+            got.append(jnp.concatenate([ahead, behind], 0))
+            offsets.append(1)
+        swapped = [lax.ppermute(w, "core", SWAP) for w in got]
 
     carried = jnp.einsum(
         "thd,hde->the", query_heads, prefix.astype(jnp.bfloat16), preferred_element_type=jnp.float32
@@ -143,6 +163,10 @@
     gain_heads = norm_gain.reshape(heads_dev, HEAD_DIM)
     normed = (attended * lax.rsqrt(mean_square + 1e-06) * gain_heads[None]).astype(jnp.bfloat16)
     normed = normed.reshape(row_count, width)
+    if order is not None and len(pending) > 1:
+        first = pending[0]
+        pinned = lax.optimization_barrier((got[:first], swapped[:first], normed))
+        got[:first], swapped[:first], normed = list(pinned[0]), list(pinned[1]), pinned[2]
     if n_head == 2:
         other = lax.ppermute(normed, "head", SWAP)
         gathered = pair_order(normed, other, place, 1)
@@ -158,6 +182,7 @@
         outcome = jnp.dot(normed_own, weight_own, preferred_element_type=jnp.float32)
         outcome = outcome + jnp.dot(normed_other, weight_other, preferred_element_type=jnp.float32)
         return outcome.astype(jnp.bfloat16)
+    weight_own, weight_other = got, swapped
     ring_place = jnp.asarray([order.index(j) for j in range(n_chip)], jnp.int32)[lax.axis_index("chip")]
     sources = jnp.asarray(order, jnp.int32)[(ring_place - jnp.asarray(offsets, jnp.int32)) % n_chip]
     by_offset = jnp.take(split, sources, axis=1)

time: 208 us -> 213 us (1.024)
  starting transfers between devices: 34.6 us -> 26.1 us
  waiting for transfers between devices: 113 us -> 121 us
  matrix products: 27.1 us -> 33.8 us
  other arithmetic: 14.8 us -> 11.6 us
    ppermute x16, waiting for transfers between devices: 39.2 us -> 46.3 us  [the longest x3 29.2 us: ring_step(): lax.ppermute(ahead, 'chip', forward)]
    ppermute x16, starting transfers between devices: 17.2 us -> 11.2 us  [the longest x8 5.61 us: local(): swapped = [lax.ppermute(w, 'core', SWAP) for w in got]]
    ppermute x2, waiting for transfers between devices: 22.9 us -> 26.5 us  [head_blocks(): other = lax.ppermute(sent, 'head', SWAP)]
    dot_general x8, matrix products: 11.1 us -> 14.6 us  [local(): jnp.dot(normed_other[:, i], weight_other[i], preferred_element_type=jnp.f...]
    ppermute x3, starting transfers between devices: 11.4 us -> 8.4 us  [exclusive_prefix(): total = total + lax.ppermute(total, axis, pairs)]
    add x2, other arithmetic: 2.99 us -> 0.14 us  [exclusive_prefix(): total = total + lax.ppermute(total, axis, pairs)]
    ppermute x3, waiting for transfers between devices: 48.4 us -> 45.7 us  [exclusive_prefix(): total = total + lax.ppermute(total, axis, pairs)]
    another operation x2 -> x0, local copies, waits for them, and re-layouts: 2.36 us -> none  [head_blocks(): stacked = jnp.stack(arrays).reshape(len(arrays), rows, 2, width)]
  transfers between devices with their start and end apart: 24 -> 24, of which waited for: 9 -> 13; matrix products, arithmetic and copies ran while one was open for 25% -> 25% of each run, Pallas kernels for 0% -> 0%
where the time goes in v5:
time: 213 us; the launch traced here: 211 us
  waiting for transfers between devices  121 us (57%)
  matrix products  33.8 us (16%)
  starting transfers between devices  26.1 us (12%)
  local copies, waits for them, and re-layouts  18.6 us (9%)
  other arithmetic  11.6 us (5%)
    ppermute x3, waiting for transfers between devices, exclusive_prefix(): total = total + lax.ppermute(total, axis, pairs)  45.7 us
    ppermute x3, waiting for transfers between devices, ring_step(): lax.ppermute(ahead, 'chip', forward)  29.2 us
    ppermute x2, waiting for transfers between devices, head_blocks(): other = lax.ppermute(sent, 'head', SWAP)  26.5 us
    dot_general x8, matrix products, local(): jnp.dot(normed_other[:, i], weight_other[i], preferred_element_type=jnp.f...  14.6 us
    dot_general x8, matrix products, local(): jnp.dot(normed_own[:, i], weight_own[i], preferred_element_type=jnp.float32)  12.4 us
    ppermute x3, starting transfers between devices, exclusive_prefix(): total = total + lax.ppermute(total, axis, pairs)  8.4 us
    ppermute x1, waiting for transfers between devices, ring_step(): lax.ppermute(behind[half_rows:], 'chip', backward)  7.49 us
    ppermute x3, waiting for transfers between devices, ring_step(): lax.ppermute(behind, 'chip', backward)  5.76 us
  transfers between devices with their start and end apart: 24, of which 13 were waited for; matrix products, arithmetic and copies ran while one was open for 25% of the time, Pallas kernels for 0%

profile of v5, /device:TPU:13, one launch (start us, length us, event | category | flops | bytes accessed | tf_op | source)
XLA Modules:
  0.0 211.5 jit_solution(12125388904040327112)
XLA Ops:
  3.6 2.3 %copy.20 = bf16[2,128,1,2048]{3,1,0,2:T(8,128)(2,1)} copy(bf16[2,128,1,2048]{1,3,2,0:T(8,128)(2,1)} %get-tuple-element.50) | data formatting | bytes 2097152 | tf_op jit(solution)/shard_map/jit(dynamic_index_in_dim)/dynamic_slice | solution.py:35
  9.1 21.1 %collective-permute-done.2 = bf16[2,128,2048]{2,1,0:T(8,128)(2,1)S(1)} collective-permute-done((bf16[2,128,2048]{2,1,0:T(8,128)(2,1)}, bf16[2,128,2048]{2,1,0:T(8,128)(2,1)S(1)}, u32[]{:S(2)}, u32[]{:S(2)}) %collective-permute-start.2) | collective-permute-done | bytes 1048608 | tf_op jit(solution)/shard_map/ppermute | solution.py:36
  33.1 2.2 %collective-permute-start.3 = (f32[16,128,128]{2,1,0:T(8,128)S(1)}, f32[16,128,128]{2,1,0:T(8,128)}, u32[]{:S(2)}, u32[]{:S(2)}) collective-permute-start(f32[16,128,128]{2,1,0:T(8,128)S(1)} %fusion.16), channel_id=1, source_target_pairs={{0,2},{2,0},{1,3},{3,1},{4,6},{6,4},{5,7},{7,5},{8,10},{10,8},{9,1... | collective-permute-start | bytes 3145736 | tf_op jit(solution)/shard_map/ppermute | solution.py:107
  35.3 2.4 %collective-permute-done.3 = f32[16,128,128]{2,1,0:T(8,128)} collective-permute-done((f32[16,128,128]{2,1,0:T(8,128)S(1)}, f32[16,128,128]{2,1,0:T(8,128)}, u32[]{:S(2)}, u32[]{:S(2)}) %collective-permute-start.3) | collective-permute-done | bytes 1048608 | tf_op jit(solution)/shard_map/ppermute | solution.py:107
  38.8 2.0 collective-permute-start.4
  40.9 13.0 %collective-permute-done.4 = f32[8,128,128]{2,1,0:T(8,128)S(1)} collective-permute-done((f32[8,128,128]{2,1,0:T(8,128)S(1)}, f32[8,128,128]{2,1,0:T(8,128)S(1)}, u32[]{:S(2)}, u32[]{:S(2)}) %collective-permute-start.4) | collective-permute-done | bytes 524320 | tf_op jit(solution)/shard_map/ppermute | solution.py:18
  54.0 3.2 %collective-permute-start.5 = (f32[8,128,128]{2,1,0:T(8,128)S(1)}, f32[8,128,128]{2,1,0:T(8,128)S(1)}, u32[]{:S(2)}, u32[]{:S(2)}) collective-permute-start(f32[8,128,128]{2,1,0:T(8,128)S(1)} %add.134), channel_id=1, source_target_pairs={{0,8},{4,12},{8,16},{12,20},{16,24},{20,28},{1,9},{5,13},{9,17},{1... | collective-permute-start | bytes 1572872 | tf_op jit(solution)/shard_map/ppermute | solution.py:18
  57.2 10.9 %collective-permute-done.5 = f32[8,128,128]{2,1,0:T(8,128)S(1)} collective-permute-done((f32[8,128,128]{2,1,0:T(8,128)S(1)}, f32[8,128,128]{2,1,0:T(8,128)S(1)}, u32[]{:S(2)}, u32[]{:S(2)}) %collective-permute-start.5) | collective-permute-done | bytes 524320 | tf_op jit(solution)/shard_map/ppermute | solution.py:18
  68.1 3.2 %collective-permute-start.6 = (f32[8,128,128]{2,1,0:T(8,128)S(1)}, f32[8,128,128]{2,1,0:T(8,128)S(1)}, u32[]{:S(2)}, u32[]{:S(2)}) collective-permute-start(f32[8,128,128]{2,1,0:T(8,128)S(1)} %add.135), channel_id=1, source_target_pairs={{0,16},{4,20},{8,24},{12,28},{1,17},{5,21},{9,25},{13,29},{2,18},{... | collective-permute-start | bytes 1572872 | tf_op jit(solution)/shard_map/ppermute | solution.py:18
  71.3 21.8 %collective-permute-done.6 = f32[8,128,128]{2,1,0:T(8,128)S(1)} collective-permute-done((f32[8,128,128]{2,1,0:T(8,128)S(1)}, f32[8,128,128]{2,1,0:T(8,128)S(1)}, u32[]{:S(2)}, u32[]{:S(2)}) %collective-permute-start.6) | collective-permute-done | bytes 524320 | tf_op jit(solution)/shard_map/ppermute | solution.py:18
  98.2 2.0 copy.25
  103.6 2.2 %maximum_add_fusion = bf16[16,128,128]{2,1,0:T(8,128)(2,1)} fusion(f32[8,128,128]{2,1,0:T(8,128)S(1)} %get-tuple-element.56, f32[8,128,128]{2,1,0:T(8,128)S(1)} %get-tuple-element.55, f32[16,128,128]{2,1,0:T(8,128)} %collective-permute-done.3, pred[]{:T(512)S(6)} %eq.9), kind=kLoop, calls=%fused_computation.43 | loop fusion | flops 1048576 | bytes 2621441 | tf_op jit(solution)/shard_map/add | solution.py:114
  108.2 5.3 %collective-permute-done.15 = bf16[1,128,2048]{2,1,0:T(8,128)(2,1)S(1)} collective-permute-done((bf16[1,128,2048]{2,1,0:T(8,128)(2,1)}, bf16[1,128,2048]{2,1,0:T(8,128)(2,1)S(1)}, u32[]{:S(2)}, u32[]{:S(2)}) %collective-permute-start.15) | collective-permute-done | bytes 524320 | tf_op jit(solution)/shard_map/ppermute | solution.py:36
  116.2 15.1 %collective-permute-done.8 = bf16[256,2048]{1,0:T(8,128)(2,1)} collective-permute-done((bf16[256,2048]{1,0:T(8,128)(2,1)}, bf16[256,2048]{1,0:T(8,128)(2,1)}, u32[]{:S(2)}, u32[]{:S(2)}) %collective-permute-start.8) | collective-permute-done | bytes 1048608 | tf_op jit(solution)/shard_map/ppermute | solution.py:83
  133.6 4.0 %fusion.11 = f32[16,128,256]{2,1,0:T(8,128)} fusion(bf16[256,16,128]{0,2,1:T(8,128)(2,1)S(1)} %bitcast.129, bf16[256,16,128]{0,2,1:T(8,128)(2,1)} %bitcast.133, pred[256,256]{1,0:T(8,128)(4,1)S(1)} %iota_compare_fusion, bf16[256,2048]{1,0:T(8,128)(2,1)S(1)} %get-tuple-element.25), kind=kOutput, calls=%fused_computation.32 | convolution fusion | flops 538968064 | bytes 5308416 | tf_op jit(solution)/shard_map/hts,she->the/dot_general | solution.py:156
  137.7 2.3 %fusion.8 = (f32[256,16]{0,1:T(8,128)S(1)}, f32[16,128,256]{2,1,0:T(8,128)S(1)}) fusion(f32[16,128,256]{2,1,0:T(8,128)} %fusion.11, bf16[16,128,128]{2,1,0:T(8,128)(2,1)} %maximum_add_fusion, bf16[256,16,128]{0,2,1:T(8,128)(2,1)S(1)} %bitcast.134), kind=kOutput, calls=%fused_computation.28 | convolution fusion | flops 135786496 | bytes 5783552 | tf_op jit(solution)/shard_map/thd,hde->the/dot_general | solution.py:137
  142.3 13.6 %collective-permute-done.17 = bf16[256,2048]{1,0:T(8,128)(2,1)} collective-permute-done((bf16[256,2048]{1,0:T(8,128)(2,1)}, bf16[256,2048]{1,0:T(8,128)(2,1)}, u32[]{:S(2)}, u32[]{:S(2)}) %collective-permute-start.17) | collective-permute-done | bytes 1048608 | tf_op jit(solution)/shard_map/ppermute | solution.py:83
  158.2 4.7 %collective-permute-done.19 = bf16[256,2048]{1,0:T(8,128)(2,1)} collective-permute-done((bf16[256,2048]{1,0:T(8,128)(2,1)}, bf16[256,2048]{1,0:T(8,128)(2,1)}, u32[]{:S(2)}, u32[]{:S(2)}) %collective-permute-start.19) | collective-permute-done | bytes 1048608 | tf_op jit(solution)/shard_map/ppermute | solution.py:83
  165.4 3.8 %collective-permute-done.21 = bf16[128,2048]{1,0:T(8,128)(2,1)S(1)} collective-permute-done((bf16[128,2048]{1,0:T(8,128)(2,1)S(1)}, bf16[128,2048]{1,0:T(8,128)(2,1)S(1)}, u32[]{:S(2)}, u32[]{:S(2)}) %collective-permute-start.21) | collective-permute-done | bytes 524320 | tf_op jit(solution)/shard_map/ppermute | solution.py:80
  169.2 7.5 %collective-permute-done.22 = bf16[128,2048]{1,0:T(8,128)(2,1)S(1)} collective-permute-done((bf16[128,2048]{1,0:T(8,128)(2,1)S(1)}, bf16[128,2048]{1,0:T(8,128)(2,1)S(1)}, u32[]{:S(2)}, u32[]{:S(2)}) %collective-permute-start.22) | collective-permute-done | bytes 524320 | tf_op jit(solution)/shard_map/ppermute | solution.py:80
  176.8 1.9 collective-permute-start.23
  180.2 2.0 gather_fusion.1
  182.3 1.9 broadcast_select_fusion
  208.7 2.7 %fusion.7 = bf16[256,2048]{1,0:T(8,128)(2,1)} fusion(f32[256,2048]{1,0:T(8,128)S(1)} %convolution_add_fusion, f32[256,2048]{1,0:T(8,128)S(1)} %fusion.2, f32[256,2048]{1,0:T(8,128)S(1)} %fusion.26, bf16[256,2048]{1,0:T(8,128)(2,1)} %collective-permute-done.20, bf16[256,8,256]{0,2,1:T(8,128)(2,1)S(1)} %get-tuple-element.42), kind=kOutput, calls=%fused_computation.18 | convolution fusion | flops 270532608 | bytes 8519680 | tf_op jit(solution)/shard_map/dot_general | solution.py:194
  (95 shorter events, 59.8 us)
Async XLA Ops:
  5.8 24.3 %collective-permute-start.2 = (bf16[2,128,2048]{2,1,0:T(8,128)(2,1)}, bf16[2,128,2048]{2,1,0:T(8,128)(2,1)S(1)}, u32[]{:S(2)}, u32[]{:S(2)}) collective-permute-start(bf16[2,128,2048]{2,1,0:T(8,128)(2,1)} %bitcast.4), channel_id=1, source_target_pairs={{0,1},{1,0},{2,3},{3,2},{4,5},{5,4},{6,7},{7,6},{8,9},{9,8},{10,11... | collective-permute-start | bytes 3145736 | tf_op jit(solution)/shard_map/ppermute | solution.py:36
  7.1 24.0 %collective-permute-start = (bf16[256,2048]{1,0:T(8,128)(2,1)}, bf16[256,2048]{1,0:T(8,128)(2,1)}, u32[]{:S(2)}, u32[]{:S(2)}) collective-permute-start(bf16[256,2048]{1,0:T(8,128)(2,1)} %param.11), channel_id=1, source_target_pairs={{0,4},{4,12},{12,20},{20,28},{28,24},{24,16},{16,8},{8,0},{1,5},{5... | collective-permute-start | bytes 3145736 | tf_op jit(solution)/shard_map/ppermute | solution.py:83
  8.3 23.7 %collective-permute-start.1 = (bf16[256,2048]{1,0:T(8,128)(2,1)}, bf16[256,2048]{1,0:T(8,128)(2,1)}, u32[]{:S(2)}, u32[]{:S(2)}) collective-permute-start(bf16[256,2048]{1,0:T(8,128)(2,1)} %param.11), channel_id=1, source_target_pairs={{4,0},{12,4},{20,12},{28,20},{24,28},{16,24},{8,16},{0,8},{5,1},{1... | collective-permute-start | bytes 3145736 | tf_op jit(solution)/shard_map/ppermute | solution.py:83
  33.1 4.6 %collective-permute-start.3 = (f32[16,128,128]{2,1,0:T(8,128)S(1)}, f32[16,128,128]{2,1,0:T(8,128)}, u32[]{:S(2)}, u32[]{:S(2)}) collective-permute-start(f32[16,128,128]{2,1,0:T(8,128)S(1)} %fusion.16), channel_id=1, source_target_pairs={{0,2},{2,0},{1,3},{3,1},{4,6},{6,4},{5,7},{7,5},{8,10},{10,8},{9,1... | collective-permute-start | bytes 3145736 | tf_op jit(solution)/shard_map/ppermute | solution.py:107
  38.8 15.0 %collective-permute-start.4 = (f32[8,128,128]{2,1,0:T(8,128)S(1)}, f32[8,128,128]{2,1,0:T(8,128)S(1)}, u32[]{:S(2)}, u32[]{:S(2)}) collective-permute-start(f32[8,128,128]{2,1,0:T(8,128)S(1)} %dynamic-slice_add_fusion), channel_id=1, source_target_pairs={{0,4},{4,8},{8,12},{12,16},{16,20},{20,24},{24,28},{1,5},{5,9},{9,... | collective-permute-start | bytes 1572872 | tf_op jit(solution)/shard_map/ppermute | solution.py:18
  54.0 14.1 %collective-permute-start.5 = (f32[8,128,128]{2,1,0:T(8,128)S(1)}, f32[8,128,128]{2,1,0:T(8,128)S(1)}, u32[]{:S(2)}, u32[]{:S(2)}) collective-permute-start(f32[8,128,128]{2,1,0:T(8,128)S(1)} %add.134), channel_id=1, source_target_pairs={{0,8},{4,12},{8,16},{12,20},{16,24},{20,28},{1,9},{5,13},{9,17},{1... | collective-permute-start | bytes 1572872 | tf_op jit(solution)/shard_map/ppermute | solution.py:18
  68.1 25.0 %collective-permute-start.6 = (f32[8,128,128]{2,1,0:T(8,128)S(1)}, f32[8,128,128]{2,1,0:T(8,128)S(1)}, u32[]{:S(2)}, u32[]{:S(2)}) collective-permute-start(f32[8,128,128]{2,1,0:T(8,128)S(1)} %add.135), channel_id=1, source_target_pairs={{0,16},{4,20},{8,24},{12,28},{1,17},{5,21},{9,25},{13,29},{2,18},{... | collective-permute-start | bytes 1572872 | tf_op jit(solution)/shard_map/ppermute | solution.py:18
  94.0 8.3 %collective-permute-start.7 = (f32[8,128,128]{2,1,0:T(8,128)}, f32[8,128,128]{2,1,0:T(8,128)}, u32[]{:S(2)}, u32[]{:S(2)}) collective-permute-start(f32[8,128,128]{2,1,0:T(8,128)} %add_subtract_fusion), channel_id=1, source_target_pairs={{0,2},{2,0},{1,3},{3,1},{4,6},{6,4},{5,7},{7,5},{8,10},{10,8},{9,1... | collective-permute-start | bytes 1572872 | tf_op jit(solution)/shard_map/ppermute | solution.py:112
  95.5 37.0 %collective-permute-start.10 = (bf16[256,2048]{1,0:T(8,128)(2,1)}, bf16[256,2048]{1,0:T(8,128)(2,1)}, u32[]{:S(2)}, u32[]{:S(2)}) collective-permute-start(bf16[256,2048]{1,0:T(8,128)(2,1)} %param.11), channel_id=1, source_target_pairs={{0,2},{2,0},{1,3},{3,1},{4,6},{6,4},{5,7},{7,5},{8,10},{10,8},{9,1... | collective-permute-start | bytes 3145736 | tf_op jit(solution)/shard_map/ppermute | solution.py:135
  100.2 13.3 %collective-permute-start.15 = (bf16[1,128,2048]{2,1,0:T(8,128)(2,1)}, bf16[1,128,2048]{2,1,0:T(8,128)(2,1)S(1)}, u32[]{:S(2)}, u32[]{:S(2)}) collective-permute-start(bf16[1,128,2048]{2,1,0:T(8,128)(2,1)} %bitcast.9), channel_id=1, source_target_pairs={{0,1},{1,0},{2,3},{3,2},{4,5},{5,4},{6,7},{7,6},{8,9},{9,8},{10,11... | collective-permute-start | bytes 1572872 | tf_op jit(solution)/shard_map/ppermute | solution.py:36
  105.8 25.5 %collective-permute-start.8 = (bf16[256,2048]{1,0:T(8,128)(2,1)}, bf16[256,2048]{1,0:T(8,128)(2,1)}, u32[]{:S(2)}, u32[]{:S(2)}) collective-permute-start(bf16[256,2048]{1,0:T(8,128)(2,1)} %collective-permute-done), channel_id=1, source_target_pairs={{0,4},{4,12},{12,20},{20,28},{28,24},{24,16},{16,8},{8,0},{1,5},{5... | collective-permute-start | bytes 3145736 | tf_op jit(solution)/shard_map/ppermute | solution.py:83
  105.8 27.4 %collective-permute-start.9 = (bf16[256,2048]{1,0:T(8,128)(2,1)}, bf16[256,2048]{1,0:T(8,128)(2,1)}, u32[]{:S(2)}, u32[]{:S(2)}) collective-permute-start(bf16[256,2048]{1,0:T(8,128)(2,1)} %collective-permute-done.1), channel_id=1, source_target_pairs={{4,0},{12,4},{20,12},{28,20},{24,28},{16,24},{8,16},{0,8},{5,1},{1... | collective-permute-start | bytes 3145736 | tf_op jit(solution)/shard_map/ppermute | solution.py:83
  108.0 29.7 %collective-permute-start.11 = (bf16[256,2048]{1,0:T(8,128)(2,1)}, bf16[256,2048]{1,0:T(8,128)(2,1)}, u32[]{:S(2)}, u32[]{:S(2)}) collective-permute-start(bf16[256,2048]{1,0:T(8,128)(2,1)} %collective-permute-done), channel_id=1, source_target_pairs={{0,2},{2,0},{1,3},{3,1},{4,6},{6,4},{5,7},{7,5},{8,10},{10,8},{9,1... | collective-permute-start | bytes 3145736 | tf_op jit(solution)/shard_map/ppermute | solution.py:135
  115.0 25.4 %collective-permute-start.12 = (bf16[256,2048]{1,0:T(8,128)(2,1)}, bf16[256,2048]{1,0:T(8,128)(2,1)}, u32[]{:S(2)}, u32[]{:S(2)}) collective-permute-start(bf16[256,2048]{1,0:T(8,128)(2,1)} %collective-permute-done.1), channel_id=1, source_target_pairs={{0,2},{2,0},{1,3},{3,1},{4,6},{6,4},{5,7},{7,5},{8,10},{10,8},{9,1... | collective-permute-start | bytes 3145736 | tf_op jit(solution)/shard_map/ppermute | solution.py:135
  131.3 24.6 %collective-permute-start.17 = (bf16[256,2048]{1,0:T(8,128)(2,1)}, bf16[256,2048]{1,0:T(8,128)(2,1)}, u32[]{:S(2)}, u32[]{:S(2)}) collective-permute-start(bf16[256,2048]{1,0:T(8,128)(2,1)} %collective-permute-done.8), channel_id=1, source_target_pairs={{0,4},{4,12},{12,20},{20,28},{28,24},{24,16},{16,8},{8,0},{1,5},{5... | collective-permute-start | bytes 3145736 | tf_op jit(solution)/shard_map/ppermute | solution.py:83
  132.5 7.9 %collective-permute-start.13 = (bf16[256,2048]{1,0:T(8,128)(2,1)}, bf16[256,2048]{1,0:T(8,128)(2,1)}, u32[]{:S(2)}, u32[]{:S(2)}) collective-permute-start(bf16[256,2048]{1,0:T(8,128)(2,1)} %collective-permute-done.8), channel_id=1, source_target_pairs={{0,2},{2,0},{1,3},{3,1},{4,6},{6,4},{5,7},{7,5},{8,10},{10,8},{9,1... | collective-permute-start | bytes 3145736 | tf_op jit(solution)/shard_map/ppermute | solution.py:135
  133.2 7.2 %collective-permute-start.14 = (bf16[256,2048]{1,0:T(8,128)(2,1)}, bf16[256,2048]{1,0:T(8,128)(2,1)}, u32[]{:S(2)}, u32[]{:S(2)}) collective-permute-start(bf16[256,2048]{1,0:T(8,128)(2,1)} %collective-permute-done.9), channel_id=1, source_target_pairs={{0,2},{2,0},{1,3},{3,1},{4,6},{6,4},{5,7},{7,5},{8,10},{10,8},{9,1... | collective-permute-start | bytes 3145736 | tf_op jit(solution)/shard_map/ppermute | solution.py:135
  137.7 25.3 %collective-permute-start.19 = (bf16[256,2048]{1,0:T(8,128)(2,1)}, bf16[256,2048]{1,0:T(8,128)(2,1)}, u32[]{:S(2)}, u32[]{:S(2)}) collective-permute-start(bf16[256,2048]{1,0:T(8,128)(2,1)} %collective-permute-done.9), channel_id=1, source_target_pairs={{4,0},{12,4},{20,12},{28,20},{24,28},{16,24},{8,16},{0,8},{5,1},{1... | collective-permute-start | bytes 3145736 | tf_op jit(solution)/shard_map/ppermute | solution.py:83
  140.4 38.3 %collective-permute-start.16 = (bf16[256,2048]{0,1:T(8,128)(2,1)S(1)}, bf16[256,2048]{0,1:T(8,128)(2,1)}, u32[]{:S(2)}, u32[]{:S(2)}) collective-permute-start(bf16[256,2048]{0,1:T(8,128)(2,1)S(1)} %bitcast.126), channel_id=1, source_target_pairs={{0,1},{1,0},{2,3},{3,2},{4,5},{5,4},{6,7},{7,6},{8,9},{9,8},{10,11... | collective-permute-start | bytes 3145736 | tf_op jit(solution)/shard_map/ppermute | solution.py:171
  157.0 12.2 %collective-permute-start.21 = (bf16[128,2048]{1,0:T(8,128)(2,1)S(1)}, bf16[128,2048]{1,0:T(8,128)(2,1)S(1)}, u32[]{:S(2)}, u32[]{:S(2)}) collective-permute-start(bf16[128,2048]{1,0:T(8,128)(2,1)S(1)} %slice.101), channel_id=1, source_target_pairs={{0,4},{4,12},{12,20},{20,28},{28,24},{24,16},{16,8},{8,0},{1,5},{5... | collective-permute-start | bytes 1572872 | tf_op jit(solution)/shard_map/ppermute | solution.py:80
  164.0 12.7 %collective-permute-start.22 = (bf16[128,2048]{1,0:T(8,128)(2,1)S(1)}, bf16[128,2048]{1,0:T(8,128)(2,1)S(1)}, u32[]{:S(2)}, u32[]{:S(2)}) collective-permute-start(bf16[128,2048]{1,0:T(8,128)(2,1)S(1)} %slice.102), channel_id=1, source_target_pairs={{4,0},{12,4},{20,12},{28,20},{24,28},{16,24},{8,16},{0,8},{5,1},{1... | collective-permute-start | bytes 1572872 | tf_op jit(solution)/shard_map/ppermute | solution.py:80
  164.3 40.5 %collective-permute-start.18 = (bf16[256,2048]{1,0:T(8,128)(2,1)}, bf16[256,2048]{1,0:T(8,128)(2,1)}, u32[]{:S(2)}, u32[]{:S(2)}) collective-permute-start(bf16[256,2048]{1,0:T(8,128)(2,1)} %collective-permute-done.17), channel_id=1, source_target_pairs={{0,2},{2,0},{1,3},{3,1},{4,6},{6,4},{5,7},{7,5},{8,10},{10,8},{9,1... | collective-permute-start | bytes 3145736 | tf_op jit(solution)/shard_map/ppermute | solution.py:135
  165.3 43.4 %collective-permute-start.20 = (bf16[256,2048]{1,0:T(8,128)(2,1)}, bf16[256,2048]{1,0:T(8,128)(2,1)}, u32[]{:S(2)}, u32[]{:S(2)}) collective-permute-start(bf16[256,2048]{1,0:T(8,128)(2,1)} %collective-permute-done.19), channel_id=1, source_target_pairs={{0,2},{2,0},{1,3},{3,1},{4,6},{6,4},{5,7},{7,5},{8,10},{10,8},{9,1... | collective-permute-start | bytes 3145736 | tf_op jit(solution)/shard_map/ppermute | solution.py:135
  176.8 29.8 %collective-permute-start.23 = (bf16[256,2048]{1,0:T(8,128)(2,1)S(1)}, bf16[256,2048]{1,0:T(8,128)(2,1)}, u32[]{:S(2)}, u32[]{:S(2)}) collective-permute-start(bf16[256,2048]{1,0:T(8,128)(2,1)S(1)} %constant_dynamic-update-slice_fusion), channel_id=1, source_target_pairs={{0,2},{2,0},{1,3},{3,1},{4,6},{6,4},{5,7},{7,5},{8,10},{10,8},{9,1... | collective-permute-start | bytes 3145736 | tf_op jit(solution)/shard_map/ppermute | solution.py:135
  (6 other events, 19.4 us)

commit v6 on v5

--- a/solution.py
+++ b/solution.py
@@ -44,7 +44,7 @@
 def chip_cycle(devices):
     n = devices.shape[0]
     coords = [getattr(devices[j, 0, 0], "coords", None) for j in range(n)]
-    if n > 16 or any(c is None for c in coords):
+    if n < 4 or n > 16 or any(c is None for c in coords):
         return None
 
     def adjacent(a, b):
@@ -88,7 +88,7 @@
     width = heads_dev * HEAD_DIM
     core = lax.axis_index("core")
     place = lax.axis_index("head") if n_head == 2 else 0
-    key_block, value_block = head_blocks([keys, values], n_head, place)
+    query_block, key_block, value_block = head_blocks([queries, keys, values], n_head, place)
     if order is None:
         weight_own, offsets = [lax.all_gather(out_weight, "chip", axis=0, tiled=True)], [0]
     else:
@@ -96,7 +96,6 @@
         ahead, behind, key_block, value_block = lax.optimization_barrier(
             (ahead, behind, key_block, value_block)
         )
-    (query_block,) = head_blocks([queries], n_head, place)
     row_count = query_block.shape[0]
     query_heads = query_block.reshape(row_count, heads_dev, HEAD_DIM)
     key_heads = key_block.reshape(row_count, heads_dev, HEAD_DIM)
@@ -108,19 +107,26 @@
     chip_state = kv_state + partner_state
     half = heads_dev // 2
     chip_half = lax.dynamic_slice_in_dim(chip_state, core * half, half, 0)
-    chip_prefix_half = exclusive_prefix(chip_half, "chip", n_chip)
-    other_half = lax.ppermute(chip_prefix_half, "core", SWAP)
-    chip_prefix = pair_order(chip_prefix_half, other_half, core, 0)
-    prefix = chip_prefix + jnp.where(core == 1, partner_state, jnp.zeros_like(partner_state))
     if order is not None:
         n_steps = len(order) // 2
         got, offsets = [out_weight], [0]
         if n_steps > 1:
             got += [ahead, behind]
             offsets += [1, -1]
+        if n_steps > 2:
+            ahead, behind = ring_step(ahead, behind, order, last=n_steps == 2)
+            got += [ahead, behind]
+            offsets += [2, -2]
+        ahead, behind, chip_half = lax.optimization_barrier((ahead, behind, chip_half))
+        got[-2:] = [ahead, behind]
+    chip_prefix_half = exclusive_prefix(chip_half, "chip", n_chip)
+    other_half = lax.ppermute(chip_prefix_half, "core", SWAP)
+    chip_prefix = pair_order(chip_prefix_half, other_half, core, 0)
+    prefix = chip_prefix + jnp.where(core == 1, partner_state, jnp.zeros_like(partner_state))
+    if order is not None:
         ahead, behind, prefix = lax.optimization_barrier((ahead, behind, prefix))
         pending = []
-        for step in range(2, n_steps + 1):
+        for step in range(min(3, n_steps), n_steps + 1):
             ahead, behind = ring_step(ahead, behind, order, last=step == n_steps)
             if step == n_steps:
                 got.append(jnp.concatenate([ahead, behind], 0))
@@ -186,13 +192,11 @@
     ring_place = jnp.asarray([order.index(j) for j in range(n_chip)], jnp.int32)[lax.axis_index("chip")]
     sources = jnp.asarray(order, jnp.int32)[(ring_place - jnp.asarray(offsets, jnp.int32)) % n_chip]
     by_offset = jnp.take(split, sources, axis=1)
-    normed_own = lax.dynamic_index_in_dim(by_offset, core, 2, False)
-    normed_other = lax.dynamic_index_in_dim(by_offset, 1 - core, 2, False)
-    outcome = None
-    for i in range(len(offsets)):
-        part = jnp.dot(normed_own[:, i], weight_own[i], preferred_element_type=jnp.float32)
-        part = part + jnp.dot(normed_other[:, i], weight_other[i], preferred_element_type=jnp.float32)
-        outcome = part if outcome is None else outcome + part
+    by_offset = jnp.where(core == 0, by_offset, by_offset[:, :, ::-1])
+    weight_all = jnp.concatenate([w for pair in zip(weight_own, weight_other) for w in pair], 0)
+    outcome = jnp.dot(
+        by_offset.reshape(row_count, -1), weight_all, preferred_element_type=jnp.float32
+    )
     return outcome.astype(jnp.bfloat16)
 
 

time: 213 us -> 236 us (1.11)
  local copies, waits for them, and re-layouts: 18.6 us -> 49.6 us
  matrix products: 33.8 us -> 17.1 us
  waiting for transfers between devices: 121 us -> 130 us
  starting transfers between devices: 26.1 us -> 23.7 us
    unnamed x16 -> x29, local copies, waits for them, and re-layouts: 4.04 us -> 36.2 us
    dot_general x16 -> x1, matrix products: 27.1 us -> 9.29 us  [local(): jnp.dot(by_offset.reshape(row_count, -1), weight_all, preferred_element_t...]
    ppermute x3, waiting for transfers between devices: 29.2 us -> 42.4 us  [ring_step(): lax.ppermute(ahead, 'chip', forward)]
    ppermute x2 -> x1, waiting for transfers between devices: 26.5 us -> 32.2 us  [head_blocks(): other = lax.ppermute(sent, 'head', SWAP)]
    ppermute x3, waiting for transfers between devices: 5.76 us -> 0.98 us  [ring_step(): lax.ppermute(behind, 'chip', backward)]
    ppermute x1, waiting for transfers between devices: 7.49 us -> 2.95 us  [ring_step(): lax.ppermute(behind[half_rows:], 'chip', backward)]
    dynamic_slice x2 -> x1, local copies, waits for them, and re-layouts: 4.31 us -> 1.6 us  [head_blocks(): sent = lax.dynamic_index_in_dim(stacked, 1 - place, 2, False)]
  transfers between devices with their start and end apart: 24 -> 23, of which waited for: 13 -> 11; matrix products, arithmetic and copies ran while one was open for 25% -> 22% of each run, Pallas kernels for 0% -> 0%
where the time goes in v6:
time: 236 us; the launch traced here: 234 us
  waiting for transfers between devices  130 us (55%)
  local copies, waits for them, and re-layouts  49.6 us (21%)
  starting transfers between devices  23.7 us (10%)
  matrix products  17.1 us (7%)
  other arithmetic  13.9 us (6%)
    ppermute x3, waiting for transfers between devices, exclusive_prefix(): total = total + lax.ppermute(total, axis, pairs)  44.2 us
    ppermute x3, waiting for transfers between devices, ring_step(): lax.ppermute(ahead, 'chip', forward)  42.4 us
    unnamed x29, local copies, waits for them, and re-layouts  36.2 us
    ppermute x1, waiting for transfers between devices, head_blocks(): other = lax.ppermute(sent, 'head', SWAP)  32.2 us
    dot_general x1, matrix products, local(): jnp.dot(by_offset.reshape(row_count, -1), weight_all, preferred_element_t...  9.29 us
    ppermute x3, starting transfers between devices, exclusive_prefix(): total = total + lax.ppermute(total, axis, pairs)  8.96 us
  transfers between devices with their start and end apart: 23, of which 11 were waited for; matrix products, arithmetic and copies ran while one was open for 22% of the time, Pallas kernels for 0%

profile of v6, /device:TPU:13, one launch (start us, length us, event | category | flops | bytes accessed | tf_op | source)
XLA Modules:
  0.0 234.1 jit_solution(12682126905714566000)
XLA Ops:
  10.4 32.2 %collective-permute-done.2 = bf16[3,128,2048]{2,1,0:T(8,128)(2,1)} collective-permute-done((bf16[3,128,2048]{2,1,0:T(8,128)(2,1)}, bf16[3,128,2048]{2,1,0:T(8,128)(2,1)}, u32[]{:S(2)}, u32[]{:S(2)}) %collective-permute-start.2) | collective-permute-done | bytes 1572896 | tf_op jit(solution)/shard_map/ppermute | solution.py:36
  53.9 21.2 %collective-permute-done.3 = bf16[256,2048]{1,0:T(8,128)(2,1)} collective-permute-done((bf16[256,2048]{1,0:T(8,128)(2,1)}, bf16[256,2048]{1,0:T(8,128)(2,1)}, u32[]{:S(2)}, u32[]{:S(2)}) %collective-permute-start.3) | collective-permute-done | bytes 1048608 | tf_op jit(solution)/shard_map/ppermute | solution.py:83
  78.2 12.0 %collective-permute-done.6 = f32[8,128,128]{2,1,0:T(8,128)S(1)} collective-permute-done((f32[8,128,128]{2,1,0:T(8,128)S(1)}, f32[8,128,128]{2,1,0:T(8,128)S(1)}, u32[]{:S(2)}, u32[]{:S(2)}) %collective-permute-start.6) | collective-permute-done | bytes 524320 | tf_op jit(solution)/shard_map/ppermute | solution.py:18
  90.4 3.2 %collective-permute-start.7 = (f32[8,128,128]{2,1,0:T(8,128)S(1)}, f32[8,128,128]{2,1,0:T(8,128)S(1)}, u32[]{:S(2)}, u32[]{:S(2)}) collective-permute-start(f32[8,128,128]{2,1,0:T(8,128)S(1)} %add.78), channel_id=1, source_target_pairs={{0,8},{4,12},{8,16},{12,20},{16,24},{20,28},{1,9},{5,13},{9,17},{1... | collective-permute-start | bytes 1572872 | tf_op jit(solution)/shard_map/ppermute | solution.py:18
  93.6 10.1 %collective-permute-done.7 = f32[8,128,128]{2,1,0:T(8,128)S(1)} collective-permute-done((f32[8,128,128]{2,1,0:T(8,128)S(1)}, f32[8,128,128]{2,1,0:T(8,128)S(1)}, u32[]{:S(2)}, u32[]{:S(2)}) %collective-permute-start.7) | collective-permute-done | bytes 524320 | tf_op jit(solution)/shard_map/ppermute | solution.py:18
  103.7 3.6 %collective-permute-start.8 = (f32[8,128,128]{2,1,0:T(8,128)S(1)}, f32[8,128,128]{2,1,0:T(8,128)S(1)}, u32[]{:S(2)}, u32[]{:S(2)}) collective-permute-start(f32[8,128,128]{2,1,0:T(8,128)S(1)} %add.79), channel_id=1, source_target_pairs={{0,16},{4,20},{8,24},{12,28},{1,17},{5,21},{9,25},{13,29},{2,18},{... | collective-permute-start | bytes 1572872 | tf_op jit(solution)/shard_map/ppermute | solution.py:18
  107.3 22.1 %collective-permute-done.8 = f32[8,128,128]{2,1,0:T(8,128)S(1)} collective-permute-done((f32[8,128,128]{2,1,0:T(8,128)S(1)}, f32[8,128,128]{2,1,0:T(8,128)S(1)}, u32[]{:S(2)}, u32[]{:S(2)}) %collective-permute-start.8) | collective-permute-done | bytes 524320 | tf_op jit(solution)/shard_map/ppermute | solution.py:18
  134.7 2.2 maximum_add_fusion
  140.9 21.1 %collective-permute-done.10 = bf16[256,2048]{1,0:T(8,128)(2,1)} collective-permute-done((bf16[256,2048]{1,0:T(8,128)(2,1)}, bf16[256,2048]{1,0:T(8,128)(2,1)}, u32[]{:S(2)}, u32[]{:S(2)}) %collective-permute-start.10) | collective-permute-done | bytes 1048608 | tf_op jit(solution)/shard_map/ppermute | solution.py:83
  169.3 4.1 %fusion.3 = f32[16,128,256]{2,1,0:T(8,128)} fusion(bf16[256,16,128]{0,2,1:T(8,128)(2,1)S(1)} %bitcast.59, bf16[256,16,128]{0,2,1:T(8,128)(2,1)} %bitcast.60, pred[256,256]{1,0:T(8,128)(4,1)S(1)} %iota_compare_fusion, bf16[256,2048]{1,0:T(8,128)(2,1)S(1)} %get-tuple-element.32), kind=kOutput, calls=%fused_computation.17 | convolution fusion | flops 538968064 | bytes 5308416 | tf_op jit(solution)/shard_map/hts,she->the/dot_general | solution.py:162
  173.9 3.8 %collective-permute-done.20 = bf16[128,2048]{1,0:T(8,128)(2,1)} collective-permute-done((bf16[128,2048]{1,0:T(8,128)(2,1)}, bf16[128,2048]{1,0:T(8,128)(2,1)}, u32[]{:S(2)}, u32[]{:S(2)}) %collective-permute-start.20) | collective-permute-done | bytes 524320 | tf_op jit(solution)/shard_map/ppermute | solution.py:80
  178.6 3.0 %collective-permute-done.21 = bf16[128,2048]{1,0:T(8,128)(2,1)} collective-permute-done((bf16[128,2048]{1,0:T(8,128)(2,1)}, bf16[128,2048]{1,0:T(8,128)(2,1)}, u32[]{:S(2)}, u32[]{:S(2)}) %collective-permute-start.21) | collective-permute-done | bytes 524320 | tf_op jit(solution)/shard_map/ppermute | solution.py:80
  182.4 2.3 fusion
  186.5 2.3 constant_dynamic-update-slice_fusion.16
  190.1 2.3 constant_dynamic-update-slice_fusion.15
  192.4 2.3 constant_dynamic-update-slice_fusion.14
  194.7 2.3 constant_dynamic-update-slice_fusion.13
  197.0 2.4 %constant_dynamic-update-slice_fusion.12 = bf16[4096,2048]{1,0:T(8,128)(2,1)} fusion(bf16[4096,2048]{1,0:T(8,128)(2,1)} %constant_dynamic-update-slice_fusion.13, bf16[256,2048]{1,0:T(8,128)(2,1)} %collective-permute-done.1), kind=kLoop, calls=%fused_computation.53 | loop fusion | bytes 2097152
  199.3 2.3 constant_dynamic-update-slice_fusion.11
  201.7 2.3 constant_dynamic-update-slice_fusion.10
  205.1 2.4 %constant_dynamic-update-slice_fusion.8 = bf16[4096,2048]{1,0:T(8,128)(2,1)} fusion(bf16[4096,2048]{1,0:T(8,128)(2,1)} %constant_dynamic-update-slice_fusion.9, bf16[256,2048]{1,0:T(8,128)(2,1)} %collective-permute-done.4), kind=kLoop, calls=%fused_computation.49 | loop fusion | bytes 2097152
  208.6 2.3 constant_dynamic-update-slice_fusion.6
  211.9 2.3 constant_dynamic-update-slice_fusion.4
  224.8 9.3 %convolution_convert_fusion = bf16[256,2048]{1,0:T(8,128)(2,1)} fusion(bf16[256,4096]{0,1:T(8,128)(2,1)S(1)} %bitcast.54, bf16[4096,2048]{1,0:T(8,128)(2,1)} %constant_dynamic-update-slice_fusion), kind=kOutput, calls=%fused_computation.9 | convolution fusion | flops 4295491584 | bytes 19922944 | tf_op jit(solution)/shard_map/dot_general | solution.py:197
  (88 shorter events, 60.5 us)
Async XLA Ops:
  7.0 35.6 %collective-permute-start.2 = (bf16[3,128,2048]{2,1,0:T(8,128)(2,1)}, bf16[3,128,2048]{2,1,0:T(8,128)(2,1)}, u32[]{:S(2)}, u32[]{:S(2)}) collective-permute-start(bf16[3,128,2048]{2,1,0:T(8,128)(2,1)} %bitcast.65), channel_id=1, source_target_pairs={{0,1},{1,0},{2,3},{3,2},{4,5},{5,4},{6,7},{7,6},{8,9},{9,8},{10,11... | collective-permute-start | bytes 4718600 | tf_op jit(solution)/shard_map/ppermute | solution.py:36
  8.3 37.2 %collective-permute-start = (bf16[256,2048]{1,0:T(8,128)(2,1)}, bf16[256,2048]{1,0:T(8,128)(2,1)}, u32[]{:S(2)}, u32[]{:S(2)}) collective-permute-start(bf16[256,2048]{1,0:T(8,128)(2,1)} %param.11), channel_id=1, source_target_pairs={{0,4},{4,12},{12,20},{20,28},{28,24},{24,16},{16,8},{8,0},{1,5},{5... | collective-permute-start | bytes 3145736 | tf_op jit(solution)/shard_map/ppermute | solution.py:83
  9.6 35.9 %collective-permute-start.1 = (bf16[256,2048]{1,0:T(8,128)(2,1)}, bf16[256,2048]{1,0:T(8,128)(2,1)}, u32[]{:S(2)}, u32[]{:S(2)}) collective-permute-start(bf16[256,2048]{1,0:T(8,128)(2,1)} %param.11), channel_id=1, source_target_pairs={{4,0},{12,4},{20,12},{28,20},{24,28},{16,24},{8,16},{0,8},{5,1},{1... | collective-permute-start | bytes 3145736 | tf_op jit(solution)/shard_map/ppermute | solution.py:83
  48.4 4.2 %collective-permute-start.5 = (f32[16,128,128]{2,1,0:T(8,128)}, f32[16,128,128]{2,1,0:T(8,128)}, u32[]{:S(2)}, u32[]{:S(2)}) collective-permute-start(f32[16,128,128]{2,1,0:T(8,128)} %fusion.8), channel_id=1, source_target_pairs={{0,2},{2,0},{1,3},{3,1},{4,6},{6,4},{5,7},{7,5},{8,10},{10,8},{9,1... | collective-permute-start | bytes 3145736 | tf_op jit(solution)/shard_map/ppermute | solution.py:106
  50.0 25.1 %collective-permute-start.3 = (bf16[256,2048]{1,0:T(8,128)(2,1)}, bf16[256,2048]{1,0:T(8,128)(2,1)}, u32[]{:S(2)}, u32[]{:S(2)}) collective-permute-start(bf16[256,2048]{1,0:T(8,128)(2,1)} %collective-permute-done), channel_id=1, source_target_pairs={{0,4},{4,12},{12,20},{20,28},{28,24},{24,16},{16,8},{8,0},{1,5},{5... | collective-permute-start | bytes 3145736 | tf_op jit(solution)/shard_map/ppermute | solution.py:83
  51.3 24.8 %collective-permute-start.4 = (bf16[256,2048]{1,0:T(8,128)(2,1)}, bf16[256,2048]{1,0:T(8,128)(2,1)}, u32[]{:S(2)}, u32[]{:S(2)}) collective-permute-start(bf16[256,2048]{1,0:T(8,128)(2,1)} %collective-permute-done.1), channel_id=1, source_target_pairs={{4,0},{12,4},{20,12},{28,20},{24,28},{16,24},{8,16},{0,8},{5,1},{1... | collective-permute-start | bytes 3145736 | tf_op jit(solution)/shard_map/ppermute | solution.py:83
  76.1 14.2 %collective-permute-start.6 = (f32[8,128,128]{2,1,0:T(8,128)S(1)}, f32[8,128,128]{2,1,0:T(8,128)S(1)}, u32[]{:S(2)}, u32[]{:S(2)}) collective-permute-start(f32[8,128,128]{2,1,0:T(8,128)S(1)} %dynamic-slice_add_fusion), channel_id=1, source_target_pairs={{0,4},{4,8},{8,12},{12,16},{16,20},{20,24},{24,28},{1,5},{5,9},{9,... | collective-permute-start | bytes 1572872 | tf_op jit(solution)/shard_map/ppermute | solution.py:18
  90.4 13.3 %collective-permute-start.7 = (f32[8,128,128]{2,1,0:T(8,128)S(1)}, f32[8,128,128]{2,1,0:T(8,128)S(1)}, u32[]{:S(2)}, u32[]{:S(2)}) collective-permute-start(f32[8,128,128]{2,1,0:T(8,128)S(1)} %add.78), channel_id=1, source_target_pairs={{0,8},{4,12},{8,16},{12,20},{16,24},{20,28},{1,9},{5,13},{9,17},{1... | collective-permute-start | bytes 1572872 | tf_op jit(solution)/shard_map/ppermute | solution.py:18
  103.7 36.5 %copy-start = (s32[8]{0:T(128)S(1)}, s32[8]{0:T(128)}, u32[]{:S(2)}) copy-start(s32[8]{0:T(128)} %constant.72.clone) | copy-start | bytes 100
  103.7 25.7 %collective-permute-start.8 = (f32[8,128,128]{2,1,0:T(8,128)S(1)}, f32[8,128,128]{2,1,0:T(8,128)S(1)}, u32[]{:S(2)}, u32[]{:S(2)}) collective-permute-start(f32[8,128,128]{2,1,0:T(8,128)S(1)} %add.79), channel_id=1, source_target_pairs={{0,16},{4,20},{8,24},{12,28},{1,17},{5,21},{9,25},{13,29},{2,18},{... | collective-permute-start | bytes 1572872 | tf_op jit(solution)/shard_map/ppermute | solution.py:18
  130.3 3.1 %collective-permute-start.9 = (f32[8,128,128]{2,1,0:T(8,128)}, f32[8,128,128]{2,1,0:T(8,128)}, u32[]{:S(2)}, u32[]{:S(2)}) collective-permute-start(f32[8,128,128]{2,1,0:T(8,128)} %add_subtract_fusion), channel_id=1, source_target_pairs={{0,2},{2,0},{1,3},{3,1},{4,6},{6,4},{5,7},{7,5},{8,10},{10,8},{9,1... | collective-permute-start | bytes 1572872 | tf_op jit(solution)/shard_map/ppermute | solution.py:123
  136.9 25.1 %collective-permute-start.10 = (bf16[256,2048]{1,0:T(8,128)(2,1)}, bf16[256,2048]{1,0:T(8,128)(2,1)}, u32[]{:S(2)}, u32[]{:S(2)}) collective-permute-start(bf16[256,2048]{1,0:T(8,128)(2,1)} %collective-permute-done.3), channel_id=1, source_target_pairs={{0,4},{4,12},{12,20},{20,28},{28,24},{24,16},{16,8},{8,0},{1,5},{5... | collective-permute-start | bytes 3145736 | tf_op jit(solution)/shard_map/ppermute | solution.py:83
  136.9 28.2 %collective-permute-start.11 = (bf16[256,2048]{1,0:T(8,128)(2,1)}, bf16[256,2048]{1,0:T(8,128)(2,1)}, u32[]{:S(2)}, u32[]{:S(2)}) collective-permute-start(bf16[256,2048]{1,0:T(8,128)(2,1)} %collective-permute-done.4), channel_id=1, source_target_pairs={{4,0},{12,4},{20,12},{28,20},{24,28},{16,24},{8,16},{0,8},{5,1},{1... | collective-permute-start | bytes 3145736 | tf_op jit(solution)/shard_map/ppermute | solution.py:83
  138.4 35.0 %collective-permute-start.12 = (bf16[256,2048]{1,0:T(8,128)(2,1)}, bf16[256,2048]{1,0:T(8,128)(2,1)}, u32[]{:S(2)}, u32[]{:S(2)}) collective-permute-start(bf16[256,2048]{1,0:T(8,128)(2,1)} %param.11), channel_id=1, source_target_pairs={{0,2},{2,0},{1,3},{3,1},{4,6},{6,4},{5,7},{7,5},{8,10},{10,8},{9,1... | collective-permute-start | bytes 3145736 | tf_op jit(solution)/shard_map/ppermute | solution.py:141
  139.6 33.8 %collective-permute-start.13 = (bf16[256,2048]{1,0:T(8,128)(2,1)}, bf16[256,2048]{1,0:T(8,128)(2,1)}, u32[]{:S(2)}, u32[]{:S(2)}) collective-permute-start(bf16[256,2048]{1,0:T(8,128)(2,1)} %collective-permute-done), channel_id=1, source_target_pairs={{0,2},{2,0},{1,3},{3,1},{4,6},{6,4},{5,7},{7,5},{8,10},{10,8},{9,1... | collective-permute-start | bytes 3145736 | tf_op jit(solution)/shard_map/ppermute | solution.py:141
  163.9 13.8 %collective-permute-start.20 = (bf16[128,2048]{1,0:T(8,128)(2,1)}, bf16[128,2048]{1,0:T(8,128)(2,1)}, u32[]{:S(2)}, u32[]{:S(2)}) collective-permute-start(bf16[128,2048]{1,0:T(8,128)(2,1)} %slice.28), channel_id=1, source_target_pairs={{0,4},{4,12},{12,20},{20,28},{28,24},{24,16},{16,8},{8,0},{1,5},{5... | collective-permute-start | bytes 1572872 | tf_op jit(solution)/shard_map/ppermute | solution.py:80
  167.0 14.5 %collective-permute-start.21 = (bf16[128,2048]{1,0:T(8,128)(2,1)}, bf16[128,2048]{1,0:T(8,128)(2,1)}, u32[]{:S(2)}, u32[]{:S(2)}) collective-permute-start(bf16[128,2048]{1,0:T(8,128)(2,1)} %slice.29), channel_id=1, source_target_pairs={{4,0},{12,4},{20,12},{28,20},{24,28},{16,24},{8,16},{0,8},{5,1},{1... | collective-permute-start | bytes 1572872 | tf_op jit(solution)/shard_map/ppermute | solution.py:80
  167.3 19.1 %collective-permute-start.14 = (bf16[256,2048]{1,0:T(8,128)(2,1)}, bf16[256,2048]{1,0:T(8,128)(2,1)}, u32[]{:S(2)}, u32[]{:S(2)}) collective-permute-start(bf16[256,2048]{1,0:T(8,128)(2,1)} %collective-permute-done.1), channel_id=1, source_target_pairs={{0,2},{2,0},{1,3},{3,1},{4,6},{6,4},{5,7},{7,5},{8,10},{10,8},{9,1... | collective-permute-start | bytes 3145736 | tf_op jit(solution)/shard_map/ppermute | solution.py:141
  173.4 13.1 %collective-permute-start.15 = (bf16[256,2048]{1,0:T(8,128)(2,1)}, bf16[256,2048]{1,0:T(8,128)(2,1)S(1)}, u32[]{:S(2)}, u32[]{:S(2)}) collective-permute-start(bf16[256,2048]{1,0:T(8,128)(2,1)} %collective-permute-done.3), channel_id=1, source_target_pairs={{0,2},{2,0},{1,3},{3,1},{4,6},{6,4},{5,7},{7,5},{8,10},{10,8},{9,1... | collective-permute-start | bytes 3145736 | tf_op jit(solution)/shard_map/ppermute | solution.py:141
  173.4 13.1 %collective-permute-start.16 = (bf16[256,2048]{1,0:T(8,128)(2,1)}, bf16[256,2048]{1,0:T(8,128)(2,1)S(1)}, u32[]{:S(2)}, u32[]{:S(2)}) collective-permute-start(bf16[256,2048]{1,0:T(8,128)(2,1)} %collective-permute-done.4), channel_id=1, source_target_pairs={{0,2},{2,0},{1,3},{3,1},{4,6},{6,4},{5,7},{7,5},{8,10},{10,8},{9,1... | collective-permute-start | bytes 3145736 | tf_op jit(solution)/shard_map/ppermute | solution.py:141
  177.7 8.8 %collective-permute-start.17 = (bf16[256,2048]{1,0:T(8,128)(2,1)}, bf16[256,2048]{1,0:T(8,128)(2,1)S(1)}, u32[]{:S(2)}, u32[]{:S(2)}) collective-permute-start(bf16[256,2048]{1,0:T(8,128)(2,1)} %collective-permute-done.10), channel_id=1, source_target_pairs={{0,2},{2,0},{1,3},{3,1},{4,6},{6,4},{5,7},{7,5},{8,10},{10,8},{9,1... | collective-permute-start | bytes 3145736 | tf_op jit(solution)/shard_map/ppermute | solution.py:141
  181.5 5.0 %collective-permute-start.18 = (bf16[256,2048]{1,0:T(8,128)(2,1)}, bf16[256,2048]{1,0:T(8,128)(2,1)S(1)}, u32[]{:S(2)}, u32[]{:S(2)}) collective-permute-start(bf16[256,2048]{1,0:T(8,128)(2,1)} %collective-permute-done.11), channel_id=1, source_target_pairs={{0,2},{2,0},{1,3},{3,1},{4,6},{6,4},{5,7},{7,5},{8,10},{10,8},{9,1... | collective-permute-start | bytes 3145736 | tf_op jit(solution)/shard_map/ppermute | solution.py:141
  186.4 32.7 %collective-permute-start.22 = (bf16[256,2048]{1,0:T(8,128)(2,1)S(1)}, bf16[256,2048]{1,0:T(8,128)(2,1)S(1)}, u32[]{:S(2)}, u32[]{:S(2)}) collective-permute-start(bf16[256,2048]{1,0:T(8,128)(2,1)S(1)} %pad_maximum_fusion.3), channel_id=1, source_target_pairs={{0,2},{2,0},{1,3},{3,1},{4,6},{6,4},{5,7},{7,5},{8,10},{10,8},{9,1... | collective-permute-start | bytes 3145736 | tf_op jit(solution)/shard_map/ppermute | solution.py:141
  188.8 31.3 %collective-permute-start.19 = (bf16[256,2048]{0,1:T(8,128)(2,1)S(1)}, bf16[256,2048]{0,1:T(8,128)(2,1)S(1)}, u32[]{:S(2)}, u32[]{:S(2)}) collective-permute-start(bf16[256,2048]{0,1:T(8,128)(2,1)S(1)} %bitcast.56), channel_id=1, source_target_pairs={{0,1},{1,0},{2,3},{3,2},{4,5},{5,4},{6,7},{7,6},{8,9},{9,8},{10,11... | collective-permute-start | bytes 3145736 | tf_op jit(solution)/shard_map/ppermute | solution.py:177
  (4 other events, 94.3 us)

commit v7 on v3

v7 whole, which is shorter than its diff:
```python
import functools

import jax
import jax.numpy as jnp
from jax import lax
from jax.sharding import Mesh
from jax.sharding import PartitionSpec as P

HEAD_DIM = 128
SWAP = [(0, 1), (1, 0)]


def exclusive_prefix(state, axis, size):
    total = state
    shift = 1
    while shift < size:
        pairs = [(i, i + shift) for i in range(size - shift)]
        total = total + lax.ppermute(total, axis, pairs)
        shift *= 2
    return total - state


def pair_order(own, other, place, axis):
    first = jnp.where(place == 0, own, other)
    second = jnp.where(place == 0, other, own)
    return jnp.concatenate([first, second], axis=axis)


def head_blocks(arrays, n_head, place):
    if n_head == 2:
        rows = arrays[0].shape[0]
        width = arrays[0].shape[1] // 2
        stacked = jnp.stack(arrays).reshape(len(arrays), rows, 2, width)
        own = lax.dynamic_index_in_dim(stacked, place, 2, False)
        sent = lax.dynamic_index_in_dim(stacked, 1 - place, 2, False)
        other = lax.ppermute(sent, "head", SWAP)
        block = pair_order(own, other, place, 1)
        return [block[i] for i in range(len(arrays))]
    return [
        lax.all_to_all(a, "head", split_axis=1, concat_axis=0, tiled=True) for a in arrays
    ]


def chip_cycle(devices):
    n = devices.shape[0]
    coords = [getattr(devices[j, 0, 0], "coords", None) for j in range(n)]
    if n < 4 or n > 16 or any(c is None for c in coords):
        return None

    def adjacent(a, b):
        return sum(abs(int(u) - int(v)) for u, v in zip(coords[a], coords[b])) == 1

    path = [0]

    def search():
        if len(path) == n:
            return adjacent(path[-1], path[0])
        for k in range(n):
            if k not in path and adjacent(path[-1], k):
                path.append(k)
                if search():
                    return True
                path.pop()
        return False

    return list(path) if search() else None


def ring_links(order):
    n = len(order)
    forward = [(order[i], order[(i + 1) % n]) for i in range(n)]
    backward = [(order[(i + 1) % n], order[i]) for i in range(n)]
    return forward, backward


def ring_step(ahead, behind, order, last=False):
    forward, backward = ring_links(order)
    if last:
        half_rows = ahead.shape[0] // 2
        return lax.ppermute(ahead[:half_rows], "chip", forward), lax.ppermute(
            behind[half_rows:], "chip", backward
        )
    return lax.ppermute(ahead, "chip", forward), lax.ppermute(behind, "chip", backward)


def within_block_part(query_heads, key_heads, value_heads):
    row_count = query_heads.shape[0]
    block_rows = min(512, row_count)
    parts_list = []
    for first_row in range(0, row_count, block_rows):
        last_row = min(first_row + block_rows, row_count)
        scores = jnp.einsum(
            "thd,shd->hts",
            query_heads[first_row:last_row],
            key_heads[:last_row],
            preferred_element_type=jnp.float32,
        )
        row_index = first_row + lax.broadcasted_iota(jnp.int32, (last_row - first_row, last_row), 0)
        col_index = lax.broadcasted_iota(jnp.int32, (last_row - first_row, last_row), 1)
        scores = jnp.where((col_index <= row_index)[None], scores, jnp.zeros_like(scores)).astype(
            jnp.bfloat16
        )
        parts_list.append(
            jnp.einsum(
                "hts,she->the", scores, value_heads[:last_row], preferred_element_type=jnp.float32
            )
        )
    return jnp.concatenate(parts_list, axis=0)


def normalize(query_heads, prefix, within_block, norm_gain):
    heads_dev = query_heads.shape[1]
    carried = jnp.einsum(
        "thd,hde->the", query_heads, prefix.astype(jnp.bfloat16), preferred_element_type=jnp.float32
    )
    attended = carried + within_block
    mean_square = jnp.mean(attended * attended, axis=2, keepdims=True)
    gain_heads = norm_gain.reshape(heads_dev, HEAD_DIM)
    normed = (attended * lax.rsqrt(mean_square + 1e-06) * gain_heads[None]).astype(jnp.bfloat16)
    return normed.reshape(query_heads.shape[0], heads_dev * HEAD_DIM)


def gather_head(normed, n_head, place):
    if n_head == 2:
        other = lax.ppermute(normed, "head", SWAP)
        return pair_order(normed, other, place, 1)
    return lax.all_gather(normed, "head", axis=1, tiled=True)


def chip_scan(kv_state, core, n_chip):
    partner_state = lax.ppermute(kv_state, "core", SWAP)
    chip_state = kv_state + partner_state
    half = kv_state.shape[0] // 2
    chip_half = lax.dynamic_slice_in_dim(chip_state, core * half, half, 0)
    return partner_state, chip_half


def chip_finish(chip_prefix_half, partner_state, core):
    other_half = lax.ppermute(chip_prefix_half, "core", SWAP)
    chip_prefix = pair_order(chip_prefix_half, other_half, core, 0)
    return chip_prefix + jnp.where(core == 1, partner_state, jnp.zeros_like(partner_state))


def split_heads(block, heads_dev):
    return block.reshape(block.shape[0], heads_dev, HEAD_DIM)


def local_gather(queries, keys, values, out_weight, norm_gain, n_chip, n_head):
    heads_dev = norm_gain.shape[0] // HEAD_DIM
    core = lax.axis_index("core")
    place = lax.axis_index("head") if n_head == 2 else 0
    weight_own = lax.all_gather(out_weight, "chip", axis=0, tiled=True)
    query_block, key_block, value_block = head_blocks([queries, keys, values], n_head, place)
    query_heads, key_heads, value_heads = (
        split_heads(b, heads_dev) for b in (query_block, key_block, value_block)
    )
    kv_state = jnp.einsum(
        "thd,the->hde", key_heads, value_heads, preferred_element_type=jnp.float32
    )
    partner_state, chip_half = chip_scan(kv_state, core, n_chip)
    prefix = chip_finish(exclusive_prefix(chip_half, "chip", n_chip), partner_state, core)
    within_block = within_block_part(query_heads, key_heads, value_heads)
    normed = normalize(query_heads, prefix, within_block, norm_gain)
    gathered = gather_head(normed, n_head, place)
    row_count = gathered.shape[0]
    split = gathered.reshape(row_count, n_chip, 2, out_weight.shape[0])
    weight_own, split = lax.optimization_barrier((weight_own, split))
    weight_other = lax.ppermute(weight_own, "core", SWAP)
    normed_own = lax.dynamic_index_in_dim(split, core, 2, False).reshape(row_count, -1)
    normed_other = lax.dynamic_index_in_dim(split, 1 - core, 2, False).reshape(row_count, -1)
    outcome = jnp.dot(normed_own, weight_own, preferred_element_type=jnp.float32)
    outcome = outcome + jnp.dot(normed_other, weight_other, preferred_element_type=jnp.float32)
    return outcome.astype(jnp.bfloat16)


def local_ring(queries, keys, values, out_weight, norm_gain, n_chip, n_head, order):
    heads_dev = norm_gain.shape[0] // HEAD_DIM
    core = lax.axis_index("core")
    place = lax.axis_index("head")
    n_steps = n_chip // 2
    barrier = lax.optimization_barrier
    key_block, value_block = head_blocks([keys, values], n_head, place)
    ahead, behind = ring_step(out_weight, out_weight, order)
    ahead, behind, key_block, value_block = barrier((ahead, behind, key_block, value_block))
    got = [out_weight, ahead, behind]
    offsets = [0, 1, -1]
    (query_block,) = head_blocks([queries], n_head, place)
    ahead, behind = ring_step(ahead, behind, order, last=n_steps == 2)
    swapped = [lax.ppermute(w, "core", SWAP) for w in got]
    key_heads, value_heads = split_heads(key_block, heads_dev), split_heads(value_block, heads_dev)
    kv_state = jnp.einsum(
        "thd,the->hde", key_heads, value_heads, preferred_element_type=jnp.float32
    )
    partner_state, chip_half = chip_scan(kv_state, core, n_chip)
    ahead, behind, swapped, partner_state, chip_half = barrier(
        (ahead, behind, swapped, partner_state, chip_half)
    )
    if n_steps == 2:
        got.append(jnp.concatenate([ahead, behind], 0))
        offsets.append(2)
    else:
        got += [ahead, behind]
        offsets += [2, -2]
    chip_prefix_half = exclusive_prefix(chip_half, "chip", n_chip)
    query_heads = split_heads(query_block, heads_dev)
    within_block = within_block_part(query_heads, key_heads, value_heads)
    swapped += [lax.ppermute(w, "core", SWAP) for w in got[len(swapped):]]
    chip_prefix_half, within_block, swapped = barrier((chip_prefix_half, within_block, swapped))
    for step in range(3, n_steps + 1):
        ahead, behind = ring_step(ahead, behind, order, last=step == n_steps)
        if step == n_steps:
            got.append(jnp.concatenate([ahead, behind], 0))
            offsets.append(step)
        else:
            got += [ahead, behind]
            offsets += [step, -step]
    swapped += [lax.ppermute(w, "core", SWAP) for w in got[len(swapped):]]
    prefix = chip_finish(chip_prefix_half, partner_state, core)
    normed = normalize(query_heads, prefix, within_block, norm_gain)
    gathered = gather_head(normed, n_head, place)
    row_count = gathered.shape[0]
    split = gathered.reshape(row_count, n_chip, 2, out_weight.shape[0])
    ring_place = jnp.asarray([order.index(j) for j in range(n_chip)], jnp.int32)[lax.axis_index("chip")]
    sources = jnp.asarray(order, jnp.int32)[(ring_place - jnp.asarray(offsets, jnp.int32)) % n_chip]
    by_offset = jnp.take(split, sources, axis=1)
    normed_own = lax.dynamic_index_in_dim(by_offset, core, 2, False)
    normed_other = lax.dynamic_index_in_dim(by_offset, 1 - core, 2, False)
    outcome = None
    for i in range(len(offsets)):
        part = jnp.dot(normed_own[:, i], got[i], preferred_element_type=jnp.float32)
        part = part + jnp.dot(normed_other[:, i], swapped[i], preferred_element_type=jnp.float32)
        outcome = part if outcome is None else outcome + part
    return outcome.astype(jnp.bfloat16)


def solution(mesh):
    n_seq = mesh.shape["seq"]
    n_head = mesh.shape["head"]
    fine = Mesh(mesh.devices.reshape(n_seq // 2, 2, n_head), ("chip", "core", "head"))
    rows = ("chip", "core", "head")
    order = chip_cycle(fine.devices) if n_head == 2 else None
    if order is None:
        body = functools.partial(local_gather, n_chip=n_seq // 2, n_head=n_head)
    else:
        body = functools.partial(local_ring, n_chip=n_seq // 2, n_head=n_head, order=order)
    return jax.shard_map(
        body,
        mesh=fine,
        in_specs=(
            P(rows, None),
            P(rows, None),
            P(rows, None),
            P(("chip", "core"), "head"),
            P("head"),
        ),
        out_specs=P(("chip", "core"), "head"),
        check_vma=False,
    )
```

time: 230 us -> 198 us (0.86); the launches traced: 226 us -> 196 us
  waiting for transfers between devices: 155 us -> 112 us
  matrix products: 17.5 us -> 31.3 us
  between operations: 13.6 us -> 0.43 us
  starting transfers between devices: 16.1 us -> 25.3 us
  local copies, waits for them, and re-layouts: 11.1 us -> 16.8 us
    ppermute x3, waiting for transfers between devices: 98.3 us -> 36.9 us  [exclusive_prefix(): total = total + lax.ppermute(total, axis, pairs)]
    ppermute x4 -> x19, waiting for transfers between devices: 33 us -> 54 us  [the longest x3 38.3 us: ring_step(): lax.ppermute(ahead, 'chip', forward)]
    dot_general x5 -> x19, matrix products: 17.5 us -> 31.3 us  [the longest x8 14.6 us: local_ring(): jnp.dot(normed_other[:, i], swapped[i], preferred_element_type=jnp.float32)]
    ppermute x4 -> x19, starting transfers between devices: 5.22 us -> 17 us  [the longest x5 5.42 us: local_ring(): swapped += [lax.ppermute(w, 'core', SWAP) for w in got[len(swapped):]]]
    gather x0 -> x2, local copies, waits for them, and re-layouts: none -> 2.68 us  [the longest x1 2.04 us: local_ring(): by_offset = jnp.take(split, sources, axis=1)]
    select_n x0 -> x4, other arithmetic: none -> 2.64 us  [the longest x2 1.86 us: local_ring(): by_offset = jnp.take(split, sources, axis=1)]
    select_n x4 -> x3, other arithmetic: 4.15 us -> 1.56 us  [pair_order(): first = jnp.where(place == 0, own, other)]
    unnamed x11 -> x24, local copies, waits for them, and re-layouts: 2.73 us -> 5.13 us
  transfers between devices with their start and end apart: 10 -> 24, of which waited for: 7 -> 12; matrix products, arithmetic and copies ran while one was open for 15% -> 24% of each run, Pallas kernels for 0% -> 0%
where the time goes in v7:
time: 198 us; the launch traced here: 196 us
  waiting for transfers between devices  112 us (57%)
  matrix products  31.3 us (16%)
  starting transfers between devices  25.3 us (13%)
  local copies, waits for them, and re-layouts  16.8 us (8%)
  other arithmetic  10.4 us (5%)
    ppermute x3, waiting for transfers between devices, ring_step(): lax.ppermute(ahead, 'chip', forward)  38.3 us
    ppermute x3, waiting for transfers between devices, exclusive_prefix(): total = total + lax.ppermute(total, axis, pairs)  36.9 us
    ppermute x2, waiting for transfers between devices, head_blocks(): other = lax.ppermute(sent, 'head', SWAP)  21.1 us
    dot_general x8, matrix products, local_ring(): jnp.dot(normed_other[:, i], swapped[i], preferred_element_type=jnp.float32)  14.6 us
    dot_general x8, matrix products, local_ring(): part = jnp.dot(normed_own[:, i], got[i], preferred_element_type=jnp.float32)  12.4 us
    ppermute x1, waiting for transfers between devices, ring_step(): lax.ppermute(ahead[:half_rows], 'chip', forward)  8.28 us
    ppermute x3, starting transfers between devices, exclusive_prefix(): total = total + lax.ppermute(total, axis, pairs)  6.88 us
    ppermute x5, starting transfers between devices, local_ring(): swapped += [lax.ppermute(w, 'core', SWAP) for w in got[len(swapped):]]  5.42 us
  transfers between devices with their start and end apart: 24, of which 12 were waited for; matrix products, arithmetic and copies ran while one was open for 24% of the time, Pallas kernels for 0%

profile of v7, /device:TPU:13, one launch (start us, length us, event | category | flops | bytes accessed | tf_op | source)
XLA Modules:
  0.0 196.4 jit_solution(10172255700592348960)
XLA Ops:
  3.6 2.3 %copy.20 = bf16[2,128,1,2048]{3,1,0,2:T(8,128)(2,1)} copy(bf16[2,128,1,2048]{1,3,2,0:T(8,128)(2,1)} %get-tuple-element.50) | data formatting | bytes 2097152 | tf_op jit(solution)/shard_map/jit(dynamic_index_in_dim)/dynamic_slice | solution.py:35
  9.0 21.1 %collective-permute-done.2 = bf16[2,128,2048]{2,1,0:T(8,128)(2,1)S(1)} collective-permute-done((bf16[2,128,2048]{2,1,0:T(8,128)(2,1)}, bf16[2,128,2048]{2,1,0:T(8,128)(2,1)S(1)}, u32[]{:S(2)}, u32[]{:S(2)}) %collective-permute-start.2) | collective-permute-done | bytes 1048608 | tf_op jit(solution)/shard_map/ppermute | solution.py:36
  33.1 2.2 %collective-permute-start.8 = (f32[16,128,128]{2,1,0:T(8,128)S(1)}, f32[16,128,128]{2,1,0:T(8,128)S(1)}, u32[]{:S(2)}, u32[]{:S(2)}) collective-permute-start(f32[16,128,128]{2,1,0:T(8,128)S(1)} %fusion.14), channel_id=1, source_target_pairs={{0,2},{2,0},{1,3},{3,1},{4,6},{6,4},{5,7},{7,5},{8,10},{10,8},{9,1... | collective-permute-start | bytes 3145736 | tf_op jit(solution)/shard_map/ppermute | solution.py:131
  42.4 17.6 %collective-permute-done.3 = bf16[256,2048]{1,0:T(8,128)(2,1)} collective-permute-done((bf16[256,2048]{1,0:T(8,128)(2,1)}, bf16[256,2048]{1,0:T(8,128)(2,1)}, u32[]{:S(2)}, u32[]{:S(2)}) %collective-permute-start.3) | collective-permute-done | bytes 1048608 | tf_op jit(solution)/shard_map/ppermute | solution.py:83
  60.0 2.5 %collective-permute-done.4 = bf16[256,2048]{1,0:T(8,128)(2,1)} collective-permute-done((bf16[256,2048]{1,0:T(8,128)(2,1)}, bf16[256,2048]{1,0:T(8,128)(2,1)}, u32[]{:S(2)}, u32[]{:S(2)}) %collective-permute-start.4) | collective-permute-done | bytes 1048608 | tf_op jit(solution)/shard_map/ppermute | solution.py:83
  62.5 1.9 collective-permute-start.9
  65.8 11.3 %collective-permute-done.9 = f32[8,128,128]{2,1,0:T(8,128)S(1)} collective-permute-done((f32[8,128,128]{2,1,0:T(8,128)S(1)}, f32[8,128,128]{2,1,0:T(8,128)S(1)}, u32[]{:S(2)}, u32[]{:S(2)}) %collective-permute-start.9) | collective-permute-done | bytes 524320 | tf_op jit(solution)/shard_map/ppermute | solution.py:18
  77.1 2.1 %collective-permute-start.10 = (f32[8,128,128]{2,1,0:T(8,128)S(1)}, f32[8,128,128]{2,1,0:T(8,128)S(1)}, u32[]{:S(2)}, u32[]{:S(2)}) collective-permute-start(f32[8,128,128]{2,1,0:T(8,128)S(1)} %add.131), channel_id=1, source_target_pairs={{0,8},{4,12},{8,16},{12,20},{16,24},{20,28},{1,9},{5,13},{9,17},{1... | collective-permute-start | bytes 1572872 | tf_op jit(solution)/shard_map/ppermute | solution.py:18
  79.5 2.0 %collective-permute-start.13 = (bf16[256,2048]{1,0:T(8,128)(2,1)}, bf16[256,2048]{1,0:T(8,128)(2,1)}, u32[]{:S(2)}, u32[]{:S(2)}) collective-permute-start(bf16[256,2048]{1,0:T(8,128)(2,1)} %collective-permute-done.3), channel_id=1, source_target_pairs={{0,2},{2,0},{1,3},{3,1},{4,6},{6,4},{5,7},{7,5},{8,10},{10,8},{9,1... | collective-permute-start | bytes 3145736 | tf_op jit(solution)/shard_map/ppermute | solution.py:207
  81.7 9.1 %collective-permute-done.10 = f32[8,128,128]{2,1,0:T(8,128)S(1)} collective-permute-done((f32[8,128,128]{2,1,0:T(8,128)S(1)}, f32[8,128,128]{2,1,0:T(8,128)S(1)}, u32[]{:S(2)}, u32[]{:S(2)}) %collective-permute-start.10) | collective-permute-done | bytes 524320 | tf_op jit(solution)/shard_map/ppermute | solution.py:18
  91.6 2.8 %collective-permute-start.11 = (f32[8,128,128]{2,1,0:T(8,128)}, f32[8,128,128]{2,1,0:T(8,128)}, u32[]{:S(2)}, u32[]{:S(2)}) collective-permute-start(f32[8,128,128]{2,1,0:T(8,128)} %add.132), channel_id=1, source_target_pairs={{0,16},{4,20},{8,24},{12,28},{1,17},{5,21},{9,25},{13,29},{2,18},{... | collective-permute-start | bytes 1572872 | tf_op jit(solution)/shard_map/ppermute | solution.py:18
  95.9 3.2 %fusion.9 = f32[256,16,128]{0,2,1:T(8,128)S(1)} fusion(bf16[256,16,128]{0,2,1:T(8,128)(2,1)} %bitcast.128, bf16[256,16,128]{0,2,1:T(8,128)(2,1)} %bitcast.132, pred[256,256]{1,0:T(8,128)(4,1)S(1)} %iota_compare_fusion, bf16[256,2048]{1,0:T(8,128)(2,1)} %copy-done.2), kind=kOutput, calls=%fused_computation.31 | convolution fusion | flops 538968064 | bytes 5308416 | tf_op jit(solution)/shard_map/hts,she->the/dot_general | solution.py:104
  99.2 16.6 %collective-permute-done.11 = f32[8,128,128]{2,1,0:T(8,128)} collective-permute-done((f32[8,128,128]{2,1,0:T(8,128)}, f32[8,128,128]{2,1,0:T(8,128)}, u32[]{:S(2)}, u32[]{:S(2)}) %collective-permute-start.11) | collective-permute-done | bytes 524320 | tf_op jit(solution)/shard_map/ppermute | solution.py:18
  115.8 2.1 %add_subtract_fusion = f32[8,128,128]{2,1,0:T(8,128)} fusion(f32[8,128,128]{2,1,0:T(8,128)S(1)} %dynamic-slice_add_fusion, f32[8,128,128]{2,1,0:T(8,128)} %add.132, f32[8,128,128]{2,1,0:T(8,128)} %collective-permute-done.11), kind=kLoop, calls=%fused_computation.57 | loop fusion | flops 262144 | bytes 2097152 | tf_op jit(solution)/shard_map/sub | solution.py:20
  125.8 20.1 %collective-permute-done.17 = bf16[256,2048]{1,0:T(8,128)(2,1)} collective-permute-done((bf16[256,2048]{1,0:T(8,128)(2,1)}, bf16[256,2048]{1,0:T(8,128)(2,1)}, u32[]{:S(2)}, u32[]{:S(2)}) %collective-permute-start.17) | collective-permute-done | bytes 1048608 | tf_op jit(solution)/shard_map/ppermute | solution.py:83
  151.4 8.3 %collective-permute-done.21 = bf16[128,2048]{1,0:T(8,128)(2,1)S(1)} collective-permute-done((bf16[128,2048]{1,0:T(8,128)(2,1)S(1)}, bf16[128,2048]{1,0:T(8,128)(2,1)S(1)}, u32[]{:S(2)}, u32[]{:S(2)}) %collective-permute-start.21) | collective-permute-done | bytes 524320 | tf_op jit(solution)/shard_map/ppermute | solution.py:80
  159.7 3.2 %collective-permute-done.22 = bf16[128,2048]{1,0:T(8,128)(2,1)S(1)} collective-permute-done((bf16[128,2048]{1,0:T(8,128)(2,1)S(1)}, bf16[128,2048]{1,0:T(8,128)(2,1)S(1)}, u32[]{:S(2)}, u32[]{:S(2)}) %collective-permute-start.22) | collective-permute-done | bytes 524320 | tf_op jit(solution)/shard_map/ppermute | solution.py:80
  162.9 1.8 collective-permute-start.23
  165.1 2.0 %gather_fusion.1 = bf16[8,256,2,256]{1,3,2,0:T(8,128)(2,1)} fusion(bf16[256,8,2,256]{0,3,2,1:T(8,128)(2,1)S(1)} %bitcast.125, s32[1024]{0:T(1024)S(1)} %pad_clamp_fusion), kind=kCustom, calls=%fused_computation.1 | custom fusion | bytes 4194336 | tf_op jit(solution)/shard_map/jit(_take)/gather | solution.py:225
  167.1 1.9 broadcast_select_fusion
  179.8 1.7 fusion.6
  183.2 1.8 fusion.4
  191.8 1.8 fusion.2
  193.6 2.7 %fusion.7 = bf16[256,2048]{1,0:T(8,128)(2,1)} fusion(f32[256,2048]{1,0:T(8,128)S(1)} %convolution_add_fusion, f32[256,2048]{1,0:T(8,128)S(1)} %fusion.2, f32[256,2048]{1,0:T(8,128)S(1)} %fusion.28, bf16[256,2048]{1,0:T(8,128)(2,1)} %collective-permute-done.20, bf16[256,8,256]{0,2,1:T(8,128)(2,1)S(1)} %get-tuple-element.42), kind=kOutput, calls=%fused_computation.18 | convolution fusion | flops 270532608 | bytes 8519680 | tf_op jit(solution)/shard_map/dot_general | solution.py:231
  (102 shorter events, 53.8 us)
Async XLA Ops:
  5.8 24.3 %collective-permute-start.2 = (bf16[2,128,2048]{2,1,0:T(8,128)(2,1)}, bf16[2,128,2048]{2,1,0:T(8,128)(2,1)S(1)}, u32[]{:S(2)}, u32[]{:S(2)}) collective-permute-start(bf16[2,128,2048]{2,1,0:T(8,128)(2,1)} %bitcast.4), channel_id=1, source_target_pairs={{0,1},{1,0},{2,3},{3,2},{4,5},{5,4},{6,7},{7,6},{8,9},{9,8},{10,11... | collective-permute-start | bytes 3145736 | tf_op jit(solution)/shard_map/ppermute | solution.py:36
  7.1 24.0 %collective-permute-start = (bf16[256,2048]{1,0:T(8,128)(2,1)}, bf16[256,2048]{1,0:T(8,128)(2,1)}, u32[]{:S(2)}, u32[]{:S(2)}) collective-permute-start(bf16[256,2048]{1,0:T(8,128)(2,1)} %param.11), channel_id=1, source_target_pairs={{0,4},{4,12},{12,20},{20,28},{28,24},{24,16},{16,8},{8,0},{1,5},{5... | collective-permute-start | bytes 3145736 | tf_op jit(solution)/shard_map/ppermute | solution.py:83
  8.3 23.7 %collective-permute-start.1 = (bf16[256,2048]{1,0:T(8,128)(2,1)}, bf16[256,2048]{1,0:T(8,128)(2,1)}, u32[]{:S(2)}, u32[]{:S(2)}) collective-permute-start(bf16[256,2048]{1,0:T(8,128)(2,1)} %param.11), channel_id=1, source_target_pairs={{4,0},{12,4},{20,12},{28,20},{24,28},{16,24},{8,16},{0,8},{5,1},{1... | collective-permute-start | bytes 3145736 | tf_op jit(solution)/shard_map/ppermute | solution.py:83
  33.1 5.2 %collective-permute-start.8 = (f32[16,128,128]{2,1,0:T(8,128)S(1)}, f32[16,128,128]{2,1,0:T(8,128)S(1)}, u32[]{:S(2)}, u32[]{:S(2)}) collective-permute-start(f32[16,128,128]{2,1,0:T(8,128)S(1)} %fusion.14), channel_id=1, source_target_pairs={{0,2},{2,0},{1,3},{3,1},{4,6},{6,4},{5,7},{7,5},{8,10},{10,8},{9,1... | collective-permute-start | bytes 3145736 | tf_op jit(solution)/shard_map/ppermute | solution.py:131
  35.3 7.1 %collective-permute-start.5 = (bf16[256,2048]{1,0:T(8,128)(2,1)}, bf16[256,2048]{1,0:T(8,128)(2,1)}, u32[]{:S(2)}, u32[]{:S(2)}) collective-permute-start(bf16[256,2048]{1,0:T(8,128)(2,1)} %param.11), channel_id=1, source_target_pairs={{0,2},{2,0},{1,3},{3,1},{4,6},{6,4},{5,7},{7,5},{8,10},{10,8},{9,1... | collective-permute-start | bytes 3145736 | tf_op jit(solution)/shard_map/ppermute | solution.py:189
  35.4 24.6 %collective-permute-start.3 = (bf16[256,2048]{1,0:T(8,128)(2,1)}, bf16[256,2048]{1,0:T(8,128)(2,1)}, u32[]{:S(2)}, u32[]{:S(2)}) collective-permute-start(bf16[256,2048]{1,0:T(8,128)(2,1)} %collective-permute-done), channel_id=1, source_target_pairs={{0,4},{4,12},{12,20},{20,28},{28,24},{24,16},{16,8},{8,0},{1,5},{5... | collective-permute-start | bytes 3145736 | tf_op jit(solution)/shard_map/ppermute | solution.py:83
  36.7 25.8 %collective-permute-start.6 = (bf16[256,2048]{1,0:T(8,128)(2,1)}, bf16[256,2048]{1,0:T(8,128)(2,1)}, u32[]{:S(2)}, u32[]{:S(2)}) collective-permute-start(bf16[256,2048]{1,0:T(8,128)(2,1)} %collective-permute-done), channel_id=1, source_target_pairs={{0,2},{2,0},{1,3},{3,1},{4,6},{6,4},{5,7},{7,5},{8,10},{10,8},{9,1... | collective-permute-start | bytes 3145736 | tf_op jit(solution)/shard_map/ppermute | solution.py:189
  37.4 25.1 %collective-permute-start.4 = (bf16[256,2048]{1,0:T(8,128)(2,1)}, bf16[256,2048]{1,0:T(8,128)(2,1)}, u32[]{:S(2)}, u32[]{:S(2)}) collective-permute-start(bf16[256,2048]{1,0:T(8,128)(2,1)} %collective-permute-done.1), channel_id=1, source_target_pairs={{4,0},{12,4},{20,12},{28,20},{24,28},{16,24},{8,16},{0,8},{5,1},{1... | collective-permute-start | bytes 3145736 | tf_op jit(solution)/shard_map/ppermute | solution.py:83
  39.3 23.2 %collective-permute-start.7 = (bf16[256,2048]{1,0:T(8,128)(2,1)}, bf16[256,2048]{1,0:T(8,128)(2,1)}, u32[]{:S(2)}, u32[]{:S(2)}) collective-permute-start(bf16[256,2048]{1,0:T(8,128)(2,1)} %collective-permute-done.1), channel_id=1, source_target_pairs={{0,2},{2,0},{1,3},{3,1},{4,6},{6,4},{5,7},{7,5},{8,10},{10,8},{9,1... | collective-permute-start | bytes 3145736 | tf_op jit(solution)/shard_map/ppermute | solution.py:189
  62.5 14.6 %collective-permute-start.9 = (f32[8,128,128]{2,1,0:T(8,128)S(1)}, f32[8,128,128]{2,1,0:T(8,128)S(1)}, u32[]{:S(2)}, u32[]{:S(2)}) collective-permute-start(f32[8,128,128]{2,1,0:T(8,128)S(1)} %dynamic-slice_add_fusion), channel_id=1, source_target_pairs={{0,4},{4,8},{8,12},{12,16},{16,20},{20,24},{24,28},{1,5},{5,9},{9,... | collective-permute-start | bytes 1572872 | tf_op jit(solution)/shard_map/ppermute | solution.py:18
  65.6 16.1 %collective-permute-start.12 = (bf16[1,128,2048]{2,1,0:T(8,128)(2,1)}, bf16[1,128,2048]{2,1,0:T(8,128)(2,1)S(1)}, u32[]{:S(2)}, u32[]{:S(2)}) collective-permute-start(bf16[1,128,2048]{2,1,0:T(8,128)(2,1)} %bitcast.9), channel_id=1, source_target_pairs={{0,1},{1,0},{2,3},{3,2},{4,5},{5,4},{6,7},{7,6},{8,9},{9,8},{10,11... | collective-permute-start | bytes 1572872 | tf_op jit(solution)/shard_map/ppermute | solution.py:36
  77.1 13.6 %collective-permute-start.10 = (f32[8,128,128]{2,1,0:T(8,128)S(1)}, f32[8,128,128]{2,1,0:T(8,128)S(1)}, u32[]{:S(2)}, u32[]{:S(2)}) collective-permute-start(f32[8,128,128]{2,1,0:T(8,128)S(1)} %add.131), channel_id=1, source_target_pairs={{0,8},{4,12},{8,16},{12,20},{16,24},{20,28},{1,9},{5,13},{9,17},{1... | collective-permute-start | bytes 1572872 | tf_op jit(solution)/shard_map/ppermute | solution.py:18
  79.5 38.3 %collective-permute-start.13 = (bf16[256,2048]{1,0:T(8,128)(2,1)}, bf16[256,2048]{1,0:T(8,128)(2,1)}, u32[]{:S(2)}, u32[]{:S(2)}) collective-permute-start(bf16[256,2048]{1,0:T(8,128)(2,1)} %collective-permute-done.3), channel_id=1, source_target_pairs={{0,2},{2,0},{1,3},{3,1},{4,6},{6,4},{5,7},{7,5},{8,10},{10,8},{9,1... | collective-permute-start | bytes 3145736 | tf_op jit(solution)/shard_map/ppermute | solution.py:207
  81.6 36.3 %collective-permute-start.14 = (bf16[256,2048]{1,0:T(8,128)(2,1)}, bf16[256,2048]{1,0:T(8,128)(2,1)}, u32[]{:S(2)}, u32[]{:S(2)}) collective-permute-start(bf16[256,2048]{1,0:T(8,128)(2,1)} %collective-permute-done.4), channel_id=1, source_target_pairs={{0,2},{2,0},{1,3},{3,1},{4,6},{6,4},{5,7},{7,5},{8,10},{10,8},{9,1... | collective-permute-start | bytes 3145736 | tf_op jit(solution)/shard_map/ppermute | solution.py:207
  91.6 24.1 %collective-permute-start.11 = (f32[8,128,128]{2,1,0:T(8,128)}, f32[8,128,128]{2,1,0:T(8,128)}, u32[]{:S(2)}, u32[]{:S(2)}) collective-permute-start(f32[8,128,128]{2,1,0:T(8,128)} %add.132), channel_id=1, source_target_pairs={{0,16},{4,20},{8,24},{12,28},{1,17},{5,21},{9,25},{13,29},{2,18},{... | collective-permute-start | bytes 1572872 | tf_op jit(solution)/shard_map/ppermute | solution.py:18
  117.8 4.5 %collective-permute-start.15 = (f32[8,128,128]{2,1,0:T(8,128)}, f32[8,128,128]{2,1,0:T(8,128)}, u32[]{:S(2)}, u32[]{:S(2)}) collective-permute-start(f32[8,128,128]{2,1,0:T(8,128)} %add_subtract_fusion), channel_id=1, source_target_pairs={{0,2},{2,0},{1,3},{3,1},{4,6},{6,4},{5,7},{7,5},{8,10},{10,8},{9,1... | collective-permute-start | bytes 1572872 | tf_op jit(solution)/shard_map/ppermute | solution.py:139
  120.8 25.1 %collective-permute-start.17 = (bf16[256,2048]{1,0:T(8,128)(2,1)}, bf16[256,2048]{1,0:T(8,128)(2,1)}, u32[]{:S(2)}, u32[]{:S(2)}) collective-permute-start(bf16[256,2048]{1,0:T(8,128)(2,1)} %collective-permute-done.3), channel_id=1, source_target_pairs={{0,4},{4,12},{12,20},{20,28},{28,24},{24,16},{16,8},{8,0},{1,5},{5... | collective-permute-start | bytes 3145736 | tf_op jit(solution)/shard_map/ppermute | solution.py:83
  120.8 27.4 %collective-permute-start.19 = (bf16[256,2048]{1,0:T(8,128)(2,1)}, bf16[256,2048]{1,0:T(8,128)(2,1)}, u32[]{:S(2)}, u32[]{:S(2)}) collective-permute-start(bf16[256,2048]{1,0:T(8,128)(2,1)} %collective-permute-done.4), channel_id=1, source_target_pairs={{4,0},{12,4},{20,12},{28,20},{24,28},{16,24},{8,16},{0,8},{5,1},{1... | collective-permute-start | bytes 3145736 | tf_op jit(solution)/shard_map/ppermute | solution.py:83
  124.9 39.9 %collective-permute-start.16 = (bf16[256,2048]{0,1:T(8,128)(2,1)S(1)}, bf16[256,2048]{0,1:T(8,128)(2,1)S(1)}, u32[]{:S(2)}, u32[]{:S(2)}) collective-permute-start(bf16[256,2048]{0,1:T(8,128)(2,1)S(1)} %bitcast.126), channel_id=1, source_target_pairs={{0,1},{1,0},{2,3},{3,2},{4,5},{5,4},{6,7},{7,6},{8,9},{9,8},{10,11... | collective-permute-start | bytes 3145736 | tf_op jit(solution)/shard_map/ppermute | solution.py:125
  147.0 12.7 %collective-permute-start.21 = (bf16[128,2048]{1,0:T(8,128)(2,1)S(1)}, bf16[128,2048]{1,0:T(8,128)(2,1)S(1)}, u32[]{:S(2)}, u32[]{:S(2)}) collective-permute-start(bf16[128,2048]{1,0:T(8,128)(2,1)S(1)} %slice.101), channel_id=1, source_target_pairs={{0,4},{4,12},{12,20},{20,28},{28,24},{24,16},{16,8},{8,0},{1,5},{5... | collective-permute-start | bytes 1572872 | tf_op jit(solution)/shard_map/ppermute | solution.py:80
  149.3 13.6 %collective-permute-start.22 = (bf16[128,2048]{1,0:T(8,128)(2,1)S(1)}, bf16[128,2048]{1,0:T(8,128)(2,1)S(1)}, u32[]{:S(2)}, u32[]{:S(2)}) collective-permute-start(bf16[128,2048]{1,0:T(8,128)(2,1)S(1)} %slice.102), channel_id=1, source_target_pairs={{4,0},{12,4},{20,12},{28,20},{24,28},{16,24},{8,16},{0,8},{5,1},{1... | collective-permute-start | bytes 1572872 | tf_op jit(solution)/shard_map/ppermute | solution.py:80
  149.8 42.0 %collective-permute-start.18 = (bf16[256,2048]{1,0:T(8,128)(2,1)}, bf16[256,2048]{1,0:T(8,128)(2,1)}, u32[]{:S(2)}, u32[]{:S(2)}) collective-permute-start(bf16[256,2048]{1,0:T(8,128)(2,1)} %collective-permute-done.17), channel_id=1, source_target_pairs={{0,2},{2,0},{1,3},{3,1},{4,6},{6,4},{5,7},{7,5},{8,10},{10,8},{9,1... | collective-permute-start | bytes 3145736 | tf_op jit(solution)/shard_map/ppermute | solution.py:217
  151.3 42.3 %collective-permute-start.20 = (bf16[256,2048]{1,0:T(8,128)(2,1)}, bf16[256,2048]{1,0:T(8,128)(2,1)}, u32[]{:S(2)}, u32[]{:S(2)}) collective-permute-start(bf16[256,2048]{1,0:T(8,128)(2,1)} %collective-permute-done.19), channel_id=1, source_target_pairs={{0,2},{2,0},{1,3},{3,1},{4,6},{6,4},{5,7},{7,5},{8,10},{10,8},{9,1... | collective-permute-start | bytes 3145736 | tf_op jit(solution)/shard_map/ppermute | solution.py:217
  162.9 13.0 %collective-permute-start.23 = (bf16[256,2048]{1,0:T(8,128)(2,1)S(1)}, bf16[256,2048]{1,0:T(8,128)(2,1)}, u32[]{:S(2)}, u32[]{:S(2)}) collective-permute-start(bf16[256,2048]{1,0:T(8,128)(2,1)S(1)} %constant_dynamic-update-slice_fusion), channel_id=1, source_target_pairs={{0,2},{2,0},{1,3},{3,1},{4,6},{6,4},{5,7},{7,5},{8,10},{10,8},{9,1... | collective-permute-start | bytes 3145736 | tf_op jit(solution)/shard_map/ppermute | solution.py:217
  (10 other events, 66.8 us)

commit v8 on v7

--- a/solution.py
+++ b/solution.py
@@ -3,6 +3,8 @@
 import jax
 import jax.numpy as jnp
 from jax import lax
+from jax.experimental import pallas as pl
+from jax.experimental.pallas import tpu as pltpu
 from jax.sharding import Mesh
 from jax.sharding import PartitionSpec as P
 
@@ -143,6 +145,46 @@
 
 def split_heads(block, heads_dev):
     return block.reshape(block.shape[0], heads_dev, HEAD_DIM)
+
+
+def project_blocks(normed, blocks, group=4):
+    n = len(blocks)
+    rows, cols = blocks[0].shape
+    tokens = normed.shape[0]
+    def kernel(normed_ref, *refs):
+        block_refs = refs[:n]
+        out_ref, weights, sems, acc = refs[n:]
+        copies = [
+            pltpu.make_async_copy(block_refs[i], weights.at[pl.ds(i * rows, rows), :], sems.at[i])
+            for i in range(n)
+        ]
+        for c in copies:
+            c.start()
+        for g in range(0, n, group):
+            last = min(g + group, n)
+            for i in range(g, last):
+                copies[i].wait()
+            part = jnp.dot(
+                normed_ref[:, g * rows:last * rows],
+                weights[g * rows:last * rows, :],
+                preferred_element_type=jnp.float32,
+            )
+            if g == 0:
+                acc[...] = part
+            else:
+                acc[...] += part
+        out_ref[...] = acc[...].astype(out_ref.dtype)
+    return pl.pallas_call(
+        kernel,
+        out_shape=jax.ShapeDtypeStruct((tokens, cols), jnp.bfloat16),
+        in_specs=[pl.BlockSpec(memory_space=pltpu.VMEM)] + [pl.BlockSpec(memory_space=pl.ANY)] * n,
+        out_specs=pl.BlockSpec(memory_space=pltpu.VMEM),
+        scratch_shapes=[
+            pltpu.VMEM((n * rows, cols), blocks[0].dtype),
+            pltpu.SemaphoreType.DMA((n,)),
+            pltpu.VMEM((tokens, cols), jnp.float32),
+        ],
+    )(normed, *blocks)
 
 
 def local_gather(queries, keys, values, out_weight, norm_gain, n_chip, n_head):
@@ -223,14 +265,8 @@
     ring_place = jnp.asarray([order.index(j) for j in range(n_chip)], jnp.int32)[lax.axis_index("chip")]
     sources = jnp.asarray(order, jnp.int32)[(ring_place - jnp.asarray(offsets, jnp.int32)) % n_chip]
     by_offset = jnp.take(split, sources, axis=1)
-    normed_own = lax.dynamic_index_in_dim(by_offset, core, 2, False)
-    normed_other = lax.dynamic_index_in_dim(by_offset, 1 - core, 2, False)
-    outcome = None
-    for i in range(len(offsets)):
-        part = jnp.dot(normed_own[:, i], got[i], preferred_element_type=jnp.float32)
-        part = part + jnp.dot(normed_other[:, i], swapped[i], preferred_element_type=jnp.float32)
-        outcome = part if outcome is None else outcome + part
-    return outcome.astype(jnp.bfloat16)
+    by_offset = jnp.where(core == 0, by_offset, by_offset[:, :, ::-1]).reshape(row_count, -1)
+    return project_blocks(by_offset, [w for pair in zip(got, swapped) for w in pair])
 
 
 def solution(mesh):

time: 198 us -> 190 us (0.960)
  matrix products: 31.3 us -> 4.27 us
  local copies, waits for them, and re-layouts: 16.8 us -> 28.4 us
  Pallas kernels: 0 us -> 9.75 us
  waiting for transfers between devices: 112 us -> 109 us
  other arithmetic: 10.4 us -> 12.5 us
    dot_general x16 -> x0, matrix products: 27.1 us -> none  [the longest x8 14.6 us: local_ring(): jnp.dot(normed_other[:, i], swapped[i], preferred_element_type=jnp.float32)]
    pallas_call x0 -> x1, Pallas kernels: none -> 9.75 us  [project_blocks(): pl.pallas_call(kernel, out_shape=jax.ShapeDtypeStruct((tokens, cols), jnp...]
    reshape x0 -> x2, local copies, waits for them, and re-layouts: none -> 5.27 us  [the longest x1 2.85 us: local_ring(): jnp.where(core == 0, by_offset, by_offset[:, :, ::-1])]
    select_n x0 -> x1, local copies, waits for them, and re-layouts: none -> 2.16 us  [local_ring(): jnp.where(core == 0, by_offset, by_offset[:, :, ::-1])]
    add x2, other arithmetic: 0.91 us -> 3.01 us  [exclusive_prefix(): total = total + lax.ppermute(total, axis, pairs)]
    unnamed x24 -> x30, local copies, waits for them, and re-layouts: 5.13 us -> 6.6 us
  transfers between devices with their start and end apart: 24 -> 24, of which waited for: 12 -> 12; matrix products, arithmetic and copies ran while one was open for 24% -> 19% of each run, Pallas kernels for 0% -> 0%
where the time goes in v8:
time: 190 us; the launch traced here: 189 us
  waiting for transfers between devices  109 us (57%)
  local copies, waits for them, and re-layouts  28.4 us (15%)
  starting transfers between devices  24.4 us (13%)
  other arithmetic  12.5 us (7%)
  Pallas kernels  9.75 us (5%)
  matrix products  4.27 us (2%)
    ppermute x3, waiting for transfers between devices, ring_step(): lax.ppermute(ahead, 'chip', forward)  37.4 us
    ppermute x3, waiting for transfers between devices, exclusive_prefix(): total = total + lax.ppermute(total, axis, pairs)  35 us
    ppermute x2, waiting for transfers between devices, head_blocks(): other = lax.ppermute(sent, 'head', SWAP)  21.1 us
    pallas_call x1, Pallas kernels, project_blocks(): pl.pallas_call(kernel, out_shape=jax.ShapeDtypeStruct((tokens, cols), jnp...  9.75 us
    ppermute x1, waiting for transfers between devices, ring_step(): lax.ppermute(ahead[:half_rows], 'chip', forward)  8.28 us
    unnamed x30, local copies, waits for them, and re-layouts  6.6 us
    ppermute x3, starting transfers between devices, exclusive_prefix(): total = total + lax.ppermute(total, axis, pairs)  6.08 us
    ppermute x5, starting transfers between devices, local_ring(): swapped += [lax.ppermute(w, 'core', SWAP) for w in got[len(swapped):]]  5.35 us
  transfers between devices with their start and end apart: 24, of which 12 were waited for; matrix products, arithmetic and copies ran while one was open for 19% of the time, Pallas kernels for 0%

profile of v8, /device:TPU:13, one launch (start us, length us, event | category | flops | bytes accessed | tf_op | source)
XLA Modules:
  0.0 189.3 jit_solution(9368730598659837881)
XLA Ops:
  3.6 2.3 %copy.21 = bf16[2,128,1,2048]{3,1,0,2:T(8,128)(2,1)} copy(bf16[2,128,1,2048]{1,3,2,0:T(8,128)(2,1)} %get-tuple-element.48) | data formatting | bytes 2097152 | tf_op jit(solution)/shard_map/jit(dynamic_index_in_dim)/dynamic_slice | solution.py:37
  9.1 21.1 %collective-permute-done.2 = bf16[2,128,2048]{2,1,0:T(8,128)(2,1)S(1)} collective-permute-done((bf16[2,128,2048]{2,1,0:T(8,128)(2,1)}, bf16[2,128,2048]{2,1,0:T(8,128)(2,1)S(1)}, u32[]{:S(2)}, u32[]{:S(2)}) %collective-permute-start.2) | collective-permute-done | bytes 1048608 | tf_op jit(solution)/shard_map/ppermute | solution.py:38
  34.1 2.2 %collective-permute-start.8 = (f32[16,128,128]{2,1,0:T(8,128)S(1)}, f32[16,128,128]{2,1,0:T(8,128)S(1)}, u32[]{:S(2)}, u32[]{:S(2)}) collective-permute-start(f32[16,128,128]{2,1,0:T(8,128)S(1)} %fusion.6), channel_id=1, source_target_pairs={{0,2},{2,0},{1,3},{3,1},{4,6},{6,4},{5,7},{7,5},{8,10},{10,8},{9,1... | collective-permute-start | bytes 3145736 | tf_op jit(solution)/shard_map/ppermute | solution.py:133
  44.1 16.8 %collective-permute-done.3.refs_6_ = bf16[256,2048]{1,0:T(8,128)(2,1)} collective-permute-done((bf16[256,2048]{1,0:T(8,128)(2,1)}, bf16[256,2048]{1,0:T(8,128)(2,1)}, u32[]{:S(2)}, u32[]{:S(2)}) %collective-permute-start.3) | collective-permute-done | bytes 1048608 | tf_op jit(solution)/shard_map/ppermute | solution.py:85
  60.8 2.7 %collective-permute-done.4.refs_8_ = bf16[256,2048]{1,0:T(8,128)(2,1)} collective-permute-done((bf16[256,2048]{1,0:T(8,128)(2,1)}, bf16[256,2048]{1,0:T(8,128)(2,1)}, u32[]{:S(2)}, u32[]{:S(2)}) %collective-permute-start.4) | collective-permute-done | bytes 1048608 | tf_op jit(solution)/shard_map/ppermute | solution.py:85
  63.5 1.9 %collective-permute-start.9 = (f32[8,128,128]{2,1,0:T(8,128)S(1)}, f32[8,128,128]{2,1,0:T(8,128)}, u32[]{:S(2)}, u32[]{:S(2)}) collective-permute-start(f32[8,128,128]{2,1,0:T(8,128)S(1)} %dynamic-slice_add_fusion), channel_id=1, source_target_pairs={{0,4},{4,8},{8,12},{12,16},{16,20},{20,24},{24,28},{1,5},{5,9},{9,... | collective-permute-start | bytes 1572872 | tf_op jit(solution)/shard_map/ppermute | solution.py:20
  67.6 10.6 %collective-permute-done.9 = f32[8,128,128]{2,1,0:T(8,128)} collective-permute-done((f32[8,128,128]{2,1,0:T(8,128)S(1)}, f32[8,128,128]{2,1,0:T(8,128)}, u32[]{:S(2)}, u32[]{:S(2)}) %collective-permute-start.9) | collective-permute-done | bytes 524320 | tf_op jit(solution)/shard_map/ppermute | solution.py:20
  79.3 2.1 %collective-permute-start.10 = (f32[8,128,128]{2,1,0:T(8,128)S(1)}, f32[8,128,128]{2,1,0:T(8,128)}, u32[]{:S(2)}, u32[]{:S(2)}) collective-permute-start(f32[8,128,128]{2,1,0:T(8,128)S(1)} %add.78), channel_id=1, source_target_pairs={{0,8},{4,12},{8,16},{12,20},{16,24},{20,28},{1,9},{5,13},{9,17},{1... | collective-permute-start | bytes 1572872 | tf_op jit(solution)/shard_map/ppermute | solution.py:20
  82.7 2.0 %collective-permute-start.13 = (bf16[256,2048]{1,0:T(8,128)(2,1)}, bf16[256,2048]{1,0:T(8,128)(2,1)}, u32[]{:S(2)}, u32[]{:S(2)}) collective-permute-start(bf16[256,2048]{1,0:T(8,128)(2,1)} %collective-permute-done.3.refs_6_), channel_id=1, source_target_pairs={{0,2},{2,0},{1,3},{3,1},{4,6},{6,4},{5,7},{7,5},{8,10},{10,8},{9,1... | collective-permute-start | bytes 3145736 | tf_op jit(solution)/shard_map/ppermute | solution.py:249
  85.9 7.1 %collective-permute-done.10 = f32[8,128,128]{2,1,0:T(8,128)} collective-permute-done((f32[8,128,128]{2,1,0:T(8,128)S(1)}, f32[8,128,128]{2,1,0:T(8,128)}, u32[]{:S(2)}, u32[]{:S(2)}) %collective-permute-start.10) | collective-permute-done | bytes 524320 | tf_op jit(solution)/shard_map/ppermute | solution.py:20
  93.0 1.9 %add.79 = f32[8,128,128]{2,1,0:T(8,128)} add(f32[8,128,128]{2,1,0:T(8,128)S(1)} %add.78, f32[8,128,128]{2,1,0:T(8,128)} %collective-permute-done.10) | non-fusion elementwise | flops 131072 | bytes 1572864 | tf_op jit(solution)/shard_map/add | solution.py:20
  94.9 2.0 %collective-permute-start.11 = (f32[8,128,128]{2,1,0:T(8,128)}, f32[8,128,128]{2,1,0:T(8,128)S(1)}, u32[]{:S(2)}, u32[]{:S(2)}) collective-permute-start(f32[8,128,128]{2,1,0:T(8,128)} %add.79), channel_id=1, source_target_pairs={{0,16},{4,20},{8,24},{12,28},{1,17},{5,21},{9,25},{13,29},{2,18},{... | collective-permute-start | bytes 1572872 | tf_op jit(solution)/shard_map/ppermute | solution.py:20
  98.4 3.2 %fusion.1 = f32[256,16,128]{0,2,1:T(8,128)S(1)} fusion(bf16[256,16,128]{0,2,1:T(8,128)(2,1)} %bitcast.58, bf16[256,16,128]{0,2,1:T(8,128)(2,1)} %bitcast.62, pred[256,256]{1,0:T(8,128)(4,1)S(1)} %iota_compare_fusion, bf16[256,2048]{1,0:T(8,128)(2,1)} %copy-done.2), kind=kOutput, calls=%fused_computation.16 | convolution fusion | flops 538968064 | bytes 5308416 | tf_op jit(solution)/shard_map/hts,she->the/dot_general | solution.py:106
  101.6 17.4 %collective-permute-done.11 = f32[8,128,128]{2,1,0:T(8,128)S(1)} collective-permute-done((f32[8,128,128]{2,1,0:T(8,128)}, f32[8,128,128]{2,1,0:T(8,128)S(1)}, u32[]{:S(2)}, u32[]{:S(2)}) %collective-permute-start.11) | collective-permute-done | bytes 524320 | tf_op jit(solution)/shard_map/ppermute | solution.py:20
  119.0 1.9 %add_subtract_fusion = f32[8,128,128]{2,1,0:T(8,128)} fusion(f32[8,128,128]{2,1,0:T(8,128)S(1)} %dynamic-slice_add_fusion, f32[8,128,128]{2,1,0:T(8,128)} %add.79, f32[8,128,128]{2,1,0:T(8,128)S(1)} %collective-permute-done.11), kind=kLoop, calls=%fused_computation.40 | loop fusion | flops 262144 | bytes 2097152 | tf_op jit(solution)/shard_map/sub | solution.py:22
  129.0 20.1 %collective-permute-done.17.refs_10_ = bf16[256,2048]{1,0:T(8,128)(2,1)} collective-permute-done((bf16[256,2048]{1,0:T(8,128)(2,1)}, bf16[256,2048]{1,0:T(8,128)(2,1)}, u32[]{:S(2)}, u32[]{:S(2)}) %collective-permute-start.17) | collective-permute-done | bytes 1048608 | tf_op jit(solution)/shard_map/ppermute | solution.py:85
  154.5 8.3 %collective-permute-done.21 = bf16[128,2048]{1,0:T(8,128)(2,1)S(1)} collective-permute-done((bf16[128,2048]{1,0:T(8,128)(2,1)S(1)}, bf16[128,2048]{1,0:T(8,128)(2,1)S(1)}, u32[]{:S(2)}, u32[]{:S(2)}) %collective-permute-start.21) | collective-permute-done | bytes 524320 | tf_op jit(solution)/shard_map/ppermute | solution.py:82
  163.6 2.3 %collective-permute-done.22 = bf16[128,2048]{1,0:T(8,128)(2,1)S(1)} collective-permute-done((bf16[128,2048]{1,0:T(8,128)(2,1)S(1)}, bf16[128,2048]{1,0:T(8,128)(2,1)S(1)}, u32[]{:S(2)}, u32[]{:S(2)}) %collective-permute-start.22) | collective-permute-done | bytes 524320 | tf_op jit(solution)/shard_map/ppermute | solution.py:82
  166.8 1.7 collective-permute-start.23
  168.9 2.4 %copy.33 = bf16[256,8,2,256]{3,0,2,1:T(8,128)(2,1)} copy(bf16[256,8,2,256]{0,3,2,1:T(8,128)(2,1)S(1)} %bitcast.55) | data formatting | bytes 4194304 | tf_op jit(solution)/shard_map/reshape | solution.py:264
  171.3 2.3 %gather_fusion.1 = bf16[8,256,2,256]{3,1,2,0:T(8,128)(2,1)S(1)} fusion(bf16[256,8,2,256]{3,0,2,1:T(8,128)(2,1)} %copy.33, s32[1024]{0:T(1024)S(1)} %pad_clamp_fusion), kind=kCustom, calls=%fused_computation.1 | custom fusion | bytes 4194336 | tf_op jit(solution)/shard_map/jit(_take)/gather | solution.py:267
  174.3 2.2 %copy.34 = bf16[256,8,2,256]{3,2,1,0:T(2,128)(2,1)S(1)} copy(bf16[256,8,2,256]{3,0,2,1:T(8,128)(2,1)S(1)} %reverse_select_fusion) | data formatting | bytes 4194304 | tf_op jit(solution)/shard_map/jit(_where)/select_n | solution.py:268
  176.5 2.9 %reshape.58.normed_ref = bf16[256,4096]{1,0:T(8,128)(2,1)} reshape(bf16[256,8,2,256]{3,2,1,0:T(2,128)(2,1)S(1)} %copy.34) | data formatting | bytes 4194304 | tf_op jit(solution)/shard_map/reshape | solution.py:268
  179.4 9.8 %shard_map.82 = bf16[256,2048]{1,0:T(8,128)(2,1)} custom-call(bf16[256,4096]{1,0:T(8,128)(2,1)} %reshape.58.normed_ref, bf16[256,2048]{1,0:T(8,128)(2,1)} %refs_0_.1, bf16[256,2048]{1,0:T(8,128)(2,1)} %collective-permute-done.5.refs_1_, bf16[256,2048]{1,0:T(8,128)(2,1)} %collective-permute-done.refs_2_, bf16[256,2048]{1,0:T(8,128)(2,1)} %collective-permute-done.6.refs_3_, ...), custom_call_target="tpu_custom_call" | custom-call | tf_op jit(solution)/shard_map/pallas_call | solution.py:177
  (96 shorter events, 41.7 us)
Async XLA Ops:
  5.9 24.3 %collective-permute-start.2 = (bf16[2,128,2048]{2,1,0:T(8,128)(2,1)}, bf16[2,128,2048]{2,1,0:T(8,128)(2,1)S(1)}, u32[]{:S(2)}, u32[]{:S(2)}) collective-permute-start(bf16[2,128,2048]{2,1,0:T(8,128)(2,1)} %bitcast.4), channel_id=1, source_target_pairs={{0,1},{1,0},{2,3},{3,2},{4,5},{5,4},{6,7},{7,6},{8,9},{9,8},{10,11... | collective-permute-start | bytes 3145736 | tf_op jit(solution)/shard_map/ppermute | solution.py:38
  7.1 24.0 %collective-permute-start = (bf16[256,2048]{1,0:T(8,128)(2,1)}, bf16[256,2048]{1,0:T(8,128)(2,1)}, u32[]{:S(2)}, u32[]{:S(2)}) collective-permute-start(bf16[256,2048]{1,0:T(8,128)(2,1)} %refs_0_.1), channel_id=1, source_target_pairs={{0,4},{4,12},{12,20},{20,28},{28,24},{24,16},{16,8},{8,0},{1,5},{5... | collective-permute-start | bytes 3145736 | tf_op jit(solution)/shard_map/ppermute | solution.py:85
  8.4 23.7 %collective-permute-start.1 = (bf16[256,2048]{1,0:T(8,128)(2,1)}, bf16[256,2048]{1,0:T(8,128)(2,1)}, u32[]{:S(2)}, u32[]{:S(2)}) collective-permute-start(bf16[256,2048]{1,0:T(8,128)(2,1)} %refs_0_.1), channel_id=1, source_target_pairs={{4,0},{12,4},{20,12},{28,20},{24,28},{16,24},{8,16},{0,8},{5,1},{1... | collective-permute-start | bytes 3145736 | tf_op jit(solution)/shard_map/ppermute | solution.py:85
  34.1 5.9 %collective-permute-start.8 = (f32[16,128,128]{2,1,0:T(8,128)S(1)}, f32[16,128,128]{2,1,0:T(8,128)S(1)}, u32[]{:S(2)}, u32[]{:S(2)}) collective-permute-start(f32[16,128,128]{2,1,0:T(8,128)S(1)} %fusion.6), channel_id=1, source_target_pairs={{0,2},{2,0},{1,3},{3,1},{4,6},{6,4},{5,7},{7,5},{8,10},{10,8},{9,1... | collective-permute-start | bytes 3145736 | tf_op jit(solution)/shard_map/ppermute | solution.py:133
  36.3 7.8 %collective-permute-start.5 = (bf16[256,2048]{1,0:T(8,128)(2,1)}, bf16[256,2048]{1,0:T(8,128)(2,1)}, u32[]{:S(2)}, u32[]{:S(2)}) collective-permute-start(bf16[256,2048]{1,0:T(8,128)(2,1)} %refs_0_.1), channel_id=1, source_target_pairs={{0,2},{2,0},{1,3},{3,1},{4,6},{6,4},{5,7},{7,5},{8,10},{10,8},{9,1... | collective-permute-start | bytes 3145736 | tf_op jit(solution)/shard_map/ppermute | solution.py:231
  36.3 24.5 %collective-permute-start.3 = (bf16[256,2048]{1,0:T(8,128)(2,1)}, bf16[256,2048]{1,0:T(8,128)(2,1)}, u32[]{:S(2)}, u32[]{:S(2)}) collective-permute-start(bf16[256,2048]{1,0:T(8,128)(2,1)} %collective-permute-done.refs_2_), channel_id=1, source_target_pairs={{0,4},{4,12},{12,20},{20,28},{28,24},{24,16},{16,8},{8,0},{1,5},{5... | collective-permute-start | bytes 3145736 | tf_op jit(solution)/shard_map/ppermute | solution.py:85
  37.6 25.9 %collective-permute-start.6 = (bf16[256,2048]{1,0:T(8,128)(2,1)}, bf16[256,2048]{1,0:T(8,128)(2,1)}, u32[]{:S(2)}, u32[]{:S(2)}) collective-permute-start(bf16[256,2048]{1,0:T(8,128)(2,1)} %collective-permute-done.refs_2_), channel_id=1, source_target_pairs={{0,2},{2,0},{1,3},{3,1},{4,6},{6,4},{5,7},{7,5},{8,10},{10,8},{9,1... | collective-permute-start | bytes 3145736 | tf_op jit(solution)/shard_map/ppermute | solution.py:231
  38.4 25.1 %collective-permute-start.4 = (bf16[256,2048]{1,0:T(8,128)(2,1)}, bf16[256,2048]{1,0:T(8,128)(2,1)}, u32[]{:S(2)}, u32[]{:S(2)}) collective-permute-start(bf16[256,2048]{1,0:T(8,128)(2,1)} %collective-permute-done.1.refs_4_), channel_id=1, source_target_pairs={{4,0},{12,4},{20,12},{28,20},{24,28},{16,24},{8,16},{0,8},{5,1},{1... | collective-permute-start | bytes 3145736 | tf_op jit(solution)/shard_map/ppermute | solution.py:85
  41.0 22.5 %collective-permute-start.7 = (bf16[256,2048]{1,0:T(8,128)(2,1)}, bf16[256,2048]{1,0:T(8,128)(2,1)}, u32[]{:S(2)}, u32[]{:S(2)}) collective-permute-start(bf16[256,2048]{1,0:T(8,128)(2,1)} %collective-permute-done.1.refs_4_), channel_id=1, source_target_pairs={{0,2},{2,0},{1,3},{3,1},{4,6},{6,4},{5,7},{7,5},{8,10},{10,8},{9,1... | collective-permute-start | bytes 3145736 | tf_op jit(solution)/shard_map/ppermute | solution.py:231
  63.5 14.7 %collective-permute-start.9 = (f32[8,128,128]{2,1,0:T(8,128)S(1)}, f32[8,128,128]{2,1,0:T(8,128)}, u32[]{:S(2)}, u32[]{:S(2)}) collective-permute-start(f32[8,128,128]{2,1,0:T(8,128)S(1)} %dynamic-slice_add_fusion), channel_id=1, source_target_pairs={{0,4},{4,8},{8,12},{12,16},{16,20},{20,24},{24,28},{1,5},{5,9},{9,... | collective-permute-start | bytes 1572872 | tf_op jit(solution)/shard_map/ppermute | solution.py:20
  67.3 17.5 %collective-permute-start.12 = (bf16[1,128,2048]{2,1,0:T(8,128)(2,1)}, bf16[1,128,2048]{2,1,0:T(8,128)(2,1)}, u32[]{:S(2)}, u32[]{:S(2)}) collective-permute-start(bf16[1,128,2048]{2,1,0:T(8,128)(2,1)} %bitcast.64), channel_id=1, source_target_pairs={{0,1},{1,0},{2,3},{3,2},{4,5},{5,4},{6,7},{7,6},{8,9},{9,8},{10,11... | collective-permute-start | bytes 1572872 | tf_op jit(solution)/shard_map/ppermute | solution.py:38
  79.3 13.7 %collective-permute-start.10 = (f32[8,128,128]{2,1,0:T(8,128)S(1)}, f32[8,128,128]{2,1,0:T(8,128)}, u32[]{:S(2)}, u32[]{:S(2)}) collective-permute-start(f32[8,128,128]{2,1,0:T(8,128)S(1)} %add.78), channel_id=1, source_target_pairs={{0,8},{4,12},{8,16},{12,20},{16,24},{20,28},{1,9},{5,13},{9,17},{1... | collective-permute-start | bytes 1572872 | tf_op jit(solution)/shard_map/ppermute | solution.py:20
  82.7 38.2 %collective-permute-start.13 = (bf16[256,2048]{1,0:T(8,128)(2,1)}, bf16[256,2048]{1,0:T(8,128)(2,1)}, u32[]{:S(2)}, u32[]{:S(2)}) collective-permute-start(bf16[256,2048]{1,0:T(8,128)(2,1)} %collective-permute-done.3.refs_6_), channel_id=1, source_target_pairs={{0,2},{2,0},{1,3},{3,1},{4,6},{6,4},{5,7},{7,5},{8,10},{10,8},{9,1... | collective-permute-start | bytes 3145736 | tf_op jit(solution)/shard_map/ppermute | solution.py:249
  84.7 36.2 %collective-permute-start.14 = (bf16[256,2048]{1,0:T(8,128)(2,1)}, bf16[256,2048]{1,0:T(8,128)(2,1)}, u32[]{:S(2)}, u32[]{:S(2)}) collective-permute-start(bf16[256,2048]{1,0:T(8,128)(2,1)} %collective-permute-done.4.refs_8_), channel_id=1, source_target_pairs={{0,2},{2,0},{1,3},{3,1},{4,6},{6,4},{5,7},{7,5},{8,10},{10,8},{9,1... | collective-permute-start | bytes 3145736 | tf_op jit(solution)/shard_map/ppermute | solution.py:249
  94.9 24.1 %collective-permute-start.11 = (f32[8,128,128]{2,1,0:T(8,128)}, f32[8,128,128]{2,1,0:T(8,128)S(1)}, u32[]{:S(2)}, u32[]{:S(2)}) collective-permute-start(f32[8,128,128]{2,1,0:T(8,128)} %add.79), channel_id=1, source_target_pairs={{0,16},{4,20},{8,24},{12,28},{1,17},{5,21},{9,25},{13,29},{2,18},{... | collective-permute-start | bytes 1572872 | tf_op jit(solution)/shard_map/ppermute | solution.py:20
  120.9 4.5 %collective-permute-start.15 = (f32[8,128,128]{2,1,0:T(8,128)}, f32[8,128,128]{2,1,0:T(8,128)}, u32[]{:S(2)}, u32[]{:S(2)}) collective-permute-start(f32[8,128,128]{2,1,0:T(8,128)} %add_subtract_fusion), channel_id=1, source_target_pairs={{0,2},{2,0},{1,3},{3,1},{4,6},{6,4},{5,7},{7,5},{8,10},{10,8},{9,1... | collective-permute-start | bytes 1572872 | tf_op jit(solution)/shard_map/ppermute | solution.py:141
  123.9 25.1 %collective-permute-start.17 = (bf16[256,2048]{1,0:T(8,128)(2,1)}, bf16[256,2048]{1,0:T(8,128)(2,1)}, u32[]{:S(2)}, u32[]{:S(2)}) collective-permute-start(bf16[256,2048]{1,0:T(8,128)(2,1)} %collective-permute-done.3.refs_6_), channel_id=1, source_target_pairs={{0,4},{4,12},{12,20},{20,28},{28,24},{24,16},{16,8},{8,0},{1,5},{5... | collective-permute-start | bytes 3145736 | tf_op jit(solution)/shard_map/ppermute | solution.py:85
  124.0 27.3 %collective-permute-start.19 = (bf16[256,2048]{1,0:T(8,128)(2,1)}, bf16[256,2048]{1,0:T(8,128)(2,1)}, u32[]{:S(2)}, u32[]{:S(2)}) collective-permute-start(bf16[256,2048]{1,0:T(8,128)(2,1)} %collective-permute-done.4.refs_8_), channel_id=1, source_target_pairs={{4,0},{12,4},{20,12},{28,20},{24,28},{16,24},{8,16},{0,8},{5,1},{1... | collective-permute-start | bytes 3145736 | tf_op jit(solution)/shard_map/ppermute | solution.py:85
  128.0 40.5 %collective-permute-start.16 = (bf16[256,2048]{0,1:T(8,128)(2,1)S(1)}, bf16[256,2048]{0,1:T(8,128)(2,1)S(1)}, u32[]{:S(2)}, u32[]{:S(2)}) collective-permute-start(bf16[256,2048]{0,1:T(8,128)(2,1)S(1)} %bitcast.56), channel_id=1, source_target_pairs={{0,1},{1,0},{2,3},{3,2},{4,5},{5,4},{6,7},{7,6},{8,9},{9,8},{10,11... | collective-permute-start | bytes 3145736 | tf_op jit(solution)/shard_map/ppermute | solution.py:127
  150.1 12.7 %collective-permute-start.21 = (bf16[128,2048]{1,0:T(8,128)(2,1)S(1)}, bf16[128,2048]{1,0:T(8,128)(2,1)S(1)}, u32[]{:S(2)}, u32[]{:S(2)}) collective-permute-start(bf16[128,2048]{1,0:T(8,128)(2,1)S(1)} %slice.22), channel_id=1, source_target_pairs={{0,4},{4,12},{12,20},{20,28},{28,24},{24,16},{16,8},{8,0},{1,5},{5... | collective-permute-start | bytes 1572872 | tf_op jit(solution)/shard_map/ppermute | solution.py:82
  152.3 13.6 %collective-permute-start.22 = (bf16[128,2048]{1,0:T(8,128)(2,1)S(1)}, bf16[128,2048]{1,0:T(8,128)(2,1)S(1)}, u32[]{:S(2)}, u32[]{:S(2)}) collective-permute-start(bf16[128,2048]{1,0:T(8,128)(2,1)S(1)} %slice.23), channel_id=1, source_target_pairs={{4,0},{12,4},{20,12},{28,20},{24,28},{16,24},{8,16},{0,8},{5,1},{1... | collective-permute-start | bytes 1572872 | tf_op jit(solution)/shard_map/ppermute | solution.py:82
  153.0 26.4 %collective-permute-start.18 = (bf16[256,2048]{1,0:T(8,128)(2,1)}, bf16[256,2048]{1,0:T(8,128)(2,1)}, u32[]{:S(2)}, u32[]{:S(2)}) collective-permute-start(bf16[256,2048]{1,0:T(8,128)(2,1)} %collective-permute-done.17.refs_10_), channel_id=1, source_target_pairs={{0,2},{2,0},{1,3},{3,1},{4,6},{6,4},{5,7},{7,5},{8,10},{10,8},{9,1... | collective-permute-start | bytes 3145736 | tf_op jit(solution)/shard_map/ppermute | solution.py:259
  154.4 24.9 %collective-permute-start.20 = (bf16[256,2048]{1,0:T(8,128)(2,1)}, bf16[256,2048]{1,0:T(8,128)(2,1)}, u32[]{:S(2)}, u32[]{:S(2)}) collective-permute-start(bf16[256,2048]{1,0:T(8,128)(2,1)} %collective-permute-done.19.refs_12_), channel_id=1, source_target_pairs={{0,2},{2,0},{1,3},{3,1},{4,6},{6,4},{5,7},{7,5},{8,10},{10,8},{9,1... | collective-permute-start | bytes 3145736 | tf_op jit(solution)/shard_map/ppermute | solution.py:259
  166.8 12.6 %collective-permute-start.23 = (bf16[256,2048]{1,0:T(8,128)(2,1)}, bf16[256,2048]{1,0:T(8,128)(2,1)}, u32[]{:S(2)}, u32[]{:S(2)}) collective-permute-start(bf16[256,2048]{1,0:T(8,128)(2,1)} %constant_dynamic-update-slice_fusion.refs_14_), channel_id=1, source_target_pairs={{0,2},{2,0},{1,3},{3,1},{4,6},{6,4},{5,7},{7,5},{8,10},{10,8},{9,1... | collective-permute-start | bytes 3145736 | tf_op jit(solution)/shard_map/ppermute | solution.py:259
  (13 other events, 188.1 us)

commit v9 on v8

--- a/solution.py
+++ b/solution.py
@@ -227,28 +227,18 @@
     got = [out_weight, ahead, behind]
     offsets = [0, 1, -1]
     (query_block,) = head_blocks([queries], n_head, place)
-    ahead, behind = ring_step(ahead, behind, order, last=n_steps == 2)
     swapped = [lax.ppermute(w, "core", SWAP) for w in got]
     key_heads, value_heads = split_heads(key_block, heads_dev), split_heads(value_block, heads_dev)
     kv_state = jnp.einsum(
         "thd,the->hde", key_heads, value_heads, preferred_element_type=jnp.float32
     )
     partner_state, chip_half = chip_scan(kv_state, core, n_chip)
-    ahead, behind, swapped, partner_state, chip_half = barrier(
-        (ahead, behind, swapped, partner_state, chip_half)
-    )
-    if n_steps == 2:
-        got.append(jnp.concatenate([ahead, behind], 0))
-        offsets.append(2)
-    else:
-        got += [ahead, behind]
-        offsets += [2, -2]
     chip_prefix_half = exclusive_prefix(chip_half, "chip", n_chip)
     query_heads = split_heads(query_block, heads_dev)
     within_block = within_block_part(query_heads, key_heads, value_heads)
     swapped += [lax.ppermute(w, "core", SWAP) for w in got[len(swapped):]]
     chip_prefix_half, within_block, swapped = barrier((chip_prefix_half, within_block, swapped))
-    for step in range(3, n_steps + 1):
+    for step in range(2, n_steps + 1):
         ahead, behind = ring_step(ahead, behind, order, last=step == n_steps)
         if step == n_steps:
             got.append(jnp.concatenate([ahead, behind], 0))

time: 190 us -> 184 us (0.968)
  waiting for transfers between devices: 109 us -> 91.6 us
  starting transfers between devices: 24.4 us -> 32.5 us
  local copies, waits for them, and re-layouts: 28.4 us -> 30.6 us
    ppermute x3, waiting for transfers between devices: 37.4 us -> 29.6 us  [ring_step(): lax.ppermute(ahead, 'chip', forward)]
    ppermute x1, waiting for transfers between devices: 8.28 us -> 4.55 us  [ring_step(): lax.ppermute(ahead[:half_rows], 'chip', forward)]
    ppermute x5, starting transfers between devices: 5.35 us -> 8.93 us  [local_ring(): swapped += [lax.ppermute(w, 'core', SWAP) for w in got[len(swapped):]]]
    ppermute x3, waiting for transfers between devices: 3.66 us -> 1.01 us  [ring_step(): lax.ppermute(behind, 'chip', backward)]
    ppermute x1, waiting for transfers between devices: 2.32 us -> 0.01 us  [ring_step(): lax.ppermute(behind[half_rows:], 'chip', backward)]
    ppermute x3, starting transfers between devices: 6.08 us -> 8.4 us  [exclusive_prefix(): total = total + lax.ppermute(total, axis, pairs)]
    ppermute x3, waiting for transfers between devices: 35 us -> 32.9 us  [exclusive_prefix(): total = total + lax.ppermute(total, axis, pairs)]
    unnamed x30 -> x28, local copies, waits for them, and re-layouts: 6.6 us -> 6.34 us
  transfers between devices with their start and end apart: 24 -> 24, of which waited for: 12 -> 10; matrix products, arithmetic and copies ran while one was open for 19% -> 21% of each run, Pallas kernels for 0% -> 0%
where the time goes in v9:
time: 184 us; the launch traced here: 182 us
  waiting for transfers between devices  91.6 us (50%)
  starting transfers between devices  32.5 us (18%)
  local copies, waits for them, and re-layouts  30.6 us (17%)
  other arithmetic  11.6 us (6%)
  Pallas kernels  9.75 us (5%)
  matrix products  5.58 us (3%)
    ppermute x3, waiting for transfers between devices, exclusive_prefix(): total = total + lax.ppermute(total, axis, pairs)  32.9 us
    ppermute x3, waiting for transfers between devices, ring_step(): lax.ppermute(ahead, 'chip', forward)  29.6 us
    ppermute x2, waiting for transfers between devices, head_blocks(): other = lax.ppermute(sent, 'head', SWAP)  21.1 us
    pallas_call x1, Pallas kernels, project_blocks(): pl.pallas_call(kernel, out_shape=jax.ShapeDtypeStruct((tokens, cols), jnp...  9.75 us
    ppermute x5, starting transfers between devices, local_ring(): swapped += [lax.ppermute(w, 'core', SWAP) for w in got[len(swapped):]]  8.93 us
    ppermute x3, starting transfers between devices, exclusive_prefix(): total = total + lax.ppermute(total, axis, pairs)  8.4 us
    unnamed x28, local copies, waits for them, and re-layouts  6.34 us
    ppermute x1, waiting for transfers between devices, ring_step(): lax.ppermute(ahead[:half_rows], 'chip', forward)  4.55 us
  transfers between devices with their start and end apart: 24, of which 10 were waited for; matrix products, arithmetic and copies ran while one was open for 21% of the time, Pallas kernels for 0%

profile of v9, /device:TPU:13, one launch (start us, length us, event | category | flops | bytes accessed | tf_op | source)
XLA Modules:
  0.0 182.3 jit_solution(17405780900621450948)
XLA Ops:
  3.6 2.3 %copy.21 = bf16[2,128,1,2048]{3,1,0,2:T(8,128)(2,1)} copy(bf16[2,128,1,2048]{1,3,2,0:T(8,128)(2,1)} %get-tuple-element.30) | data formatting | bytes 2097152 | tf_op jit(solution)/shard_map/jit(dynamic_index_in_dim)/dynamic_slice | solution.py:37
  9.1 21.1 %collective-permute-done.2 = bf16[2,128,2048]{2,1,0:T(8,128)(2,1)S(1)} collective-permute-done((bf16[2,128,2048]{2,1,0:T(8,128)(2,1)}, bf16[2,128,2048]{2,1,0:T(8,128)(2,1)S(1)}, u32[]{:S(2)}, u32[]{:S(2)}) %collective-permute-start.2) | collective-permute-done | bytes 1048608 | tf_op jit(solution)/shard_map/ppermute | solution.py:38
  33.1 2.2 %collective-permute-start.3 = (f32[16,128,128]{2,1,0:T(8,128)S(1)}, f32[16,128,128]{2,1,0:T(8,128)}, u32[]{:S(2)}, u32[]{:S(2)}) collective-permute-start(f32[16,128,128]{2,1,0:T(8,128)S(1)} %fusion.6), channel_id=1, source_target_pairs={{0,2},{2,0},{1,3},{3,1},{4,6},{6,4},{5,7},{7,5},{8,10},{10,8},{9,1... | collective-permute-start | bytes 3145736 | tf_op jit(solution)/shard_map/ppermute | solution.py:133
  35.4 2.4 %collective-permute-done.3 = f32[16,128,128]{2,1,0:T(8,128)} collective-permute-done((f32[16,128,128]{2,1,0:T(8,128)S(1)}, f32[16,128,128]{2,1,0:T(8,128)}, u32[]{:S(2)}, u32[]{:S(2)}) %collective-permute-start.3) | collective-permute-done | bytes 1048608 | tf_op jit(solution)/shard_map/ppermute | solution.py:133
  41.1 2.3 %copy.24 = bf16[128,4096]{0,1:T(8,128)(2,1)} copy(bf16[128,4096]{1,0:T(8,128)(2,1)} %param.8) | data formatting | bytes 2097152 | tf_op args[0]
  43.4 2.3 %constant_dynamic-slice_fusion.1 = (bf16[1,128,1,2048]{1,3,2,0:T(8,128)(2,1)}, bf16[1,128,1,2048]{1,3,2,0:T(8,128)(2,1)}) fusion(bf16[1,128,2,2048]{1,3,2,0:T(8,128)(2,1)} %bitcast.61, s32[]{:T(128)S(6)} %select_n.122, s32[]{:T(128)S(6)} %select_n.123), kind=kLoop, calls=%fused_computation.56 | loop fusion | bytes 2097160 | tf_op jit(solution)/shard_map/jit(dynamic_index_in_dim)/dynamic_slice | solution.py:36
  45.6 8.5 %collective-permute-done.4 = f32[8,128,128]{2,1,0:T(8,128)} collective-permute-done((f32[8,128,128]{2,1,0:T(8,128)S(1)}, f32[8,128,128]{2,1,0:T(8,128)}, u32[]{:S(2)}, u32[]{:S(2)}) %collective-permute-start.4) | collective-permute-done | bytes 524320 | tf_op jit(solution)/shard_map/ppermute | solution.py:20
  55.3 3.2 %collective-permute-start.5 = (f32[8,128,128]{2,1,0:T(8,128)S(1)}, f32[8,128,128]{2,1,0:T(8,128)}, u32[]{:S(2)}, u32[]{:S(2)}) collective-permute-start(f32[8,128,128]{2,1,0:T(8,128)S(1)} %add.78), channel_id=1, source_target_pairs={{0,8},{4,12},{8,16},{12,20},{16,24},{20,28},{1,9},{5,13},{9,17},{1... | collective-permute-start | bytes 1572872 | tf_op jit(solution)/shard_map/ppermute | solution.py:20
  64.5 5.0 %collective-permute-done.5 = f32[8,128,128]{2,1,0:T(8,128)} collective-permute-done((f32[8,128,128]{2,1,0:T(8,128)S(1)}, f32[8,128,128]{2,1,0:T(8,128)}, u32[]{:S(2)}, u32[]{:S(2)}) %collective-permute-start.5) | collective-permute-done | bytes 524320 | tf_op jit(solution)/shard_map/ppermute | solution.py:20
  70.6 3.2 %collective-permute-start.6 = (f32[8,128,128]{2,1,0:T(8,128)S(1)}, f32[8,128,128]{2,1,0:T(8,128)S(1)}, u32[]{:S(2)}, u32[]{:S(2)}) collective-permute-start(f32[8,128,128]{2,1,0:T(8,128)S(1)} %add.79), channel_id=1, source_target_pairs={{0,16},{4,20},{8,24},{12,28},{1,17},{5,21},{9,25},{13,29},{2,18},{... | collective-permute-start | bytes 1572872 | tf_op jit(solution)/shard_map/ppermute | solution.py:20
  76.3 19.3 %collective-permute-done.6 = f32[8,128,128]{2,1,0:T(8,128)S(1)} collective-permute-done((f32[8,128,128]{2,1,0:T(8,128)S(1)}, f32[8,128,128]{2,1,0:T(8,128)S(1)}, u32[]{:S(2)}, u32[]{:S(2)}) %collective-permute-start.6) | collective-permute-done | bytes 524320 | tf_op jit(solution)/shard_map/ppermute | solution.py:20
  96.4 3.3 %fusion.1 = f32[256,16,128]{0,2,1:T(8,128)S(1)} fusion(bf16[256,16,128]{0,2,1:T(8,128)(2,1)} %bitcast.58, bf16[256,16,128]{0,2,1:T(8,128)(2,1)} %bitcast.62, pred[256,256]{1,0:T(8,128)(4,1)S(1)} %iota_compare_fusion, bf16[256,2048]{1,0:T(8,128)(2,1)} %copy-done.2), kind=kOutput, calls=%fused_computation.16 | convolution fusion | flops 538968064 | bytes 5308416 | tf_op jit(solution)/shard_map/hts,she->the/dot_general | solution.py:106
  101.7 2.7 %collective-permute-start.11 = (f32[8,128,128]{2,1,0:T(8,128)}, f32[8,128,128]{2,1,0:T(8,128)}, u32[]{:S(2)}, u32[]{:S(2)}) collective-permute-start(f32[8,128,128]{2,1,0:T(8,128)} %add_subtract_fusion), channel_id=1, source_target_pairs={{0,2},{2,0},{1,3},{3,1},{4,6},{6,4},{5,7},{7,5},{8,10},{10,8},{9,1... | collective-permute-start | bytes 1572872 | tf_op jit(solution)/shard_map/ppermute | solution.py:141
  105.7 12.5 %collective-permute-done.13.refs_6_ = bf16[256,2048]{1,0:T(8,128)(2,1)} collective-permute-done((bf16[256,2048]{1,0:T(8,128)(2,1)}, bf16[256,2048]{1,0:T(8,128)(2,1)}, u32[]{:S(2)}, u32[]{:S(2)}) %collective-permute-start.13) | collective-permute-done | bytes 1048608 | tf_op jit(solution)/shard_map/ppermute | solution.py:85
  125.1 16.5 %collective-permute-done.17.refs_10_ = bf16[256,2048]{1,0:T(8,128)(2,1)} collective-permute-done((bf16[256,2048]{1,0:T(8,128)(2,1)}, bf16[256,2048]{1,0:T(8,128)(2,1)}, u32[]{:S(2)}, u32[]{:S(2)}) %collective-permute-start.17) | collective-permute-done | bytes 1048608 | tf_op jit(solution)/shard_map/ppermute | solution.py:85
  142.7 2.3 %collective-permute-start.21 = (bf16[128,2048]{1,0:T(8,128)(2,1)S(1)}, bf16[128,2048]{1,0:T(8,128)(2,1)S(1)}, u32[]{:S(2)}, u32[]{:S(2)}) collective-permute-start(bf16[128,2048]{1,0:T(8,128)(2,1)S(1)} %slice.22), channel_id=1, source_target_pairs={{0,4},{4,12},{12,20},{20,28},{28,24},{24,16},{16,8},{8,0},{1,5},{5... | collective-permute-start | bytes 1572872 | tf_op jit(solution)/shard_map/ppermute | solution.py:82
  146.3 2.8 %collective-permute-start.14 = (bf16[256,2048]{1,0:T(8,128)(2,1)}, bf16[256,2048]{1,0:T(8,128)(2,1)}, u32[]{:S(2)}, u32[]{:S(2)}) collective-permute-start(bf16[256,2048]{1,0:T(8,128)(2,1)} %collective-permute-done.13.refs_6_), channel_id=1, source_target_pairs={{0,2},{2,0},{1,3},{3,1},{4,6},{6,4},{5,7},{7,5},{8,10},{10,8},{9,1... | collective-permute-start | bytes 3145736 | tf_op jit(solution)/shard_map/ppermute | solution.py:249
  149.2 4.5 %collective-permute-done.21 = bf16[128,2048]{1,0:T(8,128)(2,1)S(1)} collective-permute-done((bf16[128,2048]{1,0:T(8,128)(2,1)S(1)}, bf16[128,2048]{1,0:T(8,128)(2,1)S(1)}, u32[]{:S(2)}, u32[]{:S(2)}) %collective-permute-start.21) | collective-permute-done | bytes 524320 | tf_op jit(solution)/shard_map/ppermute | solution.py:82
  153.8 3.4 %collective-permute-start.18 = (bf16[256,2048]{1,0:T(8,128)(2,1)}, bf16[256,2048]{1,0:T(8,128)(2,1)}, u32[]{:S(2)}, u32[]{:S(2)}) collective-permute-start(bf16[256,2048]{1,0:T(8,128)(2,1)} %collective-permute-done.17.refs_10_), channel_id=1, source_target_pairs={{0,2},{2,0},{1,3},{3,1},{4,6},{6,4},{5,7},{7,5},{8,10},{10,8},{9,1... | collective-permute-start | bytes 3145736 | tf_op jit(solution)/shard_map/ppermute | solution.py:249
  157.9 2.7 %collective-permute-start.20 = (bf16[256,2048]{1,0:T(8,128)(2,1)}, bf16[256,2048]{1,0:T(8,128)(2,1)}, u32[]{:S(2)}, u32[]{:S(2)}) collective-permute-start(bf16[256,2048]{1,0:T(8,128)(2,1)} %collective-permute-done.19.refs_12_), channel_id=1, source_target_pairs={{0,2},{2,0},{1,3},{3,1},{4,6},{6,4},{5,7},{7,5},{8,10},{10,8},{9,1... | collective-permute-start | bytes 3145736 | tf_op jit(solution)/shard_map/ppermute | solution.py:249
  161.9 2.4 %copy.33 = bf16[256,8,2,256]{3,0,2,1:T(8,128)(2,1)} copy(bf16[256,8,2,256]{0,3,2,1:T(8,128)(2,1)S(1)} %bitcast.55) | data formatting | bytes 4194304 | tf_op jit(solution)/shard_map/reshape | solution.py:254
  164.3 2.3 %gather_fusion.1 = bf16[8,256,2,256]{3,1,2,0:T(8,128)(2,1)S(1)} fusion(bf16[256,8,2,256]{3,0,2,1:T(8,128)(2,1)} %copy.33, s32[1024]{0:T(1024)S(1)} %pad_clamp_fusion), kind=kCustom, calls=%fused_computation.1 | custom fusion | bytes 4194336 | tf_op jit(solution)/shard_map/jit(_take)/gather | solution.py:257
  169.5 2.8 %reshape.58.normed_ref = bf16[256,4096]{1,0:T(8,128)(2,1)} reshape(bf16[256,8,2,256]{3,2,1,0:T(2,128)(2,1)S(1)} %copy.34) | data formatting | bytes 4194304 | tf_op jit(solution)/shard_map/reshape | solution.py:258
  172.3 9.8 %shard_map.82 = bf16[256,2048]{1,0:T(8,128)(2,1)} custom-call(bf16[256,4096]{1,0:T(8,128)(2,1)} %reshape.58.normed_ref, bf16[256,2048]{1,0:T(8,128)(2,1)} %refs_0_.1, bf16[256,2048]{1,0:T(8,128)(2,1)} %collective-permute-done.8.refs_1_, bf16[256,2048]{1,0:T(8,128)(2,1)} %collective-permute-done.refs_2_, bf16[256,2048]{1,0:T(8,128)(2,1)} %collective-permute-done.9.refs_3_, ...), custom_call_target="tpu_custom_call" | custom-call | tf_op jit(solution)/shard_map/pallas_call | solution.py:177
  (94 shorter events, 41.9 us)
Async XLA Ops:
  5.9 24.3 %collective-permute-start.2 = (bf16[2,128,2048]{2,1,0:T(8,128)(2,1)}, bf16[2,128,2048]{2,1,0:T(8,128)(2,1)S(1)}, u32[]{:S(2)}, u32[]{:S(2)}) collective-permute-start(bf16[2,128,2048]{2,1,0:T(8,128)(2,1)} %bitcast.4), channel_id=1, source_target_pairs={{0,1},{1,0},{2,3},{3,2},{4,5},{5,4},{6,7},{7,6},{8,9},{9,8},{10,11... | collective-permute-start | bytes 3145736 | tf_op jit(solution)/shard_map/ppermute | solution.py:38
  7.1 24.0 %collective-permute-start = (bf16[256,2048]{1,0:T(8,128)(2,1)}, bf16[256,2048]{1,0:T(8,128)(2,1)}, u32[]{:S(2)}, u32[]{:S(2)}) collective-permute-start(bf16[256,2048]{1,0:T(8,128)(2,1)} %refs_0_.1), channel_id=1, source_target_pairs={{0,4},{4,12},{12,20},{20,28},{28,24},{24,16},{16,8},{8,0},{1,5},{5... | collective-permute-start | bytes 3145736 | tf_op jit(solution)/shard_map/ppermute | solution.py:85
  8.4 23.7 %collective-permute-start.1 = (bf16[256,2048]{1,0:T(8,128)(2,1)}, bf16[256,2048]{1,0:T(8,128)(2,1)}, u32[]{:S(2)}, u32[]{:S(2)}) collective-permute-start(bf16[256,2048]{1,0:T(8,128)(2,1)} %refs_0_.1), channel_id=1, source_target_pairs={{4,0},{12,4},{20,12},{28,20},{24,28},{16,24},{8,16},{0,8},{5,1},{1... | collective-permute-start | bytes 3145736 | tf_op jit(solution)/shard_map/ppermute | solution.py:85
  33.1 4.6 %collective-permute-start.3 = (f32[16,128,128]{2,1,0:T(8,128)S(1)}, f32[16,128,128]{2,1,0:T(8,128)}, u32[]{:S(2)}, u32[]{:S(2)}) collective-permute-start(f32[16,128,128]{2,1,0:T(8,128)S(1)} %fusion.6), channel_id=1, source_target_pairs={{0,2},{2,0},{1,3},{3,1},{4,6},{6,4},{5,7},{7,5},{8,10},{10,8},{9,1... | collective-permute-start | bytes 3145736 | tf_op jit(solution)/shard_map/ppermute | solution.py:133
  39.0 15.1 %collective-permute-start.4 = (f32[8,128,128]{2,1,0:T(8,128)S(1)}, f32[8,128,128]{2,1,0:T(8,128)}, u32[]{:S(2)}, u32[]{:S(2)}) collective-permute-start(f32[8,128,128]{2,1,0:T(8,128)S(1)} %dynamic-slice_add_fusion), channel_id=1, source_target_pairs={{0,4},{4,8},{8,12},{12,16},{16,20},{20,24},{24,28},{1,5},{5,9},{9,... | collective-permute-start | bytes 1572872 | tf_op jit(solution)/shard_map/ppermute | solution.py:20
  55.3 14.2 %collective-permute-start.5 = (f32[8,128,128]{2,1,0:T(8,128)S(1)}, f32[8,128,128]{2,1,0:T(8,128)}, u32[]{:S(2)}, u32[]{:S(2)}) collective-permute-start(f32[8,128,128]{2,1,0:T(8,128)S(1)} %add.78), channel_id=1, source_target_pairs={{0,8},{4,12},{8,16},{12,20},{16,24},{20,28},{1,9},{5,13},{9,17},{1... | collective-permute-start | bytes 1572872 | tf_op jit(solution)/shard_map/ppermute | solution.py:20
  60.6 13.2 %collective-permute-start.7 = (bf16[1,128,2048]{2,1,0:T(8,128)(2,1)}, bf16[1,128,2048]{2,1,0:T(8,128)(2,1)}, u32[]{:S(2)}, u32[]{:S(2)}) collective-permute-start(bf16[1,128,2048]{2,1,0:T(8,128)(2,1)} %bitcast.9), channel_id=1, source_target_pairs={{0,1},{1,0},{2,3},{3,2},{4,5},{5,4},{6,7},{7,6},{8,9},{9,8},{10,11... | collective-permute-start | bytes 1572872 | tf_op jit(solution)/shard_map/ppermute | solution.py:38
  60.8 40.9 %collective-permute-start.8 = (bf16[256,2048]{1,0:T(8,128)(2,1)}, bf16[256,2048]{1,0:T(8,128)(2,1)}, u32[]{:S(2)}, u32[]{:S(2)}) collective-permute-start(bf16[256,2048]{1,0:T(8,128)(2,1)} %refs_0_.1), channel_id=1, source_target_pairs={{0,2},{2,0},{1,3},{3,1},{4,6},{6,4},{5,7},{7,5},{8,10},{10,8},{9,1... | collective-permute-start | bytes 3145736 | tf_op jit(solution)/shard_map/ppermute | solution.py:230
  63.9 37.8 %collective-permute-start.10 = (bf16[256,2048]{1,0:T(8,128)(2,1)}, bf16[256,2048]{1,0:T(8,128)(2,1)}, u32[]{:S(2)}, u32[]{:S(2)}) collective-permute-start(bf16[256,2048]{1,0:T(8,128)(2,1)} %collective-permute-done.1.refs_4_), channel_id=1, source_target_pairs={{0,2},{2,0},{1,3},{3,1},{4,6},{6,4},{5,7},{7,5},{8,10},{10,8},{9,1... | collective-permute-start | bytes 3145736 | tf_op jit(solution)/shard_map/ppermute | solution.py:230
  64.0 37.8 %collective-permute-start.9 = (bf16[256,2048]{1,0:T(8,128)(2,1)}, bf16[256,2048]{1,0:T(8,128)(2,1)}, u32[]{:S(2)}, u32[]{:S(2)}) collective-permute-start(bf16[256,2048]{1,0:T(8,128)(2,1)} %collective-permute-done.refs_2_), channel_id=1, source_target_pairs={{0,2},{2,0},{1,3},{3,1},{4,6},{6,4},{5,7},{7,5},{8,10},{10,8},{9,1... | collective-permute-start | bytes 3145736 | tf_op jit(solution)/shard_map/ppermute | solution.py:230
  70.6 25.0 %collective-permute-start.6 = (f32[8,128,128]{2,1,0:T(8,128)S(1)}, f32[8,128,128]{2,1,0:T(8,128)S(1)}, u32[]{:S(2)}, u32[]{:S(2)}) collective-permute-start(f32[8,128,128]{2,1,0:T(8,128)S(1)} %add.79), channel_id=1, source_target_pairs={{0,16},{4,20},{8,24},{12,28},{1,17},{5,21},{9,25},{13,29},{2,18},{... | collective-permute-start | bytes 1572872 | tf_op jit(solution)/shard_map/ppermute | solution.py:20
  76.3 41.9 %collective-permute-start.13 = (bf16[256,2048]{1,0:T(8,128)(2,1)}, bf16[256,2048]{1,0:T(8,128)(2,1)}, u32[]{:S(2)}, u32[]{:S(2)}) collective-permute-start(bf16[256,2048]{1,0:T(8,128)(2,1)} %collective-permute-done.refs_2_), channel_id=1, source_target_pairs={{0,4},{4,12},{12,20},{20,28},{28,24},{24,16},{16,8},{8,0},{1,5},{5... | collective-permute-start | bytes 3145736 | tf_op jit(solution)/shard_map/ppermute | solution.py:85
  95.6 24.8 %collective-permute-start.15 = (bf16[256,2048]{1,0:T(8,128)(2,1)}, bf16[256,2048]{1,0:T(8,128)(2,1)}, u32[]{:S(2)}, u32[]{:S(2)}) collective-permute-start(bf16[256,2048]{1,0:T(8,128)(2,1)} %collective-permute-done.1.refs_4_), channel_id=1, source_target_pairs={{4,0},{12,4},{20,12},{28,20},{24,28},{16,24},{8,16},{0,8},{5,1},{1... | collective-permute-start | bytes 3145736 | tf_op jit(solution)/shard_map/ppermute | solution.py:85
  101.7 18.7 %collective-permute-start.11 = (f32[8,128,128]{2,1,0:T(8,128)}, f32[8,128,128]{2,1,0:T(8,128)}, u32[]{:S(2)}, u32[]{:S(2)}) collective-permute-start(f32[8,128,128]{2,1,0:T(8,128)} %add_subtract_fusion), channel_id=1, source_target_pairs={{0,2},{2,0},{1,3},{3,1},{4,6},{6,4},{5,7},{7,5},{8,10},{10,8},{9,1... | collective-permute-start | bytes 1572872 | tf_op jit(solution)/shard_map/ppermute | solution.py:141
  118.2 23.4 %collective-permute-start.17 = (bf16[256,2048]{1,0:T(8,128)(2,1)}, bf16[256,2048]{1,0:T(8,128)(2,1)}, u32[]{:S(2)}, u32[]{:S(2)}) collective-permute-start(bf16[256,2048]{1,0:T(8,128)(2,1)} %collective-permute-done.13.refs_6_), channel_id=1, source_target_pairs={{0,4},{4,12},{12,20},{20,28},{28,24},{24,16},{16,8},{8,0},{1,5},{5... | collective-permute-start | bytes 3145736 | tf_op jit(solution)/shard_map/ppermute | solution.py:85
  120.4 24.6 %collective-permute-start.19 = (bf16[256,2048]{1,0:T(8,128)(2,1)}, bf16[256,2048]{1,0:T(8,128)(2,1)}, u32[]{:S(2)}, u32[]{:S(2)}) collective-permute-start(bf16[256,2048]{1,0:T(8,128)(2,1)} %collective-permute-done.15.refs_8_), channel_id=1, source_target_pairs={{4,0},{12,4},{20,12},{28,20},{24,28},{16,24},{8,16},{0,8},{5,1},{1... | collective-permute-start | bytes 3145736 | tf_op jit(solution)/shard_map/ppermute | solution.py:85
  124.1 37.4 %collective-permute-start.12 = (bf16[256,2048]{0,1:T(8,128)(2,1)S(1)}, bf16[256,2048]{0,1:T(8,128)(2,1)S(1)}, u32[]{:S(2)}, u32[]{:S(2)}) collective-permute-start(bf16[256,2048]{0,1:T(8,128)(2,1)S(1)} %bitcast.56), channel_id=1, source_target_pairs={{0,1},{1,0},{2,3},{3,2},{4,5},{5,4},{6,7},{7,6},{8,9},{9,8},{10,11... | collective-permute-start | bytes 3145736 | tf_op jit(solution)/shard_map/ppermute | solution.py:127
  142.7 11.0 %collective-permute-start.21 = (bf16[128,2048]{1,0:T(8,128)(2,1)S(1)}, bf16[128,2048]{1,0:T(8,128)(2,1)S(1)}, u32[]{:S(2)}, u32[]{:S(2)}) collective-permute-start(bf16[128,2048]{1,0:T(8,128)(2,1)S(1)} %slice.22), channel_id=1, source_target_pairs={{0,4},{4,12},{12,20},{20,28},{28,24},{24,16},{16,8},{8,0},{1,5},{5... | collective-permute-start | bytes 1572872 | tf_op jit(solution)/shard_map/ppermute | solution.py:82
  146.1 11.9 %collective-permute-start.22 = (bf16[128,2048]{1,0:T(8,128)(2,1)S(1)}, bf16[128,2048]{1,0:T(8,128)(2,1)S(1)}, u32[]{:S(2)}, u32[]{:S(2)}) collective-permute-start(bf16[128,2048]{1,0:T(8,128)(2,1)S(1)} %slice.23), channel_id=1, source_target_pairs={{4,0},{12,4},{20,12},{28,20},{24,28},{16,24},{8,16},{0,8},{5,1},{1... | collective-permute-start | bytes 1572872 | tf_op jit(solution)/shard_map/ppermute | solution.py:82
  146.3 26.0 %collective-permute-start.14 = (bf16[256,2048]{1,0:T(8,128)(2,1)}, bf16[256,2048]{1,0:T(8,128)(2,1)}, u32[]{:S(2)}, u32[]{:S(2)}) collective-permute-start(bf16[256,2048]{1,0:T(8,128)(2,1)} %collective-permute-done.13.refs_6_), channel_id=1, source_target_pairs={{0,2},{2,0},{1,3},{3,1},{4,6},{6,4},{5,7},{7,5},{8,10},{10,8},{9,1... | collective-permute-start | bytes 3145736 | tf_op jit(solution)/shard_map/ppermute | solution.py:249
  149.1 23.2 %collective-permute-start.16 = (bf16[256,2048]{1,0:T(8,128)(2,1)}, bf16[256,2048]{1,0:T(8,128)(2,1)}, u32[]{:S(2)}, u32[]{:S(2)}) collective-permute-start(bf16[256,2048]{1,0:T(8,128)(2,1)} %collective-permute-done.15.refs_8_), channel_id=1, source_target_pairs={{0,2},{2,0},{1,3},{3,1},{4,6},{6,4},{5,7},{7,5},{8,10},{10,8},{9,1... | collective-permute-start | bytes 3145736 | tf_op jit(solution)/shard_map/ppermute | solution.py:249
  153.8 18.6 %collective-permute-start.18 = (bf16[256,2048]{1,0:T(8,128)(2,1)}, bf16[256,2048]{1,0:T(8,128)(2,1)}, u32[]{:S(2)}, u32[]{:S(2)}) collective-permute-start(bf16[256,2048]{1,0:T(8,128)(2,1)} %collective-permute-done.17.refs_10_), channel_id=1, source_target_pairs={{0,2},{2,0},{1,3},{3,1},{4,6},{6,4},{5,7},{7,5},{8,10},{10,8},{9,1... | collective-permute-start | bytes 3145736 | tf_op jit(solution)/shard_map/ppermute | solution.py:249
  157.9 14.4 %collective-permute-start.20 = (bf16[256,2048]{1,0:T(8,128)(2,1)}, bf16[256,2048]{1,0:T(8,128)(2,1)}, u32[]{:S(2)}, u32[]{:S(2)}) collective-permute-start(bf16[256,2048]{1,0:T(8,128)(2,1)} %collective-permute-done.19.refs_12_), channel_id=1, source_target_pairs={{0,2},{2,0},{1,3},{3,1},{4,6},{6,4},{5,7},{7,5},{8,10},{10,8},{9,1... | collective-permute-start | bytes 3145736 | tf_op jit(solution)/shard_map/ppermute | solution.py:249
  161.5 10.8 %collective-permute-start.23 = (bf16[256,2048]{1,0:T(8,128)(2,1)}, bf16[256,2048]{1,0:T(8,128)(2,1)}, u32[]{:S(2)}, u32[]{:S(2)}) collective-permute-start(bf16[256,2048]{1,0:T(8,128)(2,1)} %constant_dynamic-update-slice_fusion.refs_14_), channel_id=1, source_target_pairs={{0,2},{2,0},{1,3},{3,1},{4,6},{6,4},{5,7},{7,5},{8,10},{10,8},{9,1... | collective-permute-start | bytes 3145736 | tf_op jit(solution)/shard_map/ppermute | solution.py:249
  (12 other events, 101.2 us)

commit v10 on v9

--- a/solution.py
+++ b/solution.py
@@ -236,9 +236,17 @@
     chip_prefix_half = exclusive_prefix(chip_half, "chip", n_chip)
     query_heads = split_heads(query_block, heads_dev)
     within_block = within_block_part(query_heads, key_heads, value_heads)
-    swapped += [lax.ppermute(w, "core", SWAP) for w in got[len(swapped):]]
-    chip_prefix_half, within_block, swapped = barrier((chip_prefix_half, within_block, swapped))
-    for step in range(2, n_steps + 1):
+    ahead, behind = ring_step(ahead, behind, order, last=n_steps == 2)
+    chip_prefix_half, within_block, swapped, ahead, behind = barrier(
+        (chip_prefix_half, within_block, swapped, ahead, behind)
+    )
+    if n_steps == 2:
+        got.append(jnp.concatenate([ahead, behind], 0))
+        offsets.append(2)
+    else:
+        got += [ahead, behind]
+        offsets += [2, -2]
+    for step in range(3, n_steps + 1):
         ahead, behind = ring_step(ahead, behind, order, last=step == n_steps)
         if step == n_steps:
             got.append(jnp.concatenate([ahead, behind], 0))

time: 184 us -> 188 us (1.022)
  waiting for transfers between devices: 91.6 us -> 98.3 us
    ppermute x5, starting transfers between devices: 8.93 us -> 4.99 us  [local_ring(): swapped += [lax.ppermute(w, 'core', SWAP) for w in got[len(swapped):]]]
    ppermute x1, waiting for transfers between devices: 4.55 us -> 7.81 us  [ring_step(): lax.ppermute(ahead[:half_rows], 'chip', forward)]
    ppermute x3, starting transfers between devices: 8.4 us -> 11.5 us  [exclusive_prefix(): total = total + lax.ppermute(total, axis, pairs)]
    ppermute x3, waiting for transfers between devices: 29.6 us -> 32.3 us  [ring_step(): lax.ppermute(ahead, 'chip', forward)]
    ppermute x1, starting transfers between devices: 2.7 us -> 0.56 us  [chip_finish(): other_half = lax.ppermute(chip_prefix_half, 'core', SWAP)]
    unnamed x28 -> x30, local copies, waits for them, and re-layouts: 6.34 us -> 5.55 us
  transfers between devices with their start and end apart: 24 -> 24, of which waited for: 10 -> 10; matrix products, arithmetic and copies ran while one was open for 21% -> 20% of each run, Pallas kernels for 0% -> 0%
where the time goes in v10:
time: 188 us; the launch traced here: 186 us
  waiting for transfers between devices  98.3 us (52%)
  starting transfers between devices  32 us (17%)
  local copies, waits for them, and re-layouts  28.9 us (15%)
  other arithmetic  10.7 us (6%)
  Pallas kernels  9.75 us (5%)
  matrix products  5.58 us (3%)
    ppermute x3, waiting for transfers between devices, exclusive_prefix(): total = total + lax.ppermute(total, axis, pairs)  33.3 us
    ppermute x3, waiting for transfers between devices, ring_step(): lax.ppermute(ahead, 'chip', forward)  32.3 us
    ppermute x2, waiting for transfers between devices, head_blocks(): other = lax.ppermute(sent, 'head', SWAP)  21.1 us
    ppermute x3, starting transfers between devices, exclusive_prefix(): total = total + lax.ppermute(total, axis, pairs)  11.5 us
    pallas_call x1, Pallas kernels, project_blocks(): pl.pallas_call(kernel, out_shape=jax.ShapeDtypeStruct((tokens, cols), jnp...  9.75 us
    ppermute x1, waiting for transfers between devices, ring_step(): lax.ppermute(ahead[:half_rows], 'chip', forward)  7.81 us
    unnamed x30, local copies, waits for them, and re-layouts  5.55 us
    ppermute x5, starting transfers between devices, local_ring(): swapped += [lax.ppermute(w, 'core', SWAP) for w in got[len(swapped):]]  4.99 us
  transfers between devices with their start and end apart: 24, of which 10 were waited for; matrix products, arithmetic and copies ran while one was open for 20% of the time, Pallas kernels for 0%

profile of v10, /device:TPU:13, one launch (start us, length us, event | category | flops | bytes accessed | tf_op | source)
XLA Modules:
  0.0 185.7 jit_solution(18292929185824592102)
XLA Ops:
  3.6 2.3 %copy.21 = bf16[2,128,1,2048]{3,1,0,2:T(8,128)(2,1)} copy(bf16[2,128,1,2048]{1,3,2,0:T(8,128)(2,1)} %get-tuple-element.34) | data formatting | bytes 2097152 | tf_op jit(solution)/shard_map/jit(dynamic_index_in_dim)/dynamic_slice | solution.py:37
  9.1 21.1 %collective-permute-done.2 = bf16[2,128,2048]{2,1,0:T(8,128)(2,1)S(1)} collective-permute-done((bf16[2,128,2048]{2,1,0:T(8,128)(2,1)}, bf16[2,128,2048]{2,1,0:T(8,128)(2,1)S(1)}, u32[]{:S(2)}, u32[]{:S(2)}) %collective-permute-start.2) | collective-permute-done | bytes 1048608 | tf_op jit(solution)/shard_map/ppermute | solution.py:38
  34.2 2.4 %collective-permute-done.3 = f32[16,128,128]{2,1,0:T(8,128)} collective-permute-done((f32[16,128,128]{2,1,0:T(8,128)S(1)}, f32[16,128,128]{2,1,0:T(8,128)}, u32[]{:S(2)}, u32[]{:S(2)}) %collective-permute-start.3) | collective-permute-done | bytes 1048608 | tf_op jit(solution)/shard_map/ppermute | solution.py:133
  37.9 4.3 %collective-permute-start.4 = (f32[8,128,128]{2,1,0:T(8,128)S(1)}, f32[8,128,128]{2,1,0:T(8,128)S(1)}, u32[]{:S(2)}, u32[]{:S(2)}) collective-permute-start(f32[8,128,128]{2,1,0:T(8,128)S(1)} %dynamic-slice_add_fusion), channel_id=1, source_target_pairs={{0,4},{4,8},{8,12},{12,16},{16,20},{20,24},{24,28},{1,5},{5,9},{9,... | collective-permute-start | bytes 1572872 | tf_op jit(solution)/shard_map/ppermute | solution.py:20
  42.2 10.9 %collective-permute-done.4 = f32[8,128,128]{2,1,0:T(8,128)S(1)} collective-permute-done((f32[8,128,128]{2,1,0:T(8,128)S(1)}, f32[8,128,128]{2,1,0:T(8,128)S(1)}, u32[]{:S(2)}, u32[]{:S(2)}) %collective-permute-start.4) | collective-permute-done | bytes 524320 | tf_op jit(solution)/shard_map/ppermute | solution.py:20
  53.2 3.1 %collective-permute-start.5 = (f32[8,128,128]{2,1,0:T(8,128)S(1)}, f32[8,128,128]{2,1,0:T(8,128)}, u32[]{:S(2)}, u32[]{:S(2)}) collective-permute-start(f32[8,128,128]{2,1,0:T(8,128)S(1)} %add.78), channel_id=1, source_target_pairs={{0,8},{4,12},{8,16},{12,20},{16,24},{20,28},{1,9},{5,13},{9,17},{1... | collective-permute-start | bytes 1572872 | tf_op jit(solution)/shard_map/ppermute | solution.py:20
  56.4 2.3 %copy.24 = bf16[128,4096]{0,1:T(8,128)(2,1)} copy(bf16[128,4096]{1,0:T(8,128)(2,1)} %param.8) | data formatting | bytes 2097152 | tf_op args[0]
  58.7 2.3 %constant_dynamic-slice_fusion.1 = (bf16[1,128,1,2048]{1,3,2,0:T(8,128)(2,1)}, bf16[1,128,1,2048]{1,3,2,0:T(8,128)(2,1)}) fusion(bf16[1,128,2,2048]{1,3,2,0:T(8,128)(2,1)} %bitcast.61, s32[]{:T(128)S(6)} %select_n.122, s32[]{:T(128)S(6)} %select_n.123), kind=kLoop, calls=%fused_computation.56 | loop fusion | bytes 2097160 | tf_op jit(solution)/shard_map/jit(dynamic_index_in_dim)/dynamic_slice | solution.py:36
  60.9 2.2 %copy.26 = bf16[1,128,1,2048]{3,1,2,0:T(8,128)(2,1)} copy(bf16[1,128,1,2048]{1,3,2,0:T(8,128)(2,1)} %get-tuple-element.40) | data formatting | bytes 1048576 | tf_op jit(solution)/shard_map/jit(dynamic_index_in_dim)/dynamic_slice | solution.py:37
  63.3 4.1 %collective-permute-done.5 = f32[8,128,128]{2,1,0:T(8,128)} collective-permute-done((f32[8,128,128]{2,1,0:T(8,128)S(1)}, f32[8,128,128]{2,1,0:T(8,128)}, u32[]{:S(2)}, u32[]{:S(2)}) %collective-permute-start.5) | collective-permute-done | bytes 524320 | tf_op jit(solution)/shard_map/ppermute | solution.py:20
  68.5 4.1 %collective-permute-start.6 = (f32[8,128,128]{2,1,0:T(8,128)S(1)}, f32[8,128,128]{2,1,0:T(8,128)S(1)}, u32[]{:S(2)}, u32[]{:S(2)}) collective-permute-start(f32[8,128,128]{2,1,0:T(8,128)S(1)} %add.79), channel_id=1, source_target_pairs={{0,16},{4,20},{8,24},{12,28},{1,17},{5,21},{9,25},{13,29},{2,18},{... | collective-permute-start | bytes 1572872 | tf_op jit(solution)/shard_map/ppermute | solution.py:20
  72.6 2.5 %collective-permute-start.8 = (bf16[256,2048]{1,0:T(8,128)(2,1)}, bf16[256,2048]{1,0:T(8,128)(2,1)}, u32[]{:S(2)}, u32[]{:S(2)}) collective-permute-start(bf16[256,2048]{1,0:T(8,128)(2,1)} %refs_0_.1), channel_id=1, source_target_pairs={{0,2},{2,0},{1,3},{3,1},{4,6},{6,4},{5,7},{7,5},{8,10},{10,8},{9,1... | collective-permute-start | bytes 3145736 | tf_op jit(solution)/shard_map/ppermute | solution.py:230
  77.2 18.3 %collective-permute-done.6 = f32[8,128,128]{2,1,0:T(8,128)S(1)} collective-permute-done((f32[8,128,128]{2,1,0:T(8,128)S(1)}, f32[8,128,128]{2,1,0:T(8,128)S(1)}, u32[]{:S(2)}, u32[]{:S(2)}) %collective-permute-start.6) | collective-permute-done | bytes 524320 | tf_op jit(solution)/shard_map/ppermute | solution.py:20
  98.6 3.3 %fusion.1 = f32[256,16,128]{0,2,1:T(8,128)S(1)} fusion(bf16[256,16,128]{0,2,1:T(8,128)(2,1)} %bitcast.58, bf16[256,16,128]{0,2,1:T(8,128)(2,1)} %bitcast.62, pred[256,256]{1,0:T(8,128)(4,1)S(1)} %iota_compare_fusion, bf16[256,2048]{1,0:T(8,128)(2,1)} %copy-done.2), kind=kOutput, calls=%fused_computation.16 | convolution fusion | flops 538968064 | bytes 5308416 | tf_op jit(solution)/shard_map/hts,she->the/dot_general | solution.py:106
  103.9 14.2 %collective-permute-done.11.refs_6_ = bf16[256,2048]{1,0:T(8,128)(2,1)} collective-permute-done((bf16[256,2048]{1,0:T(8,128)(2,1)}, bf16[256,2048]{1,0:T(8,128)(2,1)}, u32[]{:S(2)}, u32[]{:S(2)}) %collective-permute-start.11) | collective-permute-done | bytes 1048608 | tf_op jit(solution)/shard_map/ppermute | solution.py:85
  120.0 2.3 %collective-permute-start.17 = (bf16[256,2048]{1,0:T(8,128)(2,1)}, bf16[256,2048]{1,0:T(8,128)(2,1)}, u32[]{:S(2)}, u32[]{:S(2)}) collective-permute-start(bf16[256,2048]{1,0:T(8,128)(2,1)} %collective-permute-done.11.refs_6_), channel_id=1, source_target_pairs={{0,4},{4,12},{12,20},{20,28},{28,24},{24,16},{16,8},{8,0},{1,5},{5... | collective-permute-start | bytes 3145736 | tf_op jit(solution)/shard_map/ppermute | solution.py:85
  126.9 18.2 %collective-permute-done.17.refs_10_ = bf16[256,2048]{1,0:T(8,128)(2,1)} collective-permute-done((bf16[256,2048]{1,0:T(8,128)(2,1)}, bf16[256,2048]{1,0:T(8,128)(2,1)}, u32[]{:S(2)}, u32[]{:S(2)}) %collective-permute-start.17) | collective-permute-done | bytes 1048608 | tf_op jit(solution)/shard_map/ppermute | solution.py:85
  146.2 2.3 %collective-permute-start.21 = (bf16[128,2048]{1,0:T(8,128)(2,1)S(1)}, bf16[128,2048]{1,0:T(8,128)(2,1)S(1)}, u32[]{:S(2)}, u32[]{:S(2)}) collective-permute-start(bf16[128,2048]{1,0:T(8,128)(2,1)S(1)} %slice.22), channel_id=1, source_target_pairs={{0,4},{4,12},{12,20},{20,28},{28,24},{24,16},{16,8},{8,0},{1,5},{5... | collective-permute-start | bytes 1572872 | tf_op jit(solution)/shard_map/ppermute | solution.py:82
  151.0 7.8 %collective-permute-done.21 = bf16[128,2048]{1,0:T(8,128)(2,1)S(1)} collective-permute-done((bf16[128,2048]{1,0:T(8,128)(2,1)S(1)}, bf16[128,2048]{1,0:T(8,128)(2,1)S(1)}, u32[]{:S(2)}, u32[]{:S(2)}) %collective-permute-start.21) | collective-permute-done | bytes 524320 | tf_op jit(solution)/shard_map/ppermute | solution.py:82
  165.3 2.4 %copy.33 = bf16[256,8,2,256]{3,0,2,1:T(8,128)(2,1)} copy(bf16[256,8,2,256]{0,3,2,1:T(8,128)(2,1)S(1)} %bitcast.55) | data formatting | bytes 4194304 | tf_op jit(solution)/shard_map/reshape | solution.py:262
  167.7 2.3 %gather_fusion.1 = bf16[8,256,2,256]{3,1,2,0:T(8,128)(2,1)S(1)} fusion(bf16[256,8,2,256]{3,0,2,1:T(8,128)(2,1)} %copy.33, s32[1024]{0:T(1024)S(1)} %pad_clamp_fusion), kind=kCustom, calls=%fused_computation.1 | custom fusion | bytes 4194336 | tf_op jit(solution)/shard_map/jit(_take)/gather | solution.py:265
  170.8 2.2 %copy.34 = bf16[256,8,2,256]{3,2,1,0:T(2,128)(2,1)S(1)} copy(bf16[256,8,2,256]{3,0,2,1:T(8,128)(2,1)S(1)} %reverse_select_fusion) | data formatting | bytes 4194304 | tf_op jit(solution)/shard_map/jit(_where)/select_n | solution.py:266
  172.9 2.9 %reshape.58.normed_ref = bf16[256,4096]{1,0:T(8,128)(2,1)} reshape(bf16[256,8,2,256]{3,2,1,0:T(2,128)(2,1)S(1)} %copy.34) | data formatting | bytes 4194304 | tf_op jit(solution)/shard_map/reshape | solution.py:266
  175.8 9.8 %shard_map.82 = bf16[256,2048]{1,0:T(8,128)(2,1)} custom-call(bf16[256,4096]{1,0:T(8,128)(2,1)} %reshape.58.normed_ref, bf16[256,2048]{1,0:T(8,128)(2,1)} %refs_0_.1, bf16[256,2048]{1,0:T(8,128)(2,1)} %collective-permute-done.8.refs_1_, bf16[256,2048]{1,0:T(8,128)(2,1)} %collective-permute-done.refs_2_, bf16[256,2048]{1,0:T(8,128)(2,1)} %collective-permute-done.9.refs_3_, ...), custom_call_target="tpu_custom_call" | custom-call | tf_op jit(solution)/shard_map/pallas_call | solution.py:177
  (96 shorter events, 37.9 us)
Async XLA Ops:
  5.9 24.3 %collective-permute-start.2 = (bf16[2,128,2048]{2,1,0:T(8,128)(2,1)}, bf16[2,128,2048]{2,1,0:T(8,128)(2,1)S(1)}, u32[]{:S(2)}, u32[]{:S(2)}) collective-permute-start(bf16[2,128,2048]{2,1,0:T(8,128)(2,1)} %bitcast.4), channel_id=1, source_target_pairs={{0,1},{1,0},{2,3},{3,2},{4,5},{5,4},{6,7},{7,6},{8,9},{9,8},{10,11... | collective-permute-start | bytes 3145736 | tf_op jit(solution)/shard_map/ppermute | solution.py:38
  7.1 24.0 %collective-permute-start.1 = (bf16[256,2048]{1,0:T(8,128)(2,1)}, bf16[256,2048]{1,0:T(8,128)(2,1)}, u32[]{:S(2)}, u32[]{:S(2)}) collective-permute-start(bf16[256,2048]{1,0:T(8,128)(2,1)} %refs_0_.1), channel_id=1, source_target_pairs={{4,0},{12,4},{20,12},{28,20},{24,28},{16,24},{8,16},{0,8},{5,1},{1... | collective-permute-start | bytes 3145736 | tf_op jit(solution)/shard_map/ppermute | solution.py:85
  7.3 23.9 %collective-permute-start = (bf16[256,2048]{1,0:T(8,128)(2,1)}, bf16[256,2048]{1,0:T(8,128)(2,1)}, u32[]{:S(2)}, u32[]{:S(2)}) collective-permute-start(bf16[256,2048]{1,0:T(8,128)(2,1)} %refs_0_.1), channel_id=1, source_target_pairs={{0,4},{4,12},{12,20},{20,28},{28,24},{24,16},{16,8},{8,0},{1,5},{5... | collective-permute-start | bytes 3145736 | tf_op jit(solution)/shard_map/ppermute | solution.py:85
  32.1 4.5 %collective-permute-start.3 = (f32[16,128,128]{2,1,0:T(8,128)S(1)}, f32[16,128,128]{2,1,0:T(8,128)}, u32[]{:S(2)}, u32[]{:S(2)}) collective-permute-start(f32[16,128,128]{2,1,0:T(8,128)S(1)} %fusion.6), channel_id=1, source_target_pairs={{0,2},{2,0},{1,3},{3,1},{4,6},{6,4},{5,7},{7,5},{8,10},{10,8},{9,1... | collective-permute-start | bytes 3145736 | tf_op jit(solution)/shard_map/ppermute | solution.py:133
  37.9 15.2 %collective-permute-start.4 = (f32[8,128,128]{2,1,0:T(8,128)S(1)}, f32[8,128,128]{2,1,0:T(8,128)S(1)}, u32[]{:S(2)}, u32[]{:S(2)}) collective-permute-start(f32[8,128,128]{2,1,0:T(8,128)S(1)} %dynamic-slice_add_fusion), channel_id=1, source_target_pairs={{0,4},{4,8},{8,12},{12,16},{16,20},{20,24},{24,28},{1,5},{5,9},{9,... | collective-permute-start | bytes 1572872 | tf_op jit(solution)/shard_map/ppermute | solution.py:20
  53.2 14.2 %collective-permute-start.5 = (f32[8,128,128]{2,1,0:T(8,128)S(1)}, f32[8,128,128]{2,1,0:T(8,128)}, u32[]{:S(2)}, u32[]{:S(2)}) collective-permute-start(f32[8,128,128]{2,1,0:T(8,128)S(1)} %add.78), channel_id=1, source_target_pairs={{0,8},{4,12},{8,16},{12,20},{16,24},{20,28},{1,9},{5,13},{9,17},{1... | collective-permute-start | bytes 1572872 | tf_op jit(solution)/shard_map/ppermute | solution.py:20
  63.1 12.4 %collective-permute-start.7 = (bf16[1,128,2048]{2,1,0:T(8,128)(2,1)}, bf16[1,128,2048]{2,1,0:T(8,128)(2,1)}, u32[]{:S(2)}, u32[]{:S(2)}) collective-permute-start(bf16[1,128,2048]{2,1,0:T(8,128)(2,1)} %bitcast.9), channel_id=1, source_target_pairs={{0,1},{1,0},{2,3},{3,2},{4,5},{5,4},{6,7},{7,6},{8,9},{9,8},{10,11... | collective-permute-start | bytes 1572872 | tf_op jit(solution)/shard_map/ppermute | solution.py:38
  68.5 27.0 %collective-permute-start.6 = (f32[8,128,128]{2,1,0:T(8,128)S(1)}, f32[8,128,128]{2,1,0:T(8,128)S(1)}, u32[]{:S(2)}, u32[]{:S(2)}) collective-permute-start(f32[8,128,128]{2,1,0:T(8,128)S(1)} %add.79), channel_id=1, source_target_pairs={{0,16},{4,20},{8,24},{12,28},{1,17},{5,21},{9,25},{13,29},{2,18},{... | collective-permute-start | bytes 1572872 | tf_op jit(solution)/shard_map/ppermute | solution.py:20
  72.6 31.3 %collective-permute-start.8 = (bf16[256,2048]{1,0:T(8,128)(2,1)}, bf16[256,2048]{1,0:T(8,128)(2,1)}, u32[]{:S(2)}, u32[]{:S(2)}) collective-permute-start(bf16[256,2048]{1,0:T(8,128)(2,1)} %refs_0_.1), channel_id=1, source_target_pairs={{0,2},{2,0},{1,3},{3,1},{4,6},{6,4},{5,7},{7,5},{8,10},{10,8},{9,1... | collective-permute-start | bytes 3145736 | tf_op jit(solution)/shard_map/ppermute | solution.py:230
  75.3 42.7 %collective-permute-start.11 = (bf16[256,2048]{1,0:T(8,128)(2,1)}, bf16[256,2048]{1,0:T(8,128)(2,1)}, u32[]{:S(2)}, u32[]{:S(2)}) collective-permute-start(bf16[256,2048]{1,0:T(8,128)(2,1)} %collective-permute-done.refs_2_), channel_id=1, source_target_pairs={{0,4},{4,12},{12,20},{20,28},{28,24},{24,16},{16,8},{8,0},{1,5},{5... | collective-permute-start | bytes 3145736 | tf_op jit(solution)/shard_map/ppermute | solution.py:85
  75.4 42.7 %collective-permute-start.9 = (bf16[256,2048]{1,0:T(8,128)(2,1)}, bf16[256,2048]{1,0:T(8,128)(2,1)}, u32[]{:S(2)}, u32[]{:S(2)}) collective-permute-start(bf16[256,2048]{1,0:T(8,128)(2,1)} %collective-permute-done.refs_2_), channel_id=1, source_target_pairs={{0,2},{2,0},{1,3},{3,1},{4,6},{6,4},{5,7},{7,5},{8,10},{10,8},{9,1... | collective-permute-start | bytes 3145736 | tf_op jit(solution)/shard_map/ppermute | solution.py:230
  75.5 42.6 %collective-permute-start.12 = (bf16[256,2048]{1,0:T(8,128)(2,1)}, bf16[256,2048]{1,0:T(8,128)(2,1)}, u32[]{:S(2)}, u32[]{:S(2)}) collective-permute-start(bf16[256,2048]{1,0:T(8,128)(2,1)} %collective-permute-done.1.refs_4_), channel_id=1, source_target_pairs={{4,0},{12,4},{20,12},{28,20},{24,28},{16,24},{8,16},{0,8},{5,1},{1... | collective-permute-start | bytes 3145736 | tf_op jit(solution)/shard_map/ppermute | solution.py:85
  95.5 22.6 %collective-permute-start.10 = (bf16[256,2048]{1,0:T(8,128)(2,1)}, bf16[256,2048]{1,0:T(8,128)(2,1)}, u32[]{:S(2)}, u32[]{:S(2)}) collective-permute-start(bf16[256,2048]{1,0:T(8,128)(2,1)} %collective-permute-done.1.refs_4_), channel_id=1, source_target_pairs={{0,2},{2,0},{1,3},{3,1},{4,6},{6,4},{5,7},{7,5},{8,10},{10,8},{9,1... | collective-permute-start | bytes 3145736 | tf_op jit(solution)/shard_map/ppermute | solution.py:230
  118.1 4.2 %collective-permute-start.13 = (f32[8,128,128]{2,1,0:T(8,128)}, f32[8,128,128]{2,1,0:T(8,128)}, u32[]{:S(2)}, u32[]{:S(2)}) collective-permute-start(f32[8,128,128]{2,1,0:T(8,128)} %add_subtract_fusion), channel_id=1, source_target_pairs={{0,2},{2,0},{1,3},{3,1},{4,6},{6,4},{5,7},{7,5},{8,10},{10,8},{9,1... | collective-permute-start | bytes 1572872 | tf_op jit(solution)/shard_map/ppermute | solution.py:141
  120.0 25.1 %collective-permute-start.17 = (bf16[256,2048]{1,0:T(8,128)(2,1)}, bf16[256,2048]{1,0:T(8,128)(2,1)}, u32[]{:S(2)}, u32[]{:S(2)}) collective-permute-start(bf16[256,2048]{1,0:T(8,128)(2,1)} %collective-permute-done.11.refs_6_), channel_id=1, source_target_pairs={{0,4},{4,12},{12,20},{20,28},{28,24},{24,16},{16,8},{8,0},{1,5},{5... | collective-permute-start | bytes 3145736 | tf_op jit(solution)/shard_map/ppermute | solution.py:85
  122.2 26.2 %collective-permute-start.19 = (bf16[256,2048]{1,0:T(8,128)(2,1)}, bf16[256,2048]{1,0:T(8,128)(2,1)}, u32[]{:S(2)}, u32[]{:S(2)}) collective-permute-start(bf16[256,2048]{1,0:T(8,128)(2,1)} %collective-permute-done.12.refs_8_), channel_id=1, source_target_pairs={{4,0},{12,4},{20,12},{28,20},{24,28},{16,24},{8,16},{0,8},{5,1},{1... | collective-permute-start | bytes 3145736 | tf_op jit(solution)/shard_map/ppermute | solution.py:85
  126.0 39.0 %collective-permute-start.14 = (bf16[256,2048]{0,1:T(8,128)(2,1)S(1)}, bf16[256,2048]{0,1:T(8,128)(2,1)S(1)}, u32[]{:S(2)}, u32[]{:S(2)}) collective-permute-start(bf16[256,2048]{0,1:T(8,128)(2,1)S(1)} %bitcast.56), channel_id=1, source_target_pairs={{0,1},{1,0},{2,3},{3,2},{4,5},{5,4},{6,7},{7,6},{8,9},{9,8},{10,11... | collective-permute-start | bytes 3145736 | tf_op jit(solution)/shard_map/ppermute | solution.py:127
  146.2 12.7 %collective-permute-start.21 = (bf16[128,2048]{1,0:T(8,128)(2,1)S(1)}, bf16[128,2048]{1,0:T(8,128)(2,1)S(1)}, u32[]{:S(2)}, u32[]{:S(2)}) collective-permute-start(bf16[128,2048]{1,0:T(8,128)(2,1)S(1)} %slice.22), channel_id=1, source_target_pairs={{0,4},{4,12},{12,20},{20,28},{28,24},{24,16},{16,8},{8,0},{1,5},{5... | collective-permute-start | bytes 1572872 | tf_op jit(solution)/shard_map/ppermute | solution.py:82
  149.5 12.5 %collective-permute-start.22 = (bf16[128,2048]{1,0:T(8,128)(2,1)S(1)}, bf16[128,2048]{1,0:T(8,128)(2,1)S(1)}, u32[]{:S(2)}, u32[]{:S(2)}) collective-permute-start(bf16[128,2048]{1,0:T(8,128)(2,1)S(1)} %slice.23), channel_id=1, source_target_pairs={{4,0},{12,4},{20,12},{28,20},{24,28},{16,24},{8,16},{0,8},{5,1},{1... | collective-permute-start | bytes 1572872 | tf_op jit(solution)/shard_map/ppermute | solution.py:82
  149.8 26.0 %collective-permute-start.15 = (bf16[256,2048]{1,0:T(8,128)(2,1)}, bf16[256,2048]{1,0:T(8,128)(2,1)}, u32[]{:S(2)}, u32[]{:S(2)}) collective-permute-start(bf16[256,2048]{1,0:T(8,128)(2,1)} %collective-permute-done.11.refs_6_), channel_id=1, source_target_pairs={{0,2},{2,0},{1,3},{3,1},{4,6},{6,4},{5,7},{7,5},{8,10},{10,8},{9,1... | collective-permute-start | bytes 3145736 | tf_op jit(solution)/shard_map/ppermute | solution.py:257
  151.0 24.8 %collective-permute-start.16 = (bf16[256,2048]{1,0:T(8,128)(2,1)}, bf16[256,2048]{1,0:T(8,128)(2,1)}, u32[]{:S(2)}, u32[]{:S(2)}) collective-permute-start(bf16[256,2048]{1,0:T(8,128)(2,1)} %collective-permute-done.12.refs_8_), channel_id=1, source_target_pairs={{0,2},{2,0},{1,3},{3,1},{4,6},{6,4},{5,7},{7,5},{8,10},{10,8},{9,1... | collective-permute-start | bytes 3145736 | tf_op jit(solution)/shard_map/ppermute | solution.py:257
  158.9 17.0 %collective-permute-start.18 = (bf16[256,2048]{1,0:T(8,128)(2,1)}, bf16[256,2048]{1,0:T(8,128)(2,1)}, u32[]{:S(2)}, u32[]{:S(2)}) collective-permute-start(bf16[256,2048]{1,0:T(8,128)(2,1)} %collective-permute-done.17.refs_10_), channel_id=1, source_target_pairs={{0,2},{2,0},{1,3},{3,1},{4,6},{6,4},{5,7},{7,5},{8,10},{10,8},{9,1... | collective-permute-start | bytes 3145736 | tf_op jit(solution)/shard_map/ppermute | solution.py:257
  162.1 13.7 %collective-permute-start.20 = (bf16[256,2048]{1,0:T(8,128)(2,1)}, bf16[256,2048]{1,0:T(8,128)(2,1)}, u32[]{:S(2)}, u32[]{:S(2)}) collective-permute-start(bf16[256,2048]{1,0:T(8,128)(2,1)} %collective-permute-done.19.refs_12_), channel_id=1, source_target_pairs={{0,2},{2,0},{1,3},{3,1},{4,6},{6,4},{5,7},{7,5},{8,10},{10,8},{9,1... | collective-permute-start | bytes 3145736 | tf_op jit(solution)/shard_map/ppermute | solution.py:257
  165.0 10.9 %collective-permute-start.23 = (bf16[256,2048]{1,0:T(8,128)(2,1)}, bf16[256,2048]{1,0:T(8,128)(2,1)}, u32[]{:S(2)}, u32[]{:S(2)}) collective-permute-start(bf16[256,2048]{1,0:T(8,128)(2,1)} %constant_dynamic-update-slice_fusion.refs_14_), channel_id=1, source_target_pairs={{0,2},{2,0},{1,3},{3,1},{4,6},{6,4},{5,7},{7,5},{8,10},{10,8},{9,1... | collective-permute-start | bytes 3145736 | tf_op jit(solution)/shard_map/ppermute | solution.py:257
  (13 other events, 175.6 us)

commit v11 on v9

--- a/solution.py
+++ b/solution.py
@@ -147,25 +147,39 @@
     return block.reshape(block.shape[0], heads_dev, HEAD_DIM)
 
 
-def project_blocks(normed, blocks, group=4):
+def project_blocks(normed, starts, blocks, group=4):
     n = len(blocks)
     rows, cols = blocks[0].shape
     tokens = normed.shape[0]
-    def kernel(normed_ref, *refs):
+
+    def kernel(starts_ref, normed_ref, *refs):
         block_refs = refs[:n]
-        out_ref, weights, sems, acc = refs[n:]
-        copies = [
-            pltpu.make_async_copy(block_refs[i], weights.at[pl.ds(i * rows, rows), :], sems.at[i])
-            for i in range(n)
-        ]
-        for c in copies:
-            c.start()
+        out_ref, features, weights, sems, acc = refs[n:]
+        copies = []
+        for i in range(n):
+            start = pl.multiple_of(starts_ref[i], rows)
+            copies.append(
+                (
+                    pltpu.make_async_copy(
+                        normed_ref.at[:, pl.ds(start, rows)],
+                        features.at[:, pl.ds(i * rows, rows)],
+                        sems.at[0, i],
+                    ),
+                    pltpu.make_async_copy(
+                        block_refs[i], weights.at[pl.ds(i * rows, rows), :], sems.at[1, i]
+                    ),
+                )
+            )
+        for pair in copies:
+            for c in pair:
+                c.start()
         for g in range(0, n, group):
             last = min(g + group, n)
             for i in range(g, last):
-                copies[i].wait()
+                for c in copies[i]:
+                    c.wait()
             part = jnp.dot(
-                normed_ref[:, g * rows:last * rows],
+                features[:, g * rows:last * rows],
                 weights[g * rows:last * rows, :],
                 preferred_element_type=jnp.float32,
             )
@@ -174,17 +188,20 @@
             else:
                 acc[...] += part
         out_ref[...] = acc[...].astype(out_ref.dtype)
+
     return pl.pallas_call(
         kernel,
         out_shape=jax.ShapeDtypeStruct((tokens, cols), jnp.bfloat16),
-        in_specs=[pl.BlockSpec(memory_space=pltpu.VMEM)] + [pl.BlockSpec(memory_space=pl.ANY)] * n,
+        in_specs=[pl.BlockSpec(memory_space=pltpu.SMEM), pl.BlockSpec(memory_space=pl.ANY)]
+        + [pl.BlockSpec(memory_space=pl.ANY)] * n,
         out_specs=pl.BlockSpec(memory_space=pltpu.VMEM),
         scratch_shapes=[
+            pltpu.VMEM((tokens, n * rows), normed.dtype),
             pltpu.VMEM((n * rows, cols), blocks[0].dtype),
-            pltpu.SemaphoreType.DMA((n,)),
+            pltpu.SemaphoreType.DMA((2, n)),
             pltpu.VMEM((tokens, cols), jnp.float32),
         ],
-    )(normed, *blocks)
+    )(starts, normed, *blocks)
 
 
 def local_gather(queries, keys, values, out_weight, norm_gain, n_chip, n_head):
@@ -251,12 +268,11 @@
     normed = normalize(query_heads, prefix, within_block, norm_gain)
     gathered = gather_head(normed, n_head, place)
     row_count = gathered.shape[0]
-    split = gathered.reshape(row_count, n_chip, 2, out_weight.shape[0])
     ring_place = jnp.asarray([order.index(j) for j in range(n_chip)], jnp.int32)[lax.axis_index("chip")]
     sources = jnp.asarray(order, jnp.int32)[(ring_place - jnp.asarray(offsets, jnp.int32)) % n_chip]
-    by_offset = jnp.take(split, sources, axis=1)
-    by_offset = jnp.where(core == 0, by_offset, by_offset[:, :, ::-1]).reshape(row_count, -1)
-    return project_blocks(by_offset, [w for pair in zip(got, swapped) for w in pair])
+    cores = jnp.stack([core, 1 - core]).astype(jnp.int32)
+    starts = ((sources[:, None] * 2 + cores[None, :]) * out_weight.shape[0]).reshape(-1)
+    return project_blocks(gathered, starts, [w for pair in zip(got, swapped) for w in pair])
 
 
 def solution(mesh):

time: 184 us -> 175 us (0.951)
  local copies, waits for them, and re-layouts: 30.6 us -> 20.8 us
  waiting for transfers between devices: 91.6 us -> 96.2 us
  other arithmetic: 11.6 us -> 8.14 us
    ppermute x3, waiting for transfers between devices: 32.9 us -> 38.6 us  [exclusive_prefix(): total = total + lax.ppermute(total, axis, pairs)]
    reshape x2 -> x1, local copies, waits for them, and re-layouts: 5.24 us -> 1.49 us  [normalize(): return normed.reshape(query_heads.shape[0], heads_dev * HEAD_DIM)]
    dynamic_slice x3, local copies, waits for them, and re-layouts: 4.03 us -> 0.81 us  [head_blocks(): own = lax.dynamic_index_in_dim(stacked, place, 2, False)]
    select_n x3, other arithmetic: 2.62 us -> 0.29 us  [pair_order(): first = jnp.where(place == 0, own, other)]
    gather x1 -> x0, local copies, waits for them, and re-layouts: 2.27 us -> none  [local_ring(): by_offset = jnp.take(split, sources, axis=1)]
    select_n x1 -> x0, local copies, waits for them, and re-layouts: 2.16 us -> none  [local_ring(): jnp.where(core == 0, by_offset, by_offset[:, :, ::-1])]
    add x2, other arithmetic: 2.19 us -> 0.11 us  [exclusive_prefix(): total = total + lax.ppermute(total, axis, pairs)]
  transfers between devices with their start and end apart: 24 -> 24, of which waited for: 10 -> 11; matrix products, arithmetic and copies ran while one was open for 21% -> 14% of each run, Pallas kernels for 0% -> 0%
where the time goes in v11:
time: 175 us; the launch traced here: 173 us
  waiting for transfers between devices  96.2 us (55%)
  starting transfers between devices  32 us (18%)
  local copies, waits for them, and re-layouts  20.8 us (12%)
  Pallas kernels  9.62 us (5%)
  other arithmetic  8.14 us (5%)
  matrix products  5.53 us (3%)
    ppermute x3, waiting for transfers between devices, exclusive_prefix(): total = total + lax.ppermute(total, axis, pairs)  38.6 us
    ppermute x3, waiting for transfers between devices, ring_step(): lax.ppermute(ahead, 'chip', forward)  29.2 us
    ppermute x2, waiting for transfers between devices, head_blocks(): other = lax.ppermute(sent, 'head', SWAP)  21.1 us
    pallas_call x1, Pallas kernels, project_blocks(): pl.pallas_call(kernel, out_shape=jax.ShapeDtypeStruct((tokens, cols), jnp...  9.62 us
    ppermute x5, starting transfers between devices, local_ring(): swapped += [lax.ppermute(w, 'core', SWAP) for w in got[len(swapped):]]  8.6 us
    ppermute x3, starting transfers between devices, exclusive_prefix(): total = total + lax.ppermute(total, axis, pairs)  8.4 us
    unnamed x28, local copies, waits for them, and re-layouts  7.43 us
    ppermute x1, waiting for transfers between devices, ring_step(): lax.ppermute(ahead[:half_rows], 'chip', forward)  3.52 us
  transfers between devices with their start and end apart: 24, of which 11 were waited for; matrix products, arithmetic and copies ran while one was open for 14% of the time, Pallas kernels for 0%

profile of v11, /device:TPU:13, one launch (start us, length us, event | category | flops | bytes accessed | tf_op | source)
XLA Modules:
  0.0 172.8 jit_solution(12556372985501974862)
XLA Ops:
  3.6 2.3 %copy.22 = bf16[2,128,1,2048]{3,1,0,2:T(8,128)(2,1)} copy(bf16[2,128,1,2048]{1,3,2,0:T(8,128)(2,1)} %get-tuple-element.30) | data formatting | bytes 2097152 | tf_op jit(solution)/shard_map/jit(dynamic_index_in_dim)/dynamic_slice | solution.py:37
  9.1 21.1 %collective-permute-done.2 = bf16[2,128,2048]{2,1,0:T(8,128)(2,1)S(1)} collective-permute-done((bf16[2,128,2048]{2,1,0:T(8,128)(2,1)}, bf16[2,128,2048]{2,1,0:T(8,128)(2,1)S(1)}, u32[]{:S(2)}, u32[]{:S(2)}) %collective-permute-start.2) | collective-permute-done | bytes 1048608 | tf_op jit(solution)/shard_map/ppermute | solution.py:38
  33.1 2.2 %collective-permute-start.3 = (f32[16,128,128]{2,1,0:T(8,128)S(1)}, f32[16,128,128]{2,1,0:T(8,128)}, u32[]{:S(2)}, u32[]{:S(2)}) collective-permute-start(f32[16,128,128]{2,1,0:T(8,128)S(1)} %fusion.6), channel_id=1, source_target_pairs={{0,2},{2,0},{1,3},{3,1},{4,6},{6,4},{5,7},{7,5},{8,10},{10,8},{9,1... | collective-permute-start | bytes 3145736 | tf_op jit(solution)/shard_map/ppermute | solution.py:133
  35.4 2.4 %collective-permute-done.3 = f32[16,128,128]{2,1,0:T(8,128)} collective-permute-done((f32[16,128,128]{2,1,0:T(8,128)S(1)}, f32[16,128,128]{2,1,0:T(8,128)}, u32[]{:S(2)}, u32[]{:S(2)}) %collective-permute-start.3) | collective-permute-done | bytes 1048608 | tf_op jit(solution)/shard_map/ppermute | solution.py:133
  38.9 2.0 %collective-permute-start.4 = (f32[8,128,128]{2,1,0:T(8,128)S(1)}, f32[8,128,128]{2,1,0:T(8,128)S(1)}, u32[]{:S(2)}, u32[]{:S(2)}) collective-permute-start(f32[8,128,128]{2,1,0:T(8,128)S(1)} %dynamic-slice_add_fusion), channel_id=1, source_target_pairs={{0,4},{4,8},{8,12},{12,16},{16,20},{20,24},{24,28},{1,5},{5,9},{9,... | collective-permute-start | bytes 1572872 | tf_op jit(solution)/shard_map/ppermute | solution.py:20
  42.6 11.3 %collective-permute-done.4 = f32[8,128,128]{2,1,0:T(8,128)S(1)} collective-permute-done((f32[8,128,128]{2,1,0:T(8,128)S(1)}, f32[8,128,128]{2,1,0:T(8,128)S(1)}, u32[]{:S(2)}, u32[]{:S(2)}) %collective-permute-start.4) | collective-permute-done | bytes 524320 | tf_op jit(solution)/shard_map/ppermute | solution.py:20
  54.0 3.2 %collective-permute-start.5 = (f32[8,128,128]{2,1,0:T(8,128)S(1)}, f32[8,128,128]{2,1,0:T(8,128)S(1)}, u32[]{:S(2)}, u32[]{:S(2)}) collective-permute-start(f32[8,128,128]{2,1,0:T(8,128)S(1)} %add.80), channel_id=1, source_target_pairs={{0,8},{4,12},{8,16},{12,20},{16,24},{20,28},{1,9},{5,13},{9,17},{1... | collective-permute-start | bytes 1572872 | tf_op jit(solution)/shard_map/ppermute | solution.py:20
  58.5 1.8 %collective-permute-start.8 = (bf16[256,2048]{1,0:T(8,128)(2,1)}, bf16[256,2048]{1,0:T(8,128)(2,1)}, u32[]{:S(2)}, u32[]{:S(2)}) collective-permute-start(bf16[256,2048]{1,0:T(8,128)(2,1)} %refs_0_.1), channel_id=1, source_target_pairs={{0,2},{2,0},{1,3},{3,1},{4,6},{6,4},{5,7},{7,5},{8,10},{10,8},{9,1... | collective-permute-start | bytes 3145736 | tf_op jit(solution)/shard_map/ppermute | solution.py:247
  61.1 7.0 %collective-permute-done.5 = f32[8,128,128]{2,1,0:T(8,128)S(1)} collective-permute-done((f32[8,128,128]{2,1,0:T(8,128)S(1)}, f32[8,128,128]{2,1,0:T(8,128)S(1)}, u32[]{:S(2)}, u32[]{:S(2)}) %collective-permute-start.5) | collective-permute-done | bytes 524320 | tf_op jit(solution)/shard_map/ppermute | solution.py:20
  68.1 3.2 %collective-permute-start.6 = (f32[8,128,128]{2,1,0:T(8,128)S(1)}, f32[8,128,128]{2,1,0:T(8,128)S(1)}, u32[]{:S(2)}, u32[]{:S(2)}) collective-permute-start(f32[8,128,128]{2,1,0:T(8,128)S(1)} %add.81), channel_id=1, source_target_pairs={{0,16},{4,20},{8,24},{12,28},{1,17},{5,21},{9,25},{13,29},{2,18},{... | collective-permute-start | bytes 1572872 | tf_op jit(solution)/shard_map/ppermute | solution.py:20
  72.8 20.3 %collective-permute-done.6 = f32[8,128,128]{2,1,0:T(8,128)S(1)} collective-permute-done((f32[8,128,128]{2,1,0:T(8,128)S(1)}, f32[8,128,128]{2,1,0:T(8,128)S(1)}, u32[]{:S(2)}, u32[]{:S(2)}) %collective-permute-start.6) | collective-permute-done | bytes 524320 | tf_op jit(solution)/shard_map/ppermute | solution.py:20
  94.0 3.2 %fusion.1 = f32[256,16,128]{0,2,1:T(8,128)S(1)} fusion(bf16[256,16,128]{0,2,1:T(8,128)(2,1)} %bitcast.49, bf16[256,16,128]{0,2,1:T(8,128)(2,1)} %bitcast.54, pred[256,256]{1,0:T(8,128)(4,1)S(1)} %iota_compare_fusion, bf16[256,2048]{1,0:T(8,128)(2,1)} %copy-done.2), kind=kOutput, calls=%fused_computation.13 | convolution fusion | flops 538968064 | bytes 5308416 | tf_op jit(solution)/shard_map/hts,she->the/dot_general | solution.py:106
  98.6 2.7 %collective-permute-start.11 = (f32[8,128,128]{2,1,0:T(8,128)S(1)}, f32[8,128,128]{2,1,0:T(8,128)S(1)}, u32[]{:S(2)}, u32[]{:S(2)}) collective-permute-start(f32[8,128,128]{2,1,0:T(8,128)S(1)} %add_subtract_fusion), channel_id=1, source_target_pairs={{0,2},{2,0},{1,3},{3,1},{4,6},{6,4},{5,7},{7,5},{8,10},{10,8},{9,1... | collective-permute-start | bytes 1572872 | tf_op jit(solution)/shard_map/ppermute | solution.py:141
  102.5 13.2 %collective-permute-done.13.refs_6_ = bf16[256,2048]{1,0:T(8,128)(2,1)} collective-permute-done((bf16[256,2048]{1,0:T(8,128)(2,1)}, bf16[256,2048]{1,0:T(8,128)(2,1)}, u32[]{:S(2)}, u32[]{:S(2)}) %collective-permute-start.13) | collective-permute-done | bytes 1048608 | tf_op jit(solution)/shard_map/ppermute | solution.py:85
  115.7 2.2 %collective-permute-start.17 = (bf16[256,2048]{1,0:T(8,128)(2,1)}, bf16[256,2048]{1,0:T(8,128)(2,1)}, u32[]{:S(2)}, u32[]{:S(2)}) collective-permute-start(bf16[256,2048]{1,0:T(8,128)(2,1)} %collective-permute-done.13.refs_6_), channel_id=1, source_target_pairs={{0,4},{4,12},{12,20},{20,28},{28,24},{24,16},{16,8},{8,0},{1,5},{5... | collective-permute-start | bytes 3145736 | tf_op jit(solution)/shard_map/ppermute | solution.py:85
  118.1 1.8 %multiply_reduce_fusion = (f32[256,16]{0,1:T(8,128)S(1)}, f32[16,128,256]{2,1,0:T(8,128)S(1)}) fusion(f32[256,16,128]{0,2,1:T(8,128)S(1)} %fusion.1, bf16[256,16,128]{0,2,1:T(8,128)(2,1)S(1)} %bitcast.55, f32[8,128,128]{2,1,0:T(8,128)S(1)} %get-tuple-element.32, f32[8,128,128]{2,1,0:T(8,128)S(1)} %get-tuple-element.31, ...), kind=kOutput, calls=%fused_computation.11 | convolution fusion | flops 136835072 | bytes 7356417 | tf_op jit(solution)/shard_map/thd,hde->the/dot_general | solution.py:115
  123.8 15.4 %collective-permute-done.17.refs_10_ = bf16[256,2048]{1,0:T(8,128)(2,1)} collective-permute-done((bf16[256,2048]{1,0:T(8,128)(2,1)}, bf16[256,2048]{1,0:T(8,128)(2,1)}, u32[]{:S(2)}, u32[]{:S(2)}) %collective-permute-start.17) | collective-permute-done | bytes 1048608 | tf_op jit(solution)/shard_map/ppermute | solution.py:85
  140.3 2.3 %collective-permute-start.21 = (bf16[128,2048]{1,0:T(8,128)(2,1)S(1)}, bf16[128,2048]{1,0:T(8,128)(2,1)S(1)}, u32[]{:S(2)}, u32[]{:S(2)}) collective-permute-start(bf16[128,2048]{1,0:T(8,128)(2,1)S(1)} %slice.20), channel_id=1, source_target_pairs={{0,4},{4,12},{12,20},{20,28},{28,24},{24,16},{16,8},{8,0},{1,5},{5... | collective-permute-start | bytes 1572872 | tf_op jit(solution)/shard_map/ppermute | solution.py:82
  142.5 1.9 %slice.21 = bf16[128,2048]{1,0:T(8,128)(2,1)} slice(bf16[256,2048]{1,0:T(8,128)(2,1)} %collective-permute-done.19.refs_12_), slice={[128:256], [0:2048]} | slice | bytes 1048576 | tf_op jit(solution)/shard_map/slice | solution.py:83
  145.2 2.7 %collective-permute-start.14 = (bf16[256,2048]{1,0:T(8,128)(2,1)}, bf16[256,2048]{1,0:T(8,128)(2,1)}, u32[]{:S(2)}, u32[]{:S(2)}) collective-permute-start(bf16[256,2048]{1,0:T(8,128)(2,1)} %collective-permute-done.13.refs_6_), channel_id=1, source_target_pairs={{0,2},{2,0},{1,3},{3,1},{4,6},{6,4},{5,7},{7,5},{8,10},{10,8},{9,1... | collective-permute-start | bytes 3145736 | tf_op jit(solution)/shard_map/ppermute | solution.py:266
  147.9 3.5 %collective-permute-done.21 = bf16[128,2048]{1,0:T(8,128)(2,1)S(1)} collective-permute-done((bf16[128,2048]{1,0:T(8,128)(2,1)S(1)}, bf16[128,2048]{1,0:T(8,128)(2,1)S(1)}, u32[]{:S(2)}, u32[]{:S(2)}) %collective-permute-start.21) | collective-permute-done | bytes 524320 | tf_op jit(solution)/shard_map/ppermute | solution.py:82
  152.2 3.3 %collective-permute-start.18 = (bf16[256,2048]{1,0:T(8,128)(2,1)}, bf16[256,2048]{1,0:T(8,128)(2,1)}, u32[]{:S(2)}, u32[]{:S(2)}) collective-permute-start(bf16[256,2048]{1,0:T(8,128)(2,1)} %collective-permute-done.17.refs_10_), channel_id=1, source_target_pairs={{0,2},{2,0},{1,3},{3,1},{4,6},{6,4},{5,7},{7,5},{8,10},{10,8},{9,1... | collective-permute-start | bytes 3145736 | tf_op jit(solution)/shard_map/ppermute | solution.py:266
  156.5 2.6 %collective-permute-start.20 = (bf16[256,2048]{1,0:T(8,128)(2,1)}, bf16[256,2048]{1,0:T(8,128)(2,1)}, u32[]{:S(2)}, u32[]{:S(2)}) collective-permute-start(bf16[256,2048]{1,0:T(8,128)(2,1)} %collective-permute-done.19.refs_12_), channel_id=1, source_target_pairs={{0,2},{2,0},{1,3},{3,1},{4,6},{6,4},{5,7},{7,5},{8,10},{10,8},{9,1... | collective-permute-start | bytes 3145736 | tf_op jit(solution)/shard_map/ppermute | solution.py:266
  163.1 9.6 %shard_map.82 = bf16[256,2048]{1,0:T(8,128)(2,1)} custom-call(s32[16]{0:T(128)} %mul.41.starts_ref, bf16[256,4096]{1,0:T(8,128)(2,1)} %pad_maximum_fusion.normed_ref, bf16[256,2048]{1,0:T(8,128)(2,1)} %refs_0_.1, bf16[256,2048]{1,0:T(8,128)(2,1)} %collective-permute-done.8.refs_1_, bf16[256,2048]{1,0:T(8,128)(2,1)} %collective-permute-done.refs_2_, ...), custom_call_target="tpu_custom_call" | custom-call | tf_op jit(solution)/shard_map/pallas_call | solution.py:192
  (90 shorter events, 31.0 us)
Async XLA Ops:
  5.9 24.3 %collective-permute-start.2 = (bf16[2,128,2048]{2,1,0:T(8,128)(2,1)}, bf16[2,128,2048]{2,1,0:T(8,128)(2,1)S(1)}, u32[]{:S(2)}, u32[]{:S(2)}) collective-permute-start(bf16[2,128,2048]{2,1,0:T(8,128)(2,1)} %bitcast.6), channel_id=1, source_target_pairs={{0,1},{1,0},{2,3},{3,2},{4,5},{5,4},{6,7},{7,6},{8,9},{9,8},{10,11... | collective-permute-start | bytes 3145736 | tf_op jit(solution)/shard_map/ppermute | solution.py:38
  7.1 24.0 %collective-permute-start = (bf16[256,2048]{1,0:T(8,128)(2,1)}, bf16[256,2048]{1,0:T(8,128)(2,1)}, u32[]{:S(2)}, u32[]{:S(2)}) collective-permute-start(bf16[256,2048]{1,0:T(8,128)(2,1)} %refs_0_.1), channel_id=1, source_target_pairs={{0,4},{4,12},{12,20},{20,28},{28,24},{24,16},{16,8},{8,0},{1,5},{5... | collective-permute-start | bytes 3145736 | tf_op jit(solution)/shard_map/ppermute | solution.py:85
  8.4 23.7 %collective-permute-start.1 = (bf16[256,2048]{1,0:T(8,128)(2,1)}, bf16[256,2048]{1,0:T(8,128)(2,1)}, u32[]{:S(2)}, u32[]{:S(2)}) collective-permute-start(bf16[256,2048]{1,0:T(8,128)(2,1)} %refs_0_.1), channel_id=1, source_target_pairs={{4,0},{12,4},{20,12},{28,20},{24,28},{16,24},{8,16},{0,8},{5,1},{1... | collective-permute-start | bytes 3145736 | tf_op jit(solution)/shard_map/ppermute | solution.py:85
  33.1 4.6 %collective-permute-start.3 = (f32[16,128,128]{2,1,0:T(8,128)S(1)}, f32[16,128,128]{2,1,0:T(8,128)}, u32[]{:S(2)}, u32[]{:S(2)}) collective-permute-start(f32[16,128,128]{2,1,0:T(8,128)S(1)} %fusion.6), channel_id=1, source_target_pairs={{0,2},{2,0},{1,3},{3,1},{4,6},{6,4},{5,7},{7,5},{8,10},{10,8},{9,1... | collective-permute-start | bytes 3145736 | tf_op jit(solution)/shard_map/ppermute | solution.py:133
  38.9 15.0 %collective-permute-start.4 = (f32[8,128,128]{2,1,0:T(8,128)S(1)}, f32[8,128,128]{2,1,0:T(8,128)S(1)}, u32[]{:S(2)}, u32[]{:S(2)}) collective-permute-start(f32[8,128,128]{2,1,0:T(8,128)S(1)} %dynamic-slice_add_fusion), channel_id=1, source_target_pairs={{0,4},{4,8},{8,12},{12,16},{16,20},{20,24},{24,28},{1,5},{5,9},{9,... | collective-permute-start | bytes 1572872 | tf_op jit(solution)/shard_map/ppermute | solution.py:20
  54.0 14.1 %collective-permute-start.5 = (f32[8,128,128]{2,1,0:T(8,128)S(1)}, f32[8,128,128]{2,1,0:T(8,128)S(1)}, u32[]{:S(2)}, u32[]{:S(2)}) collective-permute-start(f32[8,128,128]{2,1,0:T(8,128)S(1)} %add.80), channel_id=1, source_target_pairs={{0,8},{4,12},{8,16},{12,20},{16,24},{20,28},{1,9},{5,13},{9,17},{1... | collective-permute-start | bytes 1572872 | tf_op jit(solution)/shard_map/ppermute | solution.py:20
  58.2 13.1 %collective-permute-start.7 = (bf16[1,128,2048]{2,1,0:T(8,128)(2,1)}, bf16[1,128,2048]{2,1,0:T(8,128)(2,1)S(1)}, u32[]{:S(2)}, u32[]{:S(2)}) collective-permute-start(bf16[1,128,2048]{2,1,0:T(8,128)(2,1)} %bitcast.11), channel_id=1, source_target_pairs={{0,1},{1,0},{2,3},{3,2},{4,5},{5,4},{6,7},{7,6},{8,9},{9,8},{10,11... | collective-permute-start | bytes 1572872 | tf_op jit(solution)/shard_map/ppermute | solution.py:38
  58.5 40.1 %collective-permute-start.8 = (bf16[256,2048]{1,0:T(8,128)(2,1)}, bf16[256,2048]{1,0:T(8,128)(2,1)}, u32[]{:S(2)}, u32[]{:S(2)}) collective-permute-start(bf16[256,2048]{1,0:T(8,128)(2,1)} %refs_0_.1), channel_id=1, source_target_pairs={{0,2},{2,0},{1,3},{3,1},{4,6},{6,4},{5,7},{7,5},{8,10},{10,8},{9,1... | collective-permute-start | bytes 3145736 | tf_op jit(solution)/shard_map/ppermute | solution.py:247
  60.5 38.1 %collective-permute-start.10 = (bf16[256,2048]{1,0:T(8,128)(2,1)}, bf16[256,2048]{1,0:T(8,128)(2,1)}, u32[]{:S(2)}, u32[]{:S(2)}) collective-permute-start(bf16[256,2048]{1,0:T(8,128)(2,1)} %collective-permute-done.1.refs_4_), channel_id=1, source_target_pairs={{0,2},{2,0},{1,3},{3,1},{4,6},{6,4},{5,7},{7,5},{8,10},{10,8},{9,1... | collective-permute-start | bytes 3145736 | tf_op jit(solution)/shard_map/ppermute | solution.py:247
  60.6 38.0 %collective-permute-start.9 = (bf16[256,2048]{1,0:T(8,128)(2,1)}, bf16[256,2048]{1,0:T(8,128)(2,1)}, u32[]{:S(2)}, u32[]{:S(2)}) collective-permute-start(bf16[256,2048]{1,0:T(8,128)(2,1)} %collective-permute-done.refs_2_), channel_id=1, source_target_pairs={{0,2},{2,0},{1,3},{3,1},{4,6},{6,4},{5,7},{7,5},{8,10},{10,8},{9,1... | collective-permute-start | bytes 3145736 | tf_op jit(solution)/shard_map/ppermute | solution.py:247
  68.1 25.0 %collective-permute-start.6 = (f32[8,128,128]{2,1,0:T(8,128)S(1)}, f32[8,128,128]{2,1,0:T(8,128)S(1)}, u32[]{:S(2)}, u32[]{:S(2)}) collective-permute-start(f32[8,128,128]{2,1,0:T(8,128)S(1)} %add.81), channel_id=1, source_target_pairs={{0,16},{4,20},{8,24},{12,28},{1,17},{5,21},{9,25},{13,29},{2,18},{... | collective-permute-start | bytes 1572872 | tf_op jit(solution)/shard_map/ppermute | solution.py:20
  72.8 42.9 %collective-permute-start.13 = (bf16[256,2048]{1,0:T(8,128)(2,1)}, bf16[256,2048]{1,0:T(8,128)(2,1)}, u32[]{:S(2)}, u32[]{:S(2)}) collective-permute-start(bf16[256,2048]{1,0:T(8,128)(2,1)} %collective-permute-done.refs_2_), channel_id=1, source_target_pairs={{0,4},{4,12},{12,20},{20,28},{28,24},{24,16},{16,8},{8,0},{1,5},{5... | collective-permute-start | bytes 3145736 | tf_op jit(solution)/shard_map/ppermute | solution.py:85
  93.2 24.8 %collective-permute-start.15 = (bf16[256,2048]{1,0:T(8,128)(2,1)}, bf16[256,2048]{1,0:T(8,128)(2,1)}, u32[]{:S(2)}, u32[]{:S(2)}) collective-permute-start(bf16[256,2048]{1,0:T(8,128)(2,1)} %collective-permute-done.1.refs_4_), channel_id=1, source_target_pairs={{4,0},{12,4},{20,12},{28,20},{24,28},{16,24},{8,16},{0,8},{5,1},{1... | collective-permute-start | bytes 3145736 | tf_op jit(solution)/shard_map/ppermute | solution.py:85
  98.6 19.4 %collective-permute-start.11 = (f32[8,128,128]{2,1,0:T(8,128)S(1)}, f32[8,128,128]{2,1,0:T(8,128)S(1)}, u32[]{:S(2)}, u32[]{:S(2)}) collective-permute-start(f32[8,128,128]{2,1,0:T(8,128)S(1)} %add_subtract_fusion), channel_id=1, source_target_pairs={{0,2},{2,0},{1,3},{3,1},{4,6},{6,4},{5,7},{7,5},{8,10},{10,8},{9,1... | collective-permute-start | bytes 1572872 | tf_op jit(solution)/shard_map/ppermute | solution.py:141
  115.7 23.4 %collective-permute-start.17 = (bf16[256,2048]{1,0:T(8,128)(2,1)}, bf16[256,2048]{1,0:T(8,128)(2,1)}, u32[]{:S(2)}, u32[]{:S(2)}) collective-permute-start(bf16[256,2048]{1,0:T(8,128)(2,1)} %collective-permute-done.13.refs_6_), channel_id=1, source_target_pairs={{0,4},{4,12},{12,20},{20,28},{28,24},{24,16},{16,8},{8,0},{1,5},{5... | collective-permute-start | bytes 3145736 | tf_op jit(solution)/shard_map/ppermute | solution.py:85
  117.9 24.6 %collective-permute-start.19 = (bf16[256,2048]{1,0:T(8,128)(2,1)}, bf16[256,2048]{1,0:T(8,128)(2,1)}, u32[]{:S(2)}, u32[]{:S(2)}) collective-permute-start(bf16[256,2048]{1,0:T(8,128)(2,1)} %collective-permute-done.15.refs_8_), channel_id=1, source_target_pairs={{4,0},{12,4},{20,12},{28,20},{24,28},{16,24},{8,16},{0,8},{5,1},{1... | collective-permute-start | bytes 3145736 | tf_op jit(solution)/shard_map/ppermute | solution.py:85
  122.8 37.4 %collective-permute-start.12 = (bf16[256,2048]{1,0:T(8,128)(2,1)S(1)}, bf16[256,2048]{1,0:T(8,128)(2,1)S(1)}, u32[]{:S(2)}, u32[]{:S(2)}) collective-permute-start(bf16[256,2048]{1,0:T(8,128)(2,1)S(1)} %copy.38), channel_id=1, source_target_pairs={{0,1},{1,0},{2,3},{3,2},{4,5},{5,4},{6,7},{7,6},{8,9},{9,8},{10,11... | collective-permute-start | bytes 3145736 | tf_op jit(solution)/shard_map/ppermute | solution.py:127
  140.3 11.1 %collective-permute-start.21 = (bf16[128,2048]{1,0:T(8,128)(2,1)S(1)}, bf16[128,2048]{1,0:T(8,128)(2,1)S(1)}, u32[]{:S(2)}, u32[]{:S(2)}) collective-permute-start(bf16[128,2048]{1,0:T(8,128)(2,1)S(1)} %slice.20), channel_id=1, source_target_pairs={{0,4},{4,12},{12,20},{20,28},{28,24},{24,16},{16,8},{8,0},{1,5},{5... | collective-permute-start | bytes 1572872 | tf_op jit(solution)/shard_map/ppermute | solution.py:82
  144.4 12.1 %collective-permute-start.22 = (bf16[128,2048]{1,0:T(8,128)(2,1)}, bf16[128,2048]{1,0:T(8,128)(2,1)}, u32[]{:S(2)}, u32[]{:S(2)}) collective-permute-start(bf16[128,2048]{1,0:T(8,128)(2,1)} %slice.21), channel_id=1, source_target_pairs={{4,0},{12,4},{20,12},{28,20},{24,28},{16,24},{8,16},{0,8},{5,1},{1... | collective-permute-start | bytes 1572872 | tf_op jit(solution)/shard_map/ppermute | solution.py:82
  145.2 17.6 %collective-permute-start.14 = (bf16[256,2048]{1,0:T(8,128)(2,1)}, bf16[256,2048]{1,0:T(8,128)(2,1)}, u32[]{:S(2)}, u32[]{:S(2)}) collective-permute-start(bf16[256,2048]{1,0:T(8,128)(2,1)} %collective-permute-done.13.refs_6_), channel_id=1, source_target_pairs={{0,2},{2,0},{1,3},{3,1},{4,6},{6,4},{5,7},{7,5},{8,10},{10,8},{9,1... | collective-permute-start | bytes 3145736 | tf_op jit(solution)/shard_map/ppermute | solution.py:266
  147.9 14.9 %collective-permute-start.16 = (bf16[256,2048]{1,0:T(8,128)(2,1)}, bf16[256,2048]{1,0:T(8,128)(2,1)}, u32[]{:S(2)}, u32[]{:S(2)}) collective-permute-start(bf16[256,2048]{1,0:T(8,128)(2,1)} %collective-permute-done.15.refs_8_), channel_id=1, source_target_pairs={{0,2},{2,0},{1,3},{3,1},{4,6},{6,4},{5,7},{7,5},{8,10},{10,8},{9,1... | collective-permute-start | bytes 3145736 | tf_op jit(solution)/shard_map/ppermute | solution.py:266
  152.2 10.5 %collective-permute-start.18 = (bf16[256,2048]{1,0:T(8,128)(2,1)}, bf16[256,2048]{1,0:T(8,128)(2,1)}, u32[]{:S(2)}, u32[]{:S(2)}) collective-permute-start(bf16[256,2048]{1,0:T(8,128)(2,1)} %collective-permute-done.17.refs_10_), channel_id=1, source_target_pairs={{0,2},{2,0},{1,3},{3,1},{4,6},{6,4},{5,7},{7,5},{8,10},{10,8},{9,1... | collective-permute-start | bytes 3145736 | tf_op jit(solution)/shard_map/ppermute | solution.py:266
  156.5 6.2 %collective-permute-start.20 = (bf16[256,2048]{1,0:T(8,128)(2,1)}, bf16[256,2048]{1,0:T(8,128)(2,1)}, u32[]{:S(2)}, u32[]{:S(2)}) collective-permute-start(bf16[256,2048]{1,0:T(8,128)(2,1)} %collective-permute-done.19.refs_12_), channel_id=1, source_target_pairs={{0,2},{2,0},{1,3},{3,1},{4,6},{6,4},{5,7},{7,5},{8,10},{10,8},{9,1... | collective-permute-start | bytes 3145736 | tf_op jit(solution)/shard_map/ppermute | solution.py:266
  160.2 2.9 %collective-permute-start.23 = (bf16[256,2048]{1,0:T(8,128)(2,1)S(1)}, bf16[256,2048]{1,0:T(8,128)(2,1)}, u32[]{:S(2)}, u32[]{:S(2)}) collective-permute-start(bf16[256,2048]{1,0:T(8,128)(2,1)S(1)} %constant_dynamic-update-slice_fusion.refs_14_), channel_id=1, source_target_pairs={{0,2},{2,0},{1,3},{3,1},{4,6},{6,4},{5,7},{7,5},{8,10},{10,8},{9,1... | collective-permute-start | bytes 3145736 | tf_op jit(solution)/shard_map/ppermute | solution.py:266
  (12 other events, 42.2 us)

commit v12 on v11

--- a/solution.py
+++ b/solution.py
@@ -147,14 +147,18 @@
     return block.reshape(block.shape[0], heads_dev, HEAD_DIM)
 
 
-def project_blocks(normed, starts, blocks, group=4):
+def project_blocks(normed, starts, blocks, partial=None, group=4):
     n = len(blocks)
     rows, cols = blocks[0].shape
     tokens = normed.shape[0]
+    extra = [] if partial is None else [partial]
 
     def kernel(starts_ref, normed_ref, *refs):
         block_refs = refs[:n]
-        out_ref, features, weights, sems, acc = refs[n:]
+        refs = refs[n:]
+        if partial is not None:
+            partial_ref, refs = refs[0], refs[1:]
+        out_ref, features, weights, sems, acc = refs
         copies = []
         for i in range(n):
             start = pl.multiple_of(starts_ref[i], rows)
@@ -184,16 +188,19 @@
                 preferred_element_type=jnp.float32,
             )
             if g == 0:
-                acc[...] = part
+                acc[...] = part if partial is None else partial_ref[...] + part
             else:
                 acc[...] += part
         out_ref[...] = acc[...].astype(out_ref.dtype)
 
     return pl.pallas_call(
         kernel,
-        out_shape=jax.ShapeDtypeStruct((tokens, cols), jnp.bfloat16),
+        out_shape=jax.ShapeDtypeStruct(
+            (tokens, cols), jnp.float32 if partial is None else jnp.bfloat16
+        ),
         in_specs=[pl.BlockSpec(memory_space=pltpu.SMEM), pl.BlockSpec(memory_space=pl.ANY)]
-        + [pl.BlockSpec(memory_space=pl.ANY)] * n,
+        + [pl.BlockSpec(memory_space=pl.ANY)] * n
+        + [pl.BlockSpec(memory_space=pltpu.VMEM)] * len(extra),
         out_specs=pl.BlockSpec(memory_space=pltpu.VMEM),
         scratch_shapes=[
             pltpu.VMEM((tokens, n * rows), normed.dtype),
@@ -201,7 +208,7 @@
             pltpu.SemaphoreType.DMA((2, n)),
             pltpu.VMEM((tokens, cols), jnp.float32),
         ],
-    )(starts, normed, *blocks)
+    )(starts, normed, *blocks, *extra)
 
 
 def local_gather(queries, keys, values, out_weight, norm_gain, n_chip, n_head):
@@ -272,7 +279,9 @@
     sources = jnp.asarray(order, jnp.int32)[(ring_place - jnp.asarray(offsets, jnp.int32)) % n_chip]
     cores = jnp.stack([core, 1 - core]).astype(jnp.int32)
     starts = ((sources[:, None] * 2 + cores[None, :]) * out_weight.shape[0]).reshape(-1)
-    return project_blocks(gathered, starts, [w for pair in zip(got, swapped) for w in pair])
+    blocks = [w for pair in zip(got, swapped) for w in pair]
+    early = project_blocks(gathered, starts[:-2], blocks[:-2])
+    return project_blocks(gathered, starts[-2:], blocks[-2:], partial=early)
 
 
 def solution(mesh):

time: 175 us -> 181 us (1.034)
  Pallas kernels: 9.62 us -> 14.2 us
    pallas_call x1 -> x2, Pallas kernels: 9.62 us -> 14.2 us  [project_blocks(): pl.pallas_call(kernel, out_shape=jax.ShapeDtypeStruct((tokens, cols), jnp...]
  transfers between devices with their start and end apart: 24 -> 24, of which waited for: 11 -> 10; matrix products, arithmetic and copies ran while one was open for 14% -> 14% of each run, Pallas kernels for 0% -> 5%
where the time goes in v12:
time: 181 us; the launch traced here: 178 us
  waiting for transfers between devices  96.2 us (53%)
  starting transfers between devices  32.8 us (18%)
  local copies, waits for them, and re-layouts  19.7 us (11%)
  Pallas kernels  14.2 us (8%)
  other arithmetic  9.54 us (5%)
  matrix products  5.52 us (3%)
    ppermute x3, waiting for transfers between devices, exclusive_prefix(): total = total + lax.ppermute(total, axis, pairs)  38 us
    ppermute x3, waiting for transfers between devices, ring_step(): lax.ppermute(ahead, 'chip', forward)  30.7 us
    ppermute x2, waiting for transfers between devices, head_blocks(): other = lax.ppermute(sent, 'head', SWAP)  21.1 us
    pallas_call x2, Pallas kernels, project_blocks(): pl.pallas_call(kernel, out_shape=jax.ShapeDtypeStruct((tokens, cols), jnp...  14.2 us
    ppermute x3, starting transfers between devices, exclusive_prefix(): total = total + lax.ppermute(total, axis, pairs)  9.19 us
    ppermute x5, starting transfers between devices, local_ring(): swapped += [lax.ppermute(w, 'core', SWAP) for w in got[len(swapped):]]  8.64 us
    unnamed x28, local copies, waits for them, and re-layouts  6.64 us
  transfers between devices with their start and end apart: 24, of which 10 were waited for; matrix products, arithmetic and copies ran while one was open for 14% of the time, Pallas kernels for 5%

profile of v12, /device:TPU:13, one launch (start us, length us, event | category | flops | bytes accessed | tf_op | source)
XLA Modules:
  0.0 178.5 jit_solution(16066871898049921257)
XLA Ops:
  3.6 2.3 %copy.22 = bf16[2,128,1,2048]{3,1,0,2:T(8,128)(2,1)} copy(bf16[2,128,1,2048]{1,3,2,0:T(8,128)(2,1)} %get-tuple-element.30) | data formatting | bytes 2097152 | tf_op jit(solution)/shard_map/jit(dynamic_index_in_dim)/dynamic_slice | solution.py:37
  9.1 21.1 %collective-permute-done.2 = bf16[2,128,2048]{2,1,0:T(8,128)(2,1)S(1)} collective-permute-done((bf16[2,128,2048]{2,1,0:T(8,128)(2,1)}, bf16[2,128,2048]{2,1,0:T(8,128)(2,1)S(1)}, u32[]{:S(2)}, u32[]{:S(2)}) %collective-permute-start.2) | collective-permute-done | bytes 1048608 | tf_op jit(solution)/shard_map/ppermute | solution.py:38
  33.1 2.2 %collective-permute-start.3 = (f32[16,128,128]{2,1,0:T(8,128)S(1)}, f32[16,128,128]{2,1,0:T(8,128)}, u32[]{:S(2)}, u32[]{:S(2)}) collective-permute-start(f32[16,128,128]{2,1,0:T(8,128)S(1)} %fusion.6), channel_id=1, source_target_pairs={{0,2},{2,0},{1,3},{3,1},{4,6},{6,4},{5,7},{7,5},{8,10},{10,8},{9,1... | collective-permute-start | bytes 3145736 | tf_op jit(solution)/shard_map/ppermute | solution.py:133
  35.4 2.4 %collective-permute-done.3 = f32[16,128,128]{2,1,0:T(8,128)} collective-permute-done((f32[16,128,128]{2,1,0:T(8,128)S(1)}, f32[16,128,128]{2,1,0:T(8,128)}, u32[]{:S(2)}, u32[]{:S(2)}) %collective-permute-start.3) | collective-permute-done | bytes 1048608 | tf_op jit(solution)/shard_map/ppermute | solution.py:133
  39.0 2.0 %collective-permute-start.4 = (f32[8,128,128]{2,1,0:T(8,128)S(1)}, f32[8,128,128]{2,1,0:T(8,128)S(1)}, u32[]{:S(2)}, u32[]{:S(2)}) collective-permute-start(f32[8,128,128]{2,1,0:T(8,128)S(1)} %dynamic-slice_add_fusion), channel_id=1, source_target_pairs={{0,4},{4,8},{8,12},{12,16},{16,20},{20,24},{24,28},{1,5},{5,9},{9,... | collective-permute-start | bytes 1572872 | tf_op jit(solution)/shard_map/ppermute | solution.py:20
  42.8 11.3 %collective-permute-done.4 = f32[8,128,128]{2,1,0:T(8,128)S(1)} collective-permute-done((f32[8,128,128]{2,1,0:T(8,128)S(1)}, f32[8,128,128]{2,1,0:T(8,128)S(1)}, u32[]{:S(2)}, u32[]{:S(2)}) %collective-permute-start.4) | collective-permute-done | bytes 524320 | tf_op jit(solution)/shard_map/ppermute | solution.py:20
  54.1 3.2 %collective-permute-start.5 = (f32[8,128,128]{2,1,0:T(8,128)S(1)}, f32[8,128,128]{2,1,0:T(8,128)}, u32[]{:S(2)}, u32[]{:S(2)}) collective-permute-start(f32[8,128,128]{2,1,0:T(8,128)S(1)} %add.78), channel_id=1, source_target_pairs={{0,8},{4,12},{8,16},{12,20},{16,24},{20,28},{1,9},{5,13},{9,17},{1... | collective-permute-start | bytes 1572872 | tf_op jit(solution)/shard_map/ppermute | solution.py:20
  61.2 7.1 %collective-permute-done.5 = f32[8,128,128]{2,1,0:T(8,128)} collective-permute-done((f32[8,128,128]{2,1,0:T(8,128)S(1)}, f32[8,128,128]{2,1,0:T(8,128)}, u32[]{:S(2)}, u32[]{:S(2)}) %collective-permute-start.5) | collective-permute-done | bytes 524320 | tf_op jit(solution)/shard_map/ppermute | solution.py:20
  69.5 4.0 %collective-permute-start.6 = (f32[8,128,128]{2,1,0:T(8,128)S(1)}, f32[8,128,128]{2,1,0:T(8,128)}, u32[]{:S(2)}, u32[]{:S(2)}) collective-permute-start(f32[8,128,128]{2,1,0:T(8,128)S(1)} %add.79), channel_id=1, source_target_pairs={{0,16},{4,20},{8,24},{12,28},{1,17},{5,21},{9,25},{13,29},{2,18},{... | collective-permute-start | bytes 1572872 | tf_op jit(solution)/shard_map/ppermute | solution.py:20
  74.9 19.6 %collective-permute-done.6 = f32[8,128,128]{2,1,0:T(8,128)} collective-permute-done((f32[8,128,128]{2,1,0:T(8,128)S(1)}, f32[8,128,128]{2,1,0:T(8,128)}, u32[]{:S(2)}, u32[]{:S(2)}) %collective-permute-start.6) | collective-permute-done | bytes 524320 | tf_op jit(solution)/shard_map/ppermute | solution.py:20
  94.5 3.2 %fusion.1 = f32[256,16,128]{0,2,1:T(8,128)S(1)} fusion(bf16[256,16,128]{0,2,1:T(8,128)(2,1)} %bitcast.52, bf16[256,16,128]{0,2,1:T(8,128)(2,1)} %bitcast.57, pred[256,256]{1,0:T(8,128)(4,1)S(1)} %iota_compare_fusion, bf16[256,2048]{1,0:T(8,128)(2,1)} %copy-done.2), kind=kOutput, calls=%fused_computation.13 | convolution fusion | flops 538968064 | bytes 5308416 | tf_op jit(solution)/shard_map/hts,she->the/dot_general | solution.py:106
  99.1 2.7 %collective-permute-start.11 = (f32[8,128,128]{2,1,0:T(8,128)S(1)}, f32[8,128,128]{2,1,0:T(8,128)}, u32[]{:S(2)}, u32[]{:S(2)}) collective-permute-start(f32[8,128,128]{2,1,0:T(8,128)S(1)} %add_subtract_fusion), channel_id=1, source_target_pairs={{0,2},{2,0},{1,3},{3,1},{4,6},{6,4},{5,7},{7,5},{8,10},{10,8},{9,1... | collective-permute-start | bytes 1572872 | tf_op jit(solution)/shard_map/ppermute | solution.py:141
  103.7 13.3 %collective-permute-done.13.refs_6_ = bf16[256,2048]{1,0:T(8,128)(2,1)} collective-permute-done((bf16[256,2048]{1,0:T(8,128)(2,1)}, bf16[256,2048]{1,0:T(8,128)(2,1)}, u32[]{:S(2)}, u32[]{:S(2)}) %collective-permute-start.13) | collective-permute-done | bytes 1048608 | tf_op jit(solution)/shard_map/ppermute | solution.py:85
  117.1 2.2 %collective-permute-start.14 = (bf16[256,2048]{1,0:T(8,128)(2,1)}, bf16[256,2048]{1,0:T(8,128)(2,1)}, u32[]{:S(2)}, u32[]{:S(2)}) collective-permute-start(bf16[256,2048]{1,0:T(8,128)(2,1)} %collective-permute-done.13.refs_6_), channel_id=1, source_target_pairs={{0,4},{4,12},{12,20},{20,28},{28,24},{24,16},{16,8},{8,0},{1,5},{5... | collective-permute-start | bytes 3145736 | tf_op jit(solution)/shard_map/ppermute | solution.py:85
  120.4 1.8 %multiply_reduce_fusion = (f32[256,16]{0,1:T(8,128)S(1)}, f32[16,128,256]{2,1,0:T(8,128)S(1)}) fusion(f32[256,16,128]{0,2,1:T(8,128)S(1)} %fusion.1, bf16[256,16,128]{0,2,1:T(8,128)(2,1)S(1)} %bitcast.58, f32[8,128,128]{2,1,0:T(8,128)S(1)} %get-tuple-element.32, f32[8,128,128]{2,1,0:T(8,128)S(1)} %get-tuple-element.31, ...), kind=kOutput, calls=%fused_computation.11 | convolution fusion | flops 136835072 | bytes 7356417 | tf_op jit(solution)/shard_map/thd,hde->the/dot_general | solution.py:115
  123.8 16.7 %collective-permute-done.14.refs_10_ = bf16[256,2048]{1,0:T(8,128)(2,1)} collective-permute-done((bf16[256,2048]{1,0:T(8,128)(2,1)}, bf16[256,2048]{1,0:T(8,128)(2,1)}, u32[]{:S(2)}, u32[]{:S(2)}) %collective-permute-start.14) | collective-permute-done | bytes 1048608 | tf_op jit(solution)/shard_map/ppermute | solution.py:85
  141.6 2.3 %collective-permute-start.15 = (bf16[128,2048]{1,0:T(8,128)(2,1)S(1)}, bf16[128,2048]{1,0:T(8,128)(2,1)S(1)}, u32[]{:S(2)}, u32[]{:S(2)}) collective-permute-start(bf16[128,2048]{1,0:T(8,128)(2,1)S(1)} %slice.36), channel_id=1, source_target_pairs={{0,4},{4,12},{12,20},{20,28},{28,24},{24,16},{16,8},{8,0},{1,5},{5... | collective-permute-start | bytes 1572872 | tf_op jit(solution)/shard_map/ppermute | solution.py:82
  143.9 1.9 %slice.37 = bf16[128,2048]{1,0:T(8,128)(2,1)} slice(bf16[256,2048]{1,0:T(8,128)(2,1)} %collective-permute-done.17.refs_12_), slice={[128:256], [0:2048]} | slice | bytes 1048576 | tf_op jit(solution)/shard_map/slice | solution.py:83
  147.1 2.7 %collective-permute-start.20 = (bf16[256,2048]{1,0:T(8,128)(2,1)}, bf16[256,2048]{1,0:T(8,128)(2,1)}, u32[]{:S(2)}, u32[]{:S(2)}) collective-permute-start(bf16[256,2048]{1,0:T(8,128)(2,1)} %collective-permute-done.13.refs_6_), channel_id=1, source_target_pairs={{0,2},{2,0},{1,3},{3,1},{4,6},{6,4},{5,7},{7,5},{8,10},{10,8},{9,1... | collective-permute-start | bytes 3145736 | tf_op jit(solution)/shard_map/ppermute | solution.py:273
  149.8 2.9 %collective-permute-done.15 = bf16[128,2048]{1,0:T(8,128)(2,1)S(1)} collective-permute-done((bf16[128,2048]{1,0:T(8,128)(2,1)S(1)}, bf16[128,2048]{1,0:T(8,128)(2,1)S(1)}, u32[]{:S(2)}, u32[]{:S(2)}) %collective-permute-start.15) | collective-permute-done | bytes 524320 | tf_op jit(solution)/shard_map/ppermute | solution.py:82
  153.5 3.3 %collective-permute-start.22 = (bf16[256,2048]{1,0:T(8,128)(2,1)}, bf16[256,2048]{1,0:T(8,128)(2,1)}, u32[]{:S(2)}, u32[]{:S(2)}) collective-permute-start(bf16[256,2048]{1,0:T(8,128)(2,1)} %collective-permute-done.14.refs_10_), channel_id=1, source_target_pairs={{0,2},{2,0},{1,3},{3,1},{4,6},{6,4},{5,7},{7,5},{8,10},{10,8},{9,1... | collective-permute-start | bytes 3145736 | tf_op jit(solution)/shard_map/ppermute | solution.py:273
  157.9 2.6 %collective-permute-start.23 = (bf16[256,2048]{1,0:T(8,128)(2,1)}, bf16[256,2048]{1,0:T(8,128)(2,1)}, u32[]{:S(2)}, u32[]{:S(2)}) collective-permute-start(bf16[256,2048]{1,0:T(8,128)(2,1)} %collective-permute-done.17.refs_12_), channel_id=1, source_target_pairs={{0,2},{2,0},{1,3},{3,1},{4,6},{6,4},{5,7},{7,5},{8,10},{10,8},{9,1... | collective-permute-start | bytes 3145736 | tf_op jit(solution)/shard_map/ppermute | solution.py:273
  164.1 9.2 %shard_map.82.refs_2_ = f32[256,2048]{1,0:T(8,128)} custom-call(s32[14]{0:T(128)} %slice.31.starts_ref, bf16[256,4096]{1,0:T(8,128)(2,1)} %pad_maximum_fusion.normed_ref, bf16[256,2048]{1,0:T(8,128)(2,1)} %refs_0_.1, bf16[256,2048]{1,0:T(8,128)(2,1)} %collective-permute-done.8.refs_1_, bf16[256,2048]{1,0:T(8,128)(2,1)} %collective-permute-done.refs_2_, ...), custom_call_target="tpu_custom_call" | custom-call | tf_op jit(solution)/shard_map/pallas_call | solution.py:196
  173.3 5.0 %shard_map.83 = bf16[256,2048]{1,0:T(8,128)(2,1)} custom-call(s32[2]{0:T(128)} %slice_bitcast_fusion.starts_ref, bf16[256,4096]{1,0:T(8,128)(2,1)} %pad_maximum_fusion.normed_ref, bf16[256,2048]{1,0:T(8,128)(2,1)} %copy-done.5, bf16[256,2048]{1,0:T(8,128)(2,1)} %collective-permute-done.19.refs_1_, f32[256,2048]{1,0:T(8,128)} %shard_map.82.refs_2_), custom_call_target="tpu_custom_call" | custom-call | tf_op jit(solution)/shard_map/pallas_call | solution.py:196
  (92 shorter events, 32.8 us)
Async XLA Ops:
  5.9 24.3 %collective-permute-start.2 = (bf16[2,128,2048]{2,1,0:T(8,128)(2,1)}, bf16[2,128,2048]{2,1,0:T(8,128)(2,1)S(1)}, u32[]{:S(2)}, u32[]{:S(2)}) collective-permute-start(bf16[2,128,2048]{2,1,0:T(8,128)(2,1)} %bitcast.7), channel_id=1, source_target_pairs={{0,1},{1,0},{2,3},{3,2},{4,5},{5,4},{6,7},{7,6},{8,9},{9,8},{10,11... | collective-permute-start | bytes 3145736 | tf_op jit(solution)/shard_map/ppermute | solution.py:38
  7.1 24.0 %collective-permute-start = (bf16[256,2048]{1,0:T(8,128)(2,1)}, bf16[256,2048]{1,0:T(8,128)(2,1)}, u32[]{:S(2)}, u32[]{:S(2)}) collective-permute-start(bf16[256,2048]{1,0:T(8,128)(2,1)} %refs_0_.1), channel_id=1, source_target_pairs={{0,4},{4,12},{12,20},{20,28},{28,24},{24,16},{16,8},{8,0},{1,5},{5... | collective-permute-start | bytes 3145736 | tf_op jit(solution)/shard_map/ppermute | solution.py:85
  8.4 23.7 %collective-permute-start.1 = (bf16[256,2048]{1,0:T(8,128)(2,1)}, bf16[256,2048]{1,0:T(8,128)(2,1)}, u32[]{:S(2)}, u32[]{:S(2)}) collective-permute-start(bf16[256,2048]{1,0:T(8,128)(2,1)} %refs_0_.1), channel_id=1, source_target_pairs={{4,0},{12,4},{20,12},{28,20},{24,28},{16,24},{8,16},{0,8},{5,1},{1... | collective-permute-start | bytes 3145736 | tf_op jit(solution)/shard_map/ppermute | solution.py:85
  33.1 4.6 %collective-permute-start.3 = (f32[16,128,128]{2,1,0:T(8,128)S(1)}, f32[16,128,128]{2,1,0:T(8,128)}, u32[]{:S(2)}, u32[]{:S(2)}) collective-permute-start(f32[16,128,128]{2,1,0:T(8,128)S(1)} %fusion.6), channel_id=1, source_target_pairs={{0,2},{2,0},{1,3},{3,1},{4,6},{6,4},{5,7},{7,5},{8,10},{10,8},{9,1... | collective-permute-start | bytes 3145736 | tf_op jit(solution)/shard_map/ppermute | solution.py:133
  39.0 15.0 %collective-permute-start.4 = (f32[8,128,128]{2,1,0:T(8,128)S(1)}, f32[8,128,128]{2,1,0:T(8,128)S(1)}, u32[]{:S(2)}, u32[]{:S(2)}) collective-permute-start(f32[8,128,128]{2,1,0:T(8,128)S(1)} %dynamic-slice_add_fusion), channel_id=1, source_target_pairs={{0,4},{4,8},{8,12},{12,16},{16,20},{20,24},{24,28},{1,5},{5,9},{9,... | collective-permute-start | bytes 1572872 | tf_op jit(solution)/shard_map/ppermute | solution.py:20
  54.1 14.2 %collective-permute-start.5 = (f32[8,128,128]{2,1,0:T(8,128)S(1)}, f32[8,128,128]{2,1,0:T(8,128)}, u32[]{:S(2)}, u32[]{:S(2)}) collective-permute-start(f32[8,128,128]{2,1,0:T(8,128)S(1)} %add.78), channel_id=1, source_target_pairs={{0,8},{4,12},{8,16},{12,20},{16,24},{20,28},{1,9},{5,13},{9,17},{1... | collective-permute-start | bytes 1572872 | tf_op jit(solution)/shard_map/ppermute | solution.py:20
  58.4 15.1 %collective-permute-start.7 = (bf16[1,128,2048]{2,1,0:T(8,128)(2,1)}, bf16[1,128,2048]{2,1,0:T(8,128)(2,1)S(1)}, u32[]{:S(2)}, u32[]{:S(2)}) collective-permute-start(bf16[1,128,2048]{2,1,0:T(8,128)(2,1)} %bitcast.12), channel_id=1, source_target_pairs={{0,1},{1,0},{2,3},{3,2},{4,5},{5,4},{6,7},{7,6},{8,9},{9,8},{10,11... | collective-permute-start | bytes 1572872 | tf_op jit(solution)/shard_map/ppermute | solution.py:38
  58.6 40.5 %collective-permute-start.8 = (bf16[256,2048]{1,0:T(8,128)(2,1)}, bf16[256,2048]{1,0:T(8,128)(2,1)}, u32[]{:S(2)}, u32[]{:S(2)}) collective-permute-start(bf16[256,2048]{1,0:T(8,128)(2,1)} %refs_0_.1), channel_id=1, source_target_pairs={{0,2},{2,0},{1,3},{3,1},{4,6},{6,4},{5,7},{7,5},{8,10},{10,8},{9,1... | collective-permute-start | bytes 3145736 | tf_op jit(solution)/shard_map/ppermute | solution.py:254
  60.6 38.5 %collective-permute-start.10 = (bf16[256,2048]{1,0:T(8,128)(2,1)}, bf16[256,2048]{1,0:T(8,128)(2,1)}, u32[]{:S(2)}, u32[]{:S(2)}) collective-permute-start(bf16[256,2048]{1,0:T(8,128)(2,1)} %collective-permute-done.1.refs_4_), channel_id=1, source_target_pairs={{0,2},{2,0},{1,3},{3,1},{4,6},{6,4},{5,7},{7,5},{8,10},{10,8},{9,1... | collective-permute-start | bytes 3145736 | tf_op jit(solution)/shard_map/ppermute | solution.py:254
  60.7 38.4 %collective-permute-start.9 = (bf16[256,2048]{1,0:T(8,128)(2,1)}, bf16[256,2048]{1,0:T(8,128)(2,1)}, u32[]{:S(2)}, u32[]{:S(2)}) collective-permute-start(bf16[256,2048]{1,0:T(8,128)(2,1)} %collective-permute-done.refs_2_), channel_id=1, source_target_pairs={{0,2},{2,0},{1,3},{3,1},{4,6},{6,4},{5,7},{7,5},{8,10},{10,8},{9,1... | collective-permute-start | bytes 3145736 | tf_op jit(solution)/shard_map/ppermute | solution.py:254
  69.5 25.0 %collective-permute-start.6 = (f32[8,128,128]{2,1,0:T(8,128)S(1)}, f32[8,128,128]{2,1,0:T(8,128)}, u32[]{:S(2)}, u32[]{:S(2)}) collective-permute-start(f32[8,128,128]{2,1,0:T(8,128)S(1)} %add.79), channel_id=1, source_target_pairs={{0,16},{4,20},{8,24},{12,28},{1,17},{5,21},{9,25},{13,29},{2,18},{... | collective-permute-start | bytes 1572872 | tf_op jit(solution)/shard_map/ppermute | solution.py:20
  74.9 42.2 %collective-permute-start.13 = (bf16[256,2048]{1,0:T(8,128)(2,1)}, bf16[256,2048]{1,0:T(8,128)(2,1)}, u32[]{:S(2)}, u32[]{:S(2)}) collective-permute-start(bf16[256,2048]{1,0:T(8,128)(2,1)} %collective-permute-done.refs_2_), channel_id=1, source_target_pairs={{0,4},{4,12},{12,20},{20,28},{28,24},{24,16},{16,8},{8,0},{1,5},{5... | collective-permute-start | bytes 3145736 | tf_op jit(solution)/shard_map/ppermute | solution.py:85
  94.5 24.8 %collective-permute-start.16 = (bf16[256,2048]{1,0:T(8,128)(2,1)}, bf16[256,2048]{1,0:T(8,128)(2,1)}, u32[]{:S(2)}, u32[]{:S(2)}) collective-permute-start(bf16[256,2048]{1,0:T(8,128)(2,1)} %collective-permute-done.1.refs_4_), channel_id=1, source_target_pairs={{4,0},{12,4},{20,12},{28,20},{24,28},{16,24},{8,16},{0,8},{5,1},{1... | collective-permute-start | bytes 3145736 | tf_op jit(solution)/shard_map/ppermute | solution.py:85
  99.1 20.2 %collective-permute-start.11 = (f32[8,128,128]{2,1,0:T(8,128)S(1)}, f32[8,128,128]{2,1,0:T(8,128)}, u32[]{:S(2)}, u32[]{:S(2)}) collective-permute-start(f32[8,128,128]{2,1,0:T(8,128)S(1)} %add_subtract_fusion), channel_id=1, source_target_pairs={{0,2},{2,0},{1,3},{3,1},{4,6},{6,4},{5,7},{7,5},{8,10},{10,8},{9,1... | collective-permute-start | bytes 1572872 | tf_op jit(solution)/shard_map/ppermute | solution.py:141
  117.1 23.4 %collective-permute-start.14 = (bf16[256,2048]{1,0:T(8,128)(2,1)}, bf16[256,2048]{1,0:T(8,128)(2,1)}, u32[]{:S(2)}, u32[]{:S(2)}) collective-permute-start(bf16[256,2048]{1,0:T(8,128)(2,1)} %collective-permute-done.13.refs_6_), channel_id=1, source_target_pairs={{0,4},{4,12},{12,20},{20,28},{28,24},{24,16},{16,8},{8,0},{1,5},{5... | collective-permute-start | bytes 3145736 | tf_op jit(solution)/shard_map/ppermute | solution.py:85
  119.3 24.7 %collective-permute-start.17 = (bf16[256,2048]{1,0:T(8,128)(2,1)}, bf16[256,2048]{1,0:T(8,128)(2,1)}, u32[]{:S(2)}, u32[]{:S(2)}) collective-permute-start(bf16[256,2048]{1,0:T(8,128)(2,1)} %collective-permute-done.16.refs_8_), channel_id=1, source_target_pairs={{4,0},{12,4},{20,12},{28,20},{24,28},{16,24},{8,16},{0,8},{5,1},{1... | collective-permute-start | bytes 3145736 | tf_op jit(solution)/shard_map/ppermute | solution.py:85
  123.5 38.1 %collective-permute-start.12 = (bf16[256,2048]{1,0:T(8,128)(2,1)S(1)}, bf16[256,2048]{1,0:T(8,128)(2,1)S(1)}, u32[]{:S(2)}, u32[]{:S(2)}) collective-permute-start(bf16[256,2048]{1,0:T(8,128)(2,1)S(1)} %copy.38), channel_id=1, source_target_pairs={{0,1},{1,0},{2,3},{3,2},{4,5},{5,4},{6,7},{7,6},{8,9},{9,8},{10,11... | collective-permute-start | bytes 3145736 | tf_op jit(solution)/shard_map/ppermute | solution.py:127
  141.6 11.1 %collective-permute-start.15 = (bf16[128,2048]{1,0:T(8,128)(2,1)S(1)}, bf16[128,2048]{1,0:T(8,128)(2,1)S(1)}, u32[]{:S(2)}, u32[]{:S(2)}) collective-permute-start(bf16[128,2048]{1,0:T(8,128)(2,1)S(1)} %slice.36), channel_id=1, source_target_pairs={{0,4},{4,12},{12,20},{20,28},{28,24},{24,16},{16,8},{8,0},{1,5},{5... | collective-permute-start | bytes 1572872 | tf_op jit(solution)/shard_map/ppermute | solution.py:82
  145.8 12.1 %collective-permute-start.18 = (bf16[128,2048]{1,0:T(8,128)(2,1)}, bf16[128,2048]{1,0:T(8,128)(2,1)}, u32[]{:S(2)}, u32[]{:S(2)}) collective-permute-start(bf16[128,2048]{1,0:T(8,128)(2,1)} %slice.37), channel_id=1, source_target_pairs={{4,0},{12,4},{20,12},{28,20},{24,28},{16,24},{8,16},{0,8},{5,1},{1... | collective-permute-start | bytes 1572872 | tf_op jit(solution)/shard_map/ppermute | solution.py:82
  147.1 17.0 %collective-permute-start.20 = (bf16[256,2048]{1,0:T(8,128)(2,1)}, bf16[256,2048]{1,0:T(8,128)(2,1)}, u32[]{:S(2)}, u32[]{:S(2)}) collective-permute-start(bf16[256,2048]{1,0:T(8,128)(2,1)} %collective-permute-done.13.refs_6_), channel_id=1, source_target_pairs={{0,2},{2,0},{1,3},{3,1},{4,6},{6,4},{5,7},{7,5},{8,10},{10,8},{9,1... | collective-permute-start | bytes 3145736 | tf_op jit(solution)/shard_map/ppermute | solution.py:273
  149.8 14.3 %collective-permute-start.21 = (bf16[256,2048]{1,0:T(8,128)(2,1)}, bf16[256,2048]{1,0:T(8,128)(2,1)}, u32[]{:S(2)}, u32[]{:S(2)}) collective-permute-start(bf16[256,2048]{1,0:T(8,128)(2,1)} %collective-permute-done.16.refs_8_), channel_id=1, source_target_pairs={{0,2},{2,0},{1,3},{3,1},{4,6},{6,4},{5,7},{7,5},{8,10},{10,8},{9,1... | collective-permute-start | bytes 3145736 | tf_op jit(solution)/shard_map/ppermute | solution.py:273
  153.5 10.6 %collective-permute-start.22 = (bf16[256,2048]{1,0:T(8,128)(2,1)}, bf16[256,2048]{1,0:T(8,128)(2,1)}, u32[]{:S(2)}, u32[]{:S(2)}) collective-permute-start(bf16[256,2048]{1,0:T(8,128)(2,1)} %collective-permute-done.14.refs_10_), channel_id=1, source_target_pairs={{0,2},{2,0},{1,3},{3,1},{4,6},{6,4},{5,7},{7,5},{8,10},{10,8},{9,1... | collective-permute-start | bytes 3145736 | tf_op jit(solution)/shard_map/ppermute | solution.py:273
  157.9 6.2 %collective-permute-start.23 = (bf16[256,2048]{1,0:T(8,128)(2,1)}, bf16[256,2048]{1,0:T(8,128)(2,1)}, u32[]{:S(2)}, u32[]{:S(2)}) collective-permute-start(bf16[256,2048]{1,0:T(8,128)(2,1)} %collective-permute-done.17.refs_12_), channel_id=1, source_target_pairs={{0,2},{2,0},{1,3},{3,1},{4,6},{6,4},{5,7},{7,5},{8,10},{10,8},{9,1... | collective-permute-start | bytes 3145736 | tf_op jit(solution)/shard_map/ppermute | solution.py:273
  161.6 11.8 %collective-permute-start.19 = (bf16[256,2048]{1,0:T(8,128)(2,1)S(1)}, bf16[256,2048]{1,0:T(8,128)(2,1)}, u32[]{:S(2)}, u32[]{:S(2)}) collective-permute-start(bf16[256,2048]{1,0:T(8,128)(2,1)S(1)} %constant_dynamic-update-slice_fusion.refs_0_), channel_id=1, source_target_pairs={{0,2},{2,0},{1,3},{3,1},{4,6},{6,4},{5,7},{7,5},{8,10},{10,8},{9,1... | collective-permute-start | bytes 3145736 | tf_op jit(solution)/shard_map/ppermute | solution.py:273
  (12 other events, 51.5 us)

commit v13 on v11

--- a/solution.py
+++ b/solution.py
@@ -250,12 +250,26 @@
         "thd,the->hde", key_heads, value_heads, preferred_element_type=jnp.float32
     )
     partner_state, chip_half = chip_scan(kv_state, core, n_chip)
-    chip_prefix_half = exclusive_prefix(chip_half, "chip", n_chip)
     query_heads = split_heads(query_block, heads_dev)
     within_block = within_block_part(query_heads, key_heads, value_heads)
-    swapped += [lax.ppermute(w, "core", SWAP) for w in got[len(swapped):]]
-    chip_prefix_half, within_block, swapped = barrier((chip_prefix_half, within_block, swapped))
-    for step in range(2, n_steps + 1):
+    total = chip_half
+    shift, step = 1, 2
+    while shift < n_chip:
+        pairs = [(i, i + shift) for i in range(n_chip - shift)]
+        total = total + lax.ppermute(total, "chip", pairs)
+        if step <= n_steps:
+            ahead, behind = ring_step(ahead, behind, order, last=step == n_steps)
+            fresh = [jnp.concatenate([ahead, behind], 0)] if step == n_steps else [ahead, behind]
+            ahead, behind, total, swapped = barrier((ahead, behind, total, swapped))
+            if step < n_steps:
+                fresh = [ahead, behind]
+            got += fresh
+            offsets += [step] if step == n_steps else [step, -step]
+            swapped = swapped + [lax.ppermute(w, "core", SWAP) for w in fresh]
+            step += 1
+        shift *= 2
+    chip_prefix_half = total - chip_half
+    while step <= n_steps:
         ahead, behind = ring_step(ahead, behind, order, last=step == n_steps)
         if step == n_steps:
             got.append(jnp.concatenate([ahead, behind], 0))
@@ -263,6 +277,7 @@
         else:
             got += [ahead, behind]
             offsets += [step, -step]
+        step += 1
     swapped += [lax.ppermute(w, "core", SWAP) for w in got[len(swapped):]]
     prefix = chip_finish(chip_prefix_half, partner_state, core)
     normed = normalize(query_heads, prefix, within_block, norm_gain)

time: 175 us -> 208 us (1.19)
  waiting for transfers between devices: 96.2 us -> 123 us
  other arithmetic: 8.14 us -> 11.7 us
  local copies, waits for them, and re-layouts: 20.8 us -> 24.2 us
  starting transfers between devices: 32 us -> 29 us
    ppermute x1, waiting for transfers between devices: 0.01 us -> 20.2 us  [gather_head(): other = lax.ppermute(normed, 'head', SWAP)]
    ppermute x8, waiting for transfers between devices: 38.9 us -> 56.5 us  [the longest x3 56.5 us: local_ring(): total = total + lax.ppermute(total, 'chip', pairs)]
    ppermute x3, waiting for transfers between devices: 29.2 us -> 20.7 us  [ring_step(): lax.ppermute(ahead, 'chip', forward)]
    dynamic_slice x3, local copies, waits for them, and re-layouts: 0.81 us -> 4.85 us  [head_blocks(): own = lax.dynamic_index_in_dim(stacked, place, 2, False)]
    ppermute x1, waiting for transfers between devices: 3.52 us -> 0.01 us  [ring_step(): lax.ppermute(ahead[:half_rows], 'chip', forward)]
    select_n x3, other arithmetic: 0.29 us -> 2.8 us  [pair_order(): first = jnp.where(place == 0, own, other)]
    ppermute x8, starting transfers between devices: 17 us -> 14.7 us  [the longest x3 10.3 us: local_ring(): total = total + lax.ppermute(total, 'chip', pairs)]
    add x2 -> x3, other arithmetic: 0.11 us -> 2.43 us  [local_ring(): total = total + lax.ppermute(total, 'chip', pairs)]
  transfers between devices with their start and end apart: 24 -> 24, of which waited for: 11 -> 10; matrix products, arithmetic and copies ran while one was open for 14% -> 14% of each run, Pallas kernels for 0% -> 0%
where the time goes in v13:
time: 208 us; the launch traced here: 205 us
  waiting for transfers between devices  123 us (59%)
  starting transfers between devices  29 us (14%)
  local copies, waits for them, and re-layouts  24.2 us (12%)
  other arithmetic  11.7 us (6%)
  Pallas kernels  9.62 us (5%)
  matrix products  6.94 us (3%)
    ppermute x3, waiting for transfers between devices, local_ring(): total = total + lax.ppermute(total, 'chip', pairs)  56.5 us
    ppermute x2, waiting for transfers between devices, head_blocks(): other = lax.ppermute(sent, 'head', SWAP)  22.1 us
    ppermute x3, waiting for transfers between devices, ring_step(): lax.ppermute(ahead, 'chip', forward)  20.7 us
    ppermute x1, waiting for transfers between devices, gather_head(): other = lax.ppermute(normed, 'head', SWAP)  20.2 us
    ppermute x3, starting transfers between devices, local_ring(): total = total + lax.ppermute(total, 'chip', pairs)  10.3 us
    pallas_call x1, Pallas kernels, project_blocks(): pl.pallas_call(kernel, out_shape=jax.ShapeDtypeStruct((tokens, cols), jnp...  9.62 us
    unnamed x28, local copies, waits for them, and re-layouts  5.89 us
    dynamic_slice x3, local copies, waits for them, and re-layouts, head_blocks(): own = lax.dynamic_index_in_dim(stacked, place, 2, False)  4.85 us
  transfers between devices with their start and end apart: 24, of which 10 were waited for; matrix products, arithmetic and copies ran while one was open for 14% of the time, Pallas kernels for 0%

profile of v13, /device:TPU:13, one launch (start us, length us, event | category | flops | bytes accessed | tf_op | source)
XLA Modules:
  0.0 204.9 jit_solution(14057436131909833793)
XLA Ops:
  0.0 1.7 copy.19
  3.6 2.3 %copy.22 = bf16[2,128,1,2048]{3,1,0,2:T(8,128)(2,1)} copy(bf16[2,128,1,2048]{1,3,2,0:T(8,128)(2,1)} %get-tuple-element.64) | data formatting | bytes 2097152 | tf_op jit(solution)/shard_map/jit(dynamic_index_in_dim)/dynamic_slice | solution.py:37
  9.1 21.1 %collective-permute-done.2 = bf16[2,128,2048]{2,1,0:T(8,128)(2,1)S(1)} collective-permute-done((bf16[2,128,2048]{2,1,0:T(8,128)(2,1)}, bf16[2,128,2048]{2,1,0:T(8,128)(2,1)S(1)}, u32[]{:S(2)}, u32[]{:S(2)}) %collective-permute-start.2) | collective-permute-done | bytes 1048608 | tf_op jit(solution)/shard_map/ppermute | solution.py:38
  33.1 2.2 %collective-permute-start.5 = (f32[16,128,128]{2,1,0:T(8,128)S(1)}, f32[16,128,128]{2,1,0:T(8,128)}, u32[]{:S(2)}, u32[]{:S(2)}) collective-permute-start(f32[16,128,128]{2,1,0:T(8,128)S(1)} %fusion.8), channel_id=1, source_target_pairs={{0,2},{2,0},{1,3},{3,1},{4,6},{6,4},{5,7},{7,5},{8,10},{10,8},{9,1... | collective-permute-start | bytes 3145736 | tf_op jit(solution)/shard_map/ppermute | solution.py:133
  35.3 2.4 %collective-permute-done.5 = f32[16,128,128]{2,1,0:T(8,128)} collective-permute-done((f32[16,128,128]{2,1,0:T(8,128)S(1)}, f32[16,128,128]{2,1,0:T(8,128)}, u32[]{:S(2)}, u32[]{:S(2)}) %collective-permute-start.5) | collective-permute-done | bytes 1048608 | tf_op jit(solution)/shard_map/ppermute | solution.py:133
  39.0 2.0 collective-permute-start.6
  43.6 10.6 %collective-permute-done.6 = f32[8,128,128]{2,1,0:T(8,128)S(1)} collective-permute-done((f32[8,128,128]{2,1,0:T(8,128)S(1)}, f32[8,128,128]{2,1,0:T(8,128)S(1)}, u32[]{:S(2)}, u32[]{:S(2)}) %collective-permute-start.6) | collective-permute-done | bytes 524320 | tf_op jit(solution)/shard_map/ppermute | solution.py:259
  55.4 20.1 %collective-permute-done.3.refs_6_ = bf16[256,2048]{1,0:T(8,128)(2,1)} collective-permute-done((bf16[256,2048]{1,0:T(8,128)(2,1)}, bf16[256,2048]{1,0:T(8,128)(2,1)}, u32[]{:S(2)}, u32[]{:S(2)}) %collective-permute-start.3) | collective-permute-done | bytes 1048608 | tf_op jit(solution)/shard_map/ppermute | solution.py:85
  77.0 1.8 collective-permute-start.13
  78.8 3.2 %collective-permute-start.12 = (f32[8,128,128]{2,1,0:T(8,128)S(1)}, f32[8,128,128]{2,1,0:T(8,128)}, u32[]{:S(2)}, u32[]{:S(2)}) collective-permute-start(f32[8,128,128]{2,1,0:T(8,128)S(1)} %add.83), channel_id=1, source_target_pairs={{0,8},{4,12},{8,16},{12,20},{16,24},{20,28},{1,9},{5,13},{9,17},{1... | collective-permute-start | bytes 1572872 | tf_op jit(solution)/shard_map/ppermute | solution.py:259
  82.0 2.3 %copy.25 = bf16[128,4096]{0,1:T(8,128)(2,1)} copy(bf16[128,4096]{1,0:T(8,128)(2,1)} %param.8) | data formatting | bytes 2097152 | tf_op args[0]
  84.3 2.3 %constant_dynamic-slice_fusion.1 = (bf16[1,128,1,2048]{1,3,2,0:T(8,128)(2,1)}, bf16[1,128,1,2048]{1,3,2,0:T(8,128)(2,1)}) fusion(bf16[1,128,2,2048]{1,3,2,0:T(8,128)(2,1)} %bitcast.54, s32[]{:T(128)S(6)} %select_n.92, s32[]{:T(128)S(6)} %select_n.93), kind=kLoop, calls=%fused_computation.51 | loop fusion | bytes 2097160 | tf_op jit(solution)/shard_map/jit(dynamic_index_in_dim)/dynamic_slice | solution.py:36
  86.5 2.0 copy.27
  88.6 21.9 %collective-permute-done.12 = f32[8,128,128]{2,1,0:T(8,128)} collective-permute-done((f32[8,128,128]{2,1,0:T(8,128)S(1)}, f32[8,128,128]{2,1,0:T(8,128)}, u32[]{:S(2)}, u32[]{:S(2)}) %collective-permute-start.12) | collective-permute-done | bytes 524320 | tf_op jit(solution)/shard_map/ppermute | solution.py:259
  112.1 2.4 %collective-permute-start.18 = (bf16[256,2048]{1,0:T(8,128)(2,1)}, bf16[256,2048]{1,0:T(8,128)(2,1)}, u32[]{:S(2)}, u32[]{:S(2)}) collective-permute-start(bf16[256,2048]{1,0:T(8,128)(2,1)} %collective-permute-done.10.refs_10_), channel_id=1, source_target_pairs={{0,2},{2,0},{1,3},{3,1},{4,6},{6,4},{5,7},{7,5},{8,10},{10,8},{9,1... | collective-permute-start | bytes 3145736 | tf_op jit(solution)/shard_map/ppermute | solution.py:268
  115.9 1.9 slice.14
  117.8 1.9 slice.15
  122.1 5.1 %collective-permute-start.17 = (f32[8,128,128]{2,1,0:T(8,128)S(1)}, f32[8,128,128]{2,1,0:T(8,128)}, u32[]{:S(2)}, u32[]{:S(2)}) collective-permute-start(f32[8,128,128]{2,1,0:T(8,128)S(1)} %add.84), channel_id=1, source_target_pairs={{0,16},{4,20},{8,24},{12,28},{1,17},{5,21},{9,25},{13,29},{2,18},{... | collective-permute-start | bytes 1572872 | tf_op jit(solution)/shard_map/ppermute | solution.py:259
  127.3 2.0 copy.26
  130.6 24.0 %collective-permute-done.17 = f32[8,128,128]{2,1,0:T(8,128)} collective-permute-done((f32[8,128,128]{2,1,0:T(8,128)S(1)}, f32[8,128,128]{2,1,0:T(8,128)}, u32[]{:S(2)}, u32[]{:S(2)}) %collective-permute-start.17) | collective-permute-done | bytes 524320 | tf_op jit(solution)/shard_map/ppermute | solution.py:259
  159.2 4.0 %fusion.3 = f32[16,128,256]{2,1,0:T(8,128)} fusion(bf16[256,16,128]{0,2,1:T(8,128)(2,1)S(1)} %bitcast.50, bf16[256,16,128]{0,2,1:T(8,128)(2,1)} %bitcast.55, pred[256,256]{1,0:T(8,128)(4,1)S(1)} %iota_compare_fusion, bf16[256,2048]{1,0:T(8,128)(2,1)S(1)} %get-tuple-element.33), kind=kOutput, calls=%fused_computation.14 | convolution fusion | flops 538968064 | bytes 5308416 | tf_op jit(solution)/shard_map/hts,she->the/dot_general | solution.py:106
  164.7 2.5 %fusion = (f32[256,16]{0,1:T(8,128)S(1)}, f32[16,128,256]{2,1,0:T(8,128)S(1)}) fusion(f32[16,128,256]{2,1,0:T(8,128)} %fusion.3, bf16[256,16,128]{0,2,1:T(8,128)(2,1)S(1)} %bitcast.56, f32[8,128,128]{2,1,0:T(8,128)S(1)} %get-tuple-element.66, f32[8,128,128]{2,1,0:T(8,128)S(1)} %get-tuple-element.65, f32[16,128,128]{2,1,0:T(8,128)} %collective-permute-done.5, ...), kind=kOutput, calls=%fused_computation.11 | convolution fusion | flops 136835072 | bytes 7356417 | tf_op jit(solution)/shard_map/thd,hde->the/dot_general | solution.py:115
  173.2 20.2 %collective-permute-done.22 = bf16[256,2048]{1,0:T(8,128)(2,1)S(1)} collective-permute-done((bf16[256,2048]{1,0:T(8,128)(2,1)S(1)}, bf16[256,2048]{1,0:T(8,128)(2,1)S(1)}, u32[]{:S(2)}, u32[]{:S(2)}) %collective-permute-start.22) | collective-permute-done | bytes 1048608 | tf_op jit(solution)/shard_map/ppermute | solution.py:127
  195.1 9.6 %shard_map.82 = bf16[256,2048]{1,0:T(8,128)(2,1)} custom-call(s32[16]{0:T(128)} %mul.41.starts_ref, bf16[256,4096]{1,0:T(8,128)(2,1)} %pad_maximum_fusion.normed_ref, bf16[256,2048]{1,0:T(8,128)(2,1)} %refs_0_.1, bf16[256,2048]{1,0:T(8,128)(2,1)} %copy-done.5, bf16[256,2048]{1,0:T(8,128)(2,1)} %collective-permute-done.refs_2_, bf16[256,2048]{1,0:T(8,128)(2,1)} %copy-done.6, ...), custom_call_target="tpu_custom_call" | custom-call | tf_op jit(solution)/shard_map/pallas_call | solution.py:192
  (91 shorter events, 34.9 us)
Async XLA Ops:
  5.9 24.3 %collective-permute-start.2 = (bf16[2,128,2048]{2,1,0:T(8,128)(2,1)}, bf16[2,128,2048]{2,1,0:T(8,128)(2,1)S(1)}, u32[]{:S(2)}, u32[]{:S(2)}) collective-permute-start(bf16[2,128,2048]{2,1,0:T(8,128)(2,1)} %bitcast.6), channel_id=1, source_target_pairs={{0,1},{1,0},{2,3},{3,2},{4,5},{5,4},{6,7},{7,6},{8,9},{9,8},{10,11... | collective-permute-start | bytes 3145736 | tf_op jit(solution)/shard_map/ppermute | solution.py:38
  7.1 24.0 %collective-permute-start = (bf16[256,2048]{1,0:T(8,128)(2,1)}, bf16[256,2048]{1,0:T(8,128)(2,1)}, u32[]{:S(2)}, u32[]{:S(2)}) collective-permute-start(bf16[256,2048]{1,0:T(8,128)(2,1)} %refs_0_.1), channel_id=1, source_target_pairs={{0,4},{4,12},{12,20},{20,28},{28,24},{24,16},{16,8},{8,0},{1,5},{5... | collective-permute-start | bytes 3145736 | tf_op jit(solution)/shard_map/ppermute | solution.py:85
  8.4 23.7 %collective-permute-start.1 = (bf16[256,2048]{1,0:T(8,128)(2,1)}, bf16[256,2048]{1,0:T(8,128)(2,1)}, u32[]{:S(2)}, u32[]{:S(2)}) collective-permute-start(bf16[256,2048]{1,0:T(8,128)(2,1)} %refs_0_.1), channel_id=1, source_target_pairs={{4,0},{12,4},{20,12},{28,20},{24,28},{16,24},{8,16},{0,8},{5,1},{1... | collective-permute-start | bytes 3145736 | tf_op jit(solution)/shard_map/ppermute | solution.py:85
  33.1 4.6 %collective-permute-start.5 = (f32[16,128,128]{2,1,0:T(8,128)S(1)}, f32[16,128,128]{2,1,0:T(8,128)}, u32[]{:S(2)}, u32[]{:S(2)}) collective-permute-start(f32[16,128,128]{2,1,0:T(8,128)S(1)} %fusion.8), channel_id=1, source_target_pairs={{0,2},{2,0},{1,3},{3,1},{4,6},{6,4},{5,7},{7,5},{8,10},{10,8},{9,1... | collective-permute-start | bytes 3145736 | tf_op jit(solution)/shard_map/ppermute | solution.py:133
  39.0 15.1 %collective-permute-start.6 = (f32[8,128,128]{2,1,0:T(8,128)S(1)}, f32[8,128,128]{2,1,0:T(8,128)S(1)}, u32[]{:S(2)}, u32[]{:S(2)}) collective-permute-start(f32[8,128,128]{2,1,0:T(8,128)S(1)} %dynamic-slice_add_fusion), channel_id=1, source_target_pairs={{0,4},{4,8},{8,12},{12,16},{16,20},{20,24},{24,28},{1,5},{5,9},{9,... | collective-permute-start | bytes 1572872 | tf_op jit(solution)/shard_map/ppermute | solution.py:259
  41.0 14.3 %collective-permute-start.7 = (bf16[256,2048]{1,0:T(8,128)(2,1)}, bf16[256,2048]{1,0:T(8,128)(2,1)S(1)}, u32[]{:S(2)}, u32[]{:S(2)}) collective-permute-start(bf16[256,2048]{1,0:T(8,128)(2,1)} %refs_0_.1), channel_id=1, source_target_pairs={{0,2},{2,0},{1,3},{3,1},{4,6},{6,4},{5,7},{7,5},{8,10},{10,8},{9,1... | collective-permute-start | bytes 3145736 | tf_op jit(solution)/shard_map/ppermute | solution.py:247
  41.8 33.7 %collective-permute-start.3 = (bf16[256,2048]{1,0:T(8,128)(2,1)}, bf16[256,2048]{1,0:T(8,128)(2,1)}, u32[]{:S(2)}, u32[]{:S(2)}) collective-permute-start(bf16[256,2048]{1,0:T(8,128)(2,1)} %collective-permute-done.refs_2_), channel_id=1, source_target_pairs={{0,4},{4,12},{12,20},{20,28},{28,24},{24,16},{16,8},{8,0},{1,5},{5... | collective-permute-start | bytes 3145736 | tf_op jit(solution)/shard_map/ppermute | solution.py:85
  43.1 32.4 %collective-permute-start.8 = (bf16[256,2048]{1,0:T(8,128)(2,1)}, bf16[256,2048]{1,0:T(8,128)(2,1)S(1)}, u32[]{:S(2)}, u32[]{:S(2)}) collective-permute-start(bf16[256,2048]{1,0:T(8,128)(2,1)} %collective-permute-done.refs_2_), channel_id=1, source_target_pairs={{0,2},{2,0},{1,3},{3,1},{4,6},{6,4},{5,7},{7,5},{8,10},{10,8},{9,1... | collective-permute-start | bytes 3145736 | tf_op jit(solution)/shard_map/ppermute | solution.py:247
  43.4 32.0 %collective-permute-start.4 = (bf16[256,2048]{1,0:T(8,128)(2,1)}, bf16[256,2048]{1,0:T(8,128)(2,1)}, u32[]{:S(2)}, u32[]{:S(2)}) collective-permute-start(bf16[256,2048]{1,0:T(8,128)(2,1)} %collective-permute-done.1.refs_4_), channel_id=1, source_target_pairs={{4,0},{12,4},{20,12},{28,20},{24,28},{16,24},{8,16},{0,8},{5,1},{1... | collective-permute-start | bytes 3145736 | tf_op jit(solution)/shard_map/ppermute | solution.py:85
  54.2 21.3 %collective-permute-start.9 = (bf16[256,2048]{1,0:T(8,128)(2,1)}, bf16[256,2048]{1,0:T(8,128)(2,1)S(1)}, u32[]{:S(2)}, u32[]{:S(2)}) collective-permute-start(bf16[256,2048]{1,0:T(8,128)(2,1)} %collective-permute-done.1.refs_4_), channel_id=1, source_target_pairs={{0,2},{2,0},{1,3},{3,1},{4,6},{6,4},{5,7},{7,5},{8,10},{10,8},{9,1... | collective-permute-start | bytes 3145736 | tf_op jit(solution)/shard_map/ppermute | solution.py:247
  75.5 36.6 %collective-permute-start.10 = (bf16[256,2048]{1,0:T(8,128)(2,1)}, bf16[256,2048]{1,0:T(8,128)(2,1)}, u32[]{:S(2)}, u32[]{:S(2)}) collective-permute-start(bf16[256,2048]{1,0:T(8,128)(2,1)} %collective-permute-done.3.refs_6_), channel_id=1, source_target_pairs={{0,4},{4,12},{12,20},{20,28},{28,24},{24,16},{16,8},{8,0},{1,5},{5... | collective-permute-start | bytes 3145736 | tf_op jit(solution)/shard_map/ppermute | solution.py:85
  76.8 35.2 %collective-permute-start.11 = (bf16[256,2048]{1,0:T(8,128)(2,1)}, bf16[256,2048]{1,0:T(8,128)(2,1)}, u32[]{:S(2)}, u32[]{:S(2)}) collective-permute-start(bf16[256,2048]{1,0:T(8,128)(2,1)} %collective-permute-done.4.refs_8_), channel_id=1, source_target_pairs={{4,0},{12,4},{20,12},{28,20},{24,28},{16,24},{8,16},{0,8},{5,1},{1... | collective-permute-start | bytes 3145736 | tf_op jit(solution)/shard_map/ppermute | solution.py:85
  77.0 35.1 %collective-permute-start.13 = (bf16[256,2048]{1,0:T(8,128)(2,1)}, bf16[256,2048]{1,0:T(8,128)(2,1)}, u32[]{:S(2)}, u32[]{:S(2)}) collective-permute-start(bf16[256,2048]{1,0:T(8,128)(2,1)} %collective-permute-done.3.refs_6_), channel_id=1, source_target_pairs={{0,2},{2,0},{1,3},{3,1},{4,6},{6,4},{5,7},{7,5},{8,10},{10,8},{9,1... | collective-permute-start | bytes 3145736 | tf_op jit(solution)/shard_map/ppermute | solution.py:268
  78.8 33.3 %collective-permute-start.14 = (bf16[256,2048]{1,0:T(8,128)(2,1)}, bf16[256,2048]{1,0:T(8,128)(2,1)}, u32[]{:S(2)}, u32[]{:S(2)}) collective-permute-start(bf16[256,2048]{1,0:T(8,128)(2,1)} %collective-permute-done.4.refs_8_), channel_id=1, source_target_pairs={{0,2},{2,0},{1,3},{3,1},{4,6},{6,4},{5,7},{7,5},{8,10},{10,8},{9,1... | collective-permute-start | bytes 3145736 | tf_op jit(solution)/shard_map/ppermute | solution.py:268
  78.8 31.8 %collective-permute-start.12 = (f32[8,128,128]{2,1,0:T(8,128)S(1)}, f32[8,128,128]{2,1,0:T(8,128)}, u32[]{:S(2)}, u32[]{:S(2)}) collective-permute-start(f32[8,128,128]{2,1,0:T(8,128)S(1)} %add.83), channel_id=1, source_target_pairs={{0,8},{4,12},{8,16},{12,20},{16,24},{20,28},{1,9},{5,13},{9,17},{1... | collective-permute-start | bytes 1572872 | tf_op jit(solution)/shard_map/ppermute | solution.py:259
  110.5 11.6 %collective-permute-start.21 = (bf16[1,128,2048]{2,1,0:T(8,128)(2,1)}, bf16[1,128,2048]{2,1,0:T(8,128)(2,1)}, u32[]{:S(2)}, u32[]{:S(2)}) collective-permute-start(bf16[1,128,2048]{2,1,0:T(8,128)(2,1)} %bitcast.57), channel_id=1, source_target_pairs={{0,1},{1,0},{2,3},{3,2},{4,5},{5,4},{6,7},{7,6},{8,9},{9,8},{10,11... | collective-permute-start | bytes 1572872 | tf_op jit(solution)/shard_map/ppermute | solution.py:38
  112.1 43.6 %collective-permute-start.18 = (bf16[256,2048]{1,0:T(8,128)(2,1)}, bf16[256,2048]{1,0:T(8,128)(2,1)}, u32[]{:S(2)}, u32[]{:S(2)}) collective-permute-start(bf16[256,2048]{1,0:T(8,128)(2,1)} %collective-permute-done.10.refs_10_), channel_id=1, source_target_pairs={{0,2},{2,0},{1,3},{3,1},{4,6},{6,4},{5,7},{7,5},{8,10},{10,8},{9,1... | collective-permute-start | bytes 3145736 | tf_op jit(solution)/shard_map/ppermute | solution.py:268
  114.5 41.2 %collective-permute-start.19 = (bf16[256,2048]{1,0:T(8,128)(2,1)}, bf16[256,2048]{1,0:T(8,128)(2,1)}, u32[]{:S(2)}, u32[]{:S(2)}) collective-permute-start(bf16[256,2048]{1,0:T(8,128)(2,1)} %collective-permute-done.11.refs_12_), channel_id=1, source_target_pairs={{0,2},{2,0},{1,3},{3,1},{4,6},{6,4},{5,7},{7,5},{8,10},{10,8},{9,1... | collective-permute-start | bytes 3145736 | tf_op jit(solution)/shard_map/ppermute | solution.py:268
  119.7 36.0 %collective-permute-start.15 = (bf16[128,2048]{1,0:T(8,128)(2,1)}, bf16[128,2048]{1,0:T(8,128)(2,1)}, u32[]{:S(2)}, u32[]{:S(2)}) collective-permute-start(bf16[128,2048]{1,0:T(8,128)(2,1)} %slice.14), channel_id=1, source_target_pairs={{0,4},{4,12},{12,20},{20,28},{28,24},{24,16},{16,8},{8,0},{1,5},{5... | collective-permute-start | bytes 1572872 | tf_op jit(solution)/shard_map/ppermute | solution.py:82
  121.0 34.7 %collective-permute-start.16 = (bf16[128,2048]{1,0:T(8,128)(2,1)}, bf16[128,2048]{1,0:T(8,128)(2,1)}, u32[]{:S(2)}, u32[]{:S(2)}) collective-permute-start(bf16[128,2048]{1,0:T(8,128)(2,1)} %slice.15), channel_id=1, source_target_pairs={{4,0},{12,4},{20,12},{28,20},{24,28},{16,24},{8,16},{0,8},{5,1},{1... | collective-permute-start | bytes 1572872 | tf_op jit(solution)/shard_map/ppermute | solution.py:82
  122.1 32.4 %collective-permute-start.17 = (f32[8,128,128]{2,1,0:T(8,128)S(1)}, f32[8,128,128]{2,1,0:T(8,128)}, u32[]{:S(2)}, u32[]{:S(2)}) collective-permute-start(f32[8,128,128]{2,1,0:T(8,128)S(1)} %add.84), channel_id=1, source_target_pairs={{0,16},{4,20},{8,24},{12,28},{1,17},{5,21},{9,25},{13,29},{2,18},{... | collective-permute-start | bytes 1572872 | tf_op jit(solution)/shard_map/ppermute | solution.py:259
  156.6 6.6 %collective-permute-start.20 = (f32[8,128,128]{2,1,0:T(8,128)}, f32[8,128,128]{2,1,0:T(8,128)}, u32[]{:S(2)}, u32[]{:S(2)}) collective-permute-start(f32[8,128,128]{2,1,0:T(8,128)} %sub.20), channel_id=1, source_target_pairs={{0,2},{2,0},{1,3},{3,1},{4,6},{6,4},{5,7},{7,5},{8,10},{10,8},{9,1... | collective-permute-start | bytes 1572872 | tf_op jit(solution)/shard_map/ppermute | solution.py:141
  168.3 25.1 %collective-permute-start.22 = (bf16[256,2048]{1,0:T(8,128)(2,1)S(1)}, bf16[256,2048]{1,0:T(8,128)(2,1)S(1)}, u32[]{:S(2)}, u32[]{:S(2)}) collective-permute-start(bf16[256,2048]{1,0:T(8,128)(2,1)S(1)} %copy.38), channel_id=1, source_target_pairs={{0,1},{1,0},{2,3},{3,2},{4,5},{5,4},{6,7},{7,6},{8,9},{9,8},{10,11... | collective-permute-start | bytes 3145736 | tf_op jit(solution)/shard_map/ppermute | solution.py:127
  173.1 22.0 %collective-permute-start.23 = (bf16[256,2048]{1,0:T(8,128)(2,1)S(1)}, bf16[256,2048]{1,0:T(8,128)(2,1)}, u32[]{:S(2)}, u32[]{:S(2)}) collective-permute-start(bf16[256,2048]{1,0:T(8,128)(2,1)S(1)} %constant_dynamic-update-slice_fusion.refs_14_), channel_id=1, source_target_pairs={{0,2},{2,0},{1,3},{3,1},{4,6},{6,4},{5,7},{7,5},{8,10},{10,8},{9,1... | collective-permute-start | bytes 3145736 | tf_op jit(solution)/shard_map/ppermute | solution.py:268
  (12 other events, 153.3 us)

commit v14 on v11

--- a/solution.py
+++ b/solution.py
@@ -30,14 +30,11 @@
 
 def head_blocks(arrays, n_head, place):
     if n_head == 2:
-        rows = arrays[0].shape[0]
         width = arrays[0].shape[1] // 2
-        stacked = jnp.stack(arrays).reshape(len(arrays), rows, 2, width)
-        own = lax.dynamic_index_in_dim(stacked, place, 2, False)
-        sent = lax.dynamic_index_in_dim(stacked, 1 - place, 2, False)
-        other = lax.ppermute(sent, "head", SWAP)
-        block = pair_order(own, other, place, 1)
-        return [block[i] for i in range(len(arrays))]
+        own = [lax.dynamic_slice_in_dim(a, place * width, width, 1) for a in arrays]
+        sent = [lax.dynamic_slice_in_dim(a, (1 - place) * width, width, 1) for a in arrays]
+        other = lax.ppermute(tuple(sent), "head", SWAP)
+        return [pair_order(o, r, place, 0) for o, r in zip(own, other)]
     return [
         lax.all_to_all(a, "head", split_axis=1, concat_axis=0, tiled=True) for a in arrays
     ]
@@ -256,6 +253,10 @@
     swapped += [lax.ppermute(w, "core", SWAP) for w in got[len(swapped):]]
     chip_prefix_half, within_block, swapped = barrier((chip_prefix_half, within_block, swapped))
     for step in range(2, n_steps + 1):
+        if step >= 4:
+            early = len(got) - 2
+            swapped += [lax.ppermute(w, "core", SWAP) for w in got[len(swapped):early]]
+            ahead, behind, swapped = barrier((ahead, behind, swapped))
         ahead, behind = ring_step(ahead, behind, order, last=step == n_steps)
         if step == n_steps:
             got.append(jnp.concatenate([ahead, behind], 0))

time: 175 us -> 175 us (level)
  waiting for transfers between devices: 96.2 us -> 100 us
  local copies, waits for them, and re-layouts: 20.8 us -> 17.3 us
  other arithmetic: 8.14 us -> 11.4 us
  starting transfers between devices: 32 us -> 29.1 us
    ppermute x3, waiting for transfers between devices: 1.01 us -> 6.66 us  [ring_step(): lax.ppermute(behind, 'chip', backward)]
    ppermute x5 -> x3, starting transfers between devices: 8.6 us -> 3.46 us  [local_ring(): swapped += [lax.ppermute(w, 'core', SWAP) for w in got[len(swapped):]]]
    ppermute x1, waiting for transfers between devices: 3.52 us -> 7.32 us  [ring_step(): lax.ppermute(ahead[:half_rows], 'chip', forward)]
    ppermute x3, waiting for transfers between devices: 29.2 us -> 25.9 us  [ring_step(): lax.ppermute(ahead, 'chip', forward)]
    ppermute x2 -> x5, waiting for transfers between devices: 21.1 us -> 18 us  [the longest x3 18 us: head_blocks(): other = lax.ppermute(tuple(sent), 'head', SWAP)]
    select_n x3 -> x5, other arithmetic: 0.29 us -> 2.69 us  [pair_order(): first = jnp.where(place == 0, own, other)]
    ppermute x2 -> x5, starting transfers between devices: 1.47 us -> 3.66 us  [the longest x2 1.87 us: local_ring(): swapped += [lax.ppermute(w, 'core', SWAP) for w in got[len(swapped):early]]]
    ppermute x1, starting transfers between devices: 2.25 us -> 0.06 us  [ring_step(): lax.ppermute(ahead[:half_rows], 'chip', forward)]
  transfers between devices with their start and end apart: 24 -> 25, of which waited for: 11 -> 14; matrix products, arithmetic and copies ran while one was open for 14% -> 17% of each run, Pallas kernels for 0% -> 0%
where the time goes in v14:
time: 175 us; the launch traced here: 172 us
  waiting for transfers between devices  100 us (57%)
  starting transfers between devices  29.1 us (17%)
  local copies, waits for them, and re-layouts  17.3 us (10%)
  other arithmetic  11.4 us (7%)
  Pallas kernels  9.62 us (5%)
  matrix products  3.92 us (2%)
    ppermute x3, waiting for transfers between devices, exclusive_prefix(): total = total + lax.ppermute(total, axis, pairs)  38.6 us
    ppermute x3, waiting for transfers between devices, ring_step(): lax.ppermute(ahead, 'chip', forward)  25.9 us
    ppermute x3, waiting for transfers between devices, head_blocks(): other = lax.ppermute(tuple(sent), 'head', SWAP)  18 us
    pallas_call x1, Pallas kernels, project_blocks(): pl.pallas_call(kernel, out_shape=jax.ShapeDtypeStruct((tokens, cols), jnp...  9.62 us
    ppermute x3, starting transfers between devices, exclusive_prefix(): total = total + lax.ppermute(total, axis, pairs)  8.54 us
    ppermute x1, waiting for transfers between devices, ring_step(): lax.ppermute(ahead[:half_rows], 'chip', forward)  7.32 us
    ppermute x3, waiting for transfers between devices, ring_step(): lax.ppermute(behind, 'chip', backward)  6.66 us
    unnamed x35, local copies, waits for them, and re-layouts  6.16 us
  transfers between devices with their start and end apart: 25, of which 14 were waited for; matrix products, arithmetic and copies ran while one was open for 17% of the time, Pallas kernels for 0%

profile of v14, /device:TPU:13, one launch (start us, length us, event | category | flops | bytes accessed | tf_op | source)
XLA Modules:
  0.0 171.8 jit_solution(14122830088140832875)
XLA Ops:
  5.0 2.3 %constant_dynamic-slice_fusion.1 = (bf16[128,2048]{1,0:T(8,128)(2,1)}, bf16[128,2048]{1,0:T(8,128)(2,1)}, bf16[128,2048]{1,0:T(8,128)(2,1)S(1)}, bf16[128,2048]{1,0:T(8,128)(2,1)S(1)}) fusion(bf16[128,4096]{1,0:T(8,128)(2,1)S(1)} %copy-done.9, s32[]{:T(128)S(6)} %select_n.96, s32[]{:T(128)S(6)} %select_n.97, bf16[128,4096]{1,0:T(8,128)(2,1)} %param.10), kind=kLoop, calls=%fused_computation.38 | loop fusion | bytes 4194312 | tf_op jit(solution)/shard_map/dynamic_slice | solution.py:34
  8.5 6.9 %collective-permute-done.2 = bf16[128,2048]{0,1:T(8,128)(2,1)S(1)} collective-permute-done((bf16[128,2048]{0,1:T(8,128)(2,1)}, bf16[128,2048]{0,1:T(8,128)(2,1)S(1)}, u32[]{:S(2)}, u32[]{:S(2)}) %collective-permute-start.2) | collective-permute-done | bytes 524320 | tf_op jit(solution)/shard_map/ppermute | solution.py:36
  15.7 11.0 %collective-permute-done.3 = bf16[128,2048]{0,1:T(8,128)(2,1)S(1)} collective-permute-done((bf16[128,2048]{0,1:T(8,128)(2,1)S(1)}, bf16[128,2048]{0,1:T(8,128)(2,1)S(1)}, u32[]{:S(2)}, u32[]{:S(2)}) %collective-permute-start.3) | collective-permute-done | bytes 524320 | tf_op jit(solution)/shard_map/ppermute | solution.py:36
  29.0 2.2 %collective-permute-start.4 = (f32[16,128,128]{2,1,0:T(8,128)S(1)}, f32[16,128,128]{2,1,0:T(8,128)S(1)}, u32[]{:S(2)}, u32[]{:S(2)}) collective-permute-start(f32[16,128,128]{2,1,0:T(8,128)S(1)} %fusion.11), channel_id=1, source_target_pairs={{0,2},{2,0},{1,3},{3,1},{4,6},{6,4},{5,7},{7,5},{8,10},{10,8},{9,1... | collective-permute-start | bytes 3145736 | tf_op jit(solution)/shard_map/ppermute | solution.py:130
  31.3 2.3 %collective-permute-done.4 = f32[16,128,128]{2,1,0:T(8,128)S(1)} collective-permute-done((f32[16,128,128]{2,1,0:T(8,128)S(1)}, f32[16,128,128]{2,1,0:T(8,128)S(1)}, u32[]{:S(2)}, u32[]{:S(2)}) %collective-permute-start.4) | collective-permute-done | bytes 1048608 | tf_op jit(solution)/shard_map/ppermute | solution.py:130
  33.6 2.2 %collective-permute-start.5 = (f32[8,128,128]{2,1,0:T(8,128)S(1)}, f32[8,128,128]{2,1,0:T(8,128)S(1)}, u32[]{:S(2)}, u32[]{:S(2)}) collective-permute-start(f32[8,128,128]{2,1,0:T(8,128)S(1)} %dynamic-slice_add_fusion), channel_id=1, source_target_pairs={{0,4},{4,8},{8,12},{12,16},{16,20},{20,24},{24,28},{1,5},{5,9},{9,... | collective-permute-start | bytes 1572872 | tf_op jit(solution)/shard_map/ppermute | solution.py:20
  35.8 13.0 %collective-permute-done.5 = f32[8,128,128]{2,1,0:T(8,128)S(1)} collective-permute-done((f32[8,128,128]{2,1,0:T(8,128)S(1)}, f32[8,128,128]{2,1,0:T(8,128)S(1)}, u32[]{:S(2)}, u32[]{:S(2)}) %collective-permute-start.5) | collective-permute-done | bytes 524320 | tf_op jit(solution)/shard_map/ppermute | solution.py:20
  48.9 3.2 %collective-permute-start.6 = (f32[8,128,128]{2,1,0:T(8,128)S(1)}, f32[8,128,128]{2,1,0:T(8,128)}, u32[]{:S(2)}, u32[]{:S(2)}) collective-permute-start(f32[8,128,128]{2,1,0:T(8,128)S(1)} %add.79), channel_id=1, source_target_pairs={{0,8},{4,12},{8,16},{12,20},{16,24},{20,28},{1,9},{5,13},{9,17},{1... | collective-permute-start | bytes 1572872 | tf_op jit(solution)/shard_map/ppermute | solution.py:20
  52.1 2.1 %copy.33 = bf16[128,2048]{0,1:T(8,128)(2,1)} copy(bf16[128,2048]{1,0:T(8,128)(2,1)} %get-tuple-element.44) | data formatting | bytes 1048576
  57.0 6.0 %collective-permute-done.6 = f32[8,128,128]{2,1,0:T(8,128)} collective-permute-done((f32[8,128,128]{2,1,0:T(8,128)S(1)}, f32[8,128,128]{2,1,0:T(8,128)}, u32[]{:S(2)}, u32[]{:S(2)}) %collective-permute-start.6) | collective-permute-done | bytes 524320 | tf_op jit(solution)/shard_map/ppermute | solution.py:20
  64.2 3.2 %collective-permute-start.7 = (f32[8,128,128]{2,1,0:T(8,128)S(1)}, f32[8,128,128]{2,1,0:T(8,128)S(1)}, u32[]{:S(2)}, u32[]{:S(2)}) collective-permute-start(f32[8,128,128]{2,1,0:T(8,128)S(1)} %add.80), channel_id=1, source_target_pairs={{0,16},{4,20},{8,24},{12,28},{1,17},{5,21},{9,25},{13,29},{2,18},{... | collective-permute-start | bytes 1572872 | tf_op jit(solution)/shard_map/ppermute | solution.py:20
  69.6 19.6 %collective-permute-done.7 = f32[8,128,128]{2,1,0:T(8,128)S(1)} collective-permute-done((f32[8,128,128]{2,1,0:T(8,128)S(1)}, f32[8,128,128]{2,1,0:T(8,128)S(1)}, u32[]{:S(2)}, u32[]{:S(2)}) %collective-permute-start.7) | collective-permute-done | bytes 524320 | tf_op jit(solution)/shard_map/ppermute | solution.py:20
  90.0 2.9 %fusion.1 = f32[256,16,128]{0,2,1:T(8,128)S(1)} fusion(bf16[256,16,128]{0,2,1:T(8,128)(2,1)} %bitcast.25, bf16[256,16,128]{0,2,1:T(8,128)(2,1)} %bitcast.26, bf16[256,16,128]{0,2,1:T(8,128)(2,1)S(1)} %bitcast.23, pred[256,256]{1,0:T(8,128)(4,1)S(1)} %iota_compare_fusion), kind=kOutput, calls=%fused_computation.7 | convolution fusion | flops 538968064 | bytes 5308416 | tf_op jit(solution)/shard_map/hts,she->the/dot_general | solution.py:103
  93.0 2.3 %add_subtract_fusion = f32[8,128,128]{2,1,0:T(8,128)} fusion(f32[8,128,128]{2,1,0:T(8,128)} %copy-done.3, f32[8,128,128]{2,1,0:T(8,128)} %copy-done.8, f32[8,128,128]{2,1,0:T(8,128)} %copy-done.10), kind=kLoop, calls=%fused_computation.18 | loop fusion | flops 262144 | bytes 2097152 | tf_op jit(solution)/shard_map/sub | solution.py:22
  95.3 2.7 %collective-permute-start.12 = (f32[8,128,128]{2,1,0:T(8,128)}, f32[8,128,128]{2,1,0:T(8,128)}, u32[]{:S(2)}, u32[]{:S(2)}) collective-permute-start(f32[8,128,128]{2,1,0:T(8,128)} %add_subtract_fusion), channel_id=1, source_target_pairs={{0,2},{2,0},{1,3},{3,1},{4,6},{6,4},{5,7},{7,5},{8,10},{10,8},{9,1... | collective-permute-start | bytes 1572872 | tf_op jit(solution)/shard_map/ppermute | solution.py:138
  99.4 12.4 %collective-permute-done.14.refs_6_ = bf16[256,2048]{1,0:T(8,128)(2,1)} collective-permute-done((bf16[256,2048]{1,0:T(8,128)(2,1)}, bf16[256,2048]{1,0:T(8,128)(2,1)}, u32[]{:S(2)}, u32[]{:S(2)}) %collective-permute-start.14) | collective-permute-done | bytes 1048608 | tf_op jit(solution)/shard_map/ppermute | solution.py:82
  111.8 2.2 %collective-permute-start.15 = (bf16[256,2048]{1,0:T(8,128)(2,1)}, bf16[256,2048]{1,0:T(8,128)(2,1)}, u32[]{:S(2)}, u32[]{:S(2)}) collective-permute-start(bf16[256,2048]{1,0:T(8,128)(2,1)} %collective-permute-done.14.refs_6_), channel_id=1, source_target_pairs={{0,4},{4,12},{12,20},{20,28},{28,24},{24,16},{16,8},{8,0},{1,5},{5... | collective-permute-start | bytes 3145736 | tf_op jit(solution)/shard_map/ppermute | solution.py:82
  114.0 1.8 %collective-permute-start.18 = (bf16[256,2048]{1,0:T(8,128)(2,1)}, bf16[256,2048]{1,0:T(8,128)(2,1)}, u32[]{:S(2)}, u32[]{:S(2)}) collective-permute-start(bf16[256,2048]{1,0:T(8,128)(2,1)} %collective-permute-done.14.refs_6_), channel_id=1, source_target_pairs={{0,2},{2,0},{1,3},{3,1},{4,6},{6,4},{5,7},{7,5},{8,10},{10,8},{9,1... | collective-permute-start | bytes 3145736 | tf_op jit(solution)/shard_map/ppermute | solution.py:258
  122.4 12.8 %collective-permute-done.15.refs_10_ = bf16[256,2048]{1,0:T(8,128)(2,1)} collective-permute-done((bf16[256,2048]{1,0:T(8,128)(2,1)}, bf16[256,2048]{1,0:T(8,128)(2,1)}, u32[]{:S(2)}, u32[]{:S(2)}) %collective-permute-start.15) | collective-permute-done | bytes 1048608 | tf_op jit(solution)/shard_map/ppermute | solution.py:82
  135.2 5.7 %collective-permute-done.17.refs_12_ = bf16[256,2048]{1,0:T(8,128)(2,1)} collective-permute-done((bf16[256,2048]{1,0:T(8,128)(2,1)}, bf16[256,2048]{1,0:T(8,128)(2,1)}, u32[]{:S(2)}, u32[]{:S(2)}) %collective-permute-start.17) | collective-permute-done | bytes 1048608 | tf_op jit(solution)/shard_map/ppermute | solution.py:82
  142.1 1.9 %slice.7 = bf16[128,2048]{1,0:T(8,128)(2,1)} slice(bf16[256,2048]{1,0:T(8,128)(2,1)} %collective-permute-done.17.refs_12_), slice={[128:256], [0:2048]} | slice | bytes 1048576 | tf_op jit(solution)/shard_map/slice | solution.py:80
  147.5 7.3 %collective-permute-done.22 = bf16[128,2048]{1,0:T(8,128)(2,1)} collective-permute-done((bf16[128,2048]{1,0:T(8,128)(2,1)S(1)}, bf16[128,2048]{1,0:T(8,128)(2,1)}, u32[]{:S(2)}, u32[]{:S(2)}) %collective-permute-start.22) | collective-permute-done | bytes 524320 | tf_op jit(solution)/shard_map/ppermute | solution.py:79
  157.6 2.1 %collective-permute-start.24 = (bf16[256,2048]{1,0:T(8,128)(2,1)S(1)}, bf16[256,2048]{1,0:T(8,128)(2,1)}, u32[]{:S(2)}, u32[]{:S(2)}) collective-permute-start(bf16[256,2048]{1,0:T(8,128)(2,1)S(1)} %constant_dynamic-update-slice_fusion.refs_14_), channel_id=1, source_target_pairs={{0,2},{2,0},{1,3},{3,1},{4,6},{6,4},{5,7},{7,5},{8,10},{10,8},{9,1... | collective-permute-start | bytes 3145736 | tf_op jit(solution)/shard_map/ppermute | solution.py:267
  162.2 9.6 %shard_map.82 = bf16[256,2048]{1,0:T(8,128)(2,1)} custom-call(s32[16]{0:T(128)} %mul.51.starts_ref, bf16[256,4096]{1,0:T(8,128)(2,1)} %pad_maximum_fusion.normed_ref, bf16[256,2048]{1,0:T(8,128)(2,1)} %refs_0_.1, bf16[256,2048]{1,0:T(8,128)(2,1)} %collective-permute-done.9.refs_1_, bf16[256,2048]{1,0:T(8,128)(2,1)} %collective-permute-done.refs_2_, ...), custom_call_target="tpu_custom_call" | custom-call | tf_op jit(solution)/shard_map/pallas_call | solution.py:189
  (95 shorter events, 33.6 us)
Async XLA Ops:
  2.4 13.1 %collective-permute-start.2 = (bf16[128,2048]{0,1:T(8,128)(2,1)}, bf16[128,2048]{0,1:T(8,128)(2,1)S(1)}, u32[]{:S(2)}, u32[]{:S(2)}) collective-permute-start(bf16[128,2048]{0,1:T(8,128)(2,1)} %copy.29), channel_id=1, source_target_pairs={{0,1},{1,0},{2,3},{3,2},{4,5},{5,4},{6,7},{7,6},{8,9},{9,8},{10,11... | collective-permute-start | bytes 1572872 | tf_op jit(solution)/shard_map/ppermute | solution.py:36
  3.6 24.0 %collective-permute-start = (bf16[256,2048]{1,0:T(8,128)(2,1)}, bf16[256,2048]{1,0:T(8,128)(2,1)}, u32[]{:S(2)}, u32[]{:S(2)}) collective-permute-start(bf16[256,2048]{1,0:T(8,128)(2,1)} %refs_0_.1), channel_id=1, source_target_pairs={{0,4},{4,12},{12,20},{20,28},{28,24},{24,16},{16,8},{8,0},{1,5},{5... | collective-permute-start | bytes 3145736 | tf_op jit(solution)/shard_map/ppermute | solution.py:82
  4.9 23.7 %collective-permute-start.1 = (bf16[256,2048]{1,0:T(8,128)(2,1)}, bf16[256,2048]{1,0:T(8,128)(2,1)}, u32[]{:S(2)}, u32[]{:S(2)}) collective-permute-start(bf16[256,2048]{1,0:T(8,128)(2,1)} %refs_0_.1), channel_id=1, source_target_pairs={{4,0},{12,4},{20,12},{28,20},{24,28},{16,24},{8,16},{0,8},{5,1},{1... | collective-permute-start | bytes 3145736 | tf_op jit(solution)/shard_map/ppermute | solution.py:82
  7.7 19.0 %collective-permute-start.3 = (bf16[128,2048]{0,1:T(8,128)(2,1)S(1)}, bf16[128,2048]{0,1:T(8,128)(2,1)S(1)}, u32[]{:S(2)}, u32[]{:S(2)}) collective-permute-start(bf16[128,2048]{0,1:T(8,128)(2,1)S(1)} %copy.31), channel_id=1, source_target_pairs={{0,1},{1,0},{2,3},{3,2},{4,5},{5,4},{6,7},{7,6},{8,9},{9,8},{10,11... | collective-permute-start | bytes 1572872 | tf_op jit(solution)/shard_map/ppermute | solution.py:36
  33.6 15.2 %collective-permute-start.5 = (f32[8,128,128]{2,1,0:T(8,128)S(1)}, f32[8,128,128]{2,1,0:T(8,128)S(1)}, u32[]{:S(2)}, u32[]{:S(2)}) collective-permute-start(f32[8,128,128]{2,1,0:T(8,128)S(1)} %dynamic-slice_add_fusion), channel_id=1, source_target_pairs={{0,4},{4,8},{8,12},{12,16},{16,20},{20,24},{24,28},{1,5},{5,9},{9,... | collective-permute-start | bytes 1572872 | tf_op jit(solution)/shard_map/ppermute | solution.py:20
  48.9 14.2 %collective-permute-start.6 = (f32[8,128,128]{2,1,0:T(8,128)S(1)}, f32[8,128,128]{2,1,0:T(8,128)}, u32[]{:S(2)}, u32[]{:S(2)}) collective-permute-start(f32[8,128,128]{2,1,0:T(8,128)S(1)} %add.79), channel_id=1, source_target_pairs={{0,8},{4,12},{8,16},{12,20},{16,24},{20,28},{1,9},{5,13},{9,17},{1... | collective-permute-start | bytes 1572872 | tf_op jit(solution)/shard_map/ppermute | solution.py:20
  54.1 13.2 %collective-permute-start.8 = (bf16[128,2048]{0,1:T(8,128)(2,1)}, bf16[128,2048]{0,1:T(8,128)(2,1)}, u32[]{:S(2)}, u32[]{:S(2)}) collective-permute-start(bf16[128,2048]{0,1:T(8,128)(2,1)} %copy.33), channel_id=1, source_target_pairs={{0,1},{1,0},{2,3},{3,2},{4,5},{5,4},{6,7},{7,6},{8,9},{9,8},{10,11... | collective-permute-start | bytes 1572872 | tf_op jit(solution)/shard_map/ppermute | solution.py:36
  54.4 40.9 %collective-permute-start.9 = (bf16[256,2048]{1,0:T(8,128)(2,1)}, bf16[256,2048]{1,0:T(8,128)(2,1)}, u32[]{:S(2)}, u32[]{:S(2)}) collective-permute-start(bf16[256,2048]{1,0:T(8,128)(2,1)} %refs_0_.1), channel_id=1, source_target_pairs={{0,2},{2,0},{1,3},{3,1},{4,6},{6,4},{5,7},{7,5},{8,10},{10,8},{9,1... | collective-permute-start | bytes 3145736 | tf_op jit(solution)/shard_map/ppermute | solution.py:244
  56.5 38.8 %collective-permute-start.10 = (bf16[256,2048]{1,0:T(8,128)(2,1)}, bf16[256,2048]{1,0:T(8,128)(2,1)}, u32[]{:S(2)}, u32[]{:S(2)}) collective-permute-start(bf16[256,2048]{1,0:T(8,128)(2,1)} %collective-permute-done.refs_2_), channel_id=1, source_target_pairs={{0,2},{2,0},{1,3},{3,1},{4,6},{6,4},{5,7},{7,5},{8,10},{10,8},{9,1... | collective-permute-start | bytes 3145736 | tf_op jit(solution)/shard_map/ppermute | solution.py:244
  56.6 38.8 %collective-permute-start.11 = (bf16[256,2048]{1,0:T(8,128)(2,1)}, bf16[256,2048]{1,0:T(8,128)(2,1)}, u32[]{:S(2)}, u32[]{:S(2)}) collective-permute-start(bf16[256,2048]{1,0:T(8,128)(2,1)} %collective-permute-done.1.refs_4_), channel_id=1, source_target_pairs={{0,2},{2,0},{1,3},{3,1},{4,6},{6,4},{5,7},{7,5},{8,10},{10,8},{9,1... | collective-permute-start | bytes 3145736 | tf_op jit(solution)/shard_map/ppermute | solution.py:244
  64.2 25.0 %collective-permute-start.7 = (f32[8,128,128]{2,1,0:T(8,128)S(1)}, f32[8,128,128]{2,1,0:T(8,128)S(1)}, u32[]{:S(2)}, u32[]{:S(2)}) collective-permute-start(f32[8,128,128]{2,1,0:T(8,128)S(1)} %add.80), channel_id=1, source_target_pairs={{0,16},{4,20},{8,24},{12,28},{1,17},{5,21},{9,25},{13,29},{2,18},{... | collective-permute-start | bytes 1572872 | tf_op jit(solution)/shard_map/ppermute | solution.py:20
  69.6 42.2 %collective-permute-start.14 = (bf16[256,2048]{1,0:T(8,128)(2,1)}, bf16[256,2048]{1,0:T(8,128)(2,1)}, u32[]{:S(2)}, u32[]{:S(2)}) collective-permute-start(bf16[256,2048]{1,0:T(8,128)(2,1)} %collective-permute-done.refs_2_), channel_id=1, source_target_pairs={{0,4},{4,12},{12,20},{20,28},{28,24},{24,16},{16,8},{8,0},{1,5},{5... | collective-permute-start | bytes 3145736 | tf_op jit(solution)/shard_map/ppermute | solution.py:82
  89.2 26.6 %collective-permute-start.16 = (bf16[256,2048]{1,0:T(8,128)(2,1)}, bf16[256,2048]{1,0:T(8,128)(2,1)}, u32[]{:S(2)}, u32[]{:S(2)}) collective-permute-start(bf16[256,2048]{1,0:T(8,128)(2,1)} %collective-permute-done.1.refs_4_), channel_id=1, source_target_pairs={{4,0},{12,4},{20,12},{28,20},{24,28},{16,24},{8,16},{0,8},{5,1},{1... | collective-permute-start | bytes 3145736 | tf_op jit(solution)/shard_map/ppermute | solution.py:82
  95.3 20.6 %collective-permute-start.12 = (f32[8,128,128]{2,1,0:T(8,128)}, f32[8,128,128]{2,1,0:T(8,128)}, u32[]{:S(2)}, u32[]{:S(2)}) collective-permute-start(f32[8,128,128]{2,1,0:T(8,128)} %add_subtract_fusion), channel_id=1, source_target_pairs={{0,2},{2,0},{1,3},{3,1},{4,6},{6,4},{5,7},{7,5},{8,10},{10,8},{9,1... | collective-permute-start | bytes 1572872 | tf_op jit(solution)/shard_map/ppermute | solution.py:138
  111.8 23.4 %collective-permute-start.15 = (bf16[256,2048]{1,0:T(8,128)(2,1)}, bf16[256,2048]{1,0:T(8,128)(2,1)}, u32[]{:S(2)}, u32[]{:S(2)}) collective-permute-start(bf16[256,2048]{1,0:T(8,128)(2,1)} %collective-permute-done.14.refs_6_), channel_id=1, source_target_pairs={{0,4},{4,12},{12,20},{20,28},{28,24},{24,16},{16,8},{8,0},{1,5},{5... | collective-permute-start | bytes 3145736 | tf_op jit(solution)/shard_map/ppermute | solution.py:82
  114.0 26.9 %collective-permute-start.18 = (bf16[256,2048]{1,0:T(8,128)(2,1)}, bf16[256,2048]{1,0:T(8,128)(2,1)}, u32[]{:S(2)}, u32[]{:S(2)}) collective-permute-start(bf16[256,2048]{1,0:T(8,128)(2,1)} %collective-permute-done.14.refs_6_), channel_id=1, source_target_pairs={{0,2},{2,0},{1,3},{3,1},{4,6},{6,4},{5,7},{7,5},{8,10},{10,8},{9,1... | collective-permute-start | bytes 3145736 | tf_op jit(solution)/shard_map/ppermute | solution.py:258
  115.8 25.1 %collective-permute-start.17 = (bf16[256,2048]{1,0:T(8,128)(2,1)}, bf16[256,2048]{1,0:T(8,128)(2,1)}, u32[]{:S(2)}, u32[]{:S(2)}) collective-permute-start(bf16[256,2048]{1,0:T(8,128)(2,1)} %collective-permute-done.16.refs_8_), channel_id=1, source_target_pairs={{4,0},{12,4},{20,12},{28,20},{24,28},{16,24},{8,16},{0,8},{5,1},{1... | collective-permute-start | bytes 3145736 | tf_op jit(solution)/shard_map/ppermute | solution.py:82
  115.8 25.1 %collective-permute-start.19 = (bf16[256,2048]{1,0:T(8,128)(2,1)}, bf16[256,2048]{1,0:T(8,128)(2,1)}, u32[]{:S(2)}, u32[]{:S(2)}) collective-permute-start(bf16[256,2048]{1,0:T(8,128)(2,1)} %collective-permute-done.16.refs_8_), channel_id=1, source_target_pairs={{0,2},{2,0},{1,3},{3,1},{4,6},{6,4},{5,7},{7,5},{8,10},{10,8},{9,1... | collective-permute-start | bytes 3145736 | tf_op jit(solution)/shard_map/ppermute | solution.py:258
  120.8 39.0 %collective-permute-start.13 = (bf16[256,2048]{1,0:T(8,128)(2,1)S(1)}, bf16[256,2048]{1,0:T(8,128)(2,1)S(1)}, u32[]{:S(2)}, u32[]{:S(2)}) collective-permute-start(bf16[256,2048]{1,0:T(8,128)(2,1)S(1)} %copy.27), channel_id=1, source_target_pairs={{0,1},{1,0},{2,3},{3,2},{4,5},{5,4},{6,7},{7,6},{8,9},{9,8},{10,11... | collective-permute-start | bytes 3145736 | tf_op jit(solution)/shard_map/ppermute | solution.py:124
  142.0 12.8 %collective-permute-start.22 = (bf16[128,2048]{1,0:T(8,128)(2,1)S(1)}, bf16[128,2048]{1,0:T(8,128)(2,1)}, u32[]{:S(2)}, u32[]{:S(2)}) collective-permute-start(bf16[128,2048]{1,0:T(8,128)(2,1)S(1)} %slice.6), channel_id=1, source_target_pairs={{0,4},{4,12},{12,20},{20,28},{28,24},{24,16},{16,8},{8,0},{1,5},{5... | collective-permute-start | bytes 1572872 | tf_op jit(solution)/shard_map/ppermute | solution.py:79
  144.0 12.6 %collective-permute-start.23 = (bf16[128,2048]{1,0:T(8,128)(2,1)}, bf16[128,2048]{1,0:T(8,128)(2,1)}, u32[]{:S(2)}, u32[]{:S(2)}) collective-permute-start(bf16[128,2048]{1,0:T(8,128)(2,1)} %slice.7), channel_id=1, source_target_pairs={{4,0},{12,4},{20,12},{28,20},{24,28},{16,24},{8,16},{0,8},{5,1},{1... | collective-permute-start | bytes 1572872 | tf_op jit(solution)/shard_map/ppermute | solution.py:79
  146.1 15.4 %collective-permute-start.20 = (bf16[256,2048]{1,0:T(8,128)(2,1)}, bf16[256,2048]{1,0:T(8,128)(2,1)}, u32[]{:S(2)}, u32[]{:S(2)}) collective-permute-start(bf16[256,2048]{1,0:T(8,128)(2,1)} %collective-permute-done.15.refs_10_), channel_id=1, source_target_pairs={{0,2},{2,0},{1,3},{3,1},{4,6},{6,4},{5,7},{7,5},{8,10},{10,8},{9,1... | collective-permute-start | bytes 3145736 | tf_op jit(solution)/shard_map/ppermute | solution.py:267
  147.5 14.0 %collective-permute-start.21 = (bf16[256,2048]{1,0:T(8,128)(2,1)}, bf16[256,2048]{1,0:T(8,128)(2,1)}, u32[]{:S(2)}, u32[]{:S(2)}) collective-permute-start(bf16[256,2048]{1,0:T(8,128)(2,1)} %collective-permute-done.17.refs_12_), channel_id=1, source_target_pairs={{0,2},{2,0},{1,3},{3,1},{4,6},{6,4},{5,7},{7,5},{8,10},{10,8},{9,1... | collective-permute-start | bytes 3145736 | tf_op jit(solution)/shard_map/ppermute | solution.py:267
  157.6 4.5 %collective-permute-start.24 = (bf16[256,2048]{1,0:T(8,128)(2,1)S(1)}, bf16[256,2048]{1,0:T(8,128)(2,1)}, u32[]{:S(2)}, u32[]{:S(2)}) collective-permute-start(bf16[256,2048]{1,0:T(8,128)(2,1)S(1)} %constant_dynamic-update-slice_fusion.refs_14_), channel_id=1, source_target_pairs={{0,2},{2,0},{1,3},{3,1},{4,6},{6,4},{5,7},{7,5},{8,10},{10,8},{9,1... | collective-permute-start | bytes 3145736 | tf_op jit(solution)/shard_map/ppermute | solution.py:267
  (15 other events, 135.4 us)

commit v15 on v14

--- a/solution.py
+++ b/solution.py
@@ -144,40 +144,47 @@
     return block.reshape(block.shape[0], heads_dev, HEAD_DIM)
 
 
-def project_blocks(normed, starts, blocks, group=4):
-    n = len(blocks)
-    rows, cols = blocks[0].shape
+def project_blocks(normed, starts, blocks, chunk, group=4):
+    row_counts = [b.shape[0] for b in blocks]
+    total = sum(row_counts)
+    n = total // chunk
+    cols = blocks[0].shape[1]
     tokens = normed.shape[0]
+    firsts = [sum(row_counts[:i]) for i in range(len(blocks))]
 
     def kernel(starts_ref, normed_ref, *refs):
-        block_refs = refs[:n]
-        out_ref, features, weights, sems, acc = refs[n:]
-        copies = []
+        block_refs = refs[: len(blocks)]
+        out_ref, features, weights, sems, acc = refs[len(blocks):]
+        feature_copies = []
         for i in range(n):
-            start = pl.multiple_of(starts_ref[i], rows)
-            copies.append(
-                (
-                    pltpu.make_async_copy(
-                        normed_ref.at[:, pl.ds(start, rows)],
-                        features.at[:, pl.ds(i * rows, rows)],
-                        sems.at[0, i],
-                    ),
-                    pltpu.make_async_copy(
-                        block_refs[i], weights.at[pl.ds(i * rows, rows), :], sems.at[1, i]
-                    ),
+            start = pl.multiple_of(starts_ref[i], chunk)
+            feature_copies.append(
+                pltpu.make_async_copy(
+                    normed_ref.at[:, pl.ds(start, chunk)],
+                    features.at[:, pl.ds(i * chunk, chunk)],
+                    sems.at[0, i],
                 )
             )
-        for pair in copies:
-            for c in pair:
-                c.start()
+        weight_copies = [
+            pltpu.make_async_copy(
+                block_refs[b], weights.at[pl.ds(firsts[b], row_counts[b]), :], sems.at[1, b]
+            )
+            for b in range(len(blocks))
+        ]
+        for c in feature_copies + weight_copies:
+            c.start()
+        waited = set()
         for g in range(0, n, group):
             last = min(g + group, n)
             for i in range(g, last):
-                for c in copies[i]:
-                    c.wait()
+                feature_copies[i].wait()
+                b = max(k for k in range(len(blocks)) if firsts[k] <= i * chunk)
+                if b not in waited:
+                    weight_copies[b].wait()
+                    waited.add(b)
             part = jnp.dot(
-                features[:, g * rows:last * rows],
-                weights[g * rows:last * rows, :],
+                features[:, g * chunk:last * chunk],
+                weights[g * chunk:last * chunk, :],
                 preferred_element_type=jnp.float32,
             )
             if g == 0:
@@ -190,12 +197,12 @@
         kernel,
         out_shape=jax.ShapeDtypeStruct((tokens, cols), jnp.bfloat16),
         in_specs=[pl.BlockSpec(memory_space=pltpu.SMEM), pl.BlockSpec(memory_space=pl.ANY)]
-        + [pl.BlockSpec(memory_space=pl.ANY)] * n,
+        + [pl.BlockSpec(memory_space=pl.ANY)] * len(blocks),
         out_specs=pl.BlockSpec(memory_space=pltpu.VMEM),
         scratch_shapes=[
-            pltpu.VMEM((tokens, n * rows), normed.dtype),
-            pltpu.VMEM((n * rows, cols), blocks[0].dtype),
-            pltpu.SemaphoreType.DMA((2, n)),
+            pltpu.VMEM((tokens, total), normed.dtype),
+            pltpu.VMEM((total, cols), blocks[0].dtype),
+            pltpu.SemaphoreType.DMA((2, max(n, len(blocks)))),
             pltpu.VMEM((tokens, cols), jnp.float32),
         ],
     )(starts, normed, *blocks)
@@ -235,6 +242,9 @@
     place = lax.axis_index("head")
     n_steps = n_chip // 2
     barrier = lax.optimization_barrier
+    weight_rows, weight_cols = out_weight.shape
+    gathered_half = lax.all_gather(out_weight[:, : weight_cols // 2], "chip", axis=0, tiled=True)
+    out_weight = out_weight[:, weight_cols // 2:]
     key_block, value_block = head_blocks([keys, values], n_head, place)
     ahead, behind = ring_step(out_weight, out_weight, order)
     ahead, behind, key_block, value_block = barrier((ahead, behind, key_block, value_block))
@@ -272,8 +282,16 @@
     ring_place = jnp.asarray([order.index(j) for j in range(n_chip)], jnp.int32)[lax.axis_index("chip")]
     sources = jnp.asarray(order, jnp.int32)[(ring_place - jnp.asarray(offsets, jnp.int32)) % n_chip]
     cores = jnp.stack([core, 1 - core]).astype(jnp.int32)
-    starts = ((sources[:, None] * 2 + cores[None, :]) * out_weight.shape[0]).reshape(-1)
-    return project_blocks(gathered, starts, [w for pair in zip(got, swapped) for w in pair])
+    starts = ((sources[:, None] * 2 + cores[None, :]) * weight_rows).reshape(-1)
+    ring_part = project_blocks(
+        gathered, starts, [w for pair in zip(got, swapped) for w in pair], weight_rows
+    )
+    gathered_half, gathered = barrier((gathered_half, gathered))
+    partner_half = lax.ppermute(gathered_half, "core", SWAP)
+    chips = jnp.arange(n_chip, dtype=jnp.int32)
+    half_starts = jnp.concatenate([(chips * 2 + core) * weight_rows, (chips * 2 + 1 - core) * weight_rows])
+    gather_part = project_blocks(gathered, half_starts, [gathered_half, partner_half], weight_rows)
+    return jnp.concatenate([gather_part, ring_part], axis=1)
 
 
 def solution(mesh):

time: 175 us -> 232 us (1.33)
  waiting for transfers between devices: 100 us -> 128 us
  between operations: 0.33 us -> 13.8 us
  other arithmetic: 11.4 us -> 17.9 us
  starting transfers between devices: 29.1 us -> 35.5 us
  Pallas kernels: 9.62 us -> 14 us
    ppermute x1, waiting for transfers between devices: 0.01 us -> 23.4 us  [gather_head(): other = lax.ppermute(normed, 'head', SWAP)]
    ppermute x3, waiting for transfers between devices: 38.6 us -> 60 us  [exclusive_prefix(): total = total + lax.ppermute(total, axis, pairs)]
    ppermute x1, waiting for transfers between devices: 7.32 us -> 1.51 us  [ring_step(): lax.ppermute(ahead[:half_rows], 'chip', forward)]
    ppermute x3, waiting for transfers between devices: 25.9 us -> 20.4 us  [ring_step(): lax.ppermute(ahead, 'chip', forward)]
    ppermute x3, starting transfers between devices: 8.54 us -> 13.3 us  [exclusive_prefix(): total = total + lax.ppermute(total, axis, pairs)]
    pallas_call x1 -> x2, Pallas kernels: 9.62 us -> 14 us  [project_blocks(): pl.pallas_call(kernel, out_shape=jax.ShapeDtypeStruct((tokens, cols), jnp...]
    ppermute x3, waiting for transfers between devices: 6.66 us -> 2.56 us  [ring_step(): lax.ppermute(behind, 'chip', backward)]
    ppermute x3, waiting for transfers between devices: 18 us -> 14.4 us  [head_blocks(): other = lax.ppermute(tuple(sent), 'head', SWAP)]
  transfers between devices with their start and end apart: 25 -> 27, of which waited for: 14 -> 15; matrix products, arithmetic and copies ran while one was open for 17% -> 14% of each run, Pallas kernels for 0% -> 3%
where the time goes in v15:
time: 232 us; the launch traced here: 230 us
  waiting for transfers between devices  128 us (55%)
  starting transfers between devices  35.5 us (15%)
  other arithmetic  17.9 us (8%)
  local copies, waits for them, and re-layouts  15.7 us (7%)
  Pallas kernels  14 us (6%)
  between operations  13.8 us (6%)
  matrix products  5.15 us (2%)
    ppermute x3, waiting for transfers between devices, exclusive_prefix(): total = total + lax.ppermute(total, axis, pairs)  60 us
    ppermute x1, waiting for transfers between devices, gather_head(): other = lax.ppermute(normed, 'head', SWAP)  23.4 us
    ppermute x3, waiting for transfers between devices, ring_step(): lax.ppermute(ahead, 'chip', forward)  20.4 us
    ppermute x3, waiting for transfers between devices, head_blocks(): other = lax.ppermute(tuple(sent), 'head', SWAP)  14.4 us
    pallas_call x2, Pallas kernels, project_blocks(): pl.pallas_call(kernel, out_shape=jax.ShapeDtypeStruct((tokens, cols), jnp...  14 us
    ppermute x3, starting transfers between devices, exclusive_prefix(): total = total + lax.ppermute(total, axis, pairs)  13.3 us
    unnamed x41, local copies, waits for them, and re-layouts  5.88 us
    ppermute x3, starting transfers between devices, local_ring(): swapped += [lax.ppermute(w, 'core', SWAP) for w in got[len(swapped):]]  5.78 us
  transfers between devices with their start and end apart: 27, of which 15 were waited for; matrix products, arithmetic and copies ran while one was open for 14% of the time, Pallas kernels for 3%

profile of v15, /device:TPU:13, one launch (start us, length us, event | category | flops | bytes accessed | tf_op | source)
XLA Modules:
  0.0 230.1 jit_solution(16486881060033099378)
XLA Ops:
  10.1 2.2 constant_dynamic-slice_fusion.1
  13.5 2.1 fusion.11
  17.7 4.3 %collective-permute-done.2 = bf16[128,2048]{0,1:T(8,128)(2,1)} collective-permute-done((bf16[128,2048]{0,1:T(8,128)(2,1)}, bf16[128,2048]{0,1:T(8,128)(2,1)}, u32[]{:S(2)}, u32[]{:S(2)}) %collective-permute-start.2) | collective-permute-done | bytes 524320 | tf_op jit(solution)/shard_map/ppermute | solution.py:36
  23.1 10.1 %collective-permute-done.3 = bf16[128,2048]{0,1:T(8,128)(2,1)} collective-permute-done((bf16[128,2048]{0,1:T(8,128)(2,1)}, bf16[128,2048]{0,1:T(8,128)(2,1)}, u32[]{:S(2)}, u32[]{:S(2)}) %collective-permute-start.3) | collective-permute-done | bytes 524320 | tf_op jit(solution)/shard_map/ppermute | solution.py:36
  37.6 2.4 %collective-permute-done.4 = f32[16,128,128]{2,1,0:T(8,128)} collective-permute-done((f32[16,128,128]{2,1,0:T(8,128)S(1)}, f32[16,128,128]{2,1,0:T(8,128)}, u32[]{:S(2)}, u32[]{:S(2)}) %collective-permute-start.4) | collective-permute-done | bytes 1048608 | tf_op jit(solution)/shard_map/ppermute | solution.py:130
  41.2 3.1 %collective-permute-start.5 = (f32[8,128,128]{2,1,0:T(8,128)S(1)}, f32[8,128,128]{2,1,0:T(8,128)S(1)}, u32[]{:S(2)}, u32[]{:S(2)}) collective-permute-start(f32[8,128,128]{2,1,0:T(8,128)S(1)} %dynamic-slice_add_fusion), channel_id=1, source_target_pairs={{0,4},{4,8},{8,12},{12,16},{16,20},{20,24},{24,28},{1,5},{5,9},{9,... | collective-permute-start | bytes 1572872 | tf_op jit(solution)/shard_map/ppermute | solution.py:20
  44.3 2.0 copy.33
  48.5 13.3 %collective-permute-done.5 = f32[8,128,128]{2,1,0:T(8,128)S(1)} collective-permute-done((f32[8,128,128]{2,1,0:T(8,128)S(1)}, f32[8,128,128]{2,1,0:T(8,128)S(1)}, u32[]{:S(2)}, u32[]{:S(2)}) %collective-permute-start.5) | collective-permute-done | bytes 524320 | tf_op jit(solution)/shard_map/ppermute | solution.py:20
  61.8 2.7 %collective-permute-start.6 = (f32[8,128,128]{2,1,0:T(8,128)S(1)}, f32[8,128,128]{2,1,0:T(8,128)}, u32[]{:S(2)}, u32[]{:S(2)}) collective-permute-start(f32[8,128,128]{2,1,0:T(8,128)S(1)} %add.85), channel_id=1, source_target_pairs={{0,8},{4,12},{8,16},{12,20},{16,24},{20,28},{1,9},{5,13},{9,17},{1... | collective-permute-start | bytes 1572872 | tf_op jit(solution)/shard_map/ppermute | solution.py:20
  67.9 28.8 %collective-permute-done.6 = f32[8,128,128]{2,1,0:T(8,128)} collective-permute-done((f32[8,128,128]{2,1,0:T(8,128)S(1)}, f32[8,128,128]{2,1,0:T(8,128)}, u32[]{:S(2)}, u32[]{:S(2)}) %collective-permute-start.6) | collective-permute-done | bytes 524320 | tf_op jit(solution)/shard_map/ppermute | solution.py:20
  96.6 1.9 add.86
  98.6 7.4 %collective-permute-start.7 = (f32[8,128,128]{2,1,0:T(8,128)}, f32[8,128,128]{2,1,0:T(8,128)}, u32[]{:S(2)}, u32[]{:S(2)}) collective-permute-start(f32[8,128,128]{2,1,0:T(8,128)} %add.86), channel_id=1, source_target_pairs={{0,16},{4,20},{8,24},{12,28},{1,17},{5,21},{9,25},{13,29},{2,18},{... | collective-permute-start | bytes 1572872 | tf_op jit(solution)/shard_map/ppermute | solution.py:20
  107.1 2.9 %fusion.1 = f32[256,16,128]{0,2,1:T(8,128)S(1)} fusion(bf16[256,16,128]{0,2,1:T(8,128)(2,1)} %bitcast.25, bf16[256,16,128]{0,2,1:T(8,128)(2,1)} %bitcast.26, bf16[256,16,128]{0,2,1:T(8,128)(2,1)S(1)} %bitcast.23, pred[256,256]{1,0:T(8,128)(4,1)S(1)} %iota_compare_fusion), kind=kOutput, calls=%fused_computation.7 | convolution fusion | flops 538968064 | bytes 5308416 | tf_op jit(solution)/shard_map/hts,she->the/dot_general | solution.py:103
  110.0 17.9 %collective-permute-done.7 = f32[8,128,128]{2,1,0:T(8,128)} collective-permute-done((f32[8,128,128]{2,1,0:T(8,128)}, f32[8,128,128]{2,1,0:T(8,128)}, u32[]{:S(2)}, u32[]{:S(2)}) %collective-permute-start.7) | collective-permute-done | bytes 524320 | tf_op jit(solution)/shard_map/ppermute | solution.py:20
  128.0 2.2 add_subtract_fusion
  140.3 23.4 %collective-permute-done.13 = bf16[256,2048]{1,0:T(8,128)(2,1)S(1)} collective-permute-done((bf16[256,2048]{1,0:T(8,128)(2,1)S(1)}, bf16[256,2048]{1,0:T(8,128)(2,1)S(1)}, u32[]{:S(2)}, u32[]{:S(2)}) %collective-permute-start.13) | collective-permute-done | bytes 1048608 | tf_op jit(solution)/shard_map/ppermute | solution.py:124
  167.3 12.1 %collective-permute-done.15.refs_6_ = bf16[256,1024]{1,0:T(8,128)(2,1)S(1)} collective-permute-done((bf16[256,1024]{1,0:T(8,128)(2,1)}, bf16[256,1024]{1,0:T(8,128)(2,1)S(1)}, u32[]{:S(2)}, u32[]{:S(2)}) %collective-permute-start.15) | collective-permute-done | bytes 524320 | tf_op jit(solution)/shard_map/ppermute | solution.py:82
  183.7 8.2 %collective-permute-done.16.refs_10_ = bf16[256,1024]{1,0:T(8,128)(2,1)S(1)} collective-permute-done((bf16[256,1024]{1,0:T(8,128)(2,1)S(1)}, bf16[256,1024]{1,0:T(8,128)(2,1)S(1)}, u32[]{:S(2)}, u32[]{:S(2)}) %collective-permute-start.16) | collective-permute-done | bytes 524320 | tf_op jit(solution)/shard_map/ppermute | solution.py:82
  191.9 1.9 collective-permute-done.18.refs_12_
  196.8 2.4 %collective-permute-start.21 = (bf16[256,1024]{1,0:T(8,128)(2,1)S(1)}, bf16[256,1024]{1,0:T(8,128)(2,1)}, u32[]{:S(2)}, u32[]{:S(2)}) collective-permute-start(bf16[256,1024]{1,0:T(8,128)(2,1)S(1)} %collective-permute-done.16.refs_10_), channel_id=1, source_target_pairs={{0,2},{2,0},{1,3},{3,1},{4,6},{6,4},{5,7},{7,5},{8,10},{10,8},{9,1... | collective-permute-start | bytes 1572872 | tf_op jit(solution)/shard_map/ppermute | solution.py:277
  202.1 3.4 %collective-permute-start.25 = (bf16[256,1024]{1,0:T(8,128)(2,1)S(1)}, bf16[256,1024]{1,0:T(8,128)(2,1)}, u32[]{:S(2)}, u32[]{:S(2)}) collective-permute-start(bf16[256,1024]{1,0:T(8,128)(2,1)S(1)} %constant_dynamic-update-slice_fusion.refs_14_), channel_id=1, source_target_pairs={{0,2},{2,0},{1,3},{3,1},{4,6},{6,4},{5,7},{7,5},{8,10},{10,8},{9,1... | collective-permute-start | bytes 1572872 | tf_op jit(solution)/shard_map/ppermute | solution.py:277
  207.1 6.6 %shard_map.83 = bf16[256,1024]{1,0:T(8,128)(2,1)} custom-call(s32[16]{0:T(128)} %mul.75.starts_ref, bf16[256,4096]{1,0:T(8,128)(2,1)} %pad_maximum_fusion.normed_ref, bf16[256,1024]{1,0:T(8,128)(2,1)} %copy-done.4, bf16[256,1024]{1,0:T(8,128)(2,1)} %collective-permute-done.9.refs_1_, bf16[256,1024]{1,0:T(8,128)(2,1)} %collective-permute-done.refs_2_, ...), custom_call_target="tpu_custom_call" | custom-call | tf_op jit(solution)/shard_map/pallas_call | solution.py:196
  213.8 7.4 %shard_map.82 = bf16[256,1024]{1,0:T(8,128)(2,1)} custom-call(s32[16]{0:T(128)} %pad_add_fusion.starts_ref, bf16[256,4096]{1,0:T(8,128)(2,1)} %pad_maximum_fusion.normed_ref, bf16[2048,1024]{1,0:T(8,128)(2,1)} %all-gather.2.cloned.1.call-done.refs_0_, bf16[2048,1024]{1,0:T(8,128)(2,1)} %collective-permute-done.14.refs_1_), custom_call_target="tpu_custom_call" | custom-call | tf_op jit(solution)/shard_map/pallas_call | solution.py:196
  221.2 2.1 pad_maximum_fusion.4
  (111 shorter events, 45.3 us)
Async XLA Ops:
  6.5 158.9 %all-gather.2.cloned.1.call-start = ((), (), s32[]{:S(2)}) async-start(), calls=%async_computation | async-start | bytes 4718592 | tf_op jit(solution)/shard_map/all_gather | solution.py:246
  8.9 13.1 %collective-permute-start.2 = (bf16[128,2048]{0,1:T(8,128)(2,1)}, bf16[128,2048]{0,1:T(8,128)(2,1)}, u32[]{:S(2)}, u32[]{:S(2)}) collective-permute-start(bf16[128,2048]{0,1:T(8,128)(2,1)} %copy.29), channel_id=1, source_target_pairs={{0,1},{1,0},{2,3},{3,2},{4,5},{5,4},{6,7},{7,6},{8,9},{9,8},{10,11... | collective-permute-start | bytes 1572872 | tf_op jit(solution)/shard_map/ppermute | solution.py:36
  13.3 19.9 %collective-permute-start.3 = (bf16[128,2048]{0,1:T(8,128)(2,1)}, bf16[128,2048]{0,1:T(8,128)(2,1)}, u32[]{:S(2)}, u32[]{:S(2)}) collective-permute-start(bf16[128,2048]{0,1:T(8,128)(2,1)} %copy.31), channel_id=1, source_target_pairs={{0,1},{1,0},{2,3},{3,2},{4,5},{5,4},{6,7},{7,6},{8,9},{9,8},{10,11... | collective-permute-start | bytes 1572872 | tf_op jit(solution)/shard_map/ppermute | solution.py:36
  15.6 19.0 %collective-permute-start = (bf16[256,1024]{1,0:T(8,128)(2,1)S(1)}, bf16[256,1024]{1,0:T(8,128)(2,1)}, u32[]{:S(2)}, u32[]{:S(2)}) collective-permute-start(bf16[256,1024]{1,0:T(8,128)(2,1)S(1)} %get-tuple-element.44.refs_0_), channel_id=1, source_target_pairs={{0,4},{4,12},{12,20},{20,28},{28,24},{24,16},{16,8},{8,0},{1,5},{5... | collective-permute-start | bytes 1572872 | tf_op jit(solution)/shard_map/ppermute | solution.py:82
  16.9 17.7 %collective-permute-start.1 = (bf16[256,1024]{1,0:T(8,128)(2,1)S(1)}, bf16[256,1024]{1,0:T(8,128)(2,1)}, u32[]{:S(2)}, u32[]{:S(2)}) collective-permute-start(bf16[256,1024]{1,0:T(8,128)(2,1)S(1)} %get-tuple-element.44.refs_0_), channel_id=1, source_target_pairs={{4,0},{12,4},{20,12},{28,20},{24,28},{16,24},{8,16},{0,8},{5,1},{1... | collective-permute-start | bytes 1572872 | tf_op jit(solution)/shard_map/ppermute | solution.py:82
  41.2 20.6 %collective-permute-start.5 = (f32[8,128,128]{2,1,0:T(8,128)S(1)}, f32[8,128,128]{2,1,0:T(8,128)S(1)}, u32[]{:S(2)}, u32[]{:S(2)}) collective-permute-start(f32[8,128,128]{2,1,0:T(8,128)S(1)} %dynamic-slice_add_fusion), channel_id=1, source_target_pairs={{0,4},{4,8},{8,12},{12,16},{16,20},{20,24},{24,28},{1,5},{5,9},{9,... | collective-permute-start | bytes 1572872 | tf_op jit(solution)/shard_map/ppermute | solution.py:20
  46.4 20.4 %collective-permute-start.8 = (bf16[128,2048]{0,1:T(8,128)(2,1)}, bf16[128,2048]{0,1:T(8,128)(2,1)}, u32[]{:S(2)}, u32[]{:S(2)}) collective-permute-start(bf16[128,2048]{0,1:T(8,128)(2,1)} %copy.33), channel_id=1, source_target_pairs={{0,1},{1,0},{2,3},{3,2},{4,5},{5,4},{6,7},{7,6},{8,9},{9,8},{10,11... | collective-permute-start | bytes 1572872 | tf_op jit(solution)/shard_map/ppermute | solution.py:36
  47.6 82.6 %collective-permute-start.9 = (bf16[256,1024]{1,0:T(8,128)(2,1)}, bf16[256,1024]{1,0:T(8,128)(2,1)}, u32[]{:S(2)}, u32[]{:S(2)}) collective-permute-start(bf16[256,1024]{1,0:T(8,128)(2,1)} %copy-done.4), channel_id=1, source_target_pairs={{0,2},{2,0},{1,3},{3,1},{4,6},{6,4},{5,7},{7,5},{8,10},{10,8},{9,1... | collective-permute-start | bytes 1572872 | tf_op jit(solution)/shard_map/ppermute | solution.py:254
  61.8 34.8 %collective-permute-start.6 = (f32[8,128,128]{2,1,0:T(8,128)S(1)}, f32[8,128,128]{2,1,0:T(8,128)}, u32[]{:S(2)}, u32[]{:S(2)}) collective-permute-start(f32[8,128,128]{2,1,0:T(8,128)S(1)} %add.85), channel_id=1, source_target_pairs={{0,8},{4,12},{8,16},{12,20},{16,24},{20,28},{1,9},{5,13},{9,17},{1... | collective-permute-start | bytes 1572872 | tf_op jit(solution)/shard_map/ppermute | solution.py:20
  64.9 65.3 %collective-permute-start.10 = (bf16[256,1024]{1,0:T(8,128)(2,1)}, bf16[256,1024]{1,0:T(8,128)(2,1)}, u32[]{:S(2)}, u32[]{:S(2)}) collective-permute-start(bf16[256,1024]{1,0:T(8,128)(2,1)} %collective-permute-done.refs_2_), channel_id=1, source_target_pairs={{0,2},{2,0},{1,3},{3,1},{4,6},{6,4},{5,7},{7,5},{8,10},{10,8},{9,1... | collective-permute-start | bytes 1572872 | tf_op jit(solution)/shard_map/ppermute | solution.py:254
  66.6 63.6 %collective-permute-start.11 = (bf16[256,1024]{1,0:T(8,128)(2,1)}, bf16[256,1024]{1,0:T(8,128)(2,1)}, u32[]{:S(2)}, u32[]{:S(2)}) collective-permute-start(bf16[256,1024]{1,0:T(8,128)(2,1)} %collective-permute-done.1.refs_4_), channel_id=1, source_target_pairs={{0,2},{2,0},{1,3},{3,1},{4,6},{6,4},{5,7},{7,5},{8,10},{10,8},{9,1... | collective-permute-start | bytes 1572872 | tf_op jit(solution)/shard_map/ppermute | solution.py:254
  98.6 29.4 %collective-permute-start.7 = (f32[8,128,128]{2,1,0:T(8,128)}, f32[8,128,128]{2,1,0:T(8,128)}, u32[]{:S(2)}, u32[]{:S(2)}) collective-permute-start(f32[8,128,128]{2,1,0:T(8,128)} %add.86), channel_id=1, source_target_pairs={{0,16},{4,20},{8,24},{12,28},{1,17},{5,21},{9,25},{13,29},{2,18},{... | collective-permute-start | bytes 1572872 | tf_op jit(solution)/shard_map/ppermute | solution.py:20
  139.1 24.6 %collective-permute-start.13 = (bf16[256,2048]{1,0:T(8,128)(2,1)S(1)}, bf16[256,2048]{1,0:T(8,128)(2,1)S(1)}, u32[]{:S(2)}, u32[]{:S(2)}) collective-permute-start(bf16[256,2048]{1,0:T(8,128)(2,1)S(1)} %copy.27), channel_id=1, source_target_pairs={{0,1},{1,0},{2,3},{3,2},{4,5},{5,4},{6,7},{7,6},{8,9},{9,8},{10,11... | collective-permute-start | bytes 3145736 | tf_op jit(solution)/shard_map/ppermute | solution.py:124
  165.4 48.3 %collective-permute-start.14 = (bf16[2048,1024]{1,0:T(8,128)(2,1)}, bf16[2048,1024]{1,0:T(8,128)(2,1)}, u32[]{:S(2)}, u32[]{:S(2)}) collective-permute-start(bf16[2048,1024]{1,0:T(8,128)(2,1)} %all-gather.2.cloned.1.call-done.refs_0_), channel_id=1, source_target_pairs={{0,2},{2,0},{1,3},{3,1},{4,6},{6,4},{5,7},{7,5},{8,10},{10,8},{9,1... | collective-permute-start | bytes 12582920 | tf_op jit(solution)/shard_map/ppermute | solution.py:290
  165.8 13.6 %collective-permute-start.15 = (bf16[256,1024]{1,0:T(8,128)(2,1)}, bf16[256,1024]{1,0:T(8,128)(2,1)S(1)}, u32[]{:S(2)}, u32[]{:S(2)}) collective-permute-start(bf16[256,1024]{1,0:T(8,128)(2,1)} %collective-permute-done.refs_2_), channel_id=1, source_target_pairs={{0,4},{4,12},{12,20},{20,28},{28,24},{24,16},{16,8},{8,0},{1,5},{5... | collective-permute-start | bytes 1572872 | tf_op jit(solution)/shard_map/ppermute | solution.py:82
  165.8 15.5 %collective-permute-start.17 = (bf16[256,1024]{1,0:T(8,128)(2,1)}, bf16[256,1024]{1,0:T(8,128)(2,1)S(1)}, u32[]{:S(2)}, u32[]{:S(2)}) collective-permute-start(bf16[256,1024]{1,0:T(8,128)(2,1)} %collective-permute-done.1.refs_4_), channel_id=1, source_target_pairs={{4,0},{12,4},{20,12},{28,20},{24,28},{16,24},{8,16},{0,8},{5,1},{1... | collective-permute-start | bytes 1572872 | tf_op jit(solution)/shard_map/ppermute | solution.py:82
  179.4 12.5 %collective-permute-start.16 = (bf16[256,1024]{1,0:T(8,128)(2,1)S(1)}, bf16[256,1024]{1,0:T(8,128)(2,1)S(1)}, u32[]{:S(2)}, u32[]{:S(2)}) collective-permute-start(bf16[256,1024]{1,0:T(8,128)(2,1)S(1)} %collective-permute-done.15.refs_6_), channel_id=1, source_target_pairs={{0,4},{4,12},{12,20},{20,28},{28,24},{24,16},{16,8},{8,0},{1,5},{5... | collective-permute-start | bytes 1572872 | tf_op jit(solution)/shard_map/ppermute | solution.py:82
  181.3 12.5 %collective-permute-start.18 = (bf16[256,1024]{1,0:T(8,128)(2,1)S(1)}, bf16[256,1024]{1,0:T(8,128)(2,1)S(1)}, u32[]{:S(2)}, u32[]{:S(2)}) collective-permute-start(bf16[256,1024]{1,0:T(8,128)(2,1)S(1)} %collective-permute-done.17.refs_8_), channel_id=1, source_target_pairs={{4,0},{12,4},{20,12},{28,20},{24,28},{16,24},{8,16},{0,8},{5,1},{1... | collective-permute-start | bytes 1572872 | tf_op jit(solution)/shard_map/ppermute | solution.py:82
  181.3 12.5 %collective-permute-start.19 = (bf16[256,1024]{1,0:T(8,128)(2,1)S(1)}, bf16[256,1024]{1,0:T(8,128)(2,1)S(1)}, u32[]{:S(2)}, u32[]{:S(2)}) collective-permute-start(bf16[256,1024]{1,0:T(8,128)(2,1)S(1)} %collective-permute-done.15.refs_6_), channel_id=1, source_target_pairs={{0,2},{2,0},{1,3},{3,1},{4,6},{6,4},{5,7},{7,5},{8,10},{10,8},{9,1... | collective-permute-start | bytes 1572872 | tf_op jit(solution)/shard_map/ppermute | solution.py:268
  182.4 11.4 %collective-permute-start.20 = (bf16[256,1024]{1,0:T(8,128)(2,1)S(1)}, bf16[256,1024]{1,0:T(8,128)(2,1)S(1)}, u32[]{:S(2)}, u32[]{:S(2)}) collective-permute-start(bf16[256,1024]{1,0:T(8,128)(2,1)S(1)} %collective-permute-done.17.refs_8_), channel_id=1, source_target_pairs={{0,2},{2,0},{1,3},{3,1},{4,6},{6,4},{5,7},{7,5},{8,10},{10,8},{9,1... | collective-permute-start | bytes 1572872 | tf_op jit(solution)/shard_map/ppermute | solution.py:268
  194.6 6.1 %collective-permute-start.23 = (bf16[128,1024]{1,0:T(8,128)(2,1)}, bf16[128,1024]{1,0:T(8,128)(2,1)S(1)}, u32[]{:S(2)}, u32[]{:S(2)}) collective-permute-start(bf16[128,1024]{1,0:T(8,128)(2,1)} %slice.14), channel_id=1, source_target_pairs={{0,4},{4,12},{12,20},{20,28},{28,24},{24,16},{16,8},{8,0},{1,5},{5... | collective-permute-start | bytes 786440 | tf_op jit(solution)/shard_map/ppermute | solution.py:79
  196.5 5.6 %collective-permute-start.24 = (bf16[128,1024]{1,0:T(8,128)(2,1)S(1)}, bf16[128,1024]{1,0:T(8,128)(2,1)S(1)}, u32[]{:S(2)}, u32[]{:S(2)}) collective-permute-start(bf16[128,1024]{1,0:T(8,128)(2,1)S(1)} %slice.15), channel_id=1, source_target_pairs={{4,0},{12,4},{20,12},{28,20},{24,28},{16,24},{8,16},{0,8},{5,1},{1... | collective-permute-start | bytes 786440 | tf_op jit(solution)/shard_map/ppermute | solution.py:79
  196.8 10.0 %collective-permute-start.21 = (bf16[256,1024]{1,0:T(8,128)(2,1)S(1)}, bf16[256,1024]{1,0:T(8,128)(2,1)}, u32[]{:S(2)}, u32[]{:S(2)}) collective-permute-start(bf16[256,1024]{1,0:T(8,128)(2,1)S(1)} %collective-permute-done.16.refs_10_), channel_id=1, source_target_pairs={{0,2},{2,0},{1,3},{3,1},{4,6},{6,4},{5,7},{7,5},{8,10},{10,8},{9,1... | collective-permute-start | bytes 1572872 | tf_op jit(solution)/shard_map/ppermute | solution.py:277
  199.2 7.6 %collective-permute-start.22 = (bf16[256,1024]{1,0:T(8,128)(2,1)S(1)}, bf16[256,1024]{1,0:T(8,128)(2,1)}, u32[]{:S(2)}, u32[]{:S(2)}) collective-permute-start(bf16[256,1024]{1,0:T(8,128)(2,1)S(1)} %collective-permute-done.18.refs_12_), channel_id=1, source_target_pairs={{0,2},{2,0},{1,3},{3,1},{4,6},{6,4},{5,7},{7,5},{8,10},{10,8},{9,1... | collective-permute-start | bytes 1572872 | tf_op jit(solution)/shard_map/ppermute | solution.py:277
  (20 other events, 259.5 us)
Sparse Core Ops, SparseCore 0:
  17.2 86.3 all-gather.1

commit v16 on v14

--- a/solution.py
+++ b/solution.py
@@ -267,6 +267,7 @@
     swapped += [lax.ppermute(w, "core", SWAP) for w in got[len(swapped):]]
     prefix = chip_finish(chip_prefix_half, partner_state, core)
     normed = normalize(query_heads, prefix, within_block, norm_gain)
+    normed, held = barrier((normed, got[-1] if n_steps < 4 else got[-3]))
     gathered = gather_head(normed, n_head, place)
     row_count = gathered.shape[0]
     ring_place = jnp.asarray([order.index(j) for j in range(n_chip)], jnp.int32)[lax.axis_index("chip")]

time: 175 us -> 175 us (level)
    ppermute x3, waiting for transfers between devices: 6.66 us -> 4.01 us  [ring_step(): lax.ppermute(behind, 'chip', backward)]
where the time goes in v16:
time: 175 us; the launch traced here: 172 us
  waiting for transfers between devices  98.7 us (56%)
  starting transfers between devices  30.6 us (17%)
  local copies, waits for them, and re-layouts  17.3 us (10%)
  other arithmetic  11.4 us (7%)
  Pallas kernels  9.62 us (5%)
  matrix products  3.92 us (2%)
    ppermute x3, waiting for transfers between devices, exclusive_prefix(): total = total + lax.ppermute(total, axis, pairs)  38.6 us
    ppermute x3, waiting for transfers between devices, ring_step(): lax.ppermute(ahead, 'chip', forward)  27.6 us
    ppermute x3, waiting for transfers between devices, head_blocks(): other = lax.ppermute(tuple(sent), 'head', SWAP)  18 us
    pallas_call x1, Pallas kernels, project_blocks(): pl.pallas_call(kernel, out_shape=jax.ShapeDtypeStruct((tokens, cols), jnp...  9.62 us
    ppermute x3, starting transfers between devices, exclusive_prefix(): total = total + lax.ppermute(total, axis, pairs)  8.54 us
    ppermute x1, waiting for transfers between devices, ring_step(): lax.ppermute(ahead[:half_rows], 'chip', forward)  7.32 us
    unnamed x35, local copies, waits for them, and re-layouts  6.16 us
    ppermute x3, waiting for transfers between devices, ring_step(): lax.ppermute(behind, 'chip', backward)  4.01 us
  transfers between devices with their start and end apart: 25, of which 14 were waited for; matrix products, arithmetic and copies ran while one was open for 17% of the time, Pallas kernels for 0%

profile of v16, /device:TPU:13, one launch (start us, length us, event | category | flops | bytes accessed | tf_op | source)
XLA Modules:
  0.0 171.8 jit_solution(11095014658018326224)
XLA Ops:
  5.0 2.3 %constant_dynamic-slice_fusion.1 = (bf16[128,2048]{1,0:T(8,128)(2,1)}, bf16[128,2048]{1,0:T(8,128)(2,1)}, bf16[128,2048]{1,0:T(8,128)(2,1)S(1)}, bf16[128,2048]{1,0:T(8,128)(2,1)S(1)}) fusion(bf16[128,4096]{1,0:T(8,128)(2,1)S(1)} %copy-done.9, s32[]{:T(128)S(6)} %select_n.96, s32[]{:T(128)S(6)} %select_n.97, bf16[128,4096]{1,0:T(8,128)(2,1)} %param.10), kind=kLoop, calls=%fused_computation.38 | loop fusion | bytes 4194312 | tf_op jit(solution)/shard_map/dynamic_slice | solution.py:34
  8.5 6.9 %collective-permute-done.2 = bf16[128,2048]{0,1:T(8,128)(2,1)S(1)} collective-permute-done((bf16[128,2048]{0,1:T(8,128)(2,1)}, bf16[128,2048]{0,1:T(8,128)(2,1)S(1)}, u32[]{:S(2)}, u32[]{:S(2)}) %collective-permute-start.2) | collective-permute-done | bytes 524320 | tf_op jit(solution)/shard_map/ppermute | solution.py:36
  15.7 11.0 %collective-permute-done.3 = bf16[128,2048]{0,1:T(8,128)(2,1)S(1)} collective-permute-done((bf16[128,2048]{0,1:T(8,128)(2,1)S(1)}, bf16[128,2048]{0,1:T(8,128)(2,1)S(1)}, u32[]{:S(2)}, u32[]{:S(2)}) %collective-permute-start.3) | collective-permute-done | bytes 524320 | tf_op jit(solution)/shard_map/ppermute | solution.py:36
  29.0 2.2 %collective-permute-start.4 = (f32[16,128,128]{2,1,0:T(8,128)S(1)}, f32[16,128,128]{2,1,0:T(8,128)S(1)}, u32[]{:S(2)}, u32[]{:S(2)}) collective-permute-start(f32[16,128,128]{2,1,0:T(8,128)S(1)} %fusion.11), channel_id=1, source_target_pairs={{0,2},{2,0},{1,3},{3,1},{4,6},{6,4},{5,7},{7,5},{8,10},{10,8},{9,1... | collective-permute-start | bytes 3145736 | tf_op jit(solution)/shard_map/ppermute | solution.py:130
  31.3 2.3 %collective-permute-done.4 = f32[16,128,128]{2,1,0:T(8,128)S(1)} collective-permute-done((f32[16,128,128]{2,1,0:T(8,128)S(1)}, f32[16,128,128]{2,1,0:T(8,128)S(1)}, u32[]{:S(2)}, u32[]{:S(2)}) %collective-permute-start.4) | collective-permute-done | bytes 1048608 | tf_op jit(solution)/shard_map/ppermute | solution.py:130
  33.6 2.2 %collective-permute-start.5 = (f32[8,128,128]{2,1,0:T(8,128)S(1)}, f32[8,128,128]{2,1,0:T(8,128)S(1)}, u32[]{:S(2)}, u32[]{:S(2)}) collective-permute-start(f32[8,128,128]{2,1,0:T(8,128)S(1)} %dynamic-slice_add_fusion), channel_id=1, source_target_pairs={{0,4},{4,8},{8,12},{12,16},{16,20},{20,24},{24,28},{1,5},{5,9},{9,... | collective-permute-start | bytes 1572872 | tf_op jit(solution)/shard_map/ppermute | solution.py:20
  35.8 13.0 %collective-permute-done.5 = f32[8,128,128]{2,1,0:T(8,128)S(1)} collective-permute-done((f32[8,128,128]{2,1,0:T(8,128)S(1)}, f32[8,128,128]{2,1,0:T(8,128)S(1)}, u32[]{:S(2)}, u32[]{:S(2)}) %collective-permute-start.5) | collective-permute-done | bytes 524320 | tf_op jit(solution)/shard_map/ppermute | solution.py:20
  48.9 3.2 %collective-permute-start.6 = (f32[8,128,128]{2,1,0:T(8,128)S(1)}, f32[8,128,128]{2,1,0:T(8,128)}, u32[]{:S(2)}, u32[]{:S(2)}) collective-permute-start(f32[8,128,128]{2,1,0:T(8,128)S(1)} %add.79), channel_id=1, source_target_pairs={{0,8},{4,12},{8,16},{12,20},{16,24},{20,28},{1,9},{5,13},{9,17},{1... | collective-permute-start | bytes 1572872 | tf_op jit(solution)/shard_map/ppermute | solution.py:20
  52.1 2.1 %copy.33 = bf16[128,2048]{0,1:T(8,128)(2,1)} copy(bf16[128,2048]{1,0:T(8,128)(2,1)} %get-tuple-element.46) | data formatting | bytes 1048576
  57.0 6.0 %collective-permute-done.6 = f32[8,128,128]{2,1,0:T(8,128)} collective-permute-done((f32[8,128,128]{2,1,0:T(8,128)S(1)}, f32[8,128,128]{2,1,0:T(8,128)}, u32[]{:S(2)}, u32[]{:S(2)}) %collective-permute-start.6) | collective-permute-done | bytes 524320 | tf_op jit(solution)/shard_map/ppermute | solution.py:20
  64.2 3.2 %collective-permute-start.7 = (f32[8,128,128]{2,1,0:T(8,128)S(1)}, f32[8,128,128]{2,1,0:T(8,128)S(1)}, u32[]{:S(2)}, u32[]{:S(2)}) collective-permute-start(f32[8,128,128]{2,1,0:T(8,128)S(1)} %add.80), channel_id=1, source_target_pairs={{0,16},{4,20},{8,24},{12,28},{1,17},{5,21},{9,25},{13,29},{2,18},{... | collective-permute-start | bytes 1572872 | tf_op jit(solution)/shard_map/ppermute | solution.py:20
  69.6 19.6 %collective-permute-done.7 = f32[8,128,128]{2,1,0:T(8,128)S(1)} collective-permute-done((f32[8,128,128]{2,1,0:T(8,128)S(1)}, f32[8,128,128]{2,1,0:T(8,128)S(1)}, u32[]{:S(2)}, u32[]{:S(2)}) %collective-permute-start.7) | collective-permute-done | bytes 524320 | tf_op jit(solution)/shard_map/ppermute | solution.py:20
  90.0 2.9 %fusion.1 = f32[256,16,128]{0,2,1:T(8,128)S(1)} fusion(bf16[256,16,128]{0,2,1:T(8,128)(2,1)} %bitcast.25, bf16[256,16,128]{0,2,1:T(8,128)(2,1)} %bitcast.26, bf16[256,16,128]{0,2,1:T(8,128)(2,1)S(1)} %bitcast.23, pred[256,256]{1,0:T(8,128)(4,1)S(1)} %iota_compare_fusion), kind=kOutput, calls=%fused_computation.7 | convolution fusion | flops 538968064 | bytes 5308416 | tf_op jit(solution)/shard_map/hts,she->the/dot_general | solution.py:103
  93.0 2.3 %add_subtract_fusion = f32[8,128,128]{2,1,0:T(8,128)} fusion(f32[8,128,128]{2,1,0:T(8,128)} %copy-done.3, f32[8,128,128]{2,1,0:T(8,128)} %copy-done.8, f32[8,128,128]{2,1,0:T(8,128)} %copy-done.10), kind=kLoop, calls=%fused_computation.18 | loop fusion | flops 262144 | bytes 2097152 | tf_op jit(solution)/shard_map/sub | solution.py:22
  95.3 2.7 %collective-permute-start.12 = (f32[8,128,128]{2,1,0:T(8,128)}, f32[8,128,128]{2,1,0:T(8,128)}, u32[]{:S(2)}, u32[]{:S(2)}) collective-permute-start(f32[8,128,128]{2,1,0:T(8,128)} %add_subtract_fusion), channel_id=1, source_target_pairs={{0,2},{2,0},{1,3},{3,1},{4,6},{6,4},{5,7},{7,5},{8,10},{10,8},{9,1... | collective-permute-start | bytes 1572872 | tf_op jit(solution)/shard_map/ppermute | solution.py:138
  99.4 12.4 %collective-permute-done.13.refs_6_ = bf16[256,2048]{1,0:T(8,128)(2,1)} collective-permute-done((bf16[256,2048]{1,0:T(8,128)(2,1)}, bf16[256,2048]{1,0:T(8,128)(2,1)}, u32[]{:S(2)}, u32[]{:S(2)}) %collective-permute-start.13) | collective-permute-done | bytes 1048608 | tf_op jit(solution)/shard_map/ppermute | solution.py:82
  111.8 2.2 %collective-permute-start.14 = (bf16[256,2048]{1,0:T(8,128)(2,1)}, bf16[256,2048]{1,0:T(8,128)(2,1)}, u32[]{:S(2)}, u32[]{:S(2)}) collective-permute-start(bf16[256,2048]{1,0:T(8,128)(2,1)} %collective-permute-done.13.refs_6_), channel_id=1, source_target_pairs={{0,4},{4,12},{12,20},{20,28},{28,24},{24,16},{16,8},{8,0},{1,5},{5... | collective-permute-start | bytes 3145736 | tf_op jit(solution)/shard_map/ppermute | solution.py:82
  120.8 14.4 %collective-permute-done.14.refs_10_ = bf16[256,2048]{1,0:T(8,128)(2,1)} collective-permute-done((bf16[256,2048]{1,0:T(8,128)(2,1)}, bf16[256,2048]{1,0:T(8,128)(2,1)}, u32[]{:S(2)}, u32[]{:S(2)}) %collective-permute-start.14) | collective-permute-done | bytes 1048608 | tf_op jit(solution)/shard_map/ppermute | solution.py:82
  135.2 2.0 %collective-permute-start.15 = (bf16[256,2048]{1,0:T(8,128)(2,1)S(1)}, bf16[256,2048]{1,0:T(8,128)(2,1)S(1)}, u32[]{:S(2)}, u32[]{:S(2)}) collective-permute-start(bf16[256,2048]{1,0:T(8,128)(2,1)S(1)} %copy.27), channel_id=1, source_target_pairs={{0,1},{1,0},{2,3},{3,2},{4,5},{5,4},{6,7},{7,6},{8,9},{9,8},{10,11... | collective-permute-start | bytes 3145736 | tf_op jit(solution)/shard_map/ppermute | solution.py:124
  137.9 3.0 %collective-permute-done.17.refs_12_ = bf16[256,2048]{1,0:T(8,128)(2,1)} collective-permute-done((bf16[256,2048]{1,0:T(8,128)(2,1)}, bf16[256,2048]{1,0:T(8,128)(2,1)}, u32[]{:S(2)}, u32[]{:S(2)}) %collective-permute-start.17) | collective-permute-done | bytes 1048608 | tf_op jit(solution)/shard_map/ppermute | solution.py:82
  142.1 1.9 %slice.7 = bf16[128,2048]{1,0:T(8,128)(2,1)} slice(bf16[256,2048]{1,0:T(8,128)(2,1)} %collective-permute-done.17.refs_12_), slice={[128:256], [0:2048]} | slice | bytes 1048576 | tf_op jit(solution)/shard_map/slice | solution.py:80
  147.5 7.3 %collective-permute-done.22 = bf16[128,2048]{1,0:T(8,128)(2,1)} collective-permute-done((bf16[128,2048]{1,0:T(8,128)(2,1)S(1)}, bf16[128,2048]{1,0:T(8,128)(2,1)}, u32[]{:S(2)}, u32[]{:S(2)}) %collective-permute-start.22) | collective-permute-done | bytes 524320 | tf_op jit(solution)/shard_map/ppermute | solution.py:79
  157.2 2.6 %collective-permute-start.24 = (bf16[256,2048]{1,0:T(8,128)(2,1)S(1)}, bf16[256,2048]{1,0:T(8,128)(2,1)}, u32[]{:S(2)}, u32[]{:S(2)}) collective-permute-start(bf16[256,2048]{1,0:T(8,128)(2,1)S(1)} %constant_dynamic-update-slice_fusion.refs_14_), channel_id=1, source_target_pairs={{0,2},{2,0},{1,3},{3,1},{4,6},{6,4},{5,7},{7,5},{8,10},{10,8},{9,1... | collective-permute-start | bytes 3145736 | tf_op jit(solution)/shard_map/ppermute | solution.py:267
  162.2 9.6 %shard_map.82 = bf16[256,2048]{1,0:T(8,128)(2,1)} custom-call(s32[16]{0:T(128)} %mul.51.starts_ref, bf16[256,4096]{1,0:T(8,128)(2,1)} %pad_maximum_fusion.normed_ref, bf16[256,2048]{1,0:T(8,128)(2,1)} %refs_0_.1, bf16[256,2048]{1,0:T(8,128)(2,1)} %collective-permute-done.9.refs_1_, bf16[256,2048]{1,0:T(8,128)(2,1)} %collective-permute-done.refs_2_, ...), custom_call_target="tpu_custom_call" | custom-call | tf_op jit(solution)/shard_map/pallas_call | solution.py:189
  (95 shorter events, 34.0 us)
Async XLA Ops:
  2.4 13.1 %collective-permute-start.2 = (bf16[128,2048]{0,1:T(8,128)(2,1)}, bf16[128,2048]{0,1:T(8,128)(2,1)S(1)}, u32[]{:S(2)}, u32[]{:S(2)}) collective-permute-start(bf16[128,2048]{0,1:T(8,128)(2,1)} %copy.29), channel_id=1, source_target_pairs={{0,1},{1,0},{2,3},{3,2},{4,5},{5,4},{6,7},{7,6},{8,9},{9,8},{10,11... | collective-permute-start | bytes 1572872 | tf_op jit(solution)/shard_map/ppermute | solution.py:36
  3.6 24.0 %collective-permute-start = (bf16[256,2048]{1,0:T(8,128)(2,1)}, bf16[256,2048]{1,0:T(8,128)(2,1)}, u32[]{:S(2)}, u32[]{:S(2)}) collective-permute-start(bf16[256,2048]{1,0:T(8,128)(2,1)} %refs_0_.1), channel_id=1, source_target_pairs={{0,4},{4,12},{12,20},{20,28},{28,24},{24,16},{16,8},{8,0},{1,5},{5... | collective-permute-start | bytes 3145736 | tf_op jit(solution)/shard_map/ppermute | solution.py:82
  4.9 23.7 %collective-permute-start.1 = (bf16[256,2048]{1,0:T(8,128)(2,1)}, bf16[256,2048]{1,0:T(8,128)(2,1)}, u32[]{:S(2)}, u32[]{:S(2)}) collective-permute-start(bf16[256,2048]{1,0:T(8,128)(2,1)} %refs_0_.1), channel_id=1, source_target_pairs={{4,0},{12,4},{20,12},{28,20},{24,28},{16,24},{8,16},{0,8},{5,1},{1... | collective-permute-start | bytes 3145736 | tf_op jit(solution)/shard_map/ppermute | solution.py:82
  7.7 19.0 %collective-permute-start.3 = (bf16[128,2048]{0,1:T(8,128)(2,1)S(1)}, bf16[128,2048]{0,1:T(8,128)(2,1)S(1)}, u32[]{:S(2)}, u32[]{:S(2)}) collective-permute-start(bf16[128,2048]{0,1:T(8,128)(2,1)S(1)} %copy.31), channel_id=1, source_target_pairs={{0,1},{1,0},{2,3},{3,2},{4,5},{5,4},{6,7},{7,6},{8,9},{9,8},{10,11... | collective-permute-start | bytes 1572872 | tf_op jit(solution)/shard_map/ppermute | solution.py:36
  33.6 15.2 %collective-permute-start.5 = (f32[8,128,128]{2,1,0:T(8,128)S(1)}, f32[8,128,128]{2,1,0:T(8,128)S(1)}, u32[]{:S(2)}, u32[]{:S(2)}) collective-permute-start(f32[8,128,128]{2,1,0:T(8,128)S(1)} %dynamic-slice_add_fusion), channel_id=1, source_target_pairs={{0,4},{4,8},{8,12},{12,16},{16,20},{20,24},{24,28},{1,5},{5,9},{9,... | collective-permute-start | bytes 1572872 | tf_op jit(solution)/shard_map/ppermute | solution.py:20
  48.9 14.2 %collective-permute-start.6 = (f32[8,128,128]{2,1,0:T(8,128)S(1)}, f32[8,128,128]{2,1,0:T(8,128)}, u32[]{:S(2)}, u32[]{:S(2)}) collective-permute-start(f32[8,128,128]{2,1,0:T(8,128)S(1)} %add.79), channel_id=1, source_target_pairs={{0,8},{4,12},{8,16},{12,20},{16,24},{20,28},{1,9},{5,13},{9,17},{1... | collective-permute-start | bytes 1572872 | tf_op jit(solution)/shard_map/ppermute | solution.py:20
  54.1 13.2 %collective-permute-start.8 = (bf16[128,2048]{0,1:T(8,128)(2,1)}, bf16[128,2048]{0,1:T(8,128)(2,1)}, u32[]{:S(2)}, u32[]{:S(2)}) collective-permute-start(bf16[128,2048]{0,1:T(8,128)(2,1)} %copy.33), channel_id=1, source_target_pairs={{0,1},{1,0},{2,3},{3,2},{4,5},{5,4},{6,7},{7,6},{8,9},{9,8},{10,11... | collective-permute-start | bytes 1572872 | tf_op jit(solution)/shard_map/ppermute | solution.py:36
  54.4 40.9 %collective-permute-start.9 = (bf16[256,2048]{1,0:T(8,128)(2,1)}, bf16[256,2048]{1,0:T(8,128)(2,1)}, u32[]{:S(2)}, u32[]{:S(2)}) collective-permute-start(bf16[256,2048]{1,0:T(8,128)(2,1)} %refs_0_.1), channel_id=1, source_target_pairs={{0,2},{2,0},{1,3},{3,1},{4,6},{6,4},{5,7},{7,5},{8,10},{10,8},{9,1... | collective-permute-start | bytes 3145736 | tf_op jit(solution)/shard_map/ppermute | solution.py:244
  56.5 38.8 %collective-permute-start.10 = (bf16[256,2048]{1,0:T(8,128)(2,1)}, bf16[256,2048]{1,0:T(8,128)(2,1)}, u32[]{:S(2)}, u32[]{:S(2)}) collective-permute-start(bf16[256,2048]{1,0:T(8,128)(2,1)} %collective-permute-done.refs_2_), channel_id=1, source_target_pairs={{0,2},{2,0},{1,3},{3,1},{4,6},{6,4},{5,7},{7,5},{8,10},{10,8},{9,1... | collective-permute-start | bytes 3145736 | tf_op jit(solution)/shard_map/ppermute | solution.py:244
  56.6 38.8 %collective-permute-start.11 = (bf16[256,2048]{1,0:T(8,128)(2,1)}, bf16[256,2048]{1,0:T(8,128)(2,1)}, u32[]{:S(2)}, u32[]{:S(2)}) collective-permute-start(bf16[256,2048]{1,0:T(8,128)(2,1)} %collective-permute-done.1.refs_4_), channel_id=1, source_target_pairs={{0,2},{2,0},{1,3},{3,1},{4,6},{6,4},{5,7},{7,5},{8,10},{10,8},{9,1... | collective-permute-start | bytes 3145736 | tf_op jit(solution)/shard_map/ppermute | solution.py:244
  64.2 25.0 %collective-permute-start.7 = (f32[8,128,128]{2,1,0:T(8,128)S(1)}, f32[8,128,128]{2,1,0:T(8,128)S(1)}, u32[]{:S(2)}, u32[]{:S(2)}) collective-permute-start(f32[8,128,128]{2,1,0:T(8,128)S(1)} %add.80), channel_id=1, source_target_pairs={{0,16},{4,20},{8,24},{12,28},{1,17},{5,21},{9,25},{13,29},{2,18},{... | collective-permute-start | bytes 1572872 | tf_op jit(solution)/shard_map/ppermute | solution.py:20
  69.6 42.2 %collective-permute-start.13 = (bf16[256,2048]{1,0:T(8,128)(2,1)}, bf16[256,2048]{1,0:T(8,128)(2,1)}, u32[]{:S(2)}, u32[]{:S(2)}) collective-permute-start(bf16[256,2048]{1,0:T(8,128)(2,1)} %collective-permute-done.refs_2_), channel_id=1, source_target_pairs={{0,4},{4,12},{12,20},{20,28},{28,24},{24,16},{16,8},{8,0},{1,5},{5... | collective-permute-start | bytes 3145736 | tf_op jit(solution)/shard_map/ppermute | solution.py:82
  89.2 26.6 %collective-permute-start.16 = (bf16[256,2048]{1,0:T(8,128)(2,1)}, bf16[256,2048]{1,0:T(8,128)(2,1)}, u32[]{:S(2)}, u32[]{:S(2)}) collective-permute-start(bf16[256,2048]{1,0:T(8,128)(2,1)} %collective-permute-done.1.refs_4_), channel_id=1, source_target_pairs={{4,0},{12,4},{20,12},{28,20},{24,28},{16,24},{8,16},{0,8},{5,1},{1... | collective-permute-start | bytes 3145736 | tf_op jit(solution)/shard_map/ppermute | solution.py:82
  95.3 20.6 %collective-permute-start.12 = (f32[8,128,128]{2,1,0:T(8,128)}, f32[8,128,128]{2,1,0:T(8,128)}, u32[]{:S(2)}, u32[]{:S(2)}) collective-permute-start(f32[8,128,128]{2,1,0:T(8,128)} %add_subtract_fusion), channel_id=1, source_target_pairs={{0,2},{2,0},{1,3},{3,1},{4,6},{6,4},{5,7},{7,5},{8,10},{10,8},{9,1... | collective-permute-start | bytes 1572872 | tf_op jit(solution)/shard_map/ppermute | solution.py:138
  111.8 23.4 %collective-permute-start.14 = (bf16[256,2048]{1,0:T(8,128)(2,1)}, bf16[256,2048]{1,0:T(8,128)(2,1)}, u32[]{:S(2)}, u32[]{:S(2)}) collective-permute-start(bf16[256,2048]{1,0:T(8,128)(2,1)} %collective-permute-done.13.refs_6_), channel_id=1, source_target_pairs={{0,4},{4,12},{12,20},{20,28},{28,24},{24,16},{16,8},{8,0},{1,5},{5... | collective-permute-start | bytes 3145736 | tf_op jit(solution)/shard_map/ppermute | solution.py:82
  114.0 26.9 %collective-permute-start.18 = (bf16[256,2048]{1,0:T(8,128)(2,1)}, bf16[256,2048]{1,0:T(8,128)(2,1)}, u32[]{:S(2)}, u32[]{:S(2)}) collective-permute-start(bf16[256,2048]{1,0:T(8,128)(2,1)} %collective-permute-done.13.refs_6_), channel_id=1, source_target_pairs={{0,2},{2,0},{1,3},{3,1},{4,6},{6,4},{5,7},{7,5},{8,10},{10,8},{9,1... | collective-permute-start | bytes 3145736 | tf_op jit(solution)/shard_map/ppermute | solution.py:258
  115.8 25.1 %collective-permute-start.17 = (bf16[256,2048]{1,0:T(8,128)(2,1)}, bf16[256,2048]{1,0:T(8,128)(2,1)}, u32[]{:S(2)}, u32[]{:S(2)}) collective-permute-start(bf16[256,2048]{1,0:T(8,128)(2,1)} %collective-permute-done.16.refs_8_), channel_id=1, source_target_pairs={{4,0},{12,4},{20,12},{28,20},{24,28},{16,24},{8,16},{0,8},{5,1},{1... | collective-permute-start | bytes 3145736 | tf_op jit(solution)/shard_map/ppermute | solution.py:82
  115.8 25.1 %collective-permute-start.19 = (bf16[256,2048]{1,0:T(8,128)(2,1)}, bf16[256,2048]{1,0:T(8,128)(2,1)}, u32[]{:S(2)}, u32[]{:S(2)}) collective-permute-start(bf16[256,2048]{1,0:T(8,128)(2,1)} %collective-permute-done.16.refs_8_), channel_id=1, source_target_pairs={{0,2},{2,0},{1,3},{3,1},{4,6},{6,4},{5,7},{7,5},{8,10},{10,8},{9,1... | collective-permute-start | bytes 3145736 | tf_op jit(solution)/shard_map/ppermute | solution.py:258
  135.2 24.5 %collective-permute-start.15 = (bf16[256,2048]{1,0:T(8,128)(2,1)S(1)}, bf16[256,2048]{1,0:T(8,128)(2,1)S(1)}, u32[]{:S(2)}, u32[]{:S(2)}) collective-permute-start(bf16[256,2048]{1,0:T(8,128)(2,1)S(1)} %copy.27), channel_id=1, source_target_pairs={{0,1},{1,0},{2,3},{3,2},{4,5},{5,4},{6,7},{7,6},{8,9},{9,8},{10,11... | collective-permute-start | bytes 3145736 | tf_op jit(solution)/shard_map/ppermute | solution.py:124
  142.0 12.8 %collective-permute-start.22 = (bf16[128,2048]{1,0:T(8,128)(2,1)S(1)}, bf16[128,2048]{1,0:T(8,128)(2,1)}, u32[]{:S(2)}, u32[]{:S(2)}) collective-permute-start(bf16[128,2048]{1,0:T(8,128)(2,1)S(1)} %slice.6), channel_id=1, source_target_pairs={{0,4},{4,12},{12,20},{20,28},{28,24},{24,16},{16,8},{8,0},{1,5},{5... | collective-permute-start | bytes 1572872 | tf_op jit(solution)/shard_map/ppermute | solution.py:79
  144.0 12.1 %collective-permute-start.23 = (bf16[128,2048]{1,0:T(8,128)(2,1)}, bf16[128,2048]{1,0:T(8,128)(2,1)}, u32[]{:S(2)}, u32[]{:S(2)}) collective-permute-start(bf16[128,2048]{1,0:T(8,128)(2,1)} %slice.7), channel_id=1, source_target_pairs={{4,0},{12,4},{20,12},{28,20},{24,28},{16,24},{8,16},{0,8},{5,1},{1... | collective-permute-start | bytes 1572872 | tf_op jit(solution)/shard_map/ppermute | solution.py:79
  146.1 15.4 %collective-permute-start.20 = (bf16[256,2048]{1,0:T(8,128)(2,1)}, bf16[256,2048]{1,0:T(8,128)(2,1)}, u32[]{:S(2)}, u32[]{:S(2)}) collective-permute-start(bf16[256,2048]{1,0:T(8,128)(2,1)} %collective-permute-done.14.refs_10_), channel_id=1, source_target_pairs={{0,2},{2,0},{1,3},{3,1},{4,6},{6,4},{5,7},{7,5},{8,10},{10,8},{9,1... | collective-permute-start | bytes 3145736 | tf_op jit(solution)/shard_map/ppermute | solution.py:267
  147.5 14.0 %collective-permute-start.21 = (bf16[256,2048]{1,0:T(8,128)(2,1)}, bf16[256,2048]{1,0:T(8,128)(2,1)}, u32[]{:S(2)}, u32[]{:S(2)}) collective-permute-start(bf16[256,2048]{1,0:T(8,128)(2,1)} %collective-permute-done.17.refs_12_), channel_id=1, source_target_pairs={{0,2},{2,0},{1,3},{3,1},{4,6},{6,4},{5,7},{7,5},{8,10},{10,8},{9,1... | collective-permute-start | bytes 3145736 | tf_op jit(solution)/shard_map/ppermute | solution.py:267
  157.2 5.0 %collective-permute-start.24 = (bf16[256,2048]{1,0:T(8,128)(2,1)S(1)}, bf16[256,2048]{1,0:T(8,128)(2,1)}, u32[]{:S(2)}, u32[]{:S(2)}) collective-permute-start(bf16[256,2048]{1,0:T(8,128)(2,1)S(1)} %constant_dynamic-update-slice_fusion.refs_14_), channel_id=1, source_target_pairs={{0,2},{2,0},{1,3},{3,1},{4,6},{6,4},{5,7},{7,5},{8,10},{10,8},{9,1... | collective-permute-start | bytes 3145736 | tf_op jit(solution)/shard_map/ppermute | solution.py:267
  (15 other events, 151.3 us)

commit v17 on v14

--- a/solution.py
+++ b/solution.py
@@ -144,7 +144,7 @@
     return block.reshape(block.shape[0], heads_dev, HEAD_DIM)
 
 
-def project_blocks(normed, starts, blocks, group=4):
+def project_blocks(normed, starts, blocks, group=4, out_dtype=jnp.bfloat16):
     n = len(blocks)
     rows, cols = blocks[0].shape
     tokens = normed.shape[0]
@@ -188,7 +188,7 @@
 
     return pl.pallas_call(
         kernel,
-        out_shape=jax.ShapeDtypeStruct((tokens, cols), jnp.bfloat16),
+        out_shape=jax.ShapeDtypeStruct((tokens, cols), out_dtype),
         in_specs=[pl.BlockSpec(memory_space=pltpu.SMEM), pl.BlockSpec(memory_space=pl.ANY)]
         + [pl.BlockSpec(memory_space=pl.ANY)] * n,
         out_specs=pl.BlockSpec(memory_space=pltpu.VMEM),
@@ -252,19 +252,17 @@
     within_block = within_block_part(query_heads, key_heads, value_heads)
     swapped += [lax.ppermute(w, "core", SWAP) for w in got[len(swapped):]]
     chip_prefix_half, within_block, swapped = barrier((chip_prefix_half, within_block, swapped))
-    for step in range(2, n_steps + 1):
+    for step in range(2, n_steps):
         if step >= 4:
             early = len(got) - 2
             swapped += [lax.ppermute(w, "core", SWAP) for w in got[len(swapped):early]]
             ahead, behind, swapped = barrier((ahead, behind, swapped))
-        ahead, behind = ring_step(ahead, behind, order, last=step == n_steps)
-        if step == n_steps:
-            got.append(jnp.concatenate([ahead, behind], 0))
-            offsets.append(step)
-        else:
-            got += [ahead, behind]
-            offsets += [step, -step]
+        ahead, behind = ring_step(ahead, behind, order)
+        got += [ahead, behind]
+        offsets += [step, -step]
     swapped += [lax.ppermute(w, "core", SWAP) for w in got[len(swapped):]]
+    last_ahead, last_behind = ring_step(ahead, behind, order, last=True)
+    offsets.append(n_steps)
     prefix = chip_finish(chip_prefix_half, partner_state, core)
     normed = normalize(query_heads, prefix, within_block, norm_gain)
     gathered = gather_head(normed, n_head, place)
@@ -272,8 +270,21 @@
     ring_place = jnp.asarray([order.index(j) for j in range(n_chip)], jnp.int32)[lax.axis_index("chip")]
     sources = jnp.asarray(order, jnp.int32)[(ring_place - jnp.asarray(offsets, jnp.int32)) % n_chip]
     cores = jnp.stack([core, 1 - core]).astype(jnp.int32)
-    starts = ((sources[:, None] * 2 + cores[None, :]) * out_weight.shape[0]).reshape(-1)
-    return project_blocks(gathered, starts, [w for pair in zip(got, swapped) for w in pair])
+    weight_rows = out_weight.shape[0]
+    starts = ((sources[:, None] * 2 + cores[None, :]) * weight_rows).reshape(-1)
+    partial = project_blocks(
+        gathered,
+        starts[:-2],
+        [w for pair in zip(got, swapped) for w in pair],
+        out_dtype=jnp.float32,
+    )
+    partial, last_ahead, last_behind = barrier((partial, last_ahead, last_behind))
+    last_own = jnp.concatenate([last_ahead, last_behind], 0)
+    last_other = lax.ppermute(last_own, "core", SWAP)
+    features = [lax.dynamic_slice_in_dim(gathered, starts[-2 + k], weight_rows, 1) for k in range(2)]
+    outcome = partial + jnp.dot(features[0], last_own, preferred_element_type=jnp.float32)
+    outcome = outcome + jnp.dot(features[1], last_other, preferred_element_type=jnp.float32)
+    return outcome.astype(jnp.bfloat16)
 
 
 def solution(mesh):

time: 175 us -> 175 us (level)
  waiting for transfers between devices: 100 us -> 89.5 us
  between operations: 0.33 us -> 4.32 us
  matrix products: 3.92 us -> 7.17 us
  local copies, waits for them, and re-layouts: 17.3 us -> 20 us
  other arithmetic: 11.4 us -> 13.4 us
    ppermute x1, waiting for transfers between devices: 7.32 us -> 0.01 us  [ring_step(): lax.ppermute(ahead[:half_rows], 'chip', forward)]
    ppermute x3, waiting for transfers between devices: 6.66 us -> 2.58 us  [ring_step(): lax.ppermute(behind, 'chip', backward)]
    dot_general x0 -> x2, matrix products: none -> 3.28 us  [the longest x1 2.75 us: local_ring(): jnp.dot(features[1], last_other, preferred_element_type=jnp.float32)]
    select_n x5, other arithmetic: 2.69 us -> 4.95 us  [pair_order(): first = jnp.where(place == 0, own, other)]
    ppermute x1, starting transfers between devices: 0.06 us -> 2.2 us  [ring_step(): lax.ppermute(ahead[:half_rows], 'chip', forward)]
    unnamed x35 -> x37, local copies, waits for them, and re-layouts: 6.16 us -> 8.14 us
    ppermute x3 -> x4, starting transfers between devices: 3.46 us -> 3.89 us  [local_ring(): swapped += [lax.ppermute(w, 'core', SWAP) for w in got[len(swapped):]]]
  transfers between devices with their start and end apart: 25 -> 25, of which waited for: 14 -> 12; matrix products, arithmetic and copies ran while one was open for 17% -> 16% of each run, Pallas kernels for 0% -> 5%
where the time goes in v17:
time: 175 us; the launch traced here: 172 us
  waiting for transfers between devices  89.5 us (51%)
  starting transfers between devices  28.7 us (16%)
  local copies, waits for them, and re-layouts  20 us (11%)
  other arithmetic  13.4 us (8%)
  Pallas kernels  9.22 us (5%)
  matrix products  7.17 us (4%)
  between operations  4.32 us (2%)
    ppermute x3, waiting for transfers between devices, exclusive_prefix(): total = total + lax.ppermute(total, axis, pairs)  38.7 us
    ppermute x3, waiting for transfers between devices, ring_step(): lax.ppermute(ahead, 'chip', forward)  25 us
    ppermute x3, waiting for transfers between devices, head_blocks(): other = lax.ppermute(tuple(sent), 'head', SWAP)  19.2 us
    pallas_call x1, Pallas kernels, project_blocks(): pl.pallas_call(kernel, out_shape=jax.ShapeDtypeStruct((tokens, cols), out...  9.22 us
    ppermute x3, starting transfers between devices, exclusive_prefix(): total = total + lax.ppermute(total, axis, pairs)  8.52 us
    unnamed x37, local copies, waits for them, and re-layouts  8.14 us
    select_n x5, other arithmetic, pair_order(): first = jnp.where(place == 0, own, other)  4.95 us
    ppermute x4, starting transfers between devices, local_ring(): swapped += [lax.ppermute(w, 'core', SWAP) for w in got[len(swapped):]]  3.89 us
  transfers between devices with their start and end apart: 25, of which 12 were waited for; matrix products, arithmetic and copies ran while one was open for 16% of the time, Pallas kernels for 5%

profile of v17, /device:TPU:13, one launch (start us, length us, event | category | flops | bytes accessed | tf_op | source)
XLA Modules:
  0.0 172.3 jit_solution(10839554749379054056)
XLA Ops:
  0.0 2.8 %constant_dynamic-slice_fusion.1 = (bf16[128,2048]{1,0:T(8,128)(2,1)}, bf16[128,2048]{1,0:T(8,128)(2,1)}, bf16[128,2048]{1,0:T(8,128)(2,1)S(1)}, bf16[128,2048]{1,0:T(8,128)(2,1)S(1)}) fusion(bf16[128,4096]{1,0:T(8,128)(2,1)} %param.8, s32[]{:T(128)S(6)} %select_n.102, s32[]{:T(128)S(6)} %select_n.103, bf16[128,4096]{1,0:T(8,128)(2,1)} %param.10), kind=kLoop, calls=%fused_computation.46 | loop fusion | bytes 4194312 | tf_op jit(solution)/shard_map/dynamic_slice | solution.py:34
  7.7 9.2 %collective-permute-done.3 = bf16[128,2048]{0,1:T(8,128)(2,1)} collective-permute-done((bf16[128,2048]{0,1:T(8,128)(2,1)}, bf16[128,2048]{0,1:T(8,128)(2,1)}, u32[]{:S(2)}, u32[]{:S(2)}) %collective-permute-start.3) | collective-permute-done | bytes 524320 | tf_op jit(solution)/shard_map/ppermute | solution.py:36
  18.1 10.0 %collective-permute-done.2 = bf16[128,2048]{0,1:T(8,128)(2,1)S(1)} collective-permute-done((bf16[128,2048]{0,1:T(8,128)(2,1)S(1)}, bf16[128,2048]{0,1:T(8,128)(2,1)S(1)}, u32[]{:S(2)}, u32[]{:S(2)}) %collective-permute-start.2) | collective-permute-done | bytes 524320 | tf_op jit(solution)/shard_map/ppermute | solution.py:36
  30.4 2.2 %collective-permute-start.4 = (f32[16,128,128]{2,1,0:T(8,128)S(1)}, f32[16,128,128]{2,1,0:T(8,128)S(1)}, u32[]{:S(2)}, u32[]{:S(2)}) collective-permute-start(f32[16,128,128]{2,1,0:T(8,128)S(1)} %fusion.24), channel_id=1, source_target_pairs={{0,2},{2,0},{1,3},{3,1},{4,6},{6,4},{5,7},{7,5},{8,10},{10,8},{9,1... | collective-permute-start | bytes 3145736 | tf_op jit(solution)/shard_map/ppermute | solution.py:130
  32.7 2.3 %collective-permute-done.4 = f32[16,128,128]{2,1,0:T(8,128)S(1)} collective-permute-done((f32[16,128,128]{2,1,0:T(8,128)S(1)}, f32[16,128,128]{2,1,0:T(8,128)S(1)}, u32[]{:S(2)}, u32[]{:S(2)}) %collective-permute-start.4) | collective-permute-done | bytes 1048608 | tf_op jit(solution)/shard_map/ppermute | solution.py:130
  35.0 2.1 %collective-permute-start.5 = (f32[8,128,128]{2,1,0:T(8,128)S(1)}, f32[8,128,128]{2,1,0:T(8,128)S(1)}, u32[]{:S(2)}, u32[]{:S(2)}) collective-permute-start(f32[8,128,128]{2,1,0:T(8,128)S(1)} %dynamic-slice_add_fusion), channel_id=1, source_target_pairs={{0,4},{4,8},{8,12},{12,16},{16,20},{20,24},{24,28},{1,5},{5,9},{9,... | collective-permute-start | bytes 1572872 | tf_op jit(solution)/shard_map/ppermute | solution.py:20
  37.2 13.0 %collective-permute-done.5 = f32[8,128,128]{2,1,0:T(8,128)S(1)} collective-permute-done((f32[8,128,128]{2,1,0:T(8,128)S(1)}, f32[8,128,128]{2,1,0:T(8,128)S(1)}, u32[]{:S(2)}, u32[]{:S(2)}) %collective-permute-start.5) | collective-permute-done | bytes 524320 | tf_op jit(solution)/shard_map/ppermute | solution.py:20
  50.3 3.2 %collective-permute-start.6 = (f32[8,128,128]{2,1,0:T(8,128)S(1)}, f32[8,128,128]{2,1,0:T(8,128)}, u32[]{:S(2)}, u32[]{:S(2)}) collective-permute-start(f32[8,128,128]{2,1,0:T(8,128)S(1)} %add.91), channel_id=1, source_target_pairs={{0,8},{4,12},{8,16},{12,20},{16,24},{20,28},{1,9},{5,13},{9,17},{1... | collective-permute-start | bytes 1572872 | tf_op jit(solution)/shard_map/ppermute | solution.py:20
  53.5 2.0 %copy.33 = bf16[128,2048]{0,1:T(8,128)(2,1)} copy(bf16[128,2048]{1,0:T(8,128)(2,1)} %get-tuple-element.36) | data formatting | bytes 1048576
  58.4 6.1 %collective-permute-done.6 = f32[8,128,128]{2,1,0:T(8,128)} collective-permute-done((f32[8,128,128]{2,1,0:T(8,128)S(1)}, f32[8,128,128]{2,1,0:T(8,128)}, u32[]{:S(2)}, u32[]{:S(2)}) %collective-permute-start.6) | collective-permute-done | bytes 524320 | tf_op jit(solution)/shard_map/ppermute | solution.py:20
  65.6 3.2 %collective-permute-start.7 = (f32[8,128,128]{2,1,0:T(8,128)S(1)}, f32[8,128,128]{2,1,0:T(8,128)S(1)}, u32[]{:S(2)}, u32[]{:S(2)}) collective-permute-start(f32[8,128,128]{2,1,0:T(8,128)S(1)} %add.92), channel_id=1, source_target_pairs={{0,16},{4,20},{8,24},{12,28},{1,17},{5,21},{9,25},{13,29},{2,18},{... | collective-permute-start | bytes 1572872 | tf_op jit(solution)/shard_map/ppermute | solution.py:20
  71.0 19.6 %collective-permute-done.7 = f32[8,128,128]{2,1,0:T(8,128)S(1)} collective-permute-done((f32[8,128,128]{2,1,0:T(8,128)S(1)}, f32[8,128,128]{2,1,0:T(8,128)S(1)}, u32[]{:S(2)}, u32[]{:S(2)}) %collective-permute-start.7) | collective-permute-done | bytes 524320 | tf_op jit(solution)/shard_map/ppermute | solution.py:20
  91.4 2.9 %fusion.1 = f32[256,16,128]{0,2,1:T(8,128)S(1)} fusion(bf16[256,16,128]{0,2,1:T(8,128)(2,1)S(1)} %bitcast.28, bf16[256,16,128]{0,2,1:T(8,128)(2,1)} %bitcast.31, bf16[256,16,128]{0,2,1:T(8,128)(2,1)} %bitcast.30, pred[256,256]{1,0:T(8,128)(4,1)S(1)} %iota_compare_fusion), kind=kOutput, calls=%fused_computation.12 | convolution fusion | flops 538968064 | bytes 5308416 | tf_op jit(solution)/shard_map/hts,she->the/dot_general | solution.py:103
  94.3 2.3 %add_subtract_fusion = f32[8,128,128]{2,1,0:T(8,128)} fusion(f32[8,128,128]{2,1,0:T(8,128)} %copy-done.4, f32[8,128,128]{2,1,0:T(8,128)} %copy-done.8, f32[8,128,128]{2,1,0:T(8,128)} %copy-done.11), kind=kLoop, calls=%fused_computation.23 | loop fusion | flops 262144 | bytes 2097152 | tf_op jit(solution)/shard_map/sub | solution.py:22
  96.7 2.7 %collective-permute-start.12 = (f32[8,128,128]{2,1,0:T(8,128)}, f32[8,128,128]{2,1,0:T(8,128)}, u32[]{:S(2)}, u32[]{:S(2)}) collective-permute-start(f32[8,128,128]{2,1,0:T(8,128)} %add_subtract_fusion), channel_id=1, source_target_pairs={{0,2},{2,0},{1,3},{3,1},{4,6},{6,4},{5,7},{7,5},{8,10},{10,8},{9,1... | collective-permute-start | bytes 1572872 | tf_op jit(solution)/shard_map/ppermute | solution.py:138
  99.4 13.8 %collective-permute-done.14.refs_6_ = bf16[256,2048]{1,0:T(8,128)(2,1)} collective-permute-done((bf16[256,2048]{1,0:T(8,128)(2,1)}, bf16[256,2048]{1,0:T(8,128)(2,1)}, u32[]{:S(2)}, u32[]{:S(2)}) %collective-permute-start.14) | collective-permute-done | bytes 1048608 | tf_op jit(solution)/shard_map/ppermute | solution.py:82
  113.2 2.2 %collective-permute-start.18 = (bf16[256,2048]{1,0:T(8,128)(2,1)}, bf16[256,2048]{1,0:T(8,128)(2,1)}, u32[]{:S(2)}, u32[]{:S(2)}) collective-permute-start(bf16[256,2048]{1,0:T(8,128)(2,1)} %collective-permute-done.14.refs_6_), channel_id=1, source_target_pairs={{0,4},{4,12},{12,20},{20,28},{28,24},{24,16},{16,8},{8,0},{1,5},{5... | collective-permute-start | bytes 3145736 | tf_op jit(solution)/shard_map/ppermute | solution.py:82
  115.4 1.8 %collective-permute-start.15 = (bf16[256,2048]{1,0:T(8,128)(2,1)}, bf16[256,2048]{1,0:T(8,128)(2,1)}, u32[]{:S(2)}, u32[]{:S(2)}) collective-permute-start(bf16[256,2048]{1,0:T(8,128)(2,1)} %collective-permute-done.14.refs_6_), channel_id=1, source_target_pairs={{0,2},{2,0},{1,3},{3,1},{4,6},{6,4},{5,7},{7,5},{8,10},{10,8},{9,1... | collective-permute-start | bytes 3145736 | tf_op jit(solution)/shard_map/ppermute | solution.py:263
  126.1 10.5 %collective-permute-done.18.refs_10_ = bf16[256,2048]{1,0:T(8,128)(2,1)} collective-permute-done((bf16[256,2048]{1,0:T(8,128)(2,1)}, bf16[256,2048]{1,0:T(8,128)(2,1)}, u32[]{:S(2)}, u32[]{:S(2)}) %collective-permute-start.18) | collective-permute-done | bytes 1048608 | tf_op jit(solution)/shard_map/ppermute | solution.py:82
  136.7 1.9 %slice.26 = bf16[128,2048]{1,0:T(8,128)(2,1)} slice(bf16[256,2048]{1,0:T(8,128)(2,1)} %collective-permute-done.18.refs_10_), slice={[0:128], [0:2048]} | slice | bytes 1048576 | tf_op jit(solution)/shard_map/slice | solution.py:79
  138.5 2.2 %collective-permute-start.22 = (bf16[128,2048]{1,0:T(8,128)(2,1)}, bf16[128,2048]{1,0:T(8,128)(2,1)}, u32[]{:S(2)}, u32[]{:S(2)}) collective-permute-start(bf16[128,2048]{1,0:T(8,128)(2,1)} %slice.26), channel_id=1, source_target_pairs={{0,4},{4,12},{12,20},{20,28},{28,24},{24,16},{16,8},{8,0},{1,5},{5... | collective-permute-start | bytes 1572872 | tf_op jit(solution)/shard_map/ppermute | solution.py:79
  142.3 1.9 %slice.27 = bf16[128,2048]{1,0:T(8,128)(2,1)} slice(bf16[256,2048]{1,0:T(8,128)(2,1)} %collective-permute-done.20.refs_12_), slice={[128:256], [0:2048]} | slice | bytes 1048576 | tf_op jit(solution)/shard_map/slice | solution.py:80
  151.6 9.2 %shard_map.82 = f32[256,2048]{1,0:T(8,128)} custom-call(s32[14]{0:T(128)} %slice.19.starts_ref, bf16[256,4096]{1,0:T(8,128)(2,1)} %pad_maximum_fusion.normed_ref, bf16[256,2048]{1,0:T(8,128)(2,1)} %refs_0_.1, bf16[256,2048]{1,0:T(8,128)(2,1)} %collective-permute-done.9.refs_1_, bf16[256,2048]{1,0:T(8,128)(2,1)} %collective-permute-done.refs_2_, ...), custom_call_target="tpu_custom_call" | custom-call | tf_op jit(solution)/shard_map/pallas_call | solution.py:189
  169.6 2.7 %add_convert_fusion = bf16[256,2048]{1,0:T(8,128)(2,1)} fusion(f32[256,2048]{1,0:T(8,128)S(1)} %copy-done.3, f32[256,2048]{1,0:T(8,128)S(1)} %fusion.8, bf16[256,2048]{1,0:T(8,128)(2,1)} %collective-permute-done.24, s32[]{:T(128)S(6)} %select_n.119, bf16[256,2048]{1,0:T(8,128)(2,1)S(1)} %get-tuple-element.29, bf16[256,2048]{1,0:T(8,128)(2,1)S(1)} %get-tuple-element.30), kind=kOutput, calls=%fused_computation.8 | convolution fusion | flops 270270464 | bytes 8388612 | tf_op jit(solution)/shard_map/dot_general | solution.py:286
  (101 shorter events, 38.1 us)
Async XLA Ops:
  3.8 13.1 %collective-permute-start.3 = (bf16[128,2048]{0,1:T(8,128)(2,1)}, bf16[128,2048]{0,1:T(8,128)(2,1)}, u32[]{:S(2)}, u32[]{:S(2)}) collective-permute-start(bf16[128,2048]{0,1:T(8,128)(2,1)} %copy.31), channel_id=1, source_target_pairs={{0,1},{1,0},{2,3},{3,2},{4,5},{5,4},{6,7},{7,6},{8,9},{9,8},{10,11... | collective-permute-start | bytes 1572872 | tf_op jit(solution)/shard_map/ppermute | solution.py:36
  5.0 24.0 %collective-permute-start = (bf16[256,2048]{1,0:T(8,128)(2,1)}, bf16[256,2048]{1,0:T(8,128)(2,1)}, u32[]{:S(2)}, u32[]{:S(2)}) collective-permute-start(bf16[256,2048]{1,0:T(8,128)(2,1)} %refs_0_.1), channel_id=1, source_target_pairs={{0,4},{4,12},{12,20},{20,28},{28,24},{24,16},{16,8},{8,0},{1,5},{5... | collective-permute-start | bytes 3145736 | tf_op jit(solution)/shard_map/ppermute | solution.py:82
  6.3 23.7 %collective-permute-start.1 = (bf16[256,2048]{1,0:T(8,128)(2,1)}, bf16[256,2048]{1,0:T(8,128)(2,1)}, u32[]{:S(2)}, u32[]{:S(2)}) collective-permute-start(bf16[256,2048]{1,0:T(8,128)(2,1)} %refs_0_.1), channel_id=1, source_target_pairs={{4,0},{12,4},{20,12},{28,20},{24,28},{16,24},{8,16},{0,8},{5,1},{1... | collective-permute-start | bytes 3145736 | tf_op jit(solution)/shard_map/ppermute | solution.py:82
  6.8 21.3 %collective-permute-start.2 = (bf16[128,2048]{0,1:T(8,128)(2,1)S(1)}, bf16[128,2048]{0,1:T(8,128)(2,1)S(1)}, u32[]{:S(2)}, u32[]{:S(2)}) collective-permute-start(bf16[128,2048]{0,1:T(8,128)(2,1)S(1)} %copy.29), channel_id=1, source_target_pairs={{0,1},{1,0},{2,3},{3,2},{4,5},{5,4},{6,7},{7,6},{8,9},{9,8},{10,11... | collective-permute-start | bytes 1572872 | tf_op jit(solution)/shard_map/ppermute | solution.py:36
  30.4 4.5 %collective-permute-start.4 = (f32[16,128,128]{2,1,0:T(8,128)S(1)}, f32[16,128,128]{2,1,0:T(8,128)S(1)}, u32[]{:S(2)}, u32[]{:S(2)}) collective-permute-start(f32[16,128,128]{2,1,0:T(8,128)S(1)} %fusion.24), channel_id=1, source_target_pairs={{0,2},{2,0},{1,3},{3,1},{4,6},{6,4},{5,7},{7,5},{8,10},{10,8},{9,1... | collective-permute-start | bytes 3145736 | tf_op jit(solution)/shard_map/ppermute | solution.py:130
  35.0 15.2 %collective-permute-start.5 = (f32[8,128,128]{2,1,0:T(8,128)S(1)}, f32[8,128,128]{2,1,0:T(8,128)S(1)}, u32[]{:S(2)}, u32[]{:S(2)}) collective-permute-start(f32[8,128,128]{2,1,0:T(8,128)S(1)} %dynamic-slice_add_fusion), channel_id=1, source_target_pairs={{0,4},{4,8},{8,12},{12,16},{16,20},{20,24},{24,28},{1,5},{5,9},{9,... | collective-permute-start | bytes 1572872 | tf_op jit(solution)/shard_map/ppermute | solution.py:20
  50.3 14.2 %collective-permute-start.6 = (f32[8,128,128]{2,1,0:T(8,128)S(1)}, f32[8,128,128]{2,1,0:T(8,128)}, u32[]{:S(2)}, u32[]{:S(2)}) collective-permute-start(f32[8,128,128]{2,1,0:T(8,128)S(1)} %add.91), channel_id=1, source_target_pairs={{0,8},{4,12},{8,16},{12,20},{16,24},{20,28},{1,9},{5,13},{9,17},{1... | collective-permute-start | bytes 1572872 | tf_op jit(solution)/shard_map/ppermute | solution.py:20
  55.5 13.3 %collective-permute-start.8 = (bf16[128,2048]{0,1:T(8,128)(2,1)}, bf16[128,2048]{0,1:T(8,128)(2,1)}, u32[]{:S(2)}, u32[]{:S(2)}) collective-permute-start(bf16[128,2048]{0,1:T(8,128)(2,1)} %copy.33), channel_id=1, source_target_pairs={{0,1},{1,0},{2,3},{3,2},{4,5},{5,4},{6,7},{7,6},{8,9},{9,8},{10,11... | collective-permute-start | bytes 1572872 | tf_op jit(solution)/shard_map/ppermute | solution.py:36
  55.8 40.9 %collective-permute-start.9 = (bf16[256,2048]{1,0:T(8,128)(2,1)}, bf16[256,2048]{1,0:T(8,128)(2,1)}, u32[]{:S(2)}, u32[]{:S(2)}) collective-permute-start(bf16[256,2048]{1,0:T(8,128)(2,1)} %refs_0_.1), channel_id=1, source_target_pairs={{0,2},{2,0},{1,3},{3,1},{4,6},{6,4},{5,7},{7,5},{8,10},{10,8},{9,1... | collective-permute-start | bytes 3145736 | tf_op jit(solution)/shard_map/ppermute | solution.py:244
  57.9 38.8 %collective-permute-start.10 = (bf16[256,2048]{1,0:T(8,128)(2,1)}, bf16[256,2048]{1,0:T(8,128)(2,1)}, u32[]{:S(2)}, u32[]{:S(2)}) collective-permute-start(bf16[256,2048]{1,0:T(8,128)(2,1)} %collective-permute-done.refs_2_), channel_id=1, source_target_pairs={{0,2},{2,0},{1,3},{3,1},{4,6},{6,4},{5,7},{7,5},{8,10},{10,8},{9,1... | collective-permute-start | bytes 3145736 | tf_op jit(solution)/shard_map/ppermute | solution.py:244
  57.9 38.7 %collective-permute-start.11 = (bf16[256,2048]{1,0:T(8,128)(2,1)}, bf16[256,2048]{1,0:T(8,128)(2,1)}, u32[]{:S(2)}, u32[]{:S(2)}) collective-permute-start(bf16[256,2048]{1,0:T(8,128)(2,1)} %collective-permute-done.1.refs_4_), channel_id=1, source_target_pairs={{0,2},{2,0},{1,3},{3,1},{4,6},{6,4},{5,7},{7,5},{8,10},{10,8},{9,1... | collective-permute-start | bytes 3145736 | tf_op jit(solution)/shard_map/ppermute | solution.py:244
  65.6 25.0 %collective-permute-start.7 = (f32[8,128,128]{2,1,0:T(8,128)S(1)}, f32[8,128,128]{2,1,0:T(8,128)S(1)}, u32[]{:S(2)}, u32[]{:S(2)}) collective-permute-start(f32[8,128,128]{2,1,0:T(8,128)S(1)} %add.92), channel_id=1, source_target_pairs={{0,16},{4,20},{8,24},{12,28},{1,17},{5,21},{9,25},{13,29},{2,18},{... | collective-permute-start | bytes 1572872 | tf_op jit(solution)/shard_map/ppermute | solution.py:20
  71.0 42.2 %collective-permute-start.14 = (bf16[256,2048]{1,0:T(8,128)(2,1)}, bf16[256,2048]{1,0:T(8,128)(2,1)}, u32[]{:S(2)}, u32[]{:S(2)}) collective-permute-start(bf16[256,2048]{1,0:T(8,128)(2,1)} %collective-permute-done.refs_2_), channel_id=1, source_target_pairs={{0,4},{4,12},{12,20},{20,28},{28,24},{24,16},{16,8},{8,0},{1,5},{5... | collective-permute-start | bytes 3145736 | tf_op jit(solution)/shard_map/ppermute | solution.py:82
  90.6 26.6 %collective-permute-start.16 = (bf16[256,2048]{1,0:T(8,128)(2,1)}, bf16[256,2048]{1,0:T(8,128)(2,1)}, u32[]{:S(2)}, u32[]{:S(2)}) collective-permute-start(bf16[256,2048]{1,0:T(8,128)(2,1)} %collective-permute-done.1.refs_4_), channel_id=1, source_target_pairs={{4,0},{12,4},{20,12},{28,20},{24,28},{16,24},{8,16},{0,8},{5,1},{1... | collective-permute-start | bytes 3145736 | tf_op jit(solution)/shard_map/ppermute | solution.py:82
  96.7 20.5 %collective-permute-start.12 = (f32[8,128,128]{2,1,0:T(8,128)}, f32[8,128,128]{2,1,0:T(8,128)}, u32[]{:S(2)}, u32[]{:S(2)}) collective-permute-start(f32[8,128,128]{2,1,0:T(8,128)} %add_subtract_fusion), channel_id=1, source_target_pairs={{0,2},{2,0},{1,3},{3,1},{4,6},{6,4},{5,7},{7,5},{8,10},{10,8},{9,1... | collective-permute-start | bytes 1572872 | tf_op jit(solution)/shard_map/ppermute | solution.py:138
  113.2 23.4 %collective-permute-start.18 = (bf16[256,2048]{1,0:T(8,128)(2,1)}, bf16[256,2048]{1,0:T(8,128)(2,1)}, u32[]{:S(2)}, u32[]{:S(2)}) collective-permute-start(bf16[256,2048]{1,0:T(8,128)(2,1)} %collective-permute-done.14.refs_6_), channel_id=1, source_target_pairs={{0,4},{4,12},{12,20},{20,28},{28,24},{24,16},{16,8},{8,0},{1,5},{5... | collective-permute-start | bytes 3145736 | tf_op jit(solution)/shard_map/ppermute | solution.py:82
  115.4 29.0 %collective-permute-start.15 = (bf16[256,2048]{1,0:T(8,128)(2,1)}, bf16[256,2048]{1,0:T(8,128)(2,1)}, u32[]{:S(2)}, u32[]{:S(2)}) collective-permute-start(bf16[256,2048]{1,0:T(8,128)(2,1)} %collective-permute-done.14.refs_6_), channel_id=1, source_target_pairs={{0,2},{2,0},{1,3},{3,1},{4,6},{6,4},{5,7},{7,5},{8,10},{10,8},{9,1... | collective-permute-start | bytes 3145736 | tf_op jit(solution)/shard_map/ppermute | solution.py:263
  117.2 25.1 %collective-permute-start.20 = (bf16[256,2048]{1,0:T(8,128)(2,1)}, bf16[256,2048]{1,0:T(8,128)(2,1)}, u32[]{:S(2)}, u32[]{:S(2)}) collective-permute-start(bf16[256,2048]{1,0:T(8,128)(2,1)} %collective-permute-done.16.refs_8_), channel_id=1, source_target_pairs={{4,0},{12,4},{20,12},{28,20},{24,28},{16,24},{8,16},{0,8},{5,1},{1... | collective-permute-start | bytes 3145736 | tf_op jit(solution)/shard_map/ppermute | solution.py:82
  122.2 24.9 %collective-permute-start.13 = (bf16[256,2048]{1,0:T(8,128)(2,1)S(1)}, bf16[256,2048]{1,0:T(8,128)(2,1)S(1)}, u32[]{:S(2)}, u32[]{:S(2)}) collective-permute-start(bf16[256,2048]{1,0:T(8,128)(2,1)S(1)} %copy.27), channel_id=1, source_target_pairs={{0,1},{1,0},{2,3},{3,2},{4,5},{5,4},{6,7},{7,6},{8,9},{9,8},{10,11... | collective-permute-start | bytes 3145736 | tf_op jit(solution)/shard_map/ppermute | solution.py:124
  125.7 25.9 %collective-permute-start.17 = (bf16[256,2048]{1,0:T(8,128)(2,1)}, bf16[256,2048]{1,0:T(8,128)(2,1)}, u32[]{:S(2)}, u32[]{:S(2)}) collective-permute-start(bf16[256,2048]{1,0:T(8,128)(2,1)} %collective-permute-done.16.refs_8_), channel_id=1, source_target_pairs={{0,2},{2,0},{1,3},{3,1},{4,6},{6,4},{5,7},{7,5},{8,10},{10,8},{9,1... | collective-permute-start | bytes 3145736 | tf_op jit(solution)/shard_map/ppermute | solution.py:263
  138.5 22.3 %collective-permute-start.22 = (bf16[128,2048]{1,0:T(8,128)(2,1)}, bf16[128,2048]{1,0:T(8,128)(2,1)}, u32[]{:S(2)}, u32[]{:S(2)}) collective-permute-start(bf16[128,2048]{1,0:T(8,128)(2,1)} %slice.26), channel_id=1, source_target_pairs={{0,4},{4,12},{12,20},{20,28},{28,24},{24,16},{16,8},{8,0},{1,5},{5... | collective-permute-start | bytes 1572872 | tf_op jit(solution)/shard_map/ppermute | solution.py:79
  144.2 16.7 %collective-permute-start.23 = (bf16[128,2048]{1,0:T(8,128)(2,1)}, bf16[128,2048]{1,0:T(8,128)(2,1)}, u32[]{:S(2)}, u32[]{:S(2)}) collective-permute-start(bf16[128,2048]{1,0:T(8,128)(2,1)} %slice.27), channel_id=1, source_target_pairs={{4,0},{12,4},{20,12},{28,20},{24,28},{16,24},{8,16},{0,8},{5,1},{1... | collective-permute-start | bytes 1572872 | tf_op jit(solution)/shard_map/ppermute | solution.py:79
  144.4 7.2 %collective-permute-start.19 = (bf16[256,2048]{1,0:T(8,128)(2,1)}, bf16[256,2048]{1,0:T(8,128)(2,1)}, u32[]{:S(2)}, u32[]{:S(2)}) collective-permute-start(bf16[256,2048]{1,0:T(8,128)(2,1)} %collective-permute-done.18.refs_10_), channel_id=1, source_target_pairs={{0,2},{2,0},{1,3},{3,1},{4,6},{6,4},{5,7},{7,5},{8,10},{10,8},{9,1... | collective-permute-start | bytes 3145736 | tf_op jit(solution)/shard_map/ppermute | solution.py:263
  163.0 5.5 %collective-permute-start.24 = (bf16[256,2048]{1,0:T(8,128)(2,1)S(1)}, bf16[256,2048]{1,0:T(8,128)(2,1)}, u32[]{:S(2)}, u32[]{:S(2)}) collective-permute-start(bf16[256,2048]{1,0:T(8,128)(2,1)S(1)} %constant_dynamic-update-slice_fusion), channel_id=1, source_target_pairs={{0,2},{2,0},{1,3},{3,1},{4,6},{6,4},{5,7},{7,5},{8,10},{10,8},{9,1... | collective-permute-start | bytes 3145736 | tf_op jit(solution)/shard_map/ppermute | solution.py:283
  (16 other events, 131.7 us)

commit v18 on v11

--- a/solution.py
+++ b/solution.py
@@ -232,16 +232,26 @@
     return outcome.astype(jnp.bfloat16)
 
 
+def ring_halves(ahead, behind, order, last=False):
+    forward, backward = ring_links(order)
+    if last:
+        return (lax.ppermute(ahead[0], "chip", forward), lax.ppermute(behind[1], "chip", backward))
+    return lax.ppermute(ahead, "chip", forward), lax.ppermute(behind, "chip", backward)
+
+
 def local_ring(queries, keys, values, out_weight, norm_gain, n_chip, n_head, order):
     heads_dev = norm_gain.shape[0] // HEAD_DIM
     core = lax.axis_index("core")
     place = lax.axis_index("head")
     n_steps = n_chip // 2
     barrier = lax.optimization_barrier
+    weight_rows = out_weight.shape[0]
+    half_rows = weight_rows // 2
+    halves = (out_weight[:half_rows], out_weight[half_rows:])
     key_block, value_block = head_blocks([keys, values], n_head, place)
-    ahead, behind = ring_step(out_weight, out_weight, order)
+    ahead, behind = ring_halves(halves, halves, order)
     ahead, behind, key_block, value_block = barrier((ahead, behind, key_block, value_block))
-    got = [out_weight, ahead, behind]
+    got = [halves, ahead, behind]
     offsets = [0, 1, -1]
     (query_block,) = head_blocks([queries], n_head, place)
     swapped = [lax.ppermute(w, "core", SWAP) for w in got]
@@ -253,12 +263,11 @@
     chip_prefix_half = exclusive_prefix(chip_half, "chip", n_chip)
     query_heads = split_heads(query_block, heads_dev)
     within_block = within_block_part(query_heads, key_heads, value_heads)
-    swapped += [lax.ppermute(w, "core", SWAP) for w in got[len(swapped):]]
     chip_prefix_half, within_block, swapped = barrier((chip_prefix_half, within_block, swapped))
     for step in range(2, n_steps + 1):
-        ahead, behind = ring_step(ahead, behind, order, last=step == n_steps)
+        ahead, behind = ring_halves(ahead, behind, order, last=step == n_steps)
         if step == n_steps:
-            got.append(jnp.concatenate([ahead, behind], 0))
+            got.append((ahead, behind))
             offsets.append(step)
         else:
             got += [ahead, behind]
@@ -267,12 +276,15 @@
     prefix = chip_finish(chip_prefix_half, partner_state, core)
     normed = normalize(query_heads, prefix, within_block, norm_gain)
     gathered = gather_head(normed, n_head, place)
-    row_count = gathered.shape[0]
     ring_place = jnp.asarray([order.index(j) for j in range(n_chip)], jnp.int32)[lax.axis_index("chip")]
     sources = jnp.asarray(order, jnp.int32)[(ring_place - jnp.asarray(offsets, jnp.int32)) % n_chip]
     cores = jnp.stack([core, 1 - core]).astype(jnp.int32)
-    starts = ((sources[:, None] * 2 + cores[None, :]) * out_weight.shape[0]).reshape(-1)
-    return project_blocks(gathered, starts, [w for pair in zip(got, swapped) for w in pair])
+    parts = jnp.asarray([0, half_rows], jnp.int32)
+    starts = (
+        (sources[:, None, None] * 2 + cores[None, :, None]) * weight_rows + parts[None, None, :]
+    ).reshape(-1)
+    blocks = [h for own, other in zip(got, swapped) for pair in (own, other) for h in pair]
+    return project_blocks(gathered, starts, blocks, group=8)
 
 
 def solution(mesh):

time: 175 us -> 192 us (1.097)
  starting transfers between devices: 32 us -> 40.9 us
  waiting for transfers between devices: 96.2 us -> 105 us
  local copies, waits for them, and re-layouts: 20.8 us -> 16 us
  other arithmetic: 8.14 us -> 11.6 us
    ppermute x8 -> x14, waiting for transfers between devices: 33.7 us -> 46.1 us  [the longest x6 31.3 us: ring_halves(): lax.ppermute(ahead, 'chip', forward)]
    ppermute x8 -> x14, starting transfers between devices: 5.93 us -> 11.2 us  [the longest x6 7.42 us: ring_halves(): lax.ppermute(ahead, 'chip', forward)]
    ppermute x3, waiting for transfers between devices: 38.6 us -> 34.6 us  [exclusive_prefix(): total = total + lax.ppermute(total, axis, pairs)]
    ppermute x3 -> x6, starting transfers between devices: 2.33 us -> 6.2 us  [local_ring(): swapped = [lax.ppermute(w, 'core', SWAP) for w in got]]
    ppermute x1, waiting for transfers between devices: 0.01 us -> 3.55 us  [gather_head(): other = lax.ppermute(normed, 'head', SWAP)]
    ppermute x2, waiting for transfers between devices: 21.1 us -> 18.6 us  [head_blocks(): other = lax.ppermute(sent, 'head', SWAP)]
    select_n x3, other arithmetic: 0.29 us -> 2.68 us  [pair_order(): first = jnp.where(place == 0, own, other)]
    ppermute x1, starting transfers between devices: 2.71 us -> 0.57 us  [chip_finish(): other_half = lax.ppermute(chip_prefix_half, 'core', SWAP)]
  transfers between devices with their start and end apart: 24 -> 38, of which waited for: 11 -> 16; matrix products, arithmetic and copies ran while one was open for 14% -> 12% of each run, Pallas kernels for 0% -> 0%
where the time goes in v18:
time: 192 us; the launch traced here: 190 us
  waiting for transfers between devices  105 us (55%)
  starting transfers between devices  40.9 us (21%)
  local copies, waits for them, and re-layouts  16 us (8%)
  other arithmetic  11.6 us (6%)
  Pallas kernels  9.9 us (5%)
  matrix products  5.52 us (3%)
    ppermute x3, waiting for transfers between devices, exclusive_prefix(): total = total + lax.ppermute(total, axis, pairs)  34.6 us
    ppermute x6, waiting for transfers between devices, ring_halves(): lax.ppermute(ahead, 'chip', forward)  31.3 us
    ppermute x2, waiting for transfers between devices, head_blocks(): other = lax.ppermute(sent, 'head', SWAP)  18.6 us
    ppermute x1, waiting for transfers between devices, ring_halves(): lax.ppermute(ahead[0], 'chip', forward)  10.3 us
    pallas_call x1, Pallas kernels, project_blocks(): pl.pallas_call(kernel, out_shape=jax.ShapeDtypeStruct((tokens, cols), jnp...  9.9 us
    ppermute x10, starting transfers between devices, local_ring(): swapped += [lax.ppermute(w, 'core', SWAP) for w in got[len(swapped):]]  9.79 us
    ppermute x3, starting transfers between devices, exclusive_prefix(): total = total + lax.ppermute(total, axis, pairs)  9.19 us
    ppermute x6, starting transfers between devices, ring_halves(): lax.ppermute(ahead, 'chip', forward)  7.42 us
  transfers between devices with their start and end apart: 38, of which 16 were waited for; matrix products, arithmetic and copies ran while one was open for 12% of the time, Pallas kernels for 0%

profile of v18, /device:TPU:13, one launch (start us, length us, event | category | flops | bytes accessed | tf_op | source)
XLA Modules:
  0.0 189.7 jit_solution(2928512472269978512)
XLA Ops:
  3.6 2.4 %copy.23 = bf16[2,128,1,2048]{3,1,0,2:T(8,128)(2,1)} copy(bf16[2,128,1,2048]{1,3,2,0:T(8,128)(2,1)} %get-tuple-element.40) | data formatting | bytes 2097152 | tf_op jit(solution)/shard_map/jit(dynamic_index_in_dim)/dynamic_slice | solution.py:37
  11.6 18.6 %collective-permute-done.4 = bf16[2,128,2048]{2,1,0:T(8,128)(2,1)S(1)} collective-permute-done((bf16[2,128,2048]{2,1,0:T(8,128)(2,1)}, bf16[2,128,2048]{2,1,0:T(8,128)(2,1)S(1)}, u32[]{:S(2)}, u32[]{:S(2)}) %collective-permute-start.4) | collective-permute-done | bytes 1048608 | tf_op jit(solution)/shard_map/ppermute | solution.py:38
  34.2 2.2 %collective-permute-start.5 = (f32[16,128,128]{2,1,0:T(8,128)S(1)}, f32[16,128,128]{2,1,0:T(8,128)}, u32[]{:S(2)}, u32[]{:S(2)}) collective-permute-start(f32[16,128,128]{2,1,0:T(8,128)S(1)} %fusion.6), channel_id=1, source_target_pairs={{0,2},{2,0},{1,3},{3,1},{4,6},{6,4},{5,7},{7,5},{8,10},{10,8},{9,1... | collective-permute-start | bytes 3145736 | tf_op jit(solution)/shard_map/ppermute | solution.py:133
  36.5 2.4 %collective-permute-done.5 = f32[16,128,128]{2,1,0:T(8,128)} collective-permute-done((f32[16,128,128]{2,1,0:T(8,128)S(1)}, f32[16,128,128]{2,1,0:T(8,128)}, u32[]{:S(2)}, u32[]{:S(2)}) %collective-permute-start.5) | collective-permute-done | bytes 1048608 | tf_op jit(solution)/shard_map/ppermute | solution.py:133
  40.1 2.0 %collective-permute-start.6 = (f32[8,128,128]{2,1,0:T(8,128)S(1)}, f32[8,128,128]{2,1,0:T(8,128)S(1)}, u32[]{:S(2)}, u32[]{:S(2)}) collective-permute-start(f32[8,128,128]{2,1,0:T(8,128)S(1)} %dynamic-slice_add_fusion), channel_id=1, source_target_pairs={{0,4},{4,8},{8,12},{12,16},{16,20},{20,24},{24,28},{1,5},{5,9},{9,... | collective-permute-start | bytes 1572872 | tf_op jit(solution)/shard_map/ppermute | solution.py:20
  43.9 11.3 %collective-permute-done.6 = f32[8,128,128]{2,1,0:T(8,128)S(1)} collective-permute-done((f32[8,128,128]{2,1,0:T(8,128)S(1)}, f32[8,128,128]{2,1,0:T(8,128)S(1)}, u32[]{:S(2)}, u32[]{:S(2)}) %collective-permute-start.6) | collective-permute-done | bytes 524320 | tf_op jit(solution)/shard_map/ppermute | solution.py:20
  55.2 3.2 %collective-permute-start.7 = (f32[8,128,128]{2,1,0:T(8,128)S(1)}, f32[8,128,128]{2,1,0:T(8,128)}, u32[]{:S(2)}, u32[]{:S(2)}) collective-permute-start(f32[8,128,128]{2,1,0:T(8,128)S(1)} %add.104), channel_id=1, source_target_pairs={{0,8},{4,12},{8,16},{12,20},{16,24},{20,28},{1,9},{5,13},{9,17},{1... | collective-permute-start | bytes 1572872 | tf_op jit(solution)/shard_map/ppermute | solution.py:20
  61.7 7.7 %collective-permute-done.7 = f32[8,128,128]{2,1,0:T(8,128)} collective-permute-done((f32[8,128,128]{2,1,0:T(8,128)S(1)}, f32[8,128,128]{2,1,0:T(8,128)}, u32[]{:S(2)}, u32[]{:S(2)}) %collective-permute-start.7) | collective-permute-done | bytes 524320 | tf_op jit(solution)/shard_map/ppermute | solution.py:20
  70.6 4.0 %collective-permute-start.8 = (f32[8,128,128]{2,1,0:T(8,128)S(1)}, f32[8,128,128]{2,1,0:T(8,128)}, u32[]{:S(2)}, u32[]{:S(2)}) collective-permute-start(f32[8,128,128]{2,1,0:T(8,128)S(1)} %add.105), channel_id=1, source_target_pairs={{0,16},{4,20},{8,24},{12,28},{1,17},{5,21},{9,25},{13,29},{2,18},{... | collective-permute-start | bytes 1572872 | tf_op jit(solution)/shard_map/ppermute | solution.py:20
  77.1 2.4 %collective-permute-start.12 = (bf16[128,2048]{1,0:T(8,128)(2,1)}, bf16[128,2048]{1,0:T(8,128)(2,1)}, u32[]{:S(2)}, u32[]{:S(2)}) collective-permute-start(bf16[128,2048]{1,0:T(8,128)(2,1)} %collective-permute-done.refs_4_), channel_id=1, source_target_pairs={{0,2},{2,0},{1,3},{3,1},{4,6},{6,4},{5,7},{7,5},{8,10},{10,8},{9,1... | collective-permute-start | bytes 1572872 | tf_op jit(solution)/shard_map/ppermute | solution.py:257
  80.0 15.6 %collective-permute-done.8 = f32[8,128,128]{2,1,0:T(8,128)} collective-permute-done((f32[8,128,128]{2,1,0:T(8,128)S(1)}, f32[8,128,128]{2,1,0:T(8,128)}, u32[]{:S(2)}, u32[]{:S(2)}) %collective-permute-start.8) | collective-permute-done | bytes 524320 | tf_op jit(solution)/shard_map/ppermute | solution.py:20
  97.1 3.2 %fusion.1 = f32[256,16,128]{0,2,1:T(8,128)S(1)} fusion(bf16[256,16,128]{0,2,1:T(8,128)(2,1)} %bitcast.49, bf16[256,16,128]{0,2,1:T(8,128)(2,1)} %bitcast.54, pred[256,256]{1,0:T(8,128)(4,1)S(1)} %iota_compare_fusion, bf16[256,2048]{1,0:T(8,128)(2,1)} %copy-done.2), kind=kOutput, calls=%fused_computation.13 | convolution fusion | flops 538968064 | bytes 5308416 | tf_op jit(solution)/shard_map/hts,she->the/dot_general | solution.py:106
  100.3 1.9 %add_subtract_fusion = f32[8,128,128]{2,1,0:T(8,128)} fusion(f32[8,128,128]{2,1,0:T(8,128)S(1)} %dynamic-slice_add_fusion, f32[8,128,128]{2,1,0:T(8,128)S(1)} %add.105, f32[8,128,128]{2,1,0:T(8,128)} %collective-permute-done.8), kind=kLoop, calls=%fused_computation.37 | loop fusion | flops 262144 | bytes 2097152 | tf_op jit(solution)/shard_map/sub | solution.py:22
  103.7 2.1 %collective-permute-start.19 = (bf16[128,2048]{1,0:T(8,128)(2,1)}, bf16[128,2048]{1,0:T(8,128)(2,1)}, u32[]{:S(2)}, u32[]{:S(2)}) collective-permute-start(bf16[128,2048]{1,0:T(8,128)(2,1)} %collective-permute-done.1.refs_5_), channel_id=1, source_target_pairs={{0,4},{4,12},{12,20},{20,28},{28,24},{24,16},{16,8},{8,0},{1,5},{5... | collective-permute-start | bytes 1572872 | tf_op jit(solution)/shard_map/ppermute | solution.py:239
  107.0 9.1 %collective-permute-done.18.refs_12_ = bf16[128,2048]{1,0:T(8,128)(2,1)} collective-permute-done((bf16[128,2048]{1,0:T(8,128)(2,1)}, bf16[128,2048]{1,0:T(8,128)(2,1)}, u32[]{:S(2)}, u32[]{:S(2)}) %collective-permute-start.18) | collective-permute-done | bytes 524320 | tf_op jit(solution)/shard_map/ppermute | solution.py:239
  119.3 8.0 %collective-permute-done.19.refs_13_ = bf16[128,2048]{1,0:T(8,128)(2,1)} collective-permute-done((bf16[128,2048]{1,0:T(8,128)(2,1)}, bf16[128,2048]{1,0:T(8,128)(2,1)}, u32[]{:S(2)}, u32[]{:S(2)}) %collective-permute-start.19) | collective-permute-done | bytes 524320 | tf_op jit(solution)/shard_map/ppermute | solution.py:239
  130.2 1.8 multiply_reduce_fusion
  133.9 4.7 %collective-permute-done.26.refs_20_ = bf16[128,2048]{1,0:T(8,128)(2,1)} collective-permute-done((bf16[128,2048]{1,0:T(8,128)(2,1)}, bf16[128,2048]{1,0:T(8,128)(2,1)}, u32[]{:S(2)}, u32[]{:S(2)}) %collective-permute-start.26) | collective-permute-done | bytes 524320 | tf_op jit(solution)/shard_map/ppermute | solution.py:239
  139.9 2.1 %collective-permute-start.24 = (bf16[128,2048]{1,0:T(8,128)(2,1)}, bf16[128,2048]{1,0:T(8,128)(2,1)}, u32[]{:S(2)}, u32[]{:S(2)}) collective-permute-start(bf16[128,2048]{1,0:T(8,128)(2,1)} %collective-permute-done.22.refs_16_), channel_id=1, source_target_pairs={{0,2},{2,0},{1,3},{3,1},{4,6},{6,4},{5,7},{7,5},{8,10},{10,8},{9,1... | collective-permute-start | bytes 1572872 | tf_op jit(solution)/shard_map/ppermute | solution.py:275
  142.0 7.8 %collective-permute-done.27.refs_21_ = bf16[128,2048]{1,0:T(8,128)(2,1)} collective-permute-done((bf16[128,2048]{1,0:T(8,128)(2,1)}, bf16[128,2048]{1,0:T(8,128)(2,1)}, u32[]{:S(2)}, u32[]{:S(2)}) %collective-permute-start.27) | collective-permute-done | bytes 524320 | tf_op jit(solution)/shard_map/ppermute | solution.py:239
  153.2 2.0 %collective-permute-start.34 = (bf16[128,2048]{1,0:T(8,128)(2,1)}, bf16[128,2048]{1,0:T(8,128)(2,1)}, u32[]{:S(2)}, u32[]{:S(2)}) collective-permute-start(bf16[128,2048]{1,0:T(8,128)(2,1)} %collective-permute-done.26.refs_20_), channel_id=1, source_target_pairs={{0,4},{4,12},{12,20},{20,28},{28,24},{24,16},{16,8},{8,0},{1,5},{5... | collective-permute-start | bytes 1572872 | tf_op jit(solution)/shard_map/ppermute | solution.py:238
  156.6 10.3 %collective-permute-done.34.refs_28_ = bf16[128,2048]{1,0:T(8,128)(2,1)} collective-permute-done((bf16[128,2048]{1,0:T(8,128)(2,1)}, bf16[128,2048]{1,0:T(8,128)(2,1)}, u32[]{:S(2)}, u32[]{:S(2)}) %collective-permute-start.34) | collective-permute-done | bytes 524320 | tf_op jit(solution)/shard_map/ppermute | solution.py:238
  170.2 3.6 %collective-permute-done.17 = bf16[256,2048]{1,0:T(8,128)(2,1)S(1)} collective-permute-done((bf16[256,2048]{1,0:T(8,128)(2,1)S(1)}, bf16[256,2048]{1,0:T(8,128)(2,1)S(1)}, u32[]{:S(2)}, u32[]{:S(2)}) %collective-permute-start.17) | collective-permute-done | bytes 1048608 | tf_op jit(solution)/shard_map/ppermute | solution.py:127
  179.7 9.9 %shard_map.91 = bf16[256,2048]{1,0:T(8,128)(2,1)} custom-call(s32[32]{0:T(128)} %add.99.starts_ref, bf16[256,4096]{1,0:T(8,128)(2,1)} %pad_maximum_fusion.normed_ref, bf16[128,2048]{1,0:T(8,128)(2,1)} %get-tuple-element.48.refs_0_, bf16[128,2048]{1,0:T(8,128)(2,1)} %get-tuple-element.47.refs_1_, bf16[128,2048]{1,0:T(8,128)(2,1)} %collective-permute-done.10.refs_2_, ...), custom_call_target="tpu_custom_call" | custom-call | tf_op jit(solution)/shard_map/pallas_call | solution.py:192
  (123 shorter events, 50.7 us)
Async XLA Ops:
  5.9 24.3 %collective-permute-start.4 = (bf16[2,128,2048]{2,1,0:T(8,128)(2,1)}, bf16[2,128,2048]{2,1,0:T(8,128)(2,1)S(1)}, u32[]{:S(2)}, u32[]{:S(2)}) collective-permute-start(bf16[2,128,2048]{2,1,0:T(8,128)(2,1)} %bitcast.56), channel_id=1, source_target_pairs={{0,1},{1,0},{2,3},{3,2},{4,5},{5,4},{6,7},{7,6},{8,9},{9,8},{10,11... | collective-permute-start | bytes 3145736 | tf_op jit(solution)/shard_map/ppermute | solution.py:38
  8.2 22.4 %collective-permute-start = (bf16[128,2048]{1,0:T(8,128)(2,1)}, bf16[128,2048]{1,0:T(8,128)(2,1)}, u32[]{:S(2)}, u32[]{:S(2)}) collective-permute-start(bf16[128,2048]{1,0:T(8,128)(2,1)} %get-tuple-element.48.refs_0_), channel_id=1, source_target_pairs={{0,4},{4,12},{12,20},{20,28},{28,24},{24,16},{16,8},{8,0},{1,5},{5... | collective-permute-start | bytes 1572872 | tf_op jit(solution)/shard_map/ppermute | solution.py:239
  9.5 22.7 %collective-permute-start.2 = (bf16[128,2048]{1,0:T(8,128)(2,1)}, bf16[128,2048]{1,0:T(8,128)(2,1)}, u32[]{:S(2)}, u32[]{:S(2)}) collective-permute-start(bf16[128,2048]{1,0:T(8,128)(2,1)} %get-tuple-element.48.refs_0_), channel_id=1, source_target_pairs={{4,0},{12,4},{20,12},{28,20},{24,28},{16,24},{8,16},{0,8},{5,1},{1... | collective-permute-start | bytes 1572872 | tf_op jit(solution)/shard_map/ppermute | solution.py:239
  9.6 22.6 %collective-permute-start.1 = (bf16[128,2048]{1,0:T(8,128)(2,1)}, bf16[128,2048]{1,0:T(8,128)(2,1)}, u32[]{:S(2)}, u32[]{:S(2)}) collective-permute-start(bf16[128,2048]{1,0:T(8,128)(2,1)} %get-tuple-element.47.refs_1_), channel_id=1, source_target_pairs={{0,4},{4,12},{12,20},{20,28},{28,24},{24,16},{16,8},{8,0},{1,5},{5... | collective-permute-start | bytes 1572872 | tf_op jit(solution)/shard_map/ppermute | solution.py:239
  10.9 22.3 %collective-permute-start.3 = (bf16[128,2048]{1,0:T(8,128)(2,1)}, bf16[128,2048]{1,0:T(8,128)(2,1)}, u32[]{:S(2)}, u32[]{:S(2)}) collective-permute-start(bf16[128,2048]{1,0:T(8,128)(2,1)} %get-tuple-element.47.refs_1_), channel_id=1, source_target_pairs={{4,0},{12,4},{20,12},{28,20},{24,28},{16,24},{8,16},{0,8},{5,1},{1... | collective-permute-start | bytes 1572872 | tf_op jit(solution)/shard_map/ppermute | solution.py:239
  40.1 15.0 %collective-permute-start.6 = (f32[8,128,128]{2,1,0:T(8,128)S(1)}, f32[8,128,128]{2,1,0:T(8,128)S(1)}, u32[]{:S(2)}, u32[]{:S(2)}) collective-permute-start(f32[8,128,128]{2,1,0:T(8,128)S(1)} %dynamic-slice_add_fusion), channel_id=1, source_target_pairs={{0,4},{4,8},{8,12},{12,16},{16,20},{20,24},{24,28},{1,5},{5,9},{9,... | collective-permute-start | bytes 1572872 | tf_op jit(solution)/shard_map/ppermute | solution.py:20
  59.5 15.1 %collective-permute-start.9 = (bf16[1,128,2048]{2,1,0:T(8,128)(2,1)}, bf16[1,128,2048]{2,1,0:T(8,128)(2,1)}, u32[]{:S(2)}, u32[]{:S(2)}) collective-permute-start(bf16[1,128,2048]{2,1,0:T(8,128)(2,1)} %bitcast.11), channel_id=1, source_target_pairs={{0,1},{1,0},{2,3},{3,2},{4,5},{5,4},{6,7},{7,6},{8,9},{9,8},{10,11... | collective-permute-start | bytes 1572872 | tf_op jit(solution)/shard_map/ppermute | solution.py:38
  59.7 19.8 %collective-permute-start.10 = (bf16[128,2048]{1,0:T(8,128)(2,1)}, bf16[128,2048]{1,0:T(8,128)(2,1)}, u32[]{:S(2)}, u32[]{:S(2)}) collective-permute-start(bf16[128,2048]{1,0:T(8,128)(2,1)} %get-tuple-element.48.refs_0_), channel_id=1, source_target_pairs={{0,2},{2,0},{1,3},{3,1},{4,6},{6,4},{5,7},{7,5},{8,10},{10,8},{9,1... | collective-permute-start | bytes 1572872 | tf_op jit(solution)/shard_map/ppermute | solution.py:257
  61.5 40.8 %collective-permute-start.11 = (bf16[128,2048]{1,0:T(8,128)(2,1)}, bf16[128,2048]{1,0:T(8,128)(2,1)}, u32[]{:S(2)}, u32[]{:S(2)}) collective-permute-start(bf16[128,2048]{1,0:T(8,128)(2,1)} %get-tuple-element.47.refs_1_), channel_id=1, source_target_pairs={{0,2},{2,0},{1,3},{3,1},{4,6},{6,4},{5,7},{7,5},{8,10},{10,8},{9,1... | collective-permute-start | bytes 1572872 | tf_op jit(solution)/shard_map/ppermute | solution.py:257
  70.6 25.0 %collective-permute-start.8 = (f32[8,128,128]{2,1,0:T(8,128)S(1)}, f32[8,128,128]{2,1,0:T(8,128)}, u32[]{:S(2)}, u32[]{:S(2)}) collective-permute-start(f32[8,128,128]{2,1,0:T(8,128)S(1)} %add.105), channel_id=1, source_target_pairs={{0,16},{4,20},{8,24},{12,28},{1,17},{5,21},{9,25},{13,29},{2,18},{... | collective-permute-start | bytes 1572872 | tf_op jit(solution)/shard_map/ppermute | solution.py:20
  77.1 25.2 %collective-permute-start.12 = (bf16[128,2048]{1,0:T(8,128)(2,1)}, bf16[128,2048]{1,0:T(8,128)(2,1)}, u32[]{:S(2)}, u32[]{:S(2)}) collective-permute-start(bf16[128,2048]{1,0:T(8,128)(2,1)} %collective-permute-done.refs_4_), channel_id=1, source_target_pairs={{0,2},{2,0},{1,3},{3,1},{4,6},{6,4},{5,7},{7,5},{8,10},{10,8},{9,1... | collective-permute-start | bytes 1572872 | tf_op jit(solution)/shard_map/ppermute | solution.py:257
  79.5 24.3 %collective-permute-start.13 = (bf16[128,2048]{1,0:T(8,128)(2,1)}, bf16[128,2048]{1,0:T(8,128)(2,1)}, u32[]{:S(2)}, u32[]{:S(2)}) collective-permute-start(bf16[128,2048]{1,0:T(8,128)(2,1)} %collective-permute-done.1.refs_5_), channel_id=1, source_target_pairs={{0,2},{2,0},{1,3},{3,1},{4,6},{6,4},{5,7},{7,5},{8,10},{10,8},{9,1... | collective-permute-start | bytes 1572872 | tf_op jit(solution)/shard_map/ppermute | solution.py:257
  79.5 26.3 %collective-permute-start.14 = (bf16[128,2048]{1,0:T(8,128)(2,1)}, bf16[128,2048]{1,0:T(8,128)(2,1)}, u32[]{:S(2)}, u32[]{:S(2)}) collective-permute-start(bf16[128,2048]{1,0:T(8,128)(2,1)} %collective-permute-done.2.refs_8_), channel_id=1, source_target_pairs={{0,2},{2,0},{1,3},{3,1},{4,6},{6,4},{5,7},{7,5},{8,10},{10,8},{9,1... | collective-permute-start | bytes 1572872 | tf_op jit(solution)/shard_map/ppermute | solution.py:257
  102.3 15.9 %collective-permute-start.23 = (bf16[128,2048]{1,0:T(8,128)(2,1)}, bf16[128,2048]{1,0:T(8,128)(2,1)}, u32[]{:S(2)}, u32[]{:S(2)}) collective-permute-start(bf16[128,2048]{1,0:T(8,128)(2,1)} %collective-permute-done.3.refs_9_), channel_id=1, source_target_pairs={{4,0},{12,4},{20,12},{28,20},{24,28},{16,24},{8,16},{0,8},{5,1},{1... | collective-permute-start | bytes 1572872 | tf_op jit(solution)/shard_map/ppermute | solution.py:239
  103.7 23.6 %collective-permute-start.19 = (bf16[128,2048]{1,0:T(8,128)(2,1)}, bf16[128,2048]{1,0:T(8,128)(2,1)}, u32[]{:S(2)}, u32[]{:S(2)}) collective-permute-start(bf16[128,2048]{1,0:T(8,128)(2,1)} %collective-permute-done.1.refs_5_), channel_id=1, source_target_pairs={{0,4},{4,12},{12,20},{20,28},{28,24},{24,16},{16,8},{8,0},{1,5},{5... | collective-permute-start | bytes 1572872 | tf_op jit(solution)/shard_map/ppermute | solution.py:239
  105.8 21.6 %collective-permute-start.16 = (f32[8,128,128]{2,1,0:T(8,128)}, f32[8,128,128]{2,1,0:T(8,128)}, u32[]{:S(2)}, u32[]{:S(2)}) collective-permute-start(f32[8,128,128]{2,1,0:T(8,128)} %add_subtract_fusion), channel_id=1, source_target_pairs={{0,2},{2,0},{1,3},{3,1},{4,6},{6,4},{5,7},{7,5},{8,10},{10,8},{9,1... | collective-permute-start | bytes 1572872 | tf_op jit(solution)/shard_map/ppermute | solution.py:141
  107.0 26.2 %collective-permute-start.22 = (bf16[128,2048]{1,0:T(8,128)(2,1)}, bf16[128,2048]{1,0:T(8,128)(2,1)}, u32[]{:S(2)}, u32[]{:S(2)}) collective-permute-start(bf16[128,2048]{1,0:T(8,128)(2,1)} %collective-permute-done.2.refs_8_), channel_id=1, source_target_pairs={{4,0},{12,4},{20,12},{28,20},{24,28},{16,24},{8,16},{0,8},{5,1},{1... | collective-permute-start | bytes 1572872 | tf_op jit(solution)/shard_map/ppermute | solution.py:239
  116.1 22.5 %collective-permute-start.26 = (bf16[128,2048]{1,0:T(8,128)(2,1)}, bf16[128,2048]{1,0:T(8,128)(2,1)}, u32[]{:S(2)}, u32[]{:S(2)}) collective-permute-start(bf16[128,2048]{1,0:T(8,128)(2,1)} %collective-permute-done.18.refs_12_), channel_id=1, source_target_pairs={{0,4},{4,12},{12,20},{20,28},{28,24},{24,16},{16,8},{8,0},{1,5},{5... | collective-permute-start | bytes 1572872 | tf_op jit(solution)/shard_map/ppermute | solution.py:239
  118.2 35.0 %collective-permute-start.20 = (bf16[128,2048]{1,0:T(8,128)(2,1)}, bf16[128,2048]{1,0:T(8,128)(2,1)}, u32[]{:S(2)}, u32[]{:S(2)}) collective-permute-start(bf16[128,2048]{1,0:T(8,128)(2,1)} %collective-permute-done.18.refs_12_), channel_id=1, source_target_pairs={{0,2},{2,0},{1,3},{3,1},{4,6},{6,4},{5,7},{7,5},{8,10},{10,8},{9,1... | collective-permute-start | bytes 1572872 | tf_op jit(solution)/shard_map/ppermute | solution.py:275
  127.4 22.5 %collective-permute-start.27 = (bf16[128,2048]{1,0:T(8,128)(2,1)}, bf16[128,2048]{1,0:T(8,128)(2,1)}, u32[]{:S(2)}, u32[]{:S(2)}) collective-permute-start(bf16[128,2048]{1,0:T(8,128)(2,1)} %collective-permute-done.19.refs_13_), channel_id=1, source_target_pairs={{0,4},{4,12},{12,20},{20,28},{28,24},{24,16},{16,8},{8,0},{1,5},{5... | collective-permute-start | bytes 1572872 | tf_op jit(solution)/shard_map/ppermute | solution.py:239
  133.2 22.0 %collective-permute-start.21 = (bf16[128,2048]{1,0:T(8,128)(2,1)}, bf16[128,2048]{1,0:T(8,128)(2,1)S(1)}, u32[]{:S(2)}, u32[]{:S(2)}) collective-permute-start(bf16[128,2048]{1,0:T(8,128)(2,1)} %collective-permute-done.19.refs_13_), channel_id=1, source_target_pairs={{0,2},{2,0},{1,3},{3,1},{4,6},{6,4},{5,7},{7,5},{8,10},{10,8},{9,1... | collective-permute-start | bytes 1572872 | tf_op jit(solution)/shard_map/ppermute | solution.py:275
  139.9 15.6 %collective-permute-start.24 = (bf16[128,2048]{1,0:T(8,128)(2,1)}, bf16[128,2048]{1,0:T(8,128)(2,1)}, u32[]{:S(2)}, u32[]{:S(2)}) collective-permute-start(bf16[128,2048]{1,0:T(8,128)(2,1)} %collective-permute-done.22.refs_16_), channel_id=1, source_target_pairs={{0,2},{2,0},{1,3},{3,1},{4,6},{6,4},{5,7},{7,5},{8,10},{10,8},{9,1... | collective-permute-start | bytes 1572872 | tf_op jit(solution)/shard_map/ppermute | solution.py:275
  149.8 23.9 %collective-permute-start.17 = (bf16[256,2048]{1,0:T(8,128)(2,1)S(1)}, bf16[256,2048]{1,0:T(8,128)(2,1)S(1)}, u32[]{:S(2)}, u32[]{:S(2)}) collective-permute-start(bf16[256,2048]{1,0:T(8,128)(2,1)S(1)} %copy.39), channel_id=1, source_target_pairs={{0,1},{1,0},{2,3},{3,2},{4,5},{5,4},{6,7},{7,6},{8,9},{9,8},{10,11... | collective-permute-start | bytes 3145736 | tf_op jit(solution)/shard_map/ppermute | solution.py:127
  156.4 21.7 %collective-permute-start.33 = (bf16[128,2048]{1,0:T(8,128)(2,1)}, bf16[128,2048]{1,0:T(8,128)(2,1)}, u32[]{:S(2)}, u32[]{:S(2)}) collective-permute-start(bf16[128,2048]{1,0:T(8,128)(2,1)} %collective-permute-done.31.refs_25_), channel_id=1, source_target_pairs={{0,2},{2,0},{1,3},{3,1},{4,6},{6,4},{5,7},{7,5},{8,10},{10,8},{9,1... | collective-permute-start | bytes 1572872 | tf_op jit(solution)/shard_map/ppermute | solution.py:275
  (29 other events, 285.2 us)

commit v19 on v11

--- a/solution.py
+++ b/solution.py
@@ -170,14 +170,19 @@
                     ),
                 )
             )
-        for pair in copies:
-            for c in pair:
-                c.start()
+        def start_group(g):
+            for i in range(g, min(g + group, n)):
+                for c in copies[i]:
+                    c.start()
+
+        start_group(0)
+        start_group(group)
         for g in range(0, n, group):
             last = min(g + group, n)
             for i in range(g, last):
                 for c in copies[i]:
                     c.wait()
+            start_group(g + 2 * group)
             part = jnp.dot(
                 features[:, g * rows:last * rows],
                 weights[g * rows:last * rows, :],

time: 175 us -> 175 us (level)
  no operation moved by 1% of the time
where the time goes in v19:
time: 175 us; the launch traced here: 173 us
  waiting for transfers between devices  96.2 us (55%)
  starting transfers between devices  32 us (18%)
  local copies, waits for them, and re-layouts  20.8 us (12%)
  Pallas kernels  9.8 us (6%)
  other arithmetic  8.14 us (5%)
  matrix products  5.53 us (3%)
    ppermute x3, waiting for transfers between devices, exclusive_prefix(): total = total + lax.ppermute(total, axis, pairs)  38.6 us
    ppermute x3, waiting for transfers between devices, ring_step(): lax.ppermute(ahead, 'chip', forward)  29.2 us
    ppermute x2, waiting for transfers between devices, head_blocks(): other = lax.ppermute(sent, 'head', SWAP)  21.1 us
    pallas_call x1, Pallas kernels, project_blocks(): pl.pallas_call(kernel, out_shape=jax.ShapeDtypeStruct((tokens, cols), jnp...  9.8 us
    ppermute x5, starting transfers between devices, local_ring(): swapped += [lax.ppermute(w, 'core', SWAP) for w in got[len(swapped):]]  8.6 us
    ppermute x3, starting transfers between devices, exclusive_prefix(): total = total + lax.ppermute(total, axis, pairs)  8.4 us
    unnamed x28, local copies, waits for them, and re-layouts  7.43 us
    ppermute x1, waiting for transfers between devices, ring_step(): lax.ppermute(ahead[:half_rows], 'chip', forward)  3.52 us
  transfers between devices with their start and end apart: 24, of which 11 were waited for; matrix products, arithmetic and copies ran while one was open for 14% of the time, Pallas kernels for 0%

profile of v19, /device:TPU:13, one launch (start us, length us, event | category | flops | bytes accessed | tf_op | source)
XLA Modules:
  0.0 173.0 jit_solution(11271325232020717074)
XLA Ops:
  3.6 2.3 %copy.22 = bf16[2,128,1,2048]{3,1,0,2:T(8,128)(2,1)} copy(bf16[2,128,1,2048]{1,3,2,0:T(8,128)(2,1)} %get-tuple-element.30) | data formatting | bytes 2097152 | tf_op jit(solution)/shard_map/jit(dynamic_index_in_dim)/dynamic_slice | solution.py:37
  9.1 21.1 %collective-permute-done.2 = bf16[2,128,2048]{2,1,0:T(8,128)(2,1)S(1)} collective-permute-done((bf16[2,128,2048]{2,1,0:T(8,128)(2,1)}, bf16[2,128,2048]{2,1,0:T(8,128)(2,1)S(1)}, u32[]{:S(2)}, u32[]{:S(2)}) %collective-permute-start.2) | collective-permute-done | bytes 1048608 | tf_op jit(solution)/shard_map/ppermute | solution.py:38
  33.1 2.2 %collective-permute-start.3 = (f32[16,128,128]{2,1,0:T(8,128)S(1)}, f32[16,128,128]{2,1,0:T(8,128)}, u32[]{:S(2)}, u32[]{:S(2)}) collective-permute-start(f32[16,128,128]{2,1,0:T(8,128)S(1)} %fusion.6), channel_id=1, source_target_pairs={{0,2},{2,0},{1,3},{3,1},{4,6},{6,4},{5,7},{7,5},{8,10},{10,8},{9,1... | collective-permute-start | bytes 3145736 | tf_op jit(solution)/shard_map/ppermute | solution.py:133
  35.4 2.4 %collective-permute-done.3 = f32[16,128,128]{2,1,0:T(8,128)} collective-permute-done((f32[16,128,128]{2,1,0:T(8,128)S(1)}, f32[16,128,128]{2,1,0:T(8,128)}, u32[]{:S(2)}, u32[]{:S(2)}) %collective-permute-start.3) | collective-permute-done | bytes 1048608 | tf_op jit(solution)/shard_map/ppermute | solution.py:133
  38.9 2.0 %collective-permute-start.4 = (f32[8,128,128]{2,1,0:T(8,128)S(1)}, f32[8,128,128]{2,1,0:T(8,128)S(1)}, u32[]{:S(2)}, u32[]{:S(2)}) collective-permute-start(f32[8,128,128]{2,1,0:T(8,128)S(1)} %dynamic-slice_add_fusion), channel_id=1, source_target_pairs={{0,4},{4,8},{8,12},{12,16},{16,20},{20,24},{24,28},{1,5},{5,9},{9,... | collective-permute-start | bytes 1572872 | tf_op jit(solution)/shard_map/ppermute | solution.py:20
  42.6 11.3 %collective-permute-done.4 = f32[8,128,128]{2,1,0:T(8,128)S(1)} collective-permute-done((f32[8,128,128]{2,1,0:T(8,128)S(1)}, f32[8,128,128]{2,1,0:T(8,128)S(1)}, u32[]{:S(2)}, u32[]{:S(2)}) %collective-permute-start.4) | collective-permute-done | bytes 524320 | tf_op jit(solution)/shard_map/ppermute | solution.py:20
  54.0 3.2 %collective-permute-start.5 = (f32[8,128,128]{2,1,0:T(8,128)S(1)}, f32[8,128,128]{2,1,0:T(8,128)S(1)}, u32[]{:S(2)}, u32[]{:S(2)}) collective-permute-start(f32[8,128,128]{2,1,0:T(8,128)S(1)} %add.80), channel_id=1, source_target_pairs={{0,8},{4,12},{8,16},{12,20},{16,24},{20,28},{1,9},{5,13},{9,17},{1... | collective-permute-start | bytes 1572872 | tf_op jit(solution)/shard_map/ppermute | solution.py:20
  58.5 1.8 %collective-permute-start.8 = (bf16[256,2048]{1,0:T(8,128)(2,1)}, bf16[256,2048]{1,0:T(8,128)(2,1)}, u32[]{:S(2)}, u32[]{:S(2)}) collective-permute-start(bf16[256,2048]{1,0:T(8,128)(2,1)} %refs_0_.1), channel_id=1, source_target_pairs={{0,2},{2,0},{1,3},{3,1},{4,6},{6,4},{5,7},{7,5},{8,10},{10,8},{9,1... | collective-permute-start | bytes 3145736 | tf_op jit(solution)/shard_map/ppermute | solution.py:252
  61.1 7.0 %collective-permute-done.5 = f32[8,128,128]{2,1,0:T(8,128)S(1)} collective-permute-done((f32[8,128,128]{2,1,0:T(8,128)S(1)}, f32[8,128,128]{2,1,0:T(8,128)S(1)}, u32[]{:S(2)}, u32[]{:S(2)}) %collective-permute-start.5) | collective-permute-done | bytes 524320 | tf_op jit(solution)/shard_map/ppermute | solution.py:20
  68.1 3.2 %collective-permute-start.6 = (f32[8,128,128]{2,1,0:T(8,128)S(1)}, f32[8,128,128]{2,1,0:T(8,128)S(1)}, u32[]{:S(2)}, u32[]{:S(2)}) collective-permute-start(f32[8,128,128]{2,1,0:T(8,128)S(1)} %add.81), channel_id=1, source_target_pairs={{0,16},{4,20},{8,24},{12,28},{1,17},{5,21},{9,25},{13,29},{2,18},{... | collective-permute-start | bytes 1572872 | tf_op jit(solution)/shard_map/ppermute | solution.py:20
  72.8 20.3 %collective-permute-done.6 = f32[8,128,128]{2,1,0:T(8,128)S(1)} collective-permute-done((f32[8,128,128]{2,1,0:T(8,128)S(1)}, f32[8,128,128]{2,1,0:T(8,128)S(1)}, u32[]{:S(2)}, u32[]{:S(2)}) %collective-permute-start.6) | collective-permute-done | bytes 524320 | tf_op jit(solution)/shard_map/ppermute | solution.py:20
  94.0 3.2 %fusion.1 = f32[256,16,128]{0,2,1:T(8,128)S(1)} fusion(bf16[256,16,128]{0,2,1:T(8,128)(2,1)} %bitcast.49, bf16[256,16,128]{0,2,1:T(8,128)(2,1)} %bitcast.54, pred[256,256]{1,0:T(8,128)(4,1)S(1)} %iota_compare_fusion, bf16[256,2048]{1,0:T(8,128)(2,1)} %copy-done.2), kind=kOutput, calls=%fused_computation.13 | convolution fusion | flops 538968064 | bytes 5308416 | tf_op jit(solution)/shard_map/hts,she->the/dot_general | solution.py:106
  98.6 2.7 %collective-permute-start.11 = (f32[8,128,128]{2,1,0:T(8,128)S(1)}, f32[8,128,128]{2,1,0:T(8,128)S(1)}, u32[]{:S(2)}, u32[]{:S(2)}) collective-permute-start(f32[8,128,128]{2,1,0:T(8,128)S(1)} %add_subtract_fusion), channel_id=1, source_target_pairs={{0,2},{2,0},{1,3},{3,1},{4,6},{6,4},{5,7},{7,5},{8,10},{10,8},{9,1... | collective-permute-start | bytes 1572872 | tf_op jit(solution)/shard_map/ppermute | solution.py:141
  102.5 13.2 %collective-permute-done.13.refs_6_ = bf16[256,2048]{1,0:T(8,128)(2,1)} collective-permute-done((bf16[256,2048]{1,0:T(8,128)(2,1)}, bf16[256,2048]{1,0:T(8,128)(2,1)}, u32[]{:S(2)}, u32[]{:S(2)}) %collective-permute-start.13) | collective-permute-done | bytes 1048608 | tf_op jit(solution)/shard_map/ppermute | solution.py:85
  115.7 2.2 %collective-permute-start.17 = (bf16[256,2048]{1,0:T(8,128)(2,1)}, bf16[256,2048]{1,0:T(8,128)(2,1)}, u32[]{:S(2)}, u32[]{:S(2)}) collective-permute-start(bf16[256,2048]{1,0:T(8,128)(2,1)} %collective-permute-done.13.refs_6_), channel_id=1, source_target_pairs={{0,4},{4,12},{12,20},{20,28},{28,24},{24,16},{16,8},{8,0},{1,5},{5... | collective-permute-start | bytes 3145736 | tf_op jit(solution)/shard_map/ppermute | solution.py:85
  118.1 1.8 %multiply_reduce_fusion = (f32[256,16]{0,1:T(8,128)S(1)}, f32[16,128,256]{2,1,0:T(8,128)S(1)}) fusion(f32[256,16,128]{0,2,1:T(8,128)S(1)} %fusion.1, bf16[256,16,128]{0,2,1:T(8,128)(2,1)S(1)} %bitcast.55, f32[8,128,128]{2,1,0:T(8,128)S(1)} %get-tuple-element.32, f32[8,128,128]{2,1,0:T(8,128)S(1)} %get-tuple-element.31, ...), kind=kOutput, calls=%fused_computation.11 | convolution fusion | flops 136835072 | bytes 7356417 | tf_op jit(solution)/shard_map/thd,hde->the/dot_general | solution.py:115
  123.8 15.4 %collective-permute-done.17.refs_10_ = bf16[256,2048]{1,0:T(8,128)(2,1)} collective-permute-done((bf16[256,2048]{1,0:T(8,128)(2,1)}, bf16[256,2048]{1,0:T(8,128)(2,1)}, u32[]{:S(2)}, u32[]{:S(2)}) %collective-permute-start.17) | collective-permute-done | bytes 1048608 | tf_op jit(solution)/shard_map/ppermute | solution.py:85
  140.3 2.3 %collective-permute-start.21 = (bf16[128,2048]{1,0:T(8,128)(2,1)S(1)}, bf16[128,2048]{1,0:T(8,128)(2,1)S(1)}, u32[]{:S(2)}, u32[]{:S(2)}) collective-permute-start(bf16[128,2048]{1,0:T(8,128)(2,1)S(1)} %slice.20), channel_id=1, source_target_pairs={{0,4},{4,12},{12,20},{20,28},{28,24},{24,16},{16,8},{8,0},{1,5},{5... | collective-permute-start | bytes 1572872 | tf_op jit(solution)/shard_map/ppermute | solution.py:82
  142.5 1.9 %slice.21 = bf16[128,2048]{1,0:T(8,128)(2,1)} slice(bf16[256,2048]{1,0:T(8,128)(2,1)} %collective-permute-done.19.refs_12_), slice={[128:256], [0:2048]} | slice | bytes 1048576 | tf_op jit(solution)/shard_map/slice | solution.py:83
  145.2 2.7 %collective-permute-start.14 = (bf16[256,2048]{1,0:T(8,128)(2,1)}, bf16[256,2048]{1,0:T(8,128)(2,1)}, u32[]{:S(2)}, u32[]{:S(2)}) collective-permute-start(bf16[256,2048]{1,0:T(8,128)(2,1)} %collective-permute-done.13.refs_6_), channel_id=1, source_target_pairs={{0,2},{2,0},{1,3},{3,1},{4,6},{6,4},{5,7},{7,5},{8,10},{10,8},{9,1... | collective-permute-start | bytes 3145736 | tf_op jit(solution)/shard_map/ppermute | solution.py:271
  147.9 3.5 %collective-permute-done.21 = bf16[128,2048]{1,0:T(8,128)(2,1)S(1)} collective-permute-done((bf16[128,2048]{1,0:T(8,128)(2,1)S(1)}, bf16[128,2048]{1,0:T(8,128)(2,1)S(1)}, u32[]{:S(2)}, u32[]{:S(2)}) %collective-permute-start.21) | collective-permute-done | bytes 524320 | tf_op jit(solution)/shard_map/ppermute | solution.py:82
  152.2 3.3 %collective-permute-start.18 = (bf16[256,2048]{1,0:T(8,128)(2,1)}, bf16[256,2048]{1,0:T(8,128)(2,1)}, u32[]{:S(2)}, u32[]{:S(2)}) collective-permute-start(bf16[256,2048]{1,0:T(8,128)(2,1)} %collective-permute-done.17.refs_10_), channel_id=1, source_target_pairs={{0,2},{2,0},{1,3},{3,1},{4,6},{6,4},{5,7},{7,5},{8,10},{10,8},{9,1... | collective-permute-start | bytes 3145736 | tf_op jit(solution)/shard_map/ppermute | solution.py:271
  156.5 2.6 %collective-permute-start.20 = (bf16[256,2048]{1,0:T(8,128)(2,1)}, bf16[256,2048]{1,0:T(8,128)(2,1)}, u32[]{:S(2)}, u32[]{:S(2)}) collective-permute-start(bf16[256,2048]{1,0:T(8,128)(2,1)} %collective-permute-done.19.refs_12_), channel_id=1, source_target_pairs={{0,2},{2,0},{1,3},{3,1},{4,6},{6,4},{5,7},{7,5},{8,10},{10,8},{9,1... | collective-permute-start | bytes 3145736 | tf_op jit(solution)/shard_map/ppermute | solution.py:271
  163.1 9.8 %shard_map.82 = bf16[256,2048]{1,0:T(8,128)(2,1)} custom-call(s32[16]{0:T(128)} %mul.41.starts_ref, bf16[256,4096]{1,0:T(8,128)(2,1)} %pad_maximum_fusion.normed_ref, bf16[256,2048]{1,0:T(8,128)(2,1)} %refs_0_.1, bf16[256,2048]{1,0:T(8,128)(2,1)} %collective-permute-done.8.refs_1_, bf16[256,2048]{1,0:T(8,128)(2,1)} %collective-permute-done.refs_2_, ...), custom_call_target="tpu_custom_call" | custom-call | tf_op jit(solution)/shard_map/pallas_call | solution.py:197
  (90 shorter events, 31.0 us)
Async XLA Ops:
  5.9 24.3 %collective-permute-start.2 = (bf16[2,128,2048]{2,1,0:T(8,128)(2,1)}, bf16[2,128,2048]{2,1,0:T(8,128)(2,1)S(1)}, u32[]{:S(2)}, u32[]{:S(2)}) collective-permute-start(bf16[2,128,2048]{2,1,0:T(8,128)(2,1)} %bitcast.6), channel_id=1, source_target_pairs={{0,1},{1,0},{2,3},{3,2},{4,5},{5,4},{6,7},{7,6},{8,9},{9,8},{10,11... | collective-permute-start | bytes 3145736 | tf_op jit(solution)/shard_map/ppermute | solution.py:38
  7.1 24.0 %collective-permute-start = (bf16[256,2048]{1,0:T(8,128)(2,1)}, bf16[256,2048]{1,0:T(8,128)(2,1)}, u32[]{:S(2)}, u32[]{:S(2)}) collective-permute-start(bf16[256,2048]{1,0:T(8,128)(2,1)} %refs_0_.1), channel_id=1, source_target_pairs={{0,4},{4,12},{12,20},{20,28},{28,24},{24,16},{16,8},{8,0},{1,5},{5... | collective-permute-start | bytes 3145736 | tf_op jit(solution)/shard_map/ppermute | solution.py:85
  8.4 23.7 %collective-permute-start.1 = (bf16[256,2048]{1,0:T(8,128)(2,1)}, bf16[256,2048]{1,0:T(8,128)(2,1)}, u32[]{:S(2)}, u32[]{:S(2)}) collective-permute-start(bf16[256,2048]{1,0:T(8,128)(2,1)} %refs_0_.1), channel_id=1, source_target_pairs={{4,0},{12,4},{20,12},{28,20},{24,28},{16,24},{8,16},{0,8},{5,1},{1... | collective-permute-start | bytes 3145736 | tf_op jit(solution)/shard_map/ppermute | solution.py:85
  33.1 4.6 %collective-permute-start.3 = (f32[16,128,128]{2,1,0:T(8,128)S(1)}, f32[16,128,128]{2,1,0:T(8,128)}, u32[]{:S(2)}, u32[]{:S(2)}) collective-permute-start(f32[16,128,128]{2,1,0:T(8,128)S(1)} %fusion.6), channel_id=1, source_target_pairs={{0,2},{2,0},{1,3},{3,1},{4,6},{6,4},{5,7},{7,5},{8,10},{10,8},{9,1... | collective-permute-start | bytes 3145736 | tf_op jit(solution)/shard_map/ppermute | solution.py:133
  38.9 15.0 %collective-permute-start.4 = (f32[8,128,128]{2,1,0:T(8,128)S(1)}, f32[8,128,128]{2,1,0:T(8,128)S(1)}, u32[]{:S(2)}, u32[]{:S(2)}) collective-permute-start(f32[8,128,128]{2,1,0:T(8,128)S(1)} %dynamic-slice_add_fusion), channel_id=1, source_target_pairs={{0,4},{4,8},{8,12},{12,16},{16,20},{20,24},{24,28},{1,5},{5,9},{9,... | collective-permute-start | bytes 1572872 | tf_op jit(solution)/shard_map/ppermute | solution.py:20
  54.0 14.1 %collective-permute-start.5 = (f32[8,128,128]{2,1,0:T(8,128)S(1)}, f32[8,128,128]{2,1,0:T(8,128)S(1)}, u32[]{:S(2)}, u32[]{:S(2)}) collective-permute-start(f32[8,128,128]{2,1,0:T(8,128)S(1)} %add.80), channel_id=1, source_target_pairs={{0,8},{4,12},{8,16},{12,20},{16,24},{20,28},{1,9},{5,13},{9,17},{1... | collective-permute-start | bytes 1572872 | tf_op jit(solution)/shard_map/ppermute | solution.py:20
  58.2 13.1 %collective-permute-start.7 = (bf16[1,128,2048]{2,1,0:T(8,128)(2,1)}, bf16[1,128,2048]{2,1,0:T(8,128)(2,1)S(1)}, u32[]{:S(2)}, u32[]{:S(2)}) collective-permute-start(bf16[1,128,2048]{2,1,0:T(8,128)(2,1)} %bitcast.11), channel_id=1, source_target_pairs={{0,1},{1,0},{2,3},{3,2},{4,5},{5,4},{6,7},{7,6},{8,9},{9,8},{10,11... | collective-permute-start | bytes 1572872 | tf_op jit(solution)/shard_map/ppermute | solution.py:38
  58.5 40.1 %collective-permute-start.8 = (bf16[256,2048]{1,0:T(8,128)(2,1)}, bf16[256,2048]{1,0:T(8,128)(2,1)}, u32[]{:S(2)}, u32[]{:S(2)}) collective-permute-start(bf16[256,2048]{1,0:T(8,128)(2,1)} %refs_0_.1), channel_id=1, source_target_pairs={{0,2},{2,0},{1,3},{3,1},{4,6},{6,4},{5,7},{7,5},{8,10},{10,8},{9,1... | collective-permute-start | bytes 3145736 | tf_op jit(solution)/shard_map/ppermute | solution.py:252
  60.5 38.1 %collective-permute-start.10 = (bf16[256,2048]{1,0:T(8,128)(2,1)}, bf16[256,2048]{1,0:T(8,128)(2,1)}, u32[]{:S(2)}, u32[]{:S(2)}) collective-permute-start(bf16[256,2048]{1,0:T(8,128)(2,1)} %collective-permute-done.1.refs_4_), channel_id=1, source_target_pairs={{0,2},{2,0},{1,3},{3,1},{4,6},{6,4},{5,7},{7,5},{8,10},{10,8},{9,1... | collective-permute-start | bytes 3145736 | tf_op jit(solution)/shard_map/ppermute | solution.py:252
  60.6 38.0 %collective-permute-start.9 = (bf16[256,2048]{1,0:T(8,128)(2,1)}, bf16[256,2048]{1,0:T(8,128)(2,1)}, u32[]{:S(2)}, u32[]{:S(2)}) collective-permute-start(bf16[256,2048]{1,0:T(8,128)(2,1)} %collective-permute-done.refs_2_), channel_id=1, source_target_pairs={{0,2},{2,0},{1,3},{3,1},{4,6},{6,4},{5,7},{7,5},{8,10},{10,8},{9,1... | collective-permute-start | bytes 3145736 | tf_op jit(solution)/shard_map/ppermute | solution.py:252
  68.1 25.0 %collective-permute-start.6 = (f32[8,128,128]{2,1,0:T(8,128)S(1)}, f32[8,128,128]{2,1,0:T(8,128)S(1)}, u32[]{:S(2)}, u32[]{:S(2)}) collective-permute-start(f32[8,128,128]{2,1,0:T(8,128)S(1)} %add.81), channel_id=1, source_target_pairs={{0,16},{4,20},{8,24},{12,28},{1,17},{5,21},{9,25},{13,29},{2,18},{... | collective-permute-start | bytes 1572872 | tf_op jit(solution)/shard_map/ppermute | solution.py:20
  72.8 42.9 %collective-permute-start.13 = (bf16[256,2048]{1,0:T(8,128)(2,1)}, bf16[256,2048]{1,0:T(8,128)(2,1)}, u32[]{:S(2)}, u32[]{:S(2)}) collective-permute-start(bf16[256,2048]{1,0:T(8,128)(2,1)} %collective-permute-done.refs_2_), channel_id=1, source_target_pairs={{0,4},{4,12},{12,20},{20,28},{28,24},{24,16},{16,8},{8,0},{1,5},{5... | collective-permute-start | bytes 3145736 | tf_op jit(solution)/shard_map/ppermute | solution.py:85
  93.2 24.8 %collective-permute-start.15 = (bf16[256,2048]{1,0:T(8,128)(2,1)}, bf16[256,2048]{1,0:T(8,128)(2,1)}, u32[]{:S(2)}, u32[]{:S(2)}) collective-permute-start(bf16[256,2048]{1,0:T(8,128)(2,1)} %collective-permute-done.1.refs_4_), channel_id=1, source_target_pairs={{4,0},{12,4},{20,12},{28,20},{24,28},{16,24},{8,16},{0,8},{5,1},{1... | collective-permute-start | bytes 3145736 | tf_op jit(solution)/shard_map/ppermute | solution.py:85
  98.6 19.4 %collective-permute-start.11 = (f32[8,128,128]{2,1,0:T(8,128)S(1)}, f32[8,128,128]{2,1,0:T(8,128)S(1)}, u32[]{:S(2)}, u32[]{:S(2)}) collective-permute-start(f32[8,128,128]{2,1,0:T(8,128)S(1)} %add_subtract_fusion), channel_id=1, source_target_pairs={{0,2},{2,0},{1,3},{3,1},{4,6},{6,4},{5,7},{7,5},{8,10},{10,8},{9,1... | collective-permute-start | bytes 1572872 | tf_op jit(solution)/shard_map/ppermute | solution.py:141
  115.7 23.4 %collective-permute-start.17 = (bf16[256,2048]{1,0:T(8,128)(2,1)}, bf16[256,2048]{1,0:T(8,128)(2,1)}, u32[]{:S(2)}, u32[]{:S(2)}) collective-permute-start(bf16[256,2048]{1,0:T(8,128)(2,1)} %collective-permute-done.13.refs_6_), channel_id=1, source_target_pairs={{0,4},{4,12},{12,20},{20,28},{28,24},{24,16},{16,8},{8,0},{1,5},{5... | collective-permute-start | bytes 3145736 | tf_op jit(solution)/shard_map/ppermute | solution.py:85
  117.9 24.6 %collective-permute-start.19 = (bf16[256,2048]{1,0:T(8,128)(2,1)}, bf16[256,2048]{1,0:T(8,128)(2,1)}, u32[]{:S(2)}, u32[]{:S(2)}) collective-permute-start(bf16[256,2048]{1,0:T(8,128)(2,1)} %collective-permute-done.15.refs_8_), channel_id=1, source_target_pairs={{4,0},{12,4},{20,12},{28,20},{24,28},{16,24},{8,16},{0,8},{5,1},{1... | collective-permute-start | bytes 3145736 | tf_op jit(solution)/shard_map/ppermute | solution.py:85
  122.8 37.4 %collective-permute-start.12 = (bf16[256,2048]{1,0:T(8,128)(2,1)S(1)}, bf16[256,2048]{1,0:T(8,128)(2,1)S(1)}, u32[]{:S(2)}, u32[]{:S(2)}) collective-permute-start(bf16[256,2048]{1,0:T(8,128)(2,1)S(1)} %copy.38), channel_id=1, source_target_pairs={{0,1},{1,0},{2,3},{3,2},{4,5},{5,4},{6,7},{7,6},{8,9},{9,8},{10,11... | collective-permute-start | bytes 3145736 | tf_op jit(solution)/shard_map/ppermute | solution.py:127
  140.3 11.1 %collective-permute-start.21 = (bf16[128,2048]{1,0:T(8,128)(2,1)S(1)}, bf16[128,2048]{1,0:T(8,128)(2,1)S(1)}, u32[]{:S(2)}, u32[]{:S(2)}) collective-permute-start(bf16[128,2048]{1,0:T(8,128)(2,1)S(1)} %slice.20), channel_id=1, source_target_pairs={{0,4},{4,12},{12,20},{20,28},{28,24},{24,16},{16,8},{8,0},{1,5},{5... | collective-permute-start | bytes 1572872 | tf_op jit(solution)/shard_map/ppermute | solution.py:82
  144.4 12.1 %collective-permute-start.22 = (bf16[128,2048]{1,0:T(8,128)(2,1)}, bf16[128,2048]{1,0:T(8,128)(2,1)}, u32[]{:S(2)}, u32[]{:S(2)}) collective-permute-start(bf16[128,2048]{1,0:T(8,128)(2,1)} %slice.21), channel_id=1, source_target_pairs={{4,0},{12,4},{20,12},{28,20},{24,28},{16,24},{8,16},{0,8},{5,1},{1... | collective-permute-start | bytes 1572872 | tf_op jit(solution)/shard_map/ppermute | solution.py:82
  145.2 17.6 %collective-permute-start.14 = (bf16[256,2048]{1,0:T(8,128)(2,1)}, bf16[256,2048]{1,0:T(8,128)(2,1)}, u32[]{:S(2)}, u32[]{:S(2)}) collective-permute-start(bf16[256,2048]{1,0:T(8,128)(2,1)} %collective-permute-done.13.refs_6_), channel_id=1, source_target_pairs={{0,2},{2,0},{1,3},{3,1},{4,6},{6,4},{5,7},{7,5},{8,10},{10,8},{9,1... | collective-permute-start | bytes 3145736 | tf_op jit(solution)/shard_map/ppermute | solution.py:271
  147.9 14.9 %collective-permute-start.16 = (bf16[256,2048]{1,0:T(8,128)(2,1)}, bf16[256,2048]{1,0:T(8,128)(2,1)}, u32[]{:S(2)}, u32[]{:S(2)}) collective-permute-start(bf16[256,2048]{1,0:T(8,128)(2,1)} %collective-permute-done.15.refs_8_), channel_id=1, source_target_pairs={{0,2},{2,0},{1,3},{3,1},{4,6},{6,4},{5,7},{7,5},{8,10},{10,8},{9,1... | collective-permute-start | bytes 3145736 | tf_op jit(solution)/shard_map/ppermute | solution.py:271
  152.2 10.5 %collective-permute-start.18 = (bf16[256,2048]{1,0:T(8,128)(2,1)}, bf16[256,2048]{1,0:T(8,128)(2,1)}, u32[]{:S(2)}, u32[]{:S(2)}) collective-permute-start(bf16[256,2048]{1,0:T(8,128)(2,1)} %collective-permute-done.17.refs_10_), channel_id=1, source_target_pairs={{0,2},{2,0},{1,3},{3,1},{4,6},{6,4},{5,7},{7,5},{8,10},{10,8},{9,1... | collective-permute-start | bytes 3145736 | tf_op jit(solution)/shard_map/ppermute | solution.py:271
  156.5 6.2 %collective-permute-start.20 = (bf16[256,2048]{1,0:T(8,128)(2,1)}, bf16[256,2048]{1,0:T(8,128)(2,1)}, u32[]{:S(2)}, u32[]{:S(2)}) collective-permute-start(bf16[256,2048]{1,0:T(8,128)(2,1)} %collective-permute-done.19.refs_12_), channel_id=1, source_target_pairs={{0,2},{2,0},{1,3},{3,1},{4,6},{6,4},{5,7},{7,5},{8,10},{10,8},{9,1... | collective-permute-start | bytes 3145736 | tf_op jit(solution)/shard_map/ppermute | solution.py:271
  160.2 2.9 %collective-permute-start.23 = (bf16[256,2048]{1,0:T(8,128)(2,1)S(1)}, bf16[256,2048]{1,0:T(8,128)(2,1)}, u32[]{:S(2)}, u32[]{:S(2)}) collective-permute-start(bf16[256,2048]{1,0:T(8,128)(2,1)S(1)} %constant_dynamic-update-slice_fusion.refs_14_), channel_id=1, source_target_pairs={{0,2},{2,0},{1,3},{3,1},{4,6},{6,4},{5,7},{7,5},{8,10},{10,8},{9,1... | collective-permute-start | bytes 3145736 | tf_op jit(solution)/shard_map/ppermute | solution.py:271
  (12 other events, 42.2 us)

commit v20 on v11

--- a/solution.py
+++ b/solution.py
@@ -272,7 +272,7 @@
     sources = jnp.asarray(order, jnp.int32)[(ring_place - jnp.asarray(offsets, jnp.int32)) % n_chip]
     cores = jnp.stack([core, 1 - core]).astype(jnp.int32)
     starts = ((sources[:, None] * 2 + cores[None, :]) * out_weight.shape[0]).reshape(-1)
-    return project_blocks(gathered, starts, [w for pair in zip(got, swapped) for w in pair])
+    return project_blocks(gathered, starts, [w for pair in zip(got, swapped) for w in pair], group=16)
 
 
 def solution(mesh):

time: 175 us -> 178 us (1.017)
  Pallas kernels: 9.62 us -> 12.9 us
    pallas_call x1, Pallas kernels: 9.62 us -> 12.9 us  [project_blocks(): pl.pallas_call(kernel, out_shape=jax.ShapeDtypeStruct((tokens, cols), jnp...]
where the time goes in v20:
time: 178 us; the launch traced here: 176 us
  waiting for transfers between devices  96.2 us (54%)
  starting transfers between devices  32 us (18%)
  local copies, waits for them, and re-layouts  20.8 us (12%)
  Pallas kernels  12.9 us (7%)
  other arithmetic  8.14 us (5%)
  matrix products  5.53 us (3%)
    ppermute x3, waiting for transfers between devices, exclusive_prefix(): total = total + lax.ppermute(total, axis, pairs)  38.6 us
    ppermute x3, waiting for transfers between devices, ring_step(): lax.ppermute(ahead, 'chip', forward)  29.2 us
    ppermute x2, waiting for transfers between devices, head_blocks(): other = lax.ppermute(sent, 'head', SWAP)  21.1 us
    pallas_call x1, Pallas kernels, project_blocks(): pl.pallas_call(kernel, out_shape=jax.ShapeDtypeStruct((tokens, cols), jnp...  12.9 us
    ppermute x5, starting transfers between devices, local_ring(): swapped += [lax.ppermute(w, 'core', SWAP) for w in got[len(swapped):]]  8.6 us
    ppermute x3, starting transfers between devices, exclusive_prefix(): total = total + lax.ppermute(total, axis, pairs)  8.4 us
    unnamed x28, local copies, waits for them, and re-layouts  7.43 us
  transfers between devices with their start and end apart: 24, of which 11 were waited for; matrix products, arithmetic and copies ran while one was open for 14% of the time, Pallas kernels for 0%

profile of v20, /device:TPU:13, one launch (start us, length us, event | category | flops | bytes accessed | tf_op | source)
XLA Modules:
  0.0 176.1 jit_solution(3895300198871851457)
XLA Ops:
  3.6 2.3 %copy.22 = bf16[2,128,1,2048]{3,1,0,2:T(8,128)(2,1)} copy(bf16[2,128,1,2048]{1,3,2,0:T(8,128)(2,1)} %get-tuple-element.30) | data formatting | bytes 2097152 | tf_op jit(solution)/shard_map/jit(dynamic_index_in_dim)/dynamic_slice | solution.py:37
  9.1 21.1 %collective-permute-done.2 = bf16[2,128,2048]{2,1,0:T(8,128)(2,1)S(1)} collective-permute-done((bf16[2,128,2048]{2,1,0:T(8,128)(2,1)}, bf16[2,128,2048]{2,1,0:T(8,128)(2,1)S(1)}, u32[]{:S(2)}, u32[]{:S(2)}) %collective-permute-start.2) | collective-permute-done | bytes 1048608 | tf_op jit(solution)/shard_map/ppermute | solution.py:38
  33.1 2.2 %collective-permute-start.3 = (f32[16,128,128]{2,1,0:T(8,128)S(1)}, f32[16,128,128]{2,1,0:T(8,128)}, u32[]{:S(2)}, u32[]{:S(2)}) collective-permute-start(f32[16,128,128]{2,1,0:T(8,128)S(1)} %fusion.6), channel_id=1, source_target_pairs={{0,2},{2,0},{1,3},{3,1},{4,6},{6,4},{5,7},{7,5},{8,10},{10,8},{9,1... | collective-permute-start | bytes 3145736 | tf_op jit(solution)/shard_map/ppermute | solution.py:133
  35.4 2.4 %collective-permute-done.3 = f32[16,128,128]{2,1,0:T(8,128)} collective-permute-done((f32[16,128,128]{2,1,0:T(8,128)S(1)}, f32[16,128,128]{2,1,0:T(8,128)}, u32[]{:S(2)}, u32[]{:S(2)}) %collective-permute-start.3) | collective-permute-done | bytes 1048608 | tf_op jit(solution)/shard_map/ppermute | solution.py:133
  38.9 2.0 %collective-permute-start.4 = (f32[8,128,128]{2,1,0:T(8,128)S(1)}, f32[8,128,128]{2,1,0:T(8,128)S(1)}, u32[]{:S(2)}, u32[]{:S(2)}) collective-permute-start(f32[8,128,128]{2,1,0:T(8,128)S(1)} %dynamic-slice_add_fusion), channel_id=1, source_target_pairs={{0,4},{4,8},{8,12},{12,16},{16,20},{20,24},{24,28},{1,5},{5,9},{9,... | collective-permute-start | bytes 1572872 | tf_op jit(solution)/shard_map/ppermute | solution.py:20
  42.6 11.3 %collective-permute-done.4 = f32[8,128,128]{2,1,0:T(8,128)S(1)} collective-permute-done((f32[8,128,128]{2,1,0:T(8,128)S(1)}, f32[8,128,128]{2,1,0:T(8,128)S(1)}, u32[]{:S(2)}, u32[]{:S(2)}) %collective-permute-start.4) | collective-permute-done | bytes 524320 | tf_op jit(solution)/shard_map/ppermute | solution.py:20
  54.0 3.2 %collective-permute-start.5 = (f32[8,128,128]{2,1,0:T(8,128)S(1)}, f32[8,128,128]{2,1,0:T(8,128)S(1)}, u32[]{:S(2)}, u32[]{:S(2)}) collective-permute-start(f32[8,128,128]{2,1,0:T(8,128)S(1)} %add.80), channel_id=1, source_target_pairs={{0,8},{4,12},{8,16},{12,20},{16,24},{20,28},{1,9},{5,13},{9,17},{1... | collective-permute-start | bytes 1572872 | tf_op jit(solution)/shard_map/ppermute | solution.py:20
  58.5 1.8 %collective-permute-start.8 = (bf16[256,2048]{1,0:T(8,128)(2,1)}, bf16[256,2048]{1,0:T(8,128)(2,1)}, u32[]{:S(2)}, u32[]{:S(2)}) collective-permute-start(bf16[256,2048]{1,0:T(8,128)(2,1)} %refs_0_.1), channel_id=1, source_target_pairs={{0,2},{2,0},{1,3},{3,1},{4,6},{6,4},{5,7},{7,5},{8,10},{10,8},{9,1... | collective-permute-start | bytes 3145736 | tf_op jit(solution)/shard_map/ppermute | solution.py:247
  61.1 7.0 %collective-permute-done.5 = f32[8,128,128]{2,1,0:T(8,128)S(1)} collective-permute-done((f32[8,128,128]{2,1,0:T(8,128)S(1)}, f32[8,128,128]{2,1,0:T(8,128)S(1)}, u32[]{:S(2)}, u32[]{:S(2)}) %collective-permute-start.5) | collective-permute-done | bytes 524320 | tf_op jit(solution)/shard_map/ppermute | solution.py:20
  68.1 3.2 %collective-permute-start.6 = (f32[8,128,128]{2,1,0:T(8,128)S(1)}, f32[8,128,128]{2,1,0:T(8,128)S(1)}, u32[]{:S(2)}, u32[]{:S(2)}) collective-permute-start(f32[8,128,128]{2,1,0:T(8,128)S(1)} %add.81), channel_id=1, source_target_pairs={{0,16},{4,20},{8,24},{12,28},{1,17},{5,21},{9,25},{13,29},{2,18},{... | collective-permute-start | bytes 1572872 | tf_op jit(solution)/shard_map/ppermute | solution.py:20
  72.8 20.3 %collective-permute-done.6 = f32[8,128,128]{2,1,0:T(8,128)S(1)} collective-permute-done((f32[8,128,128]{2,1,0:T(8,128)S(1)}, f32[8,128,128]{2,1,0:T(8,128)S(1)}, u32[]{:S(2)}, u32[]{:S(2)}) %collective-permute-start.6) | collective-permute-done | bytes 524320 | tf_op jit(solution)/shard_map/ppermute | solution.py:20
  94.0 3.2 %fusion.1 = f32[256,16,128]{0,2,1:T(8,128)S(1)} fusion(bf16[256,16,128]{0,2,1:T(8,128)(2,1)} %bitcast.49, bf16[256,16,128]{0,2,1:T(8,128)(2,1)} %bitcast.54, pred[256,256]{1,0:T(8,128)(4,1)S(1)} %iota_compare_fusion, bf16[256,2048]{1,0:T(8,128)(2,1)} %copy-done.2), kind=kOutput, calls=%fused_computation.13 | convolution fusion | flops 538968064 | bytes 5308416 | tf_op jit(solution)/shard_map/hts,she->the/dot_general | solution.py:106
  98.6 2.7 %collective-permute-start.11 = (f32[8,128,128]{2,1,0:T(8,128)S(1)}, f32[8,128,128]{2,1,0:T(8,128)S(1)}, u32[]{:S(2)}, u32[]{:S(2)}) collective-permute-start(f32[8,128,128]{2,1,0:T(8,128)S(1)} %add_subtract_fusion), channel_id=1, source_target_pairs={{0,2},{2,0},{1,3},{3,1},{4,6},{6,4},{5,7},{7,5},{8,10},{10,8},{9,1... | collective-permute-start | bytes 1572872 | tf_op jit(solution)/shard_map/ppermute | solution.py:141
  102.5 13.2 %collective-permute-done.13.refs_6_ = bf16[256,2048]{1,0:T(8,128)(2,1)} collective-permute-done((bf16[256,2048]{1,0:T(8,128)(2,1)}, bf16[256,2048]{1,0:T(8,128)(2,1)}, u32[]{:S(2)}, u32[]{:S(2)}) %collective-permute-start.13) | collective-permute-done | bytes 1048608 | tf_op jit(solution)/shard_map/ppermute | solution.py:85
  115.7 2.2 %collective-permute-start.17 = (bf16[256,2048]{1,0:T(8,128)(2,1)}, bf16[256,2048]{1,0:T(8,128)(2,1)}, u32[]{:S(2)}, u32[]{:S(2)}) collective-permute-start(bf16[256,2048]{1,0:T(8,128)(2,1)} %collective-permute-done.13.refs_6_), channel_id=1, source_target_pairs={{0,4},{4,12},{12,20},{20,28},{28,24},{24,16},{16,8},{8,0},{1,5},{5... | collective-permute-start | bytes 3145736 | tf_op jit(solution)/shard_map/ppermute | solution.py:85
  118.1 1.8 %multiply_reduce_fusion = (f32[256,16]{0,1:T(8,128)S(1)}, f32[16,128,256]{2,1,0:T(8,128)S(1)}) fusion(f32[256,16,128]{0,2,1:T(8,128)S(1)} %fusion.1, bf16[256,16,128]{0,2,1:T(8,128)(2,1)S(1)} %bitcast.55, f32[8,128,128]{2,1,0:T(8,128)S(1)} %get-tuple-element.32, f32[8,128,128]{2,1,0:T(8,128)S(1)} %get-tuple-element.31, ...), kind=kOutput, calls=%fused_computation.11 | convolution fusion | flops 136835072 | bytes 7356417 | tf_op jit(solution)/shard_map/thd,hde->the/dot_general | solution.py:115
  123.8 15.4 %collective-permute-done.17.refs_10_ = bf16[256,2048]{1,0:T(8,128)(2,1)} collective-permute-done((bf16[256,2048]{1,0:T(8,128)(2,1)}, bf16[256,2048]{1,0:T(8,128)(2,1)}, u32[]{:S(2)}, u32[]{:S(2)}) %collective-permute-start.17) | collective-permute-done | bytes 1048608 | tf_op jit(solution)/shard_map/ppermute | solution.py:85
  140.3 2.3 %collective-permute-start.21 = (bf16[128,2048]{1,0:T(8,128)(2,1)S(1)}, bf16[128,2048]{1,0:T(8,128)(2,1)S(1)}, u32[]{:S(2)}, u32[]{:S(2)}) collective-permute-start(bf16[128,2048]{1,0:T(8,128)(2,1)S(1)} %slice.20), channel_id=1, source_target_pairs={{0,4},{4,12},{12,20},{20,28},{28,24},{24,16},{16,8},{8,0},{1,5},{5... | collective-permute-start | bytes 1572872 | tf_op jit(solution)/shard_map/ppermute | solution.py:82
  142.5 1.9 %slice.21 = bf16[128,2048]{1,0:T(8,128)(2,1)} slice(bf16[256,2048]{1,0:T(8,128)(2,1)} %collective-permute-done.19.refs_12_), slice={[128:256], [0:2048]} | slice | bytes 1048576 | tf_op jit(solution)/shard_map/slice | solution.py:83
  145.2 2.7 %collective-permute-start.14 = (bf16[256,2048]{1,0:T(8,128)(2,1)}, bf16[256,2048]{1,0:T(8,128)(2,1)}, u32[]{:S(2)}, u32[]{:S(2)}) collective-permute-start(bf16[256,2048]{1,0:T(8,128)(2,1)} %collective-permute-done.13.refs_6_), channel_id=1, source_target_pairs={{0,2},{2,0},{1,3},{3,1},{4,6},{6,4},{5,7},{7,5},{8,10},{10,8},{9,1... | collective-permute-start | bytes 3145736 | tf_op jit(solution)/shard_map/ppermute | solution.py:266
  147.9 3.5 %collective-permute-done.21 = bf16[128,2048]{1,0:T(8,128)(2,1)S(1)} collective-permute-done((bf16[128,2048]{1,0:T(8,128)(2,1)S(1)}, bf16[128,2048]{1,0:T(8,128)(2,1)S(1)}, u32[]{:S(2)}, u32[]{:S(2)}) %collective-permute-start.21) | collective-permute-done | bytes 524320 | tf_op jit(solution)/shard_map/ppermute | solution.py:82
  152.2 3.3 %collective-permute-start.18 = (bf16[256,2048]{1,0:T(8,128)(2,1)}, bf16[256,2048]{1,0:T(8,128)(2,1)}, u32[]{:S(2)}, u32[]{:S(2)}) collective-permute-start(bf16[256,2048]{1,0:T(8,128)(2,1)} %collective-permute-done.17.refs_10_), channel_id=1, source_target_pairs={{0,2},{2,0},{1,3},{3,1},{4,6},{6,4},{5,7},{7,5},{8,10},{10,8},{9,1... | collective-permute-start | bytes 3145736 | tf_op jit(solution)/shard_map/ppermute | solution.py:266
  156.5 2.6 %collective-permute-start.20 = (bf16[256,2048]{1,0:T(8,128)(2,1)}, bf16[256,2048]{1,0:T(8,128)(2,1)}, u32[]{:S(2)}, u32[]{:S(2)}) collective-permute-start(bf16[256,2048]{1,0:T(8,128)(2,1)} %collective-permute-done.19.refs_12_), channel_id=1, source_target_pairs={{0,2},{2,0},{1,3},{3,1},{4,6},{6,4},{5,7},{7,5},{8,10},{10,8},{9,1... | collective-permute-start | bytes 3145736 | tf_op jit(solution)/shard_map/ppermute | solution.py:266
  163.1 12.9 %shard_map.82 = bf16[256,2048]{1,0:T(8,128)(2,1)} custom-call(s32[16]{0:T(128)} %mul.41.starts_ref, bf16[256,4096]{1,0:T(8,128)(2,1)} %pad_maximum_fusion.normed_ref, bf16[256,2048]{1,0:T(8,128)(2,1)} %refs_0_.1, bf16[256,2048]{1,0:T(8,128)(2,1)} %collective-permute-done.8.refs_1_, bf16[256,2048]{1,0:T(8,128)(2,1)} %collective-permute-done.refs_2_, ...), custom_call_target="tpu_custom_call" | custom-call | tf_op jit(solution)/shard_map/pallas_call | solution.py:192
  (90 shorter events, 31.0 us)
Async XLA Ops:
  5.9 24.3 %collective-permute-start.2 = (bf16[2,128,2048]{2,1,0:T(8,128)(2,1)}, bf16[2,128,2048]{2,1,0:T(8,128)(2,1)S(1)}, u32[]{:S(2)}, u32[]{:S(2)}) collective-permute-start(bf16[2,128,2048]{2,1,0:T(8,128)(2,1)} %bitcast.6), channel_id=1, source_target_pairs={{0,1},{1,0},{2,3},{3,2},{4,5},{5,4},{6,7},{7,6},{8,9},{9,8},{10,11... | collective-permute-start | bytes 3145736 | tf_op jit(solution)/shard_map/ppermute | solution.py:38
  7.1 24.0 %collective-permute-start = (bf16[256,2048]{1,0:T(8,128)(2,1)}, bf16[256,2048]{1,0:T(8,128)(2,1)}, u32[]{:S(2)}, u32[]{:S(2)}) collective-permute-start(bf16[256,2048]{1,0:T(8,128)(2,1)} %refs_0_.1), channel_id=1, source_target_pairs={{0,4},{4,12},{12,20},{20,28},{28,24},{24,16},{16,8},{8,0},{1,5},{5... | collective-permute-start | bytes 3145736 | tf_op jit(solution)/shard_map/ppermute | solution.py:85
  8.4 23.7 %collective-permute-start.1 = (bf16[256,2048]{1,0:T(8,128)(2,1)}, bf16[256,2048]{1,0:T(8,128)(2,1)}, u32[]{:S(2)}, u32[]{:S(2)}) collective-permute-start(bf16[256,2048]{1,0:T(8,128)(2,1)} %refs_0_.1), channel_id=1, source_target_pairs={{4,0},{12,4},{20,12},{28,20},{24,28},{16,24},{8,16},{0,8},{5,1},{1... | collective-permute-start | bytes 3145736 | tf_op jit(solution)/shard_map/ppermute | solution.py:85
  33.1 4.6 %collective-permute-start.3 = (f32[16,128,128]{2,1,0:T(8,128)S(1)}, f32[16,128,128]{2,1,0:T(8,128)}, u32[]{:S(2)}, u32[]{:S(2)}) collective-permute-start(f32[16,128,128]{2,1,0:T(8,128)S(1)} %fusion.6), channel_id=1, source_target_pairs={{0,2},{2,0},{1,3},{3,1},{4,6},{6,4},{5,7},{7,5},{8,10},{10,8},{9,1... | collective-permute-start | bytes 3145736 | tf_op jit(solution)/shard_map/ppermute | solution.py:133
  38.9 15.0 %collective-permute-start.4 = (f32[8,128,128]{2,1,0:T(8,128)S(1)}, f32[8,128,128]{2,1,0:T(8,128)S(1)}, u32[]{:S(2)}, u32[]{:S(2)}) collective-permute-start(f32[8,128,128]{2,1,0:T(8,128)S(1)} %dynamic-slice_add_fusion), channel_id=1, source_target_pairs={{0,4},{4,8},{8,12},{12,16},{16,20},{20,24},{24,28},{1,5},{5,9},{9,... | collective-permute-start | bytes 1572872 | tf_op jit(solution)/shard_map/ppermute | solution.py:20
  54.0 14.1 %collective-permute-start.5 = (f32[8,128,128]{2,1,0:T(8,128)S(1)}, f32[8,128,128]{2,1,0:T(8,128)S(1)}, u32[]{:S(2)}, u32[]{:S(2)}) collective-permute-start(f32[8,128,128]{2,1,0:T(8,128)S(1)} %add.80), channel_id=1, source_target_pairs={{0,8},{4,12},{8,16},{12,20},{16,24},{20,28},{1,9},{5,13},{9,17},{1... | collective-permute-start | bytes 1572872 | tf_op jit(solution)/shard_map/ppermute | solution.py:20
  58.2 13.1 %collective-permute-start.7 = (bf16[1,128,2048]{2,1,0:T(8,128)(2,1)}, bf16[1,128,2048]{2,1,0:T(8,128)(2,1)S(1)}, u32[]{:S(2)}, u32[]{:S(2)}) collective-permute-start(bf16[1,128,2048]{2,1,0:T(8,128)(2,1)} %bitcast.11), channel_id=1, source_target_pairs={{0,1},{1,0},{2,3},{3,2},{4,5},{5,4},{6,7},{7,6},{8,9},{9,8},{10,11... | collective-permute-start | bytes 1572872 | tf_op jit(solution)/shard_map/ppermute | solution.py:38
  58.5 40.1 %collective-permute-start.8 = (bf16[256,2048]{1,0:T(8,128)(2,1)}, bf16[256,2048]{1,0:T(8,128)(2,1)}, u32[]{:S(2)}, u32[]{:S(2)}) collective-permute-start(bf16[256,2048]{1,0:T(8,128)(2,1)} %refs_0_.1), channel_id=1, source_target_pairs={{0,2},{2,0},{1,3},{3,1},{4,6},{6,4},{5,7},{7,5},{8,10},{10,8},{9,1... | collective-permute-start | bytes 3145736 | tf_op jit(solution)/shard_map/ppermute | solution.py:247
  60.5 38.1 %collective-permute-start.10 = (bf16[256,2048]{1,0:T(8,128)(2,1)}, bf16[256,2048]{1,0:T(8,128)(2,1)}, u32[]{:S(2)}, u32[]{:S(2)}) collective-permute-start(bf16[256,2048]{1,0:T(8,128)(2,1)} %collective-permute-done.1.refs_4_), channel_id=1, source_target_pairs={{0,2},{2,0},{1,3},{3,1},{4,6},{6,4},{5,7},{7,5},{8,10},{10,8},{9,1... | collective-permute-start | bytes 3145736 | tf_op jit(solution)/shard_map/ppermute | solution.py:247
  60.6 38.0 %collective-permute-start.9 = (bf16[256,2048]{1,0:T(8,128)(2,1)}, bf16[256,2048]{1,0:T(8,128)(2,1)}, u32[]{:S(2)}, u32[]{:S(2)}) collective-permute-start(bf16[256,2048]{1,0:T(8,128)(2,1)} %collective-permute-done.refs_2_), channel_id=1, source_target_pairs={{0,2},{2,0},{1,3},{3,1},{4,6},{6,4},{5,7},{7,5},{8,10},{10,8},{9,1... | collective-permute-start | bytes 3145736 | tf_op jit(solution)/shard_map/ppermute | solution.py:247
  68.1 25.0 %collective-permute-start.6 = (f32[8,128,128]{2,1,0:T(8,128)S(1)}, f32[8,128,128]{2,1,0:T(8,128)S(1)}, u32[]{:S(2)}, u32[]{:S(2)}) collective-permute-start(f32[8,128,128]{2,1,0:T(8,128)S(1)} %add.81), channel_id=1, source_target_pairs={{0,16},{4,20},{8,24},{12,28},{1,17},{5,21},{9,25},{13,29},{2,18},{... | collective-permute-start | bytes 1572872 | tf_op jit(solution)/shard_map/ppermute | solution.py:20
  72.8 42.9 %collective-permute-start.13 = (bf16[256,2048]{1,0:T(8,128)(2,1)}, bf16[256,2048]{1,0:T(8,128)(2,1)}, u32[]{:S(2)}, u32[]{:S(2)}) collective-permute-start(bf16[256,2048]{1,0:T(8,128)(2,1)} %collective-permute-done.refs_2_), channel_id=1, source_target_pairs={{0,4},{4,12},{12,20},{20,28},{28,24},{24,16},{16,8},{8,0},{1,5},{5... | collective-permute-start | bytes 3145736 | tf_op jit(solution)/shard_map/ppermute | solution.py:85
  93.2 24.8 %collective-permute-start.15 = (bf16[256,2048]{1,0:T(8,128)(2,1)}, bf16[256,2048]{1,0:T(8,128)(2,1)}, u32[]{:S(2)}, u32[]{:S(2)}) collective-permute-start(bf16[256,2048]{1,0:T(8,128)(2,1)} %collective-permute-done.1.refs_4_), channel_id=1, source_target_pairs={{4,0},{12,4},{20,12},{28,20},{24,28},{16,24},{8,16},{0,8},{5,1},{1... | collective-permute-start | bytes 3145736 | tf_op jit(solution)/shard_map/ppermute | solution.py:85
  98.6 19.4 %collective-permute-start.11 = (f32[8,128,128]{2,1,0:T(8,128)S(1)}, f32[8,128,128]{2,1,0:T(8,128)S(1)}, u32[]{:S(2)}, u32[]{:S(2)}) collective-permute-start(f32[8,128,128]{2,1,0:T(8,128)S(1)} %add_subtract_fusion), channel_id=1, source_target_pairs={{0,2},{2,0},{1,3},{3,1},{4,6},{6,4},{5,7},{7,5},{8,10},{10,8},{9,1... | collective-permute-start | bytes 1572872 | tf_op jit(solution)/shard_map/ppermute | solution.py:141
  115.7 23.4 %collective-permute-start.17 = (bf16[256,2048]{1,0:T(8,128)(2,1)}, bf16[256,2048]{1,0:T(8,128)(2,1)}, u32[]{:S(2)}, u32[]{:S(2)}) collective-permute-start(bf16[256,2048]{1,0:T(8,128)(2,1)} %collective-permute-done.13.refs_6_), channel_id=1, source_target_pairs={{0,4},{4,12},{12,20},{20,28},{28,24},{24,16},{16,8},{8,0},{1,5},{5... | collective-permute-start | bytes 3145736 | tf_op jit(solution)/shard_map/ppermute | solution.py:85
  117.9 24.6 %collective-permute-start.19 = (bf16[256,2048]{1,0:T(8,128)(2,1)}, bf16[256,2048]{1,0:T(8,128)(2,1)}, u32[]{:S(2)}, u32[]{:S(2)}) collective-permute-start(bf16[256,2048]{1,0:T(8,128)(2,1)} %collective-permute-done.15.refs_8_), channel_id=1, source_target_pairs={{4,0},{12,4},{20,12},{28,20},{24,28},{16,24},{8,16},{0,8},{5,1},{1... | collective-permute-start | bytes 3145736 | tf_op jit(solution)/shard_map/ppermute | solution.py:85
  122.8 37.4 %collective-permute-start.12 = (bf16[256,2048]{1,0:T(8,128)(2,1)S(1)}, bf16[256,2048]{1,0:T(8,128)(2,1)S(1)}, u32[]{:S(2)}, u32[]{:S(2)}) collective-permute-start(bf16[256,2048]{1,0:T(8,128)(2,1)S(1)} %copy.38), channel_id=1, source_target_pairs={{0,1},{1,0},{2,3},{3,2},{4,5},{5,4},{6,7},{7,6},{8,9},{9,8},{10,11... | collective-permute-start | bytes 3145736 | tf_op jit(solution)/shard_map/ppermute | solution.py:127
  140.3 11.1 %collective-permute-start.21 = (bf16[128,2048]{1,0:T(8,128)(2,1)S(1)}, bf16[128,2048]{1,0:T(8,128)(2,1)S(1)}, u32[]{:S(2)}, u32[]{:S(2)}) collective-permute-start(bf16[128,2048]{1,0:T(8,128)(2,1)S(1)} %slice.20), channel_id=1, source_target_pairs={{0,4},{4,12},{12,20},{20,28},{28,24},{24,16},{16,8},{8,0},{1,5},{5... | collective-permute-start | bytes 1572872 | tf_op jit(solution)/shard_map/ppermute | solution.py:82
  144.4 12.1 %collective-permute-start.22 = (bf16[128,2048]{1,0:T(8,128)(2,1)}, bf16[128,2048]{1,0:T(8,128)(2,1)}, u32[]{:S(2)}, u32[]{:S(2)}) collective-permute-start(bf16[128,2048]{1,0:T(8,128)(2,1)} %slice.21), channel_id=1, source_target_pairs={{4,0},{12,4},{20,12},{28,20},{24,28},{16,24},{8,16},{0,8},{5,1},{1... | collective-permute-start | bytes 1572872 | tf_op jit(solution)/shard_map/ppermute | solution.py:82
  145.2 17.6 %collective-permute-start.14 = (bf16[256,2048]{1,0:T(8,128)(2,1)}, bf16[256,2048]{1,0:T(8,128)(2,1)}, u32[]{:S(2)}, u32[]{:S(2)}) collective-permute-start(bf16[256,2048]{1,0:T(8,128)(2,1)} %collective-permute-done.13.refs_6_), channel_id=1, source_target_pairs={{0,2},{2,0},{1,3},{3,1},{4,6},{6,4},{5,7},{7,5},{8,10},{10,8},{9,1... | collective-permute-start | bytes 3145736 | tf_op jit(solution)/shard_map/ppermute | solution.py:266
  147.9 14.9 %collective-permute-start.16 = (bf16[256,2048]{1,0:T(8,128)(2,1)}, bf16[256,2048]{1,0:T(8,128)(2,1)}, u32[]{:S(2)}, u32[]{:S(2)}) collective-permute-start(bf16[256,2048]{1,0:T(8,128)(2,1)} %collective-permute-done.15.refs_8_), channel_id=1, source_target_pairs={{0,2},{2,0},{1,3},{3,1},{4,6},{6,4},{5,7},{7,5},{8,10},{10,8},{9,1... | collective-permute-start | bytes 3145736 | tf_op jit(solution)/shard_map/ppermute | solution.py:266
  152.2 10.5 %collective-permute-start.18 = (bf16[256,2048]{1,0:T(8,128)(2,1)}, bf16[256,2048]{1,0:T(8,128)(2,1)}, u32[]{:S(2)}, u32[]{:S(2)}) collective-permute-start(bf16[256,2048]{1,0:T(8,128)(2,1)} %collective-permute-done.17.refs_10_), channel_id=1, source_target_pairs={{0,2},{2,0},{1,3},{3,1},{4,6},{6,4},{5,7},{7,5},{8,10},{10,8},{9,1... | collective-permute-start | bytes 3145736 | tf_op jit(solution)/shard_map/ppermute | solution.py:266
  156.5 6.2 %collective-permute-start.20 = (bf16[256,2048]{1,0:T(8,128)(2,1)}, bf16[256,2048]{1,0:T(8,128)(2,1)}, u32[]{:S(2)}, u32[]{:S(2)}) collective-permute-start(bf16[256,2048]{1,0:T(8,128)(2,1)} %collective-permute-done.19.refs_12_), channel_id=1, source_target_pairs={{0,2},{2,0},{1,3},{3,1},{4,6},{6,4},{5,7},{7,5},{8,10},{10,8},{9,1... | collective-permute-start | bytes 3145736 | tf_op jit(solution)/shard_map/ppermute | solution.py:266
  160.2 2.9 %collective-permute-start.23 = (bf16[256,2048]{1,0:T(8,128)(2,1)S(1)}, bf16[256,2048]{1,0:T(8,128)(2,1)}, u32[]{:S(2)}, u32[]{:S(2)}) collective-permute-start(bf16[256,2048]{1,0:T(8,128)(2,1)S(1)} %constant_dynamic-update-slice_fusion.refs_14_), channel_id=1, source_target_pairs={{0,2},{2,0},{1,3},{3,1},{4,6},{6,4},{5,7},{7,5},{8,10},{10,8},{9,1... | collective-permute-start | bytes 3145736 | tf_op jit(solution)/shard_map/ppermute | solution.py:266
  (12 other events, 42.2 us)

commit v21 on v20

--- a/solution.py
+++ b/solution.py
@@ -272,7 +272,7 @@
     sources = jnp.asarray(order, jnp.int32)[(ring_place - jnp.asarray(offsets, jnp.int32)) % n_chip]
     cores = jnp.stack([core, 1 - core]).astype(jnp.int32)
     starts = ((sources[:, None] * 2 + cores[None, :]) * out_weight.shape[0]).reshape(-1)
-    return project_blocks(gathered, starts, [w for pair in zip(got, swapped) for w in pair], group=16)
+    return project_blocks(gathered, starts, [w for pair in zip(got, swapped) for w in pair], group=2)
 
 
 def solution(mesh):

time: 178 us -> 174 us (0.978)
  Pallas kernels: 12.9 us -> 9.08 us
    pallas_call x1, Pallas kernels: 12.9 us -> 9.08 us  [project_blocks(): pl.pallas_call(kernel, out_shape=jax.ShapeDtypeStruct((tokens, cols), jnp...]
where the time goes in v21:
time: 174 us; the launch traced here: 172 us
  waiting for transfers between devices  96.2 us (55%)
  starting transfers between devices  32 us (18%)
  local copies, waits for them, and re-layouts  20.8 us (12%)
  Pallas kernels  9.08 us (5%)
  other arithmetic  8.14 us (5%)
  matrix products  5.53 us (3%)
    ppermute x3, waiting for transfers between devices, exclusive_prefix(): total = total + lax.ppermute(total, axis, pairs)  38.6 us
    ppermute x3, waiting for transfers between devices, ring_step(): lax.ppermute(ahead, 'chip', forward)  29.2 us
    ppermute x2, waiting for transfers between devices, head_blocks(): other = lax.ppermute(sent, 'head', SWAP)  21.1 us
    pallas_call x1, Pallas kernels, project_blocks(): pl.pallas_call(kernel, out_shape=jax.ShapeDtypeStruct((tokens, cols), jnp...  9.08 us
    ppermute x5, starting transfers between devices, local_ring(): swapped += [lax.ppermute(w, 'core', SWAP) for w in got[len(swapped):]]  8.6 us
    ppermute x3, starting transfers between devices, exclusive_prefix(): total = total + lax.ppermute(total, axis, pairs)  8.4 us
    unnamed x28, local copies, waits for them, and re-layouts  7.43 us
    ppermute x1, waiting for transfers between devices, ring_step(): lax.ppermute(ahead[:half_rows], 'chip', forward)  3.52 us
  transfers between devices with their start and end apart: 24, of which 11 were waited for; matrix products, arithmetic and copies ran while one was open for 14% of the time, Pallas kernels for 0%

profile of v21, /device:TPU:13, one launch (start us, length us, event | category | flops | bytes accessed | tf_op | source)
XLA Modules:
  0.0 172.3 jit_solution(4388109671035177346)
XLA Ops:
  3.6 2.3 %copy.22 = bf16[2,128,1,2048]{3,1,0,2:T(8,128)(2,1)} copy(bf16[2,128,1,2048]{1,3,2,0:T(8,128)(2,1)} %get-tuple-element.30) | data formatting | bytes 2097152 | tf_op jit(solution)/shard_map/jit(dynamic_index_in_dim)/dynamic_slice | solution.py:37
  9.1 21.1 %collective-permute-done.2 = bf16[2,128,2048]{2,1,0:T(8,128)(2,1)S(1)} collective-permute-done((bf16[2,128,2048]{2,1,0:T(8,128)(2,1)}, bf16[2,128,2048]{2,1,0:T(8,128)(2,1)S(1)}, u32[]{:S(2)}, u32[]{:S(2)}) %collective-permute-start.2) | collective-permute-done | bytes 1048608 | tf_op jit(solution)/shard_map/ppermute | solution.py:38
  33.1 2.2 %collective-permute-start.3 = (f32[16,128,128]{2,1,0:T(8,128)S(1)}, f32[16,128,128]{2,1,0:T(8,128)}, u32[]{:S(2)}, u32[]{:S(2)}) collective-permute-start(f32[16,128,128]{2,1,0:T(8,128)S(1)} %fusion.6), channel_id=1, source_target_pairs={{0,2},{2,0},{1,3},{3,1},{4,6},{6,4},{5,7},{7,5},{8,10},{10,8},{9,1... | collective-permute-start | bytes 3145736 | tf_op jit(solution)/shard_map/ppermute | solution.py:133
  35.4 2.4 %collective-permute-done.3 = f32[16,128,128]{2,1,0:T(8,128)} collective-permute-done((f32[16,128,128]{2,1,0:T(8,128)S(1)}, f32[16,128,128]{2,1,0:T(8,128)}, u32[]{:S(2)}, u32[]{:S(2)}) %collective-permute-start.3) | collective-permute-done | bytes 1048608 | tf_op jit(solution)/shard_map/ppermute | solution.py:133
  38.9 2.0 %collective-permute-start.4 = (f32[8,128,128]{2,1,0:T(8,128)S(1)}, f32[8,128,128]{2,1,0:T(8,128)S(1)}, u32[]{:S(2)}, u32[]{:S(2)}) collective-permute-start(f32[8,128,128]{2,1,0:T(8,128)S(1)} %dynamic-slice_add_fusion), channel_id=1, source_target_pairs={{0,4},{4,8},{8,12},{12,16},{16,20},{20,24},{24,28},{1,5},{5,9},{9,... | collective-permute-start | bytes 1572872 | tf_op jit(solution)/shard_map/ppermute | solution.py:20
  42.6 11.3 %collective-permute-done.4 = f32[8,128,128]{2,1,0:T(8,128)S(1)} collective-permute-done((f32[8,128,128]{2,1,0:T(8,128)S(1)}, f32[8,128,128]{2,1,0:T(8,128)S(1)}, u32[]{:S(2)}, u32[]{:S(2)}) %collective-permute-start.4) | collective-permute-done | bytes 524320 | tf_op jit(solution)/shard_map/ppermute | solution.py:20
  54.0 3.2 %collective-permute-start.5 = (f32[8,128,128]{2,1,0:T(8,128)S(1)}, f32[8,128,128]{2,1,0:T(8,128)S(1)}, u32[]{:S(2)}, u32[]{:S(2)}) collective-permute-start(f32[8,128,128]{2,1,0:T(8,128)S(1)} %add.80), channel_id=1, source_target_pairs={{0,8},{4,12},{8,16},{12,20},{16,24},{20,28},{1,9},{5,13},{9,17},{1... | collective-permute-start | bytes 1572872 | tf_op jit(solution)/shard_map/ppermute | solution.py:20
  58.5 1.8 %collective-permute-start.8 = (bf16[256,2048]{1,0:T(8,128)(2,1)}, bf16[256,2048]{1,0:T(8,128)(2,1)}, u32[]{:S(2)}, u32[]{:S(2)}) collective-permute-start(bf16[256,2048]{1,0:T(8,128)(2,1)} %refs_0_.1), channel_id=1, source_target_pairs={{0,2},{2,0},{1,3},{3,1},{4,6},{6,4},{5,7},{7,5},{8,10},{10,8},{9,1... | collective-permute-start | bytes 3145736 | tf_op jit(solution)/shard_map/ppermute | solution.py:247
  61.1 7.0 %collective-permute-done.5 = f32[8,128,128]{2,1,0:T(8,128)S(1)} collective-permute-done((f32[8,128,128]{2,1,0:T(8,128)S(1)}, f32[8,128,128]{2,1,0:T(8,128)S(1)}, u32[]{:S(2)}, u32[]{:S(2)}) %collective-permute-start.5) | collective-permute-done | bytes 524320 | tf_op jit(solution)/shard_map/ppermute | solution.py:20
  68.1 3.2 %collective-permute-start.6 = (f32[8,128,128]{2,1,0:T(8,128)S(1)}, f32[8,128,128]{2,1,0:T(8,128)S(1)}, u32[]{:S(2)}, u32[]{:S(2)}) collective-permute-start(f32[8,128,128]{2,1,0:T(8,128)S(1)} %add.81), channel_id=1, source_target_pairs={{0,16},{4,20},{8,24},{12,28},{1,17},{5,21},{9,25},{13,29},{2,18},{... | collective-permute-start | bytes 1572872 | tf_op jit(solution)/shard_map/ppermute | solution.py:20
  72.8 20.3 %collective-permute-done.6 = f32[8,128,128]{2,1,0:T(8,128)S(1)} collective-permute-done((f32[8,128,128]{2,1,0:T(8,128)S(1)}, f32[8,128,128]{2,1,0:T(8,128)S(1)}, u32[]{:S(2)}, u32[]{:S(2)}) %collective-permute-start.6) | collective-permute-done | bytes 524320 | tf_op jit(solution)/shard_map/ppermute | solution.py:20
  94.0 3.2 %fusion.1 = f32[256,16,128]{0,2,1:T(8,128)S(1)} fusion(bf16[256,16,128]{0,2,1:T(8,128)(2,1)} %bitcast.49, bf16[256,16,128]{0,2,1:T(8,128)(2,1)} %bitcast.54, pred[256,256]{1,0:T(8,128)(4,1)S(1)} %iota_compare_fusion, bf16[256,2048]{1,0:T(8,128)(2,1)} %copy-done.2), kind=kOutput, calls=%fused_computation.13 | convolution fusion | flops 538968064 | bytes 5308416 | tf_op jit(solution)/shard_map/hts,she->the/dot_general | solution.py:106
  98.6 2.7 %collective-permute-start.11 = (f32[8,128,128]{2,1,0:T(8,128)S(1)}, f32[8,128,128]{2,1,0:T(8,128)S(1)}, u32[]{:S(2)}, u32[]{:S(2)}) collective-permute-start(f32[8,128,128]{2,1,0:T(8,128)S(1)} %add_subtract_fusion), channel_id=1, source_target_pairs={{0,2},{2,0},{1,3},{3,1},{4,6},{6,4},{5,7},{7,5},{8,10},{10,8},{9,1... | collective-permute-start | bytes 1572872 | tf_op jit(solution)/shard_map/ppermute | solution.py:141
  102.5 13.2 %collective-permute-done.13.refs_6_ = bf16[256,2048]{1,0:T(8,128)(2,1)} collective-permute-done((bf16[256,2048]{1,0:T(8,128)(2,1)}, bf16[256,2048]{1,0:T(8,128)(2,1)}, u32[]{:S(2)}, u32[]{:S(2)}) %collective-permute-start.13) | collective-permute-done | bytes 1048608 | tf_op jit(solution)/shard_map/ppermute | solution.py:85
  115.7 2.2 %collective-permute-start.17 = (bf16[256,2048]{1,0:T(8,128)(2,1)}, bf16[256,2048]{1,0:T(8,128)(2,1)}, u32[]{:S(2)}, u32[]{:S(2)}) collective-permute-start(bf16[256,2048]{1,0:T(8,128)(2,1)} %collective-permute-done.13.refs_6_), channel_id=1, source_target_pairs={{0,4},{4,12},{12,20},{20,28},{28,24},{24,16},{16,8},{8,0},{1,5},{5... | collective-permute-start | bytes 3145736 | tf_op jit(solution)/shard_map/ppermute | solution.py:85
  118.1 1.8 %multiply_reduce_fusion = (f32[256,16]{0,1:T(8,128)S(1)}, f32[16,128,256]{2,1,0:T(8,128)S(1)}) fusion(f32[256,16,128]{0,2,1:T(8,128)S(1)} %fusion.1, bf16[256,16,128]{0,2,1:T(8,128)(2,1)S(1)} %bitcast.55, f32[8,128,128]{2,1,0:T(8,128)S(1)} %get-tuple-element.32, f32[8,128,128]{2,1,0:T(8,128)S(1)} %get-tuple-element.31, ...), kind=kOutput, calls=%fused_computation.11 | convolution fusion | flops 136835072 | bytes 7356417 | tf_op jit(solution)/shard_map/thd,hde->the/dot_general | solution.py:115
  123.8 15.4 %collective-permute-done.17.refs_10_ = bf16[256,2048]{1,0:T(8,128)(2,1)} collective-permute-done((bf16[256,2048]{1,0:T(8,128)(2,1)}, bf16[256,2048]{1,0:T(8,128)(2,1)}, u32[]{:S(2)}, u32[]{:S(2)}) %collective-permute-start.17) | collective-permute-done | bytes 1048608 | tf_op jit(solution)/shard_map/ppermute | solution.py:85
  140.3 2.3 %collective-permute-start.21 = (bf16[128,2048]{1,0:T(8,128)(2,1)S(1)}, bf16[128,2048]{1,0:T(8,128)(2,1)S(1)}, u32[]{:S(2)}, u32[]{:S(2)}) collective-permute-start(bf16[128,2048]{1,0:T(8,128)(2,1)S(1)} %slice.20), channel_id=1, source_target_pairs={{0,4},{4,12},{12,20},{20,28},{28,24},{24,16},{16,8},{8,0},{1,5},{5... | collective-permute-start | bytes 1572872 | tf_op jit(solution)/shard_map/ppermute | solution.py:82
  142.5 1.9 %slice.21 = bf16[128,2048]{1,0:T(8,128)(2,1)} slice(bf16[256,2048]{1,0:T(8,128)(2,1)} %collective-permute-done.19.refs_12_), slice={[128:256], [0:2048]} | slice | bytes 1048576 | tf_op jit(solution)/shard_map/slice | solution.py:83
  145.2 2.7 %collective-permute-start.14 = (bf16[256,2048]{1,0:T(8,128)(2,1)}, bf16[256,2048]{1,0:T(8,128)(2,1)}, u32[]{:S(2)}, u32[]{:S(2)}) collective-permute-start(bf16[256,2048]{1,0:T(8,128)(2,1)} %collective-permute-done.13.refs_6_), channel_id=1, source_target_pairs={{0,2},{2,0},{1,3},{3,1},{4,6},{6,4},{5,7},{7,5},{8,10},{10,8},{9,1... | collective-permute-start | bytes 3145736 | tf_op jit(solution)/shard_map/ppermute | solution.py:266
  147.9 3.5 %collective-permute-done.21 = bf16[128,2048]{1,0:T(8,128)(2,1)S(1)} collective-permute-done((bf16[128,2048]{1,0:T(8,128)(2,1)S(1)}, bf16[128,2048]{1,0:T(8,128)(2,1)S(1)}, u32[]{:S(2)}, u32[]{:S(2)}) %collective-permute-start.21) | collective-permute-done | bytes 524320 | tf_op jit(solution)/shard_map/ppermute | solution.py:82
  152.2 3.3 %collective-permute-start.18 = (bf16[256,2048]{1,0:T(8,128)(2,1)}, bf16[256,2048]{1,0:T(8,128)(2,1)}, u32[]{:S(2)}, u32[]{:S(2)}) collective-permute-start(bf16[256,2048]{1,0:T(8,128)(2,1)} %collective-permute-done.17.refs_10_), channel_id=1, source_target_pairs={{0,2},{2,0},{1,3},{3,1},{4,6},{6,4},{5,7},{7,5},{8,10},{10,8},{9,1... | collective-permute-start | bytes 3145736 | tf_op jit(solution)/shard_map/ppermute | solution.py:266
  156.5 2.6 %collective-permute-start.20 = (bf16[256,2048]{1,0:T(8,128)(2,1)}, bf16[256,2048]{1,0:T(8,128)(2,1)}, u32[]{:S(2)}, u32[]{:S(2)}) collective-permute-start(bf16[256,2048]{1,0:T(8,128)(2,1)} %collective-permute-done.19.refs_12_), channel_id=1, source_target_pairs={{0,2},{2,0},{1,3},{3,1},{4,6},{6,4},{5,7},{7,5},{8,10},{10,8},{9,1... | collective-permute-start | bytes 3145736 | tf_op jit(solution)/shard_map/ppermute | solution.py:266
  163.1 9.1 %shard_map.82 = bf16[256,2048]{1,0:T(8,128)(2,1)} custom-call(s32[16]{0:T(128)} %mul.41.starts_ref, bf16[256,4096]{1,0:T(8,128)(2,1)} %pad_maximum_fusion.normed_ref, bf16[256,2048]{1,0:T(8,128)(2,1)} %refs_0_.1, bf16[256,2048]{1,0:T(8,128)(2,1)} %collective-permute-done.8.refs_1_, bf16[256,2048]{1,0:T(8,128)(2,1)} %collective-permute-done.refs_2_, ...), custom_call_target="tpu_custom_call" | custom-call | tf_op jit(solution)/shard_map/pallas_call | solution.py:192
  (90 shorter events, 31.0 us)
Async XLA Ops:
  5.9 24.3 %collective-permute-start.2 = (bf16[2,128,2048]{2,1,0:T(8,128)(2,1)}, bf16[2,128,2048]{2,1,0:T(8,128)(2,1)S(1)}, u32[]{:S(2)}, u32[]{:S(2)}) collective-permute-start(bf16[2,128,2048]{2,1,0:T(8,128)(2,1)} %bitcast.6), channel_id=1, source_target_pairs={{0,1},{1,0},{2,3},{3,2},{4,5},{5,4},{6,7},{7,6},{8,9},{9,8},{10,11... | collective-permute-start | bytes 3145736 | tf_op jit(solution)/shard_map/ppermute | solution.py:38
  7.1 24.0 %collective-permute-start = (bf16[256,2048]{1,0:T(8,128)(2,1)}, bf16[256,2048]{1,0:T(8,128)(2,1)}, u32[]{:S(2)}, u32[]{:S(2)}) collective-permute-start(bf16[256,2048]{1,0:T(8,128)(2,1)} %refs_0_.1), channel_id=1, source_target_pairs={{0,4},{4,12},{12,20},{20,28},{28,24},{24,16},{16,8},{8,0},{1,5},{5... | collective-permute-start | bytes 3145736 | tf_op jit(solution)/shard_map/ppermute | solution.py:85
  8.4 23.7 %collective-permute-start.1 = (bf16[256,2048]{1,0:T(8,128)(2,1)}, bf16[256,2048]{1,0:T(8,128)(2,1)}, u32[]{:S(2)}, u32[]{:S(2)}) collective-permute-start(bf16[256,2048]{1,0:T(8,128)(2,1)} %refs_0_.1), channel_id=1, source_target_pairs={{4,0},{12,4},{20,12},{28,20},{24,28},{16,24},{8,16},{0,8},{5,1},{1... | collective-permute-start | bytes 3145736 | tf_op jit(solution)/shard_map/ppermute | solution.py:85
  33.1 4.6 %collective-permute-start.3 = (f32[16,128,128]{2,1,0:T(8,128)S(1)}, f32[16,128,128]{2,1,0:T(8,128)}, u32[]{:S(2)}, u32[]{:S(2)}) collective-permute-start(f32[16,128,128]{2,1,0:T(8,128)S(1)} %fusion.6), channel_id=1, source_target_pairs={{0,2},{2,0},{1,3},{3,1},{4,6},{6,4},{5,7},{7,5},{8,10},{10,8},{9,1... | collective-permute-start | bytes 3145736 | tf_op jit(solution)/shard_map/ppermute | solution.py:133
  38.9 15.0 %collective-permute-start.4 = (f32[8,128,128]{2,1,0:T(8,128)S(1)}, f32[8,128,128]{2,1,0:T(8,128)S(1)}, u32[]{:S(2)}, u32[]{:S(2)}) collective-permute-start(f32[8,128,128]{2,1,0:T(8,128)S(1)} %dynamic-slice_add_fusion), channel_id=1, source_target_pairs={{0,4},{4,8},{8,12},{12,16},{16,20},{20,24},{24,28},{1,5},{5,9},{9,... | collective-permute-start | bytes 1572872 | tf_op jit(solution)/shard_map/ppermute | solution.py:20
  54.0 14.1 %collective-permute-start.5 = (f32[8,128,128]{2,1,0:T(8,128)S(1)}, f32[8,128,128]{2,1,0:T(8,128)S(1)}, u32[]{:S(2)}, u32[]{:S(2)}) collective-permute-start(f32[8,128,128]{2,1,0:T(8,128)S(1)} %add.80), channel_id=1, source_target_pairs={{0,8},{4,12},{8,16},{12,20},{16,24},{20,28},{1,9},{5,13},{9,17},{1... | collective-permute-start | bytes 1572872 | tf_op jit(solution)/shard_map/ppermute | solution.py:20
  58.2 13.1 %collective-permute-start.7 = (bf16[1,128,2048]{2,1,0:T(8,128)(2,1)}, bf16[1,128,2048]{2,1,0:T(8,128)(2,1)S(1)}, u32[]{:S(2)}, u32[]{:S(2)}) collective-permute-start(bf16[1,128,2048]{2,1,0:T(8,128)(2,1)} %bitcast.11), channel_id=1, source_target_pairs={{0,1},{1,0},{2,3},{3,2},{4,5},{5,4},{6,7},{7,6},{8,9},{9,8},{10,11... | collective-permute-start | bytes 1572872 | tf_op jit(solution)/shard_map/ppermute | solution.py:38
  58.5 40.1 %collective-permute-start.8 = (bf16[256,2048]{1,0:T(8,128)(2,1)}, bf16[256,2048]{1,0:T(8,128)(2,1)}, u32[]{:S(2)}, u32[]{:S(2)}) collective-permute-start(bf16[256,2048]{1,0:T(8,128)(2,1)} %refs_0_.1), channel_id=1, source_target_pairs={{0,2},{2,0},{1,3},{3,1},{4,6},{6,4},{5,7},{7,5},{8,10},{10,8},{9,1... | collective-permute-start | bytes 3145736 | tf_op jit(solution)/shard_map/ppermute | solution.py:247
  60.5 38.1 %collective-permute-start.10 = (bf16[256,2048]{1,0:T(8,128)(2,1)}, bf16[256,2048]{1,0:T(8,128)(2,1)}, u32[]{:S(2)}, u32[]{:S(2)}) collective-permute-start(bf16[256,2048]{1,0:T(8,128)(2,1)} %collective-permute-done.1.refs_4_), channel_id=1, source_target_pairs={{0,2},{2,0},{1,3},{3,1},{4,6},{6,4},{5,7},{7,5},{8,10},{10,8},{9,1... | collective-permute-start | bytes 3145736 | tf_op jit(solution)/shard_map/ppermute | solution.py:247
  60.6 38.0 %collective-permute-start.9 = (bf16[256,2048]{1,0:T(8,128)(2,1)}, bf16[256,2048]{1,0:T(8,128)(2,1)}, u32[]{:S(2)}, u32[]{:S(2)}) collective-permute-start(bf16[256,2048]{1,0:T(8,128)(2,1)} %collective-permute-done.refs_2_), channel_id=1, source_target_pairs={{0,2},{2,0},{1,3},{3,1},{4,6},{6,4},{5,7},{7,5},{8,10},{10,8},{9,1... | collective-permute-start | bytes 3145736 | tf_op jit(solution)/shard_map/ppermute | solution.py:247
  68.1 25.0 %collective-permute-start.6 = (f32[8,128,128]{2,1,0:T(8,128)S(1)}, f32[8,128,128]{2,1,0:T(8,128)S(1)}, u32[]{:S(2)}, u32[]{:S(2)}) collective-permute-start(f32[8,128,128]{2,1,0:T(8,128)S(1)} %add.81), channel_id=1, source_target_pairs={{0,16},{4,20},{8,24},{12,28},{1,17},{5,21},{9,25},{13,29},{2,18},{... | collective-permute-start | bytes 1572872 | tf_op jit(solution)/shard_map/ppermute | solution.py:20
  72.8 42.9 %collective-permute-start.13 = (bf16[256,2048]{1,0:T(8,128)(2,1)}, bf16[256,2048]{1,0:T(8,128)(2,1)}, u32[]{:S(2)}, u32[]{:S(2)}) collective-permute-start(bf16[256,2048]{1,0:T(8,128)(2,1)} %collective-permute-done.refs_2_), channel_id=1, source_target_pairs={{0,4},{4,12},{12,20},{20,28},{28,24},{24,16},{16,8},{8,0},{1,5},{5... | collective-permute-start | bytes 3145736 | tf_op jit(solution)/shard_map/ppermute | solution.py:85
  93.2 24.8 %collective-permute-start.15 = (bf16[256,2048]{1,0:T(8,128)(2,1)}, bf16[256,2048]{1,0:T(8,128)(2,1)}, u32[]{:S(2)}, u32[]{:S(2)}) collective-permute-start(bf16[256,2048]{1,0:T(8,128)(2,1)} %collective-permute-done.1.refs_4_), channel_id=1, source_target_pairs={{4,0},{12,4},{20,12},{28,20},{24,28},{16,24},{8,16},{0,8},{5,1},{1... | collective-permute-start | bytes 3145736 | tf_op jit(solution)/shard_map/ppermute | solution.py:85
  98.6 19.4 %collective-permute-start.11 = (f32[8,128,128]{2,1,0:T(8,128)S(1)}, f32[8,128,128]{2,1,0:T(8,128)S(1)}, u32[]{:S(2)}, u32[]{:S(2)}) collective-permute-start(f32[8,128,128]{2,1,0:T(8,128)S(1)} %add_subtract_fusion), channel_id=1, source_target_pairs={{0,2},{2,0},{1,3},{3,1},{4,6},{6,4},{5,7},{7,5},{8,10},{10,8},{9,1... | collective-permute-start | bytes 1572872 | tf_op jit(solution)/shard_map/ppermute | solution.py:141
  115.7 23.4 %collective-permute-start.17 = (bf16[256,2048]{1,0:T(8,128)(2,1)}, bf16[256,2048]{1,0:T(8,128)(2,1)}, u32[]{:S(2)}, u32[]{:S(2)}) collective-permute-start(bf16[256,2048]{1,0:T(8,128)(2,1)} %collective-permute-done.13.refs_6_), channel_id=1, source_target_pairs={{0,4},{4,12},{12,20},{20,28},{28,24},{24,16},{16,8},{8,0},{1,5},{5... | collective-permute-start | bytes 3145736 | tf_op jit(solution)/shard_map/ppermute | solution.py:85
  117.9 24.6 %collective-permute-start.19 = (bf16[256,2048]{1,0:T(8,128)(2,1)}, bf16[256,2048]{1,0:T(8,128)(2,1)}, u32[]{:S(2)}, u32[]{:S(2)}) collective-permute-start(bf16[256,2048]{1,0:T(8,128)(2,1)} %collective-permute-done.15.refs_8_), channel_id=1, source_target_pairs={{4,0},{12,4},{20,12},{28,20},{24,28},{16,24},{8,16},{0,8},{5,1},{1... | collective-permute-start | bytes 3145736 | tf_op jit(solution)/shard_map/ppermute | solution.py:85
  122.8 37.4 %collective-permute-start.12 = (bf16[256,2048]{1,0:T(8,128)(2,1)S(1)}, bf16[256,2048]{1,0:T(8,128)(2,1)S(1)}, u32[]{:S(2)}, u32[]{:S(2)}) collective-permute-start(bf16[256,2048]{1,0:T(8,128)(2,1)S(1)} %copy.38), channel_id=1, source_target_pairs={{0,1},{1,0},{2,3},{3,2},{4,5},{5,4},{6,7},{7,6},{8,9},{9,8},{10,11... | collective-permute-start | bytes 3145736 | tf_op jit(solution)/shard_map/ppermute | solution.py:127
  140.3 11.1 %collective-permute-start.21 = (bf16[128,2048]{1,0:T(8,128)(2,1)S(1)}, bf16[128,2048]{1,0:T(8,128)(2,1)S(1)}, u32[]{:S(2)}, u32[]{:S(2)}) collective-permute-start(bf16[128,2048]{1,0:T(8,128)(2,1)S(1)} %slice.20), channel_id=1, source_target_pairs={{0,4},{4,12},{12,20},{20,28},{28,24},{24,16},{16,8},{8,0},{1,5},{5... | collective-permute-start | bytes 1572872 | tf_op jit(solution)/shard_map/ppermute | solution.py:82
  144.4 12.1 %collective-permute-start.22 = (bf16[128,2048]{1,0:T(8,128)(2,1)}, bf16[128,2048]{1,0:T(8,128)(2,1)}, u32[]{:S(2)}, u32[]{:S(2)}) collective-permute-start(bf16[128,2048]{1,0:T(8,128)(2,1)} %slice.21), channel_id=1, source_target_pairs={{4,0},{12,4},{20,12},{28,20},{24,28},{16,24},{8,16},{0,8},{5,1},{1... | collective-permute-start | bytes 1572872 | tf_op jit(solution)/shard_map/ppermute | solution.py:82
  145.2 17.6 %collective-permute-start.14 = (bf16[256,2048]{1,0:T(8,128)(2,1)}, bf16[256,2048]{1,0:T(8,128)(2,1)}, u32[]{:S(2)}, u32[]{:S(2)}) collective-permute-start(bf16[256,2048]{1,0:T(8,128)(2,1)} %collective-permute-done.13.refs_6_), channel_id=1, source_target_pairs={{0,2},{2,0},{1,3},{3,1},{4,6},{6,4},{5,7},{7,5},{8,10},{10,8},{9,1... | collective-permute-start | bytes 3145736 | tf_op jit(solution)/shard_map/ppermute | solution.py:266
  147.9 14.9 %collective-permute-start.16 = (bf16[256,2048]{1,0:T(8,128)(2,1)}, bf16[256,2048]{1,0:T(8,128)(2,1)}, u32[]{:S(2)}, u32[]{:S(2)}) collective-permute-start(bf16[256,2048]{1,0:T(8,128)(2,1)} %collective-permute-done.15.refs_8_), channel_id=1, source_target_pairs={{0,2},{2,0},{1,3},{3,1},{4,6},{6,4},{5,7},{7,5},{8,10},{10,8},{9,1... | collective-permute-start | bytes 3145736 | tf_op jit(solution)/shard_map/ppermute | solution.py:266
  152.2 10.5 %collective-permute-start.18 = (bf16[256,2048]{1,0:T(8,128)(2,1)}, bf16[256,2048]{1,0:T(8,128)(2,1)}, u32[]{:S(2)}, u32[]{:S(2)}) collective-permute-start(bf16[256,2048]{1,0:T(8,128)(2,1)} %collective-permute-done.17.refs_10_), channel_id=1, source_target_pairs={{0,2},{2,0},{1,3},{3,1},{4,6},{6,4},{5,7},{7,5},{8,10},{10,8},{9,1... | collective-permute-start | bytes 3145736 | tf_op jit(solution)/shard_map/ppermute | solution.py:266
  156.5 6.2 %collective-permute-start.20 = (bf16[256,2048]{1,0:T(8,128)(2,1)}, bf16[256,2048]{1,0:T(8,128)(2,1)}, u32[]{:S(2)}, u32[]{:S(2)}) collective-permute-start(bf16[256,2048]{1,0:T(8,128)(2,1)} %collective-permute-done.19.refs_12_), channel_id=1, source_target_pairs={{0,2},{2,0},{1,3},{3,1},{4,6},{6,4},{5,7},{7,5},{8,10},{10,8},{9,1... | collective-permute-start | bytes 3145736 | tf_op jit(solution)/shard_map/ppermute | solution.py:266
  160.2 2.9 %collective-permute-start.23 = (bf16[256,2048]{1,0:T(8,128)(2,1)S(1)}, bf16[256,2048]{1,0:T(8,128)(2,1)}, u32[]{:S(2)}, u32[]{:S(2)}) collective-permute-start(bf16[256,2048]{1,0:T(8,128)(2,1)S(1)} %constant_dynamic-update-slice_fusion.refs_14_), channel_id=1, source_target_pairs={{0,2},{2,0},{1,3},{3,1},{4,6},{6,4},{5,7},{7,5},{8,10},{10,8},{9,1... | collective-permute-start | bytes 3145736 | tf_op jit(solution)/shard_map/ppermute | solution.py:266
  (12 other events, 42.2 us)

commit v22 on v9

--- a/solution.py
+++ b/solution.py
@@ -147,25 +147,45 @@
     return block.reshape(block.shape[0], heads_dev, HEAD_DIM)
 
 
-def project_blocks(normed, blocks, group=4):
+def project_blocks(normed_pair, starts, sources, blocks, group=4):
     n = len(blocks)
     rows, cols = blocks[0].shape
-    tokens = normed.shape[0]
-    def kernel(normed_ref, *refs):
+    tokens = normed_pair[0].shape[0]
+
+    def kernel(starts_ref, sources_ref, own_ref, other_ref, *refs):
         block_refs = refs[:n]
-        out_ref, weights, sems, acc = refs[n:]
-        copies = [
-            pltpu.make_async_copy(block_refs[i], weights.at[pl.ds(i * rows, rows), :], sems.at[i])
+        out_ref, features, weights, sems, acc = refs[n:]
+
+        def feature_copy(src_ref, i, start):
+            return pltpu.make_async_copy(
+                src_ref.at[:, pl.ds(start, rows)],
+                features.at[:, pl.ds(i * rows, rows)],
+                sems.at[0, i],
+            )
+
+        weight_copies = [
+            pltpu.make_async_copy(block_refs[i], weights.at[pl.ds(i * rows, rows), :], sems.at[1, i])
             for i in range(n)
         ]
-        for c in copies:
-            c.start()
+        for i in range(n):
+            start = pl.multiple_of(starts_ref[i], rows)
+
+            @pl.when(sources_ref[i] == 0)
+            def _():
+                feature_copy(own_ref, i, start).start()
+
+            @pl.when(sources_ref[i] != 0)
+            def _():
+                feature_copy(other_ref, i, start).start()
+
+            weight_copies[i].start()
         for g in range(0, n, group):
             last = min(g + group, n)
             for i in range(g, last):
-                copies[i].wait()
+                feature_copy(own_ref, i, 0).wait()
+                weight_copies[i].wait()
             part = jnp.dot(
-                normed_ref[:, g * rows:last * rows],
+                features[:, g * rows:last * rows],
                 weights[g * rows:last * rows, :],
                 preferred_element_type=jnp.float32,
             )
@@ -174,17 +194,20 @@
             else:
                 acc[...] += part
         out_ref[...] = acc[...].astype(out_ref.dtype)
+
     return pl.pallas_call(
         kernel,
         out_shape=jax.ShapeDtypeStruct((tokens, cols), jnp.bfloat16),
-        in_specs=[pl.BlockSpec(memory_space=pltpu.VMEM)] + [pl.BlockSpec(memory_space=pl.ANY)] * n,
+        in_specs=[pl.BlockSpec(memory_space=pltpu.SMEM)] * 2
+        + [pl.BlockSpec(memory_space=pl.ANY)] * (2 + n),
         out_specs=pl.BlockSpec(memory_space=pltpu.VMEM),
         scratch_shapes=[
+            pltpu.VMEM((tokens, n * rows), blocks[0].dtype),
             pltpu.VMEM((n * rows, cols), blocks[0].dtype),
-            pltpu.SemaphoreType.DMA((n,)),
+            pltpu.SemaphoreType.DMA((2, n)),
             pltpu.VMEM((tokens, cols), jnp.float32),
         ],
-    )(normed, *blocks)
+    )(starts, sources, normed_pair[0], normed_pair[1], *blocks)
 
 
 def local_gather(queries, keys, values, out_weight, norm_gain, n_chip, n_head):
@@ -249,14 +272,19 @@
     swapped += [lax.ppermute(w, "core", SWAP) for w in got[len(swapped):]]
     prefix = chip_finish(chip_prefix_half, partner_state, core)
     normed = normalize(query_heads, prefix, within_block, norm_gain)
-    gathered = gather_head(normed, n_head, place)
-    row_count = gathered.shape[0]
-    split = gathered.reshape(row_count, n_chip, 2, out_weight.shape[0])
+    received = lax.ppermute(normed, "head", SWAP)
+    width = normed.shape[1]
     ring_place = jnp.asarray([order.index(j) for j in range(n_chip)], jnp.int32)[lax.axis_index("chip")]
     sources = jnp.asarray(order, jnp.int32)[(ring_place - jnp.asarray(offsets, jnp.int32)) % n_chip]
-    by_offset = jnp.take(split, sources, axis=1)
-    by_offset = jnp.where(core == 0, by_offset, by_offset[:, :, ::-1]).reshape(row_count, -1)
-    return project_blocks(by_offset, [w for pair in zip(got, swapped) for w in pair])
+    cores = jnp.stack([core, 1 - core]).astype(jnp.int32)
+    starts = ((sources[:, None] * 2 + cores[None, :]) * out_weight.shape[0]).reshape(-1)
+    groups = starts // width
+    return project_blocks(
+        (normed, received),
+        starts - groups * width,
+        (groups != place).astype(jnp.int32),
+        [w for pair in zip(got, swapped) for w in pair],
+    )
 
 
 def solution(mesh):

time: 184 us -> 193 us (1.049)
  waiting for transfers between devices: 91.6 us -> 118 us
  local copies, waits for them, and re-layouts: 30.6 us -> 22.1 us
  starting transfers between devices: 32.5 us -> 25.1 us
    ppermute x1, waiting for transfers between devices: 0.01 us -> 22.5 us  [local_ring(): received = lax.ppermute(normed, 'head', SWAP)]
    ppermute x3, waiting for transfers between devices: 32.9 us -> 46.1 us  [exclusive_prefix(): total = total + lax.ppermute(total, axis, pairs)]
    ppermute x3, waiting for transfers between devices: 29.6 us -> 18.5 us  [ring_step(): lax.ppermute(ahead, 'chip', forward)]
    ppermute x5, starting transfers between devices: 8.93 us -> 2.02 us  [local_ring(): swapped += [lax.ppermute(w, 'core', SWAP) for w in got[len(swapped):]]]
    reshape x2 -> x1, local copies, waits for them, and re-layouts: 5.24 us -> 1.49 us  [normalize(): return normed.reshape(query_heads.shape[0], heads_dev * HEAD_DIM)]
    ppermute x1, waiting for transfers between devices: 4.55 us -> 7.61 us  [ring_step(): lax.ppermute(ahead[:half_rows], 'chip', forward)]
    dynamic_slice x3, local copies, waits for them, and re-layouts: 4.03 us -> 1.62 us  [head_blocks(): own = lax.dynamic_index_in_dim(stacked, place, 2, False)]
    gather x1 -> x0, local copies, waits for them, and re-layouts: 2.27 us -> none  [local_ring(): by_offset = jnp.take(split, sources, axis=1)]
  transfers between devices with their start and end apart: 24 -> 24, of which waited for: 10 -> 10; matrix products, arithmetic and copies ran while one was open for 21% -> 16% of each run, Pallas kernels for 0% -> 0%
where the time goes in v22:
time: 193 us; the launch traced here: 191 us
  waiting for transfers between devices  118 us (61%)
  starting transfers between devices  25.1 us (13%)
  local copies, waits for them, and re-layouts  22.1 us (11%)
  other arithmetic  10.5 us (5%)
  Pallas kernels  9.63 us (5%)
  matrix products  5.54 us (3%)
    ppermute x3, waiting for transfers between devices, exclusive_prefix(): total = total + lax.ppermute(total, axis, pairs)  46.1 us
    ppermute x1, waiting for transfers between devices, local_ring(): received = lax.ppermute(normed, 'head', SWAP)  22.5 us
    ppermute x2, waiting for transfers between devices, head_blocks(): other = lax.ppermute(sent, 'head', SWAP)  21.1 us
    ppermute x3, waiting for transfers between devices, ring_step(): lax.ppermute(ahead, 'chip', forward)  18.5 us
    pallas_call x1, Pallas kernels, project_blocks(): pl.pallas_call(kernel, out_shape=jax.ShapeDtypeStruct((tokens, cols), jnp...  9.63 us
    ppermute x3, starting transfers between devices, exclusive_prefix(): total = total + lax.ppermute(total, axis, pairs)  8.21 us
    ppermute x1, waiting for transfers between devices, ring_step(): lax.ppermute(ahead[:half_rows], 'chip', forward)  7.61 us
    unnamed x28, local copies, waits for them, and re-layouts  6.87 us
  transfers between devices with their start and end apart: 24, of which 10 were waited for; matrix products, arithmetic and copies ran while one was open for 16% of the time, Pallas kernels for 0%

profile of v22, /device:TPU:13, one launch (start us, length us, event | category | flops | bytes accessed | tf_op | source)
XLA Modules:
  0.0 191.1 jit_solution(2951545740399255589)
XLA Ops:
  0.0 1.7 copy.19
  3.6 2.3 %copy.22 = bf16[2,128,1,2048]{3,1,0,2:T(8,128)(2,1)} copy(bf16[2,128,1,2048]{1,3,2,0:T(8,128)(2,1)} %get-tuple-element.30) | data formatting | bytes 2097152 | tf_op jit(solution)/shard_map/jit(dynamic_index_in_dim)/dynamic_slice | solution.py:37
  9.0 21.1 %collective-permute-done.2 = bf16[2,128,2048]{2,1,0:T(8,128)(2,1)S(1)} collective-permute-done((bf16[2,128,2048]{2,1,0:T(8,128)(2,1)}, bf16[2,128,2048]{2,1,0:T(8,128)(2,1)S(1)}, u32[]{:S(2)}, u32[]{:S(2)}) %collective-permute-start.2) | collective-permute-done | bytes 1048608 | tf_op jit(solution)/shard_map/ppermute | solution.py:38
  33.1 2.2 %collective-permute-start.3 = (f32[16,128,128]{2,1,0:T(8,128)S(1)}, f32[16,128,128]{2,1,0:T(8,128)}, u32[]{:S(2)}, u32[]{:S(2)}) collective-permute-start(f32[16,128,128]{2,1,0:T(8,128)S(1)} %fusion.6), channel_id=1, source_target_pairs={{0,2},{2,0},{1,3},{3,1},{4,6},{6,4},{5,7},{7,5},{8,10},{10,8},{9,1... | collective-permute-start | bytes 3145736 | tf_op jit(solution)/shard_map/ppermute | solution.py:133
  38.8 2.0 %collective-permute-start.4 = (f32[8,128,128]{2,1,0:T(8,128)S(1)}, f32[8,128,128]{2,1,0:T(8,128)}, u32[]{:S(2)}, u32[]{:S(2)}) collective-permute-start(f32[8,128,128]{2,1,0:T(8,128)S(1)} %dynamic-slice_add_fusion), channel_id=1, source_target_pairs={{0,4},{4,8},{8,12},{12,16},{16,20},{20,24},{24,28},{1,5},{5,9},{9,... | collective-permute-start | bytes 1572872 | tf_op jit(solution)/shard_map/ppermute | solution.py:20
  40.9 1.6 copy.25
  42.5 17.9 %collective-permute-done.13.refs_6_ = bf16[256,2048]{1,0:T(8,128)(2,1)} collective-permute-done((bf16[256,2048]{1,0:T(8,128)(2,1)}, bf16[256,2048]{1,0:T(8,128)(2,1)}, u32[]{:S(2)}, u32[]{:S(2)}) %collective-permute-start.13) | collective-permute-done | bytes 1048608 | tf_op jit(solution)/shard_map/ppermute | solution.py:85
  62.5 2.1 %copy.27 = bf16[1,128,1,2048]{3,1,2,0:T(8,128)(2,1)} copy(bf16[1,128,1,2048]{1,3,2,0:T(8,128)(2,1)} %get-tuple-element.36) | data formatting | bytes 1048576 | tf_op jit(solution)/shard_map/jit(dynamic_index_in_dim)/dynamic_slice | solution.py:37
  64.9 5.7 %collective-permute-done.4 = f32[8,128,128]{2,1,0:T(8,128)} collective-permute-done((f32[8,128,128]{2,1,0:T(8,128)S(1)}, f32[8,128,128]{2,1,0:T(8,128)}, u32[]{:S(2)}, u32[]{:S(2)}) %collective-permute-start.4) | collective-permute-done | bytes 524320 | tf_op jit(solution)/shard_map/ppermute | solution.py:20
  71.7 2.2 %collective-permute-start.5 = (f32[8,128,128]{2,1,0:T(8,128)S(1)}, f32[8,128,128]{2,1,0:T(8,128)}, u32[]{:S(2)}, u32[]{:S(2)}) collective-permute-start(f32[8,128,128]{2,1,0:T(8,128)S(1)} %add.81), channel_id=1, source_target_pairs={{0,8},{4,12},{8,16},{12,20},{16,24},{20,28},{1,9},{5,13},{9,17},{1... | collective-permute-start | bytes 1572872 | tf_op jit(solution)/shard_map/ppermute | solution.py:20
  73.9 2.0 %collective-permute-start.19 = (bf16[256,2048]{1,0:T(8,128)(2,1)}, bf16[256,2048]{1,0:T(8,128)(2,1)}, u32[]{:S(2)}, u32[]{:S(2)}) collective-permute-start(bf16[256,2048]{1,0:T(8,128)(2,1)} %collective-permute-done.15.refs_8_), channel_id=1, source_target_pairs={{4,0},{12,4},{20,12},{28,20},{24,28},{16,24},{8,16},{0,8},{5,1},{1... | collective-permute-start | bytes 3145736 | tf_op jit(solution)/shard_map/ppermute | solution.py:85
  75.9 1.9 collective-permute-start.8
  79.3 26.0 %collective-permute-done.5 = f32[8,128,128]{2,1,0:T(8,128)} collective-permute-done((f32[8,128,128]{2,1,0:T(8,128)S(1)}, f32[8,128,128]{2,1,0:T(8,128)}, u32[]{:S(2)}, u32[]{:S(2)}) %collective-permute-start.5) | collective-permute-done | bytes 524320 | tf_op jit(solution)/shard_map/ppermute | solution.py:20
  108.4 4.0 %collective-permute-start.6 = (f32[8,128,128]{2,1,0:T(8,128)S(1)}, f32[8,128,128]{2,1,0:T(8,128)}, u32[]{:S(2)}, u32[]{:S(2)}) collective-permute-start(f32[8,128,128]{2,1,0:T(8,128)S(1)} %add.82), channel_id=1, source_target_pairs={{0,16},{4,20},{8,24},{12,28},{1,17},{5,21},{9,25},{13,29},{2,18},{... | collective-permute-start | bytes 1572872 | tf_op jit(solution)/shard_map/ppermute | solution.py:20
  114.7 3.2 %fusion.1 = f32[256,16,128]{0,2,1:T(8,128)S(1)} fusion(bf16[256,16,128]{0,2,1:T(8,128)(2,1)} %bitcast.49, bf16[256,16,128]{0,2,1:T(8,128)(2,1)} %bitcast.54, pred[256,256]{1,0:T(8,128)(4,1)S(1)} %iota_compare_fusion, bf16[256,2048]{1,0:T(8,128)(2,1)} %copy-done.3), kind=kOutput, calls=%fused_computation.12 | convolution fusion | flops 538968064 | bytes 5308416 | tf_op jit(solution)/shard_map/hts,she->the/dot_general | solution.py:106
  117.9 1.9 slice.21
  119.8 14.3 %collective-permute-done.6 = f32[8,128,128]{2,1,0:T(8,128)} collective-permute-done((f32[8,128,128]{2,1,0:T(8,128)S(1)}, f32[8,128,128]{2,1,0:T(8,128)}, u32[]{:S(2)}, u32[]{:S(2)}) %collective-permute-start.6) | collective-permute-done | bytes 524320 | tf_op jit(solution)/shard_map/ppermute | solution.py:20
  137.9 7.6 %collective-permute-done.21 = bf16[128,2048]{1,0:T(8,128)(2,1)} collective-permute-done((bf16[128,2048]{1,0:T(8,128)(2,1)}, bf16[128,2048]{1,0:T(8,128)(2,1)}, u32[]{:S(2)}, u32[]{:S(2)}) %collective-permute-start.21) | collective-permute-done | bytes 524320 | tf_op jit(solution)/shard_map/ppermute | solution.py:82
  146.3 1.9 constant_dynamic-update-slice_fusion.1
  148.8 1.9 constant_dynamic-update-slice_fusion.refs_14_
  150.8 1.8 multiply_reduce_fusion
  154.1 1.5 copy.38.own_ref
  157.9 22.5 %collective-permute-done.12.other_ref = bf16[256,2048]{1,0:T(8,128)(2,1)S(1)} collective-permute-done((bf16[256,2048]{1,0:T(8,128)(2,1)S(1)}, bf16[256,2048]{1,0:T(8,128)(2,1)S(1)}, u32[]{:S(2)}, u32[]{:S(2)}) %collective-permute-start.12) | collective-permute-done | bytes 1048608 | tf_op jit(solution)/shard_map/ppermute | solution.py:275
  181.4 9.6 %shard_map.82 = bf16[256,2048]{1,0:T(8,128)(2,1)} custom-call(s32[16]{0:T(128)} %multiply_subtract_fusion.starts_ref, s32[16]{0:T(128)} %get-tuple-element.23.sources_ref, bf16[256,2048]{1,0:T(8,128)(2,1)} %copy-done.2, bf16[256,2048]{1,0:T(8,128)(2,1)} %copy-done.7, bf16[256,2048]{1,0:T(8,128)(2,1)} %refs_0_.1, ...), custom_call_target="tpu_custom_call" | custom-call | tf_op jit(solution)/shard_map/pallas_call | solution.py:198
  (90 shorter events, 31.7 us)
Async XLA Ops:
  5.8 24.3 %collective-permute-start.2 = (bf16[2,128,2048]{2,1,0:T(8,128)(2,1)}, bf16[2,128,2048]{2,1,0:T(8,128)(2,1)S(1)}, u32[]{:S(2)}, u32[]{:S(2)}) collective-permute-start(bf16[2,128,2048]{2,1,0:T(8,128)(2,1)} %bitcast.6), channel_id=1, source_target_pairs={{0,1},{1,0},{2,3},{3,2},{4,5},{5,4},{6,7},{7,6},{8,9},{9,8},{10,11... | collective-permute-start | bytes 3145736 | tf_op jit(solution)/shard_map/ppermute | solution.py:38
  7.0 24.0 %collective-permute-start = (bf16[256,2048]{1,0:T(8,128)(2,1)}, bf16[256,2048]{1,0:T(8,128)(2,1)}, u32[]{:S(2)}, u32[]{:S(2)}) collective-permute-start(bf16[256,2048]{1,0:T(8,128)(2,1)} %refs_0_.1), channel_id=1, source_target_pairs={{0,4},{4,12},{12,20},{20,28},{28,24},{24,16},{16,8},{8,0},{1,5},{5... | collective-permute-start | bytes 3145736 | tf_op jit(solution)/shard_map/ppermute | solution.py:85
  8.3 23.7 %collective-permute-start.1 = (bf16[256,2048]{1,0:T(8,128)(2,1)}, bf16[256,2048]{1,0:T(8,128)(2,1)}, u32[]{:S(2)}, u32[]{:S(2)}) collective-permute-start(bf16[256,2048]{1,0:T(8,128)(2,1)} %refs_0_.1), channel_id=1, source_target_pairs={{4,0},{12,4},{20,12},{28,20},{24,28},{16,24},{8,16},{0,8},{5,1},{1... | collective-permute-start | bytes 3145736 | tf_op jit(solution)/shard_map/ppermute | solution.py:85
  33.1 4.6 %collective-permute-start.3 = (f32[16,128,128]{2,1,0:T(8,128)S(1)}, f32[16,128,128]{2,1,0:T(8,128)}, u32[]{:S(2)}, u32[]{:S(2)}) collective-permute-start(f32[16,128,128]{2,1,0:T(8,128)S(1)} %fusion.6), channel_id=1, source_target_pairs={{0,2},{2,0},{1,3},{3,1},{4,6},{6,4},{5,7},{7,5},{8,10},{10,8},{9,1... | collective-permute-start | bytes 3145736 | tf_op jit(solution)/shard_map/ppermute | solution.py:133
  35.3 25.0 %collective-permute-start.13 = (bf16[256,2048]{1,0:T(8,128)(2,1)}, bf16[256,2048]{1,0:T(8,128)(2,1)}, u32[]{:S(2)}, u32[]{:S(2)}) collective-permute-start(bf16[256,2048]{1,0:T(8,128)(2,1)} %collective-permute-done.refs_2_), channel_id=1, source_target_pairs={{0,4},{4,12},{12,20},{20,28},{28,24},{24,16},{16,8},{8,0},{1,5},{5... | collective-permute-start | bytes 3145736 | tf_op jit(solution)/shard_map/ppermute | solution.py:85
  36.6 37.2 %collective-permute-start.15 = (bf16[256,2048]{1,0:T(8,128)(2,1)}, bf16[256,2048]{1,0:T(8,128)(2,1)}, u32[]{:S(2)}, u32[]{:S(2)}) collective-permute-start(bf16[256,2048]{1,0:T(8,128)(2,1)} %collective-permute-done.1.refs_4_), channel_id=1, source_target_pairs={{4,0},{12,4},{20,12},{28,20},{24,28},{16,24},{8,16},{0,8},{5,1},{1... | collective-permute-start | bytes 3145736 | tf_op jit(solution)/shard_map/ppermute | solution.py:85
  38.8 31.7 %collective-permute-start.4 = (f32[8,128,128]{2,1,0:T(8,128)S(1)}, f32[8,128,128]{2,1,0:T(8,128)}, u32[]{:S(2)}, u32[]{:S(2)}) collective-permute-start(f32[8,128,128]{2,1,0:T(8,128)S(1)} %dynamic-slice_add_fusion), channel_id=1, source_target_pairs={{0,4},{4,8},{8,12},{12,16},{16,20},{20,24},{24,28},{1,5},{5,9},{9,... | collective-permute-start | bytes 1572872 | tf_op jit(solution)/shard_map/ppermute | solution.py:20
  60.4 48.0 %collective-permute-start.17 = (bf16[256,2048]{1,0:T(8,128)(2,1)}, bf16[256,2048]{1,0:T(8,128)(2,1)S(1)}, u32[]{:S(2)}, u32[]{:S(2)}) collective-permute-start(bf16[256,2048]{1,0:T(8,128)(2,1)} %collective-permute-done.13.refs_6_), channel_id=1, source_target_pairs={{0,4},{4,12},{12,20},{20,28},{28,24},{24,16},{16,8},{8,0},{1,5},{5... | collective-permute-start | bytes 3145736 | tf_op jit(solution)/shard_map/ppermute | solution.py:85
  64.6 14.0 %collective-permute-start.7 = (bf16[1,128,2048]{2,1,0:T(8,128)(2,1)}, bf16[1,128,2048]{2,1,0:T(8,128)(2,1)}, u32[]{:S(2)}, u32[]{:S(2)}) collective-permute-start(bf16[1,128,2048]{2,1,0:T(8,128)(2,1)} %bitcast.11), channel_id=1, source_target_pairs={{0,1},{1,0},{2,3},{3,2},{4,5},{5,4},{6,7},{7,6},{8,9},{9,8},{10,11... | collective-permute-start | bytes 1572872 | tf_op jit(solution)/shard_map/ppermute | solution.py:38
  71.7 33.6 %collective-permute-start.5 = (f32[8,128,128]{2,1,0:T(8,128)S(1)}, f32[8,128,128]{2,1,0:T(8,128)}, u32[]{:S(2)}, u32[]{:S(2)}) collective-permute-start(f32[8,128,128]{2,1,0:T(8,128)S(1)} %add.81), channel_id=1, source_target_pairs={{0,8},{4,12},{8,16},{12,20},{16,24},{20,28},{1,9},{5,13},{9,17},{1... | collective-permute-start | bytes 1572872 | tf_op jit(solution)/shard_map/ppermute | solution.py:20
  73.9 40.8 %collective-permute-start.19 = (bf16[256,2048]{1,0:T(8,128)(2,1)}, bf16[256,2048]{1,0:T(8,128)(2,1)}, u32[]{:S(2)}, u32[]{:S(2)}) collective-permute-start(bf16[256,2048]{1,0:T(8,128)(2,1)} %collective-permute-done.15.refs_8_), channel_id=1, source_target_pairs={{4,0},{12,4},{20,12},{28,20},{24,28},{16,24},{8,16},{0,8},{5,1},{1... | collective-permute-start | bytes 3145736 | tf_op jit(solution)/shard_map/ppermute | solution.py:85
  75.9 59.6 %collective-permute-start.8 = (bf16[256,2048]{1,0:T(8,128)(2,1)}, bf16[256,2048]{1,0:T(8,128)(2,1)}, u32[]{:S(2)}, u32[]{:S(2)}) collective-permute-start(bf16[256,2048]{1,0:T(8,128)(2,1)} %refs_0_.1), channel_id=1, source_target_pairs={{0,2},{2,0},{1,3},{3,1},{4,6},{6,4},{5,7},{7,5},{8,10},{10,8},{9,1... | collective-permute-start | bytes 3145736 | tf_op jit(solution)/shard_map/ppermute | solution.py:253
  78.6 56.9 %collective-permute-start.10 = (bf16[256,2048]{1,0:T(8,128)(2,1)}, bf16[256,2048]{1,0:T(8,128)(2,1)}, u32[]{:S(2)}, u32[]{:S(2)}) collective-permute-start(bf16[256,2048]{1,0:T(8,128)(2,1)} %collective-permute-done.1.refs_4_), channel_id=1, source_target_pairs={{0,2},{2,0},{1,3},{3,1},{4,6},{6,4},{5,7},{7,5},{8,10},{10,8},{9,1... | collective-permute-start | bytes 3145736 | tf_op jit(solution)/shard_map/ppermute | solution.py:253
  105.3 30.2 %collective-permute-start.9 = (bf16[256,2048]{1,0:T(8,128)(2,1)}, bf16[256,2048]{1,0:T(8,128)(2,1)}, u32[]{:S(2)}, u32[]{:S(2)}) collective-permute-start(bf16[256,2048]{1,0:T(8,128)(2,1)} %collective-permute-done.refs_2_), channel_id=1, source_target_pairs={{0,2},{2,0},{1,3},{3,1},{4,6},{6,4},{5,7},{7,5},{8,10},{10,8},{9,1... | collective-permute-start | bytes 3145736 | tf_op jit(solution)/shard_map/ppermute | solution.py:253
  108.4 25.8 %collective-permute-start.6 = (f32[8,128,128]{2,1,0:T(8,128)S(1)}, f32[8,128,128]{2,1,0:T(8,128)}, u32[]{:S(2)}, u32[]{:S(2)}) collective-permute-start(f32[8,128,128]{2,1,0:T(8,128)S(1)} %add.82), channel_id=1, source_target_pairs={{0,16},{4,20},{8,24},{12,28},{1,17},{5,21},{9,25},{13,29},{2,18},{... | collective-permute-start | bytes 1572872 | tf_op jit(solution)/shard_map/ppermute | solution.py:20
  114.7 30.8 %collective-permute-start.21 = (bf16[128,2048]{1,0:T(8,128)(2,1)}, bf16[128,2048]{1,0:T(8,128)(2,1)}, u32[]{:S(2)}, u32[]{:S(2)}) collective-permute-start(bf16[128,2048]{1,0:T(8,128)(2,1)} %slice.20), channel_id=1, source_target_pairs={{0,4},{4,12},{12,20},{20,28},{28,24},{24,16},{16,8},{8,0},{1,5},{5... | collective-permute-start | bytes 1572872 | tf_op jit(solution)/shard_map/ppermute | solution.py:82
  134.2 14.0 %collective-permute-start.22 = (bf16[128,2048]{1,0:T(8,128)(2,1)}, bf16[128,2048]{1,0:T(8,128)(2,1)}, u32[]{:S(2)}, u32[]{:S(2)}) collective-permute-start(bf16[128,2048]{1,0:T(8,128)(2,1)} %slice.21), channel_id=1, source_target_pairs={{4,0},{12,4},{20,12},{28,20},{24,28},{16,24},{8,16},{0,8},{5,1},{1... | collective-permute-start | bytes 1572872 | tf_op jit(solution)/shard_map/ppermute | solution.py:82
  135.5 15.2 %collective-permute-start.11 = (f32[8,128,128]{2,1,0:T(8,128)S(1)}, f32[8,128,128]{2,1,0:T(8,128)S(1)}, u32[]{:S(2)}, u32[]{:S(2)}) collective-permute-start(f32[8,128,128]{2,1,0:T(8,128)S(1)} %add_subtract_fusion), channel_id=1, source_target_pairs={{0,2},{2,0},{1,3},{3,1},{4,6},{6,4},{5,7},{7,5},{8,10},{10,8},{9,1... | collective-permute-start | bytes 1572872 | tf_op jit(solution)/shard_map/ppermute | solution.py:141
  137.3 18.3 %collective-permute-start.14 = (bf16[256,2048]{1,0:T(8,128)(2,1)}, bf16[256,2048]{1,0:T(8,128)(2,1)}, u32[]{:S(2)}, u32[]{:S(2)}) collective-permute-start(bf16[256,2048]{1,0:T(8,128)(2,1)} %collective-permute-done.13.refs_6_), channel_id=1, source_target_pairs={{0,2},{2,0},{1,3},{3,1},{4,6},{6,4},{5,7},{7,5},{8,10},{10,8},{9,1... | collective-permute-start | bytes 3145736 | tf_op jit(solution)/shard_map/ppermute | solution.py:272
  137.4 20.5 %collective-permute-start.16 = (bf16[256,2048]{1,0:T(8,128)(2,1)}, bf16[256,2048]{1,0:T(8,128)(2,1)}, u32[]{:S(2)}, u32[]{:S(2)}) collective-permute-start(bf16[256,2048]{1,0:T(8,128)(2,1)} %collective-permute-done.15.refs_8_), channel_id=1, source_target_pairs={{0,2},{2,0},{1,3},{3,1},{4,6},{6,4},{5,7},{7,5},{8,10},{10,8},{9,1... | collective-permute-start | bytes 3145736 | tf_op jit(solution)/shard_map/ppermute | solution.py:272
  145.5 12.4 %collective-permute-start.18 = (bf16[256,2048]{1,0:T(8,128)(2,1)}, bf16[256,2048]{1,0:T(8,128)(2,1)}, u32[]{:S(2)}, u32[]{:S(2)}) collective-permute-start(bf16[256,2048]{1,0:T(8,128)(2,1)} %copy-done.5), channel_id=1, source_target_pairs={{0,2},{2,0},{1,3},{3,1},{4,6},{6,4},{5,7},{7,5},{8,10},{10,8},{9,1... | collective-permute-start | bytes 3145736 | tf_op jit(solution)/shard_map/ppermute | solution.py:272
  148.2 9.8 %collective-permute-start.20 = (bf16[256,2048]{1,0:T(8,128)(2,1)}, bf16[256,2048]{1,0:T(8,128)(2,1)}, u32[]{:S(2)}, u32[]{:S(2)}) collective-permute-start(bf16[256,2048]{1,0:T(8,128)(2,1)} %collective-permute-done.19.refs_12_), channel_id=1, source_target_pairs={{0,2},{2,0},{1,3},{3,1},{4,6},{6,4},{5,7},{7,5},{8,10},{10,8},{9,1... | collective-permute-start | bytes 3145736 | tf_op jit(solution)/shard_map/ppermute | solution.py:272
  150.7 7.2 %collective-permute-start.23 = (bf16[256,2048]{1,0:T(8,128)(2,1)}, bf16[256,2048]{1,0:T(8,128)(2,1)}, u32[]{:S(2)}, u32[]{:S(2)}) collective-permute-start(bf16[256,2048]{1,0:T(8,128)(2,1)} %constant_dynamic-update-slice_fusion.refs_14_), channel_id=1, source_target_pairs={{0,2},{2,0},{1,3},{3,1},{4,6},{6,4},{5,7},{7,5},{8,10},{10,8},{9,1... | collective-permute-start | bytes 3145736 | tf_op jit(solution)/shard_map/ppermute | solution.py:272
  155.6 24.9 %collective-permute-start.12 = (bf16[256,2048]{1,0:T(8,128)(2,1)S(1)}, bf16[256,2048]{1,0:T(8,128)(2,1)S(1)}, u32[]{:S(2)}, u32[]{:S(2)}) collective-permute-start(bf16[256,2048]{1,0:T(8,128)(2,1)S(1)} %copy.38.own_ref), channel_id=1, source_target_pairs={{0,1},{1,0},{2,3},{3,2},{4,5},{5,4},{6,7},{7,6},{8,9},{9,8},{10,11... | collective-permute-start | bytes 3145736 | tf_op jit(solution)/shard_map/ppermute | solution.py:275
  (12 other events, 96.7 us)

commit v23 on v22

--- a/solution.py
+++ b/solution.py
@@ -261,7 +261,12 @@
     within_block = within_block_part(query_heads, key_heads, value_heads)
     swapped += [lax.ppermute(w, "core", SWAP) for w in got[len(swapped):]]
     chip_prefix_half, within_block, swapped = barrier((chip_prefix_half, within_block, swapped))
+    prefix = chip_finish(chip_prefix_half, partner_state, core)
+    normed = normalize(query_heads, prefix, within_block, norm_gain)
+    received = lax.ppermute(normed, "head", SWAP)
     for step in range(2, n_steps + 1):
+        if step == 3:
+            ahead, behind, received = barrier((ahead, behind, received))
         ahead, behind = ring_step(ahead, behind, order, last=step == n_steps)
         if step == n_steps:
             got.append(jnp.concatenate([ahead, behind], 0))
@@ -270,9 +275,6 @@
             got += [ahead, behind]
             offsets += [step, -step]
     swapped += [lax.ppermute(w, "core", SWAP) for w in got[len(swapped):]]
-    prefix = chip_finish(chip_prefix_half, partner_state, core)
-    normed = normalize(query_heads, prefix, within_block, norm_gain)
-    received = lax.ppermute(normed, "head", SWAP)
     width = normed.shape[1]
     ring_place = jnp.asarray([order.index(j) for j in range(n_chip)], jnp.int32)[lax.axis_index("chip")]
     sources = jnp.asarray(order, jnp.int32)[(ring_place - jnp.asarray(offsets, jnp.int32)) % n_chip]

time: 193 us -> 190 us (0.984)
  starting transfers between devices: 25.1 us -> 31.5 us
  waiting for transfers between devices: 118 us -> 113 us
  local copies, waits for them, and re-layouts: 22.1 us -> 17.6 us
    ppermute x3, waiting for transfers between devices: 18.5 us -> 41.2 us  [ring_step(): lax.ppermute(ahead, 'chip', forward)]
    ppermute x1, waiting for transfers between devices: 22.5 us -> 4.33 us  [local_ring(): received = lax.ppermute(normed, 'head', SWAP)]
    ppermute x3, waiting for transfers between devices: 46.1 us -> 35.7 us  [exclusive_prefix(): total = total + lax.ppermute(total, axis, pairs)]
    ppermute x3, starting transfers between devices: 8.21 us -> 12.4 us  [exclusive_prefix(): total = total + lax.ppermute(total, axis, pairs)]
    ppermute x5, starting transfers between devices: 2.02 us -> 5.69 us  [local_ring(): swapped += [lax.ppermute(w, 'core', SWAP) for w in got[len(swapped):]]]
    unnamed x28 -> x30, local copies, waits for them, and re-layouts: 6.87 us -> 5.9 us
  transfers between devices with their start and end apart: 24 -> 24, of which waited for: 10 -> 13; matrix products, arithmetic and copies ran while one was open for 16% -> 13% of each run, Pallas kernels for 0% -> 0%
where the time goes in v23:
time: 190 us; the launch traced here: 187 us
  waiting for transfers between devices  113 us (59%)
  starting transfers between devices  31.5 us (17%)
  local copies, waits for them, and re-layouts  17.6 us (9%)
  other arithmetic  9.63 us (5%)
  Pallas kernels  9.63 us (5%)
  matrix products  5.54 us (3%)
    ppermute x3, waiting for transfers between devices, ring_step(): lax.ppermute(ahead, 'chip', forward)  41.2 us
    ppermute x3, waiting for transfers between devices, exclusive_prefix(): total = total + lax.ppermute(total, axis, pairs)  35.7 us
    ppermute x2, waiting for transfers between devices, head_blocks(): other = lax.ppermute(sent, 'head', SWAP)  21.1 us
    ppermute x3, starting transfers between devices, exclusive_prefix(): total = total + lax.ppermute(total, axis, pairs)  12.4 us
    pallas_call x1, Pallas kernels, project_blocks(): pl.pallas_call(kernel, out_shape=jax.ShapeDtypeStruct((tokens, cols), jnp...  9.63 us
    ppermute x1, waiting for transfers between devices, ring_step(): lax.ppermute(ahead[:half_rows], 'chip', forward)  6.48 us
    unnamed x30, local copies, waits for them, and re-layouts  5.9 us
    ppermute x5, starting transfers between devices, local_ring(): swapped += [lax.ppermute(w, 'core', SWAP) for w in got[len(swapped):]]  5.69 us
  transfers between devices with their start and end apart: 24, of which 13 were waited for; matrix products, arithmetic and copies ran while one was open for 13% of the time, Pallas kernels for 0%

profile of v23, /device:TPU:13, one launch (start us, length us, event | category | flops | bytes accessed | tf_op | source)
XLA Modules:
  0.0 187.2 jit_solution(2758718688137701880)
XLA Ops:
  0.0 1.7 copy.19
  3.6 2.3 %copy.22 = bf16[2,128,1,2048]{3,1,0,2:T(8,128)(2,1)} copy(bf16[2,128,1,2048]{1,3,2,0:T(8,128)(2,1)} %get-tuple-element.36) | data formatting | bytes 2097152 | tf_op jit(solution)/shard_map/jit(dynamic_index_in_dim)/dynamic_slice | solution.py:37
  9.0 21.1 %collective-permute-done.2 = bf16[2,128,2048]{2,1,0:T(8,128)(2,1)S(1)} collective-permute-done((bf16[2,128,2048]{2,1,0:T(8,128)(2,1)}, bf16[2,128,2048]{2,1,0:T(8,128)(2,1)S(1)}, u32[]{:S(2)}, u32[]{:S(2)}) %collective-permute-start.2) | collective-permute-done | bytes 1048608 | tf_op jit(solution)/shard_map/ppermute | solution.py:38
  32.1 2.1 %collective-permute-start.3 = (f32[16,128,128]{2,1,0:T(8,128)S(1)}, f32[16,128,128]{2,1,0:T(8,128)}, u32[]{:S(2)}, u32[]{:S(2)}) collective-permute-start(f32[16,128,128]{2,1,0:T(8,128)S(1)} %fusion.6), channel_id=1, source_target_pairs={{0,2},{2,0},{1,3},{3,1},{4,6},{6,4},{5,7},{7,5},{8,10},{10,8},{9,1... | collective-permute-start | bytes 3145736 | tf_op jit(solution)/shard_map/ppermute | solution.py:133
  34.2 1.6 copy.25
  37.7 4.3 %collective-permute-start.4 = (f32[8,128,128]{2,1,0:T(8,128)S(1)}, f32[8,128,128]{2,1,0:T(8,128)}, u32[]{:S(2)}, u32[]{:S(2)}) collective-permute-start(f32[8,128,128]{2,1,0:T(8,128)S(1)} %dynamic-slice_add_fusion), channel_id=1, source_target_pairs={{0,4},{4,8},{8,12},{12,16},{16,20},{20,24},{24,28},{1,5},{5,9},{9,... | collective-permute-start | bytes 1572872 | tf_op jit(solution)/shard_map/ppermute | solution.py:20
  43.6 9.4 %collective-permute-done.4 = f32[8,128,128]{2,1,0:T(8,128)} collective-permute-done((f32[8,128,128]{2,1,0:T(8,128)S(1)}, f32[8,128,128]{2,1,0:T(8,128)}, u32[]{:S(2)}, u32[]{:S(2)}) %collective-permute-start.4) | collective-permute-done | bytes 524320 | tf_op jit(solution)/shard_map/ppermute | solution.py:20
  54.0 3.1 %collective-permute-start.5 = (f32[8,128,128]{2,1,0:T(8,128)S(1)}, f32[8,128,128]{2,1,0:T(8,128)}, u32[]{:S(2)}, u32[]{:S(2)}) collective-permute-start(f32[8,128,128]{2,1,0:T(8,128)S(1)} %add.81), channel_id=1, source_target_pairs={{0,8},{4,12},{8,16},{12,20},{16,24},{20,28},{1,9},{5,13},{9,17},{1... | collective-permute-start | bytes 1572872 | tf_op jit(solution)/shard_map/ppermute | solution.py:20
  59.1 9.1 %collective-permute-done.5 = f32[8,128,128]{2,1,0:T(8,128)} collective-permute-done((f32[8,128,128]{2,1,0:T(8,128)S(1)}, f32[8,128,128]{2,1,0:T(8,128)}, u32[]{:S(2)}, u32[]{:S(2)}) %collective-permute-start.5) | collective-permute-done | bytes 524320 | tf_op jit(solution)/shard_map/ppermute | solution.py:20
  69.4 5.0 %collective-permute-start.6 = (f32[8,128,128]{2,1,0:T(8,128)S(1)}, f32[8,128,128]{2,1,0:T(8,128)}, u32[]{:S(2)}, u32[]{:S(2)}) collective-permute-start(f32[8,128,128]{2,1,0:T(8,128)S(1)} %add.82), channel_id=1, source_target_pairs={{0,16},{4,20},{8,24},{12,28},{1,17},{5,21},{9,25},{13,29},{2,18},{... | collective-permute-start | bytes 1572872 | tf_op jit(solution)/shard_map/ppermute | solution.py:20
  75.7 3.2 %fusion.1 = f32[256,16,128]{0,2,1:T(8,128)S(1)} fusion(bf16[256,16,128]{0,2,1:T(8,128)(2,1)} %bitcast.49, bf16[256,16,128]{0,2,1:T(8,128)(2,1)} %bitcast.54, pred[256,256]{1,0:T(8,128)(4,1)S(1)} %iota_compare_fusion, bf16[256,2048]{1,0:T(8,128)(2,1)} %copy-done.3), kind=kOutput, calls=%fused_computation.12 | convolution fusion | flops 538968064 | bytes 5308416 | tf_op jit(solution)/shard_map/hts,she->the/dot_general | solution.py:106
  79.0 17.3 %collective-permute-done.6 = f32[8,128,128]{2,1,0:T(8,128)} collective-permute-done((f32[8,128,128]{2,1,0:T(8,128)S(1)}, f32[8,128,128]{2,1,0:T(8,128)}, u32[]{:S(2)}, u32[]{:S(2)}) %collective-permute-start.6) | collective-permute-done | bytes 524320 | tf_op jit(solution)/shard_map/ppermute | solution.py:20
  99.8 1.8 multiply_reduce_fusion
  104.9 18.3 %collective-permute-done.12.refs_6_ = bf16[256,2048]{1,0:T(8,128)(2,1)} collective-permute-done((bf16[256,2048]{1,0:T(8,128)(2,1)}, bf16[256,2048]{1,0:T(8,128)(2,1)}, u32[]{:S(2)}, u32[]{:S(2)}) %collective-permute-start.12) | collective-permute-done | bytes 1048608 | tf_op jit(solution)/shard_map/ppermute | solution.py:85
  123.2 2.0 %collective-permute-done.13.refs_8_ = bf16[256,2048]{1,0:T(8,128)(2,1)} collective-permute-done((bf16[256,2048]{1,0:T(8,128)(2,1)}, bf16[256,2048]{1,0:T(8,128)(2,1)}, u32[]{:S(2)}, u32[]{:S(2)}) %collective-permute-start.13) | collective-permute-done | bytes 1048608 | tf_op jit(solution)/shard_map/ppermute | solution.py:85
  125.2 4.3 %collective-permute-done.14.other_ref = bf16[256,2048]{1,0:T(8,128)(2,1)S(1)} collective-permute-done((bf16[256,2048]{1,0:T(8,128)(2,1)S(1)}, bf16[256,2048]{1,0:T(8,128)(2,1)S(1)}, u32[]{:S(2)}, u32[]{:S(2)}) %collective-permute-start.14) | collective-permute-done | bytes 1048608 | tf_op jit(solution)/shard_map/ppermute | solution.py:266
  129.6 1.6 collective-permute-start.17
  131.2 22.9 %collective-permute-done.17.refs_10_ = bf16[256,2048]{1,0:T(8,128)(2,1)S(1)} collective-permute-done((bf16[256,2048]{1,0:T(8,128)(2,1)}, bf16[256,2048]{1,0:T(8,128)(2,1)S(1)}, u32[]{:S(2)}, u32[]{:S(2)}) %collective-permute-start.17) | collective-permute-done | bytes 1048608 | tf_op jit(solution)/shard_map/ppermute | solution.py:85
  155.0 1.8 collective-permute-start.21
  161.0 6.5 %collective-permute-done.21 = bf16[128,2048]{1,0:T(8,128)(2,1)} collective-permute-done((bf16[128,2048]{1,0:T(8,128)(2,1)}, bf16[128,2048]{1,0:T(8,128)(2,1)}, u32[]{:S(2)}, u32[]{:S(2)}) %collective-permute-start.21) | collective-permute-done | bytes 524320 | tf_op jit(solution)/shard_map/ppermute | solution.py:82
  167.5 2.2 %collective-permute-start.20 = (bf16[256,2048]{1,0:T(8,128)(2,1)S(1)}, bf16[256,2048]{1,0:T(8,128)(2,1)}, u32[]{:S(2)}, u32[]{:S(2)}) collective-permute-start(bf16[256,2048]{1,0:T(8,128)(2,1)S(1)} %collective-permute-done.19.refs_12_), channel_id=1, source_target_pairs={{0,2},{2,0},{1,3},{3,1},{4,6},{6,4},{5,7},{7,5},{8,10},{10,8},{9,1... | collective-permute-start | bytes 3145736 | tf_op jit(solution)/shard_map/ppermute | solution.py:277
  169.6 1.9 constant_dynamic-update-slice_fusion.1
  171.5 1.9 %constant_dynamic-update-slice_fusion.refs_14_ = bf16[256,2048]{1,0:T(8,128)(2,1)} fusion(bf16[256,2048]{1,0:T(8,128)(2,1)} %constant_dynamic-update-slice_fusion.1, bf16[128,2048]{1,0:T(8,128)(2,1)} %collective-permute-done.22), kind=kLoop, calls=%fused_computation.41 | loop fusion | bytes 1048576 | tf_op jit(solution)/shard_map/concatenate | solution.py:272
  177.5 9.6 %shard_map.82 = bf16[256,2048]{1,0:T(8,128)(2,1)} custom-call(s32[16]{0:T(128)} %multiply_subtract_fusion.starts_ref, s32[16]{0:T(128)} %get-tuple-element.29.sources_ref, bf16[256,2048]{1,0:T(8,128)(2,1)} %copy-done.1, bf16[256,2048]{1,0:T(8,128)(2,1)} %copy-done.8, bf16[256,2048]{1,0:T(8,128)(2,1)} %refs_0_.1, ...), custom_call_target="tpu_custom_call" | custom-call | tf_op jit(solution)/shard_map/pallas_call | solution.py:198
  (92 shorter events, 31.8 us)
Async XLA Ops:
  5.8 24.3 %collective-permute-start.2 = (bf16[2,128,2048]{2,1,0:T(8,128)(2,1)}, bf16[2,128,2048]{2,1,0:T(8,128)(2,1)S(1)}, u32[]{:S(2)}, u32[]{:S(2)}) collective-permute-start(bf16[2,128,2048]{2,1,0:T(8,128)(2,1)} %bitcast.6), channel_id=1, source_target_pairs={{0,1},{1,0},{2,3},{3,2},{4,5},{5,4},{6,7},{7,6},{8,9},{9,8},{10,11... | collective-permute-start | bytes 3145736 | tf_op jit(solution)/shard_map/ppermute | solution.py:38
  7.1 24.0 %collective-permute-start.1 = (bf16[256,2048]{1,0:T(8,128)(2,1)}, bf16[256,2048]{1,0:T(8,128)(2,1)}, u32[]{:S(2)}, u32[]{:S(2)}) collective-permute-start(bf16[256,2048]{1,0:T(8,128)(2,1)} %refs_0_.1), channel_id=1, source_target_pairs={{4,0},{12,4},{20,12},{28,20},{24,28},{16,24},{8,16},{0,8},{5,1},{1... | collective-permute-start | bytes 3145736 | tf_op jit(solution)/shard_map/ppermute | solution.py:85
  7.2 23.9 %collective-permute-start = (bf16[256,2048]{1,0:T(8,128)(2,1)}, bf16[256,2048]{1,0:T(8,128)(2,1)}, u32[]{:S(2)}, u32[]{:S(2)}) collective-permute-start(bf16[256,2048]{1,0:T(8,128)(2,1)} %refs_0_.1), channel_id=1, source_target_pairs={{0,4},{4,12},{12,20},{20,28},{28,24},{24,16},{16,8},{8,0},{1,5},{5... | collective-permute-start | bytes 3145736 | tf_op jit(solution)/shard_map/ppermute | solution.py:85
  32.1 4.5 %collective-permute-start.3 = (f32[16,128,128]{2,1,0:T(8,128)S(1)}, f32[16,128,128]{2,1,0:T(8,128)}, u32[]{:S(2)}, u32[]{:S(2)}) collective-permute-start(f32[16,128,128]{2,1,0:T(8,128)S(1)} %fusion.6), channel_id=1, source_target_pairs={{0,2},{2,0},{1,3},{3,1},{4,6},{6,4},{5,7},{7,5},{8,10},{10,8},{9,1... | collective-permute-start | bytes 3145736 | tf_op jit(solution)/shard_map/ppermute | solution.py:133
  37.7 15.2 %collective-permute-start.4 = (f32[8,128,128]{2,1,0:T(8,128)S(1)}, f32[8,128,128]{2,1,0:T(8,128)}, u32[]{:S(2)}, u32[]{:S(2)}) collective-permute-start(f32[8,128,128]{2,1,0:T(8,128)S(1)} %dynamic-slice_add_fusion), channel_id=1, source_target_pairs={{0,4},{4,8},{8,12},{12,16},{16,20},{20,24},{24,28},{1,5},{5,9},{9,... | collective-permute-start | bytes 1572872 | tf_op jit(solution)/shard_map/ppermute | solution.py:20
  42.3 16.7 %collective-permute-start.7 = (bf16[1,128,2048]{2,1,0:T(8,128)(2,1)S(1)}, bf16[1,128,2048]{2,1,0:T(8,128)(2,1)S(1)}, u32[]{:S(2)}, u32[]{:S(2)}) collective-permute-start(bf16[1,128,2048]{2,1,0:T(8,128)(2,1)S(1)} %bitcast.56), channel_id=1, source_target_pairs={{0,1},{1,0},{2,3},{3,2},{4,5},{5,4},{6,7},{7,6},{8,9},{9,8},{10,11... | collective-permute-start | bytes 1572872 | tf_op jit(solution)/shard_map/ppermute | solution.py:38
  42.6 54.9 %collective-permute-start.8 = (bf16[256,2048]{1,0:T(8,128)(2,1)}, bf16[256,2048]{1,0:T(8,128)(2,1)}, u32[]{:S(2)}, u32[]{:S(2)}) collective-permute-start(bf16[256,2048]{1,0:T(8,128)(2,1)} %refs_0_.1), channel_id=1, source_target_pairs={{0,2},{2,0},{1,3},{3,1},{4,6},{6,4},{5,7},{7,5},{8,10},{10,8},{9,1... | collective-permute-start | bytes 3145736 | tf_op jit(solution)/shard_map/ppermute | solution.py:253
  54.0 14.2 %collective-permute-start.5 = (f32[8,128,128]{2,1,0:T(8,128)S(1)}, f32[8,128,128]{2,1,0:T(8,128)}, u32[]{:S(2)}, u32[]{:S(2)}) collective-permute-start(f32[8,128,128]{2,1,0:T(8,128)S(1)} %add.81), channel_id=1, source_target_pairs={{0,8},{4,12},{8,16},{12,20},{16,24},{20,28},{1,9},{5,13},{9,17},{1... | collective-permute-start | bytes 1572872 | tf_op jit(solution)/shard_map/ppermute | solution.py:20
  57.4 40.1 %collective-permute-start.9 = (bf16[256,2048]{1,0:T(8,128)(2,1)}, bf16[256,2048]{1,0:T(8,128)(2,1)}, u32[]{:S(2)}, u32[]{:S(2)}) collective-permute-start(bf16[256,2048]{1,0:T(8,128)(2,1)} %collective-permute-done.refs_2_), channel_id=1, source_target_pairs={{0,2},{2,0},{1,3},{3,1},{4,6},{6,4},{5,7},{7,5},{8,10},{10,8},{9,1... | collective-permute-start | bytes 3145736 | tf_op jit(solution)/shard_map/ppermute | solution.py:253
  59.0 38.6 %collective-permute-start.10 = (bf16[256,2048]{1,0:T(8,128)(2,1)}, bf16[256,2048]{1,0:T(8,128)(2,1)}, u32[]{:S(2)}, u32[]{:S(2)}) collective-permute-start(bf16[256,2048]{1,0:T(8,128)(2,1)} %collective-permute-done.1.refs_4_), channel_id=1, source_target_pairs={{0,2},{2,0},{1,3},{3,1},{4,6},{6,4},{5,7},{7,5},{8,10},{10,8},{9,1... | collective-permute-start | bytes 3145736 | tf_op jit(solution)/shard_map/ppermute | solution.py:253
  69.4 26.9 %collective-permute-start.6 = (f32[8,128,128]{2,1,0:T(8,128)S(1)}, f32[8,128,128]{2,1,0:T(8,128)}, u32[]{:S(2)}, u32[]{:S(2)}) collective-permute-start(f32[8,128,128]{2,1,0:T(8,128)S(1)} %add.82), channel_id=1, source_target_pairs={{0,16},{4,20},{8,24},{12,28},{1,17},{5,21},{9,25},{13,29},{2,18},{... | collective-permute-start | bytes 1572872 | tf_op jit(solution)/shard_map/ppermute | solution.py:20
  97.6 2.1 %collective-permute-start.11 = (f32[8,128,128]{2,1,0:T(8,128)S(1)}, f32[8,128,128]{2,1,0:T(8,128)S(1)}, u32[]{:S(2)}, u32[]{:S(2)}) collective-permute-start(f32[8,128,128]{2,1,0:T(8,128)S(1)} %add_subtract_fusion), channel_id=1, source_target_pairs={{0,2},{2,0},{1,3},{3,1},{4,6},{6,4},{5,7},{7,5},{8,10},{10,8},{9,1... | collective-permute-start | bytes 1572872 | tf_op jit(solution)/shard_map/ppermute | solution.py:141
  98.1 25.1 %collective-permute-start.12 = (bf16[256,2048]{1,0:T(8,128)(2,1)}, bf16[256,2048]{1,0:T(8,128)(2,1)}, u32[]{:S(2)}, u32[]{:S(2)}) collective-permute-start(bf16[256,2048]{1,0:T(8,128)(2,1)} %collective-permute-done.refs_2_), channel_id=1, source_target_pairs={{0,4},{4,12},{12,20},{20,28},{28,24},{24,16},{16,8},{8,0},{1,5},{5... | collective-permute-start | bytes 3145736 | tf_op jit(solution)/shard_map/ppermute | solution.py:85
  98.1 27.1 %collective-permute-start.13 = (bf16[256,2048]{1,0:T(8,128)(2,1)}, bf16[256,2048]{1,0:T(8,128)(2,1)}, u32[]{:S(2)}, u32[]{:S(2)}) collective-permute-start(bf16[256,2048]{1,0:T(8,128)(2,1)} %collective-permute-done.1.refs_4_), channel_id=1, source_target_pairs={{4,0},{12,4},{20,12},{28,20},{24,28},{16,24},{8,16},{0,8},{5,1},{1... | collective-permute-start | bytes 3145736 | tf_op jit(solution)/shard_map/ppermute | solution.py:85
  104.6 25.0 %collective-permute-start.14 = (bf16[256,2048]{1,0:T(8,128)(2,1)S(1)}, bf16[256,2048]{1,0:T(8,128)(2,1)S(1)}, u32[]{:S(2)}, u32[]{:S(2)}) collective-permute-start(bf16[256,2048]{1,0:T(8,128)(2,1)S(1)} %copy.38.own_ref), channel_id=1, source_target_pairs={{0,1},{1,0},{2,3},{3,2},{4,5},{5,4},{6,7},{7,6},{8,9},{9,8},{10,11... | collective-permute-start | bytes 3145736 | tf_op jit(solution)/shard_map/ppermute | solution.py:266
  129.6 24.6 %collective-permute-start.17 = (bf16[256,2048]{1,0:T(8,128)(2,1)}, bf16[256,2048]{1,0:T(8,128)(2,1)S(1)}, u32[]{:S(2)}, u32[]{:S(2)}) collective-permute-start(bf16[256,2048]{1,0:T(8,128)(2,1)} %collective-permute-done.12.refs_6_), channel_id=1, source_target_pairs={{0,4},{4,12},{12,20},{20,28},{28,24},{24,16},{16,8},{8,0},{1,5},{5... | collective-permute-start | bytes 3145736 | tf_op jit(solution)/shard_map/ppermute | solution.py:85
  131.2 25.6 %collective-permute-start.19 = (bf16[256,2048]{1,0:T(8,128)(2,1)}, bf16[256,2048]{1,0:T(8,128)(2,1)S(1)}, u32[]{:S(2)}, u32[]{:S(2)}) collective-permute-start(bf16[256,2048]{1,0:T(8,128)(2,1)} %collective-permute-done.13.refs_8_), channel_id=1, source_target_pairs={{4,0},{12,4},{20,12},{28,20},{24,28},{16,24},{8,16},{0,8},{5,1},{1... | collective-permute-start | bytes 3145736 | tf_op jit(solution)/shard_map/ppermute | solution.py:85
  155.0 12.5 %collective-permute-start.21 = (bf16[128,2048]{1,0:T(8,128)(2,1)}, bf16[128,2048]{1,0:T(8,128)(2,1)}, u32[]{:S(2)}, u32[]{:S(2)}) collective-permute-start(bf16[128,2048]{1,0:T(8,128)(2,1)} %slice.20), channel_id=1, source_target_pairs={{0,4},{4,12},{12,20},{20,28},{28,24},{24,16},{16,8},{8,0},{1,5},{5... | collective-permute-start | bytes 1572872 | tf_op jit(solution)/shard_map/ppermute | solution.py:82
  157.7 13.8 %collective-permute-start.22 = (bf16[128,2048]{1,0:T(8,128)(2,1)}, bf16[128,2048]{1,0:T(8,128)(2,1)}, u32[]{:S(2)}, u32[]{:S(2)}) collective-permute-start(bf16[128,2048]{1,0:T(8,128)(2,1)} %slice.21), channel_id=1, source_target_pairs={{4,0},{12,4},{20,12},{28,20},{24,28},{16,24},{8,16},{0,8},{5,1},{1... | collective-permute-start | bytes 1572872 | tf_op jit(solution)/shard_map/ppermute | solution.py:82
  158.9 18.0 %collective-permute-start.15 = (bf16[256,2048]{1,0:T(8,128)(2,1)}, bf16[256,2048]{1,0:T(8,128)(2,1)}, u32[]{:S(2)}, u32[]{:S(2)}) collective-permute-start(bf16[256,2048]{1,0:T(8,128)(2,1)} %collective-permute-done.12.refs_6_), channel_id=1, source_target_pairs={{0,2},{2,0},{1,3},{3,1},{4,6},{6,4},{5,7},{7,5},{8,10},{10,8},{9,1... | collective-permute-start | bytes 3145736 | tf_op jit(solution)/shard_map/ppermute | solution.py:277
  160.5 16.4 %collective-permute-start.16 = (bf16[256,2048]{1,0:T(8,128)(2,1)}, bf16[256,2048]{1,0:T(8,128)(2,1)}, u32[]{:S(2)}, u32[]{:S(2)}) collective-permute-start(bf16[256,2048]{1,0:T(8,128)(2,1)} %collective-permute-done.13.refs_8_), channel_id=1, source_target_pairs={{0,2},{2,0},{1,3},{3,1},{4,6},{6,4},{5,7},{7,5},{8,10},{10,8},{9,1... | collective-permute-start | bytes 3145736 | tf_op jit(solution)/shard_map/ppermute | solution.py:277
  160.6 16.4 %collective-permute-start.18 = (bf16[256,2048]{1,0:T(8,128)(2,1)S(1)}, bf16[256,2048]{1,0:T(8,128)(2,1)}, u32[]{:S(2)}, u32[]{:S(2)}) collective-permute-start(bf16[256,2048]{1,0:T(8,128)(2,1)S(1)} %collective-permute-done.17.refs_10_), channel_id=1, source_target_pairs={{0,2},{2,0},{1,3},{3,1},{4,6},{6,4},{5,7},{7,5},{8,10},{10,8},{9,1... | collective-permute-start | bytes 3145736 | tf_op jit(solution)/shard_map/ppermute | solution.py:277
  167.5 9.5 %collective-permute-start.20 = (bf16[256,2048]{1,0:T(8,128)(2,1)S(1)}, bf16[256,2048]{1,0:T(8,128)(2,1)}, u32[]{:S(2)}, u32[]{:S(2)}) collective-permute-start(bf16[256,2048]{1,0:T(8,128)(2,1)S(1)} %collective-permute-done.19.refs_12_), channel_id=1, source_target_pairs={{0,2},{2,0},{1,3},{3,1},{4,6},{6,4},{5,7},{7,5},{8,10},{10,8},{9,1... | collective-permute-start | bytes 3145736 | tf_op jit(solution)/shard_map/ppermute | solution.py:277
  173.4 4.1 %collective-permute-start.23 = (bf16[256,2048]{1,0:T(8,128)(2,1)}, bf16[256,2048]{1,0:T(8,128)(2,1)}, u32[]{:S(2)}, u32[]{:S(2)}) collective-permute-start(bf16[256,2048]{1,0:T(8,128)(2,1)} %constant_dynamic-update-slice_fusion.refs_14_), channel_id=1, source_target_pairs={{0,2},{2,0},{1,3},{3,1},{4,6},{6,4},{5,7},{7,5},{8,10},{10,8},{9,1... | collective-permute-start | bytes 3145736 | tf_op jit(solution)/shard_map/ppermute | solution.py:277
  (13 other events, 308.3 us)

commit v24 on v11

--- a/solution.py
+++ b/solution.py
@@ -256,13 +256,16 @@
     swapped += [lax.ppermute(w, "core", SWAP) for w in got[len(swapped):]]
     chip_prefix_half, within_block, swapped = barrier((chip_prefix_half, within_block, swapped))
     for step in range(2, n_steps + 1):
-        ahead, behind = ring_step(ahead, behind, order, last=step == n_steps)
         if step == n_steps:
-            got.append(jnp.concatenate([ahead, behind], 0))
+            forward, backward = ring_links(order)
+            pairs = [(a * 2, b * 2) for a, b in forward] + [(a * 2 + 1, b * 2 + 1) for a, b in backward]
+            farthest = jnp.where(core == 0, ahead, behind)
+            got.append(lax.ppermute(farthest, ("chip", "core"), pairs))
             offsets.append(step)
-        else:
-            got += [ahead, behind]
-            offsets += [step, -step]
+            continue
+        ahead, behind = ring_step(ahead, behind, order)
+        got += [ahead, behind]
+        offsets += [step, -step]
     swapped += [lax.ppermute(w, "core", SWAP) for w in got[len(swapped):]]
     prefix = chip_finish(chip_prefix_half, partner_state, core)
     normed = normalize(query_heads, prefix, within_block, norm_gain)

time: 175 us -> 187 us (1.069)
  waiting for transfers between devices: 96.2 us -> 117 us
  local copies, waits for them, and re-layouts: 20.8 us -> 14.4 us
  starting transfers between devices: 32 us -> 27.2 us
  other arithmetic: 8.14 us -> 11.4 us
    ppermute x3, waiting for transfers between devices: 38.6 us -> 58.1 us  [exclusive_prefix(): total = total + lax.ppermute(total, axis, pairs)]
    ppermute x3, waiting for transfers between devices: 29.2 us -> 15.8 us  [ring_step(): lax.ppermute(ahead, 'chip', forward)]
    ppermute x1, waiting for transfers between devices: 0.01 us -> 11.2 us  [gather_head(): other = lax.ppermute(normed, 'head', SWAP)]
    slice x2 -> x0, local copies, waits for them, and re-layouts: 2.99 us -> none  [the longest x1 1.91 us: ring_step(): behind[half_rows:]]
    ppermute x3, waiting for transfers between devices: 1.01 us -> 3.68 us  [ring_step(): lax.ppermute(behind, 'chip', backward)]
    unnamed x28 -> x23, local copies, waits for them, and re-layouts: 7.43 us -> 5.03 us
    select_n x0 -> x1, other arithmetic: none -> 2.32 us  [local_ring(): farthest = jnp.where(core == 0, ahead, behind)]
    ppermute x1, starting transfers between devices: 2.71 us -> 0.65 us  [chip_finish(): other_half = lax.ppermute(chip_prefix_half, 'core', SWAP)]
  transfers between devices with their start and end apart: 24 -> 23, of which waited for: 11 -> 12; matrix products, arithmetic and copies ran while one was open for 14% -> 12% of each run, Pallas kernels for 0% -> 0%
where the time goes in v24:
time: 187 us; the launch traced here: 186 us
  waiting for transfers between devices  117 us (63%)
  starting transfers between devices  27.2 us (15%)
  local copies, waits for them, and re-layouts  14.4 us (8%)
  other arithmetic  11.4 us (6%)
  Pallas kernels  9.62 us (5%)
  matrix products  5.54 us (3%)
    ppermute x3, waiting for transfers between devices, exclusive_prefix(): total = total + lax.ppermute(total, axis, pairs)  58.1 us
    ppermute x2, waiting for transfers between devices, head_blocks(): other = lax.ppermute(sent, 'head', SWAP)  21.1 us
    ppermute x3, waiting for transfers between devices, ring_step(): lax.ppermute(ahead, 'chip', forward)  15.8 us
    ppermute x1, waiting for transfers between devices, gather_head(): other = lax.ppermute(normed, 'head', SWAP)  11.2 us
    pallas_call x1, Pallas kernels, project_blocks(): pl.pallas_call(kernel, out_shape=jax.ShapeDtypeStruct((tokens, cols), jnp...  9.62 us
    ppermute x3, starting transfers between devices, exclusive_prefix(): total = total + lax.ppermute(total, axis, pairs)  9.52 us
    ppermute x5, starting transfers between devices, local_ring(): swapped += [lax.ppermute(w, 'core', SWAP) for w in got[len(swapped):]]  7.57 us
    unnamed x23, local copies, waits for them, and re-layouts  5.03 us
  transfers between devices with their start and end apart: 23, of which 12 were waited for; matrix products, arithmetic and copies ran while one was open for 12% of the time, Pallas kernels for 0%

profile of v24, /device:TPU:13, one launch (start us, length us, event | category | flops | bytes accessed | tf_op | source)
XLA Modules:
  0.0 185.5 jit_solution(6015341715975751910)
XLA Ops:
  0.0 1.7 copy.19
  3.6 2.3 %copy.22 = bf16[2,128,1,2048]{3,1,0,2:T(8,128)(2,1)} copy(bf16[2,128,1,2048]{1,3,2,0:T(8,128)(2,1)} %get-tuple-element.30) | data formatting | bytes 2097152 | tf_op jit(solution)/shard_map/jit(dynamic_index_in_dim)/dynamic_slice | solution.py:37
  9.0 21.1 %collective-permute-done.2 = bf16[2,128,2048]{2,1,0:T(8,128)(2,1)S(1)} collective-permute-done((bf16[2,128,2048]{2,1,0:T(8,128)(2,1)}, bf16[2,128,2048]{2,1,0:T(8,128)(2,1)S(1)}, u32[]{:S(2)}, u32[]{:S(2)}) %collective-permute-start.2) | collective-permute-done | bytes 1048608 | tf_op jit(solution)/shard_map/ppermute | solution.py:38
  33.1 2.2 %collective-permute-start.3 = (f32[16,128,128]{2,1,0:T(8,128)S(1)}, f32[16,128,128]{2,1,0:T(8,128)}, u32[]{:S(2)}, u32[]{:S(2)}) collective-permute-start(f32[16,128,128]{2,1,0:T(8,128)S(1)} %fusion.6), channel_id=1, source_target_pairs={{0,2},{2,0},{1,3},{3,1},{4,6},{6,4},{5,7},{7,5},{8,10},{10,8},{9,1... | collective-permute-start | bytes 3145736 | tf_op jit(solution)/shard_map/ppermute | solution.py:133
  35.3 2.4 %collective-permute-done.3 = f32[16,128,128]{2,1,0:T(8,128)} collective-permute-done((f32[16,128,128]{2,1,0:T(8,128)S(1)}, f32[16,128,128]{2,1,0:T(8,128)}, u32[]{:S(2)}, u32[]{:S(2)}) %collective-permute-start.3) | collective-permute-done | bytes 1048608 | tf_op jit(solution)/shard_map/ppermute | solution.py:133
  38.8 2.0 %collective-permute-start.4 = (f32[8,128,128]{2,1,0:T(8,128)S(1)}, f32[8,128,128]{2,1,0:T(8,128)S(1)}, u32[]{:S(2)}, u32[]{:S(2)}) collective-permute-start(f32[8,128,128]{2,1,0:T(8,128)S(1)} %dynamic-slice_add_fusion), channel_id=1, source_target_pairs={{0,4},{4,8},{8,12},{12,16},{16,20},{20,24},{24,28},{1,5},{5,9},{9,... | collective-permute-start | bytes 1572872 | tf_op jit(solution)/shard_map/ppermute | solution.py:20
  42.4 11.6 %collective-permute-done.4 = f32[8,128,128]{2,1,0:T(8,128)S(1)} collective-permute-done((f32[8,128,128]{2,1,0:T(8,128)S(1)}, f32[8,128,128]{2,1,0:T(8,128)S(1)}, u32[]{:S(2)}, u32[]{:S(2)}) %collective-permute-start.4) | collective-permute-done | bytes 524320 | tf_op jit(solution)/shard_map/ppermute | solution.py:20
  54.0 3.2 %collective-permute-start.5 = (f32[8,128,128]{2,1,0:T(8,128)S(1)}, f32[8,128,128]{2,1,0:T(8,128)}, u32[]{:S(2)}, u32[]{:S(2)}) collective-permute-start(f32[8,128,128]{2,1,0:T(8,128)S(1)} %add.80), channel_id=1, source_target_pairs={{0,8},{4,12},{8,16},{12,20},{16,24},{20,28},{1,9},{5,13},{9,17},{1... | collective-permute-start | bytes 1572872 | tf_op jit(solution)/shard_map/ppermute | solution.py:20
  57.3 1.6 copy.25
  60.3 26.2 %collective-permute-done.5 = f32[8,128,128]{2,1,0:T(8,128)} collective-permute-done((f32[8,128,128]{2,1,0:T(8,128)S(1)}, f32[8,128,128]{2,1,0:T(8,128)}, u32[]{:S(2)}, u32[]{:S(2)}) %collective-permute-start.5) | collective-permute-done | bytes 524320 | tf_op jit(solution)/shard_map/ppermute | solution.py:20
  87.6 4.3 %collective-permute-start.6 = (f32[8,128,128]{2,1,0:T(8,128)S(1)}, f32[8,128,128]{2,1,0:T(8,128)S(1)}, u32[]{:S(2)}, u32[]{:S(2)}) collective-permute-start(f32[8,128,128]{2,1,0:T(8,128)S(1)} %add.81), channel_id=1, source_target_pairs={{0,16},{4,20},{8,24},{12,28},{1,17},{5,21},{9,25},{13,29},{2,18},{... | collective-permute-start | bytes 1572872 | tf_op jit(solution)/shard_map/ppermute | solution.py:20
  91.9 1.5 collective-permute-start.8
  94.3 20.3 %collective-permute-done.6 = f32[8,128,128]{2,1,0:T(8,128)S(1)} collective-permute-done((f32[8,128,128]{2,1,0:T(8,128)S(1)}, f32[8,128,128]{2,1,0:T(8,128)S(1)}, u32[]{:S(2)}, u32[]{:S(2)}) %collective-permute-start.6) | collective-permute-done | bytes 524320 | tf_op jit(solution)/shard_map/ppermute | solution.py:20
  116.9 3.2 %fusion.1 = f32[256,16,128]{0,2,1:T(8,128)S(1)} fusion(bf16[256,16,128]{0,2,1:T(8,128)(2,1)} %bitcast.49, bf16[256,16,128]{0,2,1:T(8,128)(2,1)} %bitcast.54, pred[256,256]{1,0:T(8,128)(4,1)S(1)} %iota_compare_fusion, bf16[256,2048]{1,0:T(8,128)(2,1)} %copy-done.2), kind=kOutput, calls=%fused_computation.13 | convolution fusion | flops 538968064 | bytes 5308416 | tf_op jit(solution)/shard_map/hts,she->the/dot_general | solution.py:106
  122.0 15.2 %collective-permute-done.17.refs_10_ = bf16[256,2048]{1,0:T(8,128)(2,1)} collective-permute-done((bf16[256,2048]{1,0:T(8,128)(2,1)}, bf16[256,2048]{1,0:T(8,128)(2,1)}, u32[]{:S(2)}, u32[]{:S(2)}) %collective-permute-start.17) | collective-permute-done | bytes 1048608 | tf_op jit(solution)/shard_map/ppermute | solution.py:85
  137.2 2.7 %collective-permute-done.19.refs_12_ = bf16[256,2048]{1,0:T(8,128)(2,1)} collective-permute-done((bf16[256,2048]{1,0:T(8,128)(2,1)}, bf16[256,2048]{1,0:T(8,128)(2,1)}, u32[]{:S(2)}, u32[]{:S(2)}) %collective-permute-start.19) | collective-permute-done | bytes 1048608 | tf_op jit(solution)/shard_map/ppermute | solution.py:85
  139.9 2.3 %broadcast_select_fusion = bf16[256,2048]{1,0:T(8,128)(2,1)} fusion(bf16[256,2048]{1,0:T(8,128)(2,1)} %collective-permute-done.17.refs_10_, bf16[256,2048]{1,0:T(8,128)(2,1)} %collective-permute-done.19.refs_12_, pred[]{:T(512)S(6)} %eq.8), kind=kLoop, calls=%fused_computation.28 | loop fusion | flops 524288 | bytes 3145729 | tf_op jit(solution)/shard_map/jit(_where)/select_n | solution.py:262
  142.6 1.8 multiply_reduce_fusion
  150.3 2.4 %collective-permute-start.14 = (bf16[256,2048]{1,0:T(8,128)(2,1)}, bf16[256,2048]{1,0:T(8,128)(2,1)S(1)}, u32[]{:S(2)}, u32[]{:S(2)}) collective-permute-start(bf16[256,2048]{1,0:T(8,128)(2,1)} %collective-permute-done.13.refs_6_), channel_id=1, source_target_pairs={{0,2},{2,0},{1,3},{3,1},{4,6},{6,4},{5,7},{7,5},{8,10},{10,8},{9,1... | collective-permute-start | bytes 3145736 | tf_op jit(solution)/shard_map/ppermute | solution.py:269
  153.3 3.9 %collective-permute-done.21.refs_14_ = bf16[256,2048]{1,0:T(8,128)(2,1)} collective-permute-done((bf16[256,2048]{1,0:T(8,128)(2,1)}, bf16[256,2048]{1,0:T(8,128)(2,1)}, u32[]{:S(2)}, u32[]{:S(2)}) %collective-permute-start.21) | collective-permute-done | bytes 1048608 | tf_op jit(solution)/shard_map/ppermute | solution.py:263
  158.8 11.2 %collective-permute-done.12 = bf16[256,2048]{1,0:T(8,128)(2,1)S(1)} collective-permute-done((bf16[256,2048]{1,0:T(8,128)(2,1)S(1)}, bf16[256,2048]{1,0:T(8,128)(2,1)S(1)}, u32[]{:S(2)}, u32[]{:S(2)}) %collective-permute-start.12) | collective-permute-done | bytes 1048608 | tf_op jit(solution)/shard_map/ppermute | solution.py:127
  170.0 3.1 %collective-permute-start.22 = (bf16[256,2048]{1,0:T(8,128)(2,1)}, bf16[256,2048]{1,0:T(8,128)(2,1)}, u32[]{:S(2)}, u32[]{:S(2)}) collective-permute-start(bf16[256,2048]{1,0:T(8,128)(2,1)} %collective-permute-done.21.refs_14_), channel_id=1, source_target_pairs={{0,2},{2,0},{1,3},{3,1},{4,6},{6,4},{5,7},{7,5},{8,10},{10,8},{9,1... | collective-permute-start | bytes 3145736 | tf_op jit(solution)/shard_map/ppermute | solution.py:269
  173.3 1.6 pad_maximum_fusion.normed_ref
  175.9 9.6 %shard_map.82 = bf16[256,2048]{1,0:T(8,128)(2,1)} custom-call(s32[16]{0:T(128)} %mul.41.starts_ref, bf16[256,4096]{1,0:T(8,128)(2,1)} %pad_maximum_fusion.normed_ref, bf16[256,2048]{1,0:T(8,128)(2,1)} %refs_0_.1, bf16[256,2048]{1,0:T(8,128)(2,1)} %collective-permute-done.8.refs_1_, bf16[256,2048]{1,0:T(8,128)(2,1)} %collective-permute-done.refs_2_, ...), custom_call_target="tpu_custom_call" | custom-call | tf_op jit(solution)/shard_map/pallas_call | solution.py:192
  (81 shorter events, 27.5 us)
Async XLA Ops:
  5.8 24.3 %collective-permute-start.2 = (bf16[2,128,2048]{2,1,0:T(8,128)(2,1)}, bf16[2,128,2048]{2,1,0:T(8,128)(2,1)S(1)}, u32[]{:S(2)}, u32[]{:S(2)}) collective-permute-start(bf16[2,128,2048]{2,1,0:T(8,128)(2,1)} %bitcast.6), channel_id=1, source_target_pairs={{0,1},{1,0},{2,3},{3,2},{4,5},{5,4},{6,7},{7,6},{8,9},{9,8},{10,11... | collective-permute-start | bytes 3145736 | tf_op jit(solution)/shard_map/ppermute | solution.py:38
  7.0 24.0 %collective-permute-start = (bf16[256,2048]{1,0:T(8,128)(2,1)}, bf16[256,2048]{1,0:T(8,128)(2,1)}, u32[]{:S(2)}, u32[]{:S(2)}) collective-permute-start(bf16[256,2048]{1,0:T(8,128)(2,1)} %refs_0_.1), channel_id=1, source_target_pairs={{0,4},{4,12},{12,20},{20,28},{28,24},{24,16},{16,8},{8,0},{1,5},{5... | collective-permute-start | bytes 3145736 | tf_op jit(solution)/shard_map/ppermute | solution.py:85
  8.3 23.7 %collective-permute-start.1 = (bf16[256,2048]{1,0:T(8,128)(2,1)}, bf16[256,2048]{1,0:T(8,128)(2,1)}, u32[]{:S(2)}, u32[]{:S(2)}) collective-permute-start(bf16[256,2048]{1,0:T(8,128)(2,1)} %refs_0_.1), channel_id=1, source_target_pairs={{4,0},{12,4},{20,12},{28,20},{24,28},{16,24},{8,16},{0,8},{5,1},{1... | collective-permute-start | bytes 3145736 | tf_op jit(solution)/shard_map/ppermute | solution.py:85
  33.1 4.6 %collective-permute-start.3 = (f32[16,128,128]{2,1,0:T(8,128)S(1)}, f32[16,128,128]{2,1,0:T(8,128)}, u32[]{:S(2)}, u32[]{:S(2)}) collective-permute-start(f32[16,128,128]{2,1,0:T(8,128)S(1)} %fusion.6), channel_id=1, source_target_pairs={{0,2},{2,0},{1,3},{3,1},{4,6},{6,4},{5,7},{7,5},{8,10},{10,8},{9,1... | collective-permute-start | bytes 3145736 | tf_op jit(solution)/shard_map/ppermute | solution.py:133
  38.8 15.1 %collective-permute-start.4 = (f32[8,128,128]{2,1,0:T(8,128)S(1)}, f32[8,128,128]{2,1,0:T(8,128)S(1)}, u32[]{:S(2)}, u32[]{:S(2)}) collective-permute-start(f32[8,128,128]{2,1,0:T(8,128)S(1)} %dynamic-slice_add_fusion), channel_id=1, source_target_pairs={{0,4},{4,8},{8,12},{12,16},{16,20},{20,24},{24,28},{1,5},{5,9},{9,... | collective-permute-start | bytes 1572872 | tf_op jit(solution)/shard_map/ppermute | solution.py:20
  40.9 52.9 %collective-permute-start.13 = (bf16[256,2048]{1,0:T(8,128)(2,1)}, bf16[256,2048]{1,0:T(8,128)(2,1)}, u32[]{:S(2)}, u32[]{:S(2)}) collective-permute-start(bf16[256,2048]{1,0:T(8,128)(2,1)} %collective-permute-done.refs_2_), channel_id=1, source_target_pairs={{0,4},{4,12},{12,20},{20,28},{28,24},{24,16},{16,8},{8,0},{1,5},{5... | collective-permute-start | bytes 3145736 | tf_op jit(solution)/shard_map/ppermute | solution.py:85
  42.2 52.1 %collective-permute-start.15 = (bf16[256,2048]{1,0:T(8,128)(2,1)}, bf16[256,2048]{1,0:T(8,128)(2,1)}, u32[]{:S(2)}, u32[]{:S(2)}) collective-permute-start(bf16[256,2048]{1,0:T(8,128)(2,1)} %collective-permute-done.1.refs_4_), channel_id=1, source_target_pairs={{4,0},{12,4},{20,12},{28,20},{24,28},{16,24},{8,16},{0,8},{5,1},{1... | collective-permute-start | bytes 3145736 | tf_op jit(solution)/shard_map/ppermute | solution.py:85
  54.0 32.5 %collective-permute-start.5 = (f32[8,128,128]{2,1,0:T(8,128)S(1)}, f32[8,128,128]{2,1,0:T(8,128)}, u32[]{:S(2)}, u32[]{:S(2)}) collective-permute-start(f32[8,128,128]{2,1,0:T(8,128)S(1)} %add.80), channel_id=1, source_target_pairs={{0,8},{4,12},{8,16},{12,20},{16,24},{20,28},{1,9},{5,13},{9,17},{1... | collective-permute-start | bytes 1572872 | tf_op jit(solution)/shard_map/ppermute | solution.py:20
  60.0 33.7 %collective-permute-start.7 = (bf16[1,128,2048]{2,1,0:T(8,128)(2,1)}, bf16[1,128,2048]{2,1,0:T(8,128)(2,1)S(1)}, u32[]{:S(2)}, u32[]{:S(2)}) collective-permute-start(bf16[1,128,2048]{2,1,0:T(8,128)(2,1)} %bitcast.11), channel_id=1, source_target_pairs={{0,1},{1,0},{2,3},{3,2},{4,5},{5,4},{6,7},{7,6},{8,9},{9,8},{10,11... | collective-permute-start | bytes 1572872 | tf_op jit(solution)/shard_map/ppermute | solution.py:38
  87.6 27.0 %collective-permute-start.6 = (f32[8,128,128]{2,1,0:T(8,128)S(1)}, f32[8,128,128]{2,1,0:T(8,128)S(1)}, u32[]{:S(2)}, u32[]{:S(2)}) collective-permute-start(f32[8,128,128]{2,1,0:T(8,128)S(1)} %add.81), channel_id=1, source_target_pairs={{0,16},{4,20},{8,24},{12,28},{1,17},{5,21},{9,25},{13,29},{2,18},{... | collective-permute-start | bytes 1572872 | tf_op jit(solution)/shard_map/ppermute | solution.py:20
  91.9 29.4 %collective-permute-start.8 = (bf16[256,2048]{1,0:T(8,128)(2,1)}, bf16[256,2048]{1,0:T(8,128)(2,1)}, u32[]{:S(2)}, u32[]{:S(2)}) collective-permute-start(bf16[256,2048]{1,0:T(8,128)(2,1)} %refs_0_.1), channel_id=1, source_target_pairs={{0,2},{2,0},{1,3},{3,1},{4,6},{6,4},{5,7},{7,5},{8,10},{10,8},{9,1... | collective-permute-start | bytes 3145736 | tf_op jit(solution)/shard_map/ppermute | solution.py:247
  93.7 27.6 %collective-permute-start.10 = (bf16[256,2048]{1,0:T(8,128)(2,1)}, bf16[256,2048]{1,0:T(8,128)(2,1)}, u32[]{:S(2)}, u32[]{:S(2)}) collective-permute-start(bf16[256,2048]{1,0:T(8,128)(2,1)} %collective-permute-done.1.refs_4_), channel_id=1, source_target_pairs={{0,2},{2,0},{1,3},{3,1},{4,6},{6,4},{5,7},{7,5},{8,10},{10,8},{9,1... | collective-permute-start | bytes 3145736 | tf_op jit(solution)/shard_map/ppermute | solution.py:247
  93.8 27.5 %collective-permute-start.9 = (bf16[256,2048]{1,0:T(8,128)(2,1)}, bf16[256,2048]{1,0:T(8,128)(2,1)}, u32[]{:S(2)}, u32[]{:S(2)}) collective-permute-start(bf16[256,2048]{1,0:T(8,128)(2,1)} %collective-permute-done.refs_2_), channel_id=1, source_target_pairs={{0,2},{2,0},{1,3},{3,1},{4,6},{6,4},{5,7},{7,5},{8,10},{10,8},{9,1... | collective-permute-start | bytes 3145736 | tf_op jit(solution)/shard_map/ppermute | solution.py:247
  94.3 42.9 %collective-permute-start.17 = (bf16[256,2048]{1,0:T(8,128)(2,1)}, bf16[256,2048]{1,0:T(8,128)(2,1)}, u32[]{:S(2)}, u32[]{:S(2)}) collective-permute-start(bf16[256,2048]{1,0:T(8,128)(2,1)} %collective-permute-done.13.refs_6_), channel_id=1, source_target_pairs={{0,4},{4,12},{12,20},{20,28},{28,24},{24,16},{16,8},{8,0},{1,5},{5... | collective-permute-start | bytes 3145736 | tf_op jit(solution)/shard_map/ppermute | solution.py:85
  115.4 24.4 %collective-permute-start.19 = (bf16[256,2048]{1,0:T(8,128)(2,1)}, bf16[256,2048]{1,0:T(8,128)(2,1)}, u32[]{:S(2)}, u32[]{:S(2)}) collective-permute-start(bf16[256,2048]{1,0:T(8,128)(2,1)} %collective-permute-done.15.refs_8_), channel_id=1, source_target_pairs={{4,0},{12,4},{20,12},{28,20},{24,28},{16,24},{8,16},{0,8},{5,1},{1... | collective-permute-start | bytes 3145736 | tf_op jit(solution)/shard_map/ppermute | solution.py:85
  121.3 21.3 %copy-start.3 = (bf16[1,256,2048]{1,2,0:T(8,128)(2,1)S(1)}, bf16[1,256,2048]{1,2,0:T(8,128)(2,1)}, u32[]{:S(2)}) copy-start(bf16[1,256,2048]{1,2,0:T(8,128)(2,1)} %copy.28) | copy-start | bytes 3145732
  121.3 21.2 %collective-permute-start.11 = (f32[8,128,128]{2,1,0:T(8,128)S(1)}, f32[8,128,128]{2,1,0:T(8,128)S(1)}, u32[]{:S(2)}, u32[]{:S(2)}) collective-permute-start(f32[8,128,128]{2,1,0:T(8,128)S(1)} %add_subtract_fusion), channel_id=1, source_target_pairs={{0,2},{2,0},{1,3},{3,1},{4,6},{6,4},{5,7},{7,5},{8,10},{10,8},{9,1... | collective-permute-start | bytes 1572872 | tf_op jit(solution)/shard_map/ppermute | solution.py:141
  142.2 15.0 %collective-permute-start.21 = (bf16[256,2048]{1,0:T(8,128)(2,1)}, bf16[256,2048]{1,0:T(8,128)(2,1)}, u32[]{:S(2)}, u32[]{:S(2)}) collective-permute-start(bf16[256,2048]{1,0:T(8,128)(2,1)} %broadcast_select_fusion), channel_id=1, source_target_pairs={{0,4},{4,12},{12,20},{20,28},{28,24},{24,16},{16,8},{8,0},{6,2},{1... | collective-permute-start | bytes 3145736 | tf_op jit(solution)/shard_map/ppermute | solution.py:263
  147.4 22.6 %collective-permute-start.12 = (bf16[256,2048]{1,0:T(8,128)(2,1)S(1)}, bf16[256,2048]{1,0:T(8,128)(2,1)S(1)}, u32[]{:S(2)}, u32[]{:S(2)}) collective-permute-start(bf16[256,2048]{1,0:T(8,128)(2,1)S(1)} %copy.38), channel_id=1, source_target_pairs={{0,1},{1,0},{2,3},{3,2},{4,5},{5,4},{6,7},{7,6},{8,9},{9,8},{10,11... | collective-permute-start | bytes 3145736 | tf_op jit(solution)/shard_map/ppermute | solution.py:127
  150.3 24.6 %collective-permute-start.14 = (bf16[256,2048]{1,0:T(8,128)(2,1)}, bf16[256,2048]{1,0:T(8,128)(2,1)S(1)}, u32[]{:S(2)}, u32[]{:S(2)}) collective-permute-start(bf16[256,2048]{1,0:T(8,128)(2,1)} %collective-permute-done.13.refs_6_), channel_id=1, source_target_pairs={{0,2},{2,0},{1,3},{3,1},{4,6},{6,4},{5,7},{7,5},{8,10},{10,8},{9,1... | collective-permute-start | bytes 3145736 | tf_op jit(solution)/shard_map/ppermute | solution.py:269
  152.8 22.1 %collective-permute-start.16 = (bf16[256,2048]{1,0:T(8,128)(2,1)}, bf16[256,2048]{1,0:T(8,128)(2,1)}, u32[]{:S(2)}, u32[]{:S(2)}) collective-permute-start(bf16[256,2048]{1,0:T(8,128)(2,1)} %collective-permute-done.15.refs_8_), channel_id=1, source_target_pairs={{0,2},{2,0},{1,3},{3,1},{4,6},{6,4},{5,7},{7,5},{8,10},{10,8},{9,1... | collective-permute-start | bytes 3145736 | tf_op jit(solution)/shard_map/ppermute | solution.py:269
  152.8 22.1 %collective-permute-start.18 = (bf16[256,2048]{1,0:T(8,128)(2,1)}, bf16[256,2048]{1,0:T(8,128)(2,1)}, u32[]{:S(2)}, u32[]{:S(2)}) collective-permute-start(bf16[256,2048]{1,0:T(8,128)(2,1)} %collective-permute-done.17.refs_10_), channel_id=1, source_target_pairs={{0,2},{2,0},{1,3},{3,1},{4,6},{6,4},{5,7},{7,5},{8,10},{10,8},{9,1... | collective-permute-start | bytes 3145736 | tf_op jit(solution)/shard_map/ppermute | solution.py:269
  157.2 17.7 %collective-permute-start.20 = (bf16[256,2048]{1,0:T(8,128)(2,1)}, bf16[256,2048]{1,0:T(8,128)(2,1)}, u32[]{:S(2)}, u32[]{:S(2)}) collective-permute-start(bf16[256,2048]{1,0:T(8,128)(2,1)} %collective-permute-done.19.refs_12_), channel_id=1, source_target_pairs={{0,2},{2,0},{1,3},{3,1},{4,6},{6,4},{5,7},{7,5},{8,10},{10,8},{9,1... | collective-permute-start | bytes 3145736 | tf_op jit(solution)/shard_map/ppermute | solution.py:269
  170.0 5.7 %collective-permute-start.22 = (bf16[256,2048]{1,0:T(8,128)(2,1)}, bf16[256,2048]{1,0:T(8,128)(2,1)}, u32[]{:S(2)}, u32[]{:S(2)}) collective-permute-start(bf16[256,2048]{1,0:T(8,128)(2,1)} %collective-permute-done.21.refs_14_), channel_id=1, source_target_pairs={{0,2},{2,0},{1,3},{3,1},{4,6},{6,4},{5,7},{7,5},{8,10},{10,8},{9,1... | collective-permute-start | bytes 3145736 | tf_op jit(solution)/shard_map/ppermute | solution.py:269
  (9 other events, 18.0 us)

commit v25 on v14

--- a/solution.py
+++ b/solution.py
@@ -273,7 +273,7 @@
     sources = jnp.asarray(order, jnp.int32)[(ring_place - jnp.asarray(offsets, jnp.int32)) % n_chip]
     cores = jnp.stack([core, 1 - core]).astype(jnp.int32)
     starts = ((sources[:, None] * 2 + cores[None, :]) * out_weight.shape[0]).reshape(-1)
-    return project_blocks(gathered, starts, [w for pair in zip(got, swapped) for w in pair])
+    return project_blocks(gathered, starts, [w for pair in zip(got, swapped) for w in pair], group=2)
 
 
 def solution(mesh):

time: 175 us -> 174 us (level)
  no operation moved by 1% of the time
where the time goes in v25:
time: 174 us; the launch traced here: 171 us
  waiting for transfers between devices  100 us (57%)
  starting transfers between devices  29.1 us (17%)
  local copies, waits for them, and re-layouts  17.3 us (10%)
  other arithmetic  11.4 us (7%)
  Pallas kernels  9.08 us (5%)
  matrix products  3.92 us (2%)
    ppermute x3, waiting for transfers between devices, exclusive_prefix(): total = total + lax.ppermute(total, axis, pairs)  38.6 us
    ppermute x3, waiting for transfers between devices, ring_step(): lax.ppermute(ahead, 'chip', forward)  25.9 us
    ppermute x3, waiting for transfers between devices, head_blocks(): other = lax.ppermute(tuple(sent), 'head', SWAP)  18 us
    pallas_call x1, Pallas kernels, project_blocks(): pl.pallas_call(kernel, out_shape=jax.ShapeDtypeStruct((tokens, cols), jnp...  9.08 us
    ppermute x3, starting transfers between devices, exclusive_prefix(): total = total + lax.ppermute(total, axis, pairs)  8.54 us
    ppermute x1, waiting for transfers between devices, ring_step(): lax.ppermute(ahead[:half_rows], 'chip', forward)  7.32 us
    ppermute x3, waiting for transfers between devices, ring_step(): lax.ppermute(behind, 'chip', backward)  6.66 us
    unnamed x35, local copies, waits for them, and re-layouts  6.16 us
  transfers between devices with their start and end apart: 25, of which 14 were waited for; matrix products, arithmetic and copies ran while one was open for 17% of the time, Pallas kernels for 0%

profile of v25, /device:TPU:13, one launch (start us, length us, event | category | flops | bytes accessed | tf_op | source)
XLA Modules:
  0.0 171.3 jit_solution(259770058915663491)
XLA Ops:
  5.0 2.3 %constant_dynamic-slice_fusion.1 = (bf16[128,2048]{1,0:T(8,128)(2,1)}, bf16[128,2048]{1,0:T(8,128)(2,1)}, bf16[128,2048]{1,0:T(8,128)(2,1)S(1)}, bf16[128,2048]{1,0:T(8,128)(2,1)S(1)}) fusion(bf16[128,4096]{1,0:T(8,128)(2,1)S(1)} %copy-done.9, s32[]{:T(128)S(6)} %select_n.96, s32[]{:T(128)S(6)} %select_n.97, bf16[128,4096]{1,0:T(8,128)(2,1)} %param.10), kind=kLoop, calls=%fused_computation.38 | loop fusion | bytes 4194312 | tf_op jit(solution)/shard_map/dynamic_slice | solution.py:34
  8.5 6.9 %collective-permute-done.2 = bf16[128,2048]{0,1:T(8,128)(2,1)S(1)} collective-permute-done((bf16[128,2048]{0,1:T(8,128)(2,1)}, bf16[128,2048]{0,1:T(8,128)(2,1)S(1)}, u32[]{:S(2)}, u32[]{:S(2)}) %collective-permute-start.2) | collective-permute-done | bytes 524320 | tf_op jit(solution)/shard_map/ppermute | solution.py:36
  15.7 11.0 %collective-permute-done.3 = bf16[128,2048]{0,1:T(8,128)(2,1)S(1)} collective-permute-done((bf16[128,2048]{0,1:T(8,128)(2,1)S(1)}, bf16[128,2048]{0,1:T(8,128)(2,1)S(1)}, u32[]{:S(2)}, u32[]{:S(2)}) %collective-permute-start.3) | collective-permute-done | bytes 524320 | tf_op jit(solution)/shard_map/ppermute | solution.py:36
  29.0 2.2 %collective-permute-start.4 = (f32[16,128,128]{2,1,0:T(8,128)S(1)}, f32[16,128,128]{2,1,0:T(8,128)S(1)}, u32[]{:S(2)}, u32[]{:S(2)}) collective-permute-start(f32[16,128,128]{2,1,0:T(8,128)S(1)} %fusion.11), channel_id=1, source_target_pairs={{0,2},{2,0},{1,3},{3,1},{4,6},{6,4},{5,7},{7,5},{8,10},{10,8},{9,1... | collective-permute-start | bytes 3145736 | tf_op jit(solution)/shard_map/ppermute | solution.py:130
  31.3 2.3 %collective-permute-done.4 = f32[16,128,128]{2,1,0:T(8,128)S(1)} collective-permute-done((f32[16,128,128]{2,1,0:T(8,128)S(1)}, f32[16,128,128]{2,1,0:T(8,128)S(1)}, u32[]{:S(2)}, u32[]{:S(2)}) %collective-permute-start.4) | collective-permute-done | bytes 1048608 | tf_op jit(solution)/shard_map/ppermute | solution.py:130
  33.6 2.2 %collective-permute-start.5 = (f32[8,128,128]{2,1,0:T(8,128)S(1)}, f32[8,128,128]{2,1,0:T(8,128)S(1)}, u32[]{:S(2)}, u32[]{:S(2)}) collective-permute-start(f32[8,128,128]{2,1,0:T(8,128)S(1)} %dynamic-slice_add_fusion), channel_id=1, source_target_pairs={{0,4},{4,8},{8,12},{12,16},{16,20},{20,24},{24,28},{1,5},{5,9},{9,... | collective-permute-start | bytes 1572872 | tf_op jit(solution)/shard_map/ppermute | solution.py:20
  35.8 13.0 %collective-permute-done.5 = f32[8,128,128]{2,1,0:T(8,128)S(1)} collective-permute-done((f32[8,128,128]{2,1,0:T(8,128)S(1)}, f32[8,128,128]{2,1,0:T(8,128)S(1)}, u32[]{:S(2)}, u32[]{:S(2)}) %collective-permute-start.5) | collective-permute-done | bytes 524320 | tf_op jit(solution)/shard_map/ppermute | solution.py:20
  48.9 3.2 %collective-permute-start.6 = (f32[8,128,128]{2,1,0:T(8,128)S(1)}, f32[8,128,128]{2,1,0:T(8,128)}, u32[]{:S(2)}, u32[]{:S(2)}) collective-permute-start(f32[8,128,128]{2,1,0:T(8,128)S(1)} %add.79), channel_id=1, source_target_pairs={{0,8},{4,12},{8,16},{12,20},{16,24},{20,28},{1,9},{5,13},{9,17},{1... | collective-permute-start | bytes 1572872 | tf_op jit(solution)/shard_map/ppermute | solution.py:20
  52.1 2.1 %copy.33 = bf16[128,2048]{0,1:T(8,128)(2,1)} copy(bf16[128,2048]{1,0:T(8,128)(2,1)} %get-tuple-element.44) | data formatting | bytes 1048576
  57.0 6.0 %collective-permute-done.6 = f32[8,128,128]{2,1,0:T(8,128)} collective-permute-done((f32[8,128,128]{2,1,0:T(8,128)S(1)}, f32[8,128,128]{2,1,0:T(8,128)}, u32[]{:S(2)}, u32[]{:S(2)}) %collective-permute-start.6) | collective-permute-done | bytes 524320 | tf_op jit(solution)/shard_map/ppermute | solution.py:20
  64.2 3.2 %collective-permute-start.7 = (f32[8,128,128]{2,1,0:T(8,128)S(1)}, f32[8,128,128]{2,1,0:T(8,128)S(1)}, u32[]{:S(2)}, u32[]{:S(2)}) collective-permute-start(f32[8,128,128]{2,1,0:T(8,128)S(1)} %add.80), channel_id=1, source_target_pairs={{0,16},{4,20},{8,24},{12,28},{1,17},{5,21},{9,25},{13,29},{2,18},{... | collective-permute-start | bytes 1572872 | tf_op jit(solution)/shard_map/ppermute | solution.py:20
  69.6 19.6 %collective-permute-done.7 = f32[8,128,128]{2,1,0:T(8,128)S(1)} collective-permute-done((f32[8,128,128]{2,1,0:T(8,128)S(1)}, f32[8,128,128]{2,1,0:T(8,128)S(1)}, u32[]{:S(2)}, u32[]{:S(2)}) %collective-permute-start.7) | collective-permute-done | bytes 524320 | tf_op jit(solution)/shard_map/ppermute | solution.py:20
  90.0 2.9 %fusion.1 = f32[256,16,128]{0,2,1:T(8,128)S(1)} fusion(bf16[256,16,128]{0,2,1:T(8,128)(2,1)} %bitcast.25, bf16[256,16,128]{0,2,1:T(8,128)(2,1)} %bitcast.26, bf16[256,16,128]{0,2,1:T(8,128)(2,1)S(1)} %bitcast.23, pred[256,256]{1,0:T(8,128)(4,1)S(1)} %iota_compare_fusion), kind=kOutput, calls=%fused_computation.7 | convolution fusion | flops 538968064 | bytes 5308416 | tf_op jit(solution)/shard_map/hts,she->the/dot_general | solution.py:103
  93.0 2.3 %add_subtract_fusion = f32[8,128,128]{2,1,0:T(8,128)} fusion(f32[8,128,128]{2,1,0:T(8,128)} %copy-done.3, f32[8,128,128]{2,1,0:T(8,128)} %copy-done.8, f32[8,128,128]{2,1,0:T(8,128)} %copy-done.10), kind=kLoop, calls=%fused_computation.18 | loop fusion | flops 262144 | bytes 2097152 | tf_op jit(solution)/shard_map/sub | solution.py:22
  95.3 2.7 %collective-permute-start.12 = (f32[8,128,128]{2,1,0:T(8,128)}, f32[8,128,128]{2,1,0:T(8,128)}, u32[]{:S(2)}, u32[]{:S(2)}) collective-permute-start(f32[8,128,128]{2,1,0:T(8,128)} %add_subtract_fusion), channel_id=1, source_target_pairs={{0,2},{2,0},{1,3},{3,1},{4,6},{6,4},{5,7},{7,5},{8,10},{10,8},{9,1... | collective-permute-start | bytes 1572872 | tf_op jit(solution)/shard_map/ppermute | solution.py:138
  99.4 12.4 %collective-permute-done.14.refs_6_ = bf16[256,2048]{1,0:T(8,128)(2,1)} collective-permute-done((bf16[256,2048]{1,0:T(8,128)(2,1)}, bf16[256,2048]{1,0:T(8,128)(2,1)}, u32[]{:S(2)}, u32[]{:S(2)}) %collective-permute-start.14) | collective-permute-done | bytes 1048608 | tf_op jit(solution)/shard_map/ppermute | solution.py:82
  111.8 2.2 %collective-permute-start.15 = (bf16[256,2048]{1,0:T(8,128)(2,1)}, bf16[256,2048]{1,0:T(8,128)(2,1)}, u32[]{:S(2)}, u32[]{:S(2)}) collective-permute-start(bf16[256,2048]{1,0:T(8,128)(2,1)} %collective-permute-done.14.refs_6_), channel_id=1, source_target_pairs={{0,4},{4,12},{12,20},{20,28},{28,24},{24,16},{16,8},{8,0},{1,5},{5... | collective-permute-start | bytes 3145736 | tf_op jit(solution)/shard_map/ppermute | solution.py:82
  114.0 1.8 %collective-permute-start.18 = (bf16[256,2048]{1,0:T(8,128)(2,1)}, bf16[256,2048]{1,0:T(8,128)(2,1)}, u32[]{:S(2)}, u32[]{:S(2)}) collective-permute-start(bf16[256,2048]{1,0:T(8,128)(2,1)} %collective-permute-done.14.refs_6_), channel_id=1, source_target_pairs={{0,2},{2,0},{1,3},{3,1},{4,6},{6,4},{5,7},{7,5},{8,10},{10,8},{9,1... | collective-permute-start | bytes 3145736 | tf_op jit(solution)/shard_map/ppermute | solution.py:258
  122.4 12.8 %collective-permute-done.15.refs_10_ = bf16[256,2048]{1,0:T(8,128)(2,1)} collective-permute-done((bf16[256,2048]{1,0:T(8,128)(2,1)}, bf16[256,2048]{1,0:T(8,128)(2,1)}, u32[]{:S(2)}, u32[]{:S(2)}) %collective-permute-start.15) | collective-permute-done | bytes 1048608 | tf_op jit(solution)/shard_map/ppermute | solution.py:82
  135.2 5.7 %collective-permute-done.17.refs_12_ = bf16[256,2048]{1,0:T(8,128)(2,1)} collective-permute-done((bf16[256,2048]{1,0:T(8,128)(2,1)}, bf16[256,2048]{1,0:T(8,128)(2,1)}, u32[]{:S(2)}, u32[]{:S(2)}) %collective-permute-start.17) | collective-permute-done | bytes 1048608 | tf_op jit(solution)/shard_map/ppermute | solution.py:82
  142.1 1.9 %slice.7 = bf16[128,2048]{1,0:T(8,128)(2,1)} slice(bf16[256,2048]{1,0:T(8,128)(2,1)} %collective-permute-done.17.refs_12_), slice={[128:256], [0:2048]} | slice | bytes 1048576 | tf_op jit(solution)/shard_map/slice | solution.py:80
  147.5 7.3 %collective-permute-done.22 = bf16[128,2048]{1,0:T(8,128)(2,1)} collective-permute-done((bf16[128,2048]{1,0:T(8,128)(2,1)S(1)}, bf16[128,2048]{1,0:T(8,128)(2,1)}, u32[]{:S(2)}, u32[]{:S(2)}) %collective-permute-start.22) | collective-permute-done | bytes 524320 | tf_op jit(solution)/shard_map/ppermute | solution.py:79
  157.6 2.1 %collective-permute-start.24 = (bf16[256,2048]{1,0:T(8,128)(2,1)S(1)}, bf16[256,2048]{1,0:T(8,128)(2,1)}, u32[]{:S(2)}, u32[]{:S(2)}) collective-permute-start(bf16[256,2048]{1,0:T(8,128)(2,1)S(1)} %constant_dynamic-update-slice_fusion.refs_14_), channel_id=1, source_target_pairs={{0,2},{2,0},{1,3},{3,1},{4,6},{6,4},{5,7},{7,5},{8,10},{10,8},{9,1... | collective-permute-start | bytes 3145736 | tf_op jit(solution)/shard_map/ppermute | solution.py:267
  162.2 9.1 %shard_map.82 = bf16[256,2048]{1,0:T(8,128)(2,1)} custom-call(s32[16]{0:T(128)} %mul.51.starts_ref, bf16[256,4096]{1,0:T(8,128)(2,1)} %pad_maximum_fusion.normed_ref, bf16[256,2048]{1,0:T(8,128)(2,1)} %refs_0_.1, bf16[256,2048]{1,0:T(8,128)(2,1)} %collective-permute-done.9.refs_1_, bf16[256,2048]{1,0:T(8,128)(2,1)} %collective-permute-done.refs_2_, ...), custom_call_target="tpu_custom_call" | custom-call | tf_op jit(solution)/shard_map/pallas_call | solution.py:189
  (95 shorter events, 33.6 us)
Async XLA Ops:
  2.4 13.1 %collective-permute-start.2 = (bf16[128,2048]{0,1:T(8,128)(2,1)}, bf16[128,2048]{0,1:T(8,128)(2,1)S(1)}, u32[]{:S(2)}, u32[]{:S(2)}) collective-permute-start(bf16[128,2048]{0,1:T(8,128)(2,1)} %copy.29), channel_id=1, source_target_pairs={{0,1},{1,0},{2,3},{3,2},{4,5},{5,4},{6,7},{7,6},{8,9},{9,8},{10,11... | collective-permute-start | bytes 1572872 | tf_op jit(solution)/shard_map/ppermute | solution.py:36
  3.6 24.0 %collective-permute-start = (bf16[256,2048]{1,0:T(8,128)(2,1)}, bf16[256,2048]{1,0:T(8,128)(2,1)}, u32[]{:S(2)}, u32[]{:S(2)}) collective-permute-start(bf16[256,2048]{1,0:T(8,128)(2,1)} %refs_0_.1), channel_id=1, source_target_pairs={{0,4},{4,12},{12,20},{20,28},{28,24},{24,16},{16,8},{8,0},{1,5},{5... | collective-permute-start | bytes 3145736 | tf_op jit(solution)/shard_map/ppermute | solution.py:82
  4.9 23.7 %collective-permute-start.1 = (bf16[256,2048]{1,0:T(8,128)(2,1)}, bf16[256,2048]{1,0:T(8,128)(2,1)}, u32[]{:S(2)}, u32[]{:S(2)}) collective-permute-start(bf16[256,2048]{1,0:T(8,128)(2,1)} %refs_0_.1), channel_id=1, source_target_pairs={{4,0},{12,4},{20,12},{28,20},{24,28},{16,24},{8,16},{0,8},{5,1},{1... | collective-permute-start | bytes 3145736 | tf_op jit(solution)/shard_map/ppermute | solution.py:82
  7.7 19.0 %collective-permute-start.3 = (bf16[128,2048]{0,1:T(8,128)(2,1)S(1)}, bf16[128,2048]{0,1:T(8,128)(2,1)S(1)}, u32[]{:S(2)}, u32[]{:S(2)}) collective-permute-start(bf16[128,2048]{0,1:T(8,128)(2,1)S(1)} %copy.31), channel_id=1, source_target_pairs={{0,1},{1,0},{2,3},{3,2},{4,5},{5,4},{6,7},{7,6},{8,9},{9,8},{10,11... | collective-permute-start | bytes 1572872 | tf_op jit(solution)/shard_map/ppermute | solution.py:36
  33.6 15.2 %collective-permute-start.5 = (f32[8,128,128]{2,1,0:T(8,128)S(1)}, f32[8,128,128]{2,1,0:T(8,128)S(1)}, u32[]{:S(2)}, u32[]{:S(2)}) collective-permute-start(f32[8,128,128]{2,1,0:T(8,128)S(1)} %dynamic-slice_add_fusion), channel_id=1, source_target_pairs={{0,4},{4,8},{8,12},{12,16},{16,20},{20,24},{24,28},{1,5},{5,9},{9,... | collective-permute-start | bytes 1572872 | tf_op jit(solution)/shard_map/ppermute | solution.py:20
  48.9 14.2 %collective-permute-start.6 = (f32[8,128,128]{2,1,0:T(8,128)S(1)}, f32[8,128,128]{2,1,0:T(8,128)}, u32[]{:S(2)}, u32[]{:S(2)}) collective-permute-start(f32[8,128,128]{2,1,0:T(8,128)S(1)} %add.79), channel_id=1, source_target_pairs={{0,8},{4,12},{8,16},{12,20},{16,24},{20,28},{1,9},{5,13},{9,17},{1... | collective-permute-start | bytes 1572872 | tf_op jit(solution)/shard_map/ppermute | solution.py:20
  54.1 13.2 %collective-permute-start.8 = (bf16[128,2048]{0,1:T(8,128)(2,1)}, bf16[128,2048]{0,1:T(8,128)(2,1)}, u32[]{:S(2)}, u32[]{:S(2)}) collective-permute-start(bf16[128,2048]{0,1:T(8,128)(2,1)} %copy.33), channel_id=1, source_target_pairs={{0,1},{1,0},{2,3},{3,2},{4,5},{5,4},{6,7},{7,6},{8,9},{9,8},{10,11... | collective-permute-start | bytes 1572872 | tf_op jit(solution)/shard_map/ppermute | solution.py:36
  54.4 40.9 %collective-permute-start.9 = (bf16[256,2048]{1,0:T(8,128)(2,1)}, bf16[256,2048]{1,0:T(8,128)(2,1)}, u32[]{:S(2)}, u32[]{:S(2)}) collective-permute-start(bf16[256,2048]{1,0:T(8,128)(2,1)} %refs_0_.1), channel_id=1, source_target_pairs={{0,2},{2,0},{1,3},{3,1},{4,6},{6,4},{5,7},{7,5},{8,10},{10,8},{9,1... | collective-permute-start | bytes 3145736 | tf_op jit(solution)/shard_map/ppermute | solution.py:244
  56.5 38.8 %collective-permute-start.10 = (bf16[256,2048]{1,0:T(8,128)(2,1)}, bf16[256,2048]{1,0:T(8,128)(2,1)}, u32[]{:S(2)}, u32[]{:S(2)}) collective-permute-start(bf16[256,2048]{1,0:T(8,128)(2,1)} %collective-permute-done.refs_2_), channel_id=1, source_target_pairs={{0,2},{2,0},{1,3},{3,1},{4,6},{6,4},{5,7},{7,5},{8,10},{10,8},{9,1... | collective-permute-start | bytes 3145736 | tf_op jit(solution)/shard_map/ppermute | solution.py:244
  56.6 38.8 %collective-permute-start.11 = (bf16[256,2048]{1,0:T(8,128)(2,1)}, bf16[256,2048]{1,0:T(8,128)(2,1)}, u32[]{:S(2)}, u32[]{:S(2)}) collective-permute-start(bf16[256,2048]{1,0:T(8,128)(2,1)} %collective-permute-done.1.refs_4_), channel_id=1, source_target_pairs={{0,2},{2,0},{1,3},{3,1},{4,6},{6,4},{5,7},{7,5},{8,10},{10,8},{9,1... | collective-permute-start | bytes 3145736 | tf_op jit(solution)/shard_map/ppermute | solution.py:244
  64.2 25.0 %collective-permute-start.7 = (f32[8,128,128]{2,1,0:T(8,128)S(1)}, f32[8,128,128]{2,1,0:T(8,128)S(1)}, u32[]{:S(2)}, u32[]{:S(2)}) collective-permute-start(f32[8,128,128]{2,1,0:T(8,128)S(1)} %add.80), channel_id=1, source_target_pairs={{0,16},{4,20},{8,24},{12,28},{1,17},{5,21},{9,25},{13,29},{2,18},{... | collective-permute-start | bytes 1572872 | tf_op jit(solution)/shard_map/ppermute | solution.py:20
  69.6 42.2 %collective-permute-start.14 = (bf16[256,2048]{1,0:T(8,128)(2,1)}, bf16[256,2048]{1,0:T(8,128)(2,1)}, u32[]{:S(2)}, u32[]{:S(2)}) collective-permute-start(bf16[256,2048]{1,0:T(8,128)(2,1)} %collective-permute-done.refs_2_), channel_id=1, source_target_pairs={{0,4},{4,12},{12,20},{20,28},{28,24},{24,16},{16,8},{8,0},{1,5},{5... | collective-permute-start | bytes 3145736 | tf_op jit(solution)/shard_map/ppermute | solution.py:82
  89.2 26.6 %collective-permute-start.16 = (bf16[256,2048]{1,0:T(8,128)(2,1)}, bf16[256,2048]{1,0:T(8,128)(2,1)}, u32[]{:S(2)}, u32[]{:S(2)}) collective-permute-start(bf16[256,2048]{1,0:T(8,128)(2,1)} %collective-permute-done.1.refs_4_), channel_id=1, source_target_pairs={{4,0},{12,4},{20,12},{28,20},{24,28},{16,24},{8,16},{0,8},{5,1},{1... | collective-permute-start | bytes 3145736 | tf_op jit(solution)/shard_map/ppermute | solution.py:82
  95.3 20.6 %collective-permute-start.12 = (f32[8,128,128]{2,1,0:T(8,128)}, f32[8,128,128]{2,1,0:T(8,128)}, u32[]{:S(2)}, u32[]{:S(2)}) collective-permute-start(f32[8,128,128]{2,1,0:T(8,128)} %add_subtract_fusion), channel_id=1, source_target_pairs={{0,2},{2,0},{1,3},{3,1},{4,6},{6,4},{5,7},{7,5},{8,10},{10,8},{9,1... | collective-permute-start | bytes 1572872 | tf_op jit(solution)/shard_map/ppermute | solution.py:138
  111.8 23.4 %collective-permute-start.15 = (bf16[256,2048]{1,0:T(8,128)(2,1)}, bf16[256,2048]{1,0:T(8,128)(2,1)}, u32[]{:S(2)}, u32[]{:S(2)}) collective-permute-start(bf16[256,2048]{1,0:T(8,128)(2,1)} %collective-permute-done.14.refs_6_), channel_id=1, source_target_pairs={{0,4},{4,12},{12,20},{20,28},{28,24},{24,16},{16,8},{8,0},{1,5},{5... | collective-permute-start | bytes 3145736 | tf_op jit(solution)/shard_map/ppermute | solution.py:82
  114.0 26.9 %collective-permute-start.18 = (bf16[256,2048]{1,0:T(8,128)(2,1)}, bf16[256,2048]{1,0:T(8,128)(2,1)}, u32[]{:S(2)}, u32[]{:S(2)}) collective-permute-start(bf16[256,2048]{1,0:T(8,128)(2,1)} %collective-permute-done.14.refs_6_), channel_id=1, source_target_pairs={{0,2},{2,0},{1,3},{3,1},{4,6},{6,4},{5,7},{7,5},{8,10},{10,8},{9,1... | collective-permute-start | bytes 3145736 | tf_op jit(solution)/shard_map/ppermute | solution.py:258
  115.8 25.1 %collective-permute-start.17 = (bf16[256,2048]{1,0:T(8,128)(2,1)}, bf16[256,2048]{1,0:T(8,128)(2,1)}, u32[]{:S(2)}, u32[]{:S(2)}) collective-permute-start(bf16[256,2048]{1,0:T(8,128)(2,1)} %collective-permute-done.16.refs_8_), channel_id=1, source_target_pairs={{4,0},{12,4},{20,12},{28,20},{24,28},{16,24},{8,16},{0,8},{5,1},{1... | collective-permute-start | bytes 3145736 | tf_op jit(solution)/shard_map/ppermute | solution.py:82
  115.8 25.1 %collective-permute-start.19 = (bf16[256,2048]{1,0:T(8,128)(2,1)}, bf16[256,2048]{1,0:T(8,128)(2,1)}, u32[]{:S(2)}, u32[]{:S(2)}) collective-permute-start(bf16[256,2048]{1,0:T(8,128)(2,1)} %collective-permute-done.16.refs_8_), channel_id=1, source_target_pairs={{0,2},{2,0},{1,3},{3,1},{4,6},{6,4},{5,7},{7,5},{8,10},{10,8},{9,1... | collective-permute-start | bytes 3145736 | tf_op jit(solution)/shard_map/ppermute | solution.py:258
  120.8 39.0 %collective-permute-start.13 = (bf16[256,2048]{1,0:T(8,128)(2,1)S(1)}, bf16[256,2048]{1,0:T(8,128)(2,1)S(1)}, u32[]{:S(2)}, u32[]{:S(2)}) collective-permute-start(bf16[256,2048]{1,0:T(8,128)(2,1)S(1)} %copy.27), channel_id=1, source_target_pairs={{0,1},{1,0},{2,3},{3,2},{4,5},{5,4},{6,7},{7,6},{8,9},{9,8},{10,11... | collective-permute-start | bytes 3145736 | tf_op jit(solution)/shard_map/ppermute | solution.py:124
  142.0 12.8 %collective-permute-start.22 = (bf16[128,2048]{1,0:T(8,128)(2,1)S(1)}, bf16[128,2048]{1,0:T(8,128)(2,1)}, u32[]{:S(2)}, u32[]{:S(2)}) collective-permute-start(bf16[128,2048]{1,0:T(8,128)(2,1)S(1)} %slice.6), channel_id=1, source_target_pairs={{0,4},{4,12},{12,20},{20,28},{28,24},{24,16},{16,8},{8,0},{1,5},{5... | collective-permute-start | bytes 1572872 | tf_op jit(solution)/shard_map/ppermute | solution.py:79
  144.0 12.6 %collective-permute-start.23 = (bf16[128,2048]{1,0:T(8,128)(2,1)}, bf16[128,2048]{1,0:T(8,128)(2,1)}, u32[]{:S(2)}, u32[]{:S(2)}) collective-permute-start(bf16[128,2048]{1,0:T(8,128)(2,1)} %slice.7), channel_id=1, source_target_pairs={{4,0},{12,4},{20,12},{28,20},{24,28},{16,24},{8,16},{0,8},{5,1},{1... | collective-permute-start | bytes 1572872 | tf_op jit(solution)/shard_map/ppermute | solution.py:79
  146.1 15.4 %collective-permute-start.20 = (bf16[256,2048]{1,0:T(8,128)(2,1)}, bf16[256,2048]{1,0:T(8,128)(2,1)}, u32[]{:S(2)}, u32[]{:S(2)}) collective-permute-start(bf16[256,2048]{1,0:T(8,128)(2,1)} %collective-permute-done.15.refs_10_), channel_id=1, source_target_pairs={{0,2},{2,0},{1,3},{3,1},{4,6},{6,4},{5,7},{7,5},{8,10},{10,8},{9,1... | collective-permute-start | bytes 3145736 | tf_op jit(solution)/shard_map/ppermute | solution.py:267
  147.5 14.0 %collective-permute-start.21 = (bf16[256,2048]{1,0:T(8,128)(2,1)}, bf16[256,2048]{1,0:T(8,128)(2,1)}, u32[]{:S(2)}, u32[]{:S(2)}) collective-permute-start(bf16[256,2048]{1,0:T(8,128)(2,1)} %collective-permute-done.17.refs_12_), channel_id=1, source_target_pairs={{0,2},{2,0},{1,3},{3,1},{4,6},{6,4},{5,7},{7,5},{8,10},{10,8},{9,1... | collective-permute-start | bytes 3145736 | tf_op jit(solution)/shard_map/ppermute | solution.py:267
  157.6 4.5 %collective-permute-start.24 = (bf16[256,2048]{1,0:T(8,128)(2,1)S(1)}, bf16[256,2048]{1,0:T(8,128)(2,1)}, u32[]{:S(2)}, u32[]{:S(2)}) collective-permute-start(bf16[256,2048]{1,0:T(8,128)(2,1)S(1)} %constant_dynamic-update-slice_fusion.refs_14_), channel_id=1, source_target_pairs={{0,2},{2,0},{1,3},{3,1},{4,6},{6,4},{5,7},{7,5},{8,10},{10,8},{9,1... | collective-permute-start | bytes 3145736 | tf_op jit(solution)/shard_map/ppermute | solution.py:267
  (15 other events, 135.4 us)

commit v26 on v21

--- a/solution.py
+++ b/solution.py
@@ -272,7 +272,7 @@
     sources = jnp.asarray(order, jnp.int32)[(ring_place - jnp.asarray(offsets, jnp.int32)) % n_chip]
     cores = jnp.stack([core, 1 - core]).astype(jnp.int32)
     starts = ((sources[:, None] * 2 + cores[None, :]) * out_weight.shape[0]).reshape(-1)
-    return project_blocks(gathered, starts, [w for pair in zip(got, swapped) for w in pair], group=2)
+    return project_blocks(gathered, starts, [w for pair in zip(got, swapped) for w in pair], group=1)
 
 
 def solution(mesh):

time: 174 us -> 174 us (level)
  no operation moved by 1% of the time
where the time goes in v26:
time: 174 us; the launch traced here: 172 us
  waiting for transfers between devices  96.2 us (55%)
  starting transfers between devices  32 us (18%)
  local copies, waits for them, and re-layouts  20.8 us (12%)
  Pallas kernels  8.81 us (5%)
  other arithmetic  8.14 us (5%)
  matrix products  5.53 us (3%)
    ppermute x3, waiting for transfers between devices, exclusive_prefix(): total = total + lax.ppermute(total, axis, pairs)  38.6 us
    ppermute x3, waiting for transfers between devices, ring_step(): lax.ppermute(ahead, 'chip', forward)  29.2 us
    ppermute x2, waiting for transfers between devices, head_blocks(): other = lax.ppermute(sent, 'head', SWAP)  21.1 us
    pallas_call x1, Pallas kernels, project_blocks(): pl.pallas_call(kernel, out_shape=jax.ShapeDtypeStruct((tokens, cols), jnp...  8.81 us
    ppermute x5, starting transfers between devices, local_ring(): swapped += [lax.ppermute(w, 'core', SWAP) for w in got[len(swapped):]]  8.6 us
    ppermute x3, starting transfers between devices, exclusive_prefix(): total = total + lax.ppermute(total, axis, pairs)  8.4 us
    unnamed x28, local copies, waits for them, and re-layouts  7.43 us
    ppermute x1, waiting for transfers between devices, ring_step(): lax.ppermute(ahead[:half_rows], 'chip', forward)  3.52 us
  transfers between devices with their start and end apart: 24, of which 11 were waited for; matrix products, arithmetic and copies ran while one was open for 14% of the time, Pallas kernels for 0%

profile of v26, /device:TPU:13, one launch (start us, length us, event | category | flops | bytes accessed | tf_op | source)
XLA Modules:
  0.0 172.0 jit_solution(17913612030441359021)
XLA Ops:
  3.6 2.3 %copy.22 = bf16[2,128,1,2048]{3,1,0,2:T(8,128)(2,1)} copy(bf16[2,128,1,2048]{1,3,2,0:T(8,128)(2,1)} %get-tuple-element.30) | data formatting | bytes 2097152 | tf_op jit(solution)/shard_map/jit(dynamic_index_in_dim)/dynamic_slice | solution.py:37
  9.1 21.1 %collective-permute-done.2 = bf16[2,128,2048]{2,1,0:T(8,128)(2,1)S(1)} collective-permute-done((bf16[2,128,2048]{2,1,0:T(8,128)(2,1)}, bf16[2,128,2048]{2,1,0:T(8,128)(2,1)S(1)}, u32[]{:S(2)}, u32[]{:S(2)}) %collective-permute-start.2) | collective-permute-done | bytes 1048608 | tf_op jit(solution)/shard_map/ppermute | solution.py:38
  33.1 2.2 %collective-permute-start.3 = (f32[16,128,128]{2,1,0:T(8,128)S(1)}, f32[16,128,128]{2,1,0:T(8,128)}, u32[]{:S(2)}, u32[]{:S(2)}) collective-permute-start(f32[16,128,128]{2,1,0:T(8,128)S(1)} %fusion.6), channel_id=1, source_target_pairs={{0,2},{2,0},{1,3},{3,1},{4,6},{6,4},{5,7},{7,5},{8,10},{10,8},{9,1... | collective-permute-start | bytes 3145736 | tf_op jit(solution)/shard_map/ppermute | solution.py:133
  35.4 2.4 %collective-permute-done.3 = f32[16,128,128]{2,1,0:T(8,128)} collective-permute-done((f32[16,128,128]{2,1,0:T(8,128)S(1)}, f32[16,128,128]{2,1,0:T(8,128)}, u32[]{:S(2)}, u32[]{:S(2)}) %collective-permute-start.3) | collective-permute-done | bytes 1048608 | tf_op jit(solution)/shard_map/ppermute | solution.py:133
  38.9 2.0 %collective-permute-start.4 = (f32[8,128,128]{2,1,0:T(8,128)S(1)}, f32[8,128,128]{2,1,0:T(8,128)S(1)}, u32[]{:S(2)}, u32[]{:S(2)}) collective-permute-start(f32[8,128,128]{2,1,0:T(8,128)S(1)} %dynamic-slice_add_fusion), channel_id=1, source_target_pairs={{0,4},{4,8},{8,12},{12,16},{16,20},{20,24},{24,28},{1,5},{5,9},{9,... | collective-permute-start | bytes 1572872 | tf_op jit(solution)/shard_map/ppermute | solution.py:20
  42.6 11.3 %collective-permute-done.4 = f32[8,128,128]{2,1,0:T(8,128)S(1)} collective-permute-done((f32[8,128,128]{2,1,0:T(8,128)S(1)}, f32[8,128,128]{2,1,0:T(8,128)S(1)}, u32[]{:S(2)}, u32[]{:S(2)}) %collective-permute-start.4) | collective-permute-done | bytes 524320 | tf_op jit(solution)/shard_map/ppermute | solution.py:20
  54.0 3.2 %collective-permute-start.5 = (f32[8,128,128]{2,1,0:T(8,128)S(1)}, f32[8,128,128]{2,1,0:T(8,128)S(1)}, u32[]{:S(2)}, u32[]{:S(2)}) collective-permute-start(f32[8,128,128]{2,1,0:T(8,128)S(1)} %add.80), channel_id=1, source_target_pairs={{0,8},{4,12},{8,16},{12,20},{16,24},{20,28},{1,9},{5,13},{9,17},{1... | collective-permute-start | bytes 1572872 | tf_op jit(solution)/shard_map/ppermute | solution.py:20
  58.5 1.8 %collective-permute-start.8 = (bf16[256,2048]{1,0:T(8,128)(2,1)}, bf16[256,2048]{1,0:T(8,128)(2,1)}, u32[]{:S(2)}, u32[]{:S(2)}) collective-permute-start(bf16[256,2048]{1,0:T(8,128)(2,1)} %refs_0_.1), channel_id=1, source_target_pairs={{0,2},{2,0},{1,3},{3,1},{4,6},{6,4},{5,7},{7,5},{8,10},{10,8},{9,1... | collective-permute-start | bytes 3145736 | tf_op jit(solution)/shard_map/ppermute | solution.py:247
  61.1 7.0 %collective-permute-done.5 = f32[8,128,128]{2,1,0:T(8,128)S(1)} collective-permute-done((f32[8,128,128]{2,1,0:T(8,128)S(1)}, f32[8,128,128]{2,1,0:T(8,128)S(1)}, u32[]{:S(2)}, u32[]{:S(2)}) %collective-permute-start.5) | collective-permute-done | bytes 524320 | tf_op jit(solution)/shard_map/ppermute | solution.py:20
  68.1 3.2 %collective-permute-start.6 = (f32[8,128,128]{2,1,0:T(8,128)S(1)}, f32[8,128,128]{2,1,0:T(8,128)S(1)}, u32[]{:S(2)}, u32[]{:S(2)}) collective-permute-start(f32[8,128,128]{2,1,0:T(8,128)S(1)} %add.81), channel_id=1, source_target_pairs={{0,16},{4,20},{8,24},{12,28},{1,17},{5,21},{9,25},{13,29},{2,18},{... | collective-permute-start | bytes 1572872 | tf_op jit(solution)/shard_map/ppermute | solution.py:20
  72.8 20.3 %collective-permute-done.6 = f32[8,128,128]{2,1,0:T(8,128)S(1)} collective-permute-done((f32[8,128,128]{2,1,0:T(8,128)S(1)}, f32[8,128,128]{2,1,0:T(8,128)S(1)}, u32[]{:S(2)}, u32[]{:S(2)}) %collective-permute-start.6) | collective-permute-done | bytes 524320 | tf_op jit(solution)/shard_map/ppermute | solution.py:20
  94.0 3.2 %fusion.1 = f32[256,16,128]{0,2,1:T(8,128)S(1)} fusion(bf16[256,16,128]{0,2,1:T(8,128)(2,1)} %bitcast.49, bf16[256,16,128]{0,2,1:T(8,128)(2,1)} %bitcast.54, pred[256,256]{1,0:T(8,128)(4,1)S(1)} %iota_compare_fusion, bf16[256,2048]{1,0:T(8,128)(2,1)} %copy-done.2), kind=kOutput, calls=%fused_computation.13 | convolution fusion | flops 538968064 | bytes 5308416 | tf_op jit(solution)/shard_map/hts,she->the/dot_general | solution.py:106
  98.6 2.7 %collective-permute-start.11 = (f32[8,128,128]{2,1,0:T(8,128)S(1)}, f32[8,128,128]{2,1,0:T(8,128)S(1)}, u32[]{:S(2)}, u32[]{:S(2)}) collective-permute-start(f32[8,128,128]{2,1,0:T(8,128)S(1)} %add_subtract_fusion), channel_id=1, source_target_pairs={{0,2},{2,0},{1,3},{3,1},{4,6},{6,4},{5,7},{7,5},{8,10},{10,8},{9,1... | collective-permute-start | bytes 1572872 | tf_op jit(solution)/shard_map/ppermute | solution.py:141
  102.5 13.2 %collective-permute-done.13.refs_6_ = bf16[256,2048]{1,0:T(8,128)(2,1)} collective-permute-done((bf16[256,2048]{1,0:T(8,128)(2,1)}, bf16[256,2048]{1,0:T(8,128)(2,1)}, u32[]{:S(2)}, u32[]{:S(2)}) %collective-permute-start.13) | collective-permute-done | bytes 1048608 | tf_op jit(solution)/shard_map/ppermute | solution.py:85
  115.7 2.2 %collective-permute-start.17 = (bf16[256,2048]{1,0:T(8,128)(2,1)}, bf16[256,2048]{1,0:T(8,128)(2,1)}, u32[]{:S(2)}, u32[]{:S(2)}) collective-permute-start(bf16[256,2048]{1,0:T(8,128)(2,1)} %collective-permute-done.13.refs_6_), channel_id=1, source_target_pairs={{0,4},{4,12},{12,20},{20,28},{28,24},{24,16},{16,8},{8,0},{1,5},{5... | collective-permute-start | bytes 3145736 | tf_op jit(solution)/shard_map/ppermute | solution.py:85
  118.1 1.8 %multiply_reduce_fusion = (f32[256,16]{0,1:T(8,128)S(1)}, f32[16,128,256]{2,1,0:T(8,128)S(1)}) fusion(f32[256,16,128]{0,2,1:T(8,128)S(1)} %fusion.1, bf16[256,16,128]{0,2,1:T(8,128)(2,1)S(1)} %bitcast.55, f32[8,128,128]{2,1,0:T(8,128)S(1)} %get-tuple-element.32, f32[8,128,128]{2,1,0:T(8,128)S(1)} %get-tuple-element.31, ...), kind=kOutput, calls=%fused_computation.11 | convolution fusion | flops 136835072 | bytes 7356417 | tf_op jit(solution)/shard_map/thd,hde->the/dot_general | solution.py:115
  123.8 15.4 %collective-permute-done.17.refs_10_ = bf16[256,2048]{1,0:T(8,128)(2,1)} collective-permute-done((bf16[256,2048]{1,0:T(8,128)(2,1)}, bf16[256,2048]{1,0:T(8,128)(2,1)}, u32[]{:S(2)}, u32[]{:S(2)}) %collective-permute-start.17) | collective-permute-done | bytes 1048608 | tf_op jit(solution)/shard_map/ppermute | solution.py:85
  140.3 2.3 %collective-permute-start.21 = (bf16[128,2048]{1,0:T(8,128)(2,1)S(1)}, bf16[128,2048]{1,0:T(8,128)(2,1)S(1)}, u32[]{:S(2)}, u32[]{:S(2)}) collective-permute-start(bf16[128,2048]{1,0:T(8,128)(2,1)S(1)} %slice.20), channel_id=1, source_target_pairs={{0,4},{4,12},{12,20},{20,28},{28,24},{24,16},{16,8},{8,0},{1,5},{5... | collective-permute-start | bytes 1572872 | tf_op jit(solution)/shard_map/ppermute | solution.py:82
  142.5 1.9 %slice.21 = bf16[128,2048]{1,0:T(8,128)(2,1)} slice(bf16[256,2048]{1,0:T(8,128)(2,1)} %collective-permute-done.19.refs_12_), slice={[128:256], [0:2048]} | slice | bytes 1048576 | tf_op jit(solution)/shard_map/slice | solution.py:83
  145.2 2.7 %collective-permute-start.14 = (bf16[256,2048]{1,0:T(8,128)(2,1)}, bf16[256,2048]{1,0:T(8,128)(2,1)}, u32[]{:S(2)}, u32[]{:S(2)}) collective-permute-start(bf16[256,2048]{1,0:T(8,128)(2,1)} %collective-permute-done.13.refs_6_), channel_id=1, source_target_pairs={{0,2},{2,0},{1,3},{3,1},{4,6},{6,4},{5,7},{7,5},{8,10},{10,8},{9,1... | collective-permute-start | bytes 3145736 | tf_op jit(solution)/shard_map/ppermute | solution.py:266
  147.9 3.5 %collective-permute-done.21 = bf16[128,2048]{1,0:T(8,128)(2,1)S(1)} collective-permute-done((bf16[128,2048]{1,0:T(8,128)(2,1)S(1)}, bf16[128,2048]{1,0:T(8,128)(2,1)S(1)}, u32[]{:S(2)}, u32[]{:S(2)}) %collective-permute-start.21) | collective-permute-done | bytes 524320 | tf_op jit(solution)/shard_map/ppermute | solution.py:82
  152.2 3.3 %collective-permute-start.18 = (bf16[256,2048]{1,0:T(8,128)(2,1)}, bf16[256,2048]{1,0:T(8,128)(2,1)}, u32[]{:S(2)}, u32[]{:S(2)}) collective-permute-start(bf16[256,2048]{1,0:T(8,128)(2,1)} %collective-permute-done.17.refs_10_), channel_id=1, source_target_pairs={{0,2},{2,0},{1,3},{3,1},{4,6},{6,4},{5,7},{7,5},{8,10},{10,8},{9,1... | collective-permute-start | bytes 3145736 | tf_op jit(solution)/shard_map/ppermute | solution.py:266
  156.5 2.6 %collective-permute-start.20 = (bf16[256,2048]{1,0:T(8,128)(2,1)}, bf16[256,2048]{1,0:T(8,128)(2,1)}, u32[]{:S(2)}, u32[]{:S(2)}) collective-permute-start(bf16[256,2048]{1,0:T(8,128)(2,1)} %collective-permute-done.19.refs_12_), channel_id=1, source_target_pairs={{0,2},{2,0},{1,3},{3,1},{4,6},{6,4},{5,7},{7,5},{8,10},{10,8},{9,1... | collective-permute-start | bytes 3145736 | tf_op jit(solution)/shard_map/ppermute | solution.py:266
  163.1 8.8 %shard_map.82 = bf16[256,2048]{1,0:T(8,128)(2,1)} custom-call(s32[16]{0:T(128)} %mul.41.starts_ref, bf16[256,4096]{1,0:T(8,128)(2,1)} %pad_maximum_fusion.normed_ref, bf16[256,2048]{1,0:T(8,128)(2,1)} %refs_0_.1, bf16[256,2048]{1,0:T(8,128)(2,1)} %collective-permute-done.8.refs_1_, bf16[256,2048]{1,0:T(8,128)(2,1)} %collective-permute-done.refs_2_, ...), custom_call_target="tpu_custom_call" | custom-call | tf_op jit(solution)/shard_map/pallas_call | solution.py:192
  (90 shorter events, 31.0 us)
Async XLA Ops:
  5.9 24.3 %collective-permute-start.2 = (bf16[2,128,2048]{2,1,0:T(8,128)(2,1)}, bf16[2,128,2048]{2,1,0:T(8,128)(2,1)S(1)}, u32[]{:S(2)}, u32[]{:S(2)}) collective-permute-start(bf16[2,128,2048]{2,1,0:T(8,128)(2,1)} %bitcast.6), channel_id=1, source_target_pairs={{0,1},{1,0},{2,3},{3,2},{4,5},{5,4},{6,7},{7,6},{8,9},{9,8},{10,11... | collective-permute-start | bytes 3145736 | tf_op jit(solution)/shard_map/ppermute | solution.py:38
  7.1 24.0 %collective-permute-start = (bf16[256,2048]{1,0:T(8,128)(2,1)}, bf16[256,2048]{1,0:T(8,128)(2,1)}, u32[]{:S(2)}, u32[]{:S(2)}) collective-permute-start(bf16[256,2048]{1,0:T(8,128)(2,1)} %refs_0_.1), channel_id=1, source_target_pairs={{0,4},{4,12},{12,20},{20,28},{28,24},{24,16},{16,8},{8,0},{1,5},{5... | collective-permute-start | bytes 3145736 | tf_op jit(solution)/shard_map/ppermute | solution.py:85
  8.4 23.7 %collective-permute-start.1 = (bf16[256,2048]{1,0:T(8,128)(2,1)}, bf16[256,2048]{1,0:T(8,128)(2,1)}, u32[]{:S(2)}, u32[]{:S(2)}) collective-permute-start(bf16[256,2048]{1,0:T(8,128)(2,1)} %refs_0_.1), channel_id=1, source_target_pairs={{4,0},{12,4},{20,12},{28,20},{24,28},{16,24},{8,16},{0,8},{5,1},{1... | collective-permute-start | bytes 3145736 | tf_op jit(solution)/shard_map/ppermute | solution.py:85
  33.1 4.6 %collective-permute-start.3 = (f32[16,128,128]{2,1,0:T(8,128)S(1)}, f32[16,128,128]{2,1,0:T(8,128)}, u32[]{:S(2)}, u32[]{:S(2)}) collective-permute-start(f32[16,128,128]{2,1,0:T(8,128)S(1)} %fusion.6), channel_id=1, source_target_pairs={{0,2},{2,0},{1,3},{3,1},{4,6},{6,4},{5,7},{7,5},{8,10},{10,8},{9,1... | collective-permute-start | bytes 3145736 | tf_op jit(solution)/shard_map/ppermute | solution.py:133
  38.9 15.0 %collective-permute-start.4 = (f32[8,128,128]{2,1,0:T(8,128)S(1)}, f32[8,128,128]{2,1,0:T(8,128)S(1)}, u32[]{:S(2)}, u32[]{:S(2)}) collective-permute-start(f32[8,128,128]{2,1,0:T(8,128)S(1)} %dynamic-slice_add_fusion), channel_id=1, source_target_pairs={{0,4},{4,8},{8,12},{12,16},{16,20},{20,24},{24,28},{1,5},{5,9},{9,... | collective-permute-start | bytes 1572872 | tf_op jit(solution)/shard_map/ppermute | solution.py:20
  54.0 14.1 %collective-permute-start.5 = (f32[8,128,128]{2,1,0:T(8,128)S(1)}, f32[8,128,128]{2,1,0:T(8,128)S(1)}, u32[]{:S(2)}, u32[]{:S(2)}) collective-permute-start(f32[8,128,128]{2,1,0:T(8,128)S(1)} %add.80), channel_id=1, source_target_pairs={{0,8},{4,12},{8,16},{12,20},{16,24},{20,28},{1,9},{5,13},{9,17},{1... | collective-permute-start | bytes 1572872 | tf_op jit(solution)/shard_map/ppermute | solution.py:20
  58.2 13.1 %collective-permute-start.7 = (bf16[1,128,2048]{2,1,0:T(8,128)(2,1)}, bf16[1,128,2048]{2,1,0:T(8,128)(2,1)S(1)}, u32[]{:S(2)}, u32[]{:S(2)}) collective-permute-start(bf16[1,128,2048]{2,1,0:T(8,128)(2,1)} %bitcast.11), channel_id=1, source_target_pairs={{0,1},{1,0},{2,3},{3,2},{4,5},{5,4},{6,7},{7,6},{8,9},{9,8},{10,11... | collective-permute-start | bytes 1572872 | tf_op jit(solution)/shard_map/ppermute | solution.py:38
  58.5 40.1 %collective-permute-start.8 = (bf16[256,2048]{1,0:T(8,128)(2,1)}, bf16[256,2048]{1,0:T(8,128)(2,1)}, u32[]{:S(2)}, u32[]{:S(2)}) collective-permute-start(bf16[256,2048]{1,0:T(8,128)(2,1)} %refs_0_.1), channel_id=1, source_target_pairs={{0,2},{2,0},{1,3},{3,1},{4,6},{6,4},{5,7},{7,5},{8,10},{10,8},{9,1... | collective-permute-start | bytes 3145736 | tf_op jit(solution)/shard_map/ppermute | solution.py:247
  60.5 38.1 %collective-permute-start.10 = (bf16[256,2048]{1,0:T(8,128)(2,1)}, bf16[256,2048]{1,0:T(8,128)(2,1)}, u32[]{:S(2)}, u32[]{:S(2)}) collective-permute-start(bf16[256,2048]{1,0:T(8,128)(2,1)} %collective-permute-done.1.refs_4_), channel_id=1, source_target_pairs={{0,2},{2,0},{1,3},{3,1},{4,6},{6,4},{5,7},{7,5},{8,10},{10,8},{9,1... | collective-permute-start | bytes 3145736 | tf_op jit(solution)/shard_map/ppermute | solution.py:247
  60.6 38.0 %collective-permute-start.9 = (bf16[256,2048]{1,0:T(8,128)(2,1)}, bf16[256,2048]{1,0:T(8,128)(2,1)}, u32[]{:S(2)}, u32[]{:S(2)}) collective-permute-start(bf16[256,2048]{1,0:T(8,128)(2,1)} %collective-permute-done.refs_2_), channel_id=1, source_target_pairs={{0,2},{2,0},{1,3},{3,1},{4,6},{6,4},{5,7},{7,5},{8,10},{10,8},{9,1... | collective-permute-start | bytes 3145736 | tf_op jit(solution)/shard_map/ppermute | solution.py:247
  68.1 25.0 %collective-permute-start.6 = (f32[8,128,128]{2,1,0:T(8,128)S(1)}, f32[8,128,128]{2,1,0:T(8,128)S(1)}, u32[]{:S(2)}, u32[]{:S(2)}) collective-permute-start(f32[8,128,128]{2,1,0:T(8,128)S(1)} %add.81), channel_id=1, source_target_pairs={{0,16},{4,20},{8,24},{12,28},{1,17},{5,21},{9,25},{13,29},{2,18},{... | collective-permute-start | bytes 1572872 | tf_op jit(solution)/shard_map/ppermute | solution.py:20
  72.8 42.9 %collective-permute-start.13 = (bf16[256,2048]{1,0:T(8,128)(2,1)}, bf16[256,2048]{1,0:T(8,128)(2,1)}, u32[]{:S(2)}, u32[]{:S(2)}) collective-permute-start(bf16[256,2048]{1,0:T(8,128)(2,1)} %collective-permute-done.refs_2_), channel_id=1, source_target_pairs={{0,4},{4,12},{12,20},{20,28},{28,24},{24,16},{16,8},{8,0},{1,5},{5... | collective-permute-start | bytes 3145736 | tf_op jit(solution)/shard_map/ppermute | solution.py:85
  93.2 24.8 %collective-permute-start.15 = (bf16[256,2048]{1,0:T(8,128)(2,1)}, bf16[256,2048]{1,0:T(8,128)(2,1)}, u32[]{:S(2)}, u32[]{:S(2)}) collective-permute-start(bf16[256,2048]{1,0:T(8,128)(2,1)} %collective-permute-done.1.refs_4_), channel_id=1, source_target_pairs={{4,0},{12,4},{20,12},{28,20},{24,28},{16,24},{8,16},{0,8},{5,1},{1... | collective-permute-start | bytes 3145736 | tf_op jit(solution)/shard_map/ppermute | solution.py:85
  98.6 19.4 %collective-permute-start.11 = (f32[8,128,128]{2,1,0:T(8,128)S(1)}, f32[8,128,128]{2,1,0:T(8,128)S(1)}, u32[]{:S(2)}, u32[]{:S(2)}) collective-permute-start(f32[8,128,128]{2,1,0:T(8,128)S(1)} %add_subtract_fusion), channel_id=1, source_target_pairs={{0,2},{2,0},{1,3},{3,1},{4,6},{6,4},{5,7},{7,5},{8,10},{10,8},{9,1... | collective-permute-start | bytes 1572872 | tf_op jit(solution)/shard_map/ppermute | solution.py:141
  115.7 23.4 %collective-permute-start.17 = (bf16[256,2048]{1,0:T(8,128)(2,1)}, bf16[256,2048]{1,0:T(8,128)(2,1)}, u32[]{:S(2)}, u32[]{:S(2)}) collective-permute-start(bf16[256,2048]{1,0:T(8,128)(2,1)} %collective-permute-done.13.refs_6_), channel_id=1, source_target_pairs={{0,4},{4,12},{12,20},{20,28},{28,24},{24,16},{16,8},{8,0},{1,5},{5... | collective-permute-start | bytes 3145736 | tf_op jit(solution)/shard_map/ppermute | solution.py:85
  117.9 24.6 %collective-permute-start.19 = (bf16[256,2048]{1,0:T(8,128)(2,1)}, bf16[256,2048]{1,0:T(8,128)(2,1)}, u32[]{:S(2)}, u32[]{:S(2)}) collective-permute-start(bf16[256,2048]{1,0:T(8,128)(2,1)} %collective-permute-done.15.refs_8_), channel_id=1, source_target_pairs={{4,0},{12,4},{20,12},{28,20},{24,28},{16,24},{8,16},{0,8},{5,1},{1... | collective-permute-start | bytes 3145736 | tf_op jit(solution)/shard_map/ppermute | solution.py:85
  122.8 37.4 %collective-permute-start.12 = (bf16[256,2048]{1,0:T(8,128)(2,1)S(1)}, bf16[256,2048]{1,0:T(8,128)(2,1)S(1)}, u32[]{:S(2)}, u32[]{:S(2)}) collective-permute-start(bf16[256,2048]{1,0:T(8,128)(2,1)S(1)} %copy.38), channel_id=1, source_target_pairs={{0,1},{1,0},{2,3},{3,2},{4,5},{5,4},{6,7},{7,6},{8,9},{9,8},{10,11... | collective-permute-start | bytes 3145736 | tf_op jit(solution)/shard_map/ppermute | solution.py:127
  140.3 11.1 %collective-permute-start.21 = (bf16[128,2048]{1,0:T(8,128)(2,1)S(1)}, bf16[128,2048]{1,0:T(8,128)(2,1)S(1)}, u32[]{:S(2)}, u32[]{:S(2)}) collective-permute-start(bf16[128,2048]{1,0:T(8,128)(2,1)S(1)} %slice.20), channel_id=1, source_target_pairs={{0,4},{4,12},{12,20},{20,28},{28,24},{24,16},{16,8},{8,0},{1,5},{5... | collective-permute-start | bytes 1572872 | tf_op jit(solution)/shard_map/ppermute | solution.py:82
  144.4 12.1 %collective-permute-start.22 = (bf16[128,2048]{1,0:T(8,128)(2,1)}, bf16[128,2048]{1,0:T(8,128)(2,1)}, u32[]{:S(2)}, u32[]{:S(2)}) collective-permute-start(bf16[128,2048]{1,0:T(8,128)(2,1)} %slice.21), channel_id=1, source_target_pairs={{4,0},{12,4},{20,12},{28,20},{24,28},{16,24},{8,16},{0,8},{5,1},{1... | collective-permute-start | bytes 1572872 | tf_op jit(solution)/shard_map/ppermute | solution.py:82
  145.2 17.6 %collective-permute-start.14 = (bf16[256,2048]{1,0:T(8,128)(2,1)}, bf16[256,2048]{1,0:T(8,128)(2,1)}, u32[]{:S(2)}, u32[]{:S(2)}) collective-permute-start(bf16[256,2048]{1,0:T(8,128)(2,1)} %collective-permute-done.13.refs_6_), channel_id=1, source_target_pairs={{0,2},{2,0},{1,3},{3,1},{4,6},{6,4},{5,7},{7,5},{8,10},{10,8},{9,1... | collective-permute-start | bytes 3145736 | tf_op jit(solution)/shard_map/ppermute | solution.py:266
  147.9 14.9 %collective-permute-start.16 = (bf16[256,2048]{1,0:T(8,128)(2,1)}, bf16[256,2048]{1,0:T(8,128)(2,1)}, u32[]{:S(2)}, u32[]{:S(2)}) collective-permute-start(bf16[256,2048]{1,0:T(8,128)(2,1)} %collective-permute-done.15.refs_8_), channel_id=1, source_target_pairs={{0,2},{2,0},{1,3},{3,1},{4,6},{6,4},{5,7},{7,5},{8,10},{10,8},{9,1... | collective-permute-start | bytes 3145736 | tf_op jit(solution)/shard_map/ppermute | solution.py:266
  152.2 10.5 %collective-permute-start.18 = (bf16[256,2048]{1,0:T(8,128)(2,1)}, bf16[256,2048]{1,0:T(8,128)(2,1)}, u32[]{:S(2)}, u32[]{:S(2)}) collective-permute-start(bf16[256,2048]{1,0:T(8,128)(2,1)} %collective-permute-done.17.refs_10_), channel_id=1, source_target_pairs={{0,2},{2,0},{1,3},{3,1},{4,6},{6,4},{5,7},{7,5},{8,10},{10,8},{9,1... | collective-permute-start | bytes 3145736 | tf_op jit(solution)/shard_map/ppermute | solution.py:266
  156.5 6.2 %collective-permute-start.20 = (bf16[256,2048]{1,0:T(8,128)(2,1)}, bf16[256,2048]{1,0:T(8,128)(2,1)}, u32[]{:S(2)}, u32[]{:S(2)}) collective-permute-start(bf16[256,2048]{1,0:T(8,128)(2,1)} %collective-permute-done.19.refs_12_), channel_id=1, source_target_pairs={{0,2},{2,0},{1,3},{3,1},{4,6},{6,4},{5,7},{7,5},{8,10},{10,8},{9,1... | collective-permute-start | bytes 3145736 | tf_op jit(solution)/shard_map/ppermute | solution.py:266
  160.2 2.9 %collective-permute-start.23 = (bf16[256,2048]{1,0:T(8,128)(2,1)S(1)}, bf16[256,2048]{1,0:T(8,128)(2,1)}, u32[]{:S(2)}, u32[]{:S(2)}) collective-permute-start(bf16[256,2048]{1,0:T(8,128)(2,1)S(1)} %constant_dynamic-update-slice_fusion.refs_14_), channel_id=1, source_target_pairs={{0,2},{2,0},{1,3},{3,1},{4,6},{6,4},{5,7},{7,5},{8,10},{10,8},{9,1... | collective-permute-start | bytes 3145736 | tf_op jit(solution)/shard_map/ppermute | solution.py:266
  (12 other events, 42.2 us)
